TPU v7x, 32 devices: a whole 2x2x4 slice. The times are simulated.
32 devices in a mesh: groups: 2 (over x), ctx: 16 (over z, y, core).
Axes of the slice: x: 2, y: 2, z: 4, core: 2. Of those that a mesh axis runs over, the one named last changes fastest.
Arguments:
- tokens: bfloat16 [16384, 2048], P(('groups', 'ctx')), parts along dimension 0, may hold values from -14 to 14, as said below
- projected: bfloat16 [16384, 6144], P(('groups', 'ctx')), parts along dimension 0, may hold values from -6 to 6
- short_filter: float32 [3, 6144], replicated, may hold values from -3 to 3
- long_filter: bfloat16 [128, 128], replicated, may hold values from -0.5 to 0.5
- conv_bias: float32 [2048], replicated, may hold values from 0.5 to 1.5
- out_weight: bfloat16 [2048, 2048], P(None, 'ctx'), may hold values from -0.125 to 0.125
Outputs:
- result: bfloat16 [16384, 2048], P(('groups', 'ctx')), parts along dimension 0
There are 2 independent parts, one for each index of `groups`. A program takes and returns all parts, laid end to end along the dimension named above; an argument that names none is the same for every part. Nothing has to cross between parts.
Inputs may be any that keep to these rules, and one draw needn't show every extreme that they name: `tokens`: activations of the residual stream.
All inputs are finite; a program needn't handle non-finite values.
Results may differ from a plain program's by a relative error of at most 0.012.
Values may be sent and summed in bfloat16 or wider, within the bound.
No kernel may reach another device: no remote copies, remote signals or barrier semaphores. Data moves between devices by JAX's collectives and lax.ppermute only.
A program may use at most 128 MiB of HBM per device.

v0:
```python
import jax
import jax.numpy as jnp
from jax import lax
from jax.sharding import PartitionSpec as P


def shifted(block, axis, distance):
    devices = range(lax.axis_size(axis))
    route = [(i - distance, i) for i in devices if i - distance in devices]
    return lax.ppermute(block, axis, route)


def short_mixed(padded, short_filter, row_count):
    source = padded.astype(jnp.float32)
    total = short_filter[0] * source[2 : 2 + row_count]
    total = total + short_filter[1] * source[1 : 1 + row_count]
    return total + short_filter[2] * source[0:row_count]


def split_gates(mixed, channels):
    gate_rows = mixed[:, :channels]
    carried = (mixed[:, channels : 2 * channels] * mixed[:, 2 * channels :]).astype(jnp.bfloat16)
    return (gate_rows, carried)


def long_conv(extended, long_filter, row_count):
    filters, tap_count = long_filter.shape
    block = min(128, row_count)
    span = block + tap_count - 1
    reversed_taps = long_filter[:, ::-1]
    pattern = jnp.concatenate(
        [reversed_taps, jnp.zeros((filters, block), long_filter.dtype)], axis=1
    )
    toeplitz = jnp.tile(pattern, (1, block))[:, : block * span].reshape(filters, block, span)
    grouped = extended.reshape(extended.shape[0], filters, -1)

    def one_block(index):
        window = lax.dynamic_slice_in_dim(grouped, index * block, span, 0)
        part_conv = jnp.einsum("gts,sgc->tgc", toeplitz, window, preferred_element_type=jnp.float32)
        return part_conv.reshape(block, -1)

    blocks = lax.map(one_block, jnp.arange(row_count // block, dtype=jnp.int32))
    return blocks.reshape(row_count, -1)


def on_device(tokens, projected, short_filter, long_filter, conv_bias, out_weight):
    row_count = tokens.shape[0]
    tap_count = long_filter.shape[1]
    channels = out_weight.shape[0]
    edge_rows = shifted(projected[row_count - 2 :], "ctx", 1)
    mixed = short_mixed(jnp.concatenate([edge_rows, projected], axis=0), short_filter, row_count)
    gate_rows, carried = split_gates(mixed, channels)
    carried_edge = shifted(carried[row_count - tap_count + 1 :], "ctx", 1)
    extended = jnp.concatenate([carried_edge, carried], axis=0)
    conv = long_conv(extended, long_filter, row_count)
    gated = (gate_rows * (conv + conv_bias * carried.astype(jnp.float32))).astype(jnp.bfloat16)
    branch = jnp.dot(
        gated,
        lax.all_gather(out_weight, "ctx", axis=1, tiled=True),
        preferred_element_type=jnp.float32,
    )
    return (tokens.astype(jnp.float32) + branch).astype(jnp.bfloat16)


def solution(mesh):
    placed = (P(("groups", "ctx"), None), P(("groups", "ctx"), None), P(), P(), P(), P(None, "ctx"))
    return jax.shard_map(
        on_device, mesh=mesh, in_specs=placed, out_specs=P(("groups", "ctx"), None), check_vma=False
    )
```

profile of v0, /device:TPU:0, one launch (start us, length us, event | category | flops | bytes accessed | tf_op | source)
XLA Modules:
  0.0 151.2 jit_solution(11511301803925277580)
XLA Ops:
  6.5 0.7 all-gather.2.cloned.1.call-update
  7.3 0.9 slice.37
  8.2 2.4 %collective-permute-start = (bf16[2,6144]{1,0:T(2,128)(2,1)S(1)}, bf16[2,6144]{1,0:T(2,128)(2,1)S(1)}, u32[]{:S(2)}, u32[]{:S(2)}) collective-permute-start(bf16[2,6144]{1,0:T(2,128)(2,1)S(1)} %slice.37), channel_id=1, source_target_pairs={{0,1},{1,2},{2,3},{3,4},{4,5},{5,6},{6,7},{7,8},{8,9},{9,10},{10,1... | collective-permute-start | bytes 73736 | tf_op jit(solution)/shard_map/ppermute | solution.py:10
  10.5 1.1 fusion.7
  11.7 4.7 %maximum_convert_fusion = f32[514,6144]{1,0:T(8,128)S(1)} fusion(bf16[512,6144]{1,0:T(8,128)(2,1)} %param.9, bf16[2,6144]{1,0:T(2,128)(2,1)S(1)} %collective-permute-done), kind=kLoop, calls=%fused_computation.9 | loop fusion | flops 12632064 | bytes 18948096 | tf_op jit(solution)/shard_map/convert_element_type | solution.py:14
  16.3 6.6 %fusion.3 = f32[512,6144]{1,0:T(8,128)} fusion(f32[514,6144]{1,0:T(8,128)S(1)} %maximum_convert_fusion, f32[6144]{0:T(1024)S(1)} %bitcast.28, f32[6144]{0:T(1024)S(1)} %bitcast.29, f32[6144]{0:T(1024)S(1)} %bitcast.27), kind=kLoop, calls=%fused_computation.5 | loop fusion | flops 15728640 | bytes 50405376 | tf_op jit(solution)/shard_map/add | solution.py:17
  23.0 4.1 %fusion.5 = bf16[512,2048]{1,0:T(8,128)(2,1)S(1)} fusion(f32[512,6144]{1,0:T(8,128)} %fusion.3), kind=kLoop, calls=%fused_computation.11 | loop fusion | flops 2097152 | bytes 10485760 | tf_op jit(solution)/shard_map/convert_element_type | solution.py:22
  27.2 4.6 %collective-permute-start.1 = (bf16[127,2048]{1,0:T(8,128)(2,1)S(1)}, bf16[127,2048]{1,0:T(8,128)(2,1)S(1)}, u32[]{:S(2)}, u32[]{:S(2)}) collective-permute-start(bf16[127,2048]{1,0:T(8,128)(2,1)S(1)} %slice.54), channel_id=1, source_target_pairs={{0,1},{1,2},{2,3},{3,4},{4,5},{5,6},{6,7},{7,8},{8,9},{9,10},{10,1... | collective-permute-start | bytes 1560584 | tf_op jit(solution)/shard_map/ppermute | solution.py:10
  31.9 3.9 %tile.4 = bf16[128,128,256]{2,1,0:T(8,128)(2,1)} broadcast(bf16[128,256]{1,0:T(8,128)(2,1)S(1)} %concatenate.11), dimensions={0,2} | broadcast | bytes 8454144 | tf_op jit(solution)/shard_map/tile | solution.py:34
  35.8 12.4 %copy.14 = bf16[16,8,128,256]{3,1,2,0:T(8,128)(2,1)} copy(bf16[16,8,128,256]{3,2,1,0:T(8,128)(2,1)} %bitcast.24) | data formatting | bytes 16777216
  48.2 8.1 %slice.55 = bf16[128,32640]{1,0:T(8,128)(2,1)} slice(bf16[128,32768]{1,0:T(8,128)(2,1)} %bitcast.25), slice={[0:128], [0:32640]} | slice | bytes 16711680 | tf_op jit(solution)/shard_map/slice | solution.py:34
  56.3 29.5 %reshape.19 = bf16[128,128,255]{2,1,0:T(8,128)(2,1)} reshape(bf16[128,32640]{1,0:T(8,128)(2,1)} %slice.55) | data formatting | bytes 16711680 | tf_op jit(solution)/shard_map/reshape | solution.py:34
  85.8 2.0 %pad_maximum_fusion = bf16[639,2048]{1,0:T(8,128)(2,1)} fusion(bf16[512,2048]{1,0:T(8,128)(2,1)S(1)} %fusion.5, bf16[127,2048]{1,0:T(8,128)(2,1)S(1)} %collective-permute-done.1), kind=kLoop, calls=%fused_computation.16 | loop fusion | flops 5234688 | bytes 5234688 | tf_op jit(solution)/shard_map/concatenate | solution.py:54
  87.8 4.5 %copy.10 = bf16[639,2048]{0,1:T(8,128)(2,1)} copy(bf16[639,2048]{1,0:T(8,128)(2,1)} %pad_maximum_fusion) | data formatting | bytes 5234688 | tf_op jit(solution)/shard_map/concatenate | solution.py:54
  92.3 34.9 %while.10 = (s32[]{:T(128)}, f32[4,128,2048]{2,1,0:T(8,128)}, s32[4]{0:T(128)S(1)}, bf16[639,128,16]{0,2,1:T(8,128)(2,1)}, bf16[128,128,255]{2,1,0:T(8,128)(2,1)...) while((s32[]{:T(128)}, f32[4,128,2048]{2,1,0:T(8,128)}, s32[4]{0:T(128)S(1)}, ...), condition=%wide.region_1.2_spmd, body=%wide.region_0.1_spmd.sunk | while | flops 133693448 | bytes 14680731 | solution.py:42
  92.3 0.6 dynamic_slice.12
  93.4 6.2 %fusion.16 = f32[128,16,128]{2,1,0:T(8,128)S(1)} fusion(bf16[128,128,255]{2,1,0:T(8,128)(2,1)} %get-tuple-element.104, bf16[639,128,16]{0,2,1:T(8,128)(2,1)} %get-tuple-element.103, s32[]{:T(128)S(6)} %select_n.4), kind=kOutput, calls=%fused_computation.clone.1 | convolution fusion | flops 133693440 | bytes 10485764 | tf_op jit(solution)/shard_map/while/body/eval_jaxpr/gts,sgc->tgc/dot_general | solution.py:39
  99.6 0.4 copy.16
  100.0 1.1 constant_dynamic-update-slice_fusion.2
  101.0 0.6 dynamic_slice.12
  102.2 6.2 %fusion.16 = f32[128,16,128]{2,1,0:T(8,128)S(1)} fusion(bf16[128,128,255]{2,1,0:T(8,128)(2,1)} %get-tuple-element.104, bf16[639,128,16]{0,2,1:T(8,128)(2,1)} %get-tuple-element.103, s32[]{:T(128)S(6)} %select_n.4), kind=kOutput, calls=%fused_computation.clone.1 | convolution fusion | flops 133693440 | bytes 10485764 | tf_op jit(solution)/shard_map/while/body/eval_jaxpr/gts,sgc->tgc/dot_general | solution.py:39
  108.3 0.4 copy.16
  108.7 1.0 constant_dynamic-update-slice_fusion.2
  109.8 0.6 dynamic_slice.12
  110.9 6.2 %fusion.16 = f32[128,16,128]{2,1,0:T(8,128)S(1)} fusion(bf16[128,128,255]{2,1,0:T(8,128)(2,1)} %get-tuple-element.104, bf16[639,128,16]{0,2,1:T(8,128)(2,1)} %get-tuple-element.103, s32[]{:T(128)S(6)} %select_n.4), kind=kOutput, calls=%fused_computation.clone.1 | convolution fusion | flops 133693440 | bytes 10485764 | tf_op jit(solution)/shard_map/while/body/eval_jaxpr/gts,sgc->tgc/dot_general | solution.py:39
  117.1 0.4 copy.16
  117.4 1.1 constant_dynamic-update-slice_fusion.2
  118.5 0.6 dynamic_slice.12
  119.7 6.0 %fusion.16 = f32[128,16,128]{2,1,0:T(8,128)S(1)} fusion(bf16[128,128,255]{2,1,0:T(8,128)(2,1)} %get-tuple-element.104, bf16[639,128,16]{0,2,1:T(8,128)(2,1)} %get-tuple-element.103, s32[]{:T(128)S(6)} %select_n.4), kind=kOutput, calls=%fused_computation.clone.1 | convolution fusion | flops 133693440 | bytes 10485764 | tf_op jit(solution)/shard_map/while/body/eval_jaxpr/gts,sgc->tgc/dot_general | solution.py:39
  126.1 1.1 constant_dynamic-update-slice_fusion.2
  127.2 7.8 %fusion.6 = bf16[512,2048]{1,0:T(8,128)(2,1)S(1)} fusion(f32[512,6144]{1,0:T(8,128)} %fusion.3, f32[4,128,2048]{2,1,0:T(8,128)} %get-tuple-element.32, f32[2048]{0:T(1024)S(1)} %copy-done.1), kind=kLoop, calls=%fused_computation.13 | loop fusion | flops 7340032 | bytes 18882560 | tf_op jit(solution)/shard_map/convert_element_type | solution.py:56
  135.0 9.4 %add_convert_fusion = bf16[512,2048]{1,0:T(8,128)(2,1)} fusion(bf16[512,2048]{1,0:T(8,128)(2,1)} %param.8, bf16[512,2048]{1,0:T(8,128)(2,1)S(1)} %fusion.6, bf16[2048,2048]{1,0:T(8,128)(2,1)} %all-gather.2.cloned.1.call-done), kind=kOutput, calls=%fused_computation.15 | convolution fusion | flops 4298113024 | bytes 14680064 | tf_op jit(solution)/shard_map/dot_general | solution.py:57
  (14 shorter events, 0.6 us)
Async XLA Ops:
  6.5 128.5 %all-gather.2.cloned.1.call-start = ((), (), s32[]{:S(2)}) async-start(), calls=%async_computation | async-start | bytes 8912896 | tf_op jit(solution)/shard_map/all_gather | solution.py:59
  8.2 3.5 %collective-permute-start = (bf16[2,6144]{1,0:T(2,128)(2,1)S(1)}, bf16[2,6144]{1,0:T(2,128)(2,1)S(1)}, u32[]{:S(2)}, u32[]{:S(2)}) collective-permute-start(bf16[2,6144]{1,0:T(2,128)(2,1)S(1)} %slice.37), channel_id=1, source_target_pairs={{0,1},{1,2},{2,3},{3,4},{4,5},{5,6},{6,7},{7,8},{8,9},{9,10},{10,1... | collective-permute-start | bytes 73736 | tf_op jit(solution)/shard_map/ppermute | solution.py:10
  23.0 8.8 %copy-start = (bf16[128,128]{1,0:T(8,128)(2,1)S(1)}, bf16[128,128]{1,0:T(8,128)(2,1)}, u32[]{:S(2)}) copy-start(bf16[128,128]{1,0:T(8,128)(2,1)} %param.11) | copy-start | bytes 98308
  27.2 58.6 %collective-permute-start.1 = (bf16[127,2048]{1,0:T(8,128)(2,1)S(1)}, bf16[127,2048]{1,0:T(8,128)(2,1)S(1)}, u32[]{:S(2)}, u32[]{:S(2)}) collective-permute-start(bf16[127,2048]{1,0:T(8,128)(2,1)S(1)} %slice.54), channel_id=1, source_target_pairs={{0,1},{1,2},{2,3},{3,4},{4,5},{5,6},{6,7},{7,8},{8,9},{9,10},{10,1... | collective-permute-start | bytes 1560584 | tf_op jit(solution)/shard_map/ppermute | solution.py:10
  92.3 34.9 %copy-start.1 = (f32[2048]{0:T(1024)S(1)}, f32[2048]{0:T(1024)}, u32[]{:S(2)}) copy-start(f32[2048]{0:T(1024)} %param.12) | copy-start | bytes 24580
Sparse Core Ops, SparseCore 0:
  9.5 82.3 all-gather.1
where the time goes:
time: 153 us; the launch traced here: 151 us
  local copies, waits for them, and re-layouts  68.6 us (45%)
  matrix products  33.9 us (22%)
  other arithmetic  25.2 us (16%)
  between operations  13.5 us (9%)
  starting transfers between devices  6.93 us (5%)
  loops' own time  2.32 us (2%)
    reshape x1, local copies, waits for them, and re-layouts, long_conv(): jnp.tile(pattern, (1, block))[:, :block * span]  29.5 us
    dot_general x4, matrix products, one_block(): jnp.einsum('gts,sgc->tgc', toeplitz, window, preferred_element_type=jnp.f...  24.5 us
    unnamed x5, local copies, waits for them, and re-layouts  12.4 us
    dot_general x1, matrix products, on_device(): jnp.dot(gated, lax.all_gather(out_weight, 'ctx', axis=1, tiled=True), pre...  9.39 us
    slice x1, local copies, waits for them, and re-layouts, long_conv(): jnp.tile(pattern, (1, block))[:, :block * span]  8.12 us
    convert_element_type x1, other arithmetic, on_device(): (gate_rows * (conv + conv_bias * carried.astype(jnp.float32))).astype(jnp...  7.81 us
    ppermute x2, starting transfers between devices, shifted(): return lax.ppermute(block, axis, route)  6.93 us
    add x1, other arithmetic, short_mixed(): return total + short_filter[2] * source[0:row_count]  6.62 us
  transfers between devices with their start and end apart: 3, of which 0 were waited for; matrix products, arithmetic and copies ran while one was open for 78% of the time, Pallas kernels for 0%

commit v1 on v0

v1 whole, which is shorter than its diff:
```python
import jax
import jax.numpy as jnp
from jax import lax
from jax.sharding import Mesh
from jax.sharding import PartitionSpec as P

CTX = ("chip", "core")


def split_mesh(mesh):
    groups, ctx = mesh.devices.shape
    return Mesh(mesh.devices.reshape(groups, ctx // 2, 2), ("groups",) + CTX)


def shifted(block, distance):
    devices = range(lax.axis_size(CTX))
    route = [(i - distance, i) for i in devices if i - distance in devices]
    return lax.ppermute(block, CTX, route)


def ring_order(chips):
    down = [2 * i for i in range(chips // 2)]
    up = [2 * i + 1 for i in reversed(range(chips // 2))]
    return down + up


def short_mixed(padded, short_filter, row_count):
    source = padded.astype(jnp.float32)
    total = short_filter[0] * source[2 : 2 + row_count]
    total = total + short_filter[1] * source[1 : 1 + row_count]
    return total + short_filter[2] * source[0:row_count]


def long_conv(extended, long_filter, group, row_count):
    tap_count = long_filter.shape[1]
    taps = jnp.repeat(long_filter[:, ::-1].T, group, axis=1)[:, None, :]
    source = extended[extended.shape[0] - row_count - tap_count + 1 :]
    conv = lax.conv_general_dilated(
        source[None],
        taps,
        window_strides=(1,),
        padding="VALID",
        dimension_numbers=("NWC", "WIO", "NWC"),
        feature_group_count=source.shape[1],
        preferred_element_type=jnp.float32,
    )
    return conv[0]


def on_device(tokens, projected, short_filter, long_filter, conv_bias, out_weight):
    row_count = tokens.shape[0]
    channels = out_weight.shape[0]
    group = channels // long_filter.shape[0]
    chips = lax.axis_size("chip")
    width = out_weight.shape[1]

    edge_rows = shifted(projected[row_count - 2 :], 1)
    mixed = short_mixed(jnp.concatenate([edge_rows, projected], axis=0), short_filter, row_count)
    gate_rows = mixed[:, :channels]
    carried = (mixed[:, channels : 2 * channels] * mixed[:, 2 * channels :]).astype(jnp.bfloat16)
    halo = shifted(carried[row_count - 128 :], 1)
    conv = long_conv(jnp.concatenate([halo, carried], axis=0), long_filter, group, row_count)
    gated = (gate_rows * (conv + conv_bias * carried.astype(jnp.float32))).astype(jnp.bfloat16)

    chip = lax.axis_index("chip")
    core = lax.axis_index("core")
    order = ring_order(chips)
    where = [0] * chips
    for position, c in enumerate(order):
        where[c] = position
    order_arr = jnp.array(order, jnp.int32)
    position = jnp.array(where, jnp.int32)[chip]
    forward = [(order[i], order[(i + 1) % chips]) for i in range(chips)]
    backward = [(order[(i + 1) % chips], order[i]) for i in range(chips)]

    result = tokens

    def emit(result, piece, owner_chip, owner_core, start, size):
        column = (owner_chip * 2 + owner_core) * width + start
        rows = lax.dynamic_slice_in_dim(tokens, column, size, 1).astype(jnp.float32)
        out = rows + jnp.dot(gated, piece, preferred_element_type=jnp.float32)
        return lax.dynamic_update_slice_in_dim(result, out.astype(jnp.bfloat16), column, 1)

    def emit_both(result, piece, owner_chip, start=0):
        size = piece.shape[1]
        result = emit(result, piece, owner_chip, core, start, size)
        other = lax.ppermute(piece, "core", [(0, 1), (1, 0)])
        return emit(result, other, owner_chip, 1 - core, start, size)

    result = emit_both(result, out_weight, chip)
    ahead = behind = out_weight
    steps = chips // 2
    for step in range(1, steps + 1):
        last = step == steps and chips % 2 == 0
        if last:
            half = width // 2
            ahead = lax.ppermute(ahead[:, :half], "chip", forward)
            behind = lax.ppermute(behind[:, half:], "chip", backward)
            source = order_arr[(position - step) % chips]
            result = emit_both(result, ahead, source, 0)
            result = emit_both(result, behind, source, half)
        else:
            ahead = lax.ppermute(ahead, "chip", forward)
            behind = lax.ppermute(behind, "chip", backward)
            result = emit_both(result, ahead, order_arr[(position - step) % chips])
            if step < steps or chips % 2:
                result = emit_both(result, behind, order_arr[(position + step) % chips])
    return result


def solution(mesh):
    inner = split_mesh(mesh)
    rows = P(("groups",) + CTX, None)
    placed = (rows, rows, P(), P(), P(), P(None, CTX))
    return jax.shard_map(on_device, mesh=inner, in_specs=placed, out_specs=rows, check_vma=False)
```

time: 153 us -> 186 us (1.22)
  matrix products: 33.9 us -> 96.4 us
  local copies, waits for them, and re-layouts: 68.6 us -> 25.6 us
  starting transfers between devices: 6.93 us -> 24.5 us
  waiting for transfers between devices: 0.74 us -> 10.8 us
  other arithmetic: 25.2 us -> 18.4 us
  between operations: 13.5 us -> 9.41 us
  loops' own time: 2.32 us -> 0 us
    conv_general_dilated x0 -> x1, matrix products: none -> 62.4 us  [long_conv(): lax.conv_general_dilated(source[None], taps, window_strides=(1,), padding...]
    reshape x1 -> x0, local copies, waits for them, and re-layouts: 29.5 us -> none  [long_conv(): jnp.tile(pattern, (1, block))[:, :block * span]]
    ppermute x2 -> x19, starting transfers between devices: 6.93 us -> 24.5 us  [the longest x2 10.7 us: shifted(): return lax.ppermute(block, CTX, route)]
    ppermute x2 -> x19, waiting for transfers between devices: 0.01 us -> 10.8 us  [the longest x3 6.21 us: on_device(): behind = lax.ppermute(behind, 'chip', backward)]
    slice x3, local copies, waits for them, and re-layouts: 9.17 us -> 1.96 us  [the longest x1 0.92 us: on_device(): edge_rows = shifted(projected[row_count - 2:], 1)]
    unnamed x5 -> x31, local copies, waits for them, and re-layouts: 12.4 us -> 6.9 us
    convert_element_type x1, other arithmetic: 7.81 us -> 2.55 us  [on_device(): (gate_rows * (conv + conv_bias * carried.astype(jnp.float32))).astype(jnp...]
    concatenate x2 -> x0, local copies, waits for them, and re-layouts: 4.46 us -> none  [the longest x1 4.45 us: on_device(): extended = jnp.concatenate([carried_edge, carried], axis=0)]
  transfers between devices with their start and end apart: 3 -> 19, of which waited for: 0 -> 2; matrix products, arithmetic and copies ran while one was open for 78% -> 70% of each run, Pallas kernels for 0% -> 0%
where the time goes in v1:
time: 186 us; the launch traced here: 185 us
  matrix products  96.4 us (52%)
  local copies, waits for them, and re-layouts  25.6 us (14%)
  starting transfers between devices  24.5 us (13%)
  other arithmetic  18.4 us (10%)
  waiting for transfers between devices  10.8 us (6%)
  between operations  9.41 us (5%)
    conv_general_dilated x1, matrix products, long_conv(): lax.conv_general_dilated(source[None], taps, window_strides=(1,), padding...  62.4 us
    dot_general x18, matrix products, emit(): out = rows + jnp.dot(gated, piece, preferred_element_type=jnp.float32)  34.1 us
    ppermute x2, starting transfers between devices, shifted(): return lax.ppermute(block, CTX, route)  10.7 us
    dynamic_update_slice x4, local copies, waits for them, and re-layouts, emit(): lax.dynamic_update_slice_in_dim(result, out.astype(jnp.bfloat16), column, 1)  7.4 us
    unnamed x31, local copies, waits for them, and re-layouts  6.9 us
    add x1, other arithmetic, short_mixed(): return total + short_filter[2] * source[0:row_count]  6.46 us
    ppermute x3, starting transfers between devices, on_device(): behind = lax.ppermute(behind, 'chip', backward)  6.28 us
    ppermute x3, waiting for transfers between devices, on_device(): behind = lax.ppermute(behind, 'chip', backward)  6.21 us
  transfers between devices with their start and end apart: 19, of which 2 were waited for; matrix products, arithmetic and copies ran while one was open for 70% of the time, Pallas kernels for 0%

profile of v1, /device:TPU:0, one launch (start us, length us, event | category | flops | bytes accessed | tf_op | source)
XLA Modules:
  0.0 185.2 jit_solution(17979933517322670792)
XLA Ops:
  0.0 3.0 %collective-permute-start.5 = (bf16[2048,128]{1,0:T(8,128)(2,1)}, bf16[2048,128]{1,0:T(8,128)(2,1)}, u32[]{:S(2)}, u32[]{:S(2)}) collective-permute-start(bf16[2048,128]{1,0:T(8,128)(2,1)} %param.13), channel_id=1, source_target_pairs={{4,0},{8,4},{12,8},{14,12},{10,14},{6,10},{2,6},{0,2},{5,1},{9,5},... | collective-permute-start | bytes 1572872 | tf_op jit(solution)/shard_map/ppermute | solution.py:104
  4.0 1.5 collective-permute-start
  6.5 4.7 %maximum_convert_fusion = f32[514,6144]{1,0:T(8,128)S(1)} fusion(bf16[512,6144]{1,0:T(8,128)(2,1)} %param.9, bf16[2,6144]{1,0:T(2,128)(2,1)S(1)} %collective-permute-done), kind=kLoop, calls=%fused_computation.5 | loop fusion | flops 12632064 | bytes 18948096 | tf_op jit(solution)/shard_map/convert_element_type | solution.py:28
  11.2 6.5 %fusion = f32[512,6144]{1,0:T(8,128)} fusion(f32[514,6144]{1,0:T(8,128)S(1)} %maximum_convert_fusion, f32[6144]{0:T(1024)S(1)} %bitcast.68, f32[6144]{0:T(1024)S(1)} %bitcast.69, f32[6144]{0:T(1024)S(1)} %bitcast.67), kind=kLoop, calls=%fused_computation.1 | loop fusion | flops 15728640 | bytes 50405376 | tf_op jit(solution)/shard_map/add | solution.py:31
  17.7 4.1 %fusion.4 = bf16[512,2048]{1,0:T(8,128)(2,1)S(1)} fusion(f32[512,6144]{1,0:T(8,128)} %fusion), kind=kLoop, calls=%fused_computation.9 | loop fusion | flops 2097152 | bytes 10485760 | tf_op jit(solution)/shard_map/convert_element_type | solution.py:60
  22.6 9.2 %collective-permute-start.1 = (bf16[128,2048]{1,0:T(8,128)(2,1)}, bf16[128,2048]{1,0:T(8,128)(2,1)S(1)}, u32[]{:S(2)}, u32[]{:S(2)}) collective-permute-start(bf16[128,2048]{1,0:T(8,128)(2,1)} %slice.62), channel_id=1, source_target_pairs={{0,1},{1,2},{2,3},{3,4},{4,5},{5,6},{6,7},{7,8},{8,9},{9,10},{10,1... | collective-permute-start | bytes 1572872 | tf_op jit(solution)/shard_map/ppermute | solution.py:18
  31.9 2.5 %collective-permute-start.2 = (bf16[2048,128]{1,0:T(8,128)(2,1)}, bf16[2048,128]{1,0:T(8,128)(2,1)}, u32[]{:S(2)}, u32[]{:S(2)}) collective-permute-start(bf16[2048,128]{1,0:T(8,128)(2,1)} %param.13), channel_id=1, source_target_pairs={{0,1},{1,0},{2,3},{3,2},{4,5},{5,4},{6,7},{7,6},{8,9},{9,8},{10,11... | collective-permute-start | bytes 1572872 | tf_op jit(solution)/shard_map/ppermute | solution.py:87
  44.8 3.2 %copy.36 = bf16[512,2048]{1,0:T(8,128)(2,1)} copy(bf16[512,2048]{1,0:T(8,128)(2,1)} %param.8) | data formatting | bytes 4194304
  51.5 2.0 %copy.19 = bf16[128,1,2048]{2,1,0:T(2,128)(2,1)} copy(bf16[128,1,2048]{0,2,1:T(8,128)(2,1)S(1)} %bitcast.65) | data formatting | bytes 1048576 | tf_op jit(solution)/shard_map/broadcast_in_dim;reshape | solution.py:36
  56.9 1.7 collective-permute-start.9
  59.2 62.4 %fusion.2 = f32[1,512,2048]{2,0,1:T(1,128)S(1)} fusion(bf16[128,1,2048]{2,1,0:T(2,128)(2,1)S(1)} %copy-done.1, bf16[1,639,2048]{2,1,0:T(8,128)(2,1)S(1)} %fusion.6), kind=kOutput, calls=%fused_computation.6 | convolution fusion | flops 268435456 | bytes 7335936 | tf_op jit(solution)/shard_map/conv_general_dilated | solution.py:38
  121.6 2.5 %fusion.5 = bf16[512,2048]{1,0:T(8,128)(2,1)S(1)} fusion(f32[512,6144]{1,0:T(8,128)S(1)} %bitcast.64, f32[1,512,2048]{2,0,1:T(1,128)S(1)} %fusion.2, f32[2048]{0:T(1024)S(1)} %copy-done.8), kind=kLoop, calls=%fused_computation.11 | loop fusion | flops 7340032 | bytes 18882560 | tf_op jit(solution)/shard_map/convert_element_type | solution.py:63
  124.2 2.6 %fusion.8 = bf16[512,2048]{1,0:T(8,128)(2,1)} fusion(bf16[512,2048]{1,0:T(8,128)(2,1)} %copy.36, s32[]{:T(128)S(6)} %select_n.127, bf16[512,2048]{1,0:T(8,128)(2,1)S(1)} %fusion.5, bf16[2048,128]{1,0:T(8,128)(2,1)} %param.13), kind=kOutput, calls=%fused_computation.30 | convolution fusion | flops 268632064 | bytes 2883588 | tf_op jit(solution)/shard_map/dot_general | solution.py:81
  126.8 2.4 %fusion.10 = bf16[512,2048]{1,0:T(8,128)(2,1)} fusion(bf16[512,2048]{1,0:T(8,128)(2,1)} %fusion.8, s32[]{:T(128)S(6)} %select_n.128, bf16[512,2048]{1,0:T(8,128)(2,1)S(1)} %fusion.5, bf16[2048,128]{1,0:T(8,128)(2,1)} %collective-permute-done.2, bf16[512,2048]{1,0:T(8,128)(2,1)S(1)} %copy-done), kind=kOutput, calls=%fused_computation.32 | convolution fusion | flops 268632064 | bytes 2883588 | tf_op jit(solution)/shard_map/dot_general | solution.py:81
  129.2 2.4 %fusion.12 = bf16[512,2048]{1,0:T(8,128)(2,1)} fusion(bf16[512,2048]{1,0:T(8,128)(2,1)} %fusion.10, s32[]{:T(128)S(6)} %select_n.132, bf16[512,2048]{1,0:T(8,128)(2,1)S(1)} %fusion.5, bf16[2048,128]{1,0:T(8,128)(2,1)} %collective-permute-done.3, bf16[512,2048]{1,0:T(8,128)(2,1)S(1)} %copy-done), kind=kOutput, calls=%fused_computation.34 | convolution fusion | flops 268632064 | bytes 2883588 | tf_op jit(solution)/shard_map/dot_general | solution.py:81
  132.2 1.7 collective-permute-start.13
  135.3 2.4 %fusion.16 = bf16[512,2048]{1,0:T(8,128)(2,1)} fusion(bf16[512,2048]{1,0:T(8,128)(2,1)} %fusion.14, s32[]{:T(128)S(6)} %select_n.136, bf16[512,2048]{1,0:T(8,128)(2,1)S(1)} %fusion.5, bf16[2048,128]{1,0:T(8,128)(2,1)} %collective-permute-done.5, bf16[512,2048]{1,0:T(8,128)(2,1)S(1)} %copy-done), kind=kOutput, calls=%fused_computation.38 | convolution fusion | flops 268632064 | bytes 2883588 | tf_op jit(solution)/shard_map/dot_general | solution.py:81
  139.1 1.4 fusion.20
  140.4 6.2 %collective-permute-done.13 = bf16[2048,128]{1,0:T(8,128)(2,1)S(1)} collective-permute-done((bf16[2048,128]{1,0:T(8,128)(2,1)S(1)}, bf16[2048,128]{1,0:T(8,128)(2,1)S(1)}, u32[]{:S(2)}, u32[]{:S(2)}) %collective-permute-start.13) | collective-permute-done | bytes 524320 | tf_op jit(solution)/shard_map/ppermute | solution.py:104
  146.9 1.4 collective-permute-start.17
  153.6 2.4 %fusion.28 = bf16[512,2048]{1,0:T(8,128)(2,1)} fusion(bf16[512,2048]{1,0:T(8,128)(2,1)} %fusion.26, s32[]{:T(128)S(6)} %select_n.148, bf16[512,2048]{1,0:T(8,128)(2,1)S(1)} %fusion.5, bf16[2048,128]{1,0:T(8,128)(2,1)} %collective-permute-done.11, bf16[512,2048]{1,0:T(8,128)(2,1)S(1)} %copy-done), kind=kOutput, calls=%fused_computation.50 | convolution fusion | flops 268632064 | bytes 2883588 | tf_op jit(solution)/shard_map/dot_general | solution.py:81
  156.0 4.5 %collective-permute-done.17 = bf16[2048,64]{1,0:T(8,128)(2,1)S(1)} collective-permute-done((bf16[2048,64]{1,0:T(8,128)(2,1)S(1)}, bf16[2048,64]{1,0:T(8,128)(2,1)S(1)}, u32[]{:S(2)}, u32[]{:S(2)}) %collective-permute-start.17) | collective-permute-done | bytes 262176 | tf_op jit(solution)/shard_map/ppermute | solution.py:98
  162.4 1.4 fusion.35
  165.3 2.4 %fusion.38 = bf16[512,64]{0,1:T(8,128)(2,1)} fusion(bf16[512,2048]{1,0:T(8,128)(2,1)S(1)} %fusion.5, bf16[2048,64]{1,0:T(8,128)(2,1)} %collective-permute-done.18, bf16[512,64]{0,1:T(8,128)(2,1)S(1)} %copy-done.3), kind=kOutput, calls=%fused_computation.64 | convolution fusion | flops 134316032 | bytes 2490368 | tf_op jit(solution)/shard_map/dot_general | solution.py:81
  168.7 1.8 fusion.36
  170.6 2.4 %fusion.30 = bf16[512,2048]{1,0:T(8,128)(2,1)} fusion(bf16[512,2048]{1,0:T(8,128)(2,1)} %fusion.28, s32[]{:T(128)S(6)} %select_n.149, bf16[512,2048]{1,0:T(8,128)(2,1)S(1)} %fusion.5, bf16[2048,128]{1,0:T(8,128)(2,1)} %collective-permute-done.12, bf16[512,2048]{1,0:T(8,128)(2,1)} %param.8), kind=kOutput, calls=%fused_computation.52 | convolution fusion | flops 268632064 | bytes 2883588 | tf_op jit(solution)/shard_map/dot_general | solution.py:81
  173.0 2.3 %fusion.32 = bf16[512,2048]{1,0:T(8,128)(2,1)} fusion(bf16[512,2048]{1,0:T(8,128)(2,1)} %fusion.30, s32[]{:T(128)S(6)} %select_n.152, bf16[512,2048]{1,0:T(8,128)(2,1)S(1)} %fusion.5, bf16[2048,128]{1,0:T(8,128)(2,1)S(1)} %collective-permute-done.13, bf16[512,2048]{1,0:T(8,128)(2,1)} %param.8), kind=kOutput, calls=%fused_computation.54 | convolution fusion | flops 268632064 | bytes 2883588 | tf_op jit(solution)/shard_map/dot_general | solution.py:81
  175.3 2.4 %fusion.34 = bf16[512,2048]{1,0:T(8,128)(2,1)} fusion(bf16[512,2048]{1,0:T(8,128)(2,1)} %fusion.32, s32[]{:T(128)S(6)} %select_n.153, bf16[512,2048]{1,0:T(8,128)(2,1)S(1)} %fusion.5, bf16[2048,128]{1,0:T(8,128)(2,1)} %collective-permute-done.14, bf16[512,2048]{1,0:T(8,128)(2,1)} %param.8), kind=kOutput, calls=%fused_computation.56 | convolution fusion | flops 268632064 | bytes 2883588 | tf_op jit(solution)/shard_map/dot_general | solution.py:81
  177.8 1.7 dynamic_update_slice.68
  179.5 1.6 dynamic_update_slice.69
  181.1 2.2 %dynamic_update_slice.70 = bf16[512,2048]{1,0:T(8,128)(2,1)} dynamic-update-slice(bf16[512,2048]{1,0:T(8,128)(2,1)} %dynamic_update_slice.69, bf16[512,64]{1,0:T(8,128)(2,1)S(1)} %copy.25, s32[]{:T(128)} %constant.74.clone.1, s32[]{:T(128)S(6)} %select_n.158) | dynamic-update-slice | bytes 131076 | tf_op jit(solution)/shard_map/dynamic_update_slice | solution.py:82
  183.3 1.9 %dynamic_update_slice.71 = bf16[512,2048]{1,0:T(8,128)(2,1)} dynamic-update-slice(bf16[512,2048]{1,0:T(8,128)(2,1)} %dynamic_update_slice.70, bf16[512,64]{1,0:T(8,128)(2,1)S(1)} %copy.27, s32[]{:T(128)} %constant.74.clone.1, s32[]{:T(128)S(6)} %select_n.159) | dynamic-update-slice | bytes 131076 | tf_op jit(solution)/shard_map/dynamic_update_slice | solution.py:82
  (80 shorter events, 25.0 us)
Async XLA Ops:
  0.0 56.9 %collective-permute-start.5 = (bf16[2048,128]{1,0:T(8,128)(2,1)}, bf16[2048,128]{1,0:T(8,128)(2,1)}, u32[]{:S(2)}, u32[]{:S(2)}) collective-permute-start(bf16[2048,128]{1,0:T(8,128)(2,1)} %param.13), channel_id=1, source_target_pairs={{4,0},{8,4},{12,8},{14,12},{10,14},{6,10},{2,6},{0,2},{5,1},{9,5},... | collective-permute-start | bytes 1572872 | tf_op jit(solution)/shard_map/ppermute | solution.py:104
  3.0 52.7 %collective-permute-start.3 = (bf16[2048,128]{1,0:T(8,128)(2,1)}, bf16[2048,128]{1,0:T(8,128)(2,1)}, u32[]{:S(2)}, u32[]{:S(2)}) collective-permute-start(bf16[2048,128]{1,0:T(8,128)(2,1)} %param.13), channel_id=1, source_target_pairs={{0,4},{4,8},{8,12},{12,14},{14,10},{10,6},{6,2},{2,0},{1,5},{5,9},... | collective-permute-start | bytes 1572872 | tf_op jit(solution)/shard_map/ppermute | solution.py:103
  4.0 2.6 %collective-permute-start = (bf16[2,6144]{1,0:T(2,128)(2,1)S(1)}, bf16[2,6144]{1,0:T(2,128)(2,1)S(1)}, u32[]{:S(2)}, u32[]{:S(2)}) collective-permute-start(bf16[2,6144]{1,0:T(2,128)(2,1)S(1)} %slice.43), channel_id=1, source_target_pairs={{0,1},{1,2},{2,3},{3,4},{4,5},{5,6},{6,7},{7,8},{8,9},{9,10},{10,1... | collective-permute-start | bytes 73736 | tf_op jit(solution)/shard_map/ppermute | solution.py:18
  17.7 16.7 %copy-start.9 = (s32[8]{0:T(128)S(1)}, s32[8]{0:T(128)}, u32[]{:S(2)}) copy-start(s32[8]{0:T(128)} %constant.93.clone) | copy-start | bytes 100
  17.7 22.0 %copy-start.7 = (s32[8]{0:T(128)S(1)}, s32[8]{0:T(128)}, u32[]{:S(2)}) copy-start(s32[8]{0:T(128)} %constant.92.clone) | copy-start | bytes 100
  22.6 35.9 %collective-permute-start.1 = (bf16[128,2048]{1,0:T(8,128)(2,1)}, bf16[128,2048]{1,0:T(8,128)(2,1)S(1)}, u32[]{:S(2)}, u32[]{:S(2)}) collective-permute-start(bf16[128,2048]{1,0:T(8,128)(2,1)} %slice.62), channel_id=1, source_target_pairs={{0,1},{1,2},{2,3},{3,4},{4,5},{5,6},{6,7},{7,8},{8,9},{9,10},{10,1... | collective-permute-start | bytes 1572872 | tf_op jit(solution)/shard_map/ppermute | solution.py:18
  31.9 94.9 %collective-permute-start.2 = (bf16[2048,128]{1,0:T(8,128)(2,1)}, bf16[2048,128]{1,0:T(8,128)(2,1)}, u32[]{:S(2)}, u32[]{:S(2)}) collective-permute-start(bf16[2048,128]{1,0:T(8,128)(2,1)} %param.13), channel_id=1, source_target_pairs={{0,1},{1,0},{2,3},{3,2},{4,5},{5,4},{6,7},{7,6},{8,9},{9,8},{10,11... | collective-permute-start | bytes 1572872 | tf_op jit(solution)/shard_map/ppermute | solution.py:87
  44.8 5.2 %copy-start.6 = (bf16[128,128]{1,0:T(8,128)(2,1)S(1)}, bf16[128,128]{1,0:T(8,128)(2,1)}, u32[]{:S(2)}) copy-start(bf16[128,128]{1,0:T(8,128)(2,1)} %param.11) | copy-start | bytes 98308
  55.7 3.5 %copy-start.1 = (bf16[128,1,2048]{2,1,0:T(2,128)(2,1)S(1)}, bf16[128,1,2048]{2,1,0:T(2,128)(2,1)}, u32[]{:S(2)}) copy-start(bf16[128,1,2048]{2,1,0:T(2,128)(2,1)} %copy.19) | copy-start | bytes 1572868
  55.7 75.9 %collective-permute-start.7 = (bf16[2048,128]{1,0:T(8,128)(2,1)}, bf16[2048,128]{1,0:T(8,128)(2,1)S(1)}, u32[]{:S(2)}, u32[]{:S(2)}) collective-permute-start(bf16[2048,128]{1,0:T(8,128)(2,1)} %collective-permute-done.3), channel_id=1, source_target_pairs={{0,4},{4,8},{8,12},{12,14},{14,10},{10,6},{6,2},{2,0},{1,5},{5,9},... | collective-permute-start | bytes 1572872 | tf_op jit(solution)/shard_map/ppermute | solution.py:103
  56.7 77.2 %collective-permute-start.4 = (bf16[2048,128]{1,0:T(8,128)(2,1)}, bf16[2048,128]{1,0:T(8,128)(2,1)S(1)}, u32[]{:S(2)}, u32[]{:S(2)}) collective-permute-start(bf16[2048,128]{1,0:T(8,128)(2,1)} %collective-permute-done.3), channel_id=1, source_target_pairs={{0,1},{1,0},{2,3},{3,2},{4,5},{5,4},{6,7},{7,6},{8,9},{9,8},{10,11... | collective-permute-start | bytes 1572872 | tf_op jit(solution)/shard_map/ppermute | solution.py:87
  56.9 75.4 %collective-permute-start.9 = (bf16[2048,128]{1,0:T(8,128)(2,1)}, bf16[2048,128]{1,0:T(8,128)(2,1)S(1)}, u32[]{:S(2)}, u32[]{:S(2)}) collective-permute-start(bf16[2048,128]{1,0:T(8,128)(2,1)} %collective-permute-done.5), channel_id=1, source_target_pairs={{4,0},{8,4},{12,8},{14,12},{10,14},{6,10},{2,6},{0,2},{5,1},{9,5},... | collective-permute-start | bytes 1572872 | tf_op jit(solution)/shard_map/ppermute | solution.py:104
  58.5 79.2 %collective-permute-start.6 = (bf16[2048,128]{1,0:T(8,128)(2,1)}, bf16[2048,128]{1,0:T(8,128)(2,1)S(1)}, u32[]{:S(2)}, u32[]{:S(2)}) collective-permute-start(bf16[2048,128]{1,0:T(8,128)(2,1)} %collective-permute-done.5), channel_id=1, source_target_pairs={{0,1},{1,0},{2,3},{3,2},{4,5},{5,4},{6,7},{7,6},{8,9},{9,8},{10,11... | collective-permute-start | bytes 1572872 | tf_op jit(solution)/shard_map/ppermute | solution.py:87
  58.5 63.1 %slice-start = ((s8[12582912]{0:T(1024)(128)(4,1)}), s8[4194304]{0:T(1024)(128)(4,1)S(1)}, s32[]{:S(2)}) async-start(s8[12582912]{0:T(1024)(128)(4,1)} %bitcast.63), calls=%async_computation | async-start | bytes 8388608
  59.2 62.4 %slice-start.1 = ((s8[12582912]{0:T(1024)(128)(4,1)}), s8[4194304]{0:T(1024)(128)(4,1)S(1)}, s32[]{:S(2)}) async-start(s8[12582912]{0:T(1024)(128)(4,1)} %bitcast.63), calls=%async_computation.1 | async-start | bytes 8388608
  59.2 62.4 %slice-start.2 = ((s8[12582912]{0:T(1024)(128)(4,1)}), s8[4194304]{0:T(1024)(128)(4,1)S(1)}, s32[]{:S(2)}) async-start(s8[12582912]{0:T(1024)(128)(4,1)} %bitcast.63), calls=%async_computation.2 | async-start | bytes 8388608
  59.2 62.4 %copy-start.8 = (f32[2048]{0:T(1024)S(1)}, f32[2048]{0:T(1024)}, u32[]{:S(2)}) copy-start(f32[2048]{0:T(1024)} %param.12) | copy-start | bytes 24580
  124.2 2.6 %copy-start = (bf16[512,2048]{1,0:T(8,128)(2,1)S(1)}, bf16[512,2048]{1,0:T(8,128)(2,1)}, u32[]{:S(2)}) copy-start(bf16[512,2048]{1,0:T(8,128)(2,1)} %param.8) | copy-start | bytes 6291460
  131.6 16.6 %collective-permute-start.11 = (bf16[2048,128]{1,0:T(8,128)(2,1)S(1)}, bf16[2048,128]{1,0:T(8,128)(2,1)}, u32[]{:S(2)}, u32[]{:S(2)}) collective-permute-start(bf16[2048,128]{1,0:T(8,128)(2,1)S(1)} %collective-permute-done.7), channel_id=1, source_target_pairs={{0,4},{4,8},{8,12},{12,14},{14,10},{10,6},{6,2},{2,0},{1,5},{5,9},... | collective-permute-start | bytes 1572872 | tf_op jit(solution)/shard_map/ppermute | solution.py:103
  132.0 16.9 %collective-permute-start.8 = (bf16[2048,128]{1,0:T(8,128)(2,1)S(1)}, bf16[2048,128]{1,0:T(8,128)(2,1)S(1)}, u32[]{:S(2)}, u32[]{:S(2)}) collective-permute-start(bf16[2048,128]{1,0:T(8,128)(2,1)S(1)} %collective-permute-done.7), channel_id=1, source_target_pairs={{0,1},{1,0},{2,3},{3,2},{4,5},{5,4},{6,7},{7,6},{8,9},{9,8},{10,11... | collective-permute-start | bytes 1572872 | tf_op jit(solution)/shard_map/ppermute | solution.py:87
  132.2 14.4 %collective-permute-start.13 = (bf16[2048,128]{1,0:T(8,128)(2,1)S(1)}, bf16[2048,128]{1,0:T(8,128)(2,1)S(1)}, u32[]{:S(2)}, u32[]{:S(2)}) collective-permute-start(bf16[2048,128]{1,0:T(8,128)(2,1)S(1)} %collective-permute-done.9), channel_id=1, source_target_pairs={{4,0},{8,4},{12,8},{14,12},{10,14},{6,10},{2,6},{0,2},{5,1},{9,5},... | collective-permute-start | bytes 1572872 | tf_op jit(solution)/shard_map/ppermute | solution.py:104
  133.9 18.3 %collective-permute-start.10 = (bf16[2048,128]{1,0:T(8,128)(2,1)S(1)}, bf16[2048,128]{1,0:T(8,128)(2,1)S(1)}, u32[]{:S(2)}, u32[]{:S(2)}) collective-permute-start(bf16[2048,128]{1,0:T(8,128)(2,1)S(1)} %collective-permute-done.9), channel_id=1, source_target_pairs={{0,1},{1,0},{2,3},{3,2},{4,5},{5,4},{6,7},{7,6},{8,9},{9,8},{10,11... | collective-permute-start | bytes 1572872 | tf_op jit(solution)/shard_map/ppermute | solution.py:87
  146.9 13.7 %collective-permute-start.17 = (bf16[2048,64]{1,0:T(8,128)(2,1)S(1)}, bf16[2048,64]{1,0:T(8,128)(2,1)S(1)}, u32[]{:S(2)}, u32[]{:S(2)}) collective-permute-start(bf16[2048,64]{1,0:T(8,128)(2,1)S(1)} %slice.64), channel_id=1, source_target_pairs={{4,0},{8,4},{12,8},{14,12},{10,14},{6,10},{2,6},{0,2},{5,1},{9,5},... | collective-permute-start | bytes 786440 | tf_op jit(solution)/shard_map/ppermute | solution.py:98
  148.3 14.1 %collective-permute-start.15 = (bf16[2048,64]{1,0:T(8,128)(2,1)}, bf16[2048,64]{1,0:T(8,128)(2,1)S(1)}, u32[]{:S(2)}, u32[]{:S(2)}) collective-permute-start(bf16[2048,64]{1,0:T(8,128)(2,1)} %bitcast.62), channel_id=1, source_target_pairs={{0,4},{4,8},{8,12},{12,14},{14,10},{10,6},{6,2},{2,0},{1,5},{5,9},... | collective-permute-start | bytes 786440 | tf_op jit(solution)/shard_map/ppermute | solution.py:97
  148.9 21.6 %collective-permute-start.12 = (bf16[2048,128]{1,0:T(8,128)(2,1)}, bf16[2048,128]{1,0:T(8,128)(2,1)}, u32[]{:S(2)}, u32[]{:S(2)}) collective-permute-start(bf16[2048,128]{1,0:T(8,128)(2,1)} %collective-permute-done.11), channel_id=1, source_target_pairs={{0,1},{1,0},{2,3},{3,2},{4,5},{5,4},{6,7},{7,6},{8,9},{9,8},{10,11... | collective-permute-start | bytes 1572872 | tf_op jit(solution)/shard_map/ppermute | solution.py:87
  149.0 26.4 %collective-permute-start.14 = (bf16[2048,128]{1,0:T(8,128)(2,1)S(1)}, bf16[2048,128]{1,0:T(8,128)(2,1)}, u32[]{:S(2)}, u32[]{:S(2)}) collective-permute-start(bf16[2048,128]{1,0:T(8,128)(2,1)S(1)} %collective-permute-done.13), channel_id=1, source_target_pairs={{0,1},{1,0},{2,3},{3,2},{4,5},{5,4},{6,7},{7,6},{8,9},{9,8},{10,11... | collective-permute-start | bytes 1572872 | tf_op jit(solution)/shard_map/ppermute | solution.py:87
  153.6 7.8 %copy-start.5 = (bf16[512,64]{0,1:T(8,128)(2,1)S(1)}, bf16[512,64]{0,1:T(8,128)(2,1)}, u32[]{:S(2)}) copy-start(bf16[512,64]{0,1:T(8,128)(2,1)} %copy.31) | copy-start | bytes 196612
  156.0 6.3 %copy-start.4 = (bf16[512,64]{0,1:T(8,128)(2,1)S(1)}, bf16[512,64]{0,1:T(8,128)(2,1)}, u32[]{:S(2)}) copy-start(bf16[512,64]{0,1:T(8,128)(2,1)} %copy.29) | copy-start | bytes 196612
  160.6 0.8 copy-start.2
  162.1 3.1 %copy-start.3 = (bf16[512,64]{0,1:T(8,128)(2,1)S(1)}, bf16[512,64]{0,1:T(8,128)(2,1)}, u32[]{:S(2)}) copy-start(bf16[512,64]{0,1:T(8,128)(2,1)} %copy.32) | copy-start | bytes 196612
  162.3 3.0 %collective-permute-start.18 = (bf16[2048,64]{1,0:T(8,128)(2,1)}, bf16[2048,64]{1,0:T(8,128)(2,1)}, u32[]{:S(2)}, u32[]{:S(2)}) collective-permute-start(bf16[2048,64]{1,0:T(8,128)(2,1)} %copy-done.2), channel_id=1, source_target_pairs={{0,1},{1,0},{2,3},{3,2},{4,5},{5,4},{6,7},{7,6},{8,9},{9,8},{10,11... | collective-permute-start | bytes 786440 | tf_op jit(solution)/shard_map/ppermute | solution.py:87
  164.7 3.9 %collective-permute-start.16 = (bf16[2048,64]{1,0:T(8,128)(2,1)S(1)}, bf16[2048,64]{1,0:T(8,128)(2,1)}, u32[]{:S(2)}, u32[]{:S(2)}) collective-permute-start(bf16[2048,64]{1,0:T(8,128)(2,1)S(1)} %collective-permute-done.15), channel_id=1, source_target_pairs={{0,1},{1,0},{2,3},{3,2},{4,5},{5,4},{6,7},{7,6},{8,9},{9,8},{10,11... | collective-permute-start | bytes 786440 | tf_op jit(solution)/shard_map/ppermute | solution.py:87

commit v2 on v1

v2 whole, which is shorter than its diff:
```python
import jax
import jax.numpy as jnp
from jax import lax
from jax.experimental import pallas as pl
from jax.experimental.pallas import tpu as pltpu
from jax.sharding import Mesh
from jax.sharding import PartitionSpec as P

CTX = ("chip", "core")
BLOCK = 128
LANES = 128


def split_mesh(mesh):
    groups, ctx = mesh.devices.shape
    return Mesh(mesh.devices.reshape(groups, ctx // 2, 2), ("groups",) + CTX)


def shifted(block, distance):
    devices = range(lax.axis_size(CTX))
    route = [(i - distance, i) for i in devices if i - distance in devices]
    return lax.ppermute(block, CTX, route)


def ring_order(chips):
    down = [2 * i for i in range(chips // 2)]
    up = [2 * i + 1 for i in reversed(range(chips // 2))]
    return down + up


def short_mixed(edge, rows, short_filter):
    previous = jnp.concatenate([edge[1:], rows[:-1]], axis=0).astype(jnp.float32)
    before = jnp.concatenate([edge, rows[:-2]], axis=0).astype(jnp.float32)
    total = short_filter[0] * rows.astype(jnp.float32)
    total = total + short_filter[1] * previous
    return total + short_filter[2] * before


def _gate_kernel(fw_ref, bias_ref, halo_ref, carried_ref, gate_ref, out_ref):
    lanes = carried_ref.shape[1]
    per_tile = fw_ref.shape[0]
    group = lanes // per_tile
    blocks = carried_ref.shape[0] // BLOCK
    owner = lax.broadcasted_iota(jnp.int32, (1, lanes), 1) // group
    toeplitz = []
    for i in range(per_tile):
        v = jnp.broadcast_to(fw_ref[i : i + 1, :], (BLOCK, fw_ref.shape[1]))
        rolled = pltpu.roll(v, 0, 1, stride=1, stride_axis=0)
        toeplitz.append(rolled[:, : 2 * BLOCK].astype(jnp.bfloat16))
    bias = bias_ref[...]
    for b in range(blocks):
        before = halo_ref[...] if b == 0 else carried_ref[BLOCK * (b - 1) : BLOCK * b, :]
        current = carried_ref[BLOCK * b : BLOCK * (b + 1), :]
        window = jnp.concatenate([before, current], axis=0)
        acc = jnp.zeros((BLOCK, lanes), jnp.float32)
        for i in range(per_tile):
            masked = jnp.where(owner == i, window, jnp.zeros_like(window))
            acc = acc + jnp.dot(toeplitz[i], masked, preferred_element_type=jnp.float32)
        gate = gate_ref[BLOCK * b : BLOCK * (b + 1), :]
        direct = bias * current.astype(jnp.float32)
        out_ref[BLOCK * b : BLOCK * (b + 1), :] = (gate * (acc + direct)).astype(out_ref.dtype)


def long_conv_gate(halo, carried, gate_rows, long_filter, conv_bias):
    groups, taps = long_filter.shape
    row_count, channels = carried.shape
    per_tile = LANES // (channels // groups)
    fw = jnp.zeros((groups, 3 * BLOCK), jnp.float32)
    fw = fw.at[:, 1 : 1 + taps].set(long_filter[:, ::-1].astype(jnp.float32))
    return pl.pallas_call(
        _gate_kernel,
        grid=(channels // LANES,),
        in_specs=[
            pl.BlockSpec((per_tile, 3 * BLOCK), lambda j: (j, 0)),
            pl.BlockSpec((1, LANES), lambda j: (0, j)),
            pl.BlockSpec((BLOCK, LANES), lambda j: (0, j)),
            pl.BlockSpec((row_count, LANES), lambda j: (0, j)),
            pl.BlockSpec((row_count, LANES), lambda j: (0, j)),
        ],
        out_specs=pl.BlockSpec((row_count, LANES), lambda j: (0, j)),
        out_shape=jax.ShapeDtypeStruct((row_count, channels), jnp.bfloat16),
    )(fw, conv_bias.reshape(1, channels), halo, carried, gate_rows)


def on_device(tokens, projected, short_filter, long_filter, conv_bias, out_weight):
    row_count = tokens.shape[0]
    channels = out_weight.shape[0]
    chips = lax.axis_size("chip")
    width = out_weight.shape[1]

    chip = lax.axis_index("chip")
    core = lax.axis_index("core")
    order = ring_order(chips)
    where = [0] * chips
    for place, c in enumerate(order):
        where[c] = place
    order_arr = jnp.array(order, jnp.int32)
    position = jnp.array(where, jnp.int32)[chip]
    forward = [(order[i], order[(i + 1) % chips]) for i in range(chips)]
    backward = [(order[(i + 1) % chips], order[i]) for i in range(chips)]
    swap = [(0, 1), (1, 0)]

    def with_partner(piece):
        other = lax.ppermute(piece, "core", swap)
        return (piece, other)

    steps = min(chips, 8) // 2
    ahead = behind = out_weight
    arrived = [(chip, 0, with_partner(out_weight))]

    def ring_step(step, ahead, behind):
        if step == steps and chips % 2 == 0:
            half = width // 2
            ahead = lax.ppermute(ahead[:, :half], "chip", forward)
            behind = lax.ppermute(behind[:, half:], "chip", backward)
            source = order_arr[(position - step) % chips]
            got = [(source, 0, with_partner(ahead)), (source, half, with_partner(behind))]
        else:
            ahead = lax.ppermute(ahead, "chip", forward)
            behind = lax.ppermute(behind, "chip", backward)
            got = [(order_arr[(position - step) % chips], 0, with_partner(ahead))]
            if step < steps or chips % 2:
                got.append((order_arr[(position + step) % chips], 0, with_partner(behind)))
        return ahead, behind, got

    ahead, behind, got = ring_step(1, ahead, behind)
    arrived += got

    edge = shifted(projected[row_count - 2 :], 1)
    mixed = short_mixed(edge, projected, short_filter)
    gate_rows = mixed[:, :channels]
    carried = (mixed[:, channels : 2 * channels] * mixed[:, 2 * channels :]).astype(jnp.bfloat16)
    halo = shifted(carried[row_count - BLOCK :], 1)

    carried, gate_rows, ahead, behind = lax.optimization_barrier((carried, gate_rows, ahead, behind))
    if steps >= 2:
        ahead, behind, got = ring_step(2, ahead, behind)
        arrived += got

    gated = long_conv_gate(halo, carried, gate_rows, long_filter, conv_bias)

    if chips > 8:
        weight = lax.all_gather(out_weight, CTX, axis=1, tiled=True)
        branch = jnp.dot(gated, weight, preferred_element_type=jnp.float32)
        return (tokens.astype(jnp.float32) + branch).astype(jnp.bfloat16)

    result = tokens
    done = 0

    def emit(result, owner_chip, start, pieces):
        mine, other = pieces
        size = mine.shape[1]
        both = jnp.concatenate([mine, other], axis=1)
        out = jnp.dot(gated, both, preferred_element_type=jnp.float32)
        for k, half in ((core, out[:, :size]), (1 - core, out[:, size:])):
            column = (owner_chip * 2 + k) * width + start
            rows = lax.dynamic_slice_in_dim(tokens, column, size, 1).astype(jnp.float32)
            piece = (rows + half).astype(jnp.bfloat16)
            result = lax.dynamic_update_slice_in_dim(result, piece, column, 1)
        return result

    for step in range(3, steps + 1):
        gated, ahead, behind = lax.optimization_barrier((gated, ahead, behind))
        ahead, behind, got = ring_step(step, ahead, behind)
        target = len(arrived)
        while done < target - 2:
            result = emit(result, *arrived[done])
            done += 1
        arrived += got
    while done < len(arrived):
        result = emit(result, *arrived[done])
        done += 1
    return result


def solution(mesh):
    inner = split_mesh(mesh)
    rows = P(("groups",) + CTX, None)
    placed = (rows, rows, P(), P(), P(), P(None, CTX))
    return jax.shard_map(on_device, mesh=inner, in_specs=placed, out_specs=rows, check_vma=False)
```

time: 186 us -> 124 us (0.67)
  matrix products: 96.4 us -> 16.7 us
  Pallas kernels: 0 us -> 17.3 us
  other arithmetic: 18.4 us -> 28.5 us
  local copies, waits for them, and re-layouts: 25.6 us -> 18.4 us
  waiting for transfers between devices: 10.8 us -> 8.26 us
    conv_general_dilated x1 -> x0, matrix products: 62.4 us -> none  [long_conv(): lax.conv_general_dilated(source[None], taps, window_strides=(1,), padding...]
    dot_general x18 -> x9, matrix products: 34.1 us -> 16.7 us  [emit(): out = jnp.dot(gated, both, preferred_element_type=jnp.float32)]
    pallas_call x0 -> x1, Pallas kernels: none -> 17.3 us  [long_conv_gate(): pl.pallas_call(_gate_kernel, grid=(channels // LANES,), in_specs=[pl.Bloc...]
    dynamic_update_slice x0 -> x14, other arithmetic: none -> 14.3 us  [emit(): result = lax.dynamic_update_slice_in_dim(result, piece, column, 1)]
    convert_element_type x3 -> x2, other arithmetic: 11.3 us -> 0.72 us  [emit(): piece = (rows + half).astype(jnp.bfloat16)]
    unnamed x31 -> x21, local copies, waits for them, and re-layouts: 6.9 us -> 3.9 us
    add x1, other arithmetic: 6.46 us -> 9.31 us  [short_mixed(): return total + short_filter[2] * before]
    slice x0 -> x1, other arithmetic: none -> 2.85 us  [on_device(): gate_rows = mixed[:, :channels]]
  transfers between devices with their start and end apart: 19 -> 19, of which waited for: 2 -> 3; matrix products, arithmetic and copies ran while one was open for 70% -> 41% of each run, Pallas kernels for 0% -> 14%
where the time goes in v2:
time: 124 us; the launch traced here: 123 us
  other arithmetic  28.5 us (23%)
  starting transfers between devices  24.5 us (20%)
  local copies, waits for them, and re-layouts  18.4 us (15%)
  Pallas kernels  17.3 us (14%)
  matrix products  16.7 us (13%)
  between operations  9.41 us (8%)
  waiting for transfers between devices  8.26 us (7%)
    pallas_call x1, Pallas kernels, long_conv_gate(): pl.pallas_call(_gate_kernel, grid=(channels // LANES,), in_specs=[pl.Bloc...  17.3 us
    dot_general x9, matrix products, emit(): out = jnp.dot(gated, both, preferred_element_type=jnp.float32)  16.7 us
    dynamic_update_slice x14, other arithmetic, emit(): result = lax.dynamic_update_slice_in_dim(result, piece, column, 1)  14.3 us
    ppermute x2, starting transfers between devices, shifted(): return lax.ppermute(block, CTX, route)  10.8 us
    add x1, other arithmetic, short_mixed(): return total + short_filter[2] * before  9.31 us
    dynamic_update_slice x4, local copies, waits for them, and re-layouts, emit(): result = lax.dynamic_update_slice_in_dim(result, piece, column, 1)  7.4 us
    ppermute x3, starting transfers between devices, ring_step(): ahead = lax.ppermute(ahead, 'chip', forward)  6.54 us
    ppermute x1, waiting for transfers between devices, ring_step(): behind = lax.ppermute(behind[:, half:], 'chip', backward)  6.25 us
  transfers between devices with their start and end apart: 19, of which 3 were waited for; matrix products, arithmetic and copies ran while one was open for 41% of the time, Pallas kernels for 14%

profile of v2, /device:TPU:0, one launch (start us, length us, event | category | flops | bytes accessed | tf_op | source)
XLA Modules:
  0.0 123.0 jit_solution(13050297456149705899)
XLA Ops:
  0.0 3.0 %collective-permute-start.2 = (bf16[2048,128]{1,0:T(8,128)(2,1)}, bf16[2048,128]{1,0:T(8,128)(2,1)}, u32[]{:S(2)}, u32[]{:S(2)}) collective-permute-start(bf16[2048,128]{1,0:T(8,128)(2,1)} %param.15), channel_id=1, source_target_pairs={{0,4},{4,8},{8,12},{12,14},{14,10},{10,6},{6,2},{2,0},{1,5},{5,9},... | collective-permute-start | bytes 1572872 | tf_op jit(solution)/shard_map/ppermute | solution.py:119
  4.0 1.5 %collective-permute-start = (bf16[2,6144]{1,0:T(2,128)(2,1)S(1)}, bf16[2,6144]{1,0:T(2,128)(2,1)S(1)}, u32[]{:S(2)}, u32[]{:S(2)}) collective-permute-start(bf16[2,6144]{1,0:T(2,128)(2,1)S(1)} %slice.111), channel_id=1, source_target_pairs={{0,1},{1,2},{2,3},{3,4},{4,5},{5,6},{6,7},{7,8},{8,9},{9,10},{10,1... | collective-permute-start | bytes 73736 | tf_op jit(solution)/shard_map/ppermute | solution.py:22
  5.4 1.1 fusion.79
  6.6 9.3 %multiply_add_fusion = f32[512,6144]{1,0:T(8,128)S(1)} fusion(bf16[512,6144]{1,0:T(8,128)(2,1)} %param.11, bf16[511,6144]{1,0:T(8,128)(2,1)} %bitcast.30, bf16[1,6144]{1,0:T(2,128)(2,1)S(1)} %slice.140, bf16[510,6144]{1,0:T(8,128)(2,1)} %bitcast.31, bf16[2,6144]{1,0:T(2,128)(2,1)S(1)} %collective-permute-done, f32[6144]{0:T(1024)S(1)} %bitcast.33, ...), kind=kLoop, calls=%fused_computation | loop fusion | flops 44040192 | bytes 31531008 | tf_op jit(solution)/shard_map/add | solution.py:36
  15.9 2.8 %fusion.78 = (f32[512,2048]{1,0:T(8,128)}, bf16[512,2048]{1,0:T(8,128)(2,1)S(1)}) fusion(f32[512,6144]{1,0:T(8,128)S(1)} %multiply_add_fusion), kind=kLoop, calls=%fused_computation.104 | loop fusion | flops 2097152 | bytes 18874368 | tf_op jit(solution)/shard_map/slice | solution.py:131
  18.8 9.3 %collective-permute-start.1 = (bf16[128,2048]{1,0:T(8,128)(2,1)S(1)}, bf16[128,2048]{1,0:T(8,128)(2,1)S(1)}, u32[]{:S(2)}, u32[]{:S(2)}) collective-permute-start(bf16[128,2048]{1,0:T(8,128)(2,1)S(1)} %slice.143), channel_id=1, source_target_pairs={{0,1},{1,2},{2,3},{3,4},{4,5},{5,6},{6,7},{7,8},{8,9},{9,10},{10,1... | collective-permute-start | bytes 1572872 | tf_op jit(solution)/shard_map/ppermute | solution.py:22
  28.2 3.2 %collective-permute-start.4 = (bf16[2048,128]{1,0:T(8,128)(2,1)}, bf16[2048,128]{1,0:T(8,128)(2,1)}, u32[]{:S(2)}, u32[]{:S(2)}) collective-permute-start(bf16[2048,128]{1,0:T(8,128)(2,1)} %collective-permute-done.2), channel_id=1, source_target_pairs={{0,4},{4,8},{8,12},{12,14},{14,10},{10,6},{6,2},{2,0},{1,5},{5,9},... | collective-permute-start | bytes 1572872 | tf_op jit(solution)/shard_map/ppermute | solution.py:119
  31.4 1.3 %collective-permute-start.6 = (bf16[2048,128]{1,0:T(8,128)(2,1)}, bf16[2048,128]{1,0:T(8,128)(2,1)}, u32[]{:S(2)}, u32[]{:S(2)}) collective-permute-start(bf16[2048,128]{1,0:T(8,128)(2,1)} %param.15), channel_id=1, source_target_pairs={{0,1},{1,0},{2,3},{3,2},{4,5},{5,4},{6,7},{7,6},{8,9},{9,8},{10,11... | collective-permute-start | bytes 1572872 | tf_op jit(solution)/shard_map/ppermute | solution.py:104
  43.2 3.2 %copy.21 = bf16[512,2048]{1,0:T(8,128)(2,1)} copy(bf16[512,2048]{1,0:T(8,128)(2,1)} %param.10) | data formatting | bytes 4194304
  46.3 1.3 %constant_dynamic-slice_fusion = (bf16[512,64]{1,0:T(8,128)(2,1)S(1)}, bf16[512,64]{1,0:T(8,128)(2,1)S(1)}, bf16[512,64]{1,0:T(8,128)(2,1)S(1)}, bf16[512,64]{1,0:T(8,128)(2,1)S(1)}) fusion(bf16[512,2048]{1,0:T(8,128)(2,1)} %param.10, s32[]{:T(128)S(6)} %select_n.159, s32[]{:T(128)S(6)} %select_n.157, s32[]{:T(128)S(6)} %select_n.156, s32[]{:T(128)S(6)} %select_n.158), kind=kLoop, calls=%fused_computation.90 | loop fusion | bytes 524304 | tf_op jit(solution)/shard_map/dynamic_slice | solution.py:157
  51.0 17.3 %shard_map.82 = bf16[512,2048]{1,0:T(8,128)(2,1)} custom-call(f32[128,384]{1,0:T(8,128)} %scatter.4.fw_ref, f32[1,2048]{1,0:T(1,128)} %bitcast.35, bf16[128,2048]{1,0:T(8,128)(2,1)} %copy-done.3, bf16[512,2048]{1,0:T(8,128)(2,1)} %copy-done.1, f32[512,2048]{1,0:T(8,128)} %get-tuple-element.28.gate_ref), custom_call_target="tpu_custom_call" | custom-call | tf_op jit(solution)/shard_map/pallas_call | solution.py:70
  68.3 1.7 %collective-permute-start.10 = (bf16[2048,128]{1,0:T(8,128)(2,1)}, bf16[2048,128]{1,0:T(8,128)(2,1)S(1)}, u32[]{:S(2)}, u32[]{:S(2)}) collective-permute-start(bf16[2048,128]{1,0:T(8,128)(2,1)} %collective-permute-done.5), channel_id=1, source_target_pairs={{4,0},{8,4},{12,8},{14,12},{10,14},{6,10},{2,6},{0,2},{5,1},{9,5},... | collective-permute-start | bytes 1572872 | tf_op jit(solution)/shard_map/ppermute | solution.py:120
  70.4 2.5 %fusion.1 = f32[512,256]{1,0:T(8,128)S(1)} fusion(bf16[512,2048]{1,0:T(8,128)(2,1)} %shard_map.82, bf16[2048,128]{1,0:T(8,128)(2,1)} %collective-permute-done.6, bf16[2048,128]{1,0:T(8,128)(2,1)} %param.15), kind=kOutput, calls=%fused_computation.3 | convolution fusion | flops 538968064 | bytes 3670016 | tf_op jit(solution)/shard_map/dot_general | solution.py:154
  72.9 1.6 %fusion.51 = bf16[512,2048]{1,0:T(8,128)(2,1)} fusion(bf16[512,2048]{1,0:T(8,128)(2,1)} %copy.21, s32[]{:T(128)S(6)} %select_n.127, f32[512,256]{1,0:T(8,128)S(1)} %fusion.1), kind=kLoop, calls=%fused_computation.67 | loop fusion | flops 196608 | bytes 524292 | tf_op jit(solution)/shard_map/dynamic_update_slice | solution.py:159
  75.7 1.9 %fusion.5 = f32[512,256]{1,0:T(8,128)S(1)} fusion(bf16[512,2048]{1,0:T(8,128)(2,1)S(1)} %copy-done, bf16[2048,128]{1,0:T(8,128)(2,1)} %collective-permute-done.7, bf16[2048,128]{1,0:T(8,128)(2,1)} %collective-permute-done.2), kind=kOutput, calls=%fused_computation.7 | convolution fusion | flops 538968064 | bytes 3670016 | tf_op jit(solution)/shard_map/dot_general | solution.py:154
  79.1 1.9 %fusion.9 = f32[512,256]{1,0:T(8,128)S(1)} fusion(bf16[512,2048]{1,0:T(8,128)(2,1)S(1)} %copy-done, bf16[2048,128]{1,0:T(8,128)(2,1)} %collective-permute-done.8, bf16[2048,128]{1,0:T(8,128)(2,1)} %collective-permute-done.3), kind=kOutput, calls=%fused_computation.11 | convolution fusion | flops 538968064 | bytes 3670016 | tf_op jit(solution)/shard_map/dot_general | solution.py:154
  82.9 1.5 %collective-permute-done.9 = bf16[2048,128]{1,0:T(8,128)(2,1)} collective-permute-done((bf16[2048,128]{1,0:T(8,128)(2,1)}, bf16[2048,128]{1,0:T(8,128)(2,1)}, u32[]{:S(2)}, u32[]{:S(2)}) %collective-permute-start.9) | collective-permute-done | bytes 524320 | tf_op jit(solution)/shard_map/ppermute | solution.py:119
  84.6 1.6 %collective-permute-start.17 = (bf16[2048,64]{1,0:T(8,128)(2,1)S(1)}, bf16[2048,64]{1,0:T(8,128)(2,1)S(1)}, u32[]{:S(2)}, u32[]{:S(2)}) collective-permute-start(bf16[2048,64]{1,0:T(8,128)(2,1)S(1)} %slice.137), channel_id=1, source_target_pairs={{4,0},{8,4},{12,8},{14,12},{10,14},{6,10},{2,6},{0,2},{5,1},{9,5},... | collective-permute-start | bytes 786440 | tf_op jit(solution)/shard_map/ppermute | solution.py:115
  86.7 1.8 %fusion.17 = f32[512,256]{1,0:T(8,128)S(1)} fusion(bf16[512,2048]{1,0:T(8,128)(2,1)S(1)} %copy-done, bf16[2048,128]{1,0:T(8,128)(2,1)S(1)} %collective-permute-done.12, bf16[2048,128]{1,0:T(8,128)(2,1)} %collective-permute-done.5), kind=kOutput, calls=%fused_computation.19 | convolution fusion | flops 538968064 | bytes 3670016 | tf_op jit(solution)/shard_map/dot_general | solution.py:154
  88.4 1.8 %fusion.13 = f32[512,256]{1,0:T(8,128)S(1)} fusion(bf16[512,2048]{1,0:T(8,128)(2,1)S(1)} %copy-done, bf16[2048,128]{1,0:T(8,128)(2,1)S(1)} %collective-permute-done.11, bf16[2048,128]{1,0:T(8,128)(2,1)} %collective-permute-done.4), kind=kOutput, calls=%fused_computation.15 | convolution fusion | flops 538968064 | bytes 3670016 | tf_op jit(solution)/shard_map/dot_general | solution.py:154
  91.6 6.2 %collective-permute-done.17 = bf16[2048,64]{1,0:T(8,128)(2,1)S(1)} collective-permute-done((bf16[2048,64]{1,0:T(8,128)(2,1)S(1)}, bf16[2048,64]{1,0:T(8,128)(2,1)S(1)}, u32[]{:S(2)}, u32[]{:S(2)}) %collective-permute-start.17) | collective-permute-done | bytes 262176 | tf_op jit(solution)/shard_map/ppermute | solution.py:115
  103.0 2.1 %fusion.29 = f32[512,128]{0,1:T(8,128)S(1)} fusion(bf16[512,2048]{1,0:T(8,128)(2,1)S(1)} %copy-done, bf16[2048,64]{1,0:T(8,128)(2,1)} %collective-permute-done.16, bf16[2048,64]{1,0:T(8,128)(2,1)S(1)} %collective-permute-done.15), kind=kOutput, calls=%fused_computation.31 | convolution fusion | flops 269484032 | bytes 2883584 | tf_op jit(solution)/shard_map/dot_general | solution.py:154
  105.6 1.9 %fusion.21 = f32[512,256]{1,0:T(8,128)S(1)} fusion(bf16[512,2048]{1,0:T(8,128)(2,1)S(1)} %copy-done, bf16[2048,128]{1,0:T(8,128)(2,1)} %collective-permute-done.13, bf16[2048,128]{1,0:T(8,128)(2,1)} %collective-permute-done.9), kind=kOutput, calls=%fused_computation.23 | convolution fusion | flops 538968064 | bytes 3670016 | tf_op jit(solution)/shard_map/dot_general | solution.py:154
  107.5 1.6 %fusion.61 = bf16[512,2048]{1,0:T(8,128)(2,1)} fusion(bf16[512,2048]{1,0:T(8,128)(2,1)} %fusion.60, s32[]{:T(128)S(6)} %select_n.148, f32[512,256]{1,0:T(8,128)S(1)} %fusion.21, bf16[512,2048]{1,0:T(8,128)(2,1)} %param.10), kind=kLoop, calls=%fused_computation.77 | loop fusion | flops 196608 | bytes 524292 | tf_op jit(solution)/shard_map/dynamic_update_slice | solution.py:159
  109.1 1.6 %fusion.62 = bf16[512,2048]{1,0:T(8,128)(2,1)} fusion(bf16[512,2048]{1,0:T(8,128)(2,1)} %fusion.61, s32[]{:T(128)S(6)} %select_n.149, f32[512,256]{1,0:T(8,128)S(1)} %fusion.21, bf16[512,2048]{1,0:T(8,128)(2,1)} %param.10), kind=kLoop, calls=%fused_computation.78 | loop fusion | flops 196608 | bytes 524292 | tf_op jit(solution)/shard_map/dynamic_update_slice | solution.py:159
  110.7 1.8 %fusion.25 = f32[512,256]{1,0:T(8,128)S(1)} fusion(bf16[512,2048]{1,0:T(8,128)(2,1)S(1)} %copy-done, bf16[2048,128]{1,0:T(8,128)(2,1)} %collective-permute-done.14, bf16[2048,128]{1,0:T(8,128)(2,1)S(1)} %collective-permute-done.10), kind=kOutput, calls=%fused_computation.27 | convolution fusion | flops 538968064 | bytes 3670016 | tf_op jit(solution)/shard_map/dot_general | solution.py:154
  112.4 1.6 %fusion.63 = bf16[512,2048]{1,0:T(8,128)(2,1)} fusion(bf16[512,2048]{1,0:T(8,128)(2,1)} %fusion.62, s32[]{:T(128)S(6)} %select_n.152, f32[512,256]{1,0:T(8,128)S(1)} %fusion.25, bf16[512,2048]{1,0:T(8,128)(2,1)} %param.10), kind=kLoop, calls=%fused_computation.79 | loop fusion | flops 196608 | bytes 524292 | tf_op jit(solution)/shard_map/dynamic_update_slice | solution.py:159
  114.0 1.6 %fusion.64 = bf16[512,2048]{1,0:T(8,128)(2,1)} fusion(bf16[512,2048]{1,0:T(8,128)(2,1)} %fusion.63, s32[]{:T(128)S(6)} %select_n.153, f32[512,256]{1,0:T(8,128)S(1)} %fusion.25, bf16[512,2048]{1,0:T(8,128)(2,1)} %param.10), kind=kLoop, calls=%fused_computation.80 | loop fusion | flops 196608 | bytes 524292 | tf_op jit(solution)/shard_map/dynamic_update_slice | solution.py:159
  115.6 1.7 %dynamic_update_slice.68 = bf16[512,2048]{1,0:T(8,128)(2,1)} dynamic-update-slice(bf16[512,2048]{1,0:T(8,128)(2,1)} %fusion.64, bf16[512,64]{1,0:T(8,128)(2,1)S(1)} %copy.10, s32[]{:T(128)} %constant.98.clone.1, s32[]{:T(128)S(6)} %select_n.156) | dynamic-update-slice | bytes 131076 | tf_op jit(solution)/shard_map/dynamic_update_slice | solution.py:159
  117.4 1.6 %dynamic_update_slice.69 = bf16[512,2048]{1,0:T(8,128)(2,1)} dynamic-update-slice(bf16[512,2048]{1,0:T(8,128)(2,1)} %dynamic_update_slice.68, bf16[512,64]{1,0:T(8,128)(2,1)S(1)} %copy.12, s32[]{:T(128)} %constant.98.clone.1, s32[]{:T(128)S(6)} %select_n.157) | dynamic-update-slice | bytes 131076 | tf_op jit(solution)/shard_map/dynamic_update_slice | solution.py:159
  119.0 2.2 %dynamic_update_slice.70 = bf16[512,2048]{1,0:T(8,128)(2,1)} dynamic-update-slice(bf16[512,2048]{1,0:T(8,128)(2,1)} %dynamic_update_slice.69, bf16[512,64]{1,0:T(8,128)(2,1)S(1)} %copy.14, s32[]{:T(128)} %constant.98.clone.1, s32[]{:T(128)S(6)} %select_n.158) | dynamic-update-slice | bytes 131076 | tf_op jit(solution)/shard_map/dynamic_update_slice | solution.py:159
  121.2 1.9 %dynamic_update_slice.71 = bf16[512,2048]{1,0:T(8,128)(2,1)} dynamic-update-slice(bf16[512,2048]{1,0:T(8,128)(2,1)} %dynamic_update_slice.70, bf16[512,64]{1,0:T(8,128)(2,1)S(1)} %copy.16, s32[]{:T(128)} %constant.98.clone.1, s32[]{:T(128)S(6)} %select_n.159) | dynamic-update-slice | bytes 131076 | tf_op jit(solution)/shard_map/dynamic_update_slice | solution.py:159
  (75 shorter events, 18.2 us)
Async XLA Ops:
  0.0 28.2 %collective-permute-start.2 = (bf16[2048,128]{1,0:T(8,128)(2,1)}, bf16[2048,128]{1,0:T(8,128)(2,1)}, u32[]{:S(2)}, u32[]{:S(2)}) collective-permute-start(bf16[2048,128]{1,0:T(8,128)(2,1)} %param.15), channel_id=1, source_target_pairs={{0,4},{4,8},{8,12},{12,14},{14,10},{10,6},{6,2},{2,0},{1,5},{5,9},... | collective-permute-start | bytes 1572872 | tf_op jit(solution)/shard_map/ppermute | solution.py:119
  3.0 25.2 %collective-permute-start.3 = (bf16[2048,128]{1,0:T(8,128)(2,1)}, bf16[2048,128]{1,0:T(8,128)(2,1)}, u32[]{:S(2)}, u32[]{:S(2)}) collective-permute-start(bf16[2048,128]{1,0:T(8,128)(2,1)} %param.15), channel_id=1, source_target_pairs={{4,0},{8,4},{12,8},{14,12},{10,14},{6,10},{2,6},{0,2},{5,1},{9,5},... | collective-permute-start | bytes 1572872 | tf_op jit(solution)/shard_map/ppermute | solution.py:120
  4.0 2.6 %collective-permute-start = (bf16[2,6144]{1,0:T(2,128)(2,1)S(1)}, bf16[2,6144]{1,0:T(2,128)(2,1)S(1)}, u32[]{:S(2)}, u32[]{:S(2)}) collective-permute-start(bf16[2,6144]{1,0:T(2,128)(2,1)S(1)} %slice.111), channel_id=1, source_target_pairs={{0,1},{1,2},{2,3},{3,4},{4,5},{5,6},{6,7},{7,8},{8,9},{9,10},{10,1... | collective-permute-start | bytes 73736 | tf_op jit(solution)/shard_map/ppermute | solution.py:22
  15.9 16.8 %copy-start.7 = (s32[8]{0:T(128)S(1)}, s32[8]{0:T(128)}, u32[]{:S(2)}) copy-start(s32[8]{0:T(128)} %constant.120.clone) | copy-start | bytes 100
  15.9 22.1 %copy-start.6 = (s32[8]{0:T(128)S(1)}, s32[8]{0:T(128)}, u32[]{:S(2)}) copy-start(s32[8]{0:T(128)} %constant.119.clone) | copy-start | bytes 100
  15.9 27.1 %copy-start.5 = (bf16[128,128]{1,0:T(8,128)(2,1)S(1)}, bf16[128,128]{1,0:T(8,128)(2,1)}, u32[]{:S(2)}) copy-start(bf16[128,128]{1,0:T(8,128)(2,1)} %param.13) | copy-start | bytes 98308
  18.8 27.6 %copy-start.1 = (bf16[512,2048]{1,0:T(8,128)(2,1)}, bf16[512,2048]{1,0:T(8,128)(2,1)S(1)}, u32[]{:S(2)}) copy-start(bf16[512,2048]{1,0:T(8,128)(2,1)S(1)} %get-tuple-element.27.carried_ref) | copy-start | bytes 6291460
  18.8 31.3 %collective-permute-start.1 = (bf16[128,2048]{1,0:T(8,128)(2,1)S(1)}, bf16[128,2048]{1,0:T(8,128)(2,1)S(1)}, u32[]{:S(2)}, u32[]{:S(2)}) collective-permute-start(bf16[128,2048]{1,0:T(8,128)(2,1)S(1)} %slice.143), channel_id=1, source_target_pairs={{0,1},{1,2},{2,3},{3,4},{4,5},{5,6},{6,7},{7,8},{8,9},{9,10},{10,1... | collective-permute-start | bytes 1572872 | tf_op jit(solution)/shard_map/ppermute | solution.py:22
  28.2 40.1 %collective-permute-start.4 = (bf16[2048,128]{1,0:T(8,128)(2,1)}, bf16[2048,128]{1,0:T(8,128)(2,1)}, u32[]{:S(2)}, u32[]{:S(2)}) collective-permute-start(bf16[2048,128]{1,0:T(8,128)(2,1)} %collective-permute-done.2), channel_id=1, source_target_pairs={{0,4},{4,8},{8,12},{12,14},{14,10},{10,6},{6,2},{2,0},{1,5},{5,9},... | collective-permute-start | bytes 1572872 | tf_op jit(solution)/shard_map/ppermute | solution.py:119
  31.4 36.9 %collective-permute-start.5 = (bf16[2048,128]{1,0:T(8,128)(2,1)}, bf16[2048,128]{1,0:T(8,128)(2,1)}, u32[]{:S(2)}, u32[]{:S(2)}) collective-permute-start(bf16[2048,128]{1,0:T(8,128)(2,1)} %collective-permute-done.3), channel_id=1, source_target_pairs={{4,0},{8,4},{12,8},{14,12},{10,14},{6,10},{2,6},{0,2},{5,1},{9,5},... | collective-permute-start | bytes 1572872 | tf_op jit(solution)/shard_map/ppermute | solution.py:120
  31.4 39.0 %collective-permute-start.6 = (bf16[2048,128]{1,0:T(8,128)(2,1)}, bf16[2048,128]{1,0:T(8,128)(2,1)}, u32[]{:S(2)}, u32[]{:S(2)}) collective-permute-start(bf16[2048,128]{1,0:T(8,128)(2,1)} %param.15), channel_id=1, source_target_pairs={{0,1},{1,0},{2,3},{3,2},{4,5},{5,4},{6,7},{7,6},{8,9},{9,8},{10,11... | collective-permute-start | bytes 1572872 | tf_op jit(solution)/shard_map/ppermute | solution.py:104
  50.2 25.0 %collective-permute-start.7 = (bf16[2048,128]{1,0:T(8,128)(2,1)}, bf16[2048,128]{1,0:T(8,128)(2,1)}, u32[]{:S(2)}, u32[]{:S(2)}) collective-permute-start(bf16[2048,128]{1,0:T(8,128)(2,1)} %collective-permute-done.2), channel_id=1, source_target_pairs={{0,1},{1,0},{2,3},{3,2},{4,5},{5,4},{6,7},{7,6},{8,9},{9,8},{10,11... | collective-permute-start | bytes 1572872 | tf_op jit(solution)/shard_map/ppermute | solution.py:104
  50.2 0.8 copy-start.3
  50.2 28.9 %collective-permute-start.8 = (bf16[2048,128]{1,0:T(8,128)(2,1)}, bf16[2048,128]{1,0:T(8,128)(2,1)}, u32[]{:S(2)}, u32[]{:S(2)}) collective-permute-start(bf16[2048,128]{1,0:T(8,128)(2,1)} %collective-permute-done.3), channel_id=1, source_target_pairs={{0,1},{1,0},{2,3},{3,2},{4,5},{5,4},{6,7},{7,6},{8,9},{9,8},{10,11... | collective-permute-start | bytes 1572872 | tf_op jit(solution)/shard_map/ppermute | solution.py:104
  68.2 6.3 %copy-start.2 = (bf16[512,2048]{1,0:T(8,128)(2,1)S(1)}, bf16[512,2048]{1,0:T(8,128)(2,1)}, u32[]{:S(2)}) copy-start(bf16[512,2048]{1,0:T(8,128)(2,1)} %param.10) | copy-start | bytes 6291460
  68.3 7.5 %copy-start = (bf16[512,2048]{1,0:T(8,128)(2,1)S(1)}, bf16[512,2048]{1,0:T(8,128)(2,1)}, u32[]{:S(2)}) copy-start(bf16[512,2048]{1,0:T(8,128)(2,1)} %shard_map.82) | copy-start | bytes 6291460
  68.3 14.6 %collective-permute-start.10 = (bf16[2048,128]{1,0:T(8,128)(2,1)}, bf16[2048,128]{1,0:T(8,128)(2,1)S(1)}, u32[]{:S(2)}, u32[]{:S(2)}) collective-permute-start(bf16[2048,128]{1,0:T(8,128)(2,1)} %collective-permute-done.5), channel_id=1, source_target_pairs={{4,0},{8,4},{12,8},{14,12},{10,14},{6,10},{2,6},{0,2},{5,1},{9,5},... | collective-permute-start | bytes 1572872 | tf_op jit(solution)/shard_map/ppermute | solution.py:120
  70.0 14.4 %collective-permute-start.9 = (bf16[2048,128]{1,0:T(8,128)(2,1)}, bf16[2048,128]{1,0:T(8,128)(2,1)}, u32[]{:S(2)}, u32[]{:S(2)}) collective-permute-start(bf16[2048,128]{1,0:T(8,128)(2,1)} %collective-permute-done.4), channel_id=1, source_target_pairs={{0,4},{4,8},{8,12},{12,14},{14,10},{10,6},{6,2},{2,0},{1,5},{5,9},... | collective-permute-start | bytes 1572872 | tf_op jit(solution)/shard_map/ppermute | solution.py:119
  70.4 16.3 %collective-permute-start.12 = (bf16[2048,128]{1,0:T(8,128)(2,1)}, bf16[2048,128]{1,0:T(8,128)(2,1)S(1)}, u32[]{:S(2)}, u32[]{:S(2)}) collective-permute-start(bf16[2048,128]{1,0:T(8,128)(2,1)} %collective-permute-done.5), channel_id=1, source_target_pairs={{0,1},{1,0},{2,3},{3,2},{4,5},{5,4},{6,7},{7,6},{8,9},{9,8},{10,11... | collective-permute-start | bytes 1572872 | tf_op jit(solution)/shard_map/ppermute | solution.py:104
  75.2 13.2 %collective-permute-start.11 = (bf16[2048,128]{1,0:T(8,128)(2,1)}, bf16[2048,128]{1,0:T(8,128)(2,1)S(1)}, u32[]{:S(2)}, u32[]{:S(2)}) collective-permute-start(bf16[2048,128]{1,0:T(8,128)(2,1)} %collective-permute-done.4), channel_id=1, source_target_pairs={{0,1},{1,0},{2,3},{3,2},{4,5},{5,4},{6,7},{7,6},{8,9},{9,8},{10,11... | collective-permute-start | bytes 1572872 | tf_op jit(solution)/shard_map/ppermute | solution.py:104
  84.6 13.3 %collective-permute-start.17 = (bf16[2048,64]{1,0:T(8,128)(2,1)S(1)}, bf16[2048,64]{1,0:T(8,128)(2,1)S(1)}, u32[]{:S(2)}, u32[]{:S(2)}) collective-permute-start(bf16[2048,64]{1,0:T(8,128)(2,1)S(1)} %slice.137), channel_id=1, source_target_pairs={{4,0},{8,4},{12,8},{14,12},{10,14},{6,10},{2,6},{0,2},{5,1},{9,5},... | collective-permute-start | bytes 786440 | tf_op jit(solution)/shard_map/ppermute | solution.py:115
  86.2 13.6 %collective-permute-start.15 = (bf16[2048,64]{1,0:T(8,128)(2,1)}, bf16[2048,64]{1,0:T(8,128)(2,1)S(1)}, u32[]{:S(2)}, u32[]{:S(2)}) collective-permute-start(bf16[2048,64]{1,0:T(8,128)(2,1)} %bitcast.29), channel_id=1, source_target_pairs={{0,4},{4,8},{8,12},{12,14},{14,10},{10,6},{6,2},{2,0},{1,5},{5,9},... | collective-permute-start | bytes 786440 | tf_op jit(solution)/shard_map/ppermute | solution.py:114
  97.9 2.4 %collective-permute-start.18 = (bf16[2048,64]{1,0:T(8,128)(2,1)S(1)}, bf16[2048,64]{1,0:T(8,128)(2,1)S(1)}, u32[]{:S(2)}, u32[]{:S(2)}) collective-permute-start(bf16[2048,64]{1,0:T(8,128)(2,1)S(1)} %collective-permute-done.17), channel_id=1, source_target_pairs={{0,1},{1,0},{2,3},{3,2},{4,5},{5,4},{6,7},{7,6},{8,9},{9,8},{10,11... | collective-permute-start | bytes 786440 | tf_op jit(solution)/shard_map/ppermute | solution.py:104
  98.6 12.1 %collective-permute-start.14 = (bf16[2048,128]{1,0:T(8,128)(2,1)S(1)}, bf16[2048,128]{1,0:T(8,128)(2,1)}, u32[]{:S(2)}, u32[]{:S(2)}) collective-permute-start(bf16[2048,128]{1,0:T(8,128)(2,1)S(1)} %collective-permute-done.10), channel_id=1, source_target_pairs={{0,1},{1,0},{2,3},{3,2},{4,5},{5,4},{6,7},{7,6},{8,9},{9,8},{10,11... | collective-permute-start | bytes 1572872 | tf_op jit(solution)/shard_map/ppermute | solution.py:104
  99.1 6.5 %collective-permute-start.13 = (bf16[2048,128]{1,0:T(8,128)(2,1)}, bf16[2048,128]{1,0:T(8,128)(2,1)}, u32[]{:S(2)}, u32[]{:S(2)}) collective-permute-start(bf16[2048,128]{1,0:T(8,128)(2,1)} %collective-permute-done.9), channel_id=1, source_target_pairs={{0,1},{1,0},{2,3},{3,2},{4,5},{5,4},{6,7},{7,6},{8,9},{9,8},{10,11... | collective-permute-start | bytes 1572872 | tf_op jit(solution)/shard_map/ppermute | solution.py:104
  99.8 3.2 %collective-permute-start.16 = (bf16[2048,64]{1,0:T(8,128)(2,1)S(1)}, bf16[2048,64]{1,0:T(8,128)(2,1)}, u32[]{:S(2)}, u32[]{:S(2)}) collective-permute-start(bf16[2048,64]{1,0:T(8,128)(2,1)S(1)} %collective-permute-done.15), channel_id=1, source_target_pairs={{0,1},{1,0},{2,3},{3,2},{4,5},{5,4},{6,7},{7,6},{8,9},{9,8},{10,11... | collective-permute-start | bytes 786440 | tf_op jit(solution)/shard_map/ppermute | solution.py:104
  103.0 2.4 %copy-start.4 = (bf16[512,64]{0,1:T(8,128)(2,1)S(1)}, bf16[512,64]{0,1:T(8,128)(2,1)}, u32[]{:S(2)}) copy-start(bf16[512,64]{0,1:T(8,128)(2,1)} %get-tuple-element.43) | copy-start | bytes 196612

commit v3 on v2

--- a/solution.py
+++ b/solution.py
@@ -65,8 +65,7 @@
     groups, taps = long_filter.shape
     row_count, channels = carried.shape
     per_tile = LANES // (channels // groups)
-    fw = jnp.zeros((groups, 3 * BLOCK), jnp.float32)
-    fw = fw.at[:, 1 : 1 + taps].set(long_filter[:, ::-1].astype(jnp.float32))
+    fw = jnp.pad(long_filter[:, ::-1].astype(jnp.float32), ((0, 0), (1, 3 * BLOCK - 1 - taps)))
     return pl.pallas_call(
         _gate_kernel,
         grid=(channels // LANES,),
@@ -82,95 +81,90 @@
     )(fw, conv_bias.reshape(1, channels), halo, carried, gate_rows)
 
 
+def ring_place(c, chips):
+    return jnp.where(c % 2 == 0, c // 2, chips - 1 - c // 2)
+
+
+def ring_chip(q, chips):
+    return jnp.where(q < chips // 2, 2 * q, 2 * (chips - 1 - q) + 1)
+
+
+def carried_of(second, carrier):
+    return (second * carrier).astype(jnp.bfloat16)
+
+
 def on_device(tokens, projected, short_filter, long_filter, conv_bias, out_weight):
     row_count = tokens.shape[0]
     channels = out_weight.shape[0]
     chips = lax.axis_size("chip")
     width = out_weight.shape[1]
+    ring = chips % 2 == 0 and chips <= 8
 
     chip = lax.axis_index("chip")
     core = lax.axis_index("core")
+    position = ring_place(chip, chips)
     order = ring_order(chips)
-    where = [0] * chips
-    for place, c in enumerate(order):
-        where[c] = place
-    order_arr = jnp.array(order, jnp.int32)
-    position = jnp.array(where, jnp.int32)[chip]
     forward = [(order[i], order[(i + 1) % chips]) for i in range(chips)]
     backward = [(order[(i + 1) % chips], order[i]) for i in range(chips)]
     swap = [(0, 1), (1, 0)]
+    steps = chips // 2
 
-    def with_partner(piece):
+    weight = jnp.zeros((channels, chips * 2 * width), out_weight.dtype)
+
+    def place(weight, piece, owner_chip, row=0):
         other = lax.ppermute(piece, "core", swap)
-        return (piece, other)
+        for k, part in ((core, piece), (1 - core, other)):
+            weight = lax.dynamic_update_slice(weight, part, (row, (owner_chip * 2 + k) * width))
+        return weight
 
-    steps = min(chips, 8) // 2
-    ahead = behind = out_weight
-    arrived = [(chip, 0, with_partner(out_weight))]
-
-    def ring_step(step, ahead, behind):
-        if step == steps and chips % 2 == 0:
-            half = width // 2
-            ahead = lax.ppermute(ahead[:, :half], "chip", forward)
-            behind = lax.ppermute(behind[:, half:], "chip", backward)
-            source = order_arr[(position - step) % chips]
-            got = [(source, 0, with_partner(ahead)), (source, half, with_partner(behind))]
+    def ring_step(step, weight, ahead, behind):
+        if step == steps:
+            half = channels // 2
+            ahead = lax.ppermute(ahead[:half], "chip", forward)
+            behind = lax.ppermute(behind[half:], "chip", backward)
+            source = ring_chip((position - step) % chips, chips)
+            weight = place(weight, ahead, source, 0)
+            weight = place(weight, behind, source, half)
         else:
             ahead = lax.ppermute(ahead, "chip", forward)
             behind = lax.ppermute(behind, "chip", backward)
-            got = [(order_arr[(position - step) % chips], 0, with_partner(ahead))]
-            if step < steps or chips % 2:
-                got.append((order_arr[(position + step) % chips], 0, with_partner(behind)))
-        return ahead, behind, got
+            weight = place(weight, ahead, ring_chip((position - step) % chips, chips))
+            weight = place(weight, behind, ring_chip((position + step) % chips, chips))
+        return weight, ahead, behind
 
-    ahead, behind, got = ring_step(1, ahead, behind)
-    arrived += got
+    ahead = behind = out_weight
+    if ring:
+        weight = place(weight, out_weight, chip)
+        weight, ahead, behind = ring_step(1, weight, ahead, behind)
 
+    tail = projected[row_count - BLOCK - 2 :]
+    tail_mixed = [
+        short_mixed(tail[:2, k * channels : (k + 1) * channels], tail[2:, k * channels : (k + 1) * channels], short_filter[:, k * channels : (k + 1) * channels])
+        for k in (1, 2)
+    ]
+    halo = shifted(carried_of(*tail_mixed), 1)
     edge = shifted(projected[row_count - 2 :], 1)
-    mixed = short_mixed(edge, projected, short_filter)
-    gate_rows = mixed[:, :channels]
-    carried = (mixed[:, channels : 2 * channels] * mixed[:, 2 * channels :]).astype(jnp.bfloat16)
-    halo = shifted(carried[row_count - BLOCK :], 1)
+    mixed = [
+        short_mixed(edge[:, k * channels : (k + 1) * channels], projected[:, k * channels : (k + 1) * channels], short_filter[:, k * channels : (k + 1) * channels])
+        for k in (0, 1, 2)
+    ]
+    gate_rows = mixed[0]
+    carried = carried_of(mixed[1], mixed[2])
 
     carried, gate_rows, ahead, behind = lax.optimization_barrier((carried, gate_rows, ahead, behind))
-    if steps >= 2:
-        ahead, behind, got = ring_step(2, ahead, behind)
-        arrived += got
+    if ring and steps >= 2:
+        weight, ahead, behind = ring_step(2, weight, ahead, behind)
 
     gated = long_conv_gate(halo, carried, gate_rows, long_filter, conv_bias)
 
-    if chips > 8:
+    if ring:
+        gated, ahead, behind = lax.optimization_barrier((gated, ahead, behind))
+        for step in range(3, steps + 1):
+            weight, ahead, behind = ring_step(step, weight, ahead, behind)
+    else:
         weight = lax.all_gather(out_weight, CTX, axis=1, tiled=True)
-        branch = jnp.dot(gated, weight, preferred_element_type=jnp.float32)
-        return (tokens.astype(jnp.float32) + branch).astype(jnp.bfloat16)
-
-    result = tokens
-    done = 0
-
-    def emit(result, owner_chip, start, pieces):
-        mine, other = pieces
-        size = mine.shape[1]
-        both = jnp.concatenate([mine, other], axis=1)
-        out = jnp.dot(gated, both, preferred_element_type=jnp.float32)
-        for k, half in ((core, out[:, :size]), (1 - core, out[:, size:])):
-            column = (owner_chip * 2 + k) * width + start
-            rows = lax.dynamic_slice_in_dim(tokens, column, size, 1).astype(jnp.float32)
-            piece = (rows + half).astype(jnp.bfloat16)
-            result = lax.dynamic_update_slice_in_dim(result, piece, column, 1)
-        return result
-
-    for step in range(3, steps + 1):
-        gated, ahead, behind = lax.optimization_barrier((gated, ahead, behind))
-        ahead, behind, got = ring_step(step, ahead, behind)
-        target = len(arrived)
-        while done < target - 2:
-            result = emit(result, *arrived[done])
-            done += 1
-        arrived += got
-    while done < len(arrived):
-        result = emit(result, *arrived[done])
-        done += 1
-    return result
+    branch = jnp.dot(gated, weight, preferred_element_type=jnp.float32)
+    return (tokens.astype(jnp.float32) + branch).astype(jnp.bfloat16)
 
 
 def solution(mesh):

time: 124 us -> 104 us (0.84)
  local copies, waits for them, and re-layouts: 18.4 us -> 34.2 us
  other arithmetic: 28.5 us -> 15.7 us
  between operations: 9.41 us -> 0.11 us
  matrix products: 16.7 us -> 9.17 us
  starting transfers between devices: 24.5 us -> 17 us
    dynamic_update_slice x14 -> x0, other arithmetic: 14.3 us -> none  [emit(): result = lax.dynamic_update_slice_in_dim(result, piece, column, 1)]
    dynamic_update_slice x4 -> x18, local copies, waits for them, and re-layouts: 7.4 us -> 18.8 us  [place(): lax.dynamic_update_slice(weight, part, (row, (owner_chip * 2 + k) * width))]
    convert_element_type x2, other arithmetic: 0.72 us -> 10.6 us  [carried_of(): return (second * carrier).astype(jnp.bfloat16)]
    slice x2 -> x5, local copies, waits for them, and re-layouts: 0.24 us -> 8.88 us  [the longest x1 5.87 us: short_mixed(): rows[:-1]]
    dot_general x9 -> x1, matrix products: 16.7 us -> 9.17 us  [on_device(): branch = jnp.dot(gated, weight, preferred_element_type=jnp.float32)]
    ppermute x3, waiting for transfers between devices: 1.51 us -> 6.57 us  [ring_step(): ahead = lax.ppermute(ahead, 'chip', forward)]
    add x1, other arithmetic: 9.31 us -> 4.37 us  [short_mixed(): return total + short_filter[2] * before]
    ppermute x2, starting transfers between devices: 10.8 us -> 6.18 us  [shifted(): return lax.ppermute(block, CTX, route)]
  transfers between devices with their start and end apart: 19 -> 19, of which waited for: 3 -> 3; matrix products, arithmetic and copies ran while one was open for 41% -> 48% of each run, Pallas kernels for 14% -> 17%
where the time goes in v3:
time: 104 us; the launch traced here: 103 us
  local copies, waits for them, and re-layouts  34.2 us (33%)
  Pallas kernels  17.2 us (17%)
  starting transfers between devices  17 us (16%)
  other arithmetic  15.7 us (15%)
  matrix products  9.17 us (9%)
  waiting for transfers between devices  9.16 us (9%)
    dynamic_update_slice x18, local copies, waits for them, and re-layouts, place(): lax.dynamic_update_slice(weight, part, (row, (owner_chip * 2 + k) * width))  18.8 us
    pallas_call x1, Pallas kernels, long_conv_gate(): pl.pallas_call(_gate_kernel, grid=(channels // LANES,), in_specs=[pl.Bloc...  17.2 us
    convert_element_type x2, other arithmetic, carried_of(): return (second * carrier).astype(jnp.bfloat16)  10.6 us
    dot_general x1, matrix products, on_device(): branch = jnp.dot(gated, weight, preferred_element_type=jnp.float32)  9.17 us
    ppermute x3, waiting for transfers between devices, ring_step(): ahead = lax.ppermute(ahead, 'chip', forward)  6.57 us
    ppermute x3, starting transfers between devices, ring_step(): ahead = lax.ppermute(ahead, 'chip', forward)  6.35 us
    ppermute x2, starting transfers between devices, shifted(): return lax.ppermute(block, CTX, route)  6.18 us
    slice x1, local copies, waits for them, and re-layouts, short_mixed(): rows[:-1]  5.87 us
  transfers between devices with their start and end apart: 19, of which 3 were waited for; matrix products, arithmetic and copies ran while one was open for 48% of the time, Pallas kernels for 17%

profile of v3, /device:TPU:0, one launch (start us, length us, event | category | flops | bytes accessed | tf_op | source)
XLA Modules:
  0.0 102.6 jit_solution(13530241295042425589)
XLA Ops:
  0.0 3.0 %collective-permute-start.2 = (bf16[2048,128]{1,0:T(8,128)(2,1)}, bf16[2048,128]{1,0:T(8,128)(2,1)}, u32[]{:S(2)}, u32[]{:S(2)}) collective-permute-start(bf16[2048,128]{1,0:T(8,128)(2,1)} %param.11), channel_id=1, source_target_pairs={{0,4},{4,8},{8,12},{12,14},{14,10},{10,6},{6,2},{2,0},{1,5},{5,9},... | collective-permute-start | bytes 1572872 | tf_op jit(solution)/shard_map/ppermute | solution.py:129
  3.0 1.1 %fusion.2 = (f32[1,2048]{1,0:T(1,128)S(1)}, f32[1,2048]{1,0:T(1,128)S(1)}, f32[1,2048]{1,0:T(1,128)S(1)}, f32[1,2048]{1,0:T(1,128)S(1)}, f32[1,2048]{1,0:T(1,128...) fusion(f32[3,6144]{1,0:T(4,128)} %param.8), kind=kLoop, calls=%fused_computation.25 | loop fusion | bytes 147456 | tf_op jit(solution)/shard_map/slice | solution.py:34
  4.1 3.0 %multiply_convert_fusion.1 = bf16[128,2048]{1,0:T(8,128)(2,1)S(1)} fusion(bf16[512,6144]{1,0:T(8,128)(2,1)} %param.7, f32[2048]{0:T(1024)S(1)} %bitcast.14, f32[2048]{0:T(1024)S(1)} %bitcast.16, f32[2048]{0:T(1024)S(1)} %bitcast.18, f32[2048]{0:T(1024)S(1)} %bitcast.20, f32[2048]{0:T(1024)S(1)} %bitcast.22, f32[2048]{0:T(1024)S(1)} %bitcast.24), kind=kLoop, calls=%fused_computation.3 | loop fusion | flops 4718592 | bytes 3719168 | tf_op jit(solution)/shard_map/convert_element_type | solution.py:93
  7.1 3.2 %collective-permute-start = (bf16[128,2048]{1,0:T(8,128)(2,1)S(1)}, bf16[128,2048]{1,0:T(8,128)(2,1)}, u32[]{:S(2)}, u32[]{:S(2)}) collective-permute-start(bf16[128,2048]{1,0:T(8,128)(2,1)S(1)} %multiply_convert_fusion.1), channel_id=1, source_target_pairs={{0,1},{1,2},{2,3},{3,4},{4,5},{5,6},{6,7},{7,8},{8,9},{9,10},{10,1... | collective-permute-start | bytes 1572872 | tf_op jit(solution)/shard_map/ppermute | solution.py:22
  10.3 1.1 %slice.148 = bf16[2,6144]{1,0:T(2,128)(2,1)S(1)} slice(bf16[512,6144]{1,0:T(8,128)(2,1)} %param.7), slice={[510:512], [0:6144]} | slice | bytes 49152 | tf_op jit(solution)/shard_map/slice | solution.py:146
  11.4 2.9 %collective-permute-start.1 = (bf16[2,6144]{1,0:T(2,128)(2,1)S(1)}, bf16[2,6144]{1,0:T(2,128)(2,1)S(1)}, u32[]{:S(2)}, u32[]{:S(2)}) collective-permute-start(bf16[2,6144]{1,0:T(2,128)(2,1)S(1)} %slice.148), channel_id=1, source_target_pairs={{0,1},{1,2},{2,3},{3,4},{4,5},{5,6},{6,7},{7,8},{8,9},{9,10},{10,1... | collective-permute-start | bytes 73736 | tf_op jit(solution)/shard_map/ppermute | solution.py:22
  14.4 5.9 %fusion.1 = (bf16[511,2048]{1,0:T(8,128)(2,1)S(1)}, bf16[511,2048]{1,0:T(8,128)(2,1)}, bf16[511,2048]{1,0:T(8,128)(2,1)}) fusion(bf16[512,6144]{1,0:T(8,128)(2,1)} %param.7), kind=kLoop, calls=%fused_computation.24 | loop fusion | bytes 12558336 | tf_op jit(solution)/shard_map/slice | solution.py:32
  20.2 3.0 %fusion = (bf16[510,2048]{1,0:T(8,128)(2,1)}, bf16[510,2048]{1,0:T(8,128)(2,1)}, bf16[510,2048]{1,0:T(8,128)(2,1)}) fusion(bf16[512,6144]{1,0:T(8,128)(2,1)S(1)} %bitcast.13), kind=kLoop, calls=%fused_computation.23 | loop fusion | bytes 12533760 | tf_op jit(solution)/shard_map/slice | solution.py:33
  23.2 4.3 %broadcast_in_dim.3 = bf16[2048,2048]{1,0:T(8,128)(2,1)} broadcast(bf16[]{:T(256)} %constant.75.clone.1), dimensions={} | broadcast | bytes 8388610 | tf_op jit(solution)/shard_map/broadcast_in_dim | solution.py:112
  27.5 0.9 constant_dynamic-update-slice_fusion.15
  28.6 7.6 %multiply_convert_fusion.carried_ref = bf16[512,2048]{1,0:T(8,128)(2,1)} fusion(bf16[511,2048]{1,0:T(8,128)(2,1)} %get-tuple-element.24, bf16[1,2048]{1,0:T(2,128)(2,1)S(1)} %get-tuple-element.39, bf16[510,2048]{1,0:T(8,128)(2,1)} %get-tuple-element.21, bf16[2,2048]{1,0:T(2,128)(2,1)S(1)} %get-tuple-element.36, bf16[511,2048]{1,0:T(8,128)(2,1)} %get-tuple-element.23, ...), kind=kLoop, calls=%fused_computation.2 | loop fusion | flops 31457280 | bytes 14729216 | tf_op jit(solution)/shard_map/convert_element_type | solution.py:93
  36.1 4.4 %multiply_add_fusion.gate_ref = f32[512,2048]{1,0:T(8,128)} fusion(bf16[511,2048]{1,0:T(8,128)(2,1)S(1)} %get-tuple-element.22, bf16[1,2048]{1,0:T(2,128)(2,1)S(1)} %get-tuple-element.37, bf16[510,2048]{1,0:T(8,128)(2,1)S(1)} %copy-done, bf16[2,2048]{1,0:T(2,128)(2,1)S(1)} %get-tuple-element.34, f32[2048]{0:T(1024)S(1)} %bitcast.27, f32[2048]{0:T(1024)S(1)} %bitcast.28, ...), kind=kLoop, calls=%fused_computation.1 | loop fusion | flops 14680064 | bytes 10510336 | tf_op jit(solution)/shard_map/add | solution.py:36
  40.5 1.7 %collective-permute-start.4 = (bf16[2048,128]{1,0:T(8,128)(2,1)}, bf16[2048,128]{1,0:T(8,128)(2,1)S(1)}, u32[]{:S(2)}, u32[]{:S(2)}) collective-permute-start(bf16[2048,128]{1,0:T(8,128)(2,1)} %collective-permute-done.2), channel_id=1, source_target_pairs={{0,4},{4,8},{8,12},{12,14},{14,10},{10,6},{6,2},{2,0},{1,5},{5,9},... | collective-permute-start | bytes 1572872 | tf_op jit(solution)/shard_map/ppermute | solution.py:129
  43.9 1.9 %constant_dynamic-update-slice_fusion.14 = bf16[2048,2048]{1,0:T(8,128)(2,1)} fusion(bf16[2048,2048]{1,0:T(8,128)(2,1)} %constant_dynamic-update-slice_fusion.15, bf16[2048,128]{1,0:T(8,128)(2,1)} %collective-permute-done.6, s32[]{:T(128)S(6)} %select_n.115), kind=kLoop, calls=%fused_computation.19 | loop fusion | bytes 1048580 | tf_op jit(solution)/shard_map/dynamic_update_slice | solution.py:117
  45.8 2.0 %constant_dynamic-update-slice_fusion.13 = bf16[2048,2048]{1,0:T(8,128)(2,1)} fusion(bf16[2048,2048]{1,0:T(8,128)(2,1)} %constant_dynamic-update-slice_fusion.14, bf16[2048,128]{1,0:T(8,128)(2,1)} %collective-permute-done.2, s32[]{:T(128)S(6)} %select_n.121), kind=kLoop, calls=%fused_computation.18 | loop fusion | bytes 1048580 | tf_op jit(solution)/shard_map/dynamic_update_slice | solution.py:117
  47.8 17.2 %shard_map.64 = bf16[512,2048]{1,0:T(8,128)(2,1)} custom-call(f32[128,384]{1,0:T(8,128)} %pad_convert_fusion.fw_ref, f32[1,2048]{1,0:T(1,128)} %bitcast.29, bf16[128,2048]{1,0:T(8,128)(2,1)} %collective-permute-done.halo_ref, bf16[512,2048]{1,0:T(8,128)(2,1)} %multiply_convert_fusion.carried_ref, f32[512,2048]{1,0:T(8,128)} %multiply_add_fusion.gate_ref), custom_call_target="tpu_custom_call" | custom-call | tf_op jit(solution)/shard_map/pallas_call | solution.py:69
  65.0 1.7 %collective-permute-start.11 = (bf16[2048,128]{1,0:T(8,128)(2,1)S(1)}, bf16[2048,128]{1,0:T(8,128)(2,1)S(1)}, u32[]{:S(2)}, u32[]{:S(2)}) collective-permute-start(bf16[2048,128]{1,0:T(8,128)(2,1)S(1)} %collective-permute-done.4), channel_id=1, source_target_pairs={{0,4},{4,8},{8,12},{12,14},{14,10},{10,6},{6,2},{2,0},{1,5},{5,9},... | collective-permute-start | bytes 1572872 | tf_op jit(solution)/shard_map/ppermute | solution.py:129
  67.6 0.9 constant_dynamic-update-slice_fusion.12
  68.6 1.9 %constant_dynamic-update-slice_fusion.11 = bf16[2048,2048]{1,0:T(8,128)(2,1)} fusion(bf16[2048,2048]{1,0:T(8,128)(2,1)} %constant_dynamic-update-slice_fusion.12, bf16[2048,128]{1,0:T(8,128)(2,1)} %collective-permute-done.3, s32[]{:T(128)S(6)} %select_n.125), kind=kLoop, calls=%fused_computation.16 | loop fusion | bytes 1048580 | tf_op jit(solution)/shard_map/dynamic_update_slice | solution.py:117
  70.5 0.9 constant_dynamic-update-slice_fusion.10
  71.5 0.9 constant_dynamic-update-slice_fusion.9
  72.3 6.6 %collective-permute-done.11 = bf16[2048,128]{1,0:T(8,128)(2,1)S(1)} collective-permute-done((bf16[2048,128]{1,0:T(8,128)(2,1)S(1)}, bf16[2048,128]{1,0:T(8,128)(2,1)S(1)}, u32[]{:S(2)}, u32[]{:S(2)}) %collective-permute-start.11) | collective-permute-done | bytes 524320 | tf_op jit(solution)/shard_map/ppermute | solution.py:129
  78.9 1.7 %collective-permute-start.15 = (bf16[1024,128]{1,0:T(8,128)(2,1)S(1)}, bf16[1024,128]{1,0:T(8,128)(2,1)S(1)}, u32[]{:S(2)}, u32[]{:S(2)}) collective-permute-start(bf16[1024,128]{1,0:T(8,128)(2,1)S(1)} %slice.174), channel_id=1, source_target_pairs={{0,4},{4,8},{8,12},{12,14},{14,10},{10,6},{6,2},{2,0},{1,5},{5,9},... | collective-permute-start | bytes 786440 | tf_op jit(solution)/shard_map/ppermute | solution.py:123
  82.5 0.9 constant_dynamic-update-slice_fusion.7
  83.4 0.9 constant_dynamic-update-slice_fusion.6
  84.3 0.9 constant_dynamic-update-slice_fusion.5
  85.2 1.1 %collective-permute-done.15 = bf16[1024,128]{1,0:T(8,128)(2,1)S(1)} collective-permute-done((bf16[1024,128]{1,0:T(8,128)(2,1)S(1)}, bf16[1024,128]{1,0:T(8,128)(2,1)S(1)}, u32[]{:S(2)}, u32[]{:S(2)}) %collective-permute-start.15) | collective-permute-done | bytes 262176 | tf_op jit(solution)/shard_map/ppermute | solution.py:123
  86.3 1.4 %collective-permute-done.17 = bf16[1024,128]{1,0:T(8,128)(2,1)S(1)} collective-permute-done((bf16[1024,128]{1,0:T(8,128)(2,1)S(1)}, bf16[1024,128]{1,0:T(8,128)(2,1)S(1)}, u32[]{:S(2)}, u32[]{:S(2)}) %collective-permute-start.17) | collective-permute-done | bytes 262176 | tf_op jit(solution)/shard_map/ppermute | solution.py:124
  87.7 0.9 constant_dynamic-update-slice_fusion.4
  88.6 0.9 constant_dynamic-update-slice_fusion.3
  89.5 0.9 constant_dynamic-update-slice_fusion.2
  93.5 9.2 %add_convert_fusion = bf16[512,2048]{1,0:T(8,128)(2,1)} fusion(bf16[512,2048]{1,0:T(8,128)(2,1)S(1)} %copy-done.4, bf16[512,2048]{1,0:T(8,128)(2,1)S(1)} %copy-done.1, bf16[2048,2048]{1,0:T(8,128)(2,1)} %constant_dynamic-update-slice_fusion.16), kind=kOutput, calls=%fused_computation | convolution fusion | flops 4298113024 | bytes 14680064 | tf_op jit(solution)/shard_map/dot_general | solution.py:166
  (55 shorter events, 7.8 us)
Async XLA Ops:
  0.0 40.5 %collective-permute-start.2 = (bf16[2048,128]{1,0:T(8,128)(2,1)}, bf16[2048,128]{1,0:T(8,128)(2,1)}, u32[]{:S(2)}, u32[]{:S(2)}) collective-permute-start(bf16[2048,128]{1,0:T(8,128)(2,1)} %param.11), channel_id=1, source_target_pairs={{0,4},{4,8},{8,12},{12,14},{14,10},{10,6},{6,2},{2,0},{1,5},{5,9},... | collective-permute-start | bytes 1572872 | tf_op jit(solution)/shard_map/ppermute | solution.py:129
  3.0 37.5 %collective-permute-start.3 = (bf16[2048,128]{1,0:T(8,128)(2,1)}, bf16[2048,128]{1,0:T(8,128)(2,1)}, u32[]{:S(2)}, u32[]{:S(2)}) collective-permute-start(bf16[2048,128]{1,0:T(8,128)(2,1)} %param.11), channel_id=1, source_target_pairs={{4,0},{8,4},{12,8},{14,12},{10,14},{6,10},{2,6},{0,2},{5,1},{9,5},... | collective-permute-start | bytes 1572872 | tf_op jit(solution)/shard_map/ppermute | solution.py:130
  3.0 40.4 %collective-permute-start.6 = (bf16[2048,128]{1,0:T(8,128)(2,1)}, bf16[2048,128]{1,0:T(8,128)(2,1)}, u32[]{:S(2)}, u32[]{:S(2)}) collective-permute-start(bf16[2048,128]{1,0:T(8,128)(2,1)} %param.11), channel_id=1, source_target_pairs={{0,1},{1,0},{2,3},{3,2},{4,5},{5,4},{6,7},{7,6},{8,9},{9,8},{10,11... | collective-permute-start | bytes 1572872 | tf_op jit(solution)/shard_map/ppermute | solution.py:115
  7.1 40.7 %collective-permute-start = (bf16[128,2048]{1,0:T(8,128)(2,1)S(1)}, bf16[128,2048]{1,0:T(8,128)(2,1)}, u32[]{:S(2)}, u32[]{:S(2)}) collective-permute-start(bf16[128,2048]{1,0:T(8,128)(2,1)S(1)} %multiply_convert_fusion.1), channel_id=1, source_target_pairs={{0,1},{1,2},{2,3},{3,4},{4,5},{5,6},{6,7},{7,8},{8,9},{9,10},{10,1... | collective-permute-start | bytes 1572872 | tf_op jit(solution)/shard_map/ppermute | solution.py:22
  10.3 9.9 %slice-start = ((s8[6291456]{0:T(1024)(128)(4,1)}), s8[4194304]{0:T(1024)(128)(4,1)S(1)}, s32[]{:S(2)}) async-start(s8[6291456]{0:T(1024)(128)(4,1)} %bitcast.12), calls=%async_computation | async-start | bytes 8388608
  11.4 8.8 %slice-start.1 = ((s8[6291456]{0:T(1024)(128)(4,1)}), s8[2097152]{0:T(1024)(128)(4,1)S(1)}, s32[]{:S(2)}) async-start(s8[6291456]{0:T(1024)(128)(4,1)} %bitcast.12), calls=%async_computation.1 | async-start | bytes 4194304
  11.4 17.1 %collective-permute-start.1 = (bf16[2,6144]{1,0:T(2,128)(2,1)S(1)}, bf16[2,6144]{1,0:T(2,128)(2,1)S(1)}, u32[]{:S(2)}, u32[]{:S(2)}) collective-permute-start(bf16[2,6144]{1,0:T(2,128)(2,1)S(1)} %slice.148), channel_id=1, source_target_pairs={{0,1},{1,2},{2,3},{3,4},{4,5},{5,6},{6,7},{7,8},{8,9},{9,10},{10,1... | collective-permute-start | bytes 73736 | tf_op jit(solution)/shard_map/ppermute | solution.py:22
  23.2 4.3 %copy-start.2 = (bf16[2048,128]{1,0:T(8,128)(2,1)S(1)}, bf16[2048,128]{1,0:T(8,128)(2,1)}, u32[]{:S(2)}) copy-start(bf16[2048,128]{1,0:T(8,128)(2,1)} %param.11) | copy-start | bytes 1572868
  23.2 5.2 %copy-start.3 = (bf16[128,128]{1,0:T(8,128)(2,1)S(1)}, bf16[128,128]{1,0:T(8,128)(2,1)}, u32[]{:S(2)}) copy-start(bf16[128,128]{1,0:T(8,128)(2,1)} %param.9) | copy-start | bytes 98308
  28.6 7.6 %copy-start = (bf16[510,2048]{1,0:T(8,128)(2,1)S(1)}, bf16[510,2048]{1,0:T(8,128)(2,1)}, u32[]{:S(2)}) copy-start(bf16[510,2048]{1,0:T(8,128)(2,1)} %get-tuple-element.19) | copy-start | bytes 6266884
  40.5 24.5 %collective-permute-start.4 = (bf16[2048,128]{1,0:T(8,128)(2,1)}, bf16[2048,128]{1,0:T(8,128)(2,1)S(1)}, u32[]{:S(2)}, u32[]{:S(2)}) collective-permute-start(bf16[2048,128]{1,0:T(8,128)(2,1)} %collective-permute-done.2), channel_id=1, source_target_pairs={{0,4},{4,8},{8,12},{12,14},{14,10},{10,6},{6,2},{2,0},{1,5},{5,9},... | collective-permute-start | bytes 1572872 | tf_op jit(solution)/shard_map/ppermute | solution.py:129
  42.2 22.8 %collective-permute-start.5 = (bf16[2048,128]{1,0:T(8,128)(2,1)}, bf16[2048,128]{1,0:T(8,128)(2,1)S(1)}, u32[]{:S(2)}, u32[]{:S(2)}) collective-permute-start(bf16[2048,128]{1,0:T(8,128)(2,1)} %collective-permute-done.3), channel_id=1, source_target_pairs={{4,0},{8,4},{12,8},{14,12},{10,14},{6,10},{2,6},{0,2},{5,1},{9,5},... | collective-permute-start | bytes 1572872 | tf_op jit(solution)/shard_map/ppermute | solution.py:130
  42.6 24.5 %collective-permute-start.7 = (bf16[2048,128]{1,0:T(8,128)(2,1)}, bf16[2048,128]{1,0:T(8,128)(2,1)S(1)}, u32[]{:S(2)}, u32[]{:S(2)}) collective-permute-start(bf16[2048,128]{1,0:T(8,128)(2,1)} %collective-permute-done.2), channel_id=1, source_target_pairs={{0,1},{1,0},{2,3},{3,2},{4,5},{5,4},{6,7},{7,6},{8,9},{9,8},{10,11... | collective-permute-start | bytes 1572872 | tf_op jit(solution)/shard_map/ppermute | solution.py:115
  43.4 27.1 %collective-permute-start.8 = (bf16[2048,128]{1,0:T(8,128)(2,1)}, bf16[2048,128]{1,0:T(8,128)(2,1)S(1)}, u32[]{:S(2)}, u32[]{:S(2)}) collective-permute-start(bf16[2048,128]{1,0:T(8,128)(2,1)} %collective-permute-done.3), channel_id=1, source_target_pairs={{0,1},{1,0},{2,3},{3,2},{4,5},{5,4},{6,7},{7,6},{8,9},{9,8},{10,11... | collective-permute-start | bytes 1572872 | tf_op jit(solution)/shard_map/ppermute | solution.py:115
  65.0 13.9 %collective-permute-start.11 = (bf16[2048,128]{1,0:T(8,128)(2,1)S(1)}, bf16[2048,128]{1,0:T(8,128)(2,1)S(1)}, u32[]{:S(2)}, u32[]{:S(2)}) collective-permute-start(bf16[2048,128]{1,0:T(8,128)(2,1)S(1)} %collective-permute-done.4), channel_id=1, source_target_pairs={{0,4},{4,8},{8,12},{12,14},{14,10},{10,6},{6,2},{2,0},{1,5},{5,9},... | collective-permute-start | bytes 1572872 | tf_op jit(solution)/shard_map/ppermute | solution.py:129
  66.7 13.9 %collective-permute-start.13 = (bf16[2048,128]{1,0:T(8,128)(2,1)S(1)}, bf16[2048,128]{1,0:T(8,128)(2,1)S(1)}, u32[]{:S(2)}, u32[]{:S(2)}) collective-permute-start(bf16[2048,128]{1,0:T(8,128)(2,1)S(1)} %collective-permute-done.5), channel_id=1, source_target_pairs={{4,0},{8,4},{12,8},{14,12},{10,14},{6,10},{2,6},{0,2},{5,1},{9,5},... | collective-permute-start | bytes 1572872 | tf_op jit(solution)/shard_map/ppermute | solution.py:130
  67.1 14.0 %collective-permute-start.9 = (bf16[2048,128]{1,0:T(8,128)(2,1)S(1)}, bf16[2048,128]{1,0:T(8,128)(2,1)S(1)}, u32[]{:S(2)}, u32[]{:S(2)}) collective-permute-start(bf16[2048,128]{1,0:T(8,128)(2,1)S(1)} %collective-permute-done.4), channel_id=1, source_target_pairs={{0,1},{1,0},{2,3},{3,2},{4,5},{5,4},{6,7},{7,6},{8,9},{9,8},{10,11... | collective-permute-start | bytes 1572872 | tf_op jit(solution)/shard_map/ppermute | solution.py:115
  67.1 16.2 %collective-permute-start.10 = (bf16[2048,128]{1,0:T(8,128)(2,1)S(1)}, bf16[2048,128]{1,0:T(8,128)(2,1)S(1)}, u32[]{:S(2)}, u32[]{:S(2)}) collective-permute-start(bf16[2048,128]{1,0:T(8,128)(2,1)S(1)} %collective-permute-done.5), channel_id=1, source_target_pairs={{0,1},{1,0},{2,3},{3,2},{4,5},{5,4},{6,7},{7,6},{8,9},{9,8},{10,11... | collective-permute-start | bytes 1572872 | tf_op jit(solution)/shard_map/ppermute | solution.py:115
  78.9 7.4 %collective-permute-start.15 = (bf16[1024,128]{1,0:T(8,128)(2,1)S(1)}, bf16[1024,128]{1,0:T(8,128)(2,1)S(1)}, u32[]{:S(2)}, u32[]{:S(2)}) collective-permute-start(bf16[1024,128]{1,0:T(8,128)(2,1)S(1)} %slice.174), channel_id=1, source_target_pairs={{0,4},{4,8},{8,12},{12,14},{14,10},{10,6},{6,2},{2,0},{1,5},{5,9},... | collective-permute-start | bytes 786440 | tf_op jit(solution)/shard_map/ppermute | solution.py:123
  80.6 7.1 %collective-permute-start.17 = (bf16[1024,128]{1,0:T(8,128)(2,1)S(1)}, bf16[1024,128]{1,0:T(8,128)(2,1)S(1)}, u32[]{:S(2)}, u32[]{:S(2)}) collective-permute-start(bf16[1024,128]{1,0:T(8,128)(2,1)S(1)} %slice.175), channel_id=1, source_target_pairs={{4,0},{8,4},{12,8},{14,12},{10,14},{6,10},{2,6},{0,2},{5,1},{9,5},... | collective-permute-start | bytes 786440 | tf_op jit(solution)/shard_map/ppermute | solution.py:124
  81.1 6.7 %collective-permute-start.12 = (bf16[2048,128]{1,0:T(8,128)(2,1)S(1)}, bf16[2048,128]{1,0:T(8,128)(2,1)S(1)}, u32[]{:S(2)}, u32[]{:S(2)}) collective-permute-start(bf16[2048,128]{1,0:T(8,128)(2,1)S(1)} %collective-permute-done.11), channel_id=1, source_target_pairs={{0,1},{1,0},{2,3},{3,2},{4,5},{5,4},{6,7},{7,6},{8,9},{9,8},{10,11... | collective-permute-start | bytes 1572872 | tf_op jit(solution)/shard_map/ppermute | solution.py:115
  81.1 8.4 %collective-permute-start.14 = (bf16[2048,128]{1,0:T(8,128)(2,1)S(1)}, bf16[2048,128]{1,0:T(8,128)(2,1)S(1)}, u32[]{:S(2)}, u32[]{:S(2)}) collective-permute-start(bf16[2048,128]{1,0:T(8,128)(2,1)S(1)} %collective-permute-done.13), channel_id=1, source_target_pairs={{0,1},{1,0},{2,3},{3,2},{4,5},{5,4},{6,7},{7,6},{8,9},{9,8},{10,11... | collective-permute-start | bytes 1572872 | tf_op jit(solution)/shard_map/ppermute | solution.py:115
  82.5 11.0 %copy-start.1 = (bf16[512,2048]{1,0:T(8,128)(2,1)S(1)}, bf16[512,2048]{1,0:T(8,128)(2,1)}, u32[]{:S(2)}) copy-start(bf16[512,2048]{1,0:T(8,128)(2,1)} %shard_map.64) | copy-start | bytes 6291460
  82.5 11.0 %copy-start.4 = (bf16[512,2048]{1,0:T(8,128)(2,1)S(1)}, bf16[512,2048]{1,0:T(8,128)(2,1)}, u32[]{:S(2)}) copy-start(bf16[512,2048]{1,0:T(8,128)(2,1)} %param.6) | copy-start | bytes 6291460
  86.3 4.8 %collective-permute-start.16 = (bf16[1024,128]{1,0:T(8,128)(2,1)S(1)}, bf16[1024,128]{1,0:T(8,128)(2,1)S(1)}, u32[]{:S(2)}, u32[]{:S(2)}) collective-permute-start(bf16[1024,128]{1,0:T(8,128)(2,1)S(1)} %collective-permute-done.15), channel_id=1, source_target_pairs={{0,1},{1,0},{2,3},{3,2},{4,5},{5,4},{6,7},{7,6},{8,9},{9,8},{10,11... | collective-permute-start | bytes 786440 | tf_op jit(solution)/shard_map/ppermute | solution.py:115
  87.7 4.9 %collective-permute-start.18 = (bf16[1024,128]{1,0:T(8,128)(2,1)S(1)}, bf16[1024,128]{1,0:T(8,128)(2,1)S(1)}, u32[]{:S(2)}, u32[]{:S(2)}) collective-permute-start(bf16[1024,128]{1,0:T(8,128)(2,1)S(1)} %collective-permute-done.17), channel_id=1, source_target_pairs={{0,1},{1,0},{2,3},{3,2},{4,5},{5,4},{6,7},{7,6},{8,9},{9,8},{10,11... | collective-permute-start | bytes 786440 | tf_op jit(solution)/shard_map/ppermute | solution.py:115

commit v4 on v3

--- a/solution.py
+++ b/solution.py
@@ -36,11 +36,27 @@
     return total + short_filter[2] * before
 
 
-def _gate_kernel(fw_ref, bias_ref, halo_ref, carried_ref, gate_ref, out_ref):
-    lanes = carried_ref.shape[1]
+def _gate_kernel(fw_ref, bias_ref, sf_ref, edge_ref, halo_ref, gate_ref, second_ref, carrier_ref, out_ref):
+    lanes = out_ref.shape[1]
     per_tile = fw_ref.shape[0]
     group = lanes // per_tile
-    blocks = carried_ref.shape[0] // BLOCK
+    row_count = out_ref.shape[0]
+    blocks = row_count // BLOCK
+    row = lax.broadcasted_iota(jnp.int32, (row_count, lanes), 0)
+
+    def mixed(k, ref):
+        x = ref[...].astype(jnp.float32)
+        edge = edge_ref[k].astype(jnp.float32)
+        taps = sf_ref[k]
+        previous = jnp.where(row == 0, edge[1:2], pltpu.roll(x, 1, 0))
+        before = jnp.where(row == 0, edge[0:1], jnp.where(row == 1, edge[1:2], pltpu.roll(x, 2, 0)))
+        total = taps[0:1] * x
+        total = total + taps[1:2] * previous
+        return total + taps[2:3] * before
+
+    gate_rows = mixed(0, gate_ref)
+    carried = (mixed(1, second_ref) * mixed(2, carrier_ref)).astype(jnp.bfloat16)
+
     owner = lax.broadcasted_iota(jnp.int32, (1, lanes), 1) // group
     toeplitz = []
     for i in range(per_tile):
@@ -49,36 +65,44 @@
         toeplitz.append(rolled[:, : 2 * BLOCK].astype(jnp.bfloat16))
     bias = bias_ref[...]
     for b in range(blocks):
-        before = halo_ref[...] if b == 0 else carried_ref[BLOCK * (b - 1) : BLOCK * b, :]
-        current = carried_ref[BLOCK * b : BLOCK * (b + 1), :]
+        before = halo_ref[...] if b == 0 else carried[BLOCK * (b - 1) : BLOCK * b]
+        current = carried[BLOCK * b : BLOCK * (b + 1)]
         window = jnp.concatenate([before, current], axis=0)
         acc = jnp.zeros((BLOCK, lanes), jnp.float32)
         for i in range(per_tile):
             masked = jnp.where(owner == i, window, jnp.zeros_like(window))
             acc = acc + jnp.dot(toeplitz[i], masked, preferred_element_type=jnp.float32)
-        gate = gate_ref[BLOCK * b : BLOCK * (b + 1), :]
+        gate = gate_rows[BLOCK * b : BLOCK * (b + 1)]
         direct = bias * current.astype(jnp.float32)
         out_ref[BLOCK * b : BLOCK * (b + 1), :] = (gate * (acc + direct)).astype(out_ref.dtype)
 
 
-def long_conv_gate(halo, carried, gate_rows, long_filter, conv_bias):
+def hyena_gate(halo, edge, projected, short_filter, long_filter, conv_bias):
     groups, taps = long_filter.shape
-    row_count, channels = carried.shape
+    row_count = projected.shape[0]
+    channels = halo.shape[1]
     per_tile = LANES // (channels // groups)
+    tiles = channels // LANES
     fw = jnp.pad(long_filter[:, ::-1].astype(jnp.float32), ((0, 0), (1, 3 * BLOCK - 1 - taps)))
+    edges = edge.reshape(2, 3, channels).transpose(1, 0, 2)
+    filters = short_filter.reshape(3, 3, channels).transpose(1, 0, 2)
+    column = lambda k: pl.BlockSpec((row_count, LANES), lambda j: (0, j + k * tiles))
     return pl.pallas_call(
         _gate_kernel,
-        grid=(channels // LANES,),
+        grid=(tiles,),
         in_specs=[
             pl.BlockSpec((per_tile, 3 * BLOCK), lambda j: (j, 0)),
             pl.BlockSpec((1, LANES), lambda j: (0, j)),
+            pl.BlockSpec((3, 3, LANES), lambda j: (0, 0, j)),
+            pl.BlockSpec((3, 2, LANES), lambda j: (0, 0, j)),
             pl.BlockSpec((BLOCK, LANES), lambda j: (0, j)),
-            pl.BlockSpec((row_count, LANES), lambda j: (0, j)),
-            pl.BlockSpec((row_count, LANES), lambda j: (0, j)),
+            column(0),
+            column(1),
+            column(2),
         ],
         out_specs=pl.BlockSpec((row_count, LANES), lambda j: (0, j)),
         out_shape=jax.ShapeDtypeStruct((row_count, channels), jnp.bfloat16),
-    )(fw, conv_bias.reshape(1, channels), halo, carried, gate_rows)
+    )(fw, conv_bias.reshape(1, channels), filters, edges, halo, projected, projected, projected)
 
 
 def ring_place(c, chips):
@@ -144,18 +168,11 @@
     ]
     halo = shifted(carried_of(*tail_mixed), 1)
     edge = shifted(projected[row_count - 2 :], 1)
-    mixed = [
-        short_mixed(edge[:, k * channels : (k + 1) * channels], projected[:, k * channels : (k + 1) * channels], short_filter[:, k * channels : (k + 1) * channels])
-        for k in (0, 1, 2)
-    ]
-    gate_rows = mixed[0]
-    carried = carried_of(mixed[1], mixed[2])
-
-    carried, gate_rows, ahead, behind = lax.optimization_barrier((carried, gate_rows, ahead, behind))
+    halo, edge, ahead, behind = lax.optimization_barrier((halo, edge, ahead, behind))
     if ring and steps >= 2:
         weight, ahead, behind = ring_step(2, weight, ahead, behind)
 
-    gated = long_conv_gate(halo, carried, gate_rows, long_filter, conv_bias)
+    gated = hyena_gate(halo, edge, projected, short_filter, long_filter, conv_bias)
 
     if ring:
         gated, ahead, behind = lax.optimization_barrier((gated, ahead, behind))

time: 104 us -> 84 us (0.81)
  other arithmetic: 15.7 us -> 3.71 us
  local copies, waits for them, and re-layouts: 34.2 us -> 24.1 us
  starting transfers between devices: 17 us -> 19.5 us
    slice x4 -> x0, local copies, waits for them, and re-layouts: 8.87 us -> none  [the longest x1 5.87 us: short_mixed(): rows[:-1]]
    convert_element_type x2 -> x1, other arithmetic: 10.6 us -> 2.95 us  [carried_of(): return (second * carrier).astype(jnp.bfloat16)]
    add x1 -> x0, other arithmetic: 4.37 us -> none  [short_mixed(): return total + short_filter[2] * before]
    ppermute x3, starting transfers between devices: 6.35 us -> 9.82 us  [ring_step(): ahead = lax.ppermute(ahead, 'chip', forward)]
    ppermute x2, starting transfers between devices: 6.18 us -> 3.42 us  [shifted(): return lax.ppermute(block, CTX, route)]
    ppermute x9, starting transfers between devices: 1.54 us -> 4.15 us  [place(): other = lax.ppermute(piece, 'core', swap)]
    dynamic_update_slice x18, local copies, waits for them, and re-layouts: 18.8 us -> 17.7 us  [place(): lax.dynamic_update_slice(weight, part, (row, (owner_chip * 2 + k) * width))]
  transfers between devices with their start and end apart: 19 -> 19, of which waited for: 3 -> 3; matrix products, arithmetic and copies ran while one was open for 48% -> 33% of each run, Pallas kernels for 17% -> 22%
where the time goes in v4:
time: 84 us; the launch traced here: 83.1 us
  local copies, waits for them, and re-layouts  24.1 us (29%)
  starting transfers between devices  19.5 us (23%)
  Pallas kernels  17.9 us (21%)
  matrix products  9.17 us (11%)
  waiting for transfers between devices  8.52 us (10%)
  other arithmetic  3.71 us (4%)
    pallas_call x1, Pallas kernels, hyena_gate(): pl.pallas_call(_gate_kernel, grid=(tiles,), in_specs=[pl.BlockSpec((per_t...  17.9 us
    dynamic_update_slice x18, local copies, waits for them, and re-layouts, place(): lax.dynamic_update_slice(weight, part, (row, (owner_chip * 2 + k) * width))  17.7 us
    ppermute x3, starting transfers between devices, ring_step(): ahead = lax.ppermute(ahead, 'chip', forward)  9.82 us
    dot_general x1, matrix products, on_device(): branch = jnp.dot(gated, weight, preferred_element_type=jnp.float32)  9.17 us
    ppermute x3, waiting for transfers between devices, ring_step(): ahead = lax.ppermute(ahead, 'chip', forward)  5.65 us
    broadcast_in_dim x1, local copies, waits for them, and re-layouts, on_device(): weight = jnp.zeros((channels, chips * 2 * width), out_weight.dtype)  4.33 us
    ppermute x9, starting transfers between devices, place(): other = lax.ppermute(piece, 'core', swap)  4.15 us
    ppermute x2, starting transfers between devices, shifted(): return lax.ppermute(block, CTX, route)  3.42 us
  transfers between devices with their start and end apart: 19, of which 3 were waited for; matrix products, arithmetic and copies ran while one was open for 33% of the time, Pallas kernels for 22%

profile of v4, /device:TPU:0, one launch (start us, length us, event | category | flops | bytes accessed | tf_op | source)
XLA Modules:
  0.0 83.1 jit_solution(11711955834798847740)
XLA Ops:
  0.0 3.0 %collective-permute-start.2 = (bf16[2048,128]{1,0:T(8,128)(2,1)}, bf16[2048,128]{1,0:T(8,128)(2,1)S(1)}, u32[]{:S(2)}, u32[]{:S(2)}) collective-permute-start(bf16[2048,128]{1,0:T(8,128)(2,1)} %param.11), channel_id=1, source_target_pairs={{0,4},{4,8},{8,12},{12,14},{14,10},{10,6},{6,2},{2,0},{1,5},{5,9},... | collective-permute-start | bytes 1572872 | tf_op jit(solution)/shard_map/ppermute | solution.py:153
  3.0 1.0 %fusion = (f32[1,2048]{1,0:T(1,128)S(1)}, f32[1,2048]{1,0:T(1,128)S(1)}, f32[1,2048]{1,0:T(1,128)S(1)}, f32[1,2048]{1,0:T(1,128)S(1)}, f32[1,2048]{1,0:T(1,128)S(1)}, /*index=5*/f32[1,2048]{1,0:T(1,128)S(1)}) fusion(f32[3,6144]{1,0:T(4,128)} %param.8), kind=kLoop, calls=%fused_computation.21 | loop fusion | bytes 98304 | tf_op jit(solution)/shard_map/slice | solution.py:34
  4.0 3.0 %multiply_convert_fusion = bf16[128,2048]{1,0:T(8,128)(2,1)S(1)} fusion(bf16[512,6144]{1,0:T(8,128)(2,1)} %carrier_ref.1, f32[2048]{0:T(1024)S(1)} %bitcast.20, f32[2048]{0:T(1024)S(1)} %bitcast.21, f32[2048]{0:T(1024)S(1)} %bitcast.17, f32[2048]{0:T(1024)S(1)} %bitcast.18, f32[2048]{0:T(1024)S(1)} %bitcast.19, f32[2048]{0:T(1024)S(1)} %bitcast.16), kind=kLoop, calls=%fused_computation.1 | loop fusion | flops 4718592 | bytes 3719168 | tf_op jit(solution)/shard_map/convert_element_type | solution.py:117
  7.0 1.5 %collective-permute-start = (bf16[128,2048]{1,0:T(8,128)(2,1)S(1)}, bf16[128,2048]{1,0:T(8,128)(2,1)S(1)}, u32[]{:S(2)}, u32[]{:S(2)}) collective-permute-start(bf16[128,2048]{1,0:T(8,128)(2,1)S(1)} %multiply_convert_fusion), channel_id=1, source_target_pairs={{0,1},{1,2},{2,3},{3,4},{4,5},{5,6},{6,7},{7,8},{8,9},{9,10},{10,1... | collective-permute-start | bytes 1572872 | tf_op jit(solution)/shard_map/ppermute | solution.py:22
  8.5 2.6 %collective-permute-start.6 = (bf16[2048,128]{1,0:T(8,128)(2,1)}, bf16[2048,128]{1,0:T(8,128)(2,1)S(1)}, u32[]{:S(2)}, u32[]{:S(2)}) collective-permute-start(bf16[2048,128]{1,0:T(8,128)(2,1)} %param.11), channel_id=1, source_target_pairs={{0,1},{1,0},{2,3},{3,2},{4,5},{5,4},{6,7},{7,6},{8,9},{9,8},{10,11... | collective-permute-start | bytes 1572872 | tf_op jit(solution)/shard_map/ppermute | solution.py:139
  11.0 0.9 %slice.72 = bf16[2,6144]{1,0:T(2,128)(2,1)S(1)} slice(bf16[512,6144]{1,0:T(8,128)(2,1)} %carrier_ref.1), slice={[510:512], [0:6144]} | slice | bytes 49152 | tf_op jit(solution)/shard_map/slice | solution.py:170
  11.9 1.9 %collective-permute-start.1 = (bf16[2,6144]{1,0:T(2,128)(2,1)S(1)}, bf16[2,6144]{1,0:T(2,128)(2,1)S(1)}, u32[]{:S(2)}, u32[]{:S(2)}) collective-permute-start(bf16[2,6144]{1,0:T(2,128)(2,1)S(1)} %slice.72), channel_id=1, source_target_pairs={{0,1},{1,2},{2,3},{3,4},{4,5},{5,6},{6,7},{7,8},{8,9},{9,10},{10,1... | collective-permute-start | bytes 73736 | tf_op jit(solution)/shard_map/ppermute | solution.py:22
  13.9 4.3 %broadcast_in_dim.3 = bf16[2048,2048]{1,0:T(8,128)(2,1)} broadcast(bf16[]{:T(256)} %constant.75.clone.1), dimensions={} | broadcast | bytes 8388610 | tf_op jit(solution)/shard_map/broadcast_in_dim | solution.py:136
  18.2 0.9 %constant_dynamic-update-slice_fusion.15 = bf16[2048,2048]{1,0:T(8,128)(2,1)} fusion(bf16[2048,2048]{1,0:T(8,128)(2,1)} %broadcast_in_dim.3, bf16[2048,128]{1,0:T(8,128)(2,1)S(1)} %copy-done.2, s32[]{:T(128)S(6)} %select_n.114), kind=kLoop, calls=%fused_computation.18 | loop fusion | bytes 1048580 | tf_op jit(solution)/shard_map/dynamic_update_slice | solution.py:141
  19.3 4.7 %collective-permute-start.4 = (bf16[2048,128]{1,0:T(8,128)(2,1)S(1)}, bf16[2048,128]{1,0:T(8,128)(2,1)S(1)}, u32[]{:S(2)}, u32[]{:S(2)}) collective-permute-start(bf16[2048,128]{1,0:T(8,128)(2,1)S(1)} %collective-permute-done.2), channel_id=1, source_target_pairs={{0,4},{4,8},{8,12},{12,14},{14,10},{10,6},{6,2},{2,0},{1,5},{5,9},... | collective-permute-start | bytes 1572872 | tf_op jit(solution)/shard_map/ppermute | solution.py:153
  24.0 0.8 pad_convert_fusion.fw_ref
  25.3 0.9 %constant_dynamic-update-slice_fusion.14 = bf16[2048,2048]{1,0:T(8,128)(2,1)} fusion(bf16[2048,2048]{1,0:T(8,128)(2,1)} %constant_dynamic-update-slice_fusion.15, bf16[2048,128]{1,0:T(8,128)(2,1)S(1)} %collective-permute-done.6, s32[]{:T(128)S(6)} %select_n.115), kind=kLoop, calls=%fused_computation.17 | loop fusion | bytes 1048580 | tf_op jit(solution)/shard_map/dynamic_update_slice | solution.py:141
  26.2 0.9 %constant_dynamic-update-slice_fusion.13 = bf16[2048,2048]{1,0:T(8,128)(2,1)} fusion(bf16[2048,2048]{1,0:T(8,128)(2,1)} %constant_dynamic-update-slice_fusion.14, bf16[2048,128]{1,0:T(8,128)(2,1)S(1)} %collective-permute-done.2, s32[]{:T(128)S(6)} %select_n.121), kind=kLoop, calls=%fused_computation.16 | loop fusion | bytes 1048580 | tf_op jit(solution)/shard_map/dynamic_update_slice | solution.py:141
  27.1 17.9 %shard_map.64 = bf16[512,2048]{1,0:T(8,128)(2,1)} custom-call(f32[128,384]{1,0:T(8,128)} %pad_convert_fusion.fw_ref, f32[1,2048]{1,0:T(1,128)} %bitcast.23, f32[3,3,2048]{2,1,0:T(4,128)} %bitcast.15, bf16[3,2,2048]{2,1,0:T(2,128)(2,1)} %bitcast.22, bf16[128,2048]{1,0:T(8,128)(2,1)} %copy-done.1, bf16[512,6144]{1,0:T(8,128)(2,1)} %carrier_ref.1, ...), custom_call_target="tpu_custom_call" | custom-call | tf_op jit(solution)/shard_map/pallas_call | solution.py:90
  45.1 2.1 %collective-permute-start.11 = (bf16[2048,128]{1,0:T(8,128)(2,1)S(1)}, bf16[2048,128]{1,0:T(8,128)(2,1)S(1)}, u32[]{:S(2)}, u32[]{:S(2)}) collective-permute-start(bf16[2048,128]{1,0:T(8,128)(2,1)S(1)} %collective-permute-done.4), channel_id=1, source_target_pairs={{0,4},{4,8},{8,12},{12,14},{14,10},{10,6},{6,2},{2,0},{1,5},{5,9},... | collective-permute-start | bytes 1572872 | tf_op jit(solution)/shard_map/ppermute | solution.py:153
  47.7 1.9 %constant_dynamic-update-slice_fusion.12 = bf16[2048,2048]{1,0:T(8,128)(2,1)} fusion(bf16[2048,2048]{1,0:T(8,128)(2,1)} %constant_dynamic-update-slice_fusion.13, bf16[2048,128]{1,0:T(8,128)(2,1)} %collective-permute-done.7, s32[]{:T(128)S(6)} %select_n.122), kind=kLoop, calls=%fused_computation.15 | loop fusion | bytes 1048580 | tf_op jit(solution)/shard_map/dynamic_update_slice | solution.py:141
  49.6 0.9 %constant_dynamic-update-slice_fusion.11 = bf16[2048,2048]{1,0:T(8,128)(2,1)} fusion(bf16[2048,2048]{1,0:T(8,128)(2,1)} %constant_dynamic-update-slice_fusion.12, bf16[2048,128]{1,0:T(8,128)(2,1)S(1)} %collective-permute-done.3, s32[]{:T(128)S(6)} %select_n.125), kind=kLoop, calls=%fused_computation.14 | loop fusion | bytes 1048580 | tf_op jit(solution)/shard_map/dynamic_update_slice | solution.py:141
  50.5 1.9 %constant_dynamic-update-slice_fusion.10 = bf16[2048,2048]{1,0:T(8,128)(2,1)} fusion(bf16[2048,2048]{1,0:T(8,128)(2,1)} %constant_dynamic-update-slice_fusion.11, bf16[2048,128]{1,0:T(8,128)(2,1)} %collective-permute-done.8, s32[]{:T(128)S(6)} %select_n.126), kind=kLoop, calls=%fused_computation.13 | loop fusion | bytes 1048580 | tf_op jit(solution)/shard_map/dynamic_update_slice | solution.py:141
  52.4 0.9 %constant_dynamic-update-slice_fusion.9 = bf16[2048,2048]{1,0:T(8,128)(2,1)} fusion(bf16[2048,2048]{1,0:T(8,128)(2,1)} %constant_dynamic-update-slice_fusion.10, bf16[2048,128]{1,0:T(8,128)(2,1)S(1)} %collective-permute-done.4, s32[]{:T(128)S(6)} %select_n.129), kind=kLoop, calls=%fused_computation.12 | loop fusion | bytes 1048580 | tf_op jit(solution)/shard_map/dynamic_update_slice | solution.py:141
  53.3 5.6 %collective-permute-done.11 = bf16[2048,128]{1,0:T(8,128)(2,1)S(1)} collective-permute-done((bf16[2048,128]{1,0:T(8,128)(2,1)S(1)}, bf16[2048,128]{1,0:T(8,128)(2,1)S(1)}, u32[]{:S(2)}, u32[]{:S(2)}) %collective-permute-start.11) | collective-permute-done | bytes 524320 | tf_op jit(solution)/shard_map/ppermute | solution.py:153
  58.9 2.1 %collective-permute-start.15 = (bf16[1024,128]{1,0:T(8,128)(2,1)S(1)}, bf16[1024,128]{1,0:T(8,128)(2,1)S(1)}, u32[]{:S(2)}, u32[]{:S(2)}) collective-permute-start(bf16[1024,128]{1,0:T(8,128)(2,1)S(1)} %slice.75), channel_id=1, source_target_pairs={{0,4},{4,8},{8,12},{12,14},{14,10},{10,6},{6,2},{2,0},{1,5},{5,9},... | collective-permute-start | bytes 786440 | tf_op jit(solution)/shard_map/ppermute | solution.py:147
  61.7 0.9 %constant_dynamic-update-slice_fusion.8 = bf16[2048,2048]{1,0:T(8,128)(2,1)} fusion(bf16[2048,2048]{1,0:T(8,128)(2,1)} %constant_dynamic-update-slice_fusion.9, bf16[2048,128]{1,0:T(8,128)(2,1)S(1)} %collective-permute-done.9, s32[]{:T(128)S(6)} %select_n.130), kind=kLoop, calls=%fused_computation.11 | loop fusion | bytes 1048580 | tf_op jit(solution)/shard_map/dynamic_update_slice | solution.py:141
  62.6 0.9 %constant_dynamic-update-slice_fusion.7 = bf16[2048,2048]{1,0:T(8,128)(2,1)} fusion(bf16[2048,2048]{1,0:T(8,128)(2,1)} %constant_dynamic-update-slice_fusion.8, bf16[2048,128]{1,0:T(8,128)(2,1)S(1)} %collective-permute-done.5, s32[]{:T(128)S(6)} %select_n.133), kind=kLoop, calls=%fused_computation.10 | loop fusion | bytes 1048580 | tf_op jit(solution)/shard_map/dynamic_update_slice | solution.py:141
  63.5 0.9 %constant_dynamic-update-slice_fusion.6 = bf16[2048,2048]{1,0:T(8,128)(2,1)} fusion(bf16[2048,2048]{1,0:T(8,128)(2,1)} %constant_dynamic-update-slice_fusion.7, bf16[2048,128]{1,0:T(8,128)(2,1)S(1)} %collective-permute-done.10, s32[]{:T(128)S(6)} %select_n.134), kind=kLoop, calls=%fused_computation.9 | loop fusion | bytes 1048580 | tf_op jit(solution)/shard_map/dynamic_update_slice | solution.py:141
  64.4 0.9 %constant_dynamic-update-slice_fusion.5 = bf16[2048,2048]{1,0:T(8,128)(2,1)} fusion(bf16[2048,2048]{1,0:T(8,128)(2,1)} %constant_dynamic-update-slice_fusion.6, bf16[2048,128]{1,0:T(8,128)(2,1)S(1)} %collective-permute-done.11, s32[]{:T(128)S(6)} %select_n.137), kind=kLoop, calls=%fused_computation.8 | loop fusion | bytes 1048580 | tf_op jit(solution)/shard_map/dynamic_update_slice | solution.py:141
  65.3 1.0 %collective-permute-done.15 = bf16[1024,128]{1,0:T(8,128)(2,1)S(1)} collective-permute-done((bf16[1024,128]{1,0:T(8,128)(2,1)S(1)}, bf16[1024,128]{1,0:T(8,128)(2,1)S(1)}, u32[]{:S(2)}, u32[]{:S(2)}) %collective-permute-start.15) | collective-permute-done | bytes 262176 | tf_op jit(solution)/shard_map/ppermute | solution.py:147
  66.3 1.8 %collective-permute-done.17 = bf16[1024,128]{1,0:T(8,128)(2,1)S(1)} collective-permute-done((bf16[1024,128]{1,0:T(8,128)(2,1)S(1)}, bf16[1024,128]{1,0:T(8,128)(2,1)S(1)}, u32[]{:S(2)}, u32[]{:S(2)}) %collective-permute-start.17) | collective-permute-done | bytes 262176 | tf_op jit(solution)/shard_map/ppermute | solution.py:148
  68.2 0.9 %constant_dynamic-update-slice_fusion.4 = bf16[2048,2048]{1,0:T(8,128)(2,1)} fusion(bf16[2048,2048]{1,0:T(8,128)(2,1)} %constant_dynamic-update-slice_fusion.5, bf16[2048,128]{1,0:T(8,128)(2,1)S(1)} %collective-permute-done.12, s32[]{:T(128)S(6)} %select_n.138), kind=kLoop, calls=%fused_computation.7 | loop fusion | bytes 1048580 | tf_op jit(solution)/shard_map/dynamic_update_slice | solution.py:141
  69.1 0.9 %constant_dynamic-update-slice_fusion.3 = bf16[2048,2048]{1,0:T(8,128)(2,1)} fusion(bf16[2048,2048]{1,0:T(8,128)(2,1)} %constant_dynamic-update-slice_fusion.4, bf16[2048,128]{1,0:T(8,128)(2,1)S(1)} %collective-permute-done.13, s32[]{:T(128)S(6)} %select_n.141), kind=kLoop, calls=%fused_computation.6 | loop fusion | bytes 1048580 | tf_op jit(solution)/shard_map/dynamic_update_slice | solution.py:141
  70.0 0.9 %constant_dynamic-update-slice_fusion.2 = bf16[2048,2048]{1,0:T(8,128)(2,1)} fusion(bf16[2048,2048]{1,0:T(8,128)(2,1)} %constant_dynamic-update-slice_fusion.3, bf16[2048,128]{1,0:T(8,128)(2,1)S(1)} %collective-permute-done.14, s32[]{:T(128)S(6)} %select_n.142), kind=kLoop, calls=%fused_computation.5 | loop fusion | bytes 1048580 | tf_op jit(solution)/shard_map/dynamic_update_slice | solution.py:141
  72.4 0.8 constant_dynamic-update-slice_fusion.17
  73.9 9.2 %add_convert_fusion = bf16[512,2048]{1,0:T(8,128)(2,1)} fusion(bf16[512,2048]{1,0:T(8,128)(2,1)S(1)} %copy-done.5, bf16[512,2048]{1,0:T(8,128)(2,1)S(1)} %copy-done, bf16[2048,2048]{1,0:T(8,128)(2,1)} %constant_dynamic-update-slice_fusion.16), kind=kOutput, calls=%fused_computation | convolution fusion | flops 4298113024 | bytes 14680064 | tf_op jit(solution)/shard_map/dot_general | solution.py:183
  (46 shorter events, 4.1 us)
Async XLA Ops:
  0.0 18.2 %copy-start.2 = (bf16[2048,128]{1,0:T(8,128)(2,1)S(1)}, bf16[2048,128]{1,0:T(8,128)(2,1)}, u32[]{:S(2)}) copy-start(bf16[2048,128]{1,0:T(8,128)(2,1)} %param.11) | copy-start | bytes 1572868
  0.0 19.1 %copy-start.3 = (bf16[128,128]{1,0:T(8,128)(2,1)S(1)}, bf16[128,128]{1,0:T(8,128)(2,1)}, u32[]{:S(2)}) copy-start(bf16[128,128]{1,0:T(8,128)(2,1)} %param.9) | copy-start | bytes 98308
  0.0 19.2 %collective-permute-start.2 = (bf16[2048,128]{1,0:T(8,128)(2,1)}, bf16[2048,128]{1,0:T(8,128)(2,1)S(1)}, u32[]{:S(2)}, u32[]{:S(2)}) collective-permute-start(bf16[2048,128]{1,0:T(8,128)(2,1)} %param.11), channel_id=1, source_target_pairs={{0,4},{4,8},{8,12},{12,14},{14,10},{10,6},{6,2},{2,0},{1,5},{5,9},... | collective-permute-start | bytes 1572872 | tf_op jit(solution)/shard_map/ppermute | solution.py:153
  3.0 16.2 %collective-permute-start.3 = (bf16[2048,128]{1,0:T(8,128)(2,1)}, bf16[2048,128]{1,0:T(8,128)(2,1)S(1)}, u32[]{:S(2)}, u32[]{:S(2)}) collective-permute-start(bf16[2048,128]{1,0:T(8,128)(2,1)} %param.11), channel_id=1, source_target_pairs={{4,0},{8,4},{12,8},{14,12},{10,14},{6,10},{2,6},{0,2},{5,1},{9,5},... | collective-permute-start | bytes 1572872 | tf_op jit(solution)/shard_map/ppermute | solution.py:154
  7.0 12.3 %collective-permute-start = (bf16[128,2048]{1,0:T(8,128)(2,1)S(1)}, bf16[128,2048]{1,0:T(8,128)(2,1)S(1)}, u32[]{:S(2)}, u32[]{:S(2)}) collective-permute-start(bf16[128,2048]{1,0:T(8,128)(2,1)S(1)} %multiply_convert_fusion), channel_id=1, source_target_pairs={{0,1},{1,2},{2,3},{3,4},{4,5},{5,6},{6,7},{7,8},{8,9},{9,10},{10,1... | collective-permute-start | bytes 1572872 | tf_op jit(solution)/shard_map/ppermute | solution.py:22
  8.5 16.8 %collective-permute-start.6 = (bf16[2048,128]{1,0:T(8,128)(2,1)}, bf16[2048,128]{1,0:T(8,128)(2,1)S(1)}, u32[]{:S(2)}, u32[]{:S(2)}) collective-permute-start(bf16[2048,128]{1,0:T(8,128)(2,1)} %param.11), channel_id=1, source_target_pairs={{0,1},{1,0},{2,3},{3,2},{4,5},{5,4},{6,7},{7,6},{8,9},{9,8},{10,11... | collective-permute-start | bytes 1572872 | tf_op jit(solution)/shard_map/ppermute | solution.py:139
  11.9 7.3 %collective-permute-start.1 = (bf16[2,6144]{1,0:T(2,128)(2,1)S(1)}, bf16[2,6144]{1,0:T(2,128)(2,1)S(1)}, u32[]{:S(2)}, u32[]{:S(2)}) collective-permute-start(bf16[2,6144]{1,0:T(2,128)(2,1)S(1)} %slice.72), channel_id=1, source_target_pairs={{0,1},{1,2},{2,3},{3,4},{4,5},{5,6},{6,7},{7,8},{8,9},{9,10},{10,1... | collective-permute-start | bytes 73736 | tf_op jit(solution)/shard_map/ppermute | solution.py:22
  19.2 7.9 %copy-start.4 = (bf16[2,6144]{1,0:T(2,128)(2,1)}, bf16[2,6144]{1,0:T(2,128)(2,1)S(1)}, u32[]{:S(2)}) copy-start(bf16[2,6144]{1,0:T(2,128)(2,1)S(1)} %collective-permute-done.1) | copy-start | bytes 73732
  19.3 7.8 %copy-start.1 = (bf16[128,2048]{1,0:T(8,128)(2,1)}, bf16[128,2048]{1,0:T(8,128)(2,1)S(1)}, u32[]{:S(2)}) copy-start(bf16[128,2048]{1,0:T(8,128)(2,1)S(1)} %collective-permute-done.halo_ref) | copy-start | bytes 1572868
  19.3 25.8 %collective-permute-start.4 = (bf16[2048,128]{1,0:T(8,128)(2,1)S(1)}, bf16[2048,128]{1,0:T(8,128)(2,1)S(1)}, u32[]{:S(2)}, u32[]{:S(2)}) collective-permute-start(bf16[2048,128]{1,0:T(8,128)(2,1)S(1)} %collective-permute-done.2), channel_id=1, source_target_pairs={{0,4},{4,8},{8,12},{12,14},{14,10},{10,6},{6,2},{2,0},{1,5},{5,9},... | collective-permute-start | bytes 1572872 | tf_op jit(solution)/shard_map/ppermute | solution.py:153
  24.0 21.1 %collective-permute-start.5 = (bf16[2048,128]{1,0:T(8,128)(2,1)S(1)}, bf16[2048,128]{1,0:T(8,128)(2,1)S(1)}, u32[]{:S(2)}, u32[]{:S(2)}) collective-permute-start(bf16[2048,128]{1,0:T(8,128)(2,1)S(1)} %collective-permute-done.3), channel_id=1, source_target_pairs={{4,0},{8,4},{12,8},{14,12},{10,14},{6,10},{2,6},{0,2},{5,1},{9,5},... | collective-permute-start | bytes 1572872 | tf_op jit(solution)/shard_map/ppermute | solution.py:154
  24.0 23.2 %collective-permute-start.7 = (bf16[2048,128]{1,0:T(8,128)(2,1)S(1)}, bf16[2048,128]{1,0:T(8,128)(2,1)}, u32[]{:S(2)}, u32[]{:S(2)}) collective-permute-start(bf16[2048,128]{1,0:T(8,128)(2,1)S(1)} %collective-permute-done.2), channel_id=1, source_target_pairs={{0,1},{1,0},{2,3},{3,2},{4,5},{5,4},{6,7},{7,6},{8,9},{9,8},{10,11... | collective-permute-start | bytes 1572872 | tf_op jit(solution)/shard_map/ppermute | solution.py:139
  24.8 25.7 %collective-permute-start.8 = (bf16[2048,128]{1,0:T(8,128)(2,1)S(1)}, bf16[2048,128]{1,0:T(8,128)(2,1)}, u32[]{:S(2)}, u32[]{:S(2)}) collective-permute-start(bf16[2048,128]{1,0:T(8,128)(2,1)S(1)} %collective-permute-done.3), channel_id=1, source_target_pairs={{0,1},{1,0},{2,3},{3,2},{4,5},{5,4},{6,7},{7,6},{8,9},{9,8},{10,11... | collective-permute-start | bytes 1572872 | tf_op jit(solution)/shard_map/ppermute | solution.py:139
  45.0 28.9 %copy-start = (bf16[512,2048]{1,0:T(8,128)(2,1)S(1)}, bf16[512,2048]{1,0:T(8,128)(2,1)}, u32[]{:S(2)}) copy-start(bf16[512,2048]{1,0:T(8,128)(2,1)} %shard_map.64) | copy-start | bytes 6291460
  45.0 28.9 %copy-start.5 = (bf16[512,2048]{1,0:T(8,128)(2,1)S(1)}, bf16[512,2048]{1,0:T(8,128)(2,1)}, u32[]{:S(2)}) copy-start(bf16[512,2048]{1,0:T(8,128)(2,1)} %param.6) | copy-start | bytes 6291460
  45.1 13.9 %collective-permute-start.11 = (bf16[2048,128]{1,0:T(8,128)(2,1)S(1)}, bf16[2048,128]{1,0:T(8,128)(2,1)S(1)}, u32[]{:S(2)}, u32[]{:S(2)}) collective-permute-start(bf16[2048,128]{1,0:T(8,128)(2,1)S(1)} %collective-permute-done.4), channel_id=1, source_target_pairs={{0,4},{4,8},{8,12},{12,14},{14,10},{10,6},{6,2},{2,0},{1,5},{5,9},... | collective-permute-start | bytes 1572872 | tf_op jit(solution)/shard_map/ppermute | solution.py:153
  47.1 13.9 %collective-permute-start.13 = (bf16[2048,128]{1,0:T(8,128)(2,1)S(1)}, bf16[2048,128]{1,0:T(8,128)(2,1)S(1)}, u32[]{:S(2)}, u32[]{:S(2)}) collective-permute-start(bf16[2048,128]{1,0:T(8,128)(2,1)S(1)} %collective-permute-done.5), channel_id=1, source_target_pairs={{4,0},{8,4},{12,8},{14,12},{10,14},{6,10},{2,6},{0,2},{5,1},{9,5},... | collective-permute-start | bytes 1572872 | tf_op jit(solution)/shard_map/ppermute | solution.py:154
  47.1 14.0 %collective-permute-start.9 = (bf16[2048,128]{1,0:T(8,128)(2,1)S(1)}, bf16[2048,128]{1,0:T(8,128)(2,1)S(1)}, u32[]{:S(2)}, u32[]{:S(2)}) collective-permute-start(bf16[2048,128]{1,0:T(8,128)(2,1)S(1)} %collective-permute-done.4), channel_id=1, source_target_pairs={{0,1},{1,0},{2,3},{3,2},{4,5},{5,4},{6,7},{7,6},{8,9},{9,8},{10,11... | collective-permute-start | bytes 1572872 | tf_op jit(solution)/shard_map/ppermute | solution.py:139
  47.1 16.3 %collective-permute-start.10 = (bf16[2048,128]{1,0:T(8,128)(2,1)S(1)}, bf16[2048,128]{1,0:T(8,128)(2,1)S(1)}, u32[]{:S(2)}, u32[]{:S(2)}) collective-permute-start(bf16[2048,128]{1,0:T(8,128)(2,1)S(1)} %collective-permute-done.5), channel_id=1, source_target_pairs={{0,1},{1,0},{2,3},{3,2},{4,5},{5,4},{6,7},{7,6},{8,9},{9,8},{10,11... | collective-permute-start | bytes 1572872 | tf_op jit(solution)/shard_map/ppermute | solution.py:139
  58.9 7.4 %collective-permute-start.15 = (bf16[1024,128]{1,0:T(8,128)(2,1)S(1)}, bf16[1024,128]{1,0:T(8,128)(2,1)S(1)}, u32[]{:S(2)}, u32[]{:S(2)}) collective-permute-start(bf16[1024,128]{1,0:T(8,128)(2,1)S(1)} %slice.75), channel_id=1, source_target_pairs={{0,4},{4,8},{8,12},{12,14},{14,10},{10,6},{6,2},{2,0},{1,5},{5,9},... | collective-permute-start | bytes 786440 | tf_op jit(solution)/shard_map/ppermute | solution.py:147
  61.0 7.1 %collective-permute-start.17 = (bf16[1024,128]{1,0:T(8,128)(2,1)S(1)}, bf16[1024,128]{1,0:T(8,128)(2,1)S(1)}, u32[]{:S(2)}, u32[]{:S(2)}) collective-permute-start(bf16[1024,128]{1,0:T(8,128)(2,1)S(1)} %slice.76), channel_id=1, source_target_pairs={{4,0},{8,4},{12,8},{14,12},{10,14},{6,10},{2,6},{0,2},{5,1},{9,5},... | collective-permute-start | bytes 786440 | tf_op jit(solution)/shard_map/ppermute | solution.py:148
  61.1 7.0 %collective-permute-start.12 = (bf16[2048,128]{1,0:T(8,128)(2,1)S(1)}, bf16[2048,128]{1,0:T(8,128)(2,1)S(1)}, u32[]{:S(2)}, u32[]{:S(2)}) collective-permute-start(bf16[2048,128]{1,0:T(8,128)(2,1)S(1)} %collective-permute-done.11), channel_id=1, source_target_pairs={{0,1},{1,0},{2,3},{3,2},{4,5},{5,4},{6,7},{7,6},{8,9},{9,8},{10,11... | collective-permute-start | bytes 1572872 | tf_op jit(solution)/shard_map/ppermute | solution.py:139
  61.2 8.8 %collective-permute-start.14 = (bf16[2048,128]{1,0:T(8,128)(2,1)S(1)}, bf16[2048,128]{1,0:T(8,128)(2,1)S(1)}, u32[]{:S(2)}, u32[]{:S(2)}) collective-permute-start(bf16[2048,128]{1,0:T(8,128)(2,1)S(1)} %collective-permute-done.13), channel_id=1, source_target_pairs={{0,1},{1,0},{2,3},{3,2},{4,5},{5,4},{6,7},{7,6},{8,9},{9,8},{10,11... | collective-permute-start | bytes 1572872 | tf_op jit(solution)/shard_map/ppermute | solution.py:139
  66.3 5.3 %collective-permute-start.16 = (bf16[1024,128]{1,0:T(8,128)(2,1)S(1)}, bf16[1024,128]{1,0:T(8,128)(2,1)S(1)}, u32[]{:S(2)}, u32[]{:S(2)}) collective-permute-start(bf16[1024,128]{1,0:T(8,128)(2,1)S(1)} %collective-permute-done.15), channel_id=1, source_target_pairs={{0,1},{1,0},{2,3},{3,2},{4,5},{5,4},{6,7},{7,6},{8,9},{9,8},{10,11... | collective-permute-start | bytes 786440 | tf_op jit(solution)/shard_map/ppermute | solution.py:139
  68.1 5.0 %collective-permute-start.18 = (bf16[1024,128]{1,0:T(8,128)(2,1)S(1)}, bf16[1024,128]{1,0:T(8,128)(2,1)S(1)}, u32[]{:S(2)}, u32[]{:S(2)}) collective-permute-start(bf16[1024,128]{1,0:T(8,128)(2,1)S(1)} %collective-permute-done.17), channel_id=1, source_target_pairs={{0,1},{1,0},{2,3},{3,2},{4,5},{5,4},{6,7},{7,6},{8,9},{9,8},{10,11... | collective-permute-start | bytes 786440 | tf_op jit(solution)/shard_map/ppermute | solution.py:139

commit v5 on v4

--- a/solution.py
+++ b/solution.py
@@ -77,31 +77,33 @@
         out_ref[BLOCK * b : BLOCK * (b + 1), :] = (gate * (acc + direct)).astype(out_ref.dtype)
 
 
-def hyena_gate(halo, edge, projected, short_filter, long_filter, conv_bias):
+def hyena_gate(halo, edge, projected, short_filter, long_filter, conv_bias, part, parts):
     groups, taps = long_filter.shape
     row_count = projected.shape[0]
     channels = halo.shape[1]
     per_tile = LANES // (channels // groups)
     tiles = channels // LANES
+    share = tiles // parts
+    first = part * share
     fw = jnp.pad(long_filter[:, ::-1].astype(jnp.float32), ((0, 0), (1, 3 * BLOCK - 1 - taps)))
     edges = edge.reshape(2, 3, channels).transpose(1, 0, 2)
     filters = short_filter.reshape(3, 3, channels).transpose(1, 0, 2)
-    column = lambda k: pl.BlockSpec((row_count, LANES), lambda j: (0, j + k * tiles))
+    column = lambda k: pl.BlockSpec((row_count, LANES), lambda j: (0, first + j + k * tiles))
     return pl.pallas_call(
         _gate_kernel,
-        grid=(tiles,),
+        grid=(share,),
         in_specs=[
-            pl.BlockSpec((per_tile, 3 * BLOCK), lambda j: (j, 0)),
-            pl.BlockSpec((1, LANES), lambda j: (0, j)),
-            pl.BlockSpec((3, 3, LANES), lambda j: (0, 0, j)),
-            pl.BlockSpec((3, 2, LANES), lambda j: (0, 0, j)),
-            pl.BlockSpec((BLOCK, LANES), lambda j: (0, j)),
+            pl.BlockSpec((per_tile, 3 * BLOCK), lambda j: (first + j, 0)),
+            pl.BlockSpec((1, LANES), lambda j: (0, first + j)),
+            pl.BlockSpec((3, 3, LANES), lambda j: (0, 0, first + j)),
+            pl.BlockSpec((3, 2, LANES), lambda j: (0, 0, first + j)),
+            pl.BlockSpec((BLOCK, LANES), lambda j: (0, first + j)),
             column(0),
             column(1),
             column(2),
         ],
         out_specs=pl.BlockSpec((row_count, LANES), lambda j: (0, j)),
-        out_shape=jax.ShapeDtypeStruct((row_count, channels), jnp.bfloat16),
+        out_shape=jax.ShapeDtypeStruct((row_count, share * LANES), jnp.bfloat16),
     )(fw, conv_bias.reshape(1, channels), filters, edges, halo, projected, projected, projected)
 
 
@@ -172,14 +174,20 @@
     if ring and steps >= 2:
         weight, ahead, behind = ring_step(2, weight, ahead, behind)
 
-    gated = hyena_gate(halo, edge, projected, short_filter, long_filter, conv_bias)
-
+    inputs = (halo, edge, projected, short_filter, long_filter, conv_bias)
+    first = hyena_gate(*inputs, 0, 2)
     if ring:
-        gated, ahead, behind = lax.optimization_barrier((gated, ahead, behind))
-        for step in range(3, steps + 1):
+        first, ahead, behind, inputs = lax.optimization_barrier((first, ahead, behind, inputs))
+        if steps >= 3:
+            weight, ahead, behind = ring_step(3, weight, ahead, behind)
+    second = hyena_gate(*inputs, 1, 2)
+    if ring:
+        second, ahead, behind = lax.optimization_barrier((second, ahead, behind))
+        for step in range(4, steps + 1):
             weight, ahead, behind = ring_step(step, weight, ahead, behind)
     else:
         weight = lax.all_gather(out_weight, CTX, axis=1, tiled=True)
+    gated = jnp.concatenate([first, second], axis=1)
     branch = jnp.dot(gated, weight, preferred_element_type=jnp.float32)
     return (tokens.astype(jnp.float32) + branch).astype(jnp.bfloat16)
 

time: 84 us -> 83 us (0.988)
  waiting for transfers between devices: 8.52 us -> 2.82 us
  local copies, waits for them, and re-layouts: 24.1 us -> 26.3 us
  Pallas kernels: 17.9 us -> 19.5 us
    ppermute x3, waiting for transfers between devices: 5.65 us -> 0.01 us  [ring_step(): ahead = lax.ppermute(ahead, 'chip', forward)]
    dynamic_update_slice x18, local copies, waits for them, and re-layouts: 17.7 us -> 19.8 us  [place(): lax.dynamic_update_slice(weight, part, (row, (owner_chip * 2 + k) * width))]
    pallas_call x1 -> x2, Pallas kernels: 17.9 us -> 19.5 us  [hyena_gate(): pl.pallas_call(_gate_kernel, grid=(share,), in_specs=[pl.BlockSpec((per_t...]
  transfers between devices with their start and end apart: 19 -> 19, of which waited for: 3 -> 2; matrix products, arithmetic and copies ran while one was open for 33% -> 36% of each run, Pallas kernels for 22% -> 24%
where the time goes in v5:
time: 83 us; the launch traced here: 82 us
  local copies, waits for them, and re-layouts  26.3 us (32%)
  starting transfers between devices  19.6 us (24%)
  Pallas kernels  19.5 us (23%)
  matrix products  9.18 us (11%)
  other arithmetic  4.43 us (5%)
  waiting for transfers between devices  2.82 us (3%)
    dynamic_update_slice x18, local copies, waits for them, and re-layouts, place(): lax.dynamic_update_slice(weight, part, (row, (owner_chip * 2 + k) * width))  19.8 us
    pallas_call x2, Pallas kernels, hyena_gate(): pl.pallas_call(_gate_kernel, grid=(share,), in_specs=[pl.BlockSpec((per_t...  19.5 us
    ppermute x3, starting transfers between devices, ring_step(): ahead = lax.ppermute(ahead, 'chip', forward)  9.89 us
    dot_general x1, matrix products, on_device(): branch = jnp.dot(gated, weight, preferred_element_type=jnp.float32)  9.18 us
    broadcast_in_dim x1, local copies, waits for them, and re-layouts, on_device(): weight = jnp.zeros((channels, chips * 2 * width), out_weight.dtype)  4.34 us
    ppermute x9, starting transfers between devices, place(): other = lax.ppermute(piece, 'core', swap)  4.17 us
    ppermute x2, starting transfers between devices, shifted(): return lax.ppermute(block, CTX, route)  3.42 us
    convert_element_type x1, other arithmetic, carried_of(): return (second * carrier).astype(jnp.bfloat16)  2.9 us
  transfers between devices with their start and end apart: 19, of which 2 were waited for; matrix products, arithmetic and copies ran while one was open for 36% of the time, Pallas kernels for 24%

profile of v5, /device:TPU:0, one launch (start us, length us, event | category | flops | bytes accessed | tf_op | source)
XLA Modules:
  0.0 82.0 jit_solution(13643942878967169035)
XLA Ops:
  0.0 3.0 %collective-permute-start.2 = (bf16[2048,128]{1,0:T(8,128)(2,1)}, bf16[2048,128]{1,0:T(8,128)(2,1)S(1)}, u32[]{:S(2)}, u32[]{:S(2)}) collective-permute-start(bf16[2048,128]{1,0:T(8,128)(2,1)} %param.11), channel_id=1, source_target_pairs={{0,4},{4,8},{8,12},{12,14},{14,10},{10,6},{6,2},{2,0},{1,5},{5,9},... | collective-permute-start | bytes 1572872 | tf_op jit(solution)/shard_map/ppermute | solution.py:155
  3.0 1.0 %fusion.4 = (f32[1,2048]{1,0:T(1,128)S(1)}, f32[1,2048]{1,0:T(1,128)S(1)}, f32[1,2048]{1,0:T(1,128)S(1)}, f32[1,2048]{1,0:T(1,128)S(1)}, f32[1,2048]{1,0:T(1,128)S(1)}, /*index=5*/f32[1,2048]{1,0:T(1,128)S(1)}) fusion(f32[3,6144]{1,0:T(4,128)} %param.8), kind=kLoop, calls=%fused_computation.26 | loop fusion | bytes 98304 | tf_op jit(solution)/shard_map/slice | solution.py:34
  4.0 2.9 %multiply_convert_fusion = bf16[128,2048]{1,0:T(8,128)(2,1)S(1)} fusion(bf16[512,6144]{1,0:T(8,128)(2,1)} %carrier_ref.2, f32[2048]{0:T(1024)S(1)} %bitcast.32, f32[2048]{0:T(1024)S(1)} %bitcast.28, f32[2048]{0:T(1024)S(1)} %bitcast.29, f32[2048]{0:T(1024)S(1)} %bitcast.30, f32[2048]{0:T(1024)S(1)} %bitcast.31, f32[2048]{0:T(1024)S(1)} %bitcast.27), kind=kLoop, calls=%fused_computation.4 | loop fusion | flops 4718592 | bytes 3719168 | tf_op jit(solution)/shard_map/convert_element_type | solution.py:119
  6.9 1.5 %collective-permute-start = (bf16[128,2048]{1,0:T(8,128)(2,1)S(1)}, bf16[128,2048]{1,0:T(8,128)(2,1)S(1)}, u32[]{:S(2)}, u32[]{:S(2)}) collective-permute-start(bf16[128,2048]{1,0:T(8,128)(2,1)S(1)} %multiply_convert_fusion), channel_id=1, source_target_pairs={{0,1},{1,2},{2,3},{3,4},{4,5},{5,6},{6,7},{7,8},{8,9},{9,10},{10,1... | collective-permute-start | bytes 1572872 | tf_op jit(solution)/shard_map/ppermute | solution.py:22
  8.4 2.6 %collective-permute-start.8 = (bf16[2048,128]{1,0:T(8,128)(2,1)}, bf16[2048,128]{1,0:T(8,128)(2,1)}, u32[]{:S(2)}, u32[]{:S(2)}) collective-permute-start(bf16[2048,128]{1,0:T(8,128)(2,1)} %param.11), channel_id=1, source_target_pairs={{0,1},{1,0},{2,3},{3,2},{4,5},{5,4},{6,7},{7,6},{8,9},{9,8},{10,11... | collective-permute-start | bytes 1572872 | tf_op jit(solution)/shard_map/ppermute | solution.py:141
  11.0 0.9 %slice.72 = bf16[2,6144]{1,0:T(2,128)(2,1)S(1)} slice(bf16[512,6144]{1,0:T(8,128)(2,1)} %carrier_ref.2), slice={[510:512], [0:6144]} | slice | bytes 49152 | tf_op jit(solution)/shard_map/slice | solution.py:172
  11.9 1.9 %collective-permute-start.1 = (bf16[2,6144]{1,0:T(2,128)(2,1)S(1)}, bf16[2,6144]{1,0:T(2,128)(2,1)S(1)}, u32[]{:S(2)}, u32[]{:S(2)}) collective-permute-start(bf16[2,6144]{1,0:T(2,128)(2,1)S(1)} %slice.72), channel_id=1, source_target_pairs={{0,1},{1,2},{2,3},{3,4},{4,5},{5,6},{6,7},{7,8},{8,9},{9,10},{10,1... | collective-permute-start | bytes 73736 | tf_op jit(solution)/shard_map/ppermute | solution.py:22
  13.8 4.3 %broadcast_in_dim.3 = bf16[2048,2048]{1,0:T(8,128)(2,1)} broadcast(bf16[]{:T(256)} %constant.75.clone.1), dimensions={} | broadcast | bytes 8388610 | tf_op jit(solution)/shard_map/broadcast_in_dim | solution.py:138
  18.2 0.9 %constant_dynamic-update-slice_fusion.15 = bf16[2048,2048]{1,0:T(8,128)(2,1)} fusion(bf16[2048,2048]{1,0:T(8,128)(2,1)} %broadcast_in_dim.3, bf16[2048,128]{1,0:T(8,128)(2,1)S(1)} %copy-done.3, s32[]{:T(128)S(6)} %select_n.114), kind=kLoop, calls=%fused_computation.22 | loop fusion | bytes 1048580 | tf_op jit(solution)/shard_map/dynamic_update_slice | solution.py:143
  19.2 4.8 %collective-permute-start.4 = (bf16[2048,128]{1,0:T(8,128)(2,1)S(1)}, bf16[2048,128]{1,0:T(8,128)(2,1)S(1)}, u32[]{:S(2)}, u32[]{:S(2)}) collective-permute-start(bf16[2048,128]{1,0:T(8,128)(2,1)S(1)} %collective-permute-done.2), channel_id=1, source_target_pairs={{0,4},{4,8},{8,12},{12,14},{14,10},{10,6},{6,2},{2,0},{1,5},{5,9},... | collective-permute-start | bytes 1572872 | tf_op jit(solution)/shard_map/ppermute | solution.py:155
  25.3 1.9 %constant_dynamic-update-slice_fusion.14 = bf16[2048,2048]{1,0:T(8,128)(2,1)} fusion(bf16[2048,2048]{1,0:T(8,128)(2,1)} %constant_dynamic-update-slice_fusion.15, bf16[2048,128]{1,0:T(8,128)(2,1)} %collective-permute-done.8, s32[]{:T(128)S(6)} %select_n.115), kind=kLoop, calls=%fused_computation.21 | loop fusion | bytes 1048580 | tf_op jit(solution)/shard_map/dynamic_update_slice | solution.py:143
  27.2 0.9 %constant_dynamic-update-slice_fusion.13 = bf16[2048,2048]{1,0:T(8,128)(2,1)} fusion(bf16[2048,2048]{1,0:T(8,128)(2,1)} %constant_dynamic-update-slice_fusion.14, bf16[2048,128]{1,0:T(8,128)(2,1)S(1)} %collective-permute-done.2, s32[]{:T(128)S(6)} %select_n.121), kind=kLoop, calls=%fused_computation.20 | loop fusion | bytes 1048580 | tf_op jit(solution)/shard_map/dynamic_update_slice | solution.py:143
  28.1 9.7 %shard_map.64 = bf16[512,1024]{1,0:T(8,128)(2,1)} custom-call(f32[128,384]{1,0:T(8,128)} %pad_convert_fusion.1.fw_ref, f32[1,2048]{1,0:T(1,128)} %bitcast.25, f32[3,3,2048]{2,1,0:T(4,128)} %bitcast.21, bf16[3,2,2048]{2,1,0:T(2,128)(2,1)} %bitcast.23, bf16[128,2048]{1,0:T(8,128)(2,1)} %copy-done, bf16[512,6144]{1,0:T(8,128)(2,1)} %carrier_ref.2, ...), custom_call_target="tpu_custom_call" | custom-call | tf_op jit(solution)/shard_map/pallas_call | solution.py:92
  37.9 2.1 %collective-permute-start.6 = (bf16[2048,128]{1,0:T(8,128)(2,1)S(1)}, bf16[2048,128]{1,0:T(8,128)(2,1)S(1)}, u32[]{:S(2)}, u32[]{:S(2)}) collective-permute-start(bf16[2048,128]{1,0:T(8,128)(2,1)S(1)} %collective-permute-done.4), channel_id=1, source_target_pairs={{0,4},{4,8},{8,12},{12,14},{14,10},{10,6},{6,2},{2,0},{1,5},{5,9},... | collective-permute-start | bytes 1572872 | tf_op jit(solution)/shard_map/ppermute | solution.py:155
  40.7 2.0 %constant_dynamic-update-slice_fusion.12 = bf16[2048,2048]{1,0:T(8,128)(2,1)} fusion(bf16[2048,2048]{1,0:T(8,128)(2,1)} %constant_dynamic-update-slice_fusion.13, bf16[2048,128]{1,0:T(8,128)(2,1)} %collective-permute-done.9, s32[]{:T(128)S(6)} %select_n.122), kind=kLoop, calls=%fused_computation.19 | loop fusion | bytes 1048580 | tf_op jit(solution)/shard_map/dynamic_update_slice | solution.py:143
  42.6 0.9 %constant_dynamic-update-slice_fusion.11 = bf16[2048,2048]{1,0:T(8,128)(2,1)} fusion(bf16[2048,2048]{1,0:T(8,128)(2,1)} %constant_dynamic-update-slice_fusion.12, bf16[2048,128]{1,0:T(8,128)(2,1)S(1)} %collective-permute-done.3, s32[]{:T(128)S(6)} %select_n.125), kind=kLoop, calls=%fused_computation.18 | loop fusion | bytes 1048580 | tf_op jit(solution)/shard_map/dynamic_update_slice | solution.py:143
  43.5 2.0 %constant_dynamic-update-slice_fusion.10 = bf16[2048,2048]{1,0:T(8,128)(2,1)} fusion(bf16[2048,2048]{1,0:T(8,128)(2,1)} %constant_dynamic-update-slice_fusion.11, bf16[2048,128]{1,0:T(8,128)(2,1)} %collective-permute-done.10, s32[]{:T(128)S(6)} %select_n.126), kind=kLoop, calls=%fused_computation.17 | loop fusion | bytes 1048580 | tf_op jit(solution)/shard_map/dynamic_update_slice | solution.py:143
  45.5 0.9 %constant_dynamic-update-slice_fusion.9 = bf16[2048,2048]{1,0:T(8,128)(2,1)} fusion(bf16[2048,2048]{1,0:T(8,128)(2,1)} %constant_dynamic-update-slice_fusion.10, bf16[2048,128]{1,0:T(8,128)(2,1)S(1)} %collective-permute-done.4, s32[]{:T(128)S(6)} %select_n.129), kind=kLoop, calls=%fused_computation.16 | loop fusion | bytes 1048580 | tf_op jit(solution)/shard_map/dynamic_update_slice | solution.py:143
  47.2 9.7 %shard_map.65 = bf16[512,1024]{1,0:T(8,128)(2,1)} custom-call(f32[128,384]{1,0:T(8,128)} %pad_convert_fusion.fw_ref, f32[1,2048]{1,0:T(1,128)} %bitcast.26, f32[3,3,2048]{2,1,0:T(4,128)} %bitcast.22, bf16[3,2,2048]{2,1,0:T(2,128)(2,1)} %bitcast.24, bf16[128,2048]{1,0:T(8,128)(2,1)} %copy-done, bf16[512,6144]{1,0:T(8,128)(2,1)} %carrier_ref.2, ...), custom_call_target="tpu_custom_call" | custom-call | tf_op jit(solution)/shard_map/pallas_call | solution.py:92
  57.0 2.0 %collective-permute-start.15 = (bf16[1024,128]{1,0:T(8,128)(2,1)S(1)}, bf16[1024,128]{1,0:T(8,128)(2,1)S(1)}, u32[]{:S(2)}, u32[]{:S(2)}) collective-permute-start(bf16[1024,128]{1,0:T(8,128)(2,1)S(1)} %slice.73), channel_id=1, source_target_pairs={{0,4},{4,8},{8,12},{12,14},{14,10},{10,6},{6,2},{2,0},{1,5},{5,9},... | collective-permute-start | bytes 786440 | tf_op jit(solution)/shard_map/ppermute | solution.py:149
  59.7 1.9 %constant_dynamic-update-slice_fusion.8 = bf16[2048,2048]{1,0:T(8,128)(2,1)} fusion(bf16[2048,2048]{1,0:T(8,128)(2,1)} %constant_dynamic-update-slice_fusion.9, bf16[2048,128]{1,0:T(8,128)(2,1)} %collective-permute-done.11, s32[]{:T(128)S(6)} %select_n.130), kind=kLoop, calls=%fused_computation.15 | loop fusion | bytes 1048580 | tf_op jit(solution)/shard_map/dynamic_update_slice | solution.py:143
  61.6 0.9 %constant_dynamic-update-slice_fusion.7 = bf16[2048,2048]{1,0:T(8,128)(2,1)} fusion(bf16[2048,2048]{1,0:T(8,128)(2,1)} %constant_dynamic-update-slice_fusion.8, bf16[2048,128]{1,0:T(8,128)(2,1)S(1)} %collective-permute-done.5, s32[]{:T(128)S(6)} %select_n.133), kind=kLoop, calls=%fused_computation.14 | loop fusion | bytes 1048580 | tf_op jit(solution)/shard_map/dynamic_update_slice | solution.py:143
  62.5 0.9 %constant_dynamic-update-slice_fusion.6 = bf16[2048,2048]{1,0:T(8,128)(2,1)} fusion(bf16[2048,2048]{1,0:T(8,128)(2,1)} %constant_dynamic-update-slice_fusion.7, bf16[2048,128]{1,0:T(8,128)(2,1)S(1)} %collective-permute-done.12, s32[]{:T(128)S(6)} %select_n.134), kind=kLoop, calls=%fused_computation.13 | loop fusion | bytes 1048580 | tf_op jit(solution)/shard_map/dynamic_update_slice | solution.py:143
  63.4 0.9 %constant_dynamic-update-slice_fusion.5 = bf16[2048,2048]{1,0:T(8,128)(2,1)} fusion(bf16[2048,2048]{1,0:T(8,128)(2,1)} %constant_dynamic-update-slice_fusion.6, bf16[2048,128]{1,0:T(8,128)(2,1)S(1)} %collective-permute-done.6, s32[]{:T(128)S(6)} %select_n.137), kind=kLoop, calls=%fused_computation.12 | loop fusion | bytes 1048580 | tf_op jit(solution)/shard_map/dynamic_update_slice | solution.py:143
  64.3 1.0 %collective-permute-done.15 = bf16[1024,128]{1,0:T(8,128)(2,1)S(1)} collective-permute-done((bf16[1024,128]{1,0:T(8,128)(2,1)S(1)}, bf16[1024,128]{1,0:T(8,128)(2,1)S(1)}, u32[]{:S(2)}, u32[]{:S(2)}) %collective-permute-start.15) | collective-permute-done | bytes 262176 | tf_op jit(solution)/shard_map/ppermute | solution.py:149
  65.3 1.8 %collective-permute-done.17 = bf16[1024,128]{1,0:T(8,128)(2,1)S(1)} collective-permute-done((bf16[1024,128]{1,0:T(8,128)(2,1)S(1)}, bf16[1024,128]{1,0:T(8,128)(2,1)S(1)}, u32[]{:S(2)}, u32[]{:S(2)}) %collective-permute-start.17) | collective-permute-done | bytes 262176 | tf_op jit(solution)/shard_map/ppermute | solution.py:150
  67.1 0.9 %constant_dynamic-update-slice_fusion.4 = bf16[2048,2048]{1,0:T(8,128)(2,1)} fusion(bf16[2048,2048]{1,0:T(8,128)(2,1)} %constant_dynamic-update-slice_fusion.5, bf16[2048,128]{1,0:T(8,128)(2,1)S(1)} %collective-permute-done.13, s32[]{:T(128)S(6)} %select_n.138), kind=kLoop, calls=%fused_computation.11 | loop fusion | bytes 1048580 | tf_op jit(solution)/shard_map/dynamic_update_slice | solution.py:143
  68.0 0.9 %constant_dynamic-update-slice_fusion.3 = bf16[2048,2048]{1,0:T(8,128)(2,1)} fusion(bf16[2048,2048]{1,0:T(8,128)(2,1)} %constant_dynamic-update-slice_fusion.4, bf16[2048,128]{1,0:T(8,128)(2,1)S(1)} %collective-permute-done.7, s32[]{:T(128)S(6)} %select_n.141), kind=kLoop, calls=%fused_computation.10 | loop fusion | bytes 1048580 | tf_op jit(solution)/shard_map/dynamic_update_slice | solution.py:143
  68.9 0.9 %constant_dynamic-update-slice_fusion.2 = bf16[2048,2048]{1,0:T(8,128)(2,1)} fusion(bf16[2048,2048]{1,0:T(8,128)(2,1)} %constant_dynamic-update-slice_fusion.3, bf16[2048,128]{1,0:T(8,128)(2,1)S(1)} %collective-permute-done.14, s32[]{:T(128)S(6)} %select_n.142), kind=kLoop, calls=%fused_computation.9 | loop fusion | bytes 1048580 | tf_op jit(solution)/shard_map/dynamic_update_slice | solution.py:143
  70.5 0.8 constant_dynamic-update-slice_fusion
  72.0 0.8 constant_dynamic-update-slice_fusion.16
  72.8 9.2 %add_convert_fusion = bf16[512,2048]{1,0:T(8,128)(2,1)} fusion(bf16[512,2048]{1,0:T(8,128)(2,1)S(1)} %copy-done.6, bf16[2048,2048]{1,0:T(8,128)(2,1)} %constant_dynamic-update-slice_fusion.16, bf16[512,1024]{1,0:T(8,128)(2,1)S(1)} %copy-done.2, bf16[512,1024]{1,0:T(8,128)(2,1)S(1)} %copy-done.1), kind=kOutput, calls=%fused_computation | convolution fusion | flops 4302307328 | bytes 14680064 | tf_op jit(solution)/shard_map/dot_general | solution.py:191
  (51 shorter events, 5.0 us)
Async XLA Ops:
  0.0 18.2 %copy-start.3 = (bf16[2048,128]{1,0:T(8,128)(2,1)S(1)}, bf16[2048,128]{1,0:T(8,128)(2,1)}, u32[]{:S(2)}) copy-start(bf16[2048,128]{1,0:T(8,128)(2,1)} %param.11) | copy-start | bytes 1572868
  0.0 19.0 %copy-start.4 = (bf16[128,128]{1,0:T(8,128)(2,1)S(1)}, bf16[128,128]{1,0:T(8,128)(2,1)}, u32[]{:S(2)}) copy-start(bf16[128,128]{1,0:T(8,128)(2,1)} %param.9) | copy-start | bytes 98308
  0.0 19.2 %collective-permute-start.2 = (bf16[2048,128]{1,0:T(8,128)(2,1)}, bf16[2048,128]{1,0:T(8,128)(2,1)S(1)}, u32[]{:S(2)}, u32[]{:S(2)}) collective-permute-start(bf16[2048,128]{1,0:T(8,128)(2,1)} %param.11), channel_id=1, source_target_pairs={{0,4},{4,8},{8,12},{12,14},{14,10},{10,6},{6,2},{2,0},{1,5},{5,9},... | collective-permute-start | bytes 1572872 | tf_op jit(solution)/shard_map/ppermute | solution.py:155
  3.0 16.1 %collective-permute-start.3 = (bf16[2048,128]{1,0:T(8,128)(2,1)}, bf16[2048,128]{1,0:T(8,128)(2,1)S(1)}, u32[]{:S(2)}, u32[]{:S(2)}) collective-permute-start(bf16[2048,128]{1,0:T(8,128)(2,1)} %param.11), channel_id=1, source_target_pairs={{4,0},{8,4},{12,8},{14,12},{10,14},{6,10},{2,6},{0,2},{5,1},{9,5},... | collective-permute-start | bytes 1572872 | tf_op jit(solution)/shard_map/ppermute | solution.py:156
  6.9 12.3 %collective-permute-start = (bf16[128,2048]{1,0:T(8,128)(2,1)S(1)}, bf16[128,2048]{1,0:T(8,128)(2,1)S(1)}, u32[]{:S(2)}, u32[]{:S(2)}) collective-permute-start(bf16[128,2048]{1,0:T(8,128)(2,1)S(1)} %multiply_convert_fusion), channel_id=1, source_target_pairs={{0,1},{1,2},{2,3},{3,4},{4,5},{5,6},{6,7},{7,8},{8,9},{9,10},{10,1... | collective-permute-start | bytes 1572872 | tf_op jit(solution)/shard_map/ppermute | solution.py:22
  8.4 16.9 %collective-permute-start.8 = (bf16[2048,128]{1,0:T(8,128)(2,1)}, bf16[2048,128]{1,0:T(8,128)(2,1)}, u32[]{:S(2)}, u32[]{:S(2)}) collective-permute-start(bf16[2048,128]{1,0:T(8,128)(2,1)} %param.11), channel_id=1, source_target_pairs={{0,1},{1,0},{2,3},{3,2},{4,5},{5,4},{6,7},{7,6},{8,9},{9,8},{10,11... | collective-permute-start | bytes 1572872 | tf_op jit(solution)/shard_map/ppermute | solution.py:141
  11.9 7.3 %collective-permute-start.1 = (bf16[2,6144]{1,0:T(2,128)(2,1)S(1)}, bf16[2,6144]{1,0:T(2,128)(2,1)S(1)}, u32[]{:S(2)}, u32[]{:S(2)}) collective-permute-start(bf16[2,6144]{1,0:T(2,128)(2,1)S(1)} %slice.72), channel_id=1, source_target_pairs={{0,1},{1,2},{2,3},{3,4},{4,5},{5,6},{6,7},{7,8},{8,9},{9,10},{10,1... | collective-permute-start | bytes 73736 | tf_op jit(solution)/shard_map/ppermute | solution.py:22
  19.1 9.0 %copy-start.5 = (bf16[2,6144]{1,0:T(2,128)(2,1)}, bf16[2,6144]{1,0:T(2,128)(2,1)S(1)}, u32[]{:S(2)}) copy-start(bf16[2,6144]{1,0:T(2,128)(2,1)S(1)} %collective-permute-done.1) | copy-start | bytes 73732
  19.2 9.0 %copy-start = (bf16[128,2048]{1,0:T(8,128)(2,1)}, bf16[128,2048]{1,0:T(8,128)(2,1)S(1)}, u32[]{:S(2)}) copy-start(bf16[128,2048]{1,0:T(8,128)(2,1)S(1)} %collective-permute-done.halo_ref) | copy-start | bytes 1572868
  19.2 18.7 %collective-permute-start.4 = (bf16[2048,128]{1,0:T(8,128)(2,1)S(1)}, bf16[2048,128]{1,0:T(8,128)(2,1)S(1)}, u32[]{:S(2)}, u32[]{:S(2)}) collective-permute-start(bf16[2048,128]{1,0:T(8,128)(2,1)S(1)} %collective-permute-done.2), channel_id=1, source_target_pairs={{0,4},{4,8},{8,12},{12,14},{14,10},{10,6},{6,2},{2,0},{1,5},{5,9},... | collective-permute-start | bytes 1572872 | tf_op jit(solution)/shard_map/ppermute | solution.py:155
  24.0 13.9 %collective-permute-start.5 = (bf16[2048,128]{1,0:T(8,128)(2,1)S(1)}, bf16[2048,128]{1,0:T(8,128)(2,1)S(1)}, u32[]{:S(2)}, u32[]{:S(2)}) collective-permute-start(bf16[2048,128]{1,0:T(8,128)(2,1)S(1)} %collective-permute-done.3), channel_id=1, source_target_pairs={{4,0},{8,4},{12,8},{14,12},{10,14},{6,10},{2,6},{0,2},{5,1},{9,5},... | collective-permute-start | bytes 1572872 | tf_op jit(solution)/shard_map/ppermute | solution.py:156
  24.0 16.2 %collective-permute-start.9 = (bf16[2048,128]{1,0:T(8,128)(2,1)S(1)}, bf16[2048,128]{1,0:T(8,128)(2,1)}, u32[]{:S(2)}, u32[]{:S(2)}) collective-permute-start(bf16[2048,128]{1,0:T(8,128)(2,1)S(1)} %collective-permute-done.2), channel_id=1, source_target_pairs={{0,1},{1,0},{2,3},{3,2},{4,5},{5,4},{6,7},{7,6},{8,9},{9,8},{10,11... | collective-permute-start | bytes 1572872 | tf_op jit(solution)/shard_map/ppermute | solution.py:141
  24.8 18.8 %collective-permute-start.10 = (bf16[2048,128]{1,0:T(8,128)(2,1)S(1)}, bf16[2048,128]{1,0:T(8,128)(2,1)}, u32[]{:S(2)}, u32[]{:S(2)}) collective-permute-start(bf16[2048,128]{1,0:T(8,128)(2,1)S(1)} %collective-permute-done.3), channel_id=1, source_target_pairs={{0,1},{1,0},{2,3},{3,2},{4,5},{5,4},{6,7},{7,6},{8,9},{9,8},{10,11... | collective-permute-start | bytes 1572872 | tf_op jit(solution)/shard_map/ppermute | solution.py:141
  37.9 19.0 %collective-permute-start.6 = (bf16[2048,128]{1,0:T(8,128)(2,1)S(1)}, bf16[2048,128]{1,0:T(8,128)(2,1)S(1)}, u32[]{:S(2)}, u32[]{:S(2)}) collective-permute-start(bf16[2048,128]{1,0:T(8,128)(2,1)S(1)} %collective-permute-done.4), channel_id=1, source_target_pairs={{0,4},{4,8},{8,12},{12,14},{14,10},{10,6},{6,2},{2,0},{1,5},{5,9},... | collective-permute-start | bytes 1572872 | tf_op jit(solution)/shard_map/ppermute | solution.py:155
  40.0 17.0 %collective-permute-start.7 = (bf16[2048,128]{1,0:T(8,128)(2,1)S(1)}, bf16[2048,128]{1,0:T(8,128)(2,1)S(1)}, u32[]{:S(2)}, u32[]{:S(2)}) collective-permute-start(bf16[2048,128]{1,0:T(8,128)(2,1)S(1)} %collective-permute-done.5), channel_id=1, source_target_pairs={{4,0},{8,4},{12,8},{14,12},{10,14},{6,10},{2,6},{0,2},{5,1},{9,5},... | collective-permute-start | bytes 1572872 | tf_op jit(solution)/shard_map/ppermute | solution.py:156
  40.1 19.1 %collective-permute-start.11 = (bf16[2048,128]{1,0:T(8,128)(2,1)S(1)}, bf16[2048,128]{1,0:T(8,128)(2,1)}, u32[]{:S(2)}, u32[]{:S(2)}) collective-permute-start(bf16[2048,128]{1,0:T(8,128)(2,1)S(1)} %collective-permute-done.4), channel_id=1, source_target_pairs={{0,1},{1,0},{2,3},{3,2},{4,5},{5,4},{6,7},{7,6},{8,9},{9,8},{10,11... | collective-permute-start | bytes 1572872 | tf_op jit(solution)/shard_map/ppermute | solution.py:141
  40.2 22.3 %collective-permute-start.12 = (bf16[2048,128]{1,0:T(8,128)(2,1)S(1)}, bf16[2048,128]{1,0:T(8,128)(2,1)S(1)}, u32[]{:S(2)}, u32[]{:S(2)}) collective-permute-start(bf16[2048,128]{1,0:T(8,128)(2,1)S(1)} %collective-permute-done.5), channel_id=1, source_target_pairs={{0,1},{1,0},{2,3},{3,2},{4,5},{5,4},{6,7},{7,6},{8,9},{9,8},{10,11... | collective-permute-start | bytes 1572872 | tf_op jit(solution)/shard_map/ppermute | solution.py:141
  56.9 15.9 %copy-start.1 = (bf16[512,1024]{1,0:T(8,128)(2,1)S(1)}, bf16[512,1024]{1,0:T(8,128)(2,1)}, u32[]{:S(2)}) copy-start(bf16[512,1024]{1,0:T(8,128)(2,1)} %shard_map.64) | copy-start | bytes 3145732
  56.9 15.9 %copy-start.2 = (bf16[512,1024]{1,0:T(8,128)(2,1)S(1)}, bf16[512,1024]{1,0:T(8,128)(2,1)}, u32[]{:S(2)}) copy-start(bf16[512,1024]{1,0:T(8,128)(2,1)} %shard_map.65) | copy-start | bytes 3145732
  56.9 15.9 %copy-start.6 = (bf16[512,2048]{1,0:T(8,128)(2,1)S(1)}, bf16[512,2048]{1,0:T(8,128)(2,1)}, u32[]{:S(2)}) copy-start(bf16[512,2048]{1,0:T(8,128)(2,1)} %param.6) | copy-start | bytes 6291460
  57.0 8.3 %collective-permute-start.15 = (bf16[1024,128]{1,0:T(8,128)(2,1)S(1)}, bf16[1024,128]{1,0:T(8,128)(2,1)S(1)}, u32[]{:S(2)}, u32[]{:S(2)}) collective-permute-start(bf16[1024,128]{1,0:T(8,128)(2,1)S(1)} %slice.73), channel_id=1, source_target_pairs={{0,4},{4,8},{8,12},{12,14},{14,10},{10,6},{6,2},{2,0},{1,5},{5,9},... | collective-permute-start | bytes 786440 | tf_op jit(solution)/shard_map/ppermute | solution.py:149
  59.1 8.0 %collective-permute-start.17 = (bf16[1024,128]{1,0:T(8,128)(2,1)S(1)}, bf16[1024,128]{1,0:T(8,128)(2,1)S(1)}, u32[]{:S(2)}, u32[]{:S(2)}) collective-permute-start(bf16[1024,128]{1,0:T(8,128)(2,1)S(1)} %slice.74), channel_id=1, source_target_pairs={{4,0},{8,4},{12,8},{14,12},{10,14},{6,10},{2,6},{0,2},{5,1},{9,5},... | collective-permute-start | bytes 786440 | tf_op jit(solution)/shard_map/ppermute | solution.py:150
  59.2 8.0 %collective-permute-start.13 = (bf16[2048,128]{1,0:T(8,128)(2,1)S(1)}, bf16[2048,128]{1,0:T(8,128)(2,1)S(1)}, u32[]{:S(2)}, u32[]{:S(2)}) collective-permute-start(bf16[2048,128]{1,0:T(8,128)(2,1)S(1)} %collective-permute-done.6), channel_id=1, source_target_pairs={{0,1},{1,0},{2,3},{3,2},{4,5},{5,4},{6,7},{7,6},{8,9},{9,8},{10,11... | collective-permute-start | bytes 1572872 | tf_op jit(solution)/shard_map/ppermute | solution.py:141
  59.2 9.7 %collective-permute-start.14 = (bf16[2048,128]{1,0:T(8,128)(2,1)S(1)}, bf16[2048,128]{1,0:T(8,128)(2,1)S(1)}, u32[]{:S(2)}, u32[]{:S(2)}) collective-permute-start(bf16[2048,128]{1,0:T(8,128)(2,1)S(1)} %collective-permute-done.7), channel_id=1, source_target_pairs={{0,1},{1,0},{2,3},{3,2},{4,5},{5,4},{6,7},{7,6},{8,9},{9,8},{10,11... | collective-permute-start | bytes 1572872 | tf_op jit(solution)/shard_map/ppermute | solution.py:141
  65.3 5.2 %collective-permute-start.16 = (bf16[1024,128]{1,0:T(8,128)(2,1)S(1)}, bf16[1024,128]{1,0:T(8,128)(2,1)S(1)}, u32[]{:S(2)}, u32[]{:S(2)}) collective-permute-start(bf16[1024,128]{1,0:T(8,128)(2,1)S(1)} %collective-permute-done.15), channel_id=1, source_target_pairs={{0,1},{1,0},{2,3},{3,2},{4,5},{5,4},{6,7},{7,6},{8,9},{9,8},{10,11... | collective-permute-start | bytes 786440 | tf_op jit(solution)/shard_map/ppermute | solution.py:141
  67.1 4.9 %collective-permute-start.18 = (bf16[1024,128]{1,0:T(8,128)(2,1)S(1)}, bf16[1024,128]{1,0:T(8,128)(2,1)S(1)}, u32[]{:S(2)}, u32[]{:S(2)}) collective-permute-start(bf16[1024,128]{1,0:T(8,128)(2,1)S(1)} %collective-permute-done.17), channel_id=1, source_target_pairs={{0,1},{1,0},{2,3},{3,2},{4,5},{5,4},{6,7},{7,6},{8,9},{9,8},{10,11... | collective-permute-start | bytes 786440 | tf_op jit(solution)/shard_map/ppermute | solution.py:141

commit v6 on v5

--- a/solution.py
+++ b/solution.py
@@ -137,25 +137,29 @@
 
     weight = jnp.zeros((channels, chips * 2 * width), out_weight.dtype)
 
-    def place(weight, piece, owner_chip, row=0):
-        other = lax.ppermute(piece, "core", swap)
+    def put(weight, piece, other, owner_chip, row=0):
         for k, part in ((core, piece), (1 - core, other)):
             weight = lax.dynamic_update_slice(weight, part, (row, (owner_chip * 2 + k) * width))
         return weight
+
+    def place(weight, piece, owner_chip, row=0):
+        return put(weight, piece, lax.ppermute(piece, "core", swap), owner_chip, row)
 
     def ring_step(step, weight, ahead, behind):
         if step == steps:
             half = channels // 2
             ahead = lax.ppermute(ahead[:half], "chip", forward)
             behind = lax.ppermute(behind[half:], "chip", backward)
-            source = ring_chip((position - step) % chips, chips)
-            weight = place(weight, ahead, source, 0)
-            weight = place(weight, behind, source, half)
+            sources = (ring_chip((position - step) % chips, chips),) * 2
+            rows = (0, half)
         else:
             ahead = lax.ppermute(ahead, "chip", forward)
             behind = lax.ppermute(behind, "chip", backward)
-            weight = place(weight, ahead, ring_chip((position - step) % chips, chips))
-            weight = place(weight, behind, ring_chip((position + step) % chips, chips))
+            sources = (ring_chip((position - step) % chips, chips), ring_chip((position + step) % chips, chips))
+            rows = (0, 0)
+        others = lax.ppermute(jnp.stack([ahead, behind]), "core", swap)
+        weight = put(weight, ahead, others[0], sources[0], rows[0])
+        weight = put(weight, behind, others[1], sources[1], rows[1])
         return weight, ahead, behind
 
     ahead = behind = out_weight

time: 83 us -> 85.9 us (1.035)
  other arithmetic: 4.43 us -> 7.82 us
  local copies, waits for them, and re-layouts: 26.3 us -> 28.3 us
  waiting for transfers between devices: 2.82 us -> 1.23 us
  starting transfers between devices: 19.6 us -> 18.6 us
    another operation x0 -> x4, other arithmetic: none -> 3.38 us  [ring_step(): others = lax.ppermute(jnp.stack([ahead, behind]), 'core', swap)]
    dynamic_update_slice x18, local copies, waits for them, and re-layouts: 19.8 us -> 21.9 us  [put(): lax.dynamic_update_slice(weight, part, (row, (owner_chip * 2 + k) * width))]
    ppermute x9 -> x5, starting transfers between devices: 4.17 us -> 3.13 us  [the longest x1 2.56 us: place(): lax.ppermute(piece, 'core', swap)]
    ppermute x1, waiting for transfers between devices: 1 us -> 0.01 us  [ring_step(): ahead = lax.ppermute(ahead[:half], 'chip', forward)]
  transfers between devices with their start and end apart: 19 -> 15, of which waited for: 2 -> 2; matrix products, arithmetic and copies ran while one was open for 36% -> 40% of each run, Pallas kernels for 24% -> 23%
where the time goes in v6:
time: 85.9 us; the launch traced here: 84.8 us
  local copies, waits for them, and re-layouts  28.3 us (33%)
  Pallas kernels  19.5 us (23%)
  starting transfers between devices  18.6 us (22%)
  matrix products  9.18 us (11%)
  other arithmetic  7.82 us (9%)
  waiting for transfers between devices  1.23 us (1%)
    dynamic_update_slice x18, local copies, waits for them, and re-layouts, put(): lax.dynamic_update_slice(weight, part, (row, (owner_chip * 2 + k) * width))  21.9 us
    pallas_call x2, Pallas kernels, hyena_gate(): pl.pallas_call(_gate_kernel, grid=(share,), in_specs=[pl.BlockSpec((per_t...  19.5 us
    ppermute x3, starting transfers between devices, ring_step(): ahead = lax.ppermute(ahead, 'chip', forward)  9.9 us
    dot_general x1, matrix products, on_device(): branch = jnp.dot(gated, weight, preferred_element_type=jnp.float32)  9.18 us
    broadcast_in_dim x1, local copies, waits for them, and re-layouts, on_device(): weight = jnp.zeros((channels, chips * 2 * width), out_weight.dtype)  4.32 us
    ppermute x2, starting transfers between devices, shifted(): return lax.ppermute(block, CTX, route)  3.42 us
    another operation x4, other arithmetic, ring_step(): others = lax.ppermute(jnp.stack([ahead, behind]), 'core', swap)  3.38 us
    convert_element_type x1, other arithmetic, carried_of(): return (second * carrier).astype(jnp.bfloat16)  2.9 us
  transfers between devices with their start and end apart: 15, of which 2 were waited for; matrix products, arithmetic and copies ran while one was open for 40% of the time, Pallas kernels for 23%

profile of v6, /device:TPU:0, one launch (start us, length us, event | category | flops | bytes accessed | tf_op | source)
XLA Modules:
  0.0 84.8 jit_solution(9132310175888149531)
XLA Ops:
  0.0 3.0 %collective-permute-start.2 = (bf16[2048,128]{1,0:T(8,128)(2,1)}, bf16[2048,128]{1,0:T(8,128)(2,1)S(1)}, u32[]{:S(2)}, u32[]{:S(2)}) collective-permute-start(bf16[2048,128]{1,0:T(8,128)(2,1)} %param.11), channel_id=1, source_target_pairs={{0,4},{4,8},{8,12},{12,14},{14,10},{10,6},{6,2},{2,0},{1,5},{5,9},... | collective-permute-start | bytes 1572872 | tf_op jit(solution)/shard_map/ppermute | solution.py:156
  3.0 1.0 %fusion.12 = (f32[1,2048]{1,0:T(1,128)S(1)}, f32[1,2048]{1,0:T(1,128)S(1)}, f32[1,2048]{1,0:T(1,128)S(1)}, f32[1,2048]{1,0:T(1,128)S(1)}, f32[1,2048]{1,0:T(1,128)S(1)}, /*index=5*/f32[1,2048]{1,0:T(1,128)S(1)}) fusion(f32[3,6144]{1,0:T(4,128)} %param.8), kind=kLoop, calls=%fused_computation.38 | loop fusion | bytes 98304 | tf_op jit(solution)/shard_map/slice | solution.py:34
  4.0 2.9 %multiply_convert_fusion = bf16[128,2048]{1,0:T(8,128)(2,1)S(1)} fusion(bf16[512,6144]{1,0:T(8,128)(2,1)} %carrier_ref.2, f32[2048]{0:T(1024)S(1)} %bitcast.79, f32[2048]{0:T(1024)S(1)} %bitcast.75, f32[2048]{0:T(1024)S(1)} %bitcast.76, f32[2048]{0:T(1024)S(1)} %bitcast.77, f32[2048]{0:T(1024)S(1)} %bitcast.78, f32[2048]{0:T(1024)S(1)} %bitcast.74), kind=kLoop, calls=%fused_computation.7 | loop fusion | flops 4718592 | bytes 3719168 | tf_op jit(solution)/shard_map/convert_element_type | solution.py:119
  6.9 1.5 %collective-permute-start = (bf16[128,2048]{1,0:T(8,128)(2,1)S(1)}, bf16[128,2048]{1,0:T(8,128)(2,1)S(1)}, u32[]{:S(2)}, u32[]{:S(2)}) collective-permute-start(bf16[128,2048]{1,0:T(8,128)(2,1)S(1)} %multiply_convert_fusion), channel_id=1, source_target_pairs={{0,1},{1,2},{2,3},{3,4},{4,5},{5,6},{6,7},{7,8},{8,9},{9,10},{10,1... | collective-permute-start | bytes 1572872 | tf_op jit(solution)/shard_map/ppermute | solution.py:22
  8.4 2.6 %collective-permute-start.8 = (bf16[2048,128]{1,0:T(8,128)(2,1)}, bf16[2048,128]{1,0:T(8,128)(2,1)}, u32[]{:S(2)}, u32[]{:S(2)}) collective-permute-start(bf16[2048,128]{1,0:T(8,128)(2,1)} %param.11), channel_id=1, source_target_pairs={{0,1},{1,0},{2,3},{3,2},{4,5},{5,4},{6,7},{7,6},{8,9},{9,8},{10,11... | collective-permute-start | bytes 1572872 | tf_op jit(solution)/shard_map/ppermute | solution.py:146
  11.0 0.9 %slice.96 = bf16[2,6144]{1,0:T(2,128)(2,1)S(1)} slice(bf16[512,6144]{1,0:T(8,128)(2,1)} %carrier_ref.2), slice={[510:512], [0:6144]} | slice | bytes 49152 | tf_op jit(solution)/shard_map/slice | solution.py:176
  11.9 1.9 %collective-permute-start.1 = (bf16[2,6144]{1,0:T(2,128)(2,1)S(1)}, bf16[2,6144]{1,0:T(2,128)(2,1)S(1)}, u32[]{:S(2)}, u32[]{:S(2)}) collective-permute-start(bf16[2,6144]{1,0:T(2,128)(2,1)S(1)} %slice.96), channel_id=1, source_target_pairs={{0,1},{1,2},{2,3},{3,4},{4,5},{5,6},{6,7},{7,8},{8,9},{9,10},{10,1... | collective-permute-start | bytes 73736 | tf_op jit(solution)/shard_map/ppermute | solution.py:22
  13.8 4.3 %broadcast_in_dim.3 = bf16[2048,2048]{1,0:T(8,128)(2,1)} broadcast(bf16[]{:T(256)} %constant.75.clone.1), dimensions={} | broadcast | bytes 8388610 | tf_op jit(solution)/shard_map/broadcast_in_dim | solution.py:138
  18.1 0.9 %constant_dynamic-update-slice_fusion.8 = bf16[2048,2048]{1,0:T(8,128)(2,1)} fusion(bf16[2048,2048]{1,0:T(8,128)(2,1)} %broadcast_in_dim.3, bf16[2048,128]{1,0:T(8,128)(2,1)S(1)} %copy-done.3, s32[]{:T(128)S(6)} %select_n.114), kind=kLoop, calls=%fused_computation.35 | loop fusion | bytes 1048580 | tf_op jit(solution)/shard_map/dynamic_update_slice | solution.py:142
  19.2 4.8 %collective-permute-start.4 = (bf16[2048,128]{1,0:T(8,128)(2,1)S(1)}, bf16[2048,128]{1,0:T(8,128)(2,1)}, u32[]{:S(2)}, u32[]{:S(2)}) collective-permute-start(bf16[2048,128]{1,0:T(8,128)(2,1)S(1)} %collective-permute-done.2), channel_id=1, source_target_pairs={{0,4},{4,8},{8,12},{12,14},{14,10},{10,6},{6,2},{2,0},{1,5},{5,9},... | collective-permute-start | bytes 1572872 | tf_op jit(solution)/shard_map/ppermute | solution.py:156
  24.8 1.1 %pad_maximum_fusion = bf16[2,2048,128]{2,1,0:T(8,128)(2,1)} fusion(bf16[1,2048,128]{2,1,0:T(8,128)(2,1)S(1)} %bitcast.63, bf16[1,2048,128]{2,1,0:T(8,128)(2,1)S(1)} %bitcast.64), kind=kLoop, calls=%fused_computation.4 | loop fusion | flops 524288 | bytes 2097152 | tf_op jit(solution)/shard_map/stack | solution.py:160
  25.8 9.8 %shard_map.64 = bf16[512,1024]{1,0:T(8,128)(2,1)} custom-call(f32[128,384]{1,0:T(8,128)} %pad_convert_fusion.1.fw_ref, f32[1,2048]{1,0:T(1,128)} %bitcast.72, f32[3,3,2048]{2,1,0:T(4,128)} %bitcast.68, bf16[3,2,2048]{2,1,0:T(2,128)(2,1)} %bitcast.70, bf16[128,2048]{1,0:T(8,128)(2,1)} %copy-done, bf16[512,6144]{1,0:T(8,128)(2,1)} %carrier_ref.2, ...), custom_call_target="tpu_custom_call" | custom-call | tf_op jit(solution)/shard_map/pallas_call | solution.py:92
  35.6 2.0 %constant_dynamic-update-slice_fusion.7 = bf16[2048,2048]{1,0:T(8,128)(2,1)} fusion(bf16[2048,2048]{1,0:T(8,128)(2,1)} %constant_dynamic-update-slice_fusion.8, bf16[2048,128]{1,0:T(8,128)(2,1)} %collective-permute-done.8, s32[]{:T(128)S(6)} %select_n.115), kind=kLoop, calls=%fused_computation.34 | loop fusion | bytes 1048580 | tf_op jit(solution)/shard_map/dynamic_update_slice | solution.py:142
  37.6 2.1 %collective-permute-start.6 = (bf16[2048,128]{1,0:T(8,128)(2,1)}, bf16[2048,128]{1,0:T(8,128)(2,1)S(1)}, u32[]{:S(2)}, u32[]{:S(2)}) collective-permute-start(bf16[2048,128]{1,0:T(8,128)(2,1)} %collective-permute-done.4), channel_id=1, source_target_pairs={{0,4},{4,8},{8,12},{12,14},{14,10},{10,6},{6,2},{2,0},{1,5},{5,9},... | collective-permute-start | bytes 1572872 | tf_op jit(solution)/shard_map/ppermute | solution.py:156
  39.6 0.9 %constant_dynamic-update-slice_fusion.6 = bf16[2048,2048]{1,0:T(8,128)(2,1)} fusion(bf16[2048,2048]{1,0:T(8,128)(2,1)} %constant_dynamic-update-slice_fusion.7, bf16[2048,128]{1,0:T(8,128)(2,1)S(1)} %collective-permute-done.2, s32[]{:T(128)S(6)} %select_n.121), kind=kLoop, calls=%fused_computation.33 | loop fusion | bytes 1048580 | tf_op jit(solution)/shard_map/dynamic_update_slice | solution.py:142
  40.6 2.2 %pad_maximum_fusion.1 = bf16[2,2048,128]{2,1,0:T(8,128)(2,1)} fusion(bf16[1,2048,128]{2,1,0:T(8,128)(2,1)S(1)} %bitcast.65, bf16[1,2048,128]{2,1,0:T(8,128)(2,1)} %bitcast.20), kind=kLoop, calls=%fused_computation.5 | loop fusion | flops 524288 | bytes 2097152 | tf_op jit(solution)/shard_map/stack | solution.py:160
  43.0 0.8 pad_convert_fusion.fw_ref
  43.8 9.8 %shard_map.65 = bf16[512,1024]{1,0:T(8,128)(2,1)} custom-call(f32[128,384]{1,0:T(8,128)} %pad_convert_fusion.fw_ref, f32[1,2048]{1,0:T(1,128)} %bitcast.73, f32[3,3,2048]{2,1,0:T(4,128)} %bitcast.69, bf16[3,2,2048]{2,1,0:T(2,128)(2,1)} %bitcast.71, bf16[128,2048]{1,0:T(8,128)(2,1)} %copy-done, bf16[512,6144]{1,0:T(8,128)(2,1)} %carrier_ref.2, ...), custom_call_target="tpu_custom_call" | custom-call | tf_op jit(solution)/shard_map/pallas_call | solution.py:92
  54.1 2.0 %collective-permute-start.12 = (bf16[1024,128]{1,0:T(8,128)(2,1)S(1)}, bf16[1024,128]{1,0:T(8,128)(2,1)S(1)}, u32[]{:S(2)}, u32[]{:S(2)}) collective-permute-start(bf16[1024,128]{1,0:T(8,128)(2,1)S(1)} %slice.103), channel_id=1, source_target_pairs={{0,4},{4,8},{8,12},{12,14},{14,10},{10,6},{6,2},{2,0},{1,5},{5,9},... | collective-permute-start | bytes 786440 | tf_op jit(solution)/shard_map/ppermute | solution.py:151
  56.3 2.0 %fusion.8 = bf16[2048,2048]{1,0:T(8,128)(2,1)} fusion(bf16[2048,2048]{1,0:T(8,128)(2,1)} %constant_dynamic-update-slice_fusion.6, s32[]{:T(128)S(6)} %select_n.122, bf16[2,2048,128]{2,1,0:T(8,128)(2,1)} %collective-permute-done.9), kind=kLoop, calls=%fused_computation.19 | loop fusion | bytes 1048580 | tf_op jit(solution)/shard_map/dynamic_update_slice | solution.py:142
  58.2 0.9 %constant_dynamic-update-slice_fusion.5 = bf16[2048,2048]{1,0:T(8,128)(2,1)} fusion(bf16[2048,2048]{1,0:T(8,128)(2,1)} %fusion.8, bf16[2048,128]{1,0:T(8,128)(2,1)S(1)} %collective-permute-done.3, s32[]{:T(128)S(6)} %select_n.125), kind=kLoop, calls=%fused_computation.32 | loop fusion | bytes 1048580 | tf_op jit(solution)/shard_map/dynamic_update_slice | solution.py:142
  59.1 2.0 %fusion.7 = bf16[2048,2048]{1,0:T(8,128)(2,1)} fusion(bf16[2048,2048]{1,0:T(8,128)(2,1)} %constant_dynamic-update-slice_fusion.5, s32[]{:T(128)S(6)} %select_n.126, bf16[2,2048,128]{2,1,0:T(8,128)(2,1)} %collective-permute-done.9), kind=kLoop, calls=%fused_computation.17 | loop fusion | bytes 1048580 | tf_op jit(solution)/shard_map/dynamic_update_slice | solution.py:142
  61.1 1.9 %constant_dynamic-update-slice_fusion.4 = bf16[2048,2048]{1,0:T(8,128)(2,1)} fusion(bf16[2048,2048]{1,0:T(8,128)(2,1)} %fusion.7, bf16[2048,128]{1,0:T(8,128)(2,1)} %collective-permute-done.4, s32[]{:T(128)S(6)} %select_n.129), kind=kLoop, calls=%fused_computation.31 | loop fusion | bytes 1048580 | tf_op jit(solution)/shard_map/dynamic_update_slice | solution.py:142
  63.1 1.1 %collective-permute-done.13 = bf16[1024,128]{1,0:T(8,128)(2,1)S(1)} collective-permute-done((bf16[1024,128]{1,0:T(8,128)(2,1)S(1)}, bf16[1024,128]{1,0:T(8,128)(2,1)S(1)}, u32[]{:S(2)}, u32[]{:S(2)}) %collective-permute-start.13) | collective-permute-done | bytes 262176 | tf_op jit(solution)/shard_map/ppermute | solution.py:152
  64.3 1.9 %fusion.6 = bf16[2048,2048]{1,0:T(8,128)(2,1)} fusion(bf16[2048,2048]{1,0:T(8,128)(2,1)} %constant_dynamic-update-slice_fusion.4, s32[]{:T(128)S(6)} %select_n.130, bf16[2,2048,128]{2,1,0:T(8,128)(2,1)} %collective-permute-done.10), kind=kLoop, calls=%fused_computation.15 | loop fusion | bytes 1048580 | tf_op jit(solution)/shard_map/dynamic_update_slice | solution.py:142
  66.2 0.9 %constant_dynamic-update-slice_fusion.3 = bf16[2048,2048]{1,0:T(8,128)(2,1)} fusion(bf16[2048,2048]{1,0:T(8,128)(2,1)} %fusion.6, bf16[2048,128]{1,0:T(8,128)(2,1)S(1)} %collective-permute-done.5, s32[]{:T(128)S(6)} %select_n.133), kind=kLoop, calls=%fused_computation.30 | loop fusion | bytes 1048580 | tf_op jit(solution)/shard_map/dynamic_update_slice | solution.py:142
  67.1 1.9 %fusion.5 = bf16[2048,2048]{1,0:T(8,128)(2,1)} fusion(bf16[2048,2048]{1,0:T(8,128)(2,1)} %constant_dynamic-update-slice_fusion.3, s32[]{:T(128)S(6)} %select_n.134, bf16[2,2048,128]{2,1,0:T(8,128)(2,1)} %collective-permute-done.10), kind=kLoop, calls=%fused_computation.13 | loop fusion | bytes 1048580 | tf_op jit(solution)/shard_map/dynamic_update_slice | solution.py:142
  69.0 0.9 %constant_dynamic-update-slice_fusion.2 = bf16[2048,2048]{1,0:T(8,128)(2,1)} fusion(bf16[2048,2048]{1,0:T(8,128)(2,1)} %fusion.5, bf16[2048,128]{1,0:T(8,128)(2,1)S(1)} %collective-permute-done.6, s32[]{:T(128)S(6)} %select_n.137), kind=kLoop, calls=%fused_computation.29 | loop fusion | bytes 1048580 | tf_op jit(solution)/shard_map/dynamic_update_slice | solution.py:142
  69.9 0.9 %fusion.4 = bf16[2048,2048]{1,0:T(8,128)(2,1)} fusion(bf16[2048,2048]{1,0:T(8,128)(2,1)} %constant_dynamic-update-slice_fusion.2, s32[]{:T(128)S(6)} %select_n.138, bf16[2,2048,128]{2,1,0:T(8,128)(2,1)S(1)} %collective-permute-done.11), kind=kLoop, calls=%fused_computation.11 | loop fusion | bytes 1048580 | tf_op jit(solution)/shard_map/dynamic_update_slice | solution.py:142
  70.8 0.9 %constant_dynamic-update-slice_fusion.1 = bf16[2048,2048]{1,0:T(8,128)(2,1)} fusion(bf16[2048,2048]{1,0:T(8,128)(2,1)} %fusion.4, bf16[2048,128]{1,0:T(8,128)(2,1)S(1)} %collective-permute-done.7, s32[]{:T(128)S(6)} %select_n.141), kind=kLoop, calls=%fused_computation.28 | loop fusion | bytes 1048580 | tf_op jit(solution)/shard_map/dynamic_update_slice | solution.py:142
  71.7 0.9 %fusion.3 = bf16[2048,2048]{1,0:T(8,128)(2,1)} fusion(bf16[2048,2048]{1,0:T(8,128)(2,1)} %constant_dynamic-update-slice_fusion.1, s32[]{:T(128)S(6)} %select_n.142, bf16[2,2048,128]{2,1,0:T(8,128)(2,1)S(1)} %collective-permute-done.11), kind=kLoop, calls=%fused_computation.9 | loop fusion | bytes 1048580 | tf_op jit(solution)/shard_map/dynamic_update_slice | solution.py:142
  75.6 9.2 %add_convert_fusion = bf16[512,2048]{1,0:T(8,128)(2,1)} fusion(bf16[512,2048]{1,0:T(8,128)(2,1)S(1)} %copy-done.6, bf16[2048,2048]{1,0:T(8,128)(2,1)} %fusion.9, bf16[512,1024]{1,0:T(8,128)(2,1)S(1)} %copy-done.2, bf16[512,1024]{1,0:T(8,128)(2,1)S(1)} %copy-done.1), kind=kOutput, calls=%fused_computation | convolution fusion | flops 4302307328 | bytes 14680064 | tf_op jit(solution)/shard_map/dot_general | solution.py:195
  (47 shorter events, 5.0 us)
Async XLA Ops:
  0.0 18.1 %copy-start.3 = (bf16[2048,128]{1,0:T(8,128)(2,1)S(1)}, bf16[2048,128]{1,0:T(8,128)(2,1)}, u32[]{:S(2)}) copy-start(bf16[2048,128]{1,0:T(8,128)(2,1)} %param.11) | copy-start | bytes 1572868
  0.0 19.0 %copy-start.4 = (bf16[128,128]{1,0:T(8,128)(2,1)S(1)}, bf16[128,128]{1,0:T(8,128)(2,1)}, u32[]{:S(2)}) copy-start(bf16[128,128]{1,0:T(8,128)(2,1)} %param.9) | copy-start | bytes 98308
  0.0 19.1 %collective-permute-start.2 = (bf16[2048,128]{1,0:T(8,128)(2,1)}, bf16[2048,128]{1,0:T(8,128)(2,1)S(1)}, u32[]{:S(2)}, u32[]{:S(2)}) collective-permute-start(bf16[2048,128]{1,0:T(8,128)(2,1)} %param.11), channel_id=1, source_target_pairs={{0,4},{4,8},{8,12},{12,14},{14,10},{10,6},{6,2},{2,0},{1,5},{5,9},... | collective-permute-start | bytes 1572872 | tf_op jit(solution)/shard_map/ppermute | solution.py:156
  3.0 16.1 %collective-permute-start.3 = (bf16[2048,128]{1,0:T(8,128)(2,1)}, bf16[2048,128]{1,0:T(8,128)(2,1)S(1)}, u32[]{:S(2)}, u32[]{:S(2)}) collective-permute-start(bf16[2048,128]{1,0:T(8,128)(2,1)} %param.11), channel_id=1, source_target_pairs={{4,0},{8,4},{12,8},{14,12},{10,14},{6,10},{2,6},{0,2},{5,1},{9,5},... | collective-permute-start | bytes 1572872 | tf_op jit(solution)/shard_map/ppermute | solution.py:157
  6.9 12.3 %collective-permute-start = (bf16[128,2048]{1,0:T(8,128)(2,1)S(1)}, bf16[128,2048]{1,0:T(8,128)(2,1)S(1)}, u32[]{:S(2)}, u32[]{:S(2)}) collective-permute-start(bf16[128,2048]{1,0:T(8,128)(2,1)S(1)} %multiply_convert_fusion), channel_id=1, source_target_pairs={{0,1},{1,2},{2,3},{3,4},{4,5},{5,6},{6,7},{7,8},{8,9},{9,10},{10,1... | collective-permute-start | bytes 1572872 | tf_op jit(solution)/shard_map/ppermute | solution.py:22
  8.4 27.2 %collective-permute-start.8 = (bf16[2048,128]{1,0:T(8,128)(2,1)}, bf16[2048,128]{1,0:T(8,128)(2,1)}, u32[]{:S(2)}, u32[]{:S(2)}) collective-permute-start(bf16[2048,128]{1,0:T(8,128)(2,1)} %param.11), channel_id=1, source_target_pairs={{0,1},{1,0},{2,3},{3,2},{4,5},{5,4},{6,7},{7,6},{8,9},{9,8},{10,11... | collective-permute-start | bytes 1572872 | tf_op jit(solution)/shard_map/ppermute | solution.py:146
  11.9 7.2 %collective-permute-start.1 = (bf16[2,6144]{1,0:T(2,128)(2,1)S(1)}, bf16[2,6144]{1,0:T(2,128)(2,1)S(1)}, u32[]{:S(2)}, u32[]{:S(2)}) collective-permute-start(bf16[2,6144]{1,0:T(2,128)(2,1)S(1)} %slice.96), channel_id=1, source_target_pairs={{0,1},{1,2},{2,3},{3,4},{4,5},{5,6},{6,7},{7,8},{8,9},{9,10},{10,1... | collective-permute-start | bytes 73736 | tf_op jit(solution)/shard_map/ppermute | solution.py:22
  19.1 6.7 %copy-start.5 = (bf16[2,6144]{1,0:T(2,128)(2,1)}, bf16[2,6144]{1,0:T(2,128)(2,1)S(1)}, u32[]{:S(2)}) copy-start(bf16[2,6144]{1,0:T(2,128)(2,1)S(1)} %collective-permute-done.1) | copy-start | bytes 73732
  19.2 6.7 %copy-start = (bf16[128,2048]{1,0:T(8,128)(2,1)}, bf16[128,2048]{1,0:T(8,128)(2,1)S(1)}, u32[]{:S(2)}) copy-start(bf16[128,2048]{1,0:T(8,128)(2,1)S(1)} %collective-permute-done.halo_ref) | copy-start | bytes 1572868
  19.2 18.4 %collective-permute-start.4 = (bf16[2048,128]{1,0:T(8,128)(2,1)S(1)}, bf16[2048,128]{1,0:T(8,128)(2,1)}, u32[]{:S(2)}, u32[]{:S(2)}) collective-permute-start(bf16[2048,128]{1,0:T(8,128)(2,1)S(1)} %collective-permute-done.2), channel_id=1, source_target_pairs={{0,4},{4,8},{8,12},{12,14},{14,10},{10,6},{6,2},{2,0},{1,5},{5,9},... | collective-permute-start | bytes 1572872 | tf_op jit(solution)/shard_map/ppermute | solution.py:156
  24.0 13.6 %collective-permute-start.5 = (bf16[2048,128]{1,0:T(8,128)(2,1)S(1)}, bf16[2048,128]{1,0:T(8,128)(2,1)S(1)}, u32[]{:S(2)}, u32[]{:S(2)}) collective-permute-start(bf16[2048,128]{1,0:T(8,128)(2,1)S(1)} %collective-permute-done.3), channel_id=1, source_target_pairs={{4,0},{8,4},{12,8},{14,12},{10,14},{6,10},{2,6},{0,2},{5,1},{9,5},... | collective-permute-start | bytes 1572872 | tf_op jit(solution)/shard_map/ppermute | solution.py:157
  25.8 30.4 %collective-permute-start.9 = (bf16[2,2048,128]{2,1,0:T(8,128)(2,1)}, bf16[2,2048,128]{2,1,0:T(8,128)(2,1)}, u32[]{:S(2)}, u32[]{:S(2)}) collective-permute-start(bf16[2,2048,128]{2,1,0:T(8,128)(2,1)} %pad_maximum_fusion), channel_id=1, source_target_pairs={{0,1},{1,0},{2,3},{3,2},{4,5},{5,4},{6,7},{7,6},{8,9},{9,8},{10,11... | collective-permute-start | bytes 3145736 | tf_op jit(solution)/shard_map/ppermute | solution.py:160
  37.6 16.0 %collective-permute-start.6 = (bf16[2048,128]{1,0:T(8,128)(2,1)}, bf16[2048,128]{1,0:T(8,128)(2,1)S(1)}, u32[]{:S(2)}, u32[]{:S(2)}) collective-permute-start(bf16[2048,128]{1,0:T(8,128)(2,1)} %collective-permute-done.4), channel_id=1, source_target_pairs={{0,4},{4,8},{8,12},{12,14},{14,10},{10,6},{6,2},{2,0},{1,5},{5,9},... | collective-permute-start | bytes 1572872 | tf_op jit(solution)/shard_map/ppermute | solution.py:156
  39.6 14.0 %collective-permute-start.7 = (bf16[2048,128]{1,0:T(8,128)(2,1)S(1)}, bf16[2048,128]{1,0:T(8,128)(2,1)S(1)}, u32[]{:S(2)}, u32[]{:S(2)}) collective-permute-start(bf16[2048,128]{1,0:T(8,128)(2,1)S(1)} %collective-permute-done.5), channel_id=1, source_target_pairs={{4,0},{8,4},{12,8},{14,12},{10,14},{6,10},{2,6},{0,2},{5,1},{9,5},... | collective-permute-start | bytes 1572872 | tf_op jit(solution)/shard_map/ppermute | solution.py:157
  42.7 21.6 %collective-permute-start.10 = (bf16[2,2048,128]{2,1,0:T(8,128)(2,1)}, bf16[2,2048,128]{2,1,0:T(8,128)(2,1)}, u32[]{:S(2)}, u32[]{:S(2)}) collective-permute-start(bf16[2,2048,128]{2,1,0:T(8,128)(2,1)} %pad_maximum_fusion.1), channel_id=1, source_target_pairs={{0,1},{1,0},{2,3},{3,2},{4,5},{5,4},{6,7},{7,6},{8,9},{9,8},{10,11... | collective-permute-start | bytes 3145736 | tf_op jit(solution)/shard_map/ppermute | solution.py:160
  53.7 21.9 %copy-start.1 = (bf16[512,1024]{1,0:T(8,128)(2,1)S(1)}, bf16[512,1024]{1,0:T(8,128)(2,1)}, u32[]{:S(2)}) copy-start(bf16[512,1024]{1,0:T(8,128)(2,1)} %shard_map.64) | copy-start | bytes 3145732
  53.7 21.9 %copy-start.2 = (bf16[512,1024]{1,0:T(8,128)(2,1)S(1)}, bf16[512,1024]{1,0:T(8,128)(2,1)}, u32[]{:S(2)}) copy-start(bf16[512,1024]{1,0:T(8,128)(2,1)} %shard_map.65) | copy-start | bytes 3145732
  53.8 21.9 %copy-start.6 = (bf16[512,2048]{1,0:T(8,128)(2,1)S(1)}, bf16[512,2048]{1,0:T(8,128)(2,1)}, u32[]{:S(2)}) copy-start(bf16[512,2048]{1,0:T(8,128)(2,1)} %param.6) | copy-start | bytes 6291460
  53.8 16.2 %collective-permute-start.11 = (bf16[2,2048,128]{2,1,0:T(8,128)(2,1)S(1)}, bf16[2,2048,128]{2,1,0:T(8,128)(2,1)S(1)}, u32[]{:S(2)}, u32[]{:S(2)}) collective-permute-start(bf16[2,2048,128]{2,1,0:T(8,128)(2,1)S(1)} %pad_maximum_fusion.2), channel_id=1, source_target_pairs={{0,1},{1,0},{2,3},{3,2},{4,5},{5,4},{6,7},{7,6},{8,9},{9,8},{10,11... | collective-permute-start | bytes 3145736 | tf_op jit(solution)/shard_map/ppermute | solution.py:160
  54.1 8.9 %collective-permute-start.12 = (bf16[1024,128]{1,0:T(8,128)(2,1)S(1)}, bf16[1024,128]{1,0:T(8,128)(2,1)S(1)}, u32[]{:S(2)}, u32[]{:S(2)}) collective-permute-start(bf16[1024,128]{1,0:T(8,128)(2,1)S(1)} %slice.103), channel_id=1, source_target_pairs={{0,4},{4,8},{8,12},{12,14},{14,10},{10,6},{6,2},{2,0},{1,5},{5,9},... | collective-permute-start | bytes 786440 | tf_op jit(solution)/shard_map/ppermute | solution.py:151
  56.2 8.0 %collective-permute-start.13 = (bf16[1024,128]{1,0:T(8,128)(2,1)S(1)}, bf16[1024,128]{1,0:T(8,128)(2,1)S(1)}, u32[]{:S(2)}, u32[]{:S(2)}) collective-permute-start(bf16[1024,128]{1,0:T(8,128)(2,1)S(1)} %slice.104), channel_id=1, source_target_pairs={{4,0},{8,4},{12,8},{14,12},{10,14},{6,10},{2,6},{0,2},{5,1},{9,5},... | collective-permute-start | bytes 786440 | tf_op jit(solution)/shard_map/ppermute | solution.py:152
  64.2 9.2 %collective-permute-start.14 = (bf16[2,1024,128]{2,1,0:T(8,128)(2,1)S(1)}, bf16[2,1024,128]{2,1,0:T(8,128)(2,1)S(1)}, u32[]{:S(2)}, u32[]{:S(2)}) collective-permute-start(bf16[2,1024,128]{2,1,0:T(8,128)(2,1)S(1)} %pad_maximum_fusion.3), channel_id=1, source_target_pairs={{0,1},{1,0},{2,3},{3,2},{4,5},{5,4},{6,7},{7,6},{8,9},{9,8},{10,11... | collective-permute-start | bytes 1572872 | tf_op jit(solution)/shard_map/ppermute | solution.py:160

commit v7 on v5

--- a/solution.py
+++ b/solution.py
@@ -1,3 +1,5 @@
+import functools
+
 import jax
 import jax.numpy as jnp
 from jax import lax
@@ -107,6 +109,66 @@
     )(fw, conv_bias.reshape(1, channels), filters, edges, halo, projected, projected, projected)
 
 
+def _project_kernel(layout, carry, cols_ref, gated_ref, tokens_ref, *refs):
+    count = sum(len(parts) for parts in layout)
+    prev = refs[:carry]
+    pieces = refs[carry : carry + count]
+    out_ref, wbuf, sems = refs[carry + count :]
+    if carry:
+        out_ref[...] = prev[0][...]
+    copies = []
+    index = 0
+    for slot, parts in enumerate(layout):
+        group = []
+        for part, (row, rows) in enumerate(parts):
+            target = wbuf.at[slot % 2, pl.ds(row, rows)]
+            group.append(pltpu.make_async_copy(pieces[index], target, sems.at[slot % 2, part]))
+            index += 1
+        copies.append(group)
+    for c in copies[0]:
+        c.start()
+    width = wbuf.shape[2]
+    for slot in range(len(layout)):
+        for c in copies[slot]:
+            c.wait()
+        if slot + 1 < len(layout):
+            for c in copies[slot + 1]:
+                c.start()
+        column = pl.multiple_of(cols_ref[slot] * width, width)
+        acc = jnp.dot(gated_ref[...], wbuf[slot % 2], preferred_element_type=jnp.float32)
+        rows = tokens_ref[:, pl.ds(column, width)].astype(jnp.float32)
+        out_ref[:, pl.ds(column, width)] = (rows + acc).astype(out_ref.dtype)
+
+
+def project(gated, tokens, slots, previous=None):
+    layout = tuple(tuple((row, piece.shape[0]) for piece, row in parts) for _, parts in slots)
+    cols = jnp.stack([jnp.asarray(c, jnp.int32) for c, _ in slots])
+    pieces = [piece for _, parts in slots for piece, _ in parts]
+    carry = 0 if previous is None else 1
+    channels, width = gated.shape[1], pieces[0].shape[1]
+    full = lambda i, cols: (0, 0)
+    in_specs = [pl.BlockSpec(gated.shape, full), pl.BlockSpec(tokens.shape, full)]
+    in_specs += [pl.BlockSpec(tokens.shape, full)] * carry
+    in_specs += [pl.BlockSpec(memory_space=pl.ANY)] * len(pieces)
+    operands = [gated, tokens] + ([previous] if carry else []) + pieces
+    return pl.pallas_call(
+        functools.partial(_project_kernel, layout, carry),
+        grid_spec=pltpu.PrefetchScalarGridSpec(
+            num_scalar_prefetch=1,
+            grid=(1,),
+            in_specs=in_specs,
+            out_specs=pl.BlockSpec(tokens.shape, full),
+            scratch_shapes=[
+                pltpu.VMEM((2, channels, width), pieces[0].dtype),
+                pltpu.SemaphoreType.DMA((2, 2)),
+            ],
+        ),
+        out_shape=jax.ShapeDtypeStruct(tokens.shape, tokens.dtype),
+        input_output_aliases={3: 0} if carry else {},
+        compiler_params=pltpu.CompilerParams(vmem_limit_bytes=48 * 1024 * 1024),
+    )(cols, *operands)
+
+
 def ring_place(c, chips):
     return jnp.where(c % 2 == 0, c // 2, chips - 1 - c // 2)
 
@@ -123,8 +185,7 @@
     row_count = tokens.shape[0]
     channels = out_weight.shape[0]
     chips = lax.axis_size("chip")
-    width = out_weight.shape[1]
-    ring = chips % 2 == 0 and chips <= 8
+    ring = chips % 2 == 0 and chips <= 8 and out_weight.shape[1] == LANES
 
     chip = lax.axis_index("chip")
     core = lax.axis_index("core")
@@ -134,34 +195,33 @@
     backward = [(order[(i + 1) % chips], order[i]) for i in range(chips)]
     swap = [(0, 1), (1, 0)]
     steps = chips // 2
-
-    weight = jnp.zeros((channels, chips * 2 * width), out_weight.dtype)
-
-    def place(weight, piece, owner_chip, row=0):
+    slots = []
+
+    def add(piece, owner_chip):
         other = lax.ppermute(piece, "core", swap)
-        for k, part in ((core, piece), (1 - core, other)):
-            weight = lax.dynamic_update_slice(weight, part, (row, (owner_chip * 2 + k) * width))
-        return weight
-
-    def ring_step(step, weight, ahead, behind):
+        slots.append((owner_chip * 2 + core, [(piece, 0)]))
+        slots.append((owner_chip * 2 + 1 - core, [(other, 0)]))
+
+    def ring_step(step, ahead, behind):
         if step == steps:
             half = channels // 2
             ahead = lax.ppermute(ahead[:half], "chip", forward)
             behind = lax.ppermute(behind[half:], "chip", backward)
             source = ring_chip((position - step) % chips, chips)
-            weight = place(weight, ahead, source, 0)
-            weight = place(weight, behind, source, half)
+            top, bottom = lax.ppermute(ahead, "core", swap), lax.ppermute(behind, "core", swap)
+            slots.append((source * 2 + core, [(ahead, 0), (behind, half)]))
+            slots.append((source * 2 + 1 - core, [(top, 0), (bottom, half)]))
         else:
             ahead = lax.ppermute(ahead, "chip", forward)
             behind = lax.ppermute(behind, "chip", backward)
-            weight = place(weight, ahead, ring_chip((position - step) % chips, chips))
-            weight = place(weight, behind, ring_chip((position + step) % chips, chips))
-        return weight, ahead, behind
+            add(ahead, ring_chip((position - step) % chips, chips))
+            add(behind, ring_chip((position + step) % chips, chips))
+        return ahead, behind
 
     ahead = behind = out_weight
     if ring:
-        weight = place(weight, out_weight, chip)
-        weight, ahead, behind = ring_step(1, weight, ahead, behind)
+        add(out_weight, chip)
+        ahead, behind = ring_step(1, ahead, behind)
 
     tail = projected[row_count - BLOCK - 2 :]
     tail_mixed = [
@@ -172,24 +232,28 @@
     edge = shifted(projected[row_count - 2 :], 1)
     halo, edge, ahead, behind = lax.optimization_barrier((halo, edge, ahead, behind))
     if ring and steps >= 2:
-        weight, ahead, behind = ring_step(2, weight, ahead, behind)
+        ahead, behind = ring_step(2, ahead, behind)
 
     inputs = (halo, edge, projected, short_filter, long_filter, conv_bias)
     first = hyena_gate(*inputs, 0, 2)
     if ring:
         first, ahead, behind, inputs = lax.optimization_barrier((first, ahead, behind, inputs))
         if steps >= 3:
-            weight, ahead, behind = ring_step(3, weight, ahead, behind)
+            ahead, behind = ring_step(3, ahead, behind)
     second = hyena_gate(*inputs, 1, 2)
-    if ring:
-        second, ahead, behind = lax.optimization_barrier((second, ahead, behind))
-        for step in range(4, steps + 1):
-            weight, ahead, behind = ring_step(step, weight, ahead, behind)
-    else:
+    gated = jnp.concatenate([first, second], axis=1)
+    if not ring:
         weight = lax.all_gather(out_weight, CTX, axis=1, tiled=True)
-    gated = jnp.concatenate([first, second], axis=1)
-    branch = jnp.dot(gated, weight, preferred_element_type=jnp.float32)
-    return (tokens.astype(jnp.float32) + branch).astype(jnp.bfloat16)
+        branch = jnp.dot(gated, weight, preferred_element_type=jnp.float32)
+        return (tokens.astype(jnp.float32) + branch).astype(jnp.bfloat16)
+    gated, ahead, behind = lax.optimization_barrier((gated, ahead, behind))
+    early = len(slots)
+    for step in range(4, steps + 1):
+        ahead, behind = ring_step(step, ahead, behind)
+    result = project(gated, tokens, slots[:early])
+    if len(slots) > early:
+        result = project(gated, tokens, slots[early:], result)
+    return result
 
 
 def solution(mesh):

time: 83 us -> 106 us (1.28)
  waiting for transfers between devices: 2.82 us -> 27.6 us
  Pallas kernels: 19.5 us -> 43.1 us
  local copies, waits for them, and re-layouts: 26.3 us -> 3.16 us
  matrix products: 9.18 us -> 0 us
  starting transfers between devices: 19.6 us -> 23 us
  other arithmetic: 4.43 us -> 7.67 us
    pallas_call x0 -> x2, Pallas kernels: none -> 23.6 us  [project(): pl.pallas_call(functools.partial(_project_kernel, layout, carry), grid_sp...]
    dynamic_update_slice x18 -> x0, local copies, waits for them, and re-layouts: 19.8 us -> none  [place(): lax.dynamic_update_slice(weight, part, (row, (owner_chip * 2 + k) * width))]
    ppermute x3, waiting for transfers between devices: 0.01 us -> 15.7 us  [ring_step(): ahead = lax.ppermute(ahead, 'chip', forward)]
    dot_general x1 -> x0, matrix products: 9.18 us -> none  [on_device(): branch = jnp.dot(gated, weight, preferred_element_type=jnp.float32)]
    ppermute x1, waiting for transfers between devices: 1 us -> 5.81 us  [ring_step(): ahead = lax.ppermute(ahead[:half], 'chip', forward)]
    broadcast_in_dim x1 -> x0, local copies, waits for them, and re-layouts: 4.34 us -> none  [on_device(): weight = jnp.zeros((channels, chips * 2 * width), out_weight.dtype)]
    ppermute x3, starting transfers between devices: 9.89 us -> 13.1 us  [ring_step(): ahead = lax.ppermute(ahead, 'chip', forward)]
    concatenate x0 -> x1, other arithmetic: none -> 3.09 us  [on_device(): gated = jnp.concatenate([first, second], axis=1)]
  transfers between devices with their start and end apart: 19 -> 19, of which waited for: 2 -> 6; matrix products, arithmetic and copies ran while one was open for 36% -> 7% of each run, Pallas kernels for 24% -> 35%
where the time goes in v7:
time: 106 us; the launch traced here: 105 us
  Pallas kernels  43.1 us (41%)
  waiting for transfers between devices  27.6 us (26%)
  starting transfers between devices  23 us (22%)
  other arithmetic  7.67 us (7%)
  local copies, waits for them, and re-layouts  3.16 us (3%)
    pallas_call x2, Pallas kernels, project(): pl.pallas_call(functools.partial(_project_kernel, layout, carry), grid_sp...  23.6 us
    pallas_call x2, Pallas kernels, hyena_gate(): pl.pallas_call(_gate_kernel, grid=(share,), in_specs=[pl.BlockSpec((per_t...  19.5 us
    ppermute x3, waiting for transfers between devices, ring_step(): ahead = lax.ppermute(ahead, 'chip', forward)  15.7 us
    ppermute x3, starting transfers between devices, ring_step(): ahead = lax.ppermute(ahead, 'chip', forward)  13.1 us
    ppermute x1, waiting for transfers between devices, ring_step(): ahead = lax.ppermute(ahead[:half], 'chip', forward)  5.81 us
    ppermute x2, starting transfers between devices, shifted(): return lax.ppermute(block, CTX, route)  5.8 us
    concatenate x1, other arithmetic, on_device(): gated = jnp.concatenate([first, second], axis=1)  3.09 us
    convert_element_type x1, other arithmetic, carried_of(): return (second * carrier).astype(jnp.bfloat16)  2.95 us
  transfers between devices with their start and end apart: 19, of which 6 were waited for; matrix products, arithmetic and copies ran while one was open for 7% of the time, Pallas kernels for 35%

profile of v7, /device:TPU:0, one launch (start us, length us, event | category | flops | bytes accessed | tf_op | source)
XLA Modules:
  0.0 104.9 jit_solution(10909720864489346990)
XLA Ops:
  0.0 1.0 fusion
  1.0 3.0 %multiply_convert_fusion = bf16[128,2048]{1,0:T(8,128)(2,1)S(1)} fusion(bf16[512,6144]{1,0:T(8,128)(2,1)} %carrier_ref.2, f32[2048]{0:T(1024)S(1)} %bitcast.47, f32[2048]{0:T(1024)S(1)} %bitcast.43, f32[2048]{0:T(1024)S(1)} %bitcast.44, f32[2048]{0:T(1024)S(1)} %bitcast.45, f32[2048]{0:T(1024)S(1)} %bitcast.46, f32[2048]{0:T(1024)S(1)} %bitcast.42), kind=kLoop, calls=%fused_computation.1 | loop fusion | flops 4718592 | bytes 3719168 | tf_op jit(solution)/shard_map/convert_element_type | solution.py:181
  3.9 2.4 %collective-permute-start = (bf16[128,2048]{1,0:T(8,128)(2,1)S(1)}, bf16[128,2048]{1,0:T(8,128)(2,1)S(1)}, u32[]{:S(2)}, u32[]{:S(2)}) collective-permute-start(bf16[128,2048]{1,0:T(8,128)(2,1)S(1)} %multiply_convert_fusion), channel_id=1, source_target_pairs={{0,1},{1,2},{2,3},{3,4},{4,5},{5,6},{6,7},{7,8},{8,9},{9,10},{10,1... | collective-permute-start | bytes 1572872 | tf_op jit(solution)/shard_map/ppermute | solution.py:24
  6.3 2.6 %collective-permute-start.2 = (bf16[2048,128]{1,0:T(8,128)(2,1)S(1)}, bf16[2048,128]{1,0:T(8,128)(2,1)S(1)}, u32[]{:S(2)}, u32[]{:S(2)}) collective-permute-start(bf16[2048,128]{1,0:T(8,128)(2,1)S(1)} %copy-done.2), channel_id=1, source_target_pairs={{0,4},{4,8},{8,12},{12,14},{14,10},{10,6},{6,2},{2,0},{1,5},{5,9},... | collective-permute-start | bytes 1572872 | tf_op jit(solution)/shard_map/ppermute | solution.py:215
  8.9 0.0 collective-permute-start.3
  8.9 0.9 slice.72
  9.9 3.4 %collective-permute-start.1 = (bf16[2,6144]{1,0:T(2,128)(2,1)S(1)}, bf16[2,6144]{1,0:T(2,128)(2,1)S(1)}, u32[]{:S(2)}, u32[]{:S(2)}) collective-permute-start(bf16[2,6144]{1,0:T(2,128)(2,1)S(1)} %slice.72), channel_id=1, source_target_pairs={{0,1},{1,2},{2,3},{3,4},{4,5},{5,6},{6,7},{7,8},{8,9},{9,10},{10,1... | collective-permute-start | bytes 73736 | tf_op jit(solution)/shard_map/ppermute | solution.py:24
  13.3 0.8 collective-permute-done.1
  14.1 6.5 %collective-permute-done.2.refs_2_ = bf16[2048,128]{1,0:T(8,128)(2,1)S(1)} collective-permute-done((bf16[2048,128]{1,0:T(8,128)(2,1)S(1)}, bf16[2048,128]{1,0:T(8,128)(2,1)S(1)}, u32[]{:S(2)}, u32[]{:S(2)}) %collective-permute-start.2) | collective-permute-done | bytes 524320 | tf_op jit(solution)/shard_map/ppermute | solution.py:215
  20.7 2.8 %collective-permute-done.3.refs_4_ = bf16[2048,128]{1,0:T(8,128)(2,1)S(1)} collective-permute-done((bf16[2048,128]{1,0:T(8,128)(2,1)S(1)}, bf16[2048,128]{1,0:T(8,128)(2,1)S(1)}, u32[]{:S(2)}, u32[]{:S(2)}) %collective-permute-start.3) | collective-permute-done | bytes 524320 | tf_op jit(solution)/shard_map/ppermute | solution.py:216
  23.5 6.5 %collective-permute-start.4 = (bf16[2048,128]{1,0:T(8,128)(2,1)S(1)}, bf16[2048,128]{1,0:T(8,128)(2,1)S(1)}, u32[]{:S(2)}, u32[]{:S(2)}) collective-permute-start(bf16[2048,128]{1,0:T(8,128)(2,1)S(1)} %collective-permute-done.2.refs_2_), channel_id=1, source_target_pairs={{0,4},{4,8},{8,12},{12,14},{14,10},{10,6},{6,2},{2,0},{1,5},{5,9},... | collective-permute-start | bytes 1572872 | tf_op jit(solution)/shard_map/ppermute | solution.py:215
  29.9 0.1 rev.6
  30.0 0.8 pad_convert_fusion.1.fw_ref
  30.8 9.8 %shard_map.64 = bf16[512,1024]{1,0:T(8,128)(2,1)} custom-call(f32[128,384]{1,0:T(8,128)} %pad_convert_fusion.1.fw_ref, f32[1,2048]{1,0:T(1,128)} %bitcast.40, f32[3,3,2048]{2,1,0:T(4,128)} %bitcast.36, bf16[3,2,2048]{2,1,0:T(2,128)(2,1)} %bitcast.38, bf16[128,2048]{1,0:T(8,128)(2,1)} %copy-done.3, bf16[512,6144]{1,0:T(8,128)(2,1)} %carrier_ref.2, ...), custom_call_target="tpu_custom_call" | custom-call | tf_op jit(solution)/shard_map/pallas_call | solution.py:94
  40.6 4.0 %collective-permute-start.6 = (bf16[2048,128]{1,0:T(8,128)(2,1)S(1)}, bf16[2048,128]{1,0:T(8,128)(2,1)S(1)}, u32[]{:S(2)}, u32[]{:S(2)}) collective-permute-start(bf16[2048,128]{1,0:T(8,128)(2,1)S(1)} %collective-permute-done.4.refs_6_), channel_id=1, source_target_pairs={{0,4},{4,8},{8,12},{12,14},{14,10},{10,6},{6,2},{2,0},{1,5},{5,9},... | collective-permute-start | bytes 1572872 | tf_op jit(solution)/shard_map/ppermute | solution.py:215
  44.6 0.5 collective-permute-start.9
  45.1 9.2 %collective-permute-done.6.refs_10_ = bf16[2048,128]{1,0:T(8,128)(2,1)S(1)} collective-permute-done((bf16[2048,128]{1,0:T(8,128)(2,1)S(1)}, bf16[2048,128]{1,0:T(8,128)(2,1)S(1)}, u32[]{:S(2)}, u32[]{:S(2)}) %collective-permute-start.6) | collective-permute-done | bytes 524320 | tf_op jit(solution)/shard_map/ppermute | solution.py:215
  54.3 0.1 rev.7
  54.4 0.8 pad_convert_fusion.fw_ref
  55.1 9.7 %shard_map.65 = bf16[512,1024]{1,0:T(8,128)(2,1)} custom-call(f32[128,384]{1,0:T(8,128)} %pad_convert_fusion.fw_ref, f32[1,2048]{1,0:T(1,128)} %bitcast.41, f32[3,3,2048]{2,1,0:T(4,128)} %bitcast.37, bf16[3,2,2048]{2,1,0:T(2,128)(2,1)} %bitcast.39, bf16[128,2048]{1,0:T(8,128)(2,1)} %copy-done.3, bf16[512,6144]{1,0:T(8,128)(2,1)} %carrier_ref.2, ...), custom_call_target="tpu_custom_call" | custom-call | tf_op jit(solution)/shard_map/pallas_call | solution.py:94
  64.9 3.1 %pad_maximum_fusion.gated_ref = bf16[512,2048]{1,0:T(8,128)(2,1)} fusion(bf16[512,1024]{1,0:T(8,128)(2,1)} %shard_map.65, bf16[512,1024]{1,0:T(8,128)(2,1)} %shard_map.64), kind=kLoop, calls=%fused_computation | loop fusion | flops 4194304 | bytes 4194304 | tf_op jit(solution)/shard_map/concatenate | solution.py:244
  68.0 0.5 collective-permute-start.12
  68.5 1.0 slice.74
  69.5 0.1 collective-permute-start.13
  69.6 0.5 collective-permute-start.14
  70.1 2.5 %collective-permute-start.15 = (bf16[1024,128]{1,0:T(8,128)(2,1)S(1)}, bf16[1024,128]{1,0:T(8,128)(2,1)S(1)}, u32[]{:S(2)}, u32[]{:S(2)}) collective-permute-start(bf16[1024,128]{1,0:T(8,128)(2,1)S(1)} %slice.73), channel_id=1, source_target_pairs={{0,4},{4,8},{8,12},{12,14},{14,10},{10,6},{6,2},{2,0},{1,5},{5,9},... | collective-permute-start | bytes 786440 | tf_op jit(solution)/shard_map/ppermute | solution.py:208
  72.6 5.8 %collective-permute-done.15.refs_1_ = bf16[1024,128]{1,0:T(8,128)(2,1)S(1)} collective-permute-done((bf16[1024,128]{1,0:T(8,128)(2,1)S(1)}, bf16[1024,128]{1,0:T(8,128)(2,1)S(1)}, u32[]{:S(2)}, u32[]{:S(2)}) %collective-permute-start.15) | collective-permute-done | bytes 262176 | tf_op jit(solution)/shard_map/ppermute | solution.py:208
  78.4 2.5 %collective-permute-done.16.refs_2_ = bf16[1024,128]{1,0:T(8,128)(2,1)} collective-permute-done((bf16[1024,128]{1,0:T(8,128)(2,1)S(1)}, bf16[1024,128]{1,0:T(8,128)(2,1)}, u32[]{:S(2)}, u32[]{:S(2)}) %collective-permute-start.16) | collective-permute-done | bytes 262176 | tf_op jit(solution)/shard_map/ppermute | solution.py:209
  80.9 0.1 stack.71.cols_ref
  80.9 0.1 pad_add_fusion.cols_ref
  81.0 17.3 %shard_map.66.refs_0_ = bf16[512,2048]{1,0:T(8,128)(2,1)} custom-call(s32[14]{0:T(128)S(1)} %stack.71.cols_ref, bf16[512,2048]{1,0:T(8,128)(2,1)} %pad_maximum_fusion.gated_ref, bf16[512,2048]{1,0:T(8,128)(2,1)} %tokens_ref.3, bf16[2048,128]{1,0:T(8,128)(2,1)S(1)} %copy-done.2, bf16[2048,128]{1,0:T(8,128)(2,1)} %collective-permute-done.8.refs_1_, ...), custom_call_target="tpu_custom_call" | custom-call | tf_op jit(solution)/shard_map/pallas_call | solution.py:154
  98.4 6.3 %shard_map.67 = bf16[512,2048]{1,0:T(8,128)(2,1)} custom-call(s32[2]{0:T(128)S(1)} %pad_add_fusion.cols_ref, bf16[512,2048]{1,0:T(8,128)(2,1)S(1)} %copy-done, bf16[512,2048]{1,0:T(8,128)(2,1)S(1)} %copy-done.1, bf16[512,2048]{1,0:T(8,128)(2,1)} %shard_map.66.refs_0_, ...), custom_call_target="tpu_custom_call", output_to_operand_aliasing={{}: (3, {})} | custom-call | tf_op jit(solution)/shard_map/pallas_call | solution.py:154
  (34 shorter events, 0.1 us)
Async XLA Ops:
  0.0 6.3 %copy-start.2 = (bf16[2048,128]{1,0:T(8,128)(2,1)S(1)}, bf16[2048,128]{1,0:T(8,128)(2,1)}, u32[]{:S(2)}) copy-start(bf16[2048,128]{1,0:T(8,128)(2,1)} %refs_0_.1) | copy-start | bytes 1572868
  0.0 29.9 %copy-start.4 = (bf16[128,128]{1,0:T(8,128)(2,1)S(1)}, bf16[128,128]{1,0:T(8,128)(2,1)}, u32[]{:S(2)}) copy-start(bf16[128,128]{1,0:T(8,128)(2,1)} %param.9) | copy-start | bytes 98308
  3.9 10.2 %collective-permute-start = (bf16[128,2048]{1,0:T(8,128)(2,1)S(1)}, bf16[128,2048]{1,0:T(8,128)(2,1)S(1)}, u32[]{:S(2)}, u32[]{:S(2)}) collective-permute-start(bf16[128,2048]{1,0:T(8,128)(2,1)S(1)} %multiply_convert_fusion), channel_id=1, source_target_pairs={{0,1},{1,2},{2,3},{3,4},{4,5},{5,6},{6,7},{7,8},{8,9},{9,10},{10,1... | collective-permute-start | bytes 1572872 | tf_op jit(solution)/shard_map/ppermute | solution.py:24
  6.3 14.3 %collective-permute-start.2 = (bf16[2048,128]{1,0:T(8,128)(2,1)S(1)}, bf16[2048,128]{1,0:T(8,128)(2,1)S(1)}, u32[]{:S(2)}, u32[]{:S(2)}) collective-permute-start(bf16[2048,128]{1,0:T(8,128)(2,1)S(1)} %copy-done.2), channel_id=1, source_target_pairs={{0,4},{4,8},{8,12},{12,14},{14,10},{10,6},{6,2},{2,0},{1,5},{5,9},... | collective-permute-start | bytes 1572872 | tf_op jit(solution)/shard_map/ppermute | solution.py:215
  8.9 14.5 %collective-permute-start.3 = (bf16[2048,128]{1,0:T(8,128)(2,1)S(1)}, bf16[2048,128]{1,0:T(8,128)(2,1)S(1)}, u32[]{:S(2)}, u32[]{:S(2)}) collective-permute-start(bf16[2048,128]{1,0:T(8,128)(2,1)S(1)} %copy-done.2), channel_id=1, source_target_pairs={{4,0},{8,4},{12,8},{14,12},{10,14},{6,10},{2,6},{0,2},{5,1},{9,5},... | collective-permute-start | bytes 1572872 | tf_op jit(solution)/shard_map/ppermute | solution.py:216
  9.9 4.2 %collective-permute-start.1 = (bf16[2,6144]{1,0:T(2,128)(2,1)S(1)}, bf16[2,6144]{1,0:T(2,128)(2,1)S(1)}, u32[]{:S(2)}, u32[]{:S(2)}) collective-permute-start(bf16[2,6144]{1,0:T(2,128)(2,1)S(1)} %slice.72), channel_id=1, source_target_pairs={{0,1},{1,2},{2,3},{3,4},{4,5},{5,6},{6,7},{7,8},{8,9},{9,10},{10,1... | collective-permute-start | bytes 73736 | tf_op jit(solution)/shard_map/ppermute | solution.py:24
  14.1 16.7 %copy-start.5 = (bf16[2,6144]{1,0:T(2,128)(2,1)}, bf16[2,6144]{1,0:T(2,128)(2,1)S(1)}, u32[]{:S(2)}) copy-start(bf16[2,6144]{1,0:T(2,128)(2,1)S(1)} %collective-permute-done.1) | copy-start | bytes 73732
  14.1 16.7 %copy-start.3 = (bf16[128,2048]{1,0:T(8,128)(2,1)}, bf16[128,2048]{1,0:T(8,128)(2,1)S(1)}, u32[]{:S(2)}) copy-start(bf16[128,2048]{1,0:T(8,128)(2,1)S(1)} %collective-permute-done.halo_ref) | copy-start | bytes 1572868
  23.5 17.1 %collective-permute-start.4 = (bf16[2048,128]{1,0:T(8,128)(2,1)S(1)}, bf16[2048,128]{1,0:T(8,128)(2,1)S(1)}, u32[]{:S(2)}, u32[]{:S(2)}) collective-permute-start(bf16[2048,128]{1,0:T(8,128)(2,1)S(1)} %collective-permute-done.2.refs_2_), channel_id=1, source_target_pairs={{0,4},{4,8},{8,12},{12,14},{14,10},{10,6},{6,2},{2,0},{1,5},{5,9},... | collective-permute-start | bytes 1572872 | tf_op jit(solution)/shard_map/ppermute | solution.py:215
  29.9 10.6 %collective-permute-start.5 = (bf16[2048,128]{1,0:T(8,128)(2,1)S(1)}, bf16[2048,128]{1,0:T(8,128)(2,1)S(1)}, u32[]{:S(2)}, u32[]{:S(2)}) collective-permute-start(bf16[2048,128]{1,0:T(8,128)(2,1)S(1)} %collective-permute-done.3.refs_4_), channel_id=1, source_target_pairs={{4,0},{8,4},{12,8},{14,12},{10,14},{6,10},{2,6},{0,2},{5,1},{9,5},... | collective-permute-start | bytes 1572872 | tf_op jit(solution)/shard_map/ppermute | solution.py:216
  40.6 13.7 %collective-permute-start.6 = (bf16[2048,128]{1,0:T(8,128)(2,1)S(1)}, bf16[2048,128]{1,0:T(8,128)(2,1)S(1)}, u32[]{:S(2)}, u32[]{:S(2)}) collective-permute-start(bf16[2048,128]{1,0:T(8,128)(2,1)S(1)} %collective-permute-done.4.refs_6_), channel_id=1, source_target_pairs={{0,4},{4,8},{8,12},{12,14},{14,10},{10,6},{6,2},{2,0},{1,5},{5,9},... | collective-permute-start | bytes 1572872 | tf_op jit(solution)/shard_map/ppermute | solution.py:215
  44.6 23.4 %collective-permute-start.7 = (bf16[2048,128]{1,0:T(8,128)(2,1)S(1)}, bf16[2048,128]{1,0:T(8,128)(2,1)}, u32[]{:S(2)}, u32[]{:S(2)}) collective-permute-start(bf16[2048,128]{1,0:T(8,128)(2,1)S(1)} %collective-permute-done.5.refs_8_), channel_id=1, source_target_pairs={{4,0},{8,4},{12,8},{14,12},{10,14},{6,10},{2,6},{0,2},{5,1},{9,5},... | collective-permute-start | bytes 1572872 | tf_op jit(solution)/shard_map/ppermute | solution.py:216
  44.6 24.9 %collective-permute-start.8 = (bf16[2048,128]{1,0:T(8,128)(2,1)S(1)}, bf16[2048,128]{1,0:T(8,128)(2,1)}, u32[]{:S(2)}, u32[]{:S(2)}) collective-permute-start(bf16[2048,128]{1,0:T(8,128)(2,1)S(1)} %copy-done.2), channel_id=1, source_target_pairs={{0,1},{1,0},{2,3},{3,2},{4,5},{5,4},{6,7},{7,6},{8,9},{9,8},{10,11... | collective-permute-start | bytes 1572872 | tf_op jit(solution)/shard_map/ppermute | solution.py:201
  44.6 25.0 %collective-permute-start.9 = (bf16[2048,128]{1,0:T(8,128)(2,1)S(1)}, bf16[2048,128]{1,0:T(8,128)(2,1)}, u32[]{:S(2)}, u32[]{:S(2)}) collective-permute-start(bf16[2048,128]{1,0:T(8,128)(2,1)S(1)} %collective-permute-done.2.refs_2_), channel_id=1, source_target_pairs={{0,1},{1,0},{2,3},{3,2},{4,5},{5,4},{6,7},{7,6},{8,9},{9,8},{10,11... | collective-permute-start | bytes 1572872 | tf_op jit(solution)/shard_map/ppermute | solution.py:201
  45.1 25.0 %collective-permute-start.10 = (bf16[2048,128]{1,0:T(8,128)(2,1)S(1)}, bf16[2048,128]{1,0:T(8,128)(2,1)}, u32[]{:S(2)}, u32[]{:S(2)}) collective-permute-start(bf16[2048,128]{1,0:T(8,128)(2,1)S(1)} %collective-permute-done.3.refs_4_), channel_id=1, source_target_pairs={{0,1},{1,0},{2,3},{3,2},{4,5},{5,4},{6,7},{7,6},{8,9},{9,8},{10,11... | collective-permute-start | bytes 1572872 | tf_op jit(solution)/shard_map/ppermute | solution.py:201
  54.3 18.3 %collective-permute-start.11 = (bf16[2048,128]{1,0:T(8,128)(2,1)S(1)}, bf16[2048,128]{1,0:T(8,128)(2,1)}, u32[]{:S(2)}, u32[]{:S(2)}) collective-permute-start(bf16[2048,128]{1,0:T(8,128)(2,1)S(1)} %collective-permute-done.4.refs_6_), channel_id=1, source_target_pairs={{0,1},{1,0},{2,3},{3,2},{4,5},{5,4},{6,7},{7,6},{8,9},{9,8},{10,11... | collective-permute-start | bytes 1572872 | tf_op jit(solution)/shard_map/ppermute | solution.py:201
  68.0 13.1 %collective-permute-start.12 = (bf16[2048,128]{1,0:T(8,128)(2,1)S(1)}, bf16[2048,128]{1,0:T(8,128)(2,1)}, u32[]{:S(2)}, u32[]{:S(2)}) collective-permute-start(bf16[2048,128]{1,0:T(8,128)(2,1)S(1)} %collective-permute-done.5.refs_8_), channel_id=1, source_target_pairs={{0,1},{1,0},{2,3},{3,2},{4,5},{5,4},{6,7},{7,6},{8,9},{9,8},{10,11... | collective-permute-start | bytes 1572872 | tf_op jit(solution)/shard_map/ppermute | solution.py:201
  69.5 11.5 %collective-permute-start.13 = (bf16[2048,128]{1,0:T(8,128)(2,1)S(1)}, bf16[2048,128]{1,0:T(8,128)(2,1)}, u32[]{:S(2)}, u32[]{:S(2)}) collective-permute-start(bf16[2048,128]{1,0:T(8,128)(2,1)S(1)} %collective-permute-done.6.refs_10_), channel_id=1, source_target_pairs={{0,1},{1,0},{2,3},{3,2},{4,5},{5,4},{6,7},{7,6},{8,9},{9,8},{10,11... | collective-permute-start | bytes 1572872 | tf_op jit(solution)/shard_map/ppermute | solution.py:201
  69.6 11.5 %collective-permute-start.14 = (bf16[2048,128]{1,0:T(8,128)(2,1)}, bf16[2048,128]{1,0:T(8,128)(2,1)}, u32[]{:S(2)}, u32[]{:S(2)}) collective-permute-start(bf16[2048,128]{1,0:T(8,128)(2,1)} %collective-permute-done.7.refs_12_), channel_id=1, source_target_pairs={{0,1},{1,0},{2,3},{3,2},{4,5},{5,4},{6,7},{7,6},{8,9},{9,8},{10,11... | collective-permute-start | bytes 1572872 | tf_op jit(solution)/shard_map/ppermute | solution.py:201
  70.1 8.3 %collective-permute-start.15 = (bf16[1024,128]{1,0:T(8,128)(2,1)S(1)}, bf16[1024,128]{1,0:T(8,128)(2,1)S(1)}, u32[]{:S(2)}, u32[]{:S(2)}) collective-permute-start(bf16[1024,128]{1,0:T(8,128)(2,1)S(1)} %slice.73), channel_id=1, source_target_pairs={{0,4},{4,8},{8,12},{12,14},{14,10},{10,6},{6,2},{2,0},{1,5},{5,9},... | collective-permute-start | bytes 786440 | tf_op jit(solution)/shard_map/ppermute | solution.py:208
  72.6 8.3 %collective-permute-start.16 = (bf16[1024,128]{1,0:T(8,128)(2,1)S(1)}, bf16[1024,128]{1,0:T(8,128)(2,1)}, u32[]{:S(2)}, u32[]{:S(2)}) collective-permute-start(bf16[1024,128]{1,0:T(8,128)(2,1)S(1)} %slice.74), channel_id=1, source_target_pairs={{4,0},{8,4},{12,8},{14,12},{10,14},{6,10},{2,6},{0,2},{5,1},{9,5},... | collective-permute-start | bytes 786440 | tf_op jit(solution)/shard_map/ppermute | solution.py:209
  78.4 20.0 %collective-permute-start.17 = (bf16[1024,128]{1,0:T(8,128)(2,1)S(1)}, bf16[1024,128]{1,0:T(8,128)(2,1)}, u32[]{:S(2)}, u32[]{:S(2)}) collective-permute-start(bf16[1024,128]{1,0:T(8,128)(2,1)S(1)} %collective-permute-done.15.refs_1_), channel_id=1, source_target_pairs={{0,1},{1,0},{2,3},{3,2},{4,5},{5,4},{6,7},{7,6},{8,9},{9,8},{10,11... | collective-permute-start | bytes 786440 | tf_op jit(solution)/shard_map/ppermute | solution.py:211
  80.8 17.5 %collective-permute-start.18 = (bf16[1024,128]{1,0:T(8,128)(2,1)}, bf16[1024,128]{1,0:T(8,128)(2,1)}, u32[]{:S(2)}, u32[]{:S(2)}) collective-permute-start(bf16[1024,128]{1,0:T(8,128)(2,1)} %collective-permute-done.16.refs_2_), channel_id=1, source_target_pairs={{0,1},{1,0},{2,3},{3,2},{4,5},{5,4},{6,7},{7,6},{8,9},{9,8},{10,11... | collective-permute-start | bytes 786440 | tf_op jit(solution)/shard_map/ppermute | solution.py:211
  81.0 17.3 %copy-start = (bf16[512,2048]{1,0:T(8,128)(2,1)S(1)}, bf16[512,2048]{1,0:T(8,128)(2,1)}, u32[]{:S(2)}) copy-start(bf16[512,2048]{1,0:T(8,128)(2,1)} %pad_maximum_fusion.gated_ref) | copy-start | bytes 6291460
  81.0 17.3 %copy-start.1 = (bf16[512,2048]{1,0:T(8,128)(2,1)S(1)}, bf16[512,2048]{1,0:T(8,128)(2,1)}, u32[]{:S(2)}) copy-start(bf16[512,2048]{1,0:T(8,128)(2,1)} %tokens_ref.3) | copy-start | bytes 6291460

commit v8 on v5

--- a/solution.py
+++ b/solution.py
@@ -135,33 +135,31 @@
     swap = [(0, 1), (1, 0)]
     steps = chips // 2
 
-    weight = jnp.zeros((channels, chips * 2 * width), out_weight.dtype)
-
-    def place(weight, piece, owner_chip, row=0):
+    slots = []
+
+    def add(piece, owner_chip):
         other = lax.ppermute(piece, "core", swap)
-        for k, part in ((core, piece), (1 - core, other)):
-            weight = lax.dynamic_update_slice(weight, part, (row, (owner_chip * 2 + k) * width))
-        return weight
-
-    def ring_step(step, weight, ahead, behind):
+        slots.append((owner_chip * 2 + core, piece))
+        slots.append((owner_chip * 2 + 1 - core, other))
+
+    def ring_step(step, ahead, behind):
         if step == steps:
             half = channels // 2
             ahead = lax.ppermute(ahead[:half], "chip", forward)
             behind = lax.ppermute(behind[half:], "chip", backward)
             source = ring_chip((position - step) % chips, chips)
-            weight = place(weight, ahead, source, 0)
-            weight = place(weight, behind, source, half)
+            add(jnp.concatenate([ahead, behind], axis=0), source)
         else:
             ahead = lax.ppermute(ahead, "chip", forward)
             behind = lax.ppermute(behind, "chip", backward)
-            weight = place(weight, ahead, ring_chip((position - step) % chips, chips))
-            weight = place(weight, behind, ring_chip((position + step) % chips, chips))
-        return weight, ahead, behind
+            add(ahead, ring_chip((position - step) % chips, chips))
+            add(behind, ring_chip((position + step) % chips, chips))
+        return ahead, behind
 
     ahead = behind = out_weight
     if ring:
-        weight = place(weight, out_weight, chip)
-        weight, ahead, behind = ring_step(1, weight, ahead, behind)
+        add(out_weight, chip)
+        ahead, behind = ring_step(1, ahead, behind)
 
     tail = projected[row_count - BLOCK - 2 :]
     tail_mixed = [
@@ -172,24 +170,39 @@
     edge = shifted(projected[row_count - 2 :], 1)
     halo, edge, ahead, behind = lax.optimization_barrier((halo, edge, ahead, behind))
     if ring and steps >= 2:
-        weight, ahead, behind = ring_step(2, weight, ahead, behind)
+        ahead, behind = ring_step(2, ahead, behind)
 
     inputs = (halo, edge, projected, short_filter, long_filter, conv_bias)
     first = hyena_gate(*inputs, 0, 2)
     if ring:
         first, ahead, behind, inputs = lax.optimization_barrier((first, ahead, behind, inputs))
         if steps >= 3:
-            weight, ahead, behind = ring_step(3, weight, ahead, behind)
+            ahead, behind = ring_step(3, ahead, behind)
     second = hyena_gate(*inputs, 1, 2)
-    if ring:
-        second, ahead, behind = lax.optimization_barrier((second, ahead, behind))
-        for step in range(4, steps + 1):
-            weight, ahead, behind = ring_step(step, weight, ahead, behind)
-    else:
+    gated = jnp.concatenate([first, second], axis=1)
+    if not ring:
         weight = lax.all_gather(out_weight, CTX, axis=1, tiled=True)
-    gated = jnp.concatenate([first, second], axis=1)
-    branch = jnp.dot(gated, weight, preferred_element_type=jnp.float32)
-    return (tokens.astype(jnp.float32) + branch).astype(jnp.bfloat16)
+        branch = jnp.dot(gated, weight, preferred_element_type=jnp.float32)
+        return (tokens.astype(jnp.float32) + branch).astype(jnp.bfloat16)
+    gated, ahead, behind = lax.optimization_barrier((gated, ahead, behind))
+    early = len(slots)
+    for step in range(4, steps + 1):
+        ahead, behind = ring_step(step, ahead, behind)
+    chunks = [slots[:early], slots[early:]] if len(slots) > early else [slots]
+    parts = []
+    for chunk in chunks:
+        weight = jnp.concatenate([piece for _, piece in chunk], axis=1)
+        parts.append(jnp.dot(gated, weight, preferred_element_type=jnp.float32))
+    branch = jnp.concatenate(parts, axis=1)
+    blocks = len(slots)
+    owners = jnp.stack([jnp.asarray(c, jnp.int32) for c, _ in slots])
+    inverse = jnp.sum(
+        jnp.where(owners[None, :] == jnp.arange(blocks, dtype=jnp.int32)[:, None], jnp.arange(blocks, dtype=jnp.int32)[None, :], 0),
+        axis=1,
+    )
+    width = out_weight.shape[1]
+    ordered = jnp.take(branch.reshape(row_count, blocks, width), inverse, axis=1).reshape(row_count, blocks * width)
+    return (tokens.astype(jnp.float32) + ordered).astype(jnp.bfloat16)
 
 
 def solution(mesh):

time: 83 us -> 108 us (1.30)
  local copies, waits for them, and re-layouts: 26.3 us -> 45.9 us
  other arithmetic: 4.43 us -> 11.9 us
  waiting for transfers between devices: 2.82 us -> 0.05 us
  starting transfers between devices: 19.6 us -> 21.1 us
  matrix products: 9.18 us -> 7.77 us
    unnamed x14 -> x23, local copies, waits for them, and re-layouts: 0.03 us -> 25.8 us
    dynamic_update_slice x18 -> x0, local copies, waits for them, and re-layouts: 19.8 us -> none  [place(): lax.dynamic_update_slice(weight, part, (row, (owner_chip * 2 + k) * width))]
    gather x0 -> x2, local copies, waits for them, and re-layouts: none -> 10.4 us  [on_device(): jnp.take(branch.reshape(row_count, blocks, width), inverse, axis=1)]
    broadcast_in_dim x1, local copies, waits for them, and re-layouts: 4.34 us -> 0.07 us  [on_device(): jnp.take(branch.reshape(row_count, blocks, width), inverse, axis=1)]
    convert_element_type x0 -> x1, local copies, waits for them, and re-layouts: none -> 3.91 us  [on_device(): return (tokens.astype(jnp.float32) + ordered).astype(jnp.bfloat16)]
    convert_element_type x0 -> x1, other arithmetic: none -> 3.53 us  [on_device(): return (tokens.astype(jnp.float32) + ordered).astype(jnp.bfloat16)]
    ppermute x2, starting transfers between devices: 3.42 us -> 5.89 us  [shifted(): return lax.ppermute(block, CTX, route)]
    reshape x0 -> x1, other arithmetic: none -> 2.4 us  [on_device(): branch.reshape(row_count, blocks, width)]
  transfers between devices with their start and end apart: 19 -> 18, of which waited for: 2 -> 0; matrix products, arithmetic and copies ran while one was open for 36% -> 42% of each run, Pallas kernels for 24% -> 18%
where the time goes in v8:
time: 108 us; the launch traced here: 107 us
  local copies, waits for them, and re-layouts  45.9 us (42%)
  starting transfers between devices  21.1 us (20%)
  Pallas kernels  19.6 us (18%)
  other arithmetic  11.9 us (11%)
  matrix products  7.77 us (7%)
    unnamed x23, local copies, waits for them, and re-layouts  25.8 us
    pallas_call x2, Pallas kernels, hyena_gate(): pl.pallas_call(_gate_kernel, grid=(share,), in_specs=[pl.BlockSpec((per_t...  19.6 us
    ppermute x3, starting transfers between devices, ring_step(): ahead = lax.ppermute(ahead, 'chip', forward)  11.3 us
    gather x2, local copies, waits for them, and re-layouts, on_device(): jnp.take(branch.reshape(row_count, blocks, width), inverse, axis=1)  10.4 us
    dot_general x2, matrix products, on_device(): parts.append(jnp.dot(gated, weight, preferred_element_type=jnp.float32))  7.77 us
    ppermute x2, starting transfers between devices, shifted(): return lax.ppermute(block, CTX, route)  5.89 us
    convert_element_type x1, local copies, waits for them, and re-layouts, on_device(): return (tokens.astype(jnp.float32) + ordered).astype(jnp.bfloat16)  3.91 us
    convert_element_type x1, other arithmetic, on_device(): return (tokens.astype(jnp.float32) + ordered).astype(jnp.bfloat16)  3.53 us
  transfers between devices with their start and end apart: 18, of which 0 were waited for; matrix products, arithmetic and copies ran while one was open for 42% of the time, Pallas kernels for 18%

profile of v8, /device:TPU:0, one launch (start us, length us, event | category | flops | bytes accessed | tf_op | source)
XLA Modules:
  0.0 106.8 jit_solution(16428852370838375603)
XLA Ops:
  0.0 3.0 %collective-permute-start.2 = (bf16[2048,128]{1,0:T(8,128)(2,1)}, bf16[2048,128]{1,0:T(8,128)(2,1)}, u32[]{:S(2)}, u32[]{:S(2)}) collective-permute-start(bf16[2048,128]{1,0:T(8,128)(2,1)} %param.11), channel_id=1, source_target_pairs={{0,4},{4,8},{8,12},{12,14},{14,10},{10,6},{6,2},{2,0},{1,5},{5,9},... | collective-permute-start | bytes 1572872 | tf_op jit(solution)/shard_map/ppermute | solution.py:153
  3.0 1.0 fusion.8
  4.0 2.9 %multiply_convert_fusion = bf16[128,2048]{1,0:T(8,128)(2,1)S(1)} fusion(bf16[512,6144]{1,0:T(8,128)(2,1)} %carrier_ref.2, f32[2048]{0:T(1024)S(1)} %bitcast.69, f32[2048]{0:T(1024)S(1)} %bitcast.65, f32[2048]{0:T(1024)S(1)} %bitcast.66, f32[2048]{0:T(1024)S(1)} %bitcast.67, f32[2048]{0:T(1024)S(1)} %bitcast.68, f32[2048]{0:T(1024)S(1)} %bitcast.64), kind=kLoop, calls=%fused_computation.11 | loop fusion | flops 4718592 | bytes 3719168 | tf_op jit(solution)/shard_map/convert_element_type | solution.py:119
  6.9 2.4 %collective-permute-start = (bf16[128,2048]{1,0:T(8,128)(2,1)S(1)}, bf16[128,2048]{1,0:T(8,128)(2,1)S(1)}, u32[]{:S(2)}, u32[]{:S(2)}) collective-permute-start(bf16[128,2048]{1,0:T(8,128)(2,1)S(1)} %multiply_convert_fusion), channel_id=1, source_target_pairs={{0,1},{1,2},{2,3},{3,4},{4,5},{5,6},{6,7},{7,8},{8,9},{9,10},{10,1... | collective-permute-start | bytes 1572872 | tf_op jit(solution)/shard_map/ppermute | solution.py:22
  9.3 0.9 slice.72
  10.3 3.5 %collective-permute-start.1 = (bf16[2,6144]{1,0:T(2,128)(2,1)S(1)}, bf16[2,6144]{1,0:T(2,128)(2,1)S(1)}, u32[]{:S(2)}, u32[]{:S(2)}) collective-permute-start(bf16[2,6144]{1,0:T(2,128)(2,1)S(1)} %slice.72), channel_id=1, source_target_pairs={{0,1},{1,2},{2,3},{3,4},{4,5},{5,6},{6,7},{7,8},{8,9},{9,10},{10,1... | collective-permute-start | bytes 73736 | tf_op jit(solution)/shard_map/ppermute | solution.py:22
  15.1 1.9 %constant_dynamic-update-slice_fusion.13 = bf16[2048,1792]{1,0:T(8,128)(2,1)} fusion(bf16[2048,128]{1,0:T(8,128)(2,1)} %param.11), kind=kLoop, calls=%fused_computation.27 | loop fusion | bytes 1048576
  17.8 6.2 %collective-permute-start.4 = (bf16[2048,128]{1,0:T(8,128)(2,1)}, bf16[2048,128]{1,0:T(8,128)(2,1)}, u32[]{:S(2)}, u32[]{:S(2)}) collective-permute-start(bf16[2048,128]{1,0:T(8,128)(2,1)} %collective-permute-done.2), channel_id=1, source_target_pairs={{0,4},{4,8},{8,12},{12,14},{14,10},{10,6},{6,2},{2,0},{1,5},{5,9},... | collective-permute-start | bytes 1572872 | tf_op jit(solution)/shard_map/ppermute | solution.py:153
  24.0 2.9 %copy.15 = bf16[512,2048]{0,1:T(8,128)(2,1)S(1)} copy(bf16[512,2048]{1,0:T(8,128)(2,1)} %param.6) | data formatting | bytes 4194304 | tf_op args[0]
  27.4 1.9 %constant_dynamic-update-slice_fusion.12 = bf16[2048,1792]{1,0:T(8,128)(2,1)} fusion(bf16[2048,1792]{1,0:T(8,128)(2,1)} %constant_dynamic-update-slice_fusion.13, bf16[2048,128]{1,0:T(8,128)(2,1)} %collective-permute-done.8), kind=kLoop, calls=%fused_computation.26 | loop fusion | bytes 1048576
  29.3 1.9 %constant_dynamic-update-slice_fusion.11 = bf16[2048,1792]{1,0:T(8,128)(2,1)} fusion(bf16[2048,1792]{1,0:T(8,128)(2,1)} %constant_dynamic-update-slice_fusion.12, bf16[2048,128]{1,0:T(8,128)(2,1)} %collective-permute-done.2), kind=kLoop, calls=%fused_computation.25 | loop fusion | bytes 1048576
  31.2 9.8 %shard_map.64 = bf16[512,1024]{1,0:T(8,128)(2,1)} custom-call(f32[128,384]{1,0:T(8,128)} %pad_convert_fusion.1.fw_ref, f32[1,2048]{1,0:T(1,128)} %bitcast.62, f32[3,3,2048]{2,1,0:T(4,128)} %bitcast.58, bf16[3,2,2048]{2,1,0:T(2,128)(2,1)} %bitcast.60, bf16[128,2048]{1,0:T(8,128)(2,1)} %copy-done.1, bf16[512,6144]{1,0:T(8,128)(2,1)} %carrier_ref.2, ...), custom_call_target="tpu_custom_call" | custom-call | tf_op jit(solution)/shard_map/pallas_call | solution.py:92
  41.1 2.1 %collective-permute-start.6 = (bf16[2048,128]{1,0:T(8,128)(2,1)}, bf16[2048,128]{1,0:T(8,128)(2,1)}, u32[]{:S(2)}, u32[]{:S(2)}) collective-permute-start(bf16[2048,128]{1,0:T(8,128)(2,1)} %collective-permute-done.4), channel_id=1, source_target_pairs={{0,4},{4,8},{8,12},{12,14},{14,10},{10,6},{6,2},{2,0},{1,5},{5,9},... | collective-permute-start | bytes 1572872 | tf_op jit(solution)/shard_map/ppermute | solution.py:153
  43.8 1.9 %constant_dynamic-update-slice_fusion.10 = bf16[2048,1792]{1,0:T(8,128)(2,1)} fusion(bf16[2048,1792]{1,0:T(8,128)(2,1)} %constant_dynamic-update-slice_fusion.11, bf16[2048,128]{1,0:T(8,128)(2,1)} %collective-permute-done.9), kind=kLoop, calls=%fused_computation.24 | loop fusion | bytes 1048576
  46.6 1.9 %constant_dynamic-update-slice_fusion.8 = bf16[2048,1792]{1,0:T(8,128)(2,1)} fusion(bf16[2048,1792]{1,0:T(8,128)(2,1)} %constant_dynamic-update-slice_fusion.9, bf16[2048,128]{1,0:T(8,128)(2,1)} %collective-permute-done.10), kind=kLoop, calls=%fused_computation.22 | loop fusion | bytes 1048576
  49.4 9.9 %shard_map.65 = bf16[512,1024]{1,0:T(8,128)(2,1)} custom-call(f32[128,384]{1,0:T(8,128)} %pad_convert_fusion.fw_ref, f32[1,2048]{1,0:T(1,128)} %bitcast.63, f32[3,3,2048]{2,1,0:T(4,128)} %bitcast.59, bf16[3,2,2048]{2,1,0:T(2,128)(2,1)} %bitcast.61, bf16[128,2048]{1,0:T(8,128)(2,1)} %copy-done.1, bf16[512,6144]{1,0:T(8,128)(2,1)} %carrier_ref.2, ...), custom_call_target="tpu_custom_call" | custom-call | tf_op jit(solution)/shard_map/pallas_call | solution.py:92
  59.2 1.4 %pad_maximum_fusion = bf16[512,2048]{1,0:T(8,128)(2,1)S(1)} fusion(bf16[512,1024]{1,0:T(8,128)(2,1)} %shard_map.65, bf16[512,1024]{1,0:T(8,128)(2,1)S(1)} %copy-done), kind=kLoop, calls=%fused_computation.6 | loop fusion | flops 4194304 | bytes 4194304 | tf_op jit(solution)/shard_map/concatenate | solution.py:182
  60.7 1.9 %constant_dynamic-update-slice_fusion.7 = bf16[2048,1792]{1,0:T(8,128)(2,1)} fusion(bf16[2048,1792]{1,0:T(8,128)(2,1)} %constant_dynamic-update-slice_fusion.8, bf16[2048,128]{1,0:T(8,128)(2,1)} %collective-permute-done.4), kind=kLoop, calls=%fused_computation.21 | loop fusion | bytes 1048576
  62.6 1.0 slice.73
  63.5 2.1 %collective-permute-start.15 = (bf16[1024,128]{1,0:T(8,128)(2,1)S(1)}, bf16[1024,128]{1,0:T(8,128)(2,1)S(1)}, u32[]{:S(2)}, u32[]{:S(2)}) collective-permute-start(bf16[1024,128]{1,0:T(8,128)(2,1)S(1)} %slice.73), channel_id=1, source_target_pairs={{0,4},{4,8},{8,12},{12,14},{14,10},{10,6},{6,2},{2,0},{1,5},{5,9},... | collective-permute-start | bytes 786440 | tf_op jit(solution)/shard_map/ppermute | solution.py:148
  65.6 1.0 slice.74
  67.2 1.9 %constant_dynamic-update-slice_fusion.6 = bf16[2048,1792]{1,0:T(8,128)(2,1)} fusion(bf16[2048,1792]{1,0:T(8,128)(2,1)} %constant_dynamic-update-slice_fusion.7, bf16[2048,128]{1,0:T(8,128)(2,1)} %collective-permute-done.11), kind=kLoop, calls=%fused_computation.20 | loop fusion | bytes 1048576
  69.1 2.0 %constant_dynamic-update-slice_fusion.5 = bf16[2048,1792]{1,0:T(8,128)(2,1)} fusion(bf16[2048,1792]{1,0:T(8,128)(2,1)} %constant_dynamic-update-slice_fusion.6, bf16[2048,128]{1,0:T(8,128)(2,1)} %collective-permute-done.5), kind=kLoop, calls=%fused_computation.19 | loop fusion | bytes 1048576
  71.1 1.9 %constant_dynamic-update-slice_fusion.4 = bf16[2048,1792]{1,0:T(8,128)(2,1)} fusion(bf16[2048,1792]{1,0:T(8,128)(2,1)} %constant_dynamic-update-slice_fusion.5, bf16[2048,128]{1,0:T(8,128)(2,1)} %collective-permute-done.12), kind=kLoop, calls=%fused_computation.18 | loop fusion | bytes 1048576
  73.0 1.9 %constant_dynamic-update-slice_fusion.3 = bf16[2048,1792]{1,0:T(8,128)(2,1)} fusion(bf16[2048,1792]{1,0:T(8,128)(2,1)} %constant_dynamic-update-slice_fusion.4, bf16[2048,128]{1,0:T(8,128)(2,1)} %collective-permute-done.6), kind=kLoop, calls=%fused_computation.17 | loop fusion | bytes 1048576
  76.0 1.9 %constant_dynamic-update-slice_fusion.1 = bf16[2048,1792]{1,0:T(8,128)(2,1)} fusion(bf16[2048,1792]{1,0:T(8,128)(2,1)} %constant_dynamic-update-slice_fusion.2, bf16[2048,128]{1,0:T(8,128)(2,1)} %collective-permute-done.7), kind=kLoop, calls=%fused_computation.15 | loop fusion | bytes 1048576
  78.9 7.0 %fusion.9 = f32[512,1792]{1,0:T(8,128)S(1)} fusion(bf16[512,2048]{1,0:T(8,128)(2,1)S(1)} %pad_maximum_fusion, bf16[2048,1792]{1,0:T(8,128)(2,1)} %constant_dynamic-update-slice_fusion), kind=kOutput, calls=%fused_computation.40 | convolution fusion | flops 3758096384 | bytes 13107200 | tf_op jit(solution)/shard_map/dot_general | solution.py:195
  86.6 2.4 %copy_bitcast_fusion = f32[512,16,128]{2,0,1:T(8,128)} fusion(f32[512,256]{1,0:T(8,128)S(1)} %fusion.2, f32[512,1792]{1,0:T(8,128)S(1)} %fusion.9), kind=kLoop, calls=%fused_computation.1 | loop fusion | flops 1048576 | bytes 8388608 | tf_op jit(solution)/shard_map/reshape | solution.py:204
  89.0 4.9 %gather_fusion = f32[16,512,128]{2,1,0:T(8,128)} fusion(f32[512,16,128]{2,0,1:T(8,128)} %copy_bitcast_fusion, s32[1024]{0:T(1024)S(1)} %pad_clamp_fusion), kind=kCustom, calls=%fused_computation | custom fusion | bytes 8388672 | tf_op jit(solution)/shard_map/jit(_take)/gather | solution.py:204
  94.0 5.4 %copy.18 = f32[512,16,128]{0,2,1:T(8,128)} copy(f32[512,16,128]{2,0,1:T(8,128)} %bitcast.57) | data formatting | bytes 8388608 | tf_op jit(solution)/shard_map/jit(_take)/gather | solution.py:204
  99.4 3.5 %fusion.1 = bf16[512,2048]{0,1:T(8,128)(2,1)} fusion(f32[512,16,128]{0,2,1:T(8,128)} %copy.18, bf16[512,2048]{0,1:T(8,128)(2,1)S(1)} %copy.15, pred[2048]{0:T(1024)(128)(4,1)S(1)} %broadcast_bitcast_fusion), kind=kLoop, calls=%fused_computation.5 | loop fusion | flops 4194304 | bytes 8390656 | tf_op jit(solution)/shard_map/convert_element_type | solution.py:205
  102.9 3.9 %copy.19 = bf16[512,2048]{1,0:T(8,128)(2,1)} copy(bf16[512,2048]{0,1:T(8,128)(2,1)} %fusion.1) | data formatting | bytes 4194304 | tf_op jit(solution)/shard_map/convert_element_type | solution.py:205
  (54 shorter events, 8.2 us)
Async XLA Ops:
  0.0 17.8 %collective-permute-start.2 = (bf16[2048,128]{1,0:T(8,128)(2,1)}, bf16[2048,128]{1,0:T(8,128)(2,1)}, u32[]{:S(2)}, u32[]{:S(2)}) collective-permute-start(bf16[2048,128]{1,0:T(8,128)(2,1)} %param.11), channel_id=1, source_target_pairs={{0,4},{4,8},{8,12},{12,14},{14,10},{10,6},{6,2},{2,0},{1,5},{5,9},... | collective-permute-start | bytes 1572872 | tf_op jit(solution)/shard_map/ppermute | solution.py:153
  3.0 14.8 %collective-permute-start.3 = (bf16[2048,128]{1,0:T(8,128)(2,1)}, bf16[2048,128]{1,0:T(8,128)(2,1)S(1)}, u32[]{:S(2)}, u32[]{:S(2)}) collective-permute-start(bf16[2048,128]{1,0:T(8,128)(2,1)} %param.11), channel_id=1, source_target_pairs={{4,0},{8,4},{12,8},{14,12},{10,14},{6,10},{2,6},{0,2},{5,1},{9,5},... | collective-permute-start | bytes 1572872 | tf_op jit(solution)/shard_map/ppermute | solution.py:154
  3.0 24.4 %collective-permute-start.8 = (bf16[2048,128]{1,0:T(8,128)(2,1)}, bf16[2048,128]{1,0:T(8,128)(2,1)}, u32[]{:S(2)}, u32[]{:S(2)}) collective-permute-start(bf16[2048,128]{1,0:T(8,128)(2,1)} %param.11), channel_id=1, source_target_pairs={{0,1},{1,0},{2,3},{3,2},{4,5},{5,4},{6,7},{7,6},{8,9},{9,8},{10,11... | collective-permute-start | bytes 1572872 | tf_op jit(solution)/shard_map/ppermute | solution.py:141
  6.9 10.9 %collective-permute-start = (bf16[128,2048]{1,0:T(8,128)(2,1)S(1)}, bf16[128,2048]{1,0:T(8,128)(2,1)S(1)}, u32[]{:S(2)}, u32[]{:S(2)}) collective-permute-start(bf16[128,2048]{1,0:T(8,128)(2,1)S(1)} %multiply_convert_fusion), channel_id=1, source_target_pairs={{0,1},{1,2},{2,3},{3,4},{4,5},{5,6},{6,7},{7,8},{8,9},{9,10},{10,1... | collective-permute-start | bytes 1572872 | tf_op jit(solution)/shard_map/ppermute | solution.py:22
  10.3 7.5 %collective-permute-start.1 = (bf16[2,6144]{1,0:T(2,128)(2,1)S(1)}, bf16[2,6144]{1,0:T(2,128)(2,1)S(1)}, u32[]{:S(2)}, u32[]{:S(2)}) collective-permute-start(bf16[2,6144]{1,0:T(2,128)(2,1)S(1)} %slice.72), channel_id=1, source_target_pairs={{0,1},{1,2},{2,3},{3,4},{4,5},{5,6},{6,7},{7,8},{8,9},{9,10},{10,1... | collective-permute-start | bytes 73736 | tf_op jit(solution)/shard_map/ppermute | solution.py:22
  17.8 13.5 %copy-start.3 = (bf16[2,6144]{1,0:T(2,128)(2,1)}, bf16[2,6144]{1,0:T(2,128)(2,1)S(1)}, u32[]{:S(2)}) copy-start(bf16[2,6144]{1,0:T(2,128)(2,1)S(1)} %collective-permute-done.1) | copy-start | bytes 73732
  17.8 13.5 %copy-start.1 = (bf16[128,2048]{1,0:T(8,128)(2,1)}, bf16[128,2048]{1,0:T(8,128)(2,1)S(1)}, u32[]{:S(2)}) copy-start(bf16[128,2048]{1,0:T(8,128)(2,1)S(1)} %collective-permute-done.halo_ref) | copy-start | bytes 1572868
  17.8 23.2 %collective-permute-start.4 = (bf16[2048,128]{1,0:T(8,128)(2,1)}, bf16[2048,128]{1,0:T(8,128)(2,1)}, u32[]{:S(2)}, u32[]{:S(2)}) collective-permute-start(bf16[2048,128]{1,0:T(8,128)(2,1)} %collective-permute-done.2), channel_id=1, source_target_pairs={{0,4},{4,8},{8,12},{12,14},{14,10},{10,6},{6,2},{2,0},{1,5},{5,9},... | collective-permute-start | bytes 1572872 | tf_op jit(solution)/shard_map/ppermute | solution.py:153
  24.0 17.1 %collective-permute-start.5 = (bf16[2048,128]{1,0:T(8,128)(2,1)S(1)}, bf16[2048,128]{1,0:T(8,128)(2,1)}, u32[]{:S(2)}, u32[]{:S(2)}) collective-permute-start(bf16[2048,128]{1,0:T(8,128)(2,1)S(1)} %collective-permute-done.3), channel_id=1, source_target_pairs={{4,0},{8,4},{12,8},{14,12},{10,14},{6,10},{2,6},{0,2},{5,1},{9,5},... | collective-permute-start | bytes 1572872 | tf_op jit(solution)/shard_map/ppermute | solution.py:154
  24.0 19.3 %collective-permute-start.9 = (bf16[2048,128]{1,0:T(8,128)(2,1)}, bf16[2048,128]{1,0:T(8,128)(2,1)}, u32[]{:S(2)}, u32[]{:S(2)}) collective-permute-start(bf16[2048,128]{1,0:T(8,128)(2,1)} %collective-permute-done.2), channel_id=1, source_target_pairs={{0,1},{1,0},{2,3},{3,2},{4,5},{5,4},{6,7},{7,6},{8,9},{9,8},{10,11... | collective-permute-start | bytes 1572872 | tf_op jit(solution)/shard_map/ppermute | solution.py:141
  26.9 19.8 %collective-permute-start.10 = (bf16[2048,128]{1,0:T(8,128)(2,1)S(1)}, bf16[2048,128]{1,0:T(8,128)(2,1)}, u32[]{:S(2)}, u32[]{:S(2)}) collective-permute-start(bf16[2048,128]{1,0:T(8,128)(2,1)S(1)} %collective-permute-done.3), channel_id=1, source_target_pairs={{0,1},{1,0},{2,3},{3,2},{4,5},{5,4},{6,7},{7,6},{8,9},{9,8},{10,11... | collective-permute-start | bytes 1572872 | tf_op jit(solution)/shard_map/ppermute | solution.py:141
  31.2 11.9 %copy-start.2 = (bf16[128,128]{1,0:T(8,128)(2,1)S(1)}, bf16[128,128]{1,0:T(8,128)(2,1)}, u32[]{:S(2)}) copy-start(bf16[128,128]{1,0:T(8,128)(2,1)} %param.9) | copy-start | bytes 98308
  41.1 21.5 %collective-permute-start.6 = (bf16[2048,128]{1,0:T(8,128)(2,1)}, bf16[2048,128]{1,0:T(8,128)(2,1)}, u32[]{:S(2)}, u32[]{:S(2)}) collective-permute-start(bf16[2048,128]{1,0:T(8,128)(2,1)} %collective-permute-done.4), channel_id=1, source_target_pairs={{0,4},{4,8},{8,12},{12,14},{14,10},{10,6},{6,2},{2,0},{1,5},{5,9},... | collective-permute-start | bytes 1572872 | tf_op jit(solution)/shard_map/ppermute | solution.py:153
  43.1 19.4 %collective-permute-start.7 = (bf16[2048,128]{1,0:T(8,128)(2,1)}, bf16[2048,128]{1,0:T(8,128)(2,1)}, u32[]{:S(2)}, u32[]{:S(2)}) collective-permute-start(bf16[2048,128]{1,0:T(8,128)(2,1)} %collective-permute-done.5), channel_id=1, source_target_pairs={{4,0},{8,4},{12,8},{14,12},{10,14},{6,10},{2,6},{0,2},{5,1},{9,5},... | collective-permute-start | bytes 1572872 | tf_op jit(solution)/shard_map/ppermute | solution.py:154
  43.2 23.5 %collective-permute-start.11 = (bf16[2048,128]{1,0:T(8,128)(2,1)}, bf16[2048,128]{1,0:T(8,128)(2,1)}, u32[]{:S(2)}, u32[]{:S(2)}) collective-permute-start(bf16[2048,128]{1,0:T(8,128)(2,1)} %collective-permute-done.4), channel_id=1, source_target_pairs={{0,1},{1,0},{2,3},{3,2},{4,5},{5,4},{6,7},{7,6},{8,9},{9,8},{10,11... | collective-permute-start | bytes 1572872 | tf_op jit(solution)/shard_map/ppermute | solution.py:141
  43.3 27.8 %collective-permute-start.12 = (bf16[2048,128]{1,0:T(8,128)(2,1)}, bf16[2048,128]{1,0:T(8,128)(2,1)}, u32[]{:S(2)}, u32[]{:S(2)}) collective-permute-start(bf16[2048,128]{1,0:T(8,128)(2,1)} %collective-permute-done.5), channel_id=1, source_target_pairs={{0,1},{1,0},{2,3},{3,2},{4,5},{5,4},{6,7},{7,6},{8,9},{9,8},{10,11... | collective-permute-start | bytes 1572872 | tf_op jit(solution)/shard_map/ppermute | solution.py:141
  49.4 9.9 %copy-start = (bf16[512,1024]{1,0:T(8,128)(2,1)S(1)}, bf16[512,1024]{1,0:T(8,128)(2,1)}, u32[]{:S(2)}) copy-start(bf16[512,1024]{1,0:T(8,128)(2,1)} %shard_map.64) | copy-start | bytes 3145732
  63.5 11.4 %collective-permute-start.15 = (bf16[1024,128]{1,0:T(8,128)(2,1)S(1)}, bf16[1024,128]{1,0:T(8,128)(2,1)S(1)}, u32[]{:S(2)}, u32[]{:S(2)}) collective-permute-start(bf16[1024,128]{1,0:T(8,128)(2,1)S(1)} %slice.73), channel_id=1, source_target_pairs={{0,4},{4,8},{8,12},{12,14},{14,10},{10,6},{6,2},{2,0},{1,5},{5,9},... | collective-permute-start | bytes 786440 | tf_op jit(solution)/shard_map/ppermute | solution.py:148
  66.6 8.4 %collective-permute-start.16 = (bf16[1024,128]{1,0:T(8,128)(2,1)S(1)}, bf16[1024,128]{1,0:T(8,128)(2,1)S(1)}, u32[]{:S(2)}, u32[]{:S(2)}) collective-permute-start(bf16[1024,128]{1,0:T(8,128)(2,1)S(1)} %slice.74), channel_id=1, source_target_pairs={{4,0},{8,4},{12,8},{14,12},{10,14},{6,10},{2,6},{0,2},{5,1},{9,5},... | collective-permute-start | bytes 786440 | tf_op jit(solution)/shard_map/ppermute | solution.py:149
  66.6 8.5 %collective-permute-start.13 = (bf16[2048,128]{1,0:T(8,128)(2,1)}, bf16[2048,128]{1,0:T(8,128)(2,1)S(1)}, u32[]{:S(2)}, u32[]{:S(2)}) collective-permute-start(bf16[2048,128]{1,0:T(8,128)(2,1)} %collective-permute-done.6), channel_id=1, source_target_pairs={{0,1},{1,0},{2,3},{3,2},{4,5},{5,4},{6,7},{7,6},{8,9},{9,8},{10,11... | collective-permute-start | bytes 1572872 | tf_op jit(solution)/shard_map/ppermute | solution.py:141
  66.7 11.3 %collective-permute-start.14 = (bf16[2048,128]{1,0:T(8,128)(2,1)}, bf16[2048,128]{1,0:T(8,128)(2,1)S(1)}, u32[]{:S(2)}, u32[]{:S(2)}) collective-permute-start(bf16[2048,128]{1,0:T(8,128)(2,1)} %collective-permute-done.7), channel_id=1, source_target_pairs={{0,1},{1,0},{2,3},{3,2},{4,5},{5,4},{6,7},{7,6},{8,9},{9,8},{10,11... | collective-permute-start | bytes 1572872 | tf_op jit(solution)/shard_map/ppermute | solution.py:141
  75.0 10.9 %collective-permute-start.17 = (bf16[2048,128]{1,0:T(8,128)(2,1)S(1)}, bf16[2048,128]{1,0:T(8,128)(2,1)S(1)}, u32[]{:S(2)}, u32[]{:S(2)}) collective-permute-start(bf16[2048,128]{1,0:T(8,128)(2,1)S(1)} %constant_dynamic-update-slice_fusion.14), channel_id=1, source_target_pairs={{0,1},{1,0},{2,3},{3,2},{4,5},{5,4},{6,7},{7,6},{8,9},{9,8},{10,11... | collective-permute-start | bytes 1572872 | tf_op jit(solution)/shard_map/ppermute | solution.py:141

commit v9 on v5

--- a/solution.py
+++ b/solution.py
@@ -136,32 +136,37 @@
     steps = chips // 2
 
     weight = jnp.zeros((channels, chips * 2 * width), out_weight.dtype)
-
-    def place(weight, piece, owner_chip, row=0):
-        other = lax.ppermute(piece, "core", swap)
-        for k, part in ((core, piece), (1 - core, other)):
-            weight = lax.dynamic_update_slice(weight, part, (row, (owner_chip * 2 + k) * width))
-        return weight
-
-    def ring_step(step, weight, ahead, behind):
-        if step == steps:
-            half = channels // 2
-            ahead = lax.ppermute(ahead[:half], "chip", forward)
-            behind = lax.ppermute(behind[half:], "chip", backward)
-            source = ring_chip((position - step) % chips, chips)
-            weight = place(weight, ahead, source, 0)
-            weight = place(weight, behind, source, half)
-        else:
-            ahead = lax.ppermute(ahead, "chip", forward)
-            behind = lax.ppermute(behind, "chip", backward)
-            weight = place(weight, ahead, ring_chip((position - step) % chips, chips))
-            weight = place(weight, behind, ring_chip((position + step) % chips, chips))
-        return weight, ahead, behind
-
-    ahead = behind = out_weight
+    first_core = core == 0
+    clockwise = [(order[i] * 2, order[(i + 1) % chips] * 2) for i in range(chips)]
+    counter = [(order[(i + 1) % chips] * 2 + 1, order[i] * 2 + 1) for i in range(chips)]
+
+    def place(weight, pair, owner_chip):
+        return lax.dynamic_update_slice(weight, pair, (0, owner_chip * 2 * width))
+
+    def ring_step(step, weight, held):
+        last = step == steps
+        route = clockwise if last else clockwise + counter
+        held = lax.ppermute(held, CTX, route)
+        ahead = ring_chip((position - step) % chips, chips)
+        if last:
+            given = lax.ppermute(held, "core", [(0, 1)])
+            return place(weight, jnp.where(first_core, held, given), ahead), held
+        behind = ring_chip((position + step) % chips, chips)
+        given = lax.ppermute(held, "core", swap)
+        weight = place(weight, held, jnp.where(first_core, ahead, behind))
+        weight = place(weight, given, jnp.where(first_core, behind, ahead))
+        return weight, held
+
+    held = out_weight
     if ring:
-        weight = place(weight, out_weight, chip)
-        weight, ahead, behind = ring_step(1, weight, ahead, behind)
+        partner = lax.ppermute(out_weight, "core", swap)
+        held = jnp.where(
+            first_core,
+            jnp.concatenate([out_weight, partner], axis=1),
+            jnp.concatenate([partner, out_weight], axis=1),
+        )
+        weight = place(weight, held, chip)
+        weight, held = ring_step(1, weight, held)
 
     tail = projected[row_count - BLOCK - 2 :]
     tail_mixed = [
@@ -170,21 +175,21 @@
     ]
     halo = shifted(carried_of(*tail_mixed), 1)
     edge = shifted(projected[row_count - 2 :], 1)
-    halo, edge, ahead, behind = lax.optimization_barrier((halo, edge, ahead, behind))
+    halo, edge, held = lax.optimization_barrier((halo, edge, held))
     if ring and steps >= 2:
-        weight, ahead, behind = ring_step(2, weight, ahead, behind)
+        weight, held = ring_step(2, weight, held)
 
     inputs = (halo, edge, projected, short_filter, long_filter, conv_bias)
     first = hyena_gate(*inputs, 0, 2)
     if ring:
-        first, ahead, behind, inputs = lax.optimization_barrier((first, ahead, behind, inputs))
+        first, held, inputs = lax.optimization_barrier((first, held, inputs))
         if steps >= 3:
-            weight, ahead, behind = ring_step(3, weight, ahead, behind)
+            weight, held = ring_step(3, weight, held)
     second = hyena_gate(*inputs, 1, 2)
     if ring:
-        second, ahead, behind = lax.optimization_barrier((second, ahead, behind))
+        second, held = lax.optimization_barrier((second, held))
         for step in range(4, steps + 1):
-            weight, ahead, behind = ring_step(step, weight, ahead, behind)
+            weight, held = ring_step(step, weight, held)
     else:
         weight = lax.all_gather(out_weight, CTX, axis=1, tiled=True)
     gated = jnp.concatenate([first, second], axis=1)

time: 83 us -> 95.4 us (1.15)
  waiting for transfers between devices: 2.82 us -> 23.2 us
  local copies, waits for them, and re-layouts: 26.3 us -> 13.1 us
  starting transfers between devices: 19.6 us -> 24.2 us
    ppermute x17 -> x9, waiting for transfers between devices: 2.82 us -> 22.4 us  [the longest x4 20.6 us: ring_step(): held = lax.ppermute(held, CTX, route)]
    dynamic_update_slice x18 -> x6, local copies, waits for them, and re-layouts: 19.8 us -> 11.8 us  [place(): return lax.dynamic_update_slice(weight, pair, (0, owner_chip * 2 * width))]
    ppermute x17 -> x9, starting transfers between devices: 16.2 us -> 20.3 us  [the longest x4 17.8 us: ring_step(): held = lax.ppermute(held, CTX, route)]
    broadcast_in_dim x1, local copies, waits for them, and re-layouts: 4.34 us -> 1.05 us  [on_device(): weight = jnp.zeros((channels, chips * 2 * width), out_weight.dtype)]
    dynamic_update_slice x0 -> x2, other arithmetic: none -> 3.02 us  [place(): return lax.dynamic_update_slice(weight, pair, (0, owner_chip * 2 * width))]
    convert_element_type x1, other arithmetic: 2.9 us -> 0.74 us  [carried_of(): return (second * carrier).astype(jnp.bfloat16)]
  transfers between devices with their start and end apart: 19 -> 11, of which waited for: 2 -> 6; matrix products, arithmetic and copies ran while one was open for 36% -> 15% of each run, Pallas kernels for 24% -> 21%
where the time goes in v9:
time: 95.4 us; the launch traced here: 94.6 us
  starting transfers between devices  24.2 us (25%)
  waiting for transfers between devices  23.2 us (24%)
  Pallas kernels  19.5 us (20%)
  local copies, waits for them, and re-layouts  13.1 us (14%)
  matrix products  9.14 us (10%)
  other arithmetic  5.29 us (6%)
    ppermute x4, waiting for transfers between devices, ring_step(): held = lax.ppermute(held, CTX, route)  20.6 us
    pallas_call x2, Pallas kernels, hyena_gate(): pl.pallas_call(_gate_kernel, grid=(share,), in_specs=[pl.BlockSpec((per_t...  19.5 us
    ppermute x4, starting transfers between devices, ring_step(): held = lax.ppermute(held, CTX, route)  17.8 us
    dynamic_update_slice x6, local copies, waits for them, and re-layouts, place(): return lax.dynamic_update_slice(weight, pair, (0, owner_chip * 2 * width))  11.8 us
    dot_general x1, matrix products, on_device(): branch = jnp.dot(gated, weight, preferred_element_type=jnp.float32)  9.14 us
    ppermute x2, starting transfers between devices, shifted(): return lax.ppermute(block, CTX, route)  3.92 us
    dynamic_update_slice x2, other arithmetic, place(): return lax.dynamic_update_slice(weight, pair, (0, owner_chip * 2 * width))  3.02 us
  transfers between devices with their start and end apart: 11, of which 6 were waited for; matrix products, arithmetic and copies ran while one was open for 15% of the time, Pallas kernels for 21%

profile of v9, /device:TPU:0, one launch (start us, length us, event | category | flops | bytes accessed | tf_op | source)
XLA Modules:
  0.0 94.6 jit_solution(6165945876360438370)
XLA Ops:
  0.0 0.5 collective-permute-start.2
  0.5 1.7 %collective-permute-done.2 = bf16[2048,128]{1,0:T(8,128)(2,1)S(1)} collective-permute-done((bf16[2048,128]{1,0:T(8,128)(2,1)}, bf16[2048,128]{1,0:T(8,128)(2,1)S(1)}, u32[]{:S(2)}, u32[]{:S(2)}) %collective-permute-start.2) | collective-permute-done | bytes 524320 | tf_op jit(solution)/shard_map/ppermute | solution.py:162
  2.3 1.1 %broadcast_in_dim.3 = bf16[2048,2048]{1,0:T(8,128)(2,1)S(1)} broadcast(bf16[]{:T(256)} %constant.82.clone.1), dimensions={} | broadcast | bytes 8388610 | tf_op jit(solution)/shard_map/broadcast_in_dim | solution.py:138
  3.4 0.4 constant_dynamic-update-slice_fusion.6
  3.8 3.0 %collective-permute-start.3 = (bf16[2048,256]{1,0:T(8,128)(2,1)S(1)}, bf16[2048,256]{1,0:T(8,128)(2,1)}, u32[]{:S(2)}, u32[]{:S(2)}) collective-permute-start(bf16[2048,256]{1,0:T(8,128)(2,1)S(1)} %get-tuple-element.32), channel_id=1, source_target_pairs={{0,4},{4,8},{8,12},{12,14},{14,10},{10,6},{6,2},{2,0},{5,1},{9,5},... | collective-permute-start | bytes 3145736 | tf_op jit(solution)/shard_map/ppermute | solution.py:149
  6.9 0.7 multiply_convert_fusion
  7.6 1.8 %collective-permute-start = (bf16[128,2048]{1,0:T(8,128)(2,1)S(1)}, bf16[128,2048]{1,0:T(8,128)(2,1)S(1)}, u32[]{:S(2)}, u32[]{:S(2)}) collective-permute-start(bf16[128,2048]{1,0:T(8,128)(2,1)S(1)} %multiply_convert_fusion), channel_id=1, source_target_pairs={{0,1},{1,2},{2,3},{3,4},{4,5},{5,6},{6,7},{7,8},{8,9},{9,10},{10,1... | collective-permute-start | bytes 1572872 | tf_op jit(solution)/shard_map/ppermute | solution.py:22
  9.4 2.2 %collective-permute-start.1 = (bf16[2,6144]{1,0:T(2,128)(2,1)S(1)}, bf16[2,6144]{1,0:T(2,128)(2,1)S(1)}, u32[]{:S(2)}, u32[]{:S(2)}) collective-permute-start(bf16[2,6144]{1,0:T(2,128)(2,1)S(1)} %slice.66), channel_id=1, source_target_pairs={{0,1},{1,2},{2,3},{3,4},{4,5},{5,6},{6,7},{7,8},{8,9},{9,10},{10,1... | collective-permute-start | bytes 73736 | tf_op jit(solution)/shard_map/ppermute | solution.py:22
  11.6 0.8 collective-permute-done.1
  12.4 7.2 %collective-permute-done.3 = bf16[2048,256]{1,0:T(8,128)(2,1)} collective-permute-done((bf16[2048,256]{1,0:T(8,128)(2,1)S(1)}, bf16[2048,256]{1,0:T(8,128)(2,1)}, u32[]{:S(2)}, u32[]{:S(2)}) %collective-permute-start.3) | collective-permute-done | bytes 1048608 | tf_op jit(solution)/shard_map/ppermute | solution.py:149
  19.6 8.0 %collective-permute-start.4 = (bf16[2048,256]{1,0:T(8,128)(2,1)}, bf16[2048,256]{1,0:T(8,128)(2,1)}, u32[]{:S(2)}, u32[]{:S(2)}) collective-permute-start(bf16[2048,256]{1,0:T(8,128)(2,1)} %collective-permute-done.3), channel_id=1, source_target_pairs={{0,4},{4,8},{8,12},{12,14},{14,10},{10,6},{6,2},{2,0},{5,1},{9,5},... | collective-permute-start | bytes 3145736 | tf_op jit(solution)/shard_map/ppermute | solution.py:149
  27.7 0.1 rev.6
  27.8 0.8 pad_convert_fusion.1.fw_ref
  28.6 9.7 %shard_map.64 = bf16[512,1024]{1,0:T(8,128)(2,1)} custom-call(f32[128,384]{1,0:T(8,128)} %pad_convert_fusion.1.fw_ref, f32[1,2048]{1,0:T(1,128)} %bitcast.27, f32[3,3,2048]{2,1,0:T(4,128)} %bitcast.23, bf16[3,2,2048]{2,1,0:T(2,128)(2,1)} %bitcast.25, bf16[128,2048]{1,0:T(8,128)(2,1)} %copy-done.1, bf16[512,6144]{1,0:T(8,128)(2,1)} %carrier_ref.2, ...), custom_call_target="tpu_custom_call" | custom-call | tf_op jit(solution)/shard_map/pallas_call | solution.py:92
  38.3 2.0 %collective-permute-done.4 = bf16[2048,256]{1,0:T(8,128)(2,1)} collective-permute-done((bf16[2048,256]{1,0:T(8,128)(2,1)}, bf16[2048,256]{1,0:T(8,128)(2,1)}, u32[]{:S(2)}, u32[]{:S(2)}) %collective-permute-start.4) | collective-permute-done | bytes 1048608 | tf_op jit(solution)/shard_map/ppermute | solution.py:149
  40.3 2.5 %collective-permute-start.5 = (bf16[2048,256]{1,0:T(8,128)(2,1)}, bf16[2048,256]{1,0:T(8,128)(2,1)S(1)}, u32[]{:S(2)}, u32[]{:S(2)}) collective-permute-start(bf16[2048,256]{1,0:T(8,128)(2,1)} %collective-permute-done.4), channel_id=1, source_target_pairs={{0,4},{4,8},{8,12},{12,14},{14,10},{10,6},{6,2},{2,0},{5,1},{9,5},... | collective-permute-start | bytes 3145736 | tf_op jit(solution)/shard_map/ppermute | solution.py:149
  42.8 0.1 rev.7
  42.9 0.8 pad_convert_fusion.fw_ref
  43.7 9.8 %shard_map.65 = bf16[512,1024]{1,0:T(8,128)(2,1)} custom-call(f32[128,384]{1,0:T(8,128)} %pad_convert_fusion.fw_ref, f32[1,2048]{1,0:T(1,128)} %bitcast.28, f32[3,3,2048]{2,1,0:T(4,128)} %bitcast.24, bf16[3,2,2048]{2,1,0:T(2,128)(2,1)} %bitcast.26, bf16[128,2048]{1,0:T(8,128)(2,1)} %copy-done.1, bf16[512,6144]{1,0:T(8,128)(2,1)} %carrier_ref.2, ...), custom_call_target="tpu_custom_call" | custom-call | tf_op jit(solution)/shard_map/pallas_call | solution.py:92
  53.4 2.0 %collective-permute-done.5 = bf16[2048,256]{1,0:T(8,128)(2,1)S(1)} collective-permute-done((bf16[2048,256]{1,0:T(8,128)(2,1)}, bf16[2048,256]{1,0:T(8,128)(2,1)S(1)}, u32[]{:S(2)}, u32[]{:S(2)}) %collective-permute-start.5) | collective-permute-done | bytes 1048608 | tf_op jit(solution)/shard_map/ppermute | solution.py:149
  55.4 4.3 %collective-permute-start.9 = (bf16[2048,256]{1,0:T(8,128)(2,1)S(1)}, bf16[2048,256]{1,0:T(8,128)(2,1)}, u32[]{:S(2)}, u32[]{:S(2)}) collective-permute-start(bf16[2048,256]{1,0:T(8,128)(2,1)S(1)} %collective-permute-done.5), channel_id=1, source_target_pairs={{0,4},{4,8},{8,12},{12,14},{14,10},{10,6},{6,2},{2,0},{16,20},{20,... | collective-permute-start | bytes 3145736 | tf_op jit(solution)/shard_map/ppermute | solution.py:149
  59.8 0.5 collective-permute-start.7
  60.4 2.5 %constant_dynamic-update-slice_fusion.5 = bf16[2048,2048]{1,0:T(8,128)(2,1)} fusion(bf16[2048,2048]{1,0:T(8,128)(2,1)} %copy-done, bf16[2048,256]{1,0:T(8,128)(2,1)} %collective-permute-done.3, s32[]{:T(128)S(6)} %select_n.129), kind=kLoop, calls=%fused_computation.14 | loop fusion | bytes 2097156 | tf_op jit(solution)/shard_map/dynamic_update_slice | solution.py:144
  62.9 9.4 %collective-permute-done.9 = bf16[2048,256]{1,0:T(8,128)(2,1)} collective-permute-done((bf16[2048,256]{1,0:T(8,128)(2,1)S(1)}, bf16[2048,256]{1,0:T(8,128)(2,1)}, u32[]{:S(2)}, u32[]{:S(2)}) %collective-permute-start.9) | collective-permute-done | bytes 1048608 | tf_op jit(solution)/shard_map/ppermute | solution.py:149
  72.2 1.3 %collective-permute-start.10 = (bf16[2048,256]{1,0:T(8,128)(2,1)}, bf16[2048,256]{1,0:T(8,128)(2,1)S(1)}, u32[]{:S(2)}, u32[]{:S(2)}) collective-permute-start(bf16[2048,256]{1,0:T(8,128)(2,1)} %collective-permute-done.9), channel_id=1, source_target_pairs={{0,1},{2,3},{4,5},{6,7},{8,9},{10,11},{12,13},{14,15},{16,17},{18,... | collective-permute-start | bytes 3145736 | tf_op jit(solution)/shard_map/ppermute | solution.py:152
  73.6 2.4 %constant_dynamic-update-slice_fusion.4 = bf16[2048,2048]{1,0:T(8,128)(2,1)} fusion(bf16[2048,2048]{1,0:T(8,128)(2,1)} %constant_dynamic-update-slice_fusion.5, bf16[2048,256]{1,0:T(8,128)(2,1)} %collective-permute-done.6, s32[]{:T(128)S(6)} %select_n.131), kind=kLoop, calls=%fused_computation.13 | loop fusion | bytes 2097156 | tf_op jit(solution)/shard_map/dynamic_update_slice | solution.py:144
  76.0 2.3 %constant_dynamic-update-slice_fusion.3 = bf16[2048,2048]{1,0:T(8,128)(2,1)} fusion(bf16[2048,2048]{1,0:T(8,128)(2,1)} %constant_dynamic-update-slice_fusion.4, bf16[2048,256]{1,0:T(8,128)(2,1)} %collective-permute-done.4, s32[]{:T(128)S(6)} %select_n.137), kind=kLoop, calls=%fused_computation.12 | loop fusion | bytes 2097156 | tf_op jit(solution)/shard_map/dynamic_update_slice | solution.py:144
  78.3 2.4 %constant_dynamic-update-slice_fusion.2 = bf16[2048,2048]{1,0:T(8,128)(2,1)} fusion(bf16[2048,2048]{1,0:T(8,128)(2,1)} %constant_dynamic-update-slice_fusion.3, bf16[2048,256]{1,0:T(8,128)(2,1)} %collective-permute-done.7, s32[]{:T(128)S(6)} %select_n.139), kind=kLoop, calls=%fused_computation.11 | loop fusion | bytes 2097156 | tf_op jit(solution)/shard_map/dynamic_update_slice | solution.py:144
  80.7 1.1 %constant_dynamic-update-slice_fusion.1 = bf16[2048,2048]{1,0:T(8,128)(2,1)} fusion(bf16[2048,2048]{1,0:T(8,128)(2,1)} %constant_dynamic-update-slice_fusion.2, bf16[2048,256]{1,0:T(8,128)(2,1)S(1)} %collective-permute-done.5, s32[]{:T(128)S(6)} %select_n.145), kind=kLoop, calls=%fused_computation.10 | loop fusion | bytes 2097156 | tf_op jit(solution)/shard_map/dynamic_update_slice | solution.py:144
  81.8 1.1 %constant_dynamic-update-slice_fusion = bf16[2048,2048]{1,0:T(8,128)(2,1)} fusion(bf16[2048,2048]{1,0:T(8,128)(2,1)} %constant_dynamic-update-slice_fusion.1, bf16[2048,256]{1,0:T(8,128)(2,1)S(1)} %collective-permute-done.8, s32[]{:T(128)S(6)} %select_n.147), kind=kLoop, calls=%fused_computation.9 | loop fusion | bytes 2097156 | tf_op jit(solution)/shard_map/dynamic_update_slice | solution.py:144
  82.9 2.6 %select_dynamic-update-slice_fusion = bf16[2048,2048]{1,0:T(8,128)(2,1)} fusion(bf16[2048,2048]{1,0:T(8,128)(2,1)} %constant_dynamic-update-slice_fusion, s32[]{:T(128)S(6)} %select_n.151, bf16[2048,256]{1,0:T(8,128)(2,1)} %collective-permute-done.9, bf16[2048,256]{1,0:T(8,128)(2,1)S(1)} %collective-permute-done.10, pred[]{:T(512)S(6)} %eq.15), kind=kLoop, calls=%fused_computation.5 | loop fusion | flops 524288 | bytes 3145733 | tf_op jit(solution)/shard_map/dynamic_update_slice | solution.py:144
  85.5 9.1 %add_convert_fusion = bf16[512,2048]{1,0:T(8,128)(2,1)} fusion(bf16[512,2048]{1,0:T(8,128)(2,1)S(1)} %copy-done.8, bf16[2048,2048]{1,0:T(8,128)(2,1)} %select_dynamic-update-slice_fusion, bf16[512,1024]{1,0:T(8,128)(2,1)S(1)} %copy-done.3, bf16[512,1024]{1,0:T(8,128)(2,1)S(1)} %copy-done.2), kind=kOutput, calls=%fused_computation | convolution fusion | flops 4302307328 | bytes 14680064 | tf_op jit(solution)/shard_map/dot_general | solution.py:196
  (32 shorter events, 0.3 us)
Async XLA Ops:
  0.0 3.3 %copy-start.5 = (bf16[2048,128]{1,0:T(8,128)(2,1)S(1)}, bf16[2048,128]{1,0:T(8,128)(2,1)}, u32[]{:S(2)}) copy-start(bf16[2048,128]{1,0:T(8,128)(2,1)} %param.11) | copy-start | bytes 1572868
  0.0 6.8 %copy-start.4 = (f32[3,6144]{1,0:T(4,128)S(1)}, f32[3,6144]{1,0:T(4,128)}, u32[]{:S(2)}) copy-start(f32[3,6144]{1,0:T(4,128)} %param.8) | copy-start | bytes 221188
  0.0 6.8 %slice-start = ((s8[6291456]{0:T(1024)(128)(4,1)}), s8[2097152]{0:T(1024)(128)(4,1)S(1)}, s32[]{:S(2)}) async-start(s8[6291456]{0:T(1024)(128)(4,1)} %bitcast.21), calls=%async_computation | async-start | bytes 4194304
  0.0 27.7 %copy-start.6 = (bf16[128,128]{1,0:T(8,128)(2,1)S(1)}, bf16[128,128]{1,0:T(8,128)(2,1)}, u32[]{:S(2)}) copy-start(bf16[128,128]{1,0:T(8,128)(2,1)} %param.9) | copy-start | bytes 98308
  0.0 2.3 %collective-permute-start.2 = (bf16[2048,128]{1,0:T(8,128)(2,1)}, bf16[2048,128]{1,0:T(8,128)(2,1)S(1)}, u32[]{:S(2)}, u32[]{:S(2)}) collective-permute-start(bf16[2048,128]{1,0:T(8,128)(2,1)} %param.11), channel_id=1, source_target_pairs={{0,1},{1,0},{2,3},{3,2},{4,5},{5,4},{6,7},{7,6},{8,9},{9,8},{10,11... | collective-permute-start | bytes 1572872 | tf_op jit(solution)/shard_map/ppermute | solution.py:162
  0.5 6.3 %slice-start.1 = ((s8[6291456]{0:T(1024)(128)(4,1)}), s8[4194304]{0:T(1024)(128)(4,1)S(1)}, s32[]{:S(2)}) async-start(s8[6291456]{0:T(1024)(128)(4,1)} %bitcast.21), calls=%async_computation.1 | async-start | bytes 8388608
  3.8 5.6 %copy-start = (bf16[2048,2048]{1,0:T(8,128)(2,1)}, bf16[2048,2048]{1,0:T(8,128)(2,1)S(1)}, u32[]{:S(2)}) copy-start(bf16[2048,2048]{1,0:T(8,128)(2,1)S(1)} %get-tuple-element.31) | copy-start | bytes 25165828
  3.8 15.8 %collective-permute-start.3 = (bf16[2048,256]{1,0:T(8,128)(2,1)S(1)}, bf16[2048,256]{1,0:T(8,128)(2,1)}, u32[]{:S(2)}, u32[]{:S(2)}) collective-permute-start(bf16[2048,256]{1,0:T(8,128)(2,1)S(1)} %get-tuple-element.32), channel_id=1, source_target_pairs={{0,4},{4,8},{8,12},{12,14},{14,10},{10,6},{6,2},{2,0},{5,1},{9,5},... | collective-permute-start | bytes 3145736 | tf_op jit(solution)/shard_map/ppermute | solution.py:149
  7.6 4.8 %collective-permute-start = (bf16[128,2048]{1,0:T(8,128)(2,1)S(1)}, bf16[128,2048]{1,0:T(8,128)(2,1)S(1)}, u32[]{:S(2)}, u32[]{:S(2)}) collective-permute-start(bf16[128,2048]{1,0:T(8,128)(2,1)S(1)} %multiply_convert_fusion), channel_id=1, source_target_pairs={{0,1},{1,2},{2,3},{3,4},{4,5},{5,6},{6,7},{7,8},{8,9},{9,10},{10,1... | collective-permute-start | bytes 1572872 | tf_op jit(solution)/shard_map/ppermute | solution.py:22
  9.4 3.0 %collective-permute-start.1 = (bf16[2,6144]{1,0:T(2,128)(2,1)S(1)}, bf16[2,6144]{1,0:T(2,128)(2,1)S(1)}, u32[]{:S(2)}, u32[]{:S(2)}) collective-permute-start(bf16[2,6144]{1,0:T(2,128)(2,1)S(1)} %slice.66), channel_id=1, source_target_pairs={{0,1},{1,2},{2,3},{3,4},{4,5},{5,6},{6,7},{7,8},{8,9},{9,10},{10,1... | collective-permute-start | bytes 73736 | tf_op jit(solution)/shard_map/ppermute | solution.py:22
  12.4 16.1 %copy-start.7 = (bf16[2,6144]{1,0:T(2,128)(2,1)}, bf16[2,6144]{1,0:T(2,128)(2,1)S(1)}, u32[]{:S(2)}) copy-start(bf16[2,6144]{1,0:T(2,128)(2,1)S(1)} %collective-permute-done.1) | copy-start | bytes 73732
  12.4 16.1 %copy-start.1 = (bf16[128,2048]{1,0:T(8,128)(2,1)}, bf16[128,2048]{1,0:T(8,128)(2,1)S(1)}, u32[]{:S(2)}) copy-start(bf16[128,2048]{1,0:T(8,128)(2,1)S(1)} %collective-permute-done.halo_ref) | copy-start | bytes 1572868
  19.6 20.7 %collective-permute-start.4 = (bf16[2048,256]{1,0:T(8,128)(2,1)}, bf16[2048,256]{1,0:T(8,128)(2,1)}, u32[]{:S(2)}, u32[]{:S(2)}) collective-permute-start(bf16[2048,256]{1,0:T(8,128)(2,1)} %collective-permute-done.3), channel_id=1, source_target_pairs={{0,4},{4,8},{8,12},{12,14},{14,10},{10,6},{6,2},{2,0},{5,1},{9,5},... | collective-permute-start | bytes 3145736 | tf_op jit(solution)/shard_map/ppermute | solution.py:149
  40.3 15.1 %collective-permute-start.5 = (bf16[2048,256]{1,0:T(8,128)(2,1)}, bf16[2048,256]{1,0:T(8,128)(2,1)S(1)}, u32[]{:S(2)}, u32[]{:S(2)}) collective-permute-start(bf16[2048,256]{1,0:T(8,128)(2,1)} %collective-permute-done.4), channel_id=1, source_target_pairs={{0,4},{4,8},{8,12},{12,14},{14,10},{10,6},{6,2},{2,0},{5,1},{9,5},... | collective-permute-start | bytes 3145736 | tf_op jit(solution)/shard_map/ppermute | solution.py:149
  53.4 32.1 %copy-start.2 = (bf16[512,1024]{1,0:T(8,128)(2,1)S(1)}, bf16[512,1024]{1,0:T(8,128)(2,1)}, u32[]{:S(2)}) copy-start(bf16[512,1024]{1,0:T(8,128)(2,1)} %shard_map.64) | copy-start | bytes 3145732
  53.4 32.1 %copy-start.3 = (bf16[512,1024]{1,0:T(8,128)(2,1)S(1)}, bf16[512,1024]{1,0:T(8,128)(2,1)}, u32[]{:S(2)}) copy-start(bf16[512,1024]{1,0:T(8,128)(2,1)} %shard_map.65) | copy-start | bytes 3145732
  55.4 16.8 %collective-permute-start.9 = (bf16[2048,256]{1,0:T(8,128)(2,1)S(1)}, bf16[2048,256]{1,0:T(8,128)(2,1)}, u32[]{:S(2)}, u32[]{:S(2)}) collective-permute-start(bf16[2048,256]{1,0:T(8,128)(2,1)S(1)} %collective-permute-done.5), channel_id=1, source_target_pairs={{0,4},{4,8},{8,12},{12,14},{14,10},{10,6},{6,2},{2,0},{16,20},{20,... | collective-permute-start | bytes 3145736 | tf_op jit(solution)/shard_map/ppermute | solution.py:149
  59.7 13.9 %collective-permute-start.6 = (bf16[2048,256]{1,0:T(8,128)(2,1)}, bf16[2048,256]{1,0:T(8,128)(2,1)}, u32[]{:S(2)}, u32[]{:S(2)}) collective-permute-start(bf16[2048,256]{1,0:T(8,128)(2,1)} %collective-permute-done.3), channel_id=1, source_target_pairs={{0,1},{1,0},{2,3},{3,2},{4,5},{5,4},{6,7},{7,6},{8,9},{9,8},{10,11... | collective-permute-start | bytes 3145736 | tf_op jit(solution)/shard_map/ppermute | solution.py:155
  59.8 18.5 %collective-permute-start.7 = (bf16[2048,256]{1,0:T(8,128)(2,1)}, bf16[2048,256]{1,0:T(8,128)(2,1)}, u32[]{:S(2)}, u32[]{:S(2)}) collective-permute-start(bf16[2048,256]{1,0:T(8,128)(2,1)} %collective-permute-done.4), channel_id=1, source_target_pairs={{0,1},{1,0},{2,3},{3,2},{4,5},{5,4},{6,7},{7,6},{8,9},{9,8},{10,11... | collective-permute-start | bytes 3145736 | tf_op jit(solution)/shard_map/ppermute | solution.py:155
  60.3 25.2 %copy-start.8 = (bf16[512,2048]{1,0:T(8,128)(2,1)S(1)}, bf16[512,2048]{1,0:T(8,128)(2,1)}, u32[]{:S(2)}) copy-start(bf16[512,2048]{1,0:T(8,128)(2,1)} %param.6) | copy-start | bytes 6291460
  60.3 21.5 %collective-permute-start.8 = (bf16[2048,256]{1,0:T(8,128)(2,1)S(1)}, bf16[2048,256]{1,0:T(8,128)(2,1)S(1)}, u32[]{:S(2)}, u32[]{:S(2)}) collective-permute-start(bf16[2048,256]{1,0:T(8,128)(2,1)S(1)} %collective-permute-done.5), channel_id=1, source_target_pairs={{0,1},{1,0},{2,3},{3,2},{4,5},{5,4},{6,7},{7,6},{8,9},{9,8},{10,11... | collective-permute-start | bytes 3145736 | tf_op jit(solution)/shard_map/ppermute | solution.py:155
  72.2 10.7 %collective-permute-start.10 = (bf16[2048,256]{1,0:T(8,128)(2,1)}, bf16[2048,256]{1,0:T(8,128)(2,1)S(1)}, u32[]{:S(2)}, u32[]{:S(2)}) collective-permute-start(bf16[2048,256]{1,0:T(8,128)(2,1)} %collective-permute-done.9), channel_id=1, source_target_pairs={{0,1},{2,3},{4,5},{6,7},{8,9},{10,11},{12,13},{14,15},{16,17},{18,... | collective-permute-start | bytes 3145736 | tf_op jit(solution)/shard_map/ppermute | solution.py:152

commit v10 on v5

--- a/solution.py
+++ b/solution.py
@@ -63,17 +63,20 @@
         v = jnp.broadcast_to(fw_ref[i : i + 1, :], (BLOCK, fw_ref.shape[1]))
         rolled = pltpu.roll(v, 0, 1, stride=1, stride_axis=0)
         toeplitz.append(rolled[:, : 2 * BLOCK].astype(jnp.bfloat16))
+    stacked = jnp.concatenate(toeplitz, axis=1)
+    columns = []
+    for b in range(blocks):
+        before = halo_ref[...] if b == 0 else carried[BLOCK * (b - 1) : BLOCK * b]
+        window = jnp.concatenate([before, carried[BLOCK * b : BLOCK * (b + 1)]], axis=0)
+        zero = jnp.zeros_like(window)
+        columns.append(jnp.concatenate([jnp.where(owner == i, window, zero) for i in range(per_tile)], axis=0))
+    conv = jnp.dot(stacked, jnp.concatenate(columns, axis=1), preferred_element_type=jnp.float32)
     bias = bias_ref[...]
     for b in range(blocks):
-        before = halo_ref[...] if b == 0 else carried[BLOCK * (b - 1) : BLOCK * b]
         current = carried[BLOCK * b : BLOCK * (b + 1)]
-        window = jnp.concatenate([before, current], axis=0)
-        acc = jnp.zeros((BLOCK, lanes), jnp.float32)
-        for i in range(per_tile):
-            masked = jnp.where(owner == i, window, jnp.zeros_like(window))
-            acc = acc + jnp.dot(toeplitz[i], masked, preferred_element_type=jnp.float32)
         gate = gate_rows[BLOCK * b : BLOCK * (b + 1)]
         direct = bias * current.astype(jnp.float32)
+        acc = conv[:, BLOCK * b : BLOCK * (b + 1)]
         out_ref[BLOCK * b : BLOCK * (b + 1), :] = (gate * (acc + direct)).astype(out_ref.dtype)
 
 

time: 83 us -> 80.8 us (0.973)
  Pallas kernels: 19.5 us -> 17.3 us
    pallas_call x2, Pallas kernels: 19.5 us -> 17.3 us  [hyena_gate(): pl.pallas_call(_gate_kernel, grid=(share,), in_specs=[pl.BlockSpec((per_t...]
  transfers between devices with their start and end apart: 19 -> 19, of which waited for: 2 -> 2; matrix products, arithmetic and copies ran while one was open for 36% -> 37% of each run, Pallas kernels for 24% -> 22%
where the time goes in v10:
time: 80.8 us; the launch traced here: 79.9 us
  local copies, waits for them, and re-layouts  26.3 us (33%)
  starting transfers between devices  19.6 us (24%)
  Pallas kernels  17.3 us (21%)
  matrix products  9.18 us (11%)
  other arithmetic  4.43 us (5%)
  waiting for transfers between devices  2.82 us (3%)
    dynamic_update_slice x18, local copies, waits for them, and re-layouts, place(): lax.dynamic_update_slice(weight, part, (row, (owner_chip * 2 + k) * width))  19.8 us
    pallas_call x2, Pallas kernels, hyena_gate(): pl.pallas_call(_gate_kernel, grid=(share,), in_specs=[pl.BlockSpec((per_t...  17.3 us
    ppermute x3, starting transfers between devices, ring_step(): ahead = lax.ppermute(ahead, 'chip', forward)  9.91 us
    dot_general x1, matrix products, on_device(): branch = jnp.dot(gated, weight, preferred_element_type=jnp.float32)  9.18 us
    broadcast_in_dim x1, local copies, waits for them, and re-layouts, on_device(): weight = jnp.zeros((channels, chips * 2 * width), out_weight.dtype)  4.34 us
    ppermute x9, starting transfers between devices, place(): other = lax.ppermute(piece, 'core', swap)  4.16 us
    ppermute x2, starting transfers between devices, shifted(): return lax.ppermute(block, CTX, route)  3.42 us
    convert_element_type x1, other arithmetic, carried_of(): return (second * carrier).astype(jnp.bfloat16)  2.9 us
  transfers between devices with their start and end apart: 19, of which 2 were waited for; matrix products, arithmetic and copies ran while one was open for 37% of the time, Pallas kernels for 22%

profile of v10, /device:TPU:0, one launch (start us, length us, event | category | flops | bytes accessed | tf_op | source)
XLA Modules:
  0.0 79.9 jit_solution(9741967023194885472)
XLA Ops:
  0.0 3.0 %collective-permute-start.2 = (bf16[2048,128]{1,0:T(8,128)(2,1)}, bf16[2048,128]{1,0:T(8,128)(2,1)S(1)}, u32[]{:S(2)}, u32[]{:S(2)}) collective-permute-start(bf16[2048,128]{1,0:T(8,128)(2,1)} %param.11), channel_id=1, source_target_pairs={{0,4},{4,8},{8,12},{12,14},{14,10},{10,6},{6,2},{2,0},{1,5},{5,9},... | collective-permute-start | bytes 1572872 | tf_op jit(solution)/shard_map/ppermute | solution.py:158
  3.0 1.0 %fusion.4 = (f32[1,2048]{1,0:T(1,128)S(1)}, f32[1,2048]{1,0:T(1,128)S(1)}, f32[1,2048]{1,0:T(1,128)S(1)}, f32[1,2048]{1,0:T(1,128)S(1)}, f32[1,2048]{1,0:T(1,128)S(1)}, /*index=5*/f32[1,2048]{1,0:T(1,128)S(1)}) fusion(f32[3,6144]{1,0:T(4,128)} %param.8), kind=kLoop, calls=%fused_computation.26 | loop fusion | bytes 98304 | tf_op jit(solution)/shard_map/slice | solution.py:34
  4.0 2.9 %multiply_convert_fusion = bf16[128,2048]{1,0:T(8,128)(2,1)S(1)} fusion(bf16[512,6144]{1,0:T(8,128)(2,1)} %carrier_ref.2, f32[2048]{0:T(1024)S(1)} %bitcast.32, f32[2048]{0:T(1024)S(1)} %bitcast.28, f32[2048]{0:T(1024)S(1)} %bitcast.29, f32[2048]{0:T(1024)S(1)} %bitcast.30, f32[2048]{0:T(1024)S(1)} %bitcast.31, f32[2048]{0:T(1024)S(1)} %bitcast.27), kind=kLoop, calls=%fused_computation.4 | loop fusion | flops 4718592 | bytes 3719168 | tf_op jit(solution)/shard_map/convert_element_type | solution.py:122
  6.9 1.5 %collective-permute-start = (bf16[128,2048]{1,0:T(8,128)(2,1)S(1)}, bf16[128,2048]{1,0:T(8,128)(2,1)S(1)}, u32[]{:S(2)}, u32[]{:S(2)}) collective-permute-start(bf16[128,2048]{1,0:T(8,128)(2,1)S(1)} %multiply_convert_fusion), channel_id=1, source_target_pairs={{0,1},{1,2},{2,3},{3,4},{4,5},{5,6},{6,7},{7,8},{8,9},{9,10},{10,1... | collective-permute-start | bytes 1572872 | tf_op jit(solution)/shard_map/ppermute | solution.py:22
  8.4 2.6 %collective-permute-start.8 = (bf16[2048,128]{1,0:T(8,128)(2,1)}, bf16[2048,128]{1,0:T(8,128)(2,1)}, u32[]{:S(2)}, u32[]{:S(2)}) collective-permute-start(bf16[2048,128]{1,0:T(8,128)(2,1)} %param.11), channel_id=1, source_target_pairs={{0,1},{1,0},{2,3},{3,2},{4,5},{5,4},{6,7},{7,6},{8,9},{9,8},{10,11... | collective-permute-start | bytes 1572872 | tf_op jit(solution)/shard_map/ppermute | solution.py:144
  11.0 0.9 %slice.72 = bf16[2,6144]{1,0:T(2,128)(2,1)S(1)} slice(bf16[512,6144]{1,0:T(8,128)(2,1)} %carrier_ref.2), slice={[510:512], [0:6144]} | slice | bytes 49152 | tf_op jit(solution)/shard_map/slice | solution.py:175
  11.9 1.9 %collective-permute-start.1 = (bf16[2,6144]{1,0:T(2,128)(2,1)S(1)}, bf16[2,6144]{1,0:T(2,128)(2,1)S(1)}, u32[]{:S(2)}, u32[]{:S(2)}) collective-permute-start(bf16[2,6144]{1,0:T(2,128)(2,1)S(1)} %slice.72), channel_id=1, source_target_pairs={{0,1},{1,2},{2,3},{3,4},{4,5},{5,6},{6,7},{7,8},{8,9},{9,10},{10,1... | collective-permute-start | bytes 73736 | tf_op jit(solution)/shard_map/ppermute | solution.py:22
  13.8 4.3 %broadcast_in_dim.3 = bf16[2048,2048]{1,0:T(8,128)(2,1)} broadcast(bf16[]{:T(256)} %constant.75.clone.1), dimensions={} | broadcast | bytes 8388610 | tf_op jit(solution)/shard_map/broadcast_in_dim | solution.py:141
  18.2 0.9 %constant_dynamic-update-slice_fusion.15 = bf16[2048,2048]{1,0:T(8,128)(2,1)} fusion(bf16[2048,2048]{1,0:T(8,128)(2,1)} %broadcast_in_dim.3, bf16[2048,128]{1,0:T(8,128)(2,1)S(1)} %copy-done.3, s32[]{:T(128)S(6)} %select_n.114), kind=kLoop, calls=%fused_computation.22 | loop fusion | bytes 1048580 | tf_op jit(solution)/shard_map/dynamic_update_slice | solution.py:146
  19.2 4.8 %collective-permute-start.4 = (bf16[2048,128]{1,0:T(8,128)(2,1)S(1)}, bf16[2048,128]{1,0:T(8,128)(2,1)S(1)}, u32[]{:S(2)}, u32[]{:S(2)}) collective-permute-start(bf16[2048,128]{1,0:T(8,128)(2,1)S(1)} %collective-permute-done.2), channel_id=1, source_target_pairs={{0,4},{4,8},{8,12},{12,14},{14,10},{10,6},{6,2},{2,0},{1,5},{5,9},... | collective-permute-start | bytes 1572872 | tf_op jit(solution)/shard_map/ppermute | solution.py:158
  25.3 1.9 %constant_dynamic-update-slice_fusion.14 = bf16[2048,2048]{1,0:T(8,128)(2,1)} fusion(bf16[2048,2048]{1,0:T(8,128)(2,1)} %constant_dynamic-update-slice_fusion.15, bf16[2048,128]{1,0:T(8,128)(2,1)} %collective-permute-done.8, s32[]{:T(128)S(6)} %select_n.115), kind=kLoop, calls=%fused_computation.21 | loop fusion | bytes 1048580 | tf_op jit(solution)/shard_map/dynamic_update_slice | solution.py:146
  27.2 0.9 %constant_dynamic-update-slice_fusion.13 = bf16[2048,2048]{1,0:T(8,128)(2,1)} fusion(bf16[2048,2048]{1,0:T(8,128)(2,1)} %constant_dynamic-update-slice_fusion.14, bf16[2048,128]{1,0:T(8,128)(2,1)S(1)} %collective-permute-done.2, s32[]{:T(128)S(6)} %select_n.121), kind=kLoop, calls=%fused_computation.20 | loop fusion | bytes 1048580 | tf_op jit(solution)/shard_map/dynamic_update_slice | solution.py:146
  28.1 8.7 %shard_map.64 = bf16[512,1024]{1,0:T(8,128)(2,1)} custom-call(f32[128,384]{1,0:T(8,128)} %pad_convert_fusion.1.fw_ref, f32[1,2048]{1,0:T(1,128)} %bitcast.25, f32[3,3,2048]{2,1,0:T(4,128)} %bitcast.21, bf16[3,2,2048]{2,1,0:T(2,128)(2,1)} %bitcast.23, bf16[128,2048]{1,0:T(8,128)(2,1)} %copy-done, bf16[512,6144]{1,0:T(8,128)(2,1)} %carrier_ref.2, ...), custom_call_target="tpu_custom_call" | custom-call | tf_op jit(solution)/shard_map/pallas_call | solution.py:95
  36.8 2.1 %collective-permute-start.6 = (bf16[2048,128]{1,0:T(8,128)(2,1)S(1)}, bf16[2048,128]{1,0:T(8,128)(2,1)S(1)}, u32[]{:S(2)}, u32[]{:S(2)}) collective-permute-start(bf16[2048,128]{1,0:T(8,128)(2,1)S(1)} %collective-permute-done.4), channel_id=1, source_target_pairs={{0,4},{4,8},{8,12},{12,14},{14,10},{10,6},{6,2},{2,0},{1,5},{5,9},... | collective-permute-start | bytes 1572872 | tf_op jit(solution)/shard_map/ppermute | solution.py:158
  39.6 2.0 %constant_dynamic-update-slice_fusion.12 = bf16[2048,2048]{1,0:T(8,128)(2,1)} fusion(bf16[2048,2048]{1,0:T(8,128)(2,1)} %constant_dynamic-update-slice_fusion.13, bf16[2048,128]{1,0:T(8,128)(2,1)} %collective-permute-done.9, s32[]{:T(128)S(6)} %select_n.122), kind=kLoop, calls=%fused_computation.19 | loop fusion | bytes 1048580 | tf_op jit(solution)/shard_map/dynamic_update_slice | solution.py:146
  41.6 0.9 %constant_dynamic-update-slice_fusion.11 = bf16[2048,2048]{1,0:T(8,128)(2,1)} fusion(bf16[2048,2048]{1,0:T(8,128)(2,1)} %constant_dynamic-update-slice_fusion.12, bf16[2048,128]{1,0:T(8,128)(2,1)S(1)} %collective-permute-done.3, s32[]{:T(128)S(6)} %select_n.125), kind=kLoop, calls=%fused_computation.18 | loop fusion | bytes 1048580 | tf_op jit(solution)/shard_map/dynamic_update_slice | solution.py:146
  42.5 2.0 %constant_dynamic-update-slice_fusion.10 = bf16[2048,2048]{1,0:T(8,128)(2,1)} fusion(bf16[2048,2048]{1,0:T(8,128)(2,1)} %constant_dynamic-update-slice_fusion.11, bf16[2048,128]{1,0:T(8,128)(2,1)} %collective-permute-done.10, s32[]{:T(128)S(6)} %select_n.126), kind=kLoop, calls=%fused_computation.17 | loop fusion | bytes 1048580 | tf_op jit(solution)/shard_map/dynamic_update_slice | solution.py:146
  44.5 0.9 %constant_dynamic-update-slice_fusion.9 = bf16[2048,2048]{1,0:T(8,128)(2,1)} fusion(bf16[2048,2048]{1,0:T(8,128)(2,1)} %constant_dynamic-update-slice_fusion.10, bf16[2048,128]{1,0:T(8,128)(2,1)S(1)} %collective-permute-done.4, s32[]{:T(128)S(6)} %select_n.129), kind=kLoop, calls=%fused_computation.16 | loop fusion | bytes 1048580 | tf_op jit(solution)/shard_map/dynamic_update_slice | solution.py:146
  46.1 8.7 %shard_map.65 = bf16[512,1024]{1,0:T(8,128)(2,1)} custom-call(f32[128,384]{1,0:T(8,128)} %pad_convert_fusion.fw_ref, f32[1,2048]{1,0:T(1,128)} %bitcast.26, f32[3,3,2048]{2,1,0:T(4,128)} %bitcast.22, bf16[3,2,2048]{2,1,0:T(2,128)(2,1)} %bitcast.24, bf16[128,2048]{1,0:T(8,128)(2,1)} %copy-done, bf16[512,6144]{1,0:T(8,128)(2,1)} %carrier_ref.2, ...), custom_call_target="tpu_custom_call" | custom-call | tf_op jit(solution)/shard_map/pallas_call | solution.py:95
  54.8 2.0 %collective-permute-start.15 = (bf16[1024,128]{1,0:T(8,128)(2,1)S(1)}, bf16[1024,128]{1,0:T(8,128)(2,1)S(1)}, u32[]{:S(2)}, u32[]{:S(2)}) collective-permute-start(bf16[1024,128]{1,0:T(8,128)(2,1)S(1)} %slice.73), channel_id=1, source_target_pairs={{0,4},{4,8},{8,12},{12,14},{14,10},{10,6},{6,2},{2,0},{1,5},{5,9},... | collective-permute-start | bytes 786440 | tf_op jit(solution)/shard_map/ppermute | solution.py:152
  57.5 1.9 %constant_dynamic-update-slice_fusion.8 = bf16[2048,2048]{1,0:T(8,128)(2,1)} fusion(bf16[2048,2048]{1,0:T(8,128)(2,1)} %constant_dynamic-update-slice_fusion.9, bf16[2048,128]{1,0:T(8,128)(2,1)} %collective-permute-done.11, s32[]{:T(128)S(6)} %select_n.130), kind=kLoop, calls=%fused_computation.15 | loop fusion | bytes 1048580 | tf_op jit(solution)/shard_map/dynamic_update_slice | solution.py:146
  59.4 0.9 %constant_dynamic-update-slice_fusion.7 = bf16[2048,2048]{1,0:T(8,128)(2,1)} fusion(bf16[2048,2048]{1,0:T(8,128)(2,1)} %constant_dynamic-update-slice_fusion.8, bf16[2048,128]{1,0:T(8,128)(2,1)S(1)} %collective-permute-done.5, s32[]{:T(128)S(6)} %select_n.133), kind=kLoop, calls=%fused_computation.14 | loop fusion | bytes 1048580 | tf_op jit(solution)/shard_map/dynamic_update_slice | solution.py:146
  60.3 0.9 %constant_dynamic-update-slice_fusion.6 = bf16[2048,2048]{1,0:T(8,128)(2,1)} fusion(bf16[2048,2048]{1,0:T(8,128)(2,1)} %constant_dynamic-update-slice_fusion.7, bf16[2048,128]{1,0:T(8,128)(2,1)S(1)} %collective-permute-done.12, s32[]{:T(128)S(6)} %select_n.134), kind=kLoop, calls=%fused_computation.13 | loop fusion | bytes 1048580 | tf_op jit(solution)/shard_map/dynamic_update_slice | solution.py:146
  61.3 0.9 %constant_dynamic-update-slice_fusion.5 = bf16[2048,2048]{1,0:T(8,128)(2,1)} fusion(bf16[2048,2048]{1,0:T(8,128)(2,1)} %constant_dynamic-update-slice_fusion.6, bf16[2048,128]{1,0:T(8,128)(2,1)S(1)} %collective-permute-done.6, s32[]{:T(128)S(6)} %select_n.137), kind=kLoop, calls=%fused_computation.12 | loop fusion | bytes 1048580 | tf_op jit(solution)/shard_map/dynamic_update_slice | solution.py:146
  62.2 1.0 %collective-permute-done.15 = bf16[1024,128]{1,0:T(8,128)(2,1)S(1)} collective-permute-done((bf16[1024,128]{1,0:T(8,128)(2,1)S(1)}, bf16[1024,128]{1,0:T(8,128)(2,1)S(1)}, u32[]{:S(2)}, u32[]{:S(2)}) %collective-permute-start.15) | collective-permute-done | bytes 262176 | tf_op jit(solution)/shard_map/ppermute | solution.py:152
  63.2 1.8 %collective-permute-done.17 = bf16[1024,128]{1,0:T(8,128)(2,1)S(1)} collective-permute-done((bf16[1024,128]{1,0:T(8,128)(2,1)S(1)}, bf16[1024,128]{1,0:T(8,128)(2,1)S(1)}, u32[]{:S(2)}, u32[]{:S(2)}) %collective-permute-start.17) | collective-permute-done | bytes 262176 | tf_op jit(solution)/shard_map/ppermute | solution.py:153
  64.9 0.9 %constant_dynamic-update-slice_fusion.4 = bf16[2048,2048]{1,0:T(8,128)(2,1)} fusion(bf16[2048,2048]{1,0:T(8,128)(2,1)} %constant_dynamic-update-slice_fusion.5, bf16[2048,128]{1,0:T(8,128)(2,1)S(1)} %collective-permute-done.13, s32[]{:T(128)S(6)} %select_n.138), kind=kLoop, calls=%fused_computation.11 | loop fusion | bytes 1048580 | tf_op jit(solution)/shard_map/dynamic_update_slice | solution.py:146
  65.8 0.9 %constant_dynamic-update-slice_fusion.3 = bf16[2048,2048]{1,0:T(8,128)(2,1)} fusion(bf16[2048,2048]{1,0:T(8,128)(2,1)} %constant_dynamic-update-slice_fusion.4, bf16[2048,128]{1,0:T(8,128)(2,1)S(1)} %collective-permute-done.7, s32[]{:T(128)S(6)} %select_n.141), kind=kLoop, calls=%fused_computation.10 | loop fusion | bytes 1048580 | tf_op jit(solution)/shard_map/dynamic_update_slice | solution.py:146
  66.7 0.9 %constant_dynamic-update-slice_fusion.2 = bf16[2048,2048]{1,0:T(8,128)(2,1)} fusion(bf16[2048,2048]{1,0:T(8,128)(2,1)} %constant_dynamic-update-slice_fusion.3, bf16[2048,128]{1,0:T(8,128)(2,1)S(1)} %collective-permute-done.14, s32[]{:T(128)S(6)} %select_n.142), kind=kLoop, calls=%fused_computation.9 | loop fusion | bytes 1048580 | tf_op jit(solution)/shard_map/dynamic_update_slice | solution.py:146
  68.4 0.8 constant_dynamic-update-slice_fusion
  69.9 0.8 constant_dynamic-update-slice_fusion.16
  70.7 9.2 %add_convert_fusion = bf16[512,2048]{1,0:T(8,128)(2,1)} fusion(bf16[512,2048]{1,0:T(8,128)(2,1)S(1)} %copy-done.6, bf16[2048,2048]{1,0:T(8,128)(2,1)} %constant_dynamic-update-slice_fusion.16, bf16[512,1024]{1,0:T(8,128)(2,1)S(1)} %copy-done.2, bf16[512,1024]{1,0:T(8,128)(2,1)S(1)} %copy-done.1), kind=kOutput, calls=%fused_computation | convolution fusion | flops 4302307328 | bytes 14680064 | tf_op jit(solution)/shard_map/dot_general | solution.py:194
  (51 shorter events, 5.0 us)
Async XLA Ops:
  0.0 18.2 %copy-start.3 = (bf16[2048,128]{1,0:T(8,128)(2,1)S(1)}, bf16[2048,128]{1,0:T(8,128)(2,1)}, u32[]{:S(2)}) copy-start(bf16[2048,128]{1,0:T(8,128)(2,1)} %param.11) | copy-start | bytes 1572868
  0.0 19.0 %copy-start.4 = (bf16[128,128]{1,0:T(8,128)(2,1)S(1)}, bf16[128,128]{1,0:T(8,128)(2,1)}, u32[]{:S(2)}) copy-start(bf16[128,128]{1,0:T(8,128)(2,1)} %param.9) | copy-start | bytes 98308
  0.0 19.2 %collective-permute-start.2 = (bf16[2048,128]{1,0:T(8,128)(2,1)}, bf16[2048,128]{1,0:T(8,128)(2,1)S(1)}, u32[]{:S(2)}, u32[]{:S(2)}) collective-permute-start(bf16[2048,128]{1,0:T(8,128)(2,1)} %param.11), channel_id=1, source_target_pairs={{0,4},{4,8},{8,12},{12,14},{14,10},{10,6},{6,2},{2,0},{1,5},{5,9},... | collective-permute-start | bytes 1572872 | tf_op jit(solution)/shard_map/ppermute | solution.py:158
  3.0 16.1 %collective-permute-start.3 = (bf16[2048,128]{1,0:T(8,128)(2,1)}, bf16[2048,128]{1,0:T(8,128)(2,1)S(1)}, u32[]{:S(2)}, u32[]{:S(2)}) collective-permute-start(bf16[2048,128]{1,0:T(8,128)(2,1)} %param.11), channel_id=1, source_target_pairs={{4,0},{8,4},{12,8},{14,12},{10,14},{6,10},{2,6},{0,2},{5,1},{9,5},... | collective-permute-start | bytes 1572872 | tf_op jit(solution)/shard_map/ppermute | solution.py:159
  6.9 12.3 %collective-permute-start = (bf16[128,2048]{1,0:T(8,128)(2,1)S(1)}, bf16[128,2048]{1,0:T(8,128)(2,1)S(1)}, u32[]{:S(2)}, u32[]{:S(2)}) collective-permute-start(bf16[128,2048]{1,0:T(8,128)(2,1)S(1)} %multiply_convert_fusion), channel_id=1, source_target_pairs={{0,1},{1,2},{2,3},{3,4},{4,5},{5,6},{6,7},{7,8},{8,9},{9,10},{10,1... | collective-permute-start | bytes 1572872 | tf_op jit(solution)/shard_map/ppermute | solution.py:22
  8.4 16.9 %collective-permute-start.8 = (bf16[2048,128]{1,0:T(8,128)(2,1)}, bf16[2048,128]{1,0:T(8,128)(2,1)}, u32[]{:S(2)}, u32[]{:S(2)}) collective-permute-start(bf16[2048,128]{1,0:T(8,128)(2,1)} %param.11), channel_id=1, source_target_pairs={{0,1},{1,0},{2,3},{3,2},{4,5},{5,4},{6,7},{7,6},{8,9},{9,8},{10,11... | collective-permute-start | bytes 1572872 | tf_op jit(solution)/shard_map/ppermute | solution.py:144
  11.9 7.3 %collective-permute-start.1 = (bf16[2,6144]{1,0:T(2,128)(2,1)S(1)}, bf16[2,6144]{1,0:T(2,128)(2,1)S(1)}, u32[]{:S(2)}, u32[]{:S(2)}) collective-permute-start(bf16[2,6144]{1,0:T(2,128)(2,1)S(1)} %slice.72), channel_id=1, source_target_pairs={{0,1},{1,2},{2,3},{3,4},{4,5},{5,6},{6,7},{7,8},{8,9},{9,10},{10,1... | collective-permute-start | bytes 73736 | tf_op jit(solution)/shard_map/ppermute | solution.py:22
  19.1 9.0 %copy-start.5 = (bf16[2,6144]{1,0:T(2,128)(2,1)}, bf16[2,6144]{1,0:T(2,128)(2,1)S(1)}, u32[]{:S(2)}) copy-start(bf16[2,6144]{1,0:T(2,128)(2,1)S(1)} %collective-permute-done.1) | copy-start | bytes 73732
  19.2 9.0 %copy-start = (bf16[128,2048]{1,0:T(8,128)(2,1)}, bf16[128,2048]{1,0:T(8,128)(2,1)S(1)}, u32[]{:S(2)}) copy-start(bf16[128,2048]{1,0:T(8,128)(2,1)S(1)} %collective-permute-done.halo_ref) | copy-start | bytes 1572868
  19.2 17.6 %collective-permute-start.4 = (bf16[2048,128]{1,0:T(8,128)(2,1)S(1)}, bf16[2048,128]{1,0:T(8,128)(2,1)S(1)}, u32[]{:S(2)}, u32[]{:S(2)}) collective-permute-start(bf16[2048,128]{1,0:T(8,128)(2,1)S(1)} %collective-permute-done.2), channel_id=1, source_target_pairs={{0,4},{4,8},{8,12},{12,14},{14,10},{10,6},{6,2},{2,0},{1,5},{5,9},... | collective-permute-start | bytes 1572872 | tf_op jit(solution)/shard_map/ppermute | solution.py:158
  24.0 12.8 %collective-permute-start.5 = (bf16[2048,128]{1,0:T(8,128)(2,1)S(1)}, bf16[2048,128]{1,0:T(8,128)(2,1)S(1)}, u32[]{:S(2)}, u32[]{:S(2)}) collective-permute-start(bf16[2048,128]{1,0:T(8,128)(2,1)S(1)} %collective-permute-done.3), channel_id=1, source_target_pairs={{4,0},{8,4},{12,8},{14,12},{10,14},{6,10},{2,6},{0,2},{5,1},{9,5},... | collective-permute-start | bytes 1572872 | tf_op jit(solution)/shard_map/ppermute | solution.py:159
  24.0 15.1 %collective-permute-start.9 = (bf16[2048,128]{1,0:T(8,128)(2,1)S(1)}, bf16[2048,128]{1,0:T(8,128)(2,1)}, u32[]{:S(2)}, u32[]{:S(2)}) collective-permute-start(bf16[2048,128]{1,0:T(8,128)(2,1)S(1)} %collective-permute-done.2), channel_id=1, source_target_pairs={{0,1},{1,0},{2,3},{3,2},{4,5},{5,4},{6,7},{7,6},{8,9},{9,8},{10,11... | collective-permute-start | bytes 1572872 | tf_op jit(solution)/shard_map/ppermute | solution.py:144
  24.8 17.7 %collective-permute-start.10 = (bf16[2048,128]{1,0:T(8,128)(2,1)S(1)}, bf16[2048,128]{1,0:T(8,128)(2,1)}, u32[]{:S(2)}, u32[]{:S(2)}) collective-permute-start(bf16[2048,128]{1,0:T(8,128)(2,1)S(1)} %collective-permute-done.3), channel_id=1, source_target_pairs={{0,1},{1,0},{2,3},{3,2},{4,5},{5,4},{6,7},{7,6},{8,9},{9,8},{10,11... | collective-permute-start | bytes 1572872 | tf_op jit(solution)/shard_map/ppermute | solution.py:144
  36.8 18.0 %collective-permute-start.6 = (bf16[2048,128]{1,0:T(8,128)(2,1)S(1)}, bf16[2048,128]{1,0:T(8,128)(2,1)S(1)}, u32[]{:S(2)}, u32[]{:S(2)}) collective-permute-start(bf16[2048,128]{1,0:T(8,128)(2,1)S(1)} %collective-permute-done.4), channel_id=1, source_target_pairs={{0,4},{4,8},{8,12},{12,14},{14,10},{10,6},{6,2},{2,0},{1,5},{5,9},... | collective-permute-start | bytes 1572872 | tf_op jit(solution)/shard_map/ppermute | solution.py:158
  38.9 15.9 %collective-permute-start.7 = (bf16[2048,128]{1,0:T(8,128)(2,1)S(1)}, bf16[2048,128]{1,0:T(8,128)(2,1)S(1)}, u32[]{:S(2)}, u32[]{:S(2)}) collective-permute-start(bf16[2048,128]{1,0:T(8,128)(2,1)S(1)} %collective-permute-done.5), channel_id=1, source_target_pairs={{4,0},{8,4},{12,8},{14,12},{10,14},{6,10},{2,6},{0,2},{5,1},{9,5},... | collective-permute-start | bytes 1572872 | tf_op jit(solution)/shard_map/ppermute | solution.py:159
  39.0 18.0 %collective-permute-start.11 = (bf16[2048,128]{1,0:T(8,128)(2,1)S(1)}, bf16[2048,128]{1,0:T(8,128)(2,1)}, u32[]{:S(2)}, u32[]{:S(2)}) collective-permute-start(bf16[2048,128]{1,0:T(8,128)(2,1)S(1)} %collective-permute-done.4), channel_id=1, source_target_pairs={{0,1},{1,0},{2,3},{3,2},{4,5},{5,4},{6,7},{7,6},{8,9},{9,8},{10,11... | collective-permute-start | bytes 1572872 | tf_op jit(solution)/shard_map/ppermute | solution.py:144
  39.1 21.2 %collective-permute-start.12 = (bf16[2048,128]{1,0:T(8,128)(2,1)S(1)}, bf16[2048,128]{1,0:T(8,128)(2,1)S(1)}, u32[]{:S(2)}, u32[]{:S(2)}) collective-permute-start(bf16[2048,128]{1,0:T(8,128)(2,1)S(1)} %collective-permute-done.5), channel_id=1, source_target_pairs={{0,1},{1,0},{2,3},{3,2},{4,5},{5,4},{6,7},{7,6},{8,9},{9,8},{10,11... | collective-permute-start | bytes 1572872 | tf_op jit(solution)/shard_map/ppermute | solution.py:144
  54.8 15.9 %copy-start.1 = (bf16[512,1024]{1,0:T(8,128)(2,1)S(1)}, bf16[512,1024]{1,0:T(8,128)(2,1)}, u32[]{:S(2)}) copy-start(bf16[512,1024]{1,0:T(8,128)(2,1)} %shard_map.64) | copy-start | bytes 3145732
  54.8 15.9 %copy-start.2 = (bf16[512,1024]{1,0:T(8,128)(2,1)S(1)}, bf16[512,1024]{1,0:T(8,128)(2,1)}, u32[]{:S(2)}) copy-start(bf16[512,1024]{1,0:T(8,128)(2,1)} %shard_map.65) | copy-start | bytes 3145732
  54.8 15.9 %copy-start.6 = (bf16[512,2048]{1,0:T(8,128)(2,1)S(1)}, bf16[512,2048]{1,0:T(8,128)(2,1)}, u32[]{:S(2)}) copy-start(bf16[512,2048]{1,0:T(8,128)(2,1)} %param.6) | copy-start | bytes 6291460
  54.8 8.3 %collective-permute-start.15 = (bf16[1024,128]{1,0:T(8,128)(2,1)S(1)}, bf16[1024,128]{1,0:T(8,128)(2,1)S(1)}, u32[]{:S(2)}, u32[]{:S(2)}) collective-permute-start(bf16[1024,128]{1,0:T(8,128)(2,1)S(1)} %slice.73), channel_id=1, source_target_pairs={{0,4},{4,8},{8,12},{12,14},{14,10},{10,6},{6,2},{2,0},{1,5},{5,9},... | collective-permute-start | bytes 786440 | tf_op jit(solution)/shard_map/ppermute | solution.py:152
  56.9 8.0 %collective-permute-start.17 = (bf16[1024,128]{1,0:T(8,128)(2,1)S(1)}, bf16[1024,128]{1,0:T(8,128)(2,1)S(1)}, u32[]{:S(2)}, u32[]{:S(2)}) collective-permute-start(bf16[1024,128]{1,0:T(8,128)(2,1)S(1)} %slice.74), channel_id=1, source_target_pairs={{4,0},{8,4},{12,8},{14,12},{10,14},{6,10},{2,6},{0,2},{5,1},{9,5},... | collective-permute-start | bytes 786440 | tf_op jit(solution)/shard_map/ppermute | solution.py:153
  57.0 7.9 %collective-permute-start.13 = (bf16[2048,128]{1,0:T(8,128)(2,1)S(1)}, bf16[2048,128]{1,0:T(8,128)(2,1)S(1)}, u32[]{:S(2)}, u32[]{:S(2)}) collective-permute-start(bf16[2048,128]{1,0:T(8,128)(2,1)S(1)} %collective-permute-done.6), channel_id=1, source_target_pairs={{0,1},{1,0},{2,3},{3,2},{4,5},{5,4},{6,7},{7,6},{8,9},{9,8},{10,11... | collective-permute-start | bytes 1572872 | tf_op jit(solution)/shard_map/ppermute | solution.py:144
  57.0 9.7 %collective-permute-start.14 = (bf16[2048,128]{1,0:T(8,128)(2,1)S(1)}, bf16[2048,128]{1,0:T(8,128)(2,1)S(1)}, u32[]{:S(2)}, u32[]{:S(2)}) collective-permute-start(bf16[2048,128]{1,0:T(8,128)(2,1)S(1)} %collective-permute-done.7), channel_id=1, source_target_pairs={{0,1},{1,0},{2,3},{3,2},{4,5},{5,4},{6,7},{7,6},{8,9},{9,8},{10,11... | collective-permute-start | bytes 1572872 | tf_op jit(solution)/shard_map/ppermute | solution.py:144
  63.2 5.2 %collective-permute-start.16 = (bf16[1024,128]{1,0:T(8,128)(2,1)S(1)}, bf16[1024,128]{1,0:T(8,128)(2,1)S(1)}, u32[]{:S(2)}, u32[]{:S(2)}) collective-permute-start(bf16[1024,128]{1,0:T(8,128)(2,1)S(1)} %collective-permute-done.15), channel_id=1, source_target_pairs={{0,1},{1,0},{2,3},{3,2},{4,5},{5,4},{6,7},{7,6},{8,9},{9,8},{10,11... | collective-permute-start | bytes 786440 | tf_op jit(solution)/shard_map/ppermute | solution.py:144
  64.9 4.9 %collective-permute-start.18 = (bf16[1024,128]{1,0:T(8,128)(2,1)S(1)}, bf16[1024,128]{1,0:T(8,128)(2,1)S(1)}, u32[]{:S(2)}, u32[]{:S(2)}) collective-permute-start(bf16[1024,128]{1,0:T(8,128)(2,1)S(1)} %collective-permute-done.17), channel_id=1, source_target_pairs={{0,1},{1,0},{2,3},{3,2},{4,5},{5,4},{6,7},{7,6},{8,9},{9,8},{10,11... | collective-permute-start | bytes 786440 | tf_op jit(solution)/shard_map/ppermute | solution.py:144

commit v11 on v10

--- a/solution.py
+++ b/solution.py
@@ -138,19 +138,19 @@
     swap = [(0, 1), (1, 0)]
     steps = chips // 2
 
-    weight = jnp.zeros((channels, chips * 2 * width), out_weight.dtype)
+    weight = jnp.zeros((chips * 2 * width, channels), out_weight.dtype)
 
     def place(weight, piece, owner_chip, row=0):
         other = lax.ppermute(piece, "core", swap)
         for k, part in ((core, piece), (1 - core, other)):
-            weight = lax.dynamic_update_slice(weight, part, (row, (owner_chip * 2 + k) * width))
+            weight = lax.dynamic_update_slice(weight, part, ((owner_chip * 2 + k) * width, row))
         return weight
 
     def ring_step(step, weight, ahead, behind):
         if step == steps:
             half = channels // 2
-            ahead = lax.ppermute(ahead[:half], "chip", forward)
-            behind = lax.ppermute(behind[half:], "chip", backward)
+            ahead = lax.ppermute(ahead[:, :half], "chip", forward)
+            behind = lax.ppermute(behind[:, half:], "chip", backward)
             source = ring_chip((position - step) % chips, chips)
             weight = place(weight, ahead, source, 0)
             weight = place(weight, behind, source, half)
@@ -161,9 +161,9 @@
             weight = place(weight, behind, ring_chip((position + step) % chips, chips))
         return weight, ahead, behind
 
-    ahead = behind = out_weight
+    ahead = behind = out_weight.T
     if ring:
-        weight = place(weight, out_weight, chip)
+        weight = place(weight, ahead, chip)
         weight, ahead, behind = ring_step(1, weight, ahead, behind)
 
     tail = projected[row_count - BLOCK - 2 :]
@@ -189,9 +189,9 @@
         for step in range(4, steps + 1):
             weight, ahead, behind = ring_step(step, weight, ahead, behind)
     else:
-        weight = lax.all_gather(out_weight, CTX, axis=1, tiled=True)
+        weight = lax.all_gather(out_weight.T, CTX, axis=0, tiled=True)
     gated = jnp.concatenate([first, second], axis=1)
-    branch = jnp.dot(gated, weight, preferred_element_type=jnp.float32)
+    branch = lax.dot_general(gated, weight, (((1,), (1,)), ((), ())), preferred_element_type=jnp.float32)
     return (tokens.astype(jnp.float32) + branch).astype(jnp.bfloat16)
 
 

time: 80.8 us -> 80.8 us (level)
  no operation moved by 1% of the time
where the time goes in v11:
time: 80.8 us; the launch traced here: 79.9 us
  local copies, waits for them, and re-layouts  26.3 us (33%)
  starting transfers between devices  19.6 us (24%)
  Pallas kernels  17.3 us (21%)
  matrix products  9.18 us (11%)
  other arithmetic  4.43 us (5%)
  waiting for transfers between devices  2.82 us (3%)
    dynamic_update_slice x18, local copies, waits for them, and re-layouts, place(): lax.dynamic_update_slice(weight, part, ((owner_chip * 2 + k) * width, row))  19.8 us
    pallas_call x2, Pallas kernels, hyena_gate(): pl.pallas_call(_gate_kernel, grid=(share,), in_specs=[pl.BlockSpec((per_t...  17.3 us
    ppermute x3, starting transfers between devices, ring_step(): ahead = lax.ppermute(ahead, 'chip', forward)  9.91 us
    dot_general x1, matrix products, on_device(): lax.dot_general(gated, weight, (((1,), (1,)), ((), ())), preferred_elemen...  9.18 us
    broadcast_in_dim x1, local copies, waits for them, and re-layouts, on_device(): weight = jnp.zeros((chips * 2 * width, channels), out_weight.dtype)  4.34 us
    ppermute x9, starting transfers between devices, place(): other = lax.ppermute(piece, 'core', swap)  4.16 us
    ppermute x2, starting transfers between devices, shifted(): return lax.ppermute(block, CTX, route)  3.42 us
    convert_element_type x1, other arithmetic, carried_of(): return (second * carrier).astype(jnp.bfloat16)  2.9 us
  transfers between devices with their start and end apart: 19, of which 2 were waited for; matrix products, arithmetic and copies ran while one was open for 37% of the time, Pallas kernels for 22%

profile of v11, /device:TPU:0, one launch (start us, length us, event | category | flops | bytes accessed | tf_op | source)
XLA Modules:
  0.0 79.9 jit_solution(3415524400285902717)
XLA Ops:
  0.0 3.0 %collective-permute-start.2 = (bf16[128,2048]{0,1:T(8,128)(2,1)}, bf16[128,2048]{0,1:T(8,128)(2,1)S(1)}, u32[]{:S(2)}, u32[]{:S(2)}) collective-permute-start(bf16[128,2048]{0,1:T(8,128)(2,1)} %bitcast.25), channel_id=1, source_target_pairs={{0,4},{4,8},{8,12},{12,14},{14,10},{10,6},{6,2},{2,0},{1,5},{5,9},... | collective-permute-start | bytes 1572872 | tf_op jit(solution)/shard_map/ppermute | solution.py:158
  3.0 1.0 %fusion.4 = (f32[1,2048]{1,0:T(1,128)S(1)}, f32[1,2048]{1,0:T(1,128)S(1)}, f32[1,2048]{1,0:T(1,128)S(1)}, f32[1,2048]{1,0:T(1,128)S(1)}, f32[1,2048]{1,0:T(1,128)S(1)}, /*index=5*/f32[1,2048]{1,0:T(1,128)S(1)}) fusion(f32[3,6144]{1,0:T(4,128)} %param.8), kind=kLoop, calls=%fused_computation.26 | loop fusion | bytes 98304 | tf_op jit(solution)/shard_map/slice | solution.py:34
  4.0 2.9 %multiply_convert_fusion = bf16[128,2048]{1,0:T(8,128)(2,1)S(1)} fusion(bf16[512,6144]{1,0:T(8,128)(2,1)} %carrier_ref.2, f32[2048]{0:T(1024)S(1)} %bitcast.37, f32[2048]{0:T(1024)S(1)} %bitcast.33, f32[2048]{0:T(1024)S(1)} %bitcast.34, f32[2048]{0:T(1024)S(1)} %bitcast.35, f32[2048]{0:T(1024)S(1)} %bitcast.36, f32[2048]{0:T(1024)S(1)} %bitcast.32), kind=kLoop, calls=%fused_computation.4 | loop fusion | flops 4718592 | bytes 3719168 | tf_op jit(solution)/shard_map/convert_element_type | solution.py:122
  6.9 1.5 %collective-permute-start = (bf16[128,2048]{1,0:T(8,128)(2,1)S(1)}, bf16[128,2048]{1,0:T(8,128)(2,1)S(1)}, u32[]{:S(2)}, u32[]{:S(2)}) collective-permute-start(bf16[128,2048]{1,0:T(8,128)(2,1)S(1)} %multiply_convert_fusion), channel_id=1, source_target_pairs={{0,1},{1,2},{2,3},{3,4},{4,5},{5,6},{6,7},{7,8},{8,9},{9,10},{10,1... | collective-permute-start | bytes 1572872 | tf_op jit(solution)/shard_map/ppermute | solution.py:22
  8.4 2.6 %collective-permute-start.8 = (bf16[128,2048]{0,1:T(8,128)(2,1)}, bf16[128,2048]{0,1:T(8,128)(2,1)}, u32[]{:S(2)}, u32[]{:S(2)}) collective-permute-start(bf16[128,2048]{0,1:T(8,128)(2,1)} %bitcast.27), channel_id=1, source_target_pairs={{0,1},{1,0},{2,3},{3,2},{4,5},{5,4},{6,7},{7,6},{8,9},{9,8},{10,11... | collective-permute-start | bytes 1572872 | tf_op jit(solution)/shard_map/ppermute | solution.py:144
  11.0 0.9 %slice.72 = bf16[2,6144]{1,0:T(2,128)(2,1)S(1)} slice(bf16[512,6144]{1,0:T(8,128)(2,1)} %carrier_ref.2), slice={[510:512], [0:6144]} | slice | bytes 49152 | tf_op jit(solution)/shard_map/slice | solution.py:175
  11.9 1.9 %collective-permute-start.1 = (bf16[2,6144]{1,0:T(2,128)(2,1)S(1)}, bf16[2,6144]{1,0:T(2,128)(2,1)S(1)}, u32[]{:S(2)}, u32[]{:S(2)}) collective-permute-start(bf16[2,6144]{1,0:T(2,128)(2,1)S(1)} %slice.72), channel_id=1, source_target_pairs={{0,1},{1,2},{2,3},{3,4},{4,5},{5,6},{6,7},{7,8},{8,9},{9,10},{10,1... | collective-permute-start | bytes 73736 | tf_op jit(solution)/shard_map/ppermute | solution.py:22
  13.8 4.3 %broadcast_in_dim.3 = bf16[2048,2048]{0,1:T(8,128)(2,1)} broadcast(bf16[]{:T(256)} %constant.75.clone.1), dimensions={} | broadcast | bytes 8388610 | tf_op jit(solution)/shard_map/broadcast_in_dim | solution.py:141
  18.2 0.9 %constant_dynamic-update-slice_fusion.15 = bf16[2048,2048]{0,1:T(8,128)(2,1)} fusion(bf16[2048,2048]{0,1:T(8,128)(2,1)} %broadcast_in_dim.3, s32[]{:T(128)S(6)} %select_n.114, bf16[2048,128]{1,0:T(8,128)(2,1)S(1)} %copy-done.3), kind=kLoop, calls=%fused_computation.22 | loop fusion | bytes 1048580 | tf_op jit(solution)/shard_map/dynamic_update_slice | solution.py:146
  19.2 4.8 %collective-permute-start.4 = (bf16[128,2048]{0,1:T(8,128)(2,1)S(1)}, bf16[128,2048]{0,1:T(8,128)(2,1)S(1)}, u32[]{:S(2)}, u32[]{:S(2)}) collective-permute-start(bf16[128,2048]{0,1:T(8,128)(2,1)S(1)} %collective-permute-done.2), channel_id=1, source_target_pairs={{0,4},{4,8},{8,12},{12,14},{14,10},{10,6},{6,2},{2,0},{1,5},{5,9},... | collective-permute-start | bytes 1572872 | tf_op jit(solution)/shard_map/ppermute | solution.py:158
  25.3 1.9 %constant_dynamic-update-slice_fusion.14 = bf16[2048,2048]{0,1:T(8,128)(2,1)} fusion(bf16[2048,2048]{0,1:T(8,128)(2,1)} %constant_dynamic-update-slice_fusion.15, bf16[128,2048]{0,1:T(8,128)(2,1)} %collective-permute-done.8, s32[]{:T(128)S(6)} %select_n.115), kind=kLoop, calls=%fused_computation.21 | loop fusion | bytes 1048580 | tf_op jit(solution)/shard_map/dynamic_update_slice | solution.py:146
  27.2 0.9 %constant_dynamic-update-slice_fusion.13 = bf16[2048,2048]{0,1:T(8,128)(2,1)} fusion(bf16[2048,2048]{0,1:T(8,128)(2,1)} %constant_dynamic-update-slice_fusion.14, bf16[128,2048]{0,1:T(8,128)(2,1)S(1)} %collective-permute-done.2, s32[]{:T(128)S(6)} %select_n.121), kind=kLoop, calls=%fused_computation.20 | loop fusion | bytes 1048580 | tf_op jit(solution)/shard_map/dynamic_update_slice | solution.py:146
  28.1 8.7 %shard_map.64 = bf16[512,1024]{1,0:T(8,128)(2,1)} custom-call(f32[128,384]{1,0:T(8,128)} %pad_convert_fusion.1.fw_ref, f32[1,2048]{1,0:T(1,128)} %bitcast.30, f32[3,3,2048]{2,1,0:T(4,128)} %bitcast.23, bf16[3,2,2048]{2,1,0:T(2,128)(2,1)} %bitcast.28, bf16[128,2048]{1,0:T(8,128)(2,1)} %copy-done, bf16[512,6144]{1,0:T(8,128)(2,1)} %carrier_ref.2, ...), custom_call_target="tpu_custom_call" | custom-call | tf_op jit(solution)/shard_map/pallas_call | solution.py:95
  36.8 2.1 %collective-permute-start.6 = (bf16[128,2048]{0,1:T(8,128)(2,1)S(1)}, bf16[128,2048]{0,1:T(8,128)(2,1)S(1)}, u32[]{:S(2)}, u32[]{:S(2)}) collective-permute-start(bf16[128,2048]{0,1:T(8,128)(2,1)S(1)} %collective-permute-done.4), channel_id=1, source_target_pairs={{0,4},{4,8},{8,12},{12,14},{14,10},{10,6},{6,2},{2,0},{1,5},{5,9},... | collective-permute-start | bytes 1572872 | tf_op jit(solution)/shard_map/ppermute | solution.py:158
  39.6 2.0 %constant_dynamic-update-slice_fusion.12 = bf16[2048,2048]{0,1:T(8,128)(2,1)} fusion(bf16[2048,2048]{0,1:T(8,128)(2,1)} %constant_dynamic-update-slice_fusion.13, bf16[128,2048]{0,1:T(8,128)(2,1)} %collective-permute-done.9, s32[]{:T(128)S(6)} %select_n.122), kind=kLoop, calls=%fused_computation.19 | loop fusion | bytes 1048580 | tf_op jit(solution)/shard_map/dynamic_update_slice | solution.py:146
  41.6 0.9 %constant_dynamic-update-slice_fusion.11 = bf16[2048,2048]{0,1:T(8,128)(2,1)} fusion(bf16[2048,2048]{0,1:T(8,128)(2,1)} %constant_dynamic-update-slice_fusion.12, bf16[128,2048]{0,1:T(8,128)(2,1)S(1)} %collective-permute-done.3, s32[]{:T(128)S(6)} %select_n.125), kind=kLoop, calls=%fused_computation.18 | loop fusion | bytes 1048580 | tf_op jit(solution)/shard_map/dynamic_update_slice | solution.py:146
  42.5 2.0 %constant_dynamic-update-slice_fusion.10 = bf16[2048,2048]{0,1:T(8,128)(2,1)} fusion(bf16[2048,2048]{0,1:T(8,128)(2,1)} %constant_dynamic-update-slice_fusion.11, bf16[128,2048]{0,1:T(8,128)(2,1)} %collective-permute-done.10, s32[]{:T(128)S(6)} %select_n.126), kind=kLoop, calls=%fused_computation.17 | loop fusion | bytes 1048580 | tf_op jit(solution)/shard_map/dynamic_update_slice | solution.py:146
  44.5 0.9 %constant_dynamic-update-slice_fusion.9 = bf16[2048,2048]{0,1:T(8,128)(2,1)} fusion(bf16[2048,2048]{0,1:T(8,128)(2,1)} %constant_dynamic-update-slice_fusion.10, bf16[128,2048]{0,1:T(8,128)(2,1)S(1)} %collective-permute-done.4, s32[]{:T(128)S(6)} %select_n.129), kind=kLoop, calls=%fused_computation.16 | loop fusion | bytes 1048580 | tf_op jit(solution)/shard_map/dynamic_update_slice | solution.py:146
  46.1 8.7 %shard_map.65 = bf16[512,1024]{1,0:T(8,128)(2,1)} custom-call(f32[128,384]{1,0:T(8,128)} %pad_convert_fusion.fw_ref, f32[1,2048]{1,0:T(1,128)} %bitcast.31, f32[3,3,2048]{2,1,0:T(4,128)} %bitcast.24, bf16[3,2,2048]{2,1,0:T(2,128)(2,1)} %bitcast.29, bf16[128,2048]{1,0:T(8,128)(2,1)} %copy-done, bf16[512,6144]{1,0:T(8,128)(2,1)} %carrier_ref.2, ...), custom_call_target="tpu_custom_call" | custom-call | tf_op jit(solution)/shard_map/pallas_call | solution.py:95
  54.8 2.0 %collective-permute-start.15 = (bf16[128,1024]{0,1:T(8,128)(2,1)S(1)}, bf16[128,1024]{0,1:T(8,128)(2,1)S(1)}, u32[]{:S(2)}, u32[]{:S(2)}) collective-permute-start(bf16[128,1024]{0,1:T(8,128)(2,1)S(1)} %slice.73), channel_id=1, source_target_pairs={{0,4},{4,8},{8,12},{12,14},{14,10},{10,6},{6,2},{2,0},{1,5},{5,9},... | collective-permute-start | bytes 786440 | tf_op jit(solution)/shard_map/ppermute | solution.py:152
  57.5 1.9 %constant_dynamic-update-slice_fusion.8 = bf16[2048,2048]{0,1:T(8,128)(2,1)} fusion(bf16[2048,2048]{0,1:T(8,128)(2,1)} %constant_dynamic-update-slice_fusion.9, bf16[128,2048]{0,1:T(8,128)(2,1)} %collective-permute-done.11, s32[]{:T(128)S(6)} %select_n.130), kind=kLoop, calls=%fused_computation.15 | loop fusion | bytes 1048580 | tf_op jit(solution)/shard_map/dynamic_update_slice | solution.py:146
  59.4 0.9 %constant_dynamic-update-slice_fusion.7 = bf16[2048,2048]{0,1:T(8,128)(2,1)} fusion(bf16[2048,2048]{0,1:T(8,128)(2,1)} %constant_dynamic-update-slice_fusion.8, bf16[128,2048]{0,1:T(8,128)(2,1)S(1)} %collective-permute-done.5, s32[]{:T(128)S(6)} %select_n.133), kind=kLoop, calls=%fused_computation.14 | loop fusion | bytes 1048580 | tf_op jit(solution)/shard_map/dynamic_update_slice | solution.py:146
  60.3 0.9 %constant_dynamic-update-slice_fusion.6 = bf16[2048,2048]{0,1:T(8,128)(2,1)} fusion(bf16[2048,2048]{0,1:T(8,128)(2,1)} %constant_dynamic-update-slice_fusion.7, bf16[128,2048]{0,1:T(8,128)(2,1)S(1)} %collective-permute-done.12, s32[]{:T(128)S(6)} %select_n.134), kind=kLoop, calls=%fused_computation.13 | loop fusion | bytes 1048580 | tf_op jit(solution)/shard_map/dynamic_update_slice | solution.py:146
  61.3 0.9 %constant_dynamic-update-slice_fusion.5 = bf16[2048,2048]{0,1:T(8,128)(2,1)} fusion(bf16[2048,2048]{0,1:T(8,128)(2,1)} %constant_dynamic-update-slice_fusion.6, bf16[128,2048]{0,1:T(8,128)(2,1)S(1)} %collective-permute-done.6, s32[]{:T(128)S(6)} %select_n.137), kind=kLoop, calls=%fused_computation.12 | loop fusion | bytes 1048580 | tf_op jit(solution)/shard_map/dynamic_update_slice | solution.py:146
  62.2 1.0 %collective-permute-done.15 = bf16[128,1024]{0,1:T(8,128)(2,1)S(1)} collective-permute-done((bf16[128,1024]{0,1:T(8,128)(2,1)S(1)}, bf16[128,1024]{0,1:T(8,128)(2,1)S(1)}, u32[]{:S(2)}, u32[]{:S(2)}) %collective-permute-start.15) | collective-permute-done | bytes 262176 | tf_op jit(solution)/shard_map/ppermute | solution.py:152
  63.2 1.8 %collective-permute-done.17 = bf16[128,1024]{0,1:T(8,128)(2,1)S(1)} collective-permute-done((bf16[128,1024]{0,1:T(8,128)(2,1)S(1)}, bf16[128,1024]{0,1:T(8,128)(2,1)S(1)}, u32[]{:S(2)}, u32[]{:S(2)}) %collective-permute-start.17) | collective-permute-done | bytes 262176 | tf_op jit(solution)/shard_map/ppermute | solution.py:153
  64.9 0.9 %constant_dynamic-update-slice_fusion.4 = bf16[2048,2048]{0,1:T(8,128)(2,1)} fusion(bf16[2048,2048]{0,1:T(8,128)(2,1)} %constant_dynamic-update-slice_fusion.5, bf16[128,2048]{0,1:T(8,128)(2,1)S(1)} %collective-permute-done.13, s32[]{:T(128)S(6)} %select_n.138), kind=kLoop, calls=%fused_computation.11 | loop fusion | bytes 1048580 | tf_op jit(solution)/shard_map/dynamic_update_slice | solution.py:146
  65.8 0.9 %constant_dynamic-update-slice_fusion.3 = bf16[2048,2048]{0,1:T(8,128)(2,1)} fusion(bf16[2048,2048]{0,1:T(8,128)(2,1)} %constant_dynamic-update-slice_fusion.4, bf16[128,2048]{0,1:T(8,128)(2,1)S(1)} %collective-permute-done.7, s32[]{:T(128)S(6)} %select_n.141), kind=kLoop, calls=%fused_computation.10 | loop fusion | bytes 1048580 | tf_op jit(solution)/shard_map/dynamic_update_slice | solution.py:146
  66.7 0.9 %constant_dynamic-update-slice_fusion.2 = bf16[2048,2048]{0,1:T(8,128)(2,1)} fusion(bf16[2048,2048]{0,1:T(8,128)(2,1)} %constant_dynamic-update-slice_fusion.3, bf16[128,2048]{0,1:T(8,128)(2,1)S(1)} %collective-permute-done.14, s32[]{:T(128)S(6)} %select_n.142), kind=kLoop, calls=%fused_computation.9 | loop fusion | bytes 1048580 | tf_op jit(solution)/shard_map/dynamic_update_slice | solution.py:146
  68.4 0.8 constant_dynamic-update-slice_fusion
  69.9 0.8 constant_dynamic-update-slice_fusion.16
  70.7 9.2 %add_convert_fusion = bf16[512,2048]{1,0:T(8,128)(2,1)} fusion(bf16[512,2048]{1,0:T(8,128)(2,1)S(1)} %copy-done.6, bf16[2048,2048]{0,1:T(8,128)(2,1)} %constant_dynamic-update-slice_fusion.16, bf16[512,1024]{1,0:T(8,128)(2,1)S(1)} %copy-done.2, bf16[512,1024]{1,0:T(8,128)(2,1)S(1)} %copy-done.1), kind=kOutput, calls=%fused_computation | convolution fusion | flops 4302307328 | bytes 14680064 | tf_op jit(solution)/shard_map/dot_general | solution.py:194
  (51 shorter events, 5.0 us)
Async XLA Ops:
  0.0 18.2 %copy-start.3 = (bf16[2048,128]{1,0:T(8,128)(2,1)S(1)}, bf16[2048,128]{1,0:T(8,128)(2,1)}, u32[]{:S(2)}) copy-start(bf16[2048,128]{1,0:T(8,128)(2,1)} %param.11) | copy-start | bytes 1572868
  0.0 19.0 %copy-start.4 = (bf16[128,128]{1,0:T(8,128)(2,1)S(1)}, bf16[128,128]{1,0:T(8,128)(2,1)}, u32[]{:S(2)}) copy-start(bf16[128,128]{1,0:T(8,128)(2,1)} %param.9) | copy-start | bytes 98308
  0.0 19.2 %collective-permute-start.2 = (bf16[128,2048]{0,1:T(8,128)(2,1)}, bf16[128,2048]{0,1:T(8,128)(2,1)S(1)}, u32[]{:S(2)}, u32[]{:S(2)}) collective-permute-start(bf16[128,2048]{0,1:T(8,128)(2,1)} %bitcast.25), channel_id=1, source_target_pairs={{0,4},{4,8},{8,12},{12,14},{14,10},{10,6},{6,2},{2,0},{1,5},{5,9},... | collective-permute-start | bytes 1572872 | tf_op jit(solution)/shard_map/ppermute | solution.py:158
  3.0 16.1 %collective-permute-start.3 = (bf16[128,2048]{0,1:T(8,128)(2,1)}, bf16[128,2048]{0,1:T(8,128)(2,1)S(1)}, u32[]{:S(2)}, u32[]{:S(2)}) collective-permute-start(bf16[128,2048]{0,1:T(8,128)(2,1)} %bitcast.26), channel_id=1, source_target_pairs={{4,0},{8,4},{12,8},{14,12},{10,14},{6,10},{2,6},{0,2},{5,1},{9,5},... | collective-permute-start | bytes 1572872 | tf_op jit(solution)/shard_map/ppermute | solution.py:159
  6.9 12.3 %collective-permute-start = (bf16[128,2048]{1,0:T(8,128)(2,1)S(1)}, bf16[128,2048]{1,0:T(8,128)(2,1)S(1)}, u32[]{:S(2)}, u32[]{:S(2)}) collective-permute-start(bf16[128,2048]{1,0:T(8,128)(2,1)S(1)} %multiply_convert_fusion), channel_id=1, source_target_pairs={{0,1},{1,2},{2,3},{3,4},{4,5},{5,6},{6,7},{7,8},{8,9},{9,10},{10,1... | collective-permute-start | bytes 1572872 | tf_op jit(solution)/shard_map/ppermute | solution.py:22
  8.4 16.9 %collective-permute-start.8 = (bf16[128,2048]{0,1:T(8,128)(2,1)}, bf16[128,2048]{0,1:T(8,128)(2,1)}, u32[]{:S(2)}, u32[]{:S(2)}) collective-permute-start(bf16[128,2048]{0,1:T(8,128)(2,1)} %bitcast.27), channel_id=1, source_target_pairs={{0,1},{1,0},{2,3},{3,2},{4,5},{5,4},{6,7},{7,6},{8,9},{9,8},{10,11... | collective-permute-start | bytes 1572872 | tf_op jit(solution)/shard_map/ppermute | solution.py:144
  11.9 7.3 %collective-permute-start.1 = (bf16[2,6144]{1,0:T(2,128)(2,1)S(1)}, bf16[2,6144]{1,0:T(2,128)(2,1)S(1)}, u32[]{:S(2)}, u32[]{:S(2)}) collective-permute-start(bf16[2,6144]{1,0:T(2,128)(2,1)S(1)} %slice.72), channel_id=1, source_target_pairs={{0,1},{1,2},{2,3},{3,4},{4,5},{5,6},{6,7},{7,8},{8,9},{9,10},{10,1... | collective-permute-start | bytes 73736 | tf_op jit(solution)/shard_map/ppermute | solution.py:22
  19.1 9.0 %copy-start.5 = (bf16[2,6144]{1,0:T(2,128)(2,1)}, bf16[2,6144]{1,0:T(2,128)(2,1)S(1)}, u32[]{:S(2)}) copy-start(bf16[2,6144]{1,0:T(2,128)(2,1)S(1)} %collective-permute-done.1) | copy-start | bytes 73732
  19.2 9.0 %copy-start = (bf16[128,2048]{1,0:T(8,128)(2,1)}, bf16[128,2048]{1,0:T(8,128)(2,1)S(1)}, u32[]{:S(2)}) copy-start(bf16[128,2048]{1,0:T(8,128)(2,1)S(1)} %collective-permute-done.halo_ref) | copy-start | bytes 1572868
  19.2 17.6 %collective-permute-start.4 = (bf16[128,2048]{0,1:T(8,128)(2,1)S(1)}, bf16[128,2048]{0,1:T(8,128)(2,1)S(1)}, u32[]{:S(2)}, u32[]{:S(2)}) collective-permute-start(bf16[128,2048]{0,1:T(8,128)(2,1)S(1)} %collective-permute-done.2), channel_id=1, source_target_pairs={{0,4},{4,8},{8,12},{12,14},{14,10},{10,6},{6,2},{2,0},{1,5},{5,9},... | collective-permute-start | bytes 1572872 | tf_op jit(solution)/shard_map/ppermute | solution.py:158
  24.0 12.8 %collective-permute-start.5 = (bf16[128,2048]{0,1:T(8,128)(2,1)S(1)}, bf16[128,2048]{0,1:T(8,128)(2,1)S(1)}, u32[]{:S(2)}, u32[]{:S(2)}) collective-permute-start(bf16[128,2048]{0,1:T(8,128)(2,1)S(1)} %collective-permute-done.3), channel_id=1, source_target_pairs={{4,0},{8,4},{12,8},{14,12},{10,14},{6,10},{2,6},{0,2},{5,1},{9,5},... | collective-permute-start | bytes 1572872 | tf_op jit(solution)/shard_map/ppermute | solution.py:159
  24.0 15.1 %collective-permute-start.9 = (bf16[128,2048]{0,1:T(8,128)(2,1)S(1)}, bf16[128,2048]{0,1:T(8,128)(2,1)}, u32[]{:S(2)}, u32[]{:S(2)}) collective-permute-start(bf16[128,2048]{0,1:T(8,128)(2,1)S(1)} %collective-permute-done.2), channel_id=1, source_target_pairs={{0,1},{1,0},{2,3},{3,2},{4,5},{5,4},{6,7},{7,6},{8,9},{9,8},{10,11... | collective-permute-start | bytes 1572872 | tf_op jit(solution)/shard_map/ppermute | solution.py:144
  24.8 17.7 %collective-permute-start.10 = (bf16[128,2048]{0,1:T(8,128)(2,1)S(1)}, bf16[128,2048]{0,1:T(8,128)(2,1)}, u32[]{:S(2)}, u32[]{:S(2)}) collective-permute-start(bf16[128,2048]{0,1:T(8,128)(2,1)S(1)} %collective-permute-done.3), channel_id=1, source_target_pairs={{0,1},{1,0},{2,3},{3,2},{4,5},{5,4},{6,7},{7,6},{8,9},{9,8},{10,11... | collective-permute-start | bytes 1572872 | tf_op jit(solution)/shard_map/ppermute | solution.py:144
  36.8 18.0 %collective-permute-start.6 = (bf16[128,2048]{0,1:T(8,128)(2,1)S(1)}, bf16[128,2048]{0,1:T(8,128)(2,1)S(1)}, u32[]{:S(2)}, u32[]{:S(2)}) collective-permute-start(bf16[128,2048]{0,1:T(8,128)(2,1)S(1)} %collective-permute-done.4), channel_id=1, source_target_pairs={{0,4},{4,8},{8,12},{12,14},{14,10},{10,6},{6,2},{2,0},{1,5},{5,9},... | collective-permute-start | bytes 1572872 | tf_op jit(solution)/shard_map/ppermute | solution.py:158
  38.9 15.9 %collective-permute-start.7 = (bf16[128,2048]{0,1:T(8,128)(2,1)S(1)}, bf16[128,2048]{0,1:T(8,128)(2,1)S(1)}, u32[]{:S(2)}, u32[]{:S(2)}) collective-permute-start(bf16[128,2048]{0,1:T(8,128)(2,1)S(1)} %collective-permute-done.5), channel_id=1, source_target_pairs={{4,0},{8,4},{12,8},{14,12},{10,14},{6,10},{2,6},{0,2},{5,1},{9,5},... | collective-permute-start | bytes 1572872 | tf_op jit(solution)/shard_map/ppermute | solution.py:159
  39.0 18.0 %collective-permute-start.11 = (bf16[128,2048]{0,1:T(8,128)(2,1)S(1)}, bf16[128,2048]{0,1:T(8,128)(2,1)}, u32[]{:S(2)}, u32[]{:S(2)}) collective-permute-start(bf16[128,2048]{0,1:T(8,128)(2,1)S(1)} %collective-permute-done.4), channel_id=1, source_target_pairs={{0,1},{1,0},{2,3},{3,2},{4,5},{5,4},{6,7},{7,6},{8,9},{9,8},{10,11... | collective-permute-start | bytes 1572872 | tf_op jit(solution)/shard_map/ppermute | solution.py:144
  39.1 21.2 %collective-permute-start.12 = (bf16[128,2048]{0,1:T(8,128)(2,1)S(1)}, bf16[128,2048]{0,1:T(8,128)(2,1)S(1)}, u32[]{:S(2)}, u32[]{:S(2)}) collective-permute-start(bf16[128,2048]{0,1:T(8,128)(2,1)S(1)} %collective-permute-done.5), channel_id=1, source_target_pairs={{0,1},{1,0},{2,3},{3,2},{4,5},{5,4},{6,7},{7,6},{8,9},{9,8},{10,11... | collective-permute-start | bytes 1572872 | tf_op jit(solution)/shard_map/ppermute | solution.py:144
  54.8 15.9 %copy-start.1 = (bf16[512,1024]{1,0:T(8,128)(2,1)S(1)}, bf16[512,1024]{1,0:T(8,128)(2,1)}, u32[]{:S(2)}) copy-start(bf16[512,1024]{1,0:T(8,128)(2,1)} %shard_map.64) | copy-start | bytes 3145732
  54.8 15.9 %copy-start.2 = (bf16[512,1024]{1,0:T(8,128)(2,1)S(1)}, bf16[512,1024]{1,0:T(8,128)(2,1)}, u32[]{:S(2)}) copy-start(bf16[512,1024]{1,0:T(8,128)(2,1)} %shard_map.65) | copy-start | bytes 3145732
  54.8 15.9 %copy-start.6 = (bf16[512,2048]{1,0:T(8,128)(2,1)S(1)}, bf16[512,2048]{1,0:T(8,128)(2,1)}, u32[]{:S(2)}) copy-start(bf16[512,2048]{1,0:T(8,128)(2,1)} %param.6) | copy-start | bytes 6291460
  54.8 8.3 %collective-permute-start.15 = (bf16[128,1024]{0,1:T(8,128)(2,1)S(1)}, bf16[128,1024]{0,1:T(8,128)(2,1)S(1)}, u32[]{:S(2)}, u32[]{:S(2)}) collective-permute-start(bf16[128,1024]{0,1:T(8,128)(2,1)S(1)} %slice.73), channel_id=1, source_target_pairs={{0,4},{4,8},{8,12},{12,14},{14,10},{10,6},{6,2},{2,0},{1,5},{5,9},... | collective-permute-start | bytes 786440 | tf_op jit(solution)/shard_map/ppermute | solution.py:152
  56.9 8.0 %collective-permute-start.17 = (bf16[128,1024]{0,1:T(8,128)(2,1)S(1)}, bf16[128,1024]{0,1:T(8,128)(2,1)S(1)}, u32[]{:S(2)}, u32[]{:S(2)}) collective-permute-start(bf16[128,1024]{0,1:T(8,128)(2,1)S(1)} %slice.74), channel_id=1, source_target_pairs={{4,0},{8,4},{12,8},{14,12},{10,14},{6,10},{2,6},{0,2},{5,1},{9,5},... | collective-permute-start | bytes 786440 | tf_op jit(solution)/shard_map/ppermute | solution.py:153
  57.0 7.9 %collective-permute-start.13 = (bf16[128,2048]{0,1:T(8,128)(2,1)S(1)}, bf16[128,2048]{0,1:T(8,128)(2,1)S(1)}, u32[]{:S(2)}, u32[]{:S(2)}) collective-permute-start(bf16[128,2048]{0,1:T(8,128)(2,1)S(1)} %collective-permute-done.6), channel_id=1, source_target_pairs={{0,1},{1,0},{2,3},{3,2},{4,5},{5,4},{6,7},{7,6},{8,9},{9,8},{10,11... | collective-permute-start | bytes 1572872 | tf_op jit(solution)/shard_map/ppermute | solution.py:144
  57.0 9.7 %collective-permute-start.14 = (bf16[128,2048]{0,1:T(8,128)(2,1)S(1)}, bf16[128,2048]{0,1:T(8,128)(2,1)S(1)}, u32[]{:S(2)}, u32[]{:S(2)}) collective-permute-start(bf16[128,2048]{0,1:T(8,128)(2,1)S(1)} %collective-permute-done.7), channel_id=1, source_target_pairs={{0,1},{1,0},{2,3},{3,2},{4,5},{5,4},{6,7},{7,6},{8,9},{9,8},{10,11... | collective-permute-start | bytes 1572872 | tf_op jit(solution)/shard_map/ppermute | solution.py:144
  63.2 5.2 %collective-permute-start.16 = (bf16[128,1024]{0,1:T(8,128)(2,1)S(1)}, bf16[128,1024]{0,1:T(8,128)(2,1)S(1)}, u32[]{:S(2)}, u32[]{:S(2)}) collective-permute-start(bf16[128,1024]{0,1:T(8,128)(2,1)S(1)} %collective-permute-done.15), channel_id=1, source_target_pairs={{0,1},{1,0},{2,3},{3,2},{4,5},{5,4},{6,7},{7,6},{8,9},{9,8},{10,11... | collective-permute-start | bytes 786440 | tf_op jit(solution)/shard_map/ppermute | solution.py:144
  64.9 4.9 %collective-permute-start.18 = (bf16[128,1024]{0,1:T(8,128)(2,1)S(1)}, bf16[128,1024]{0,1:T(8,128)(2,1)S(1)}, u32[]{:S(2)}, u32[]{:S(2)}) collective-permute-start(bf16[128,1024]{0,1:T(8,128)(2,1)S(1)} %collective-permute-done.17), channel_id=1, source_target_pairs={{0,1},{1,0},{2,3},{3,2},{4,5},{5,4},{6,7},{7,6},{8,9},{9,8},{10,11... | collective-permute-start | bytes 786440 | tf_op jit(solution)/shard_map/ppermute | solution.py:144

commit v12 on v11

--- a/solution.py
+++ b/solution.py
@@ -142,9 +142,8 @@
 
     def place(weight, piece, owner_chip, row=0):
         other = lax.ppermute(piece, "core", swap)
-        for k, part in ((core, piece), (1 - core, other)):
-            weight = lax.dynamic_update_slice(weight, part, ((owner_chip * 2 + k) * width, row))
-        return weight
+        pair = jnp.where(core == 0, jnp.concatenate([piece, other]), jnp.concatenate([other, piece]))
+        return lax.dynamic_update_slice(weight, pair, (owner_chip * 2 * width, row))
 
     def ring_step(step, weight, ahead, behind):
         if step == steps:

time: 80.8 us -> 84.8 us (1.050)
  local copies, waits for them, and re-layouts: 26.3 us -> 6.47 us
  other arithmetic: 4.43 us -> 22.3 us
  waiting for transfers between devices: 2.82 us -> 6.08 us
  starting transfers between devices: 19.6 us -> 22.5 us
    dynamic_update_slice x18 -> x0, local copies, waits for them, and re-layouts: 19.8 us -> none  [place(): lax.dynamic_update_slice(weight, part, ((owner_chip * 2 + k) * width, row))]
    dynamic_update_slice x0 -> x9, other arithmetic: none -> 17.9 us  [place(): return lax.dynamic_update_slice(weight, pair, (owner_chip * 2 * width, row))]
    ppermute x3, starting transfers between devices: 9.91 us -> 12.9 us  [ring_step(): ahead = lax.ppermute(ahead, 'chip', forward)]
    ppermute x9, starting transfers between devices: 4.16 us -> 1.52 us  [place(): other = lax.ppermute(piece, 'core', swap)]
    ppermute x2, starting transfers between devices: 3.42 us -> 5.89 us  [shifted(): return lax.ppermute(block, CTX, route)]
    ppermute x3, waiting for transfers between devices: 0.01 us -> 1.52 us  [ring_step(): behind = lax.ppermute(behind, 'chip', backward)]
  transfers between devices with their start and end apart: 19 -> 19, of which waited for: 2 -> 7; matrix products, arithmetic and copies ran while one was open for 37% -> 33% of each run, Pallas kernels for 22% -> 21%
where the time goes in v12:
time: 84.8 us; the launch traced here: 84 us
  starting transfers between devices  22.5 us (27%)
  other arithmetic  22.3 us (26%)
  Pallas kernels  17.3 us (20%)
  matrix products  9.18 us (11%)
  local copies, waits for them, and re-layouts  6.47 us (8%)
  waiting for transfers between devices  6.08 us (7%)
    dynamic_update_slice x9, other arithmetic, place(): return lax.dynamic_update_slice(weight, pair, (owner_chip * 2 * width, row))  17.9 us
    pallas_call x2, Pallas kernels, hyena_gate(): pl.pallas_call(_gate_kernel, grid=(share,), in_specs=[pl.BlockSpec((per_t...  17.3 us
    ppermute x3, starting transfers between devices, ring_step(): ahead = lax.ppermute(ahead, 'chip', forward)  12.9 us
    dot_general x1, matrix products, on_device(): lax.dot_general(gated, weight, (((1,), (1,)), ((), ())), preferred_elemen...  9.18 us
    ppermute x2, starting transfers between devices, shifted(): return lax.ppermute(block, CTX, route)  5.89 us
    broadcast_in_dim x1, local copies, waits for them, and re-layouts, on_device(): weight = jnp.zeros((chips * 2 * width, channels), out_weight.dtype)  4.34 us
    convert_element_type x1, other arithmetic, carried_of(): return (second * carrier).astype(jnp.bfloat16)  2.9 us
    ppermute x1, starting transfers between devices, ring_step(): ahead = lax.ppermute(ahead[:, :half], 'chip', forward)  2.13 us
  transfers between devices with their start and end apart: 19, of which 7 were waited for; matrix products, arithmetic and copies ran while one was open for 33% of the time, Pallas kernels for 21%

profile of v12, /device:TPU:0, one launch (start us, length us, event | category | flops | bytes accessed | tf_op | source)
XLA Modules:
  0.0 84.0 jit_solution(16988288710998722009)
XLA Ops:
  0.0 3.0 %collective-permute-start.2 = (bf16[128,2048]{0,1:T(8,128)(2,1)}, bf16[128,2048]{0,1:T(8,128)(2,1)S(1)}, u32[]{:S(2)}, u32[]{:S(2)}) collective-permute-start(bf16[128,2048]{0,1:T(8,128)(2,1)} %bitcast.24), channel_id=1, source_target_pairs={{0,4},{4,8},{8,12},{12,14},{14,10},{10,6},{6,2},{2,0},{1,5},{5,9},... | collective-permute-start | bytes 1572872 | tf_op jit(solution)/shard_map/ppermute | solution.py:157
  3.0 1.0 %fusion.13 = (f32[1,2048]{1,0:T(1,128)S(1)}, f32[1,2048]{1,0:T(1,128)S(1)}, f32[1,2048]{1,0:T(1,128)S(1)}, f32[1,2048]{1,0:T(1,128)S(1)}, f32[1,2048]{1,0:T(1,128)S(1)}, /*index=5*/f32[1,2048]{1,0:T(1,128)S(1)}) fusion(f32[3,6144]{1,0:T(4,128)} %param.8), kind=kLoop, calls=%fused_computation.26 | loop fusion | bytes 98304 | tf_op jit(solution)/shard_map/slice | solution.py:34
  4.0 2.9 %multiply_convert_fusion = bf16[128,2048]{1,0:T(8,128)(2,1)S(1)} fusion(bf16[512,6144]{1,0:T(8,128)(2,1)} %carrier_ref.2, f32[2048]{0:T(1024)S(1)} %bitcast.37, f32[2048]{0:T(1024)S(1)} %bitcast.33, f32[2048]{0:T(1024)S(1)} %bitcast.34, f32[2048]{0:T(1024)S(1)} %bitcast.35, f32[2048]{0:T(1024)S(1)} %bitcast.36, f32[2048]{0:T(1024)S(1)} %bitcast.32), kind=kLoop, calls=%fused_computation.18 | loop fusion | flops 4718592 | bytes 3719168 | tf_op jit(solution)/shard_map/convert_element_type | solution.py:122
  6.9 1.5 %collective-permute-start = (bf16[128,2048]{1,0:T(8,128)(2,1)S(1)}, bf16[128,2048]{1,0:T(8,128)(2,1)S(1)}, u32[]{:S(2)}, u32[]{:S(2)}) collective-permute-start(bf16[128,2048]{1,0:T(8,128)(2,1)S(1)} %multiply_convert_fusion), channel_id=1, source_target_pairs={{0,1},{1,2},{2,3},{3,4},{4,5},{5,6},{6,7},{7,8},{8,9},{9,10},{10,1... | collective-permute-start | bytes 1572872 | tf_op jit(solution)/shard_map/ppermute | solution.py:22
  8.4 0.9 %slice.72 = bf16[2,6144]{1,0:T(2,128)(2,1)S(1)} slice(bf16[512,6144]{1,0:T(8,128)(2,1)} %carrier_ref.2), slice={[510:512], [0:6144]} | slice | bytes 49152 | tf_op jit(solution)/shard_map/slice | solution.py:174
  9.3 4.4 %collective-permute-start.1 = (bf16[2,6144]{1,0:T(2,128)(2,1)S(1)}, bf16[2,6144]{1,0:T(2,128)(2,1)S(1)}, u32[]{:S(2)}, u32[]{:S(2)}) collective-permute-start(bf16[2,6144]{1,0:T(2,128)(2,1)S(1)} %slice.72), channel_id=1, source_target_pairs={{0,1},{1,2},{2,3},{3,4},{4,5},{5,6},{6,7},{7,8},{8,9},{9,10},{10,1... | collective-permute-start | bytes 73736 | tf_op jit(solution)/shard_map/ppermute | solution.py:22
  13.7 0.8 collective-permute-done.1
  14.6 0.6 collective-permute-done.2
  15.2 1.5 %collective-permute-done.3 = bf16[128,2048]{0,1:T(8,128)(2,1)S(1)} collective-permute-done((bf16[128,2048]{0,1:T(8,128)(2,1)}, bf16[128,2048]{0,1:T(8,128)(2,1)S(1)}, u32[]{:S(2)}, u32[]{:S(2)}) %collective-permute-start.3) | collective-permute-done | bytes 524320 | tf_op jit(solution)/shard_map/ppermute | solution.py:158
  16.6 7.4 %collective-permute-start.4 = (bf16[128,2048]{0,1:T(8,128)(2,1)S(1)}, bf16[128,2048]{0,1:T(8,128)(2,1)S(1)}, u32[]{:S(2)}, u32[]{:S(2)}) collective-permute-start(bf16[128,2048]{0,1:T(8,128)(2,1)S(1)} %collective-permute-done.2), channel_id=1, source_target_pairs={{0,4},{4,8},{8,12},{12,14},{14,10},{10,6},{6,2},{2,0},{1,5},{5,9},... | collective-permute-start | bytes 1572872 | tf_op jit(solution)/shard_map/ppermute | solution.py:157
  24.0 0.5 collective-permute-start.9
  24.7 0.8 pad_convert_fusion.1.fw_ref
  25.5 8.7 %shard_map.64 = bf16[512,1024]{1,0:T(8,128)(2,1)} custom-call(f32[128,384]{1,0:T(8,128)} %pad_convert_fusion.1.fw_ref, f32[1,2048]{1,0:T(1,128)} %bitcast.30, f32[3,3,2048]{2,1,0:T(4,128)} %bitcast.22, bf16[3,2,2048]{2,1,0:T(2,128)(2,1)} %bitcast.28, bf16[128,2048]{1,0:T(8,128)(2,1)} %copy-done, bf16[512,6144]{1,0:T(8,128)(2,1)} %carrier_ref.2, ...), custom_call_target="tpu_custom_call" | custom-call | tf_op jit(solution)/shard_map/pallas_call | solution.py:95
  34.4 2.5 %collective-permute-start.6 = (bf16[128,2048]{0,1:T(8,128)(2,1)S(1)}, bf16[128,2048]{0,1:T(8,128)(2,1)S(1)}, u32[]{:S(2)}, u32[]{:S(2)}) collective-permute-start(bf16[128,2048]{0,1:T(8,128)(2,1)S(1)} %collective-permute-done.4), channel_id=1, source_target_pairs={{0,4},{4,8},{8,12},{12,14},{14,10},{10,6},{6,2},{2,0},{1,5},{5,9},... | collective-permute-start | bytes 1572872 | tf_op jit(solution)/shard_map/ppermute | solution.py:157
  37.0 4.3 %broadcast_in_dim.3 = bf16[2048,2048]{0,1:T(8,128)(2,1)} broadcast(bf16[]{:T(256)} %constant.83.clone.1), dimensions={} | broadcast | bytes 8388610 | tf_op jit(solution)/shard_map/broadcast_in_dim | solution.py:141
  41.3 2.6 %fusion.3 = bf16[2048,2048]{0,1:T(8,128)(2,1)} fusion(bf16[2048,2048]{0,1:T(8,128)(2,1)} %broadcast_in_dim.3, s32[]{:T(128)S(6)} %select_n.135, bf16[128,2048]{0,1:T(8,128)(2,1)} %collective-permute-done.8, bf16[128,2048]{0,1:T(8,128)(2,1)S(1)} %bitcast.27, pred[]{:T(512)S(6)} %eq.23), kind=kLoop, calls=%fused_computation.5 | loop fusion | flops 4718592 | bytes 2097157 | tf_op jit(solution)/shard_map/dynamic_update_slice | solution.py:146
  44.1 0.5 collective-permute-start.12
  44.6 2.5 %fusion.4 = bf16[2048,2048]{0,1:T(8,128)(2,1)} fusion(bf16[2048,2048]{0,1:T(8,128)(2,1)} %fusion.3, s32[]{:T(128)S(6)} %select_n.142, bf16[128,2048]{0,1:T(8,128)(2,1)} %collective-permute-done.9, bf16[128,2048]{0,1:T(8,128)(2,1)S(1)} %collective-permute-done.2, pred[]{:T(512)S(6)} %eq.23), kind=kLoop, calls=%fused_computation.7 | loop fusion | flops 4718592 | bytes 2097157 | tf_op jit(solution)/shard_map/dynamic_update_slice | solution.py:146
  47.1 2.6 %fusion.5 = bf16[2048,2048]{0,1:T(8,128)(2,1)} fusion(bf16[2048,2048]{0,1:T(8,128)(2,1)} %fusion.4, s32[]{:T(128)S(6)} %select_n.146, bf16[128,2048]{0,1:T(8,128)(2,1)} %collective-permute-done.10, bf16[128,2048]{0,1:T(8,128)(2,1)S(1)} %collective-permute-done.3, pred[]{:T(512)S(6)} %eq.23), kind=kLoop, calls=%fused_computation.9 | loop fusion | flops 4718592 | bytes 2097157 | tf_op jit(solution)/shard_map/dynamic_update_slice | solution.py:146
  49.8 0.8 pad_convert_fusion.fw_ref
  50.5 8.7 %shard_map.65 = bf16[512,1024]{1,0:T(8,128)(2,1)} custom-call(f32[128,384]{1,0:T(8,128)} %pad_convert_fusion.fw_ref, f32[1,2048]{1,0:T(1,128)} %bitcast.31, f32[3,3,2048]{2,1,0:T(4,128)} %bitcast.23, bf16[3,2,2048]{2,1,0:T(2,128)(2,1)} %bitcast.29, bf16[128,2048]{1,0:T(8,128)(2,1)} %copy-done, bf16[512,6144]{1,0:T(8,128)(2,1)} %carrier_ref.2, ...), custom_call_target="tpu_custom_call" | custom-call | tf_op jit(solution)/shard_map/pallas_call | solution.py:95
  59.2 2.1 %collective-permute-start.15 = (bf16[128,1024]{0,1:T(8,128)(2,1)S(1)}, bf16[128,1024]{0,1:T(8,128)(2,1)S(1)}, u32[]{:S(2)}, u32[]{:S(2)}) collective-permute-start(bf16[128,1024]{0,1:T(8,128)(2,1)S(1)} %slice.73), channel_id=1, source_target_pairs={{0,4},{4,8},{8,12},{12,14},{14,10},{10,6},{6,2},{2,0},{1,5},{5,9},... | collective-permute-start | bytes 786440 | tf_op jit(solution)/shard_map/ppermute | solution.py:151
  61.5 0.2 collective-permute-start.14
  61.7 2.6 %fusion.6 = bf16[2048,2048]{0,1:T(8,128)(2,1)} fusion(bf16[2048,2048]{0,1:T(8,128)(2,1)} %fusion.5, s32[]{:T(128)S(6)} %select_n.150, bf16[128,2048]{0,1:T(8,128)(2,1)} %collective-permute-done.11, bf16[128,2048]{0,1:T(8,128)(2,1)S(1)} %collective-permute-done.4, pred[]{:T(512)S(6)} %eq.23), kind=kLoop, calls=%fused_computation.11 | loop fusion | flops 4718592 | bytes 2097157 | tf_op jit(solution)/shard_map/dynamic_update_slice | solution.py:146
  64.3 2.6 %fusion.7 = bf16[2048,2048]{0,1:T(8,128)(2,1)} fusion(bf16[2048,2048]{0,1:T(8,128)(2,1)} %fusion.6, s32[]{:T(128)S(6)} %select_n.154, bf16[128,2048]{0,1:T(8,128)(2,1)} %collective-permute-done.12, bf16[128,2048]{0,1:T(8,128)(2,1)S(1)} %collective-permute-done.5, pred[]{:T(512)S(6)} %eq.23), kind=kLoop, calls=%fused_computation.13 | loop fusion | flops 4718592 | bytes 2097157 | tf_op jit(solution)/shard_map/dynamic_update_slice | solution.py:146
  66.9 1.0 %collective-permute-done.15 = bf16[128,1024]{0,1:T(8,128)(2,1)S(1)} collective-permute-done((bf16[128,1024]{0,1:T(8,128)(2,1)S(1)}, bf16[128,1024]{0,1:T(8,128)(2,1)S(1)}, u32[]{:S(2)}, u32[]{:S(2)}) %collective-permute-start.15) | collective-permute-done | bytes 262176 | tf_op jit(solution)/shard_map/ppermute | solution.py:151
  67.9 1.9 %collective-permute-done.17 = bf16[128,1024]{0,1:T(8,128)(2,1)S(1)} collective-permute-done((bf16[128,1024]{0,1:T(8,128)(2,1)S(1)}, bf16[128,1024]{0,1:T(8,128)(2,1)S(1)}, u32[]{:S(2)}, u32[]{:S(2)}) %collective-permute-start.17) | collective-permute-done | bytes 262176 | tf_op jit(solution)/shard_map/ppermute | solution.py:152
  69.8 1.4 %fusion.8 = bf16[2048,2048]{0,1:T(8,128)(2,1)} fusion(bf16[2048,2048]{0,1:T(8,128)(2,1)} %fusion.7, s32[]{:T(128)S(6)} %select_n.158, bf16[128,2048]{0,1:T(8,128)(2,1)S(1)} %collective-permute-done.13, bf16[128,2048]{0,1:T(8,128)(2,1)S(1)} %collective-permute-done.6, pred[]{:T(512)S(6)} %eq.23), kind=kLoop, calls=%fused_computation.15 | loop fusion | flops 4718592 | bytes 2097157 | tf_op jit(solution)/shard_map/dynamic_update_slice | solution.py:146
  71.3 1.5 %fusion.9 = bf16[2048,2048]{0,1:T(8,128)(2,1)} fusion(bf16[2048,2048]{0,1:T(8,128)(2,1)} %fusion.8, s32[]{:T(128)S(6)} %select_n.162, bf16[128,2048]{0,1:T(8,128)(2,1)S(1)} %collective-permute-done.14, bf16[128,2048]{0,1:T(8,128)(2,1)S(1)} %collective-permute-done.7, pred[]{:T(512)S(6)} %eq.23), kind=kLoop, calls=%fused_computation.17 | loop fusion | flops 4718592 | bytes 2097157 | tf_op jit(solution)/shard_map/dynamic_update_slice | solution.py:146
  72.7 1.0 %fusion.10 = bf16[2048,2048]{0,1:T(8,128)(2,1)} fusion(bf16[2048,2048]{0,1:T(8,128)(2,1)} %fusion.9, s32[]{:T(128)S(6)} %select_n.167, bf16[128,1024]{0,1:T(8,128)(2,1)S(1)} %collective-permute-done.16, bf16[128,1024]{0,1:T(8,128)(2,1)S(1)} %collective-permute-done.15, pred[]{:T(512)S(6)} %eq.23), kind=kLoop, calls=%fused_computation.20 | loop fusion | flops 2359296 | bytes 1048581 | tf_op jit(solution)/shard_map/dynamic_update_slice | solution.py:146
  73.8 1.0 %fusion.11 = bf16[2048,2048]{0,1:T(8,128)(2,1)} fusion(bf16[2048,2048]{0,1:T(8,128)(2,1)} %fusion.10, s32[]{:T(128)S(6)} %select_n.167, bf16[128,1024]{0,1:T(8,128)(2,1)S(1)} %collective-permute-done.18, bf16[128,1024]{0,1:T(8,128)(2,1)S(1)} %collective-permute-done.17, pred[]{:T(512)S(6)} %eq.23), kind=kLoop, calls=%fused_computation.22 | loop fusion | flops 2359296 | bytes 1048581 | tf_op jit(solution)/shard_map/dynamic_update_slice | solution.py:146
  74.8 9.2 %add_convert_fusion = bf16[512,2048]{1,0:T(8,128)(2,1)} fusion(bf16[512,2048]{1,0:T(8,128)(2,1)S(1)} %copy-done.6, bf16[2048,2048]{0,1:T(8,128)(2,1)} %fusion.11, bf16[512,1024]{1,0:T(8,128)(2,1)S(1)} %copy-done.2, bf16[512,1024]{1,0:T(8,128)(2,1)S(1)} %copy-done.1), kind=kOutput, calls=%fused_computation | convolution fusion | flops 4302307328 | bytes 14680064 | tf_op jit(solution)/shard_map/dot_general | solution.py:193
  (42 shorter events, 0.9 us)
Async XLA Ops:
  0.0 24.0 %copy-start.3 = (bf16[2048,128]{1,0:T(8,128)(2,1)S(1)}, bf16[2048,128]{1,0:T(8,128)(2,1)}, u32[]{:S(2)}) copy-start(bf16[2048,128]{1,0:T(8,128)(2,1)} %param.11) | copy-start | bytes 1572868
  0.0 24.5 %copy-start.4 = (bf16[128,128]{1,0:T(8,128)(2,1)S(1)}, bf16[128,128]{1,0:T(8,128)(2,1)}, u32[]{:S(2)}) copy-start(bf16[128,128]{1,0:T(8,128)(2,1)} %param.9) | copy-start | bytes 98308
  0.0 15.2 %collective-permute-start.2 = (bf16[128,2048]{0,1:T(8,128)(2,1)}, bf16[128,2048]{0,1:T(8,128)(2,1)S(1)}, u32[]{:S(2)}, u32[]{:S(2)}) collective-permute-start(bf16[128,2048]{0,1:T(8,128)(2,1)} %bitcast.24), channel_id=1, source_target_pairs={{0,4},{4,8},{8,12},{12,14},{14,10},{10,6},{6,2},{2,0},{1,5},{5,9},... | collective-permute-start | bytes 1572872 | tf_op jit(solution)/shard_map/ppermute | solution.py:157
  3.0 13.6 %collective-permute-start.3 = (bf16[128,2048]{0,1:T(8,128)(2,1)}, bf16[128,2048]{0,1:T(8,128)(2,1)S(1)}, u32[]{:S(2)}, u32[]{:S(2)}) collective-permute-start(bf16[128,2048]{0,1:T(8,128)(2,1)} %bitcast.25), channel_id=1, source_target_pairs={{4,0},{8,4},{12,8},{14,12},{10,14},{6,10},{2,6},{0,2},{5,1},{9,5},... | collective-permute-start | bytes 1572872 | tf_op jit(solution)/shard_map/ppermute | solution.py:158
  6.9 9.7 %collective-permute-start = (bf16[128,2048]{1,0:T(8,128)(2,1)S(1)}, bf16[128,2048]{1,0:T(8,128)(2,1)S(1)}, u32[]{:S(2)}, u32[]{:S(2)}) collective-permute-start(bf16[128,2048]{1,0:T(8,128)(2,1)S(1)} %multiply_convert_fusion), channel_id=1, source_target_pairs={{0,1},{1,2},{2,3},{3,4},{4,5},{5,6},{6,7},{7,8},{8,9},{9,10},{10,1... | collective-permute-start | bytes 1572872 | tf_op jit(solution)/shard_map/ppermute | solution.py:22
  9.3 5.2 %collective-permute-start.1 = (bf16[2,6144]{1,0:T(2,128)(2,1)S(1)}, bf16[2,6144]{1,0:T(2,128)(2,1)S(1)}, u32[]{:S(2)}, u32[]{:S(2)}) collective-permute-start(bf16[2,6144]{1,0:T(2,128)(2,1)S(1)} %slice.72), channel_id=1, source_target_pairs={{0,1},{1,2},{2,3},{3,4},{4,5},{5,6},{6,7},{7,8},{8,9},{9,10},{10,1... | collective-permute-start | bytes 73736 | tf_op jit(solution)/shard_map/ppermute | solution.py:22
  14.6 10.9 %copy-start.5 = (bf16[2,6144]{1,0:T(2,128)(2,1)}, bf16[2,6144]{1,0:T(2,128)(2,1)S(1)}, u32[]{:S(2)}) copy-start(bf16[2,6144]{1,0:T(2,128)(2,1)S(1)} %collective-permute-done.1) | copy-start | bytes 73732
  16.6 8.9 %copy-start = (bf16[128,2048]{1,0:T(8,128)(2,1)}, bf16[128,2048]{1,0:T(8,128)(2,1)S(1)}, u32[]{:S(2)}) copy-start(bf16[128,2048]{1,0:T(8,128)(2,1)S(1)} %collective-permute-done.halo_ref) | copy-start | bytes 1572868
  16.6 17.7 %collective-permute-start.4 = (bf16[128,2048]{0,1:T(8,128)(2,1)S(1)}, bf16[128,2048]{0,1:T(8,128)(2,1)S(1)}, u32[]{:S(2)}, u32[]{:S(2)}) collective-permute-start(bf16[128,2048]{0,1:T(8,128)(2,1)S(1)} %collective-permute-done.2), channel_id=1, source_target_pairs={{0,4},{4,8},{8,12},{12,14},{14,10},{10,6},{6,2},{2,0},{1,5},{5,9},... | collective-permute-start | bytes 1572872 | tf_op jit(solution)/shard_map/ppermute | solution.py:157
  24.0 10.4 %collective-permute-start.5 = (bf16[128,2048]{0,1:T(8,128)(2,1)S(1)}, bf16[128,2048]{0,1:T(8,128)(2,1)S(1)}, u32[]{:S(2)}, u32[]{:S(2)}) collective-permute-start(bf16[128,2048]{0,1:T(8,128)(2,1)S(1)} %collective-permute-done.3), channel_id=1, source_target_pairs={{4,0},{8,4},{12,8},{14,12},{10,14},{6,10},{2,6},{0,2},{5,1},{9,5},... | collective-permute-start | bytes 1572872 | tf_op jit(solution)/shard_map/ppermute | solution.py:158
  24.0 13.0 %collective-permute-start.8 = (bf16[128,2048]{0,1:T(8,128)(2,1)S(1)}, bf16[128,2048]{0,1:T(8,128)(2,1)}, u32[]{:S(2)}, u32[]{:S(2)}) collective-permute-start(bf16[128,2048]{0,1:T(8,128)(2,1)S(1)} %bitcast.26), channel_id=1, source_target_pairs={{0,1},{1,0},{2,3},{3,2},{4,5},{5,4},{6,7},{7,6},{8,9},{9,8},{10,11... | collective-permute-start | bytes 1572872 | tf_op jit(solution)/shard_map/ppermute | solution.py:144
  24.0 20.1 %collective-permute-start.9 = (bf16[128,2048]{0,1:T(8,128)(2,1)S(1)}, bf16[128,2048]{0,1:T(8,128)(2,1)}, u32[]{:S(2)}, u32[]{:S(2)}) collective-permute-start(bf16[128,2048]{0,1:T(8,128)(2,1)S(1)} %collective-permute-done.2), channel_id=1, source_target_pairs={{0,1},{1,0},{2,3},{3,2},{4,5},{5,4},{6,7},{7,6},{8,9},{9,8},{10,11... | collective-permute-start | bytes 1572872 | tf_op jit(solution)/shard_map/ppermute | solution.py:144
  24.6 22.5 %collective-permute-start.10 = (bf16[128,2048]{0,1:T(8,128)(2,1)S(1)}, bf16[128,2048]{0,1:T(8,128)(2,1)}, u32[]{:S(2)}, u32[]{:S(2)}) collective-permute-start(bf16[128,2048]{0,1:T(8,128)(2,1)S(1)} %collective-permute-done.3), channel_id=1, source_target_pairs={{0,1},{1,0},{2,3},{3,2},{4,5},{5,4},{6,7},{7,6},{8,9},{9,8},{10,11... | collective-permute-start | bytes 1572872 | tf_op jit(solution)/shard_map/ppermute | solution.py:144
  34.4 15.3 %collective-permute-start.6 = (bf16[128,2048]{0,1:T(8,128)(2,1)S(1)}, bf16[128,2048]{0,1:T(8,128)(2,1)S(1)}, u32[]{:S(2)}, u32[]{:S(2)}) collective-permute-start(bf16[128,2048]{0,1:T(8,128)(2,1)S(1)} %collective-permute-done.4), channel_id=1, source_target_pairs={{0,4},{4,8},{8,12},{12,14},{14,10},{10,6},{6,2},{2,0},{1,5},{5,9},... | collective-permute-start | bytes 1572872 | tf_op jit(solution)/shard_map/ppermute | solution.py:157
  43.9 15.3 %collective-permute-start.7 = (bf16[128,2048]{0,1:T(8,128)(2,1)S(1)}, bf16[128,2048]{0,1:T(8,128)(2,1)S(1)}, u32[]{:S(2)}, u32[]{:S(2)}) collective-permute-start(bf16[128,2048]{0,1:T(8,128)(2,1)S(1)} %collective-permute-done.5), channel_id=1, source_target_pairs={{4,0},{8,4},{12,8},{14,12},{10,14},{6,10},{2,6},{0,2},{5,1},{9,5},... | collective-permute-start | bytes 1572872 | tf_op jit(solution)/shard_map/ppermute | solution.py:158
  44.0 17.4 %collective-permute-start.11 = (bf16[128,2048]{0,1:T(8,128)(2,1)S(1)}, bf16[128,2048]{0,1:T(8,128)(2,1)}, u32[]{:S(2)}, u32[]{:S(2)}) collective-permute-start(bf16[128,2048]{0,1:T(8,128)(2,1)S(1)} %collective-permute-done.4), channel_id=1, source_target_pairs={{0,1},{1,0},{2,3},{3,2},{4,5},{5,4},{6,7},{7,6},{8,9},{9,8},{10,11... | collective-permute-start | bytes 1572872 | tf_op jit(solution)/shard_map/ppermute | solution.py:144
  44.1 20.2 %collective-permute-start.12 = (bf16[128,2048]{0,1:T(8,128)(2,1)S(1)}, bf16[128,2048]{0,1:T(8,128)(2,1)}, u32[]{:S(2)}, u32[]{:S(2)}) collective-permute-start(bf16[128,2048]{0,1:T(8,128)(2,1)S(1)} %collective-permute-done.5), channel_id=1, source_target_pairs={{0,1},{1,0},{2,3},{3,2},{4,5},{5,4},{6,7},{7,6},{8,9},{9,8},{10,11... | collective-permute-start | bytes 1572872 | tf_op jit(solution)/shard_map/ppermute | solution.py:144
  49.7 20.1 %collective-permute-start.13 = (bf16[128,2048]{0,1:T(8,128)(2,1)S(1)}, bf16[128,2048]{0,1:T(8,128)(2,1)S(1)}, u32[]{:S(2)}, u32[]{:S(2)}) collective-permute-start(bf16[128,2048]{0,1:T(8,128)(2,1)S(1)} %collective-permute-done.6), channel_id=1, source_target_pairs={{0,1},{1,0},{2,3},{3,2},{4,5},{5,4},{6,7},{7,6},{8,9},{9,8},{10,11... | collective-permute-start | bytes 1572872 | tf_op jit(solution)/shard_map/ppermute | solution.py:144
  59.2 8.7 %collective-permute-start.15 = (bf16[128,1024]{0,1:T(8,128)(2,1)S(1)}, bf16[128,1024]{0,1:T(8,128)(2,1)S(1)}, u32[]{:S(2)}, u32[]{:S(2)}) collective-permute-start(bf16[128,1024]{0,1:T(8,128)(2,1)S(1)} %slice.73), channel_id=1, source_target_pairs={{0,4},{4,8},{8,12},{12,14},{14,10},{10,6},{6,2},{2,0},{1,5},{5,9},... | collective-permute-start | bytes 786440 | tf_op jit(solution)/shard_map/ppermute | solution.py:151
  61.4 8.4 %collective-permute-start.17 = (bf16[128,1024]{0,1:T(8,128)(2,1)S(1)}, bf16[128,1024]{0,1:T(8,128)(2,1)S(1)}, u32[]{:S(2)}, u32[]{:S(2)}) collective-permute-start(bf16[128,1024]{0,1:T(8,128)(2,1)S(1)} %slice.74), channel_id=1, source_target_pairs={{4,0},{8,4},{12,8},{14,12},{10,14},{6,10},{2,6},{0,2},{5,1},{9,5},... | collective-permute-start | bytes 786440 | tf_op jit(solution)/shard_map/ppermute | solution.py:152
  61.5 9.8 %collective-permute-start.14 = (bf16[128,2048]{0,1:T(8,128)(2,1)S(1)}, bf16[128,2048]{0,1:T(8,128)(2,1)S(1)}, u32[]{:S(2)}, u32[]{:S(2)}) collective-permute-start(bf16[128,2048]{0,1:T(8,128)(2,1)S(1)} %collective-permute-done.7), channel_id=1, source_target_pairs={{0,1},{1,0},{2,3},{3,2},{4,5},{5,4},{6,7},{7,6},{8,9},{9,8},{10,11... | collective-permute-start | bytes 1572872 | tf_op jit(solution)/shard_map/ppermute | solution.py:144
  67.9 4.8 %collective-permute-start.16 = (bf16[128,1024]{0,1:T(8,128)(2,1)S(1)}, bf16[128,1024]{0,1:T(8,128)(2,1)S(1)}, u32[]{:S(2)}, u32[]{:S(2)}) collective-permute-start(bf16[128,1024]{0,1:T(8,128)(2,1)S(1)} %collective-permute-done.15), channel_id=1, source_target_pairs={{0,1},{1,0},{2,3},{3,2},{4,5},{5,4},{6,7},{7,6},{8,9},{9,8},{10,11... | collective-permute-start | bytes 786440 | tf_op jit(solution)/shard_map/ppermute | solution.py:144
  69.8 4.0 %collective-permute-start.18 = (bf16[128,1024]{0,1:T(8,128)(2,1)S(1)}, bf16[128,1024]{0,1:T(8,128)(2,1)S(1)}, u32[]{:S(2)}, u32[]{:S(2)}) collective-permute-start(bf16[128,1024]{0,1:T(8,128)(2,1)S(1)} %collective-permute-done.17), channel_id=1, source_target_pairs={{0,1},{1,0},{2,3},{3,2},{4,5},{5,4},{6,7},{7,6},{8,9},{9,8},{10,11... | collective-permute-start | bytes 786440 | tf_op jit(solution)/shard_map/ppermute | solution.py:144
  71.2 3.6 %copy-start.1 = (bf16[512,1024]{1,0:T(8,128)(2,1)S(1)}, bf16[512,1024]{1,0:T(8,128)(2,1)}, u32[]{:S(2)}) copy-start(bf16[512,1024]{1,0:T(8,128)(2,1)} %shard_map.64) | copy-start | bytes 3145732
  71.2 3.6 %copy-start.2 = (bf16[512,1024]{1,0:T(8,128)(2,1)S(1)}, bf16[512,1024]{1,0:T(8,128)(2,1)}, u32[]{:S(2)}) copy-start(bf16[512,1024]{1,0:T(8,128)(2,1)} %shard_map.65) | copy-start | bytes 3145732
  71.2 3.6 %copy-start.6 = (bf16[512,2048]{1,0:T(8,128)(2,1)S(1)}, bf16[512,2048]{1,0:T(8,128)(2,1)}, u32[]{:S(2)}) copy-start(bf16[512,2048]{1,0:T(8,128)(2,1)} %param.6) | copy-start | bytes 6291460

commit v13 on v11

--- a/solution.py
+++ b/solution.py
@@ -138,12 +138,20 @@
     swap = [(0, 1), (1, 0)]
     steps = chips // 2
 
-    weight = jnp.zeros((chips * 2 * width, channels), out_weight.dtype)
+    weight = None
+
+    pending = []
 
     def place(weight, piece, owner_chip, row=0):
         other = lax.ppermute(piece, "core", swap)
         for k, part in ((core, piece), (1 - core, other)):
-            weight = lax.dynamic_update_slice(weight, part, ((owner_chip * 2 + k) * width, row))
+            pending.append((part, (owner_chip * 2 + k) * width, row))
+        return weight
+
+    def settle(weight):
+        for part, column, row in pending:
+            weight = lax.dynamic_update_slice(weight, part, (column, row))
+        pending.clear()
         return weight
 
     def ring_step(step, weight, ahead, behind):
@@ -181,6 +189,8 @@
     first = hyena_gate(*inputs, 0, 2)
     if ring:
         first, ahead, behind, inputs = lax.optimization_barrier((first, ahead, behind, inputs))
+        weight = jnp.full((chips * 2 * width, channels), first[0, 0] * 0, out_weight.dtype)
+        weight = settle(weight)
         if steps >= 3:
             weight, ahead, behind = ring_step(3, weight, ahead, behind)
     second = hyena_gate(*inputs, 1, 2)
@@ -188,6 +198,7 @@
         second, ahead, behind = lax.optimization_barrier((second, ahead, behind))
         for step in range(4, steps + 1):
             weight, ahead, behind = ring_step(step, weight, ahead, behind)
+        weight = settle(weight)
     else:
         weight = lax.all_gather(out_weight.T, CTX, axis=0, tiled=True)
     gated = jnp.concatenate([first, second], axis=1)

time: 80.8 us -> 97.7 us (1.21)
  waiting for transfers between devices: 2.82 us -> 13.1 us
  local copies, waits for them, and re-layouts: 26.3 us -> 29.4 us
  starting transfers between devices: 19.6 us -> 22.3 us
    ppermute x3, waiting for transfers between devices: 0.01 us -> 6.85 us  [ring_step(): ahead = lax.ppermute(ahead, 'chip', forward)]
    ppermute x3, waiting for transfers between devices: 0.01 us -> 2.7 us  [ring_step(): behind = lax.ppermute(behind, 'chip', backward)]
    ppermute x3, starting transfers between devices: 9.91 us -> 12.6 us  [ring_step(): ahead = lax.ppermute(ahead, 'chip', forward)]
    ppermute x9, starting transfers between devices: 4.16 us -> 1.74 us  [place(): other = lax.ppermute(piece, 'core', swap)]
    ppermute x2, starting transfers between devices: 3.42 us -> 5.8 us  [shifted(): return lax.ppermute(block, CTX, route)]
    slice x0 -> x1, local copies, waits for them, and re-layouts: none -> 1.27 us  [on_device(): first[0, 0] * 0]
    dynamic_update_slice x18, local copies, waits for them, and re-layouts: 19.8 us -> 20.9 us  [settle(): weight = lax.dynamic_update_slice(weight, part, (column, row))]
  transfers between devices with their start and end apart: 19 -> 19, of which waited for: 2 -> 5; matrix products, arithmetic and copies ran while one was open for 37% -> 30% of each run, Pallas kernels for 22% -> 18%
where the time goes in v13:
time: 97.7 us; the launch traced here: 96.6 us
  local copies, waits for them, and re-layouts  29.4 us (30%)
  starting transfers between devices  22.3 us (23%)
  Pallas kernels  17.3 us (18%)
  waiting for transfers between devices  13.1 us (13%)
  matrix products  9.18 us (9%)
  other arithmetic  4.48 us (5%)
    dynamic_update_slice x18, local copies, waits for them, and re-layouts, settle(): weight = lax.dynamic_update_slice(weight, part, (column, row))  20.9 us
    pallas_call x2, Pallas kernels, hyena_gate(): pl.pallas_call(_gate_kernel, grid=(share,), in_specs=[pl.BlockSpec((per_t...  17.3 us
    ppermute x3, starting transfers between devices, ring_step(): ahead = lax.ppermute(ahead, 'chip', forward)  12.6 us
    dot_general x1, matrix products, on_device(): lax.dot_general(gated, weight, (((1,), (1,)), ((), ())), preferred_elemen...  9.18 us
    ppermute x3, waiting for transfers between devices, ring_step(): ahead = lax.ppermute(ahead, 'chip', forward)  6.85 us
    ppermute x2, starting transfers between devices, shifted(): return lax.ppermute(block, CTX, route)  5.8 us
    broadcast_in_dim x1, local copies, waits for them, and re-layouts, on_device(): jnp.full((chips * 2 * width, channels), first[0, 0] * 0, out_weight.dtype)  4.34 us
    convert_element_type x1, other arithmetic, carried_of(): return (second * carrier).astype(jnp.bfloat16)  2.95 us
  transfers between devices with their start and end apart: 19, of which 5 were waited for; matrix products, arithmetic and copies ran while one was open for 30% of the time, Pallas kernels for 18%

profile of v13, /device:TPU:0, one launch (start us, length us, event | category | flops | bytes accessed | tf_op | source)
XLA Modules:
  0.0 96.6 jit_solution(17158534063610236156)
XLA Ops:
  0.0 1.0 fusion.4
  1.0 3.0 %multiply_convert_fusion = bf16[128,2048]{1,0:T(8,128)(2,1)S(1)} fusion(bf16[512,6144]{1,0:T(8,128)(2,1)} %carrier_ref.2, f32[2048]{0:T(1024)S(1)} %bitcast.38, f32[2048]{0:T(1024)S(1)} %bitcast.34, f32[2048]{0:T(1024)S(1)} %bitcast.35, f32[2048]{0:T(1024)S(1)} %bitcast.36, f32[2048]{0:T(1024)S(1)} %bitcast.37, f32[2048]{0:T(1024)S(1)} %bitcast.33), kind=kLoop, calls=%fused_computation.4 | loop fusion | flops 4718592 | bytes 3719168 | tf_op jit(solution)/shard_map/convert_element_type | solution.py:122
  3.9 2.4 %collective-permute-start = (bf16[128,2048]{1,0:T(8,128)(2,1)S(1)}, bf16[128,2048]{1,0:T(8,128)(2,1)S(1)}, u32[]{:S(2)}, u32[]{:S(2)}) collective-permute-start(bf16[128,2048]{1,0:T(8,128)(2,1)S(1)} %multiply_convert_fusion), channel_id=1, source_target_pairs={{0,1},{1,2},{2,3},{3,4},{4,5},{5,6},{6,7},{7,8},{8,9},{9,10},{10,1... | collective-permute-start | bytes 1572872 | tf_op jit(solution)/shard_map/ppermute | solution.py:22
  6.3 2.6 %collective-permute-start.2 = (bf16[128,2048]{0,1:T(8,128)(2,1)}, bf16[128,2048]{0,1:T(8,128)(2,1)}, u32[]{:S(2)}, u32[]{:S(2)}) collective-permute-start(bf16[128,2048]{0,1:T(8,128)(2,1)} %bitcast.26), channel_id=1, source_target_pairs={{0,4},{4,8},{8,12},{12,14},{14,10},{10,6},{6,2},{2,0},{1,5},{5,9},... | collective-permute-start | bytes 1572872 | tf_op jit(solution)/shard_map/ppermute | solution.py:166
  8.9 0.9 slice.75
  9.9 3.4 %collective-permute-start.1 = (bf16[2,6144]{1,0:T(2,128)(2,1)S(1)}, bf16[2,6144]{1,0:T(2,128)(2,1)S(1)}, u32[]{:S(2)}, u32[]{:S(2)}) collective-permute-start(bf16[2,6144]{1,0:T(2,128)(2,1)S(1)} %slice.75), channel_id=1, source_target_pairs={{0,1},{1,2},{2,3},{3,4},{4,5},{5,6},{6,7},{7,8},{8,9},{9,10},{10,1... | collective-permute-start | bytes 73736 | tf_op jit(solution)/shard_map/ppermute | solution.py:22
  14.1 6.8 %collective-permute-done.2 = bf16[128,2048]{0,1:T(8,128)(2,1)} collective-permute-done((bf16[128,2048]{0,1:T(8,128)(2,1)}, bf16[128,2048]{0,1:T(8,128)(2,1)}, u32[]{:S(2)}, u32[]{:S(2)}) %collective-permute-start.2) | collective-permute-done | bytes 524320 | tf_op jit(solution)/shard_map/ppermute | solution.py:166
  21.0 2.7 %collective-permute-done.3 = bf16[128,2048]{0,1:T(8,128)(2,1)S(1)} collective-permute-done((bf16[128,2048]{0,1:T(8,128)(2,1)}, bf16[128,2048]{0,1:T(8,128)(2,1)S(1)}, u32[]{:S(2)}, u32[]{:S(2)}) %collective-permute-start.3) | collective-permute-done | bytes 524320 | tf_op jit(solution)/shard_map/ppermute | solution.py:167
  23.6 6.3 %collective-permute-start.4 = (bf16[128,2048]{0,1:T(8,128)(2,1)}, bf16[128,2048]{0,1:T(8,128)(2,1)S(1)}, u32[]{:S(2)}, u32[]{:S(2)}) collective-permute-start(bf16[128,2048]{0,1:T(8,128)(2,1)} %collective-permute-done.2), channel_id=1, source_target_pairs={{0,4},{4,8},{8,12},{12,14},{14,10},{10,6},{6,2},{2,0},{1,5},{5,9},... | collective-permute-start | bytes 1572872 | tf_op jit(solution)/shard_map/ppermute | solution.py:166
  31.5 8.7 %shard_map.64 = bf16[512,1024]{1,0:T(8,128)(2,1)} custom-call(f32[128,384]{1,0:T(8,128)} %pad_convert_fusion.1.fw_ref, f32[1,2048]{1,0:T(1,128)} %bitcast.31, f32[3,3,2048]{2,1,0:T(4,128)} %bitcast.24, bf16[3,2,2048]{2,1,0:T(2,128)(2,1)} %bitcast.29, bf16[128,2048]{1,0:T(8,128)(2,1)} %copy-done, bf16[512,6144]{1,0:T(8,128)(2,1)} %carrier_ref.2, ...), custom_call_target="tpu_custom_call" | custom-call | tf_op jit(solution)/shard_map/pallas_call | solution.py:95
  40.9 1.3 %slice.76 = bf16[1,1]{1,0:T(2,128)(2,1)} slice(bf16[512,1024]{1,0:T(8,128)(2,1)} %shard_map.64), slice={[0:1], [0:1]} | slice | bytes 4 | tf_op jit(solution)/shard_map/slice | solution.py:192
  42.1 3.7 %collective-permute-start.6 = (bf16[128,2048]{0,1:T(8,128)(2,1)S(1)}, bf16[128,2048]{0,1:T(8,128)(2,1)S(1)}, u32[]{:S(2)}, u32[]{:S(2)}) collective-permute-start(bf16[128,2048]{0,1:T(8,128)(2,1)S(1)} %collective-permute-done.4), channel_id=1, source_target_pairs={{0,4},{4,8},{8,12},{12,14},{14,10},{10,6},{6,2},{2,0},{1,5},{5,9},... | collective-permute-start | bytes 1572872 | tf_op jit(solution)/shard_map/ppermute | solution.py:166
  46.5 4.3 %broadcast_in_dim.3 = bf16[2048,2048]{0,1:T(8,128)(2,1)} broadcast(bf16[]{:T(256)} %bitcast.17), dimensions={} | broadcast | bytes 8388610 | tf_op jit(solution)/shard_map/broadcast_in_dim | solution.py:192
  50.9 0.9 constant_dynamic-update-slice_fusion.15
  52.0 2.0 %constant_dynamic-update-slice_fusion.14 = bf16[2048,2048]{0,1:T(8,128)(2,1)} fusion(bf16[2048,2048]{0,1:T(8,128)(2,1)} %constant_dynamic-update-slice_fusion.15, bf16[128,2048]{0,1:T(8,128)(2,1)} %collective-permute-done.8, s32[]{:T(128)S(6)} %select_n.115), kind=kLoop, calls=%fused_computation.21 | loop fusion | bytes 1048580 | tf_op jit(solution)/shard_map/dynamic_update_slice | solution.py:153
  53.9 2.0 %constant_dynamic-update-slice_fusion.13 = bf16[2048,2048]{0,1:T(8,128)(2,1)} fusion(bf16[2048,2048]{0,1:T(8,128)(2,1)} %constant_dynamic-update-slice_fusion.14, bf16[128,2048]{0,1:T(8,128)(2,1)} %collective-permute-done.2, s32[]{:T(128)S(6)} %select_n.121), kind=kLoop, calls=%fused_computation.20 | loop fusion | bytes 1048580 | tf_op jit(solution)/shard_map/dynamic_update_slice | solution.py:153
  56.3 2.0 %constant_dynamic-update-slice_fusion.12 = bf16[2048,2048]{0,1:T(8,128)(2,1)} fusion(bf16[2048,2048]{0,1:T(8,128)(2,1)} %constant_dynamic-update-slice_fusion.13, bf16[128,2048]{0,1:T(8,128)(2,1)} %collective-permute-done.9, s32[]{:T(128)S(6)} %select_n.122), kind=kLoop, calls=%fused_computation.19 | loop fusion | bytes 1048580 | tf_op jit(solution)/shard_map/dynamic_update_slice | solution.py:153
  58.3 0.9 constant_dynamic-update-slice_fusion.11
  59.2 2.0 %constant_dynamic-update-slice_fusion.10 = bf16[2048,2048]{0,1:T(8,128)(2,1)} fusion(bf16[2048,2048]{0,1:T(8,128)(2,1)} %constant_dynamic-update-slice_fusion.11, bf16[128,2048]{0,1:T(8,128)(2,1)} %collective-permute-done.10, s32[]{:T(128)S(6)} %select_n.126), kind=kLoop, calls=%fused_computation.17 | loop fusion | bytes 1048580 | tf_op jit(solution)/shard_map/dynamic_update_slice | solution.py:153
  61.2 0.9 constant_dynamic-update-slice_fusion.9
  62.9 8.7 %shard_map.65 = bf16[512,1024]{1,0:T(8,128)(2,1)} custom-call(f32[128,384]{1,0:T(8,128)} %pad_convert_fusion.fw_ref, f32[1,2048]{1,0:T(1,128)} %bitcast.32, f32[3,3,2048]{2,1,0:T(4,128)} %bitcast.25, bf16[3,2,2048]{2,1,0:T(2,128)(2,1)} %bitcast.30, bf16[128,2048]{1,0:T(8,128)(2,1)} %copy-done, bf16[512,6144]{1,0:T(8,128)(2,1)} %carrier_ref.2, ...), custom_call_target="tpu_custom_call" | custom-call | tf_op jit(solution)/shard_map/pallas_call | solution.py:95
  71.6 2.1 %collective-permute-start.15 = (bf16[128,1024]{0,1:T(8,128)(2,1)S(1)}, bf16[128,1024]{0,1:T(8,128)(2,1)S(1)}, u32[]{:S(2)}, u32[]{:S(2)}) collective-permute-start(bf16[128,1024]{0,1:T(8,128)(2,1)S(1)} %slice.77), channel_id=1, source_target_pairs={{0,4},{4,8},{8,12},{12,14},{14,10},{10,6},{6,2},{2,0},{1,5},{5,9},... | collective-permute-start | bytes 786440 | tf_op jit(solution)/shard_map/ppermute | solution.py:160
  74.3 0.9 constant_dynamic-update-slice_fusion.8
  75.2 0.9 constant_dynamic-update-slice_fusion.7
  76.1 1.9 %constant_dynamic-update-slice_fusion.6 = bf16[2048,2048]{0,1:T(8,128)(2,1)} fusion(bf16[2048,2048]{0,1:T(8,128)(2,1)} %constant_dynamic-update-slice_fusion.7, bf16[128,2048]{0,1:T(8,128)(2,1)} %collective-permute-done.12, s32[]{:T(128)S(6)} %select_n.134), kind=kLoop, calls=%fused_computation.13 | loop fusion | bytes 1048580 | tf_op jit(solution)/shard_map/dynamic_update_slice | solution.py:153
  78.0 0.9 constant_dynamic-update-slice_fusion.5
  79.0 0.9 collective-permute-done.15
  79.9 1.8 %collective-permute-done.17 = bf16[128,1024]{0,1:T(8,128)(2,1)S(1)} collective-permute-done((bf16[128,1024]{0,1:T(8,128)(2,1)S(1)}, bf16[128,1024]{0,1:T(8,128)(2,1)S(1)}, u32[]{:S(2)}, u32[]{:S(2)}) %collective-permute-start.17) | collective-permute-done | bytes 262176 | tf_op jit(solution)/shard_map/ppermute | solution.py:161
  81.7 0.9 constant_dynamic-update-slice_fusion.4
  82.6 0.9 constant_dynamic-update-slice_fusion.3
  83.4 0.9 constant_dynamic-update-slice_fusion.2
  87.4 9.2 %add_convert_fusion = bf16[512,2048]{1,0:T(8,128)(2,1)} fusion(bf16[512,2048]{1,0:T(8,128)(2,1)S(1)} %copy-done.6, bf16[2048,2048]{0,1:T(8,128)(2,1)} %constant_dynamic-update-slice_fusion.16, bf16[512,1024]{1,0:T(8,128)(2,1)S(1)} %copy-done.2, bf16[512,1024]{1,0:T(8,128)(2,1)S(1)} %copy-done.1), kind=kOutput, calls=%fused_computation | convolution fusion | flops 4302307328 | bytes 14680064 | tf_op jit(solution)/shard_map/dot_general | solution.py:205
  (52 shorter events, 8.3 us)
Async XLA Ops:
  3.9 10.2 %collective-permute-start = (bf16[128,2048]{1,0:T(8,128)(2,1)S(1)}, bf16[128,2048]{1,0:T(8,128)(2,1)S(1)}, u32[]{:S(2)}, u32[]{:S(2)}) collective-permute-start(bf16[128,2048]{1,0:T(8,128)(2,1)S(1)} %multiply_convert_fusion), channel_id=1, source_target_pairs={{0,1},{1,2},{2,3},{3,4},{4,5},{5,6},{6,7},{7,8},{8,9},{9,10},{10,1... | collective-permute-start | bytes 1572872 | tf_op jit(solution)/shard_map/ppermute | solution.py:22
  6.3 14.6 %collective-permute-start.2 = (bf16[128,2048]{0,1:T(8,128)(2,1)}, bf16[128,2048]{0,1:T(8,128)(2,1)}, u32[]{:S(2)}, u32[]{:S(2)}) collective-permute-start(bf16[128,2048]{0,1:T(8,128)(2,1)} %bitcast.26), channel_id=1, source_target_pairs={{0,4},{4,8},{8,12},{12,14},{14,10},{10,6},{6,2},{2,0},{1,5},{5,9},... | collective-permute-start | bytes 1572872 | tf_op jit(solution)/shard_map/ppermute | solution.py:166
  8.9 14.7 %collective-permute-start.3 = (bf16[128,2048]{0,1:T(8,128)(2,1)}, bf16[128,2048]{0,1:T(8,128)(2,1)S(1)}, u32[]{:S(2)}, u32[]{:S(2)}) collective-permute-start(bf16[128,2048]{0,1:T(8,128)(2,1)} %bitcast.27), channel_id=1, source_target_pairs={{4,0},{8,4},{12,8},{14,12},{10,14},{6,10},{2,6},{0,2},{5,1},{9,5},... | collective-permute-start | bytes 1572872 | tf_op jit(solution)/shard_map/ppermute | solution.py:167
  9.9 4.2 %collective-permute-start.1 = (bf16[2,6144]{1,0:T(2,128)(2,1)S(1)}, bf16[2,6144]{1,0:T(2,128)(2,1)S(1)}, u32[]{:S(2)}, u32[]{:S(2)}) collective-permute-start(bf16[2,6144]{1,0:T(2,128)(2,1)S(1)} %slice.75), channel_id=1, source_target_pairs={{0,1},{1,2},{2,3},{3,4},{4,5},{5,6},{6,7},{7,8},{8,9},{9,10},{10,1... | collective-permute-start | bytes 73736 | tf_op jit(solution)/shard_map/ppermute | solution.py:22
  14.1 17.4 %copy-start.5 = (bf16[2,6144]{1,0:T(2,128)(2,1)}, bf16[2,6144]{1,0:T(2,128)(2,1)S(1)}, u32[]{:S(2)}) copy-start(bf16[2,6144]{1,0:T(2,128)(2,1)S(1)} %collective-permute-done.1) | copy-start | bytes 73732
  14.1 17.4 %copy-start = (bf16[128,2048]{1,0:T(8,128)(2,1)}, bf16[128,2048]{1,0:T(8,128)(2,1)S(1)}, u32[]{:S(2)}) copy-start(bf16[128,2048]{1,0:T(8,128)(2,1)S(1)} %collective-permute-done.halo_ref) | copy-start | bytes 1572868
  23.6 17.2 %collective-permute-start.4 = (bf16[128,2048]{0,1:T(8,128)(2,1)}, bf16[128,2048]{0,1:T(8,128)(2,1)S(1)}, u32[]{:S(2)}, u32[]{:S(2)}) collective-permute-start(bf16[128,2048]{0,1:T(8,128)(2,1)} %collective-permute-done.2), channel_id=1, source_target_pairs={{0,4},{4,8},{8,12},{12,14},{14,10},{10,6},{6,2},{2,0},{1,5},{5,9},... | collective-permute-start | bytes 1572872 | tf_op jit(solution)/shard_map/ppermute | solution.py:166
  29.9 10.9 %collective-permute-start.5 = (bf16[128,2048]{0,1:T(8,128)(2,1)S(1)}, bf16[128,2048]{0,1:T(8,128)(2,1)S(1)}, u32[]{:S(2)}, u32[]{:S(2)}) collective-permute-start(bf16[128,2048]{0,1:T(8,128)(2,1)S(1)} %collective-permute-done.3), channel_id=1, source_target_pairs={{4,0},{8,4},{12,8},{14,12},{10,14},{6,10},{2,6},{0,2},{5,1},{9,5},... | collective-permute-start | bytes 1572872 | tf_op jit(solution)/shard_map/ppermute | solution.py:167
  29.9 21.9 %collective-permute-start.8 = (bf16[128,2048]{0,1:T(8,128)(2,1)}, bf16[128,2048]{0,1:T(8,128)(2,1)}, u32[]{:S(2)}, u32[]{:S(2)}) collective-permute-start(bf16[128,2048]{0,1:T(8,128)(2,1)} %bitcast.28), channel_id=1, source_target_pairs={{0,1},{1,0},{2,3},{3,2},{4,5},{5,4},{6,7},{7,6},{8,9},{9,8},{10,11... | collective-permute-start | bytes 1572872 | tf_op jit(solution)/shard_map/ppermute | solution.py:146
  40.2 10.7 %copy-start.3 = (bf16[2048,128]{1,0:T(8,128)(2,1)S(1)}, bf16[2048,128]{1,0:T(8,128)(2,1)}, u32[]{:S(2)}) copy-start(bf16[2048,128]{1,0:T(8,128)(2,1)} %param.11) | copy-start | bytes 1572868
  40.2 11.6 %copy-start.4 = (bf16[128,128]{1,0:T(8,128)(2,1)S(1)}, bf16[128,128]{1,0:T(8,128)(2,1)}, u32[]{:S(2)}) copy-start(bf16[128,128]{1,0:T(8,128)(2,1)} %param.9) | copy-start | bytes 98308
  40.2 15.6 %collective-permute-start.9 = (bf16[128,2048]{0,1:T(8,128)(2,1)}, bf16[128,2048]{0,1:T(8,128)(2,1)}, u32[]{:S(2)}, u32[]{:S(2)}) collective-permute-start(bf16[128,2048]{0,1:T(8,128)(2,1)} %collective-permute-done.2), channel_id=1, source_target_pairs={{0,1},{1,0},{2,3},{3,2},{4,5},{5,4},{6,7},{7,6},{8,9},{9,8},{10,11... | collective-permute-start | bytes 1572872 | tf_op jit(solution)/shard_map/ppermute | solution.py:146
  40.8 18.4 %collective-permute-start.10 = (bf16[128,2048]{0,1:T(8,128)(2,1)S(1)}, bf16[128,2048]{0,1:T(8,128)(2,1)}, u32[]{:S(2)}, u32[]{:S(2)}) collective-permute-start(bf16[128,2048]{0,1:T(8,128)(2,1)S(1)} %collective-permute-done.3), channel_id=1, source_target_pairs={{0,1},{1,0},{2,3},{3,2},{4,5},{5,4},{6,7},{7,6},{8,9},{9,8},{10,11... | collective-permute-start | bytes 1572872 | tf_op jit(solution)/shard_map/ppermute | solution.py:146
  42.1 29.4 %collective-permute-start.6 = (bf16[128,2048]{0,1:T(8,128)(2,1)S(1)}, bf16[128,2048]{0,1:T(8,128)(2,1)S(1)}, u32[]{:S(2)}, u32[]{:S(2)}) collective-permute-start(bf16[128,2048]{0,1:T(8,128)(2,1)S(1)} %collective-permute-done.4), channel_id=1, source_target_pairs={{0,4},{4,8},{8,12},{12,14},{14,10},{10,6},{6,2},{2,0},{1,5},{5,9},... | collective-permute-start | bytes 1572872 | tf_op jit(solution)/shard_map/ppermute | solution.py:166
  45.8 25.7 %collective-permute-start.7 = (bf16[128,2048]{0,1:T(8,128)(2,1)S(1)}, bf16[128,2048]{0,1:T(8,128)(2,1)S(1)}, u32[]{:S(2)}, u32[]{:S(2)}) collective-permute-start(bf16[128,2048]{0,1:T(8,128)(2,1)S(1)} %collective-permute-done.5), channel_id=1, source_target_pairs={{4,0},{8,4},{12,8},{14,12},{10,14},{6,10},{2,6},{0,2},{5,1},{9,5},... | collective-permute-start | bytes 1572872 | tf_op jit(solution)/shard_map/ppermute | solution.py:167
  51.9 22.0 %collective-permute-start.11 = (bf16[128,2048]{0,1:T(8,128)(2,1)S(1)}, bf16[128,2048]{0,1:T(8,128)(2,1)S(1)}, u32[]{:S(2)}, u32[]{:S(2)}) collective-permute-start(bf16[128,2048]{0,1:T(8,128)(2,1)S(1)} %collective-permute-done.4), channel_id=1, source_target_pairs={{0,1},{1,0},{2,3},{3,2},{4,5},{5,4},{6,7},{7,6},{8,9},{9,8},{10,11... | collective-permute-start | bytes 1572872 | tf_op jit(solution)/shard_map/ppermute | solution.py:146
  55.9 20.2 %collective-permute-start.12 = (bf16[128,2048]{0,1:T(8,128)(2,1)S(1)}, bf16[128,2048]{0,1:T(8,128)(2,1)}, u32[]{:S(2)}, u32[]{:S(2)}) collective-permute-start(bf16[128,2048]{0,1:T(8,128)(2,1)S(1)} %collective-permute-done.5), channel_id=1, source_target_pairs={{0,1},{1,0},{2,3},{3,2},{4,5},{5,4},{6,7},{7,6},{8,9},{9,8},{10,11... | collective-permute-start | bytes 1572872 | tf_op jit(solution)/shard_map/ppermute | solution.py:146
  71.5 15.9 %copy-start.1 = (bf16[512,1024]{1,0:T(8,128)(2,1)S(1)}, bf16[512,1024]{1,0:T(8,128)(2,1)}, u32[]{:S(2)}) copy-start(bf16[512,1024]{1,0:T(8,128)(2,1)} %shard_map.64) | copy-start | bytes 3145732
  71.5 15.9 %copy-start.2 = (bf16[512,1024]{1,0:T(8,128)(2,1)S(1)}, bf16[512,1024]{1,0:T(8,128)(2,1)}, u32[]{:S(2)}) copy-start(bf16[512,1024]{1,0:T(8,128)(2,1)} %shard_map.65) | copy-start | bytes 3145732
  71.5 15.9 %copy-start.6 = (bf16[512,2048]{1,0:T(8,128)(2,1)S(1)}, bf16[512,2048]{1,0:T(8,128)(2,1)}, u32[]{:S(2)}) copy-start(bf16[512,2048]{1,0:T(8,128)(2,1)} %param.6) | copy-start | bytes 6291460
  71.6 8.3 %collective-permute-start.15 = (bf16[128,1024]{0,1:T(8,128)(2,1)S(1)}, bf16[128,1024]{0,1:T(8,128)(2,1)S(1)}, u32[]{:S(2)}, u32[]{:S(2)}) collective-permute-start(bf16[128,1024]{0,1:T(8,128)(2,1)S(1)} %slice.77), channel_id=1, source_target_pairs={{0,4},{4,8},{8,12},{12,14},{14,10},{10,6},{6,2},{2,0},{1,5},{5,9},... | collective-permute-start | bytes 786440 | tf_op jit(solution)/shard_map/ppermute | solution.py:160
  73.7 8.0 %collective-permute-start.17 = (bf16[128,1024]{0,1:T(8,128)(2,1)S(1)}, bf16[128,1024]{0,1:T(8,128)(2,1)S(1)}, u32[]{:S(2)}, u32[]{:S(2)}) collective-permute-start(bf16[128,1024]{0,1:T(8,128)(2,1)S(1)} %slice.78), channel_id=1, source_target_pairs={{4,0},{8,4},{12,8},{14,12},{10,14},{6,10},{2,6},{0,2},{5,1},{9,5},... | collective-permute-start | bytes 786440 | tf_op jit(solution)/shard_map/ppermute | solution.py:161
  73.8 7.9 %collective-permute-start.13 = (bf16[128,2048]{0,1:T(8,128)(2,1)S(1)}, bf16[128,2048]{0,1:T(8,128)(2,1)S(1)}, u32[]{:S(2)}, u32[]{:S(2)}) collective-permute-start(bf16[128,2048]{0,1:T(8,128)(2,1)S(1)} %collective-permute-done.6), channel_id=1, source_target_pairs={{0,1},{1,0},{2,3},{3,2},{4,5},{5,4},{6,7},{7,6},{8,9},{9,8},{10,11... | collective-permute-start | bytes 1572872 | tf_op jit(solution)/shard_map/ppermute | solution.py:146
  73.8 9.6 %collective-permute-start.14 = (bf16[128,2048]{0,1:T(8,128)(2,1)S(1)}, bf16[128,2048]{0,1:T(8,128)(2,1)S(1)}, u32[]{:S(2)}, u32[]{:S(2)}) collective-permute-start(bf16[128,2048]{0,1:T(8,128)(2,1)S(1)} %collective-permute-done.7), channel_id=1, source_target_pairs={{0,1},{1,0},{2,3},{3,2},{4,5},{5,4},{6,7},{7,6},{8,9},{9,8},{10,11... | collective-permute-start | bytes 1572872 | tf_op jit(solution)/shard_map/ppermute | solution.py:146
  79.9 5.2 %collective-permute-start.16 = (bf16[128,1024]{0,1:T(8,128)(2,1)S(1)}, bf16[128,1024]{0,1:T(8,128)(2,1)S(1)}, u32[]{:S(2)}, u32[]{:S(2)}) collective-permute-start(bf16[128,1024]{0,1:T(8,128)(2,1)S(1)} %collective-permute-done.15), channel_id=1, source_target_pairs={{0,1},{1,0},{2,3},{3,2},{4,5},{5,4},{6,7},{7,6},{8,9},{9,8},{10,11... | collective-permute-start | bytes 786440 | tf_op jit(solution)/shard_map/ppermute | solution.py:146
  81.7 4.9 %collective-permute-start.18 = (bf16[128,1024]{0,1:T(8,128)(2,1)S(1)}, bf16[128,1024]{0,1:T(8,128)(2,1)S(1)}, u32[]{:S(2)}, u32[]{:S(2)}) collective-permute-start(bf16[128,1024]{0,1:T(8,128)(2,1)S(1)} %collective-permute-done.17), channel_id=1, source_target_pairs={{0,1},{1,0},{2,3},{3,2},{4,5},{5,4},{6,7},{7,6},{8,9},{9,8},{10,11... | collective-permute-start | bytes 786440 | tf_op jit(solution)/shard_map/ppermute | solution.py:146

commit v14 on v11

--- a/solution.py
+++ b/solution.py
@@ -138,12 +138,12 @@
     swap = [(0, 1), (1, 0)]
     steps = chips // 2
 
-    weight = jnp.zeros((chips * 2 * width, channels), out_weight.dtype)
+    weight = jnp.zeros((chips * 2, width, channels), out_weight.dtype)
 
     def place(weight, piece, owner_chip, row=0):
         other = lax.ppermute(piece, "core", swap)
         for k, part in ((core, piece), (1 - core, other)):
-            weight = lax.dynamic_update_slice(weight, part, ((owner_chip * 2 + k) * width, row))
+            weight = lax.dynamic_update_slice(weight, part[None], (owner_chip * 2 + k, 0, row))
         return weight
 
     def ring_step(step, weight, ahead, behind):
@@ -190,6 +190,7 @@
             weight, ahead, behind = ring_step(step, weight, ahead, behind)
     else:
         weight = lax.all_gather(out_weight.T, CTX, axis=0, tiled=True)
+    weight = weight.reshape(-1, channels)
     gated = jnp.concatenate([first, second], axis=1)
     branch = lax.dot_general(gated, weight, (((1,), (1,)), ((), ())), preferred_element_type=jnp.float32)
     return (tokens.astype(jnp.float32) + branch).astype(jnp.bfloat16)

time: 80.8 us -> 81.5 us (level)
  waiting for transfers between devices: 2.82 us -> 4.03 us
  starting transfers between devices: 19.6 us -> 18.6 us
    ppermute x2, starting transfers between devices: 3.42 us -> 5.87 us  [shifted(): return lax.ppermute(block, CTX, route)]
    ppermute x9, starting transfers between devices: 4.16 us -> 2.1 us  [place(): other = lax.ppermute(piece, 'core', swap)]
    ppermute x3, starting transfers between devices: 9.91 us -> 8.09 us  [ring_step(): ahead = lax.ppermute(ahead, 'chip', forward)]
    dynamic_update_slice x18, local copies, waits for them, and re-layouts: 19.8 us -> 18.2 us  [place(): lax.dynamic_update_slice(weight, part[None], (owner_chip * 2 + k, 0, row))]
    unnamed x14 -> x13, local copies, waits for them, and re-layouts: 0.03 us -> 1.27 us
    ppermute x1, waiting for transfers between devices: 1 us -> 2.07 us  [ring_step(): ahead = lax.ppermute(ahead[:, :half], 'chip', forward)]
  transfers between devices with their start and end apart: 19 -> 19, of which waited for: 2 -> 3; matrix products, arithmetic and copies ran while one was open for 37% -> 36% of each run, Pallas kernels for 22% -> 21%
where the time goes in v14:
time: 81.5 us; the launch traced here: 80.6 us
  local copies, waits for them, and re-layouts  26.6 us (33%)
  starting transfers between devices  18.6 us (23%)
  Pallas kernels  17.3 us (21%)
  matrix products  9.4 us (12%)
  other arithmetic  4.43 us (5%)
  waiting for transfers between devices  4.03 us (5%)
    dynamic_update_slice x18, local copies, waits for them, and re-layouts, place(): lax.dynamic_update_slice(weight, part[None], (owner_chip * 2 + k, 0, row))  18.2 us
    pallas_call x2, Pallas kernels, hyena_gate(): pl.pallas_call(_gate_kernel, grid=(share,), in_specs=[pl.BlockSpec((per_t...  17.3 us
    dot_general x1, matrix products, on_device(): lax.dot_general(gated, weight, (((1,), (1,)), ((), ())), preferred_elemen...  9.4 us
    ppermute x3, starting transfers between devices, ring_step(): ahead = lax.ppermute(ahead, 'chip', forward)  8.09 us
    ppermute x2, starting transfers between devices, shifted(): return lax.ppermute(block, CTX, route)  5.87 us
    broadcast_in_dim x1, local copies, waits for them, and re-layouts, on_device(): weight = jnp.zeros((chips * 2, width, channels), out_weight.dtype)  4.33 us
    convert_element_type x1, other arithmetic, carried_of(): return (second * carrier).astype(jnp.bfloat16)  2.9 us
    ppermute x9, starting transfers between devices, place(): other = lax.ppermute(piece, 'core', swap)  2.1 us
  transfers between devices with their start and end apart: 19, of which 3 were waited for; matrix products, arithmetic and copies ran while one was open for 36% of the time, Pallas kernels for 21%

profile of v14, /device:TPU:0, one launch (start us, length us, event | category | flops | bytes accessed | tf_op | source)
XLA Modules:
  0.0 80.6 jit_solution(6093922826593218902)
XLA Ops:
  0.0 1.2 %copy.7 = bf16[2048,128]{0,1:T(8,128)(2,1)S(1)} copy(bf16[2048,128]{1,0:T(8,128)(2,1)} %param.11) | data formatting | bytes 1048576 | tf_op args[5]
  1.8 2.6 %collective-permute-start.2 = (bf16[128,2048]{1,0:T(8,128)(2,1)S(1)}, bf16[128,2048]{1,0:T(8,128)(2,1)S(1)}, u32[]{:S(2)}, u32[]{:S(2)}) collective-permute-start(bf16[128,2048]{1,0:T(8,128)(2,1)S(1)} %bitcast.61), channel_id=1, source_target_pairs={{0,4},{4,8},{8,12},{12,14},{14,10},{10,6},{6,2},{2,0},{1,5},{5,9},... | collective-permute-start | bytes 1572872 | tf_op jit(solution)/shard_map/ppermute | solution.py:158
  4.4 1.0 %fusion.4 = (f32[1,2048]{1,0:T(1,128)S(1)}, f32[1,2048]{1,0:T(1,128)S(1)}, f32[1,2048]{1,0:T(1,128)S(1)}, f32[1,2048]{1,0:T(1,128)S(1)}, f32[1,2048]{1,0:T(1,128)S(1)}, /*index=5*/f32[1,2048]{1,0:T(1,128)S(1)}) fusion(f32[3,6144]{1,0:T(4,128)} %param.8), kind=kLoop, calls=%fused_computation.26 | loop fusion | bytes 98304 | tf_op jit(solution)/shard_map/slice | solution.py:34
  5.4 2.9 %multiply_convert_fusion = bf16[128,2048]{1,0:T(8,128)(2,1)S(1)} fusion(bf16[512,6144]{1,0:T(8,128)(2,1)} %carrier_ref.2, f32[2048]{0:T(1024)S(1)} %bitcast.74, f32[2048]{0:T(1024)S(1)} %bitcast.70, f32[2048]{0:T(1024)S(1)} %bitcast.71, f32[2048]{0:T(1024)S(1)} %bitcast.72, f32[2048]{0:T(1024)S(1)} %bitcast.73, f32[2048]{0:T(1024)S(1)} %bitcast.69), kind=kLoop, calls=%fused_computation.4 | loop fusion | flops 4718592 | bytes 3719168 | tf_op jit(solution)/shard_map/convert_element_type | solution.py:122
  8.3 2.1 %collective-permute-start = (bf16[128,2048]{1,0:T(8,128)(2,1)S(1)}, bf16[128,2048]{1,0:T(8,128)(2,1)S(1)}, u32[]{:S(2)}, u32[]{:S(2)}) collective-permute-start(bf16[128,2048]{1,0:T(8,128)(2,1)S(1)} %multiply_convert_fusion), channel_id=1, source_target_pairs={{0,1},{1,2},{2,3},{3,4},{4,5},{5,6},{6,7},{7,8},{8,9},{9,10},{10,1... | collective-permute-start | bytes 1572872 | tf_op jit(solution)/shard_map/ppermute | solution.py:22
  10.4 0.9 %slice.72 = bf16[2,6144]{1,0:T(2,128)(2,1)S(1)} slice(bf16[512,6144]{1,0:T(8,128)(2,1)} %carrier_ref.2), slice={[510:512], [0:6144]} | slice | bytes 49152 | tf_op jit(solution)/shard_map/slice | solution.py:175
  11.3 3.8 %collective-permute-start.1 = (bf16[2,6144]{1,0:T(2,128)(2,1)S(1)}, bf16[2,6144]{1,0:T(2,128)(2,1)S(1)}, u32[]{:S(2)}, u32[]{:S(2)}) collective-permute-start(bf16[2,6144]{1,0:T(2,128)(2,1)S(1)} %slice.72), channel_id=1, source_target_pairs={{0,1},{1,2},{2,3},{3,4},{4,5},{5,6},{6,7},{7,8},{8,9},{9,10},{10,1... | collective-permute-start | bytes 73736 | tf_op jit(solution)/shard_map/ppermute | solution.py:22
  15.1 0.8 %rev.6 = bf16[128,128]{1,0:T(8,128)(2,1)S(1)} reverse(bf16[128,128]{1,0:T(8,128)(2,1)} %param.9), dimensions={1} | reverse | bytes 65536 | tf_op jit(solution)/shard_map/rev | solution.py:91
  16.0 4.3 %broadcast_in_dim.57 = bf16[16,128,2048]{2,1,0:T(8,128)(2,1)} broadcast(bf16[]{:T(256)} %constant.74.clone.1), dimensions={} | broadcast | bytes 8388610 | tf_op jit(solution)/shard_map/broadcast_in_dim | solution.py:141
  20.3 0.8 %bitcast_dynamic-update-slice_fusion = bf16[16,128,2048]{2,1,0:T(8,128)(2,1)} fusion(bf16[16,128,2048]{2,1,0:T(8,128)(2,1)} %broadcast_in_dim.57, s32[]{:T(128)S(6)} %select_n.114, bf16[2048,128]{0,1:T(8,128)(2,1)S(1)} %copy.7), kind=kLoop, calls=%fused_computation.5 | loop fusion | bytes 1048580 | tf_op jit(solution)/shard_map/dynamic_update_slice | solution.py:146
  21.9 3.8 %collective-permute-start.4 = (bf16[128,2048]{1,0:T(8,128)(2,1)S(1)}, bf16[128,2048]{1,0:T(8,128)(2,1)}, u32[]{:S(2)}, u32[]{:S(2)}) collective-permute-start(bf16[128,2048]{1,0:T(8,128)(2,1)S(1)} %collective-permute-done.2), channel_id=1, source_target_pairs={{0,4},{4,8},{8,12},{12,14},{14,10},{10,6},{6,2},{2,0},{1,5},{5,9},... | collective-permute-start | bytes 1572872 | tf_op jit(solution)/shard_map/ppermute | solution.py:158
  25.8 8.7 %shard_map.64 = bf16[512,1024]{1,0:T(8,128)(2,1)} custom-call(f32[128,384]{1,0:T(8,128)} %pad_convert_fusion.1.fw_ref, f32[1,2048]{1,0:T(1,128)} %bitcast.67, f32[3,3,2048]{2,1,0:T(4,128)} %bitcast.63, bf16[3,2,2048]{2,1,0:T(2,128)(2,1)} %bitcast.65, bf16[128,2048]{1,0:T(8,128)(2,1)} %copy-done, bf16[512,6144]{1,0:T(8,128)(2,1)} %carrier_ref.2, ...), custom_call_target="tpu_custom_call" | custom-call | tf_op jit(solution)/shard_map/pallas_call | solution.py:95
  35.0 0.8 %bitcast_dynamic-update-slice_fusion.13 = bf16[16,128,2048]{2,1,0:T(8,128)(2,1)} fusion(bf16[16,128,2048]{2,1,0:T(8,128)(2,1)} %bitcast_dynamic-update-slice_fusion, s32[]{:T(128)S(6)} %select_n.115, bf16[128,2048]{1,0:T(8,128)(2,1)S(1)} %collective-permute-done.8), kind=kLoop, calls=%fused_computation.18 | loop fusion | bytes 1048580 | tf_op jit(solution)/shard_map/dynamic_update_slice | solution.py:146
  35.8 0.8 %bitcast_dynamic-update-slice_fusion.12 = bf16[16,128,2048]{2,1,0:T(8,128)(2,1)} fusion(bf16[16,128,2048]{2,1,0:T(8,128)(2,1)} %bitcast_dynamic-update-slice_fusion.13, s32[]{:T(128)S(6)} %select_n.121, bf16[128,2048]{1,0:T(8,128)(2,1)S(1)} %collective-permute-done.2), kind=kLoop, calls=%fused_computation.17 | loop fusion | bytes 1048580 | tf_op jit(solution)/shard_map/dynamic_update_slice | solution.py:146
  37.1 1.6 %collective-permute-start.6 = (bf16[128,2048]{1,0:T(8,128)(2,1)}, bf16[128,2048]{1,0:T(8,128)(2,1)S(1)}, u32[]{:S(2)}, u32[]{:S(2)}) collective-permute-start(bf16[128,2048]{1,0:T(8,128)(2,1)} %collective-permute-done.4), channel_id=1, source_target_pairs={{0,4},{4,8},{8,12},{12,14},{14,10},{10,6},{6,2},{2,0},{1,5},{5,9},... | collective-permute-start | bytes 1572872 | tf_op jit(solution)/shard_map/ppermute | solution.py:158
  40.0 8.6 %shard_map.65 = bf16[512,1024]{1,0:T(8,128)(2,1)} custom-call(f32[128,384]{1,0:T(8,128)} %pad_convert_fusion.fw_ref, f32[1,2048]{1,0:T(1,128)} %bitcast.68, f32[3,3,2048]{2,1,0:T(4,128)} %bitcast.64, bf16[3,2,2048]{2,1,0:T(2,128)(2,1)} %bitcast.66, bf16[128,2048]{1,0:T(8,128)(2,1)} %copy-done, bf16[512,6144]{1,0:T(8,128)(2,1)} %carrier_ref.2, ...), custom_call_target="tpu_custom_call" | custom-call | tf_op jit(solution)/shard_map/pallas_call | solution.py:95
  49.3 2.2 %bitcast_dynamic-update-slice_fusion.11 = bf16[16,128,2048]{2,1,0:T(8,128)(2,1)} fusion(bf16[16,128,2048]{2,1,0:T(8,128)(2,1)} %bitcast_dynamic-update-slice_fusion.12, s32[]{:T(128)S(6)} %select_n.122, bf16[128,2048]{1,0:T(8,128)(2,1)} %collective-permute-done.9), kind=kLoop, calls=%fused_computation.16 | loop fusion | bytes 1048580 | tf_op jit(solution)/shard_map/dynamic_update_slice | solution.py:146
  51.4 0.8 %bitcast_dynamic-update-slice_fusion.10 = bf16[16,128,2048]{2,1,0:T(8,128)(2,1)} fusion(bf16[16,128,2048]{2,1,0:T(8,128)(2,1)} %bitcast_dynamic-update-slice_fusion.11, s32[]{:T(128)S(6)} %select_n.125, bf16[128,2048]{1,0:T(8,128)(2,1)S(1)} %collective-permute-done.3), kind=kLoop, calls=%fused_computation.15 | loop fusion | bytes 1048580 | tf_op jit(solution)/shard_map/dynamic_update_slice | solution.py:146
  52.3 1.9 %bitcast_dynamic-update-slice_fusion.9 = bf16[16,128,2048]{2,1,0:T(8,128)(2,1)} fusion(bf16[16,128,2048]{2,1,0:T(8,128)(2,1)} %bitcast_dynamic-update-slice_fusion.10, s32[]{:T(128)S(6)} %select_n.126, bf16[128,2048]{1,0:T(8,128)(2,1)} %collective-permute-done.10), kind=kLoop, calls=%fused_computation.14 | loop fusion | bytes 1048580 | tf_op jit(solution)/shard_map/dynamic_update_slice | solution.py:146
  54.2 1.9 %bitcast_dynamic-update-slice_fusion.8 = bf16[16,128,2048]{2,1,0:T(8,128)(2,1)} fusion(bf16[16,128,2048]{2,1,0:T(8,128)(2,1)} %bitcast_dynamic-update-slice_fusion.9, s32[]{:T(128)S(6)} %select_n.129, bf16[128,2048]{1,0:T(8,128)(2,1)} %collective-permute-done.4), kind=kLoop, calls=%fused_computation.13 | loop fusion | bytes 1048580 | tf_op jit(solution)/shard_map/dynamic_update_slice | solution.py:146
  56.1 1.7 %collective-permute-start.15 = (bf16[128,1024]{1,0:T(8,128)(2,1)S(1)}, bf16[128,1024]{1,0:T(8,128)(2,1)S(1)}, u32[]{:S(2)}, u32[]{:S(2)}) collective-permute-start(bf16[128,1024]{1,0:T(8,128)(2,1)S(1)} %slice.73), channel_id=1, source_target_pairs={{0,4},{4,8},{8,12},{12,14},{14,10},{10,6},{6,2},{2,0},{1,5},{5,9},... | collective-permute-start | bytes 786440 | tf_op jit(solution)/shard_map/ppermute | solution.py:152
  58.7 0.8 %bitcast_dynamic-update-slice_fusion.7 = bf16[16,128,2048]{2,1,0:T(8,128)(2,1)} fusion(bf16[16,128,2048]{2,1,0:T(8,128)(2,1)} %bitcast_dynamic-update-slice_fusion.8, s32[]{:T(128)S(6)} %select_n.130, bf16[128,2048]{1,0:T(8,128)(2,1)S(1)} %collective-permute-done.11), kind=kLoop, calls=%fused_computation.12 | loop fusion | bytes 1048580 | tf_op jit(solution)/shard_map/dynamic_update_slice | solution.py:146
  59.5 0.8 %bitcast_dynamic-update-slice_fusion.6 = bf16[16,128,2048]{2,1,0:T(8,128)(2,1)} fusion(bf16[16,128,2048]{2,1,0:T(8,128)(2,1)} %bitcast_dynamic-update-slice_fusion.7, s32[]{:T(128)S(6)} %select_n.133, bf16[128,2048]{1,0:T(8,128)(2,1)S(1)} %collective-permute-done.5), kind=kLoop, calls=%fused_computation.11 | loop fusion | bytes 1048580 | tf_op jit(solution)/shard_map/dynamic_update_slice | solution.py:146
  60.4 0.8 %bitcast_dynamic-update-slice_fusion.5 = bf16[16,128,2048]{2,1,0:T(8,128)(2,1)} fusion(bf16[16,128,2048]{2,1,0:T(8,128)(2,1)} %bitcast_dynamic-update-slice_fusion.6, s32[]{:T(128)S(6)} %select_n.134, bf16[128,2048]{1,0:T(8,128)(2,1)S(1)} %collective-permute-done.12), kind=kLoop, calls=%fused_computation.10 | loop fusion | bytes 1048580 | tf_op jit(solution)/shard_map/dynamic_update_slice | solution.py:146
  61.2 0.8 %bitcast_dynamic-update-slice_fusion.4 = bf16[16,128,2048]{2,1,0:T(8,128)(2,1)} fusion(bf16[16,128,2048]{2,1,0:T(8,128)(2,1)} %bitcast_dynamic-update-slice_fusion.5, s32[]{:T(128)S(6)} %select_n.137, bf16[128,2048]{1,0:T(8,128)(2,1)S(1)} %collective-permute-done.6), kind=kLoop, calls=%fused_computation.9 | loop fusion | bytes 1048580 | tf_op jit(solution)/shard_map/dynamic_update_slice | solution.py:146
  62.0 2.1 %collective-permute-done.15 = bf16[128,1024]{1,0:T(8,128)(2,1)S(1)} collective-permute-done((bf16[128,1024]{1,0:T(8,128)(2,1)S(1)}, bf16[128,1024]{1,0:T(8,128)(2,1)S(1)}, u32[]{:S(2)}, u32[]{:S(2)}) %collective-permute-start.15) | collective-permute-done | bytes 262176 | tf_op jit(solution)/shard_map/ppermute | solution.py:152
  64.1 1.5 %collective-permute-done.17 = bf16[128,1024]{1,0:T(8,128)(2,1)S(1)} collective-permute-done((bf16[128,1024]{1,0:T(8,128)(2,1)S(1)}, bf16[128,1024]{1,0:T(8,128)(2,1)S(1)}, u32[]{:S(2)}, u32[]{:S(2)}) %collective-permute-start.17) | collective-permute-done | bytes 262176 | tf_op jit(solution)/shard_map/ppermute | solution.py:153
  65.6 0.8 %bitcast_dynamic-update-slice_fusion.3 = bf16[16,128,2048]{2,1,0:T(8,128)(2,1)} fusion(bf16[16,128,2048]{2,1,0:T(8,128)(2,1)} %bitcast_dynamic-update-slice_fusion.4, s32[]{:T(128)S(6)} %select_n.138, bf16[128,2048]{1,0:T(8,128)(2,1)S(1)} %collective-permute-done.13), kind=kLoop, calls=%fused_computation.8 | loop fusion | bytes 1048580 | tf_op jit(solution)/shard_map/dynamic_update_slice | solution.py:146
  66.4 0.8 %bitcast_dynamic-update-slice_fusion.2 = bf16[16,128,2048]{2,1,0:T(8,128)(2,1)} fusion(bf16[16,128,2048]{2,1,0:T(8,128)(2,1)} %bitcast_dynamic-update-slice_fusion.3, s32[]{:T(128)S(6)} %select_n.141, bf16[128,2048]{1,0:T(8,128)(2,1)S(1)} %collective-permute-done.7), kind=kLoop, calls=%fused_computation.7 | loop fusion | bytes 1048580 | tf_op jit(solution)/shard_map/dynamic_update_slice | solution.py:146
  67.3 0.8 %bitcast_dynamic-update-slice_fusion.1 = bf16[16,128,2048]{2,1,0:T(8,128)(2,1)} fusion(bf16[16,128,2048]{2,1,0:T(8,128)(2,1)} %bitcast_dynamic-update-slice_fusion.2, s32[]{:T(128)S(6)} %select_n.142, bf16[128,2048]{1,0:T(8,128)(2,1)S(1)} %collective-permute-done.14), kind=kLoop, calls=%fused_computation.6 | loop fusion | bytes 1048580 | tf_op jit(solution)/shard_map/dynamic_update_slice | solution.py:146
  70.4 0.8 bitcast_dynamic-update-slice_fusion.14
  71.2 9.4 %add_convert_fusion = bf16[512,2048]{1,0:T(8,128)(2,1)} fusion(bf16[512,2048]{1,0:T(8,128)(2,1)S(1)} %copy-done.5, bf16[2048,2048]{1,0:T(8,128)(2,1)} %bitcast.35, bf16[512,1024]{1,0:T(8,128)(2,1)S(1)} %copy-done.2, bf16[512,1024]{1,0:T(8,128)(2,1)S(1)} %copy-done.1), kind=kOutput, calls=%fused_computation | convolution fusion | flops 4302307328 | bytes 14680064 | tf_op jit(solution)/shard_map/dot_general | solution.py:195
  (50 shorter events, 7.4 us)
Async XLA Ops:
  1.3 33.7 %collective-permute-start.8 = (bf16[128,2048]{1,0:T(8,128)(2,1)S(1)}, bf16[128,2048]{1,0:T(8,128)(2,1)S(1)}, u32[]{:S(2)}, u32[]{:S(2)}) collective-permute-start(bf16[128,2048]{1,0:T(8,128)(2,1)S(1)} %bitcast.60), channel_id=1, source_target_pairs={{0,1},{1,0},{2,3},{3,2},{4,5},{5,4},{6,7},{7,6},{8,9},{9,8},{10,11... | collective-permute-start | bytes 1572872 | tf_op jit(solution)/shard_map/ppermute | solution.py:144
  1.8 20.1 %collective-permute-start.2 = (bf16[128,2048]{1,0:T(8,128)(2,1)S(1)}, bf16[128,2048]{1,0:T(8,128)(2,1)S(1)}, u32[]{:S(2)}, u32[]{:S(2)}) collective-permute-start(bf16[128,2048]{1,0:T(8,128)(2,1)S(1)} %bitcast.61), channel_id=1, source_target_pairs={{0,4},{4,8},{8,12},{12,14},{14,10},{10,6},{6,2},{2,0},{1,5},{5,9},... | collective-permute-start | bytes 1572872 | tf_op jit(solution)/shard_map/ppermute | solution.py:158
  4.4 17.5 %collective-permute-start.3 = (bf16[128,2048]{1,0:T(8,128)(2,1)S(1)}, bf16[128,2048]{1,0:T(8,128)(2,1)S(1)}, u32[]{:S(2)}, u32[]{:S(2)}) collective-permute-start(bf16[128,2048]{1,0:T(8,128)(2,1)S(1)} %bitcast.62), channel_id=1, source_target_pairs={{4,0},{8,4},{12,8},{14,12},{10,14},{6,10},{2,6},{0,2},{5,1},{9,5},... | collective-permute-start | bytes 1572872 | tf_op jit(solution)/shard_map/ppermute | solution.py:159
  8.3 13.6 %collective-permute-start = (bf16[128,2048]{1,0:T(8,128)(2,1)S(1)}, bf16[128,2048]{1,0:T(8,128)(2,1)S(1)}, u32[]{:S(2)}, u32[]{:S(2)}) collective-permute-start(bf16[128,2048]{1,0:T(8,128)(2,1)S(1)} %multiply_convert_fusion), channel_id=1, source_target_pairs={{0,1},{1,2},{2,3},{3,4},{4,5},{5,6},{6,7},{7,8},{8,9},{9,10},{10,1... | collective-permute-start | bytes 1572872 | tf_op jit(solution)/shard_map/ppermute | solution.py:22
  11.3 10.6 %collective-permute-start.1 = (bf16[2,6144]{1,0:T(2,128)(2,1)S(1)}, bf16[2,6144]{1,0:T(2,128)(2,1)S(1)}, u32[]{:S(2)}, u32[]{:S(2)}) collective-permute-start(bf16[2,6144]{1,0:T(2,128)(2,1)S(1)} %slice.72), channel_id=1, source_target_pairs={{0,1},{1,2},{2,3},{3,4},{4,5},{5,6},{6,7},{7,8},{8,9},{9,10},{10,1... | collective-permute-start | bytes 73736 | tf_op jit(solution)/shard_map/ppermute | solution.py:22
  21.9 3.9 %copy-start.4 = (bf16[2,6144]{1,0:T(2,128)(2,1)}, bf16[2,6144]{1,0:T(2,128)(2,1)S(1)}, u32[]{:S(2)}) copy-start(bf16[2,6144]{1,0:T(2,128)(2,1)S(1)} %collective-permute-done.1) | copy-start | bytes 73732
  21.9 3.8 %copy-start = (bf16[128,2048]{1,0:T(8,128)(2,1)}, bf16[128,2048]{1,0:T(8,128)(2,1)S(1)}, u32[]{:S(2)}) copy-start(bf16[128,2048]{1,0:T(8,128)(2,1)S(1)} %collective-permute-done.halo_ref) | copy-start | bytes 1572868
  21.9 14.7 %collective-permute-start.4 = (bf16[128,2048]{1,0:T(8,128)(2,1)S(1)}, bf16[128,2048]{1,0:T(8,128)(2,1)}, u32[]{:S(2)}, u32[]{:S(2)}) collective-permute-start(bf16[128,2048]{1,0:T(8,128)(2,1)S(1)} %collective-permute-done.2), channel_id=1, source_target_pairs={{0,4},{4,8},{8,12},{12,14},{14,10},{10,6},{6,2},{2,0},{1,5},{5,9},... | collective-permute-start | bytes 1572872 | tf_op jit(solution)/shard_map/ppermute | solution.py:158
  25.8 11.4 %collective-permute-start.5 = (bf16[128,2048]{1,0:T(8,128)(2,1)S(1)}, bf16[128,2048]{1,0:T(8,128)(2,1)S(1)}, u32[]{:S(2)}, u32[]{:S(2)}) collective-permute-start(bf16[128,2048]{1,0:T(8,128)(2,1)S(1)} %collective-permute-done.3), channel_id=1, source_target_pairs={{4,0},{8,4},{12,8},{14,12},{10,14},{6,10},{2,6},{0,2},{5,1},{9,5},... | collective-permute-start | bytes 1572872 | tf_op jit(solution)/shard_map/ppermute | solution.py:159
  25.8 13.4 %copy-start.3 = (bf16[128,128]{1,0:T(8,128)(2,1)S(1)}, bf16[128,128]{1,0:T(8,128)(2,1)}, u32[]{:S(2)}) copy-start(bf16[128,128]{1,0:T(8,128)(2,1)} %param.9) | copy-start | bytes 98308
  34.5 14.3 %collective-permute-start.9 = (bf16[128,2048]{1,0:T(8,128)(2,1)S(1)}, bf16[128,2048]{1,0:T(8,128)(2,1)}, u32[]{:S(2)}, u32[]{:S(2)}) collective-permute-start(bf16[128,2048]{1,0:T(8,128)(2,1)S(1)} %collective-permute-done.2), channel_id=1, source_target_pairs={{0,1},{1,0},{2,3},{3,2},{4,5},{5,4},{6,7},{7,6},{8,9},{9,8},{10,11... | collective-permute-start | bytes 1572872 | tf_op jit(solution)/shard_map/ppermute | solution.py:144
  34.5 17.8 %collective-permute-start.10 = (bf16[128,2048]{1,0:T(8,128)(2,1)S(1)}, bf16[128,2048]{1,0:T(8,128)(2,1)}, u32[]{:S(2)}, u32[]{:S(2)}) collective-permute-start(bf16[128,2048]{1,0:T(8,128)(2,1)S(1)} %collective-permute-done.3), channel_id=1, source_target_pairs={{0,1},{1,0},{2,3},{3,2},{4,5},{5,4},{6,7},{7,6},{8,9},{9,8},{10,11... | collective-permute-start | bytes 1572872 | tf_op jit(solution)/shard_map/ppermute | solution.py:144
  37.1 18.9 %collective-permute-start.6 = (bf16[128,2048]{1,0:T(8,128)(2,1)}, bf16[128,2048]{1,0:T(8,128)(2,1)S(1)}, u32[]{:S(2)}, u32[]{:S(2)}) collective-permute-start(bf16[128,2048]{1,0:T(8,128)(2,1)} %collective-permute-done.4), channel_id=1, source_target_pairs={{0,4},{4,8},{8,12},{12,14},{14,10},{10,6},{6,2},{2,0},{1,5},{5,9},... | collective-permute-start | bytes 1572872 | tf_op jit(solution)/shard_map/ppermute | solution.py:158
  38.8 17.3 %collective-permute-start.7 = (bf16[128,2048]{1,0:T(8,128)(2,1)S(1)}, bf16[128,2048]{1,0:T(8,128)(2,1)S(1)}, u32[]{:S(2)}, u32[]{:S(2)}) collective-permute-start(bf16[128,2048]{1,0:T(8,128)(2,1)S(1)} %collective-permute-done.5), channel_id=1, source_target_pairs={{4,0},{8,4},{12,8},{14,12},{10,14},{6,10},{2,6},{0,2},{5,1},{9,5},... | collective-permute-start | bytes 1572872 | tf_op jit(solution)/shard_map/ppermute | solution.py:159
  48.7 22.5 %copy-start.1 = (bf16[512,1024]{1,0:T(8,128)(2,1)S(1)}, bf16[512,1024]{1,0:T(8,128)(2,1)}, u32[]{:S(2)}) copy-start(bf16[512,1024]{1,0:T(8,128)(2,1)} %shard_map.64) | copy-start | bytes 3145732
  48.7 22.5 %copy-start.2 = (bf16[512,1024]{1,0:T(8,128)(2,1)S(1)}, bf16[512,1024]{1,0:T(8,128)(2,1)}, u32[]{:S(2)}) copy-start(bf16[512,1024]{1,0:T(8,128)(2,1)} %shard_map.65) | copy-start | bytes 3145732
  48.7 22.5 %copy-start.5 = (bf16[512,2048]{1,0:T(8,128)(2,1)S(1)}, bf16[512,2048]{1,0:T(8,128)(2,1)}, u32[]{:S(2)}) copy-start(bf16[512,2048]{1,0:T(8,128)(2,1)} %param.6) | copy-start | bytes 6291460
  48.7 9.5 %collective-permute-start.11 = (bf16[128,2048]{1,0:T(8,128)(2,1)}, bf16[128,2048]{1,0:T(8,128)(2,1)S(1)}, u32[]{:S(2)}, u32[]{:S(2)}) collective-permute-start(bf16[128,2048]{1,0:T(8,128)(2,1)} %collective-permute-done.4), channel_id=1, source_target_pairs={{0,1},{1,0},{2,3},{3,2},{4,5},{5,4},{6,7},{7,6},{8,9},{9,8},{10,11... | collective-permute-start | bytes 1572872 | tf_op jit(solution)/shard_map/ppermute | solution.py:144
  48.8 11.6 %collective-permute-start.12 = (bf16[128,2048]{1,0:T(8,128)(2,1)S(1)}, bf16[128,2048]{1,0:T(8,128)(2,1)S(1)}, u32[]{:S(2)}, u32[]{:S(2)}) collective-permute-start(bf16[128,2048]{1,0:T(8,128)(2,1)S(1)} %collective-permute-done.5), channel_id=1, source_target_pairs={{0,1},{1,0},{2,3},{3,2},{4,5},{5,4},{6,7},{7,6},{8,9},{9,8},{10,11... | collective-permute-start | bytes 1572872 | tf_op jit(solution)/shard_map/ppermute | solution.py:144
  56.1 8.1 %collective-permute-start.15 = (bf16[128,1024]{1,0:T(8,128)(2,1)S(1)}, bf16[128,1024]{1,0:T(8,128)(2,1)S(1)}, u32[]{:S(2)}, u32[]{:S(2)}) collective-permute-start(bf16[128,1024]{1,0:T(8,128)(2,1)S(1)} %slice.73), channel_id=1, source_target_pairs={{0,4},{4,8},{8,12},{12,14},{14,10},{10,6},{6,2},{2,0},{1,5},{5,9},... | collective-permute-start | bytes 786440 | tf_op jit(solution)/shard_map/ppermute | solution.py:152
  57.8 7.8 %collective-permute-start.17 = (bf16[128,1024]{1,0:T(8,128)(2,1)S(1)}, bf16[128,1024]{1,0:T(8,128)(2,1)S(1)}, u32[]{:S(2)}, u32[]{:S(2)}) collective-permute-start(bf16[128,1024]{1,0:T(8,128)(2,1)S(1)} %slice.74), channel_id=1, source_target_pairs={{4,0},{8,4},{12,8},{14,12},{10,14},{6,10},{2,6},{0,2},{5,1},{9,5},... | collective-permute-start | bytes 786440 | tf_op jit(solution)/shard_map/ppermute | solution.py:153
  58.2 7.4 %collective-permute-start.13 = (bf16[128,2048]{1,0:T(8,128)(2,1)S(1)}, bf16[128,2048]{1,0:T(8,128)(2,1)S(1)}, u32[]{:S(2)}, u32[]{:S(2)}) collective-permute-start(bf16[128,2048]{1,0:T(8,128)(2,1)S(1)} %collective-permute-done.6), channel_id=1, source_target_pairs={{0,1},{1,0},{2,3},{3,2},{4,5},{5,4},{6,7},{7,6},{8,9},{9,8},{10,11... | collective-permute-start | bytes 1572872 | tf_op jit(solution)/shard_map/ppermute | solution.py:144
  58.2 9.1 %collective-permute-start.14 = (bf16[128,2048]{1,0:T(8,128)(2,1)S(1)}, bf16[128,2048]{1,0:T(8,128)(2,1)S(1)}, u32[]{:S(2)}, u32[]{:S(2)}) collective-permute-start(bf16[128,2048]{1,0:T(8,128)(2,1)S(1)} %collective-permute-done.7), channel_id=1, source_target_pairs={{0,1},{1,0},{2,3},{3,2},{4,5},{5,4},{6,7},{7,6},{8,9},{9,8},{10,11... | collective-permute-start | bytes 1572872 | tf_op jit(solution)/shard_map/ppermute | solution.py:144
  64.1 4.8 %collective-permute-start.16 = (bf16[128,1024]{1,0:T(8,128)(2,1)S(1)}, bf16[128,1024]{1,0:T(8,128)(2,1)S(1)}, u32[]{:S(2)}, u32[]{:S(2)}) collective-permute-start(bf16[128,1024]{1,0:T(8,128)(2,1)S(1)} %collective-permute-done.15), channel_id=1, source_target_pairs={{0,1},{1,0},{2,3},{3,2},{4,5},{5,4},{6,7},{7,6},{8,9},{9,8},{10,11... | collective-permute-start | bytes 786440 | tf_op jit(solution)/shard_map/ppermute | solution.py:144
  65.6 4.8 %collective-permute-start.18 = (bf16[128,1024]{1,0:T(8,128)(2,1)S(1)}, bf16[128,1024]{1,0:T(8,128)(2,1)S(1)}, u32[]{:S(2)}, u32[]{:S(2)}) collective-permute-start(bf16[128,1024]{1,0:T(8,128)(2,1)S(1)} %collective-permute-done.17), channel_id=1, source_target_pairs={{0,1},{1,0},{2,3},{3,2},{4,5},{5,4},{6,7},{7,6},{8,9},{9,8},{10,11... | collective-permute-start | bytes 786440 | tf_op jit(solution)/shard_map/ppermute | solution.py:144

commit v15 on v11

--- a/solution.py
+++ b/solution.py
@@ -80,17 +80,23 @@
         out_ref[BLOCK * b : BLOCK * (b + 1), :] = (gate * (acc + direct)).astype(out_ref.dtype)
 
 
-def hyena_gate(halo, edge, projected, short_filter, long_filter, conv_bias, part, parts):
-    groups, taps = long_filter.shape
+def gate_operands(edge, short_filter, long_filter):
+    taps = long_filter.shape[1]
+    channels = edge.shape[1]
+    fw = jnp.pad(long_filter[:, ::-1].astype(jnp.float32), ((0, 0), (1, 3 * BLOCK - 1 - taps)))
+    edges = edge.reshape(2, 3, channels).transpose(1, 0, 2)
+    filters = short_filter.reshape(3, 3, channels).transpose(1, 0, 2)
+    return fw, edges, filters
+
+
+def hyena_gate(halo, projected, fw, edges, filters, conv_bias, part, parts):
+    groups = fw.shape[0]
     row_count = projected.shape[0]
     channels = halo.shape[1]
     per_tile = LANES // (channels // groups)
     tiles = channels // LANES
     share = tiles // parts
     first = part * share
-    fw = jnp.pad(long_filter[:, ::-1].astype(jnp.float32), ((0, 0), (1, 3 * BLOCK - 1 - taps)))
-    edges = edge.reshape(2, 3, channels).transpose(1, 0, 2)
-    filters = short_filter.reshape(3, 3, channels).transpose(1, 0, 2)
     column = lambda k: pl.BlockSpec((row_count, LANES), lambda j: (0, first + j + k * tiles))
     return pl.pallas_call(
         _gate_kernel,
@@ -171,13 +177,14 @@
         short_mixed(tail[:2, k * channels : (k + 1) * channels], tail[2:, k * channels : (k + 1) * channels], short_filter[:, k * channels : (k + 1) * channels])
         for k in (1, 2)
     ]
-    halo = shifted(carried_of(*tail_mixed), 1)
-    edge = shifted(projected[row_count - 2 :], 1)
+    packed = jnp.concatenate([carried_of(*tail_mixed), projected[row_count - 2 :].reshape(-1, channels)], axis=0)
+    packed = shifted(packed, 1)
+    halo, edge = packed[:BLOCK], packed[BLOCK:]
     halo, edge, ahead, behind = lax.optimization_barrier((halo, edge, ahead, behind))
     if ring and steps >= 2:
         weight, ahead, behind = ring_step(2, weight, ahead, behind)
 
-    inputs = (halo, edge, projected, short_filter, long_filter, conv_bias)
+    inputs = (halo, projected) + gate_operands(edge, short_filter, long_filter) + (conv_bias,)
     first = hyena_gate(*inputs, 0, 2)
     if ring:
         first, ahead, behind, inputs = lax.optimization_barrier((first, ahead, behind, inputs))

time: 80.8 us -> 81.2 us (level)
  local copies, waits for them, and re-layouts: 26.3 us -> 27.4 us
    ppermute x3, starting transfers between devices: 9.91 us -> 12.1 us  [ring_step(): ahead = lax.ppermute(ahead, 'chip', forward)]
    ppermute x2 -> x1, starting transfers between devices: 3.42 us -> 2.11 us  [shifted(): return lax.ppermute(block, CTX, route)]
    dynamic_update_slice x18, local copies, waits for them, and re-layouts: 19.8 us -> 18.7 us  [place(): lax.dynamic_update_slice(weight, part, ((owner_chip * 2 + k) * width, row))]
    slice x1 -> x3, local copies, waits for them, and re-layouts: 0.92 us -> 1.76 us  [the longest x1 0.92 us: on_device(): projected[row_count - 2:].reshape(-1, channels)]
  transfers between devices with their start and end apart: 19 -> 18, of which waited for: 2 -> 2; matrix products, arithmetic and copies ran while one was open for 37% -> 38% of each run, Pallas kernels for 22% -> 22%
where the time goes in v15:
time: 81.2 us; the launch traced here: 80.2 us
  local copies, waits for them, and re-layouts  27.4 us (34%)
  starting transfers between devices  19.8 us (24%)
  Pallas kernels  17.3 us (21%)
  matrix products  9.18 us (11%)
  other arithmetic  3.73 us (5%)
  waiting for transfers between devices  2.79 us (3%)
    dynamic_update_slice x18, local copies, waits for them, and re-layouts, place(): lax.dynamic_update_slice(weight, part, ((owner_chip * 2 + k) * width, row))  18.7 us
    pallas_call x2, Pallas kernels, hyena_gate(): pl.pallas_call(_gate_kernel, grid=(share,), in_specs=[pl.BlockSpec((per_t...  17.3 us
    ppermute x3, starting transfers between devices, ring_step(): ahead = lax.ppermute(ahead, 'chip', forward)  12.1 us
    dot_general x1, matrix products, on_device(): lax.dot_general(gated, weight, (((1,), (1,)), ((), ())), preferred_elemen...  9.18 us
    broadcast_in_dim x1, local copies, waits for them, and re-layouts, on_device(): weight = jnp.zeros((chips * 2 * width, channels), out_weight.dtype)  4.32 us
    ppermute x9, starting transfers between devices, place(): other = lax.ppermute(piece, 'core', swap)  3.43 us
    convert_element_type x1, other arithmetic, carried_of(): return (second * carrier).astype(jnp.bfloat16)  2.9 us
    ppermute x1, starting transfers between devices, shifted(): return lax.ppermute(block, CTX, route)  2.11 us
  transfers between devices with their start and end apart: 18, of which 2 were waited for; matrix products, arithmetic and copies ran while one was open for 38% of the time, Pallas kernels for 22%

profile of v15, /device:TPU:0, one launch (start us, length us, event | category | flops | bytes accessed | tf_op | source)
XLA Modules:
  0.0 80.2 jit_solution(13845005828557038157)
XLA Ops:
  0.5 2.6 %collective-permute-start.1 = (bf16[128,2048]{0,1:T(8,128)(2,1)}, bf16[128,2048]{0,1:T(8,128)(2,1)S(1)}, u32[]{:S(2)}, u32[]{:S(2)}) collective-permute-start(bf16[128,2048]{0,1:T(8,128)(2,1)} %bitcast.20), channel_id=1, source_target_pairs={{0,4},{4,8},{8,12},{12,14},{14,10},{10,6},{6,2},{2,0},{1,5},{5,9},... | collective-permute-start | bytes 1572872 | tf_op jit(solution)/shard_map/ppermute | solution.py:164
  3.1 0.9 %slice.78 = bf16[2,6144]{1,0:T(2,128)(2,1)S(1)} slice(bf16[512,6144]{1,0:T(8,128)(2,1)} %carrier_ref.2), slice={[510:512], [0:6144]} | slice | bytes 49152 | tf_op jit(solution)/shard_map/slice | solution.py:180
  4.0 1.0 %fusion.4 = (f32[1,2048]{1,0:T(1,128)S(1)}, f32[1,2048]{1,0:T(1,128)S(1)}, f32[1,2048]{1,0:T(1,128)S(1)}, f32[1,2048]{1,0:T(1,128)S(1)}, f32[1,2048]{1,0:T(1,128)S(1)}, /*index=5*/f32[1,2048]{1,0:T(1,128)S(1)}) fusion(f32[3,6144]{1,0:T(4,128)} %param.8), kind=kLoop, calls=%fused_computation.27 | loop fusion | bytes 98304 | tf_op jit(solution)/shard_map/slice | solution.py:34
  5.0 2.9 %multiply_convert_fusion = bf16[128,2048]{1,0:T(8,128)(2,1)S(1)} fusion(bf16[512,6144]{1,0:T(8,128)(2,1)} %carrier_ref.2, f32[2048]{0:T(1024)S(1)} %bitcast.30, f32[2048]{0:T(1024)S(1)} %bitcast.31, f32[2048]{0:T(1024)S(1)} %bitcast.27, f32[2048]{0:T(1024)S(1)} %bitcast.28, f32[2048]{0:T(1024)S(1)} %bitcast.29, f32[2048]{0:T(1024)S(1)} %bitcast.26), kind=kLoop, calls=%fused_computation.4 | loop fusion | flops 4718592 | bytes 3719168 | tf_op jit(solution)/shard_map/convert_element_type | solution.py:128
  8.0 2.1 %collective-permute-start = (bf16[134,2048]{1,0:T(8,128)(2,1)S(1)}, bf16[134,2048]{1,0:T(8,128)(2,1)S(1)}, u32[]{:S(2)}, u32[]{:S(2)}) collective-permute-start(bf16[134,2048]{1,0:T(8,128)(2,1)S(1)} %pad_maximum_fusion), channel_id=1, source_target_pairs={{0,1},{1,2},{2,3},{3,4},{4,5},{5,6},{6,7},{7,8},{8,9},{9,10},{10,1... | collective-permute-start | bytes 1646600 | tf_op jit(solution)/shard_map/ppermute | solution.py:22
  10.1 0.8 %rev.3 = bf16[128,128]{1,0:T(8,128)(2,1)S(1)} reverse(bf16[128,128]{1,0:T(8,128)(2,1)} %param.9), dimensions={1} | reverse | bytes 65536 | tf_op jit(solution)/shard_map/rev | solution.py:86
  10.9 4.3 %broadcast_in_dim.3 = bf16[2048,2048]{0,1:T(8,128)(2,1)} broadcast(bf16[]{:T(256)} %constant.75.clone.1), dimensions={} | broadcast | bytes 8388610 | tf_op jit(solution)/shard_map/broadcast_in_dim | solution.py:147
  15.3 0.9 %constant_dynamic-update-slice_fusion.15 = bf16[2048,2048]{0,1:T(8,128)(2,1)} fusion(bf16[2048,2048]{0,1:T(8,128)(2,1)} %broadcast_in_dim.3, s32[]{:T(128)S(6)} %select_n.114, bf16[2048,128]{1,0:T(8,128)(2,1)S(1)} %copy-done.2), kind=kLoop, calls=%fused_computation.23 | loop fusion | bytes 1048580 | tf_op jit(solution)/shard_map/dynamic_update_slice | solution.py:152
  16.1 1.9 %collective-permute-start.8 = (bf16[128,2048]{0,1:T(8,128)(2,1)S(1)}, bf16[128,2048]{0,1:T(8,128)(2,1)S(1)}, u32[]{:S(2)}, u32[]{:S(2)}) collective-permute-start(bf16[128,2048]{0,1:T(8,128)(2,1)S(1)} %collective-permute-done.1), channel_id=1, source_target_pairs={{0,1},{1,0},{2,3},{3,2},{4,5},{5,4},{6,7},{7,6},{8,9},{9,8},{10,11... | collective-permute-start | bytes 1572872 | tf_op jit(solution)/shard_map/ppermute | solution.py:150
  18.0 0.8 pad_convert_fusion.fw_ref
  18.8 0.8 %slice.83.halo_ref = bf16[128,2048]{1,0:T(8,128)(2,1)} slice(bf16[134,2048]{1,0:T(8,128)(2,1)S(1)} %collective-permute-done), slice={[0:128], [0:2048]} | slice | bytes 1048576 | tf_op jit(solution)/shard_map/slice | solution.py:182
  19.7 5.8 %collective-permute-start.3 = (bf16[128,2048]{0,1:T(8,128)(2,1)S(1)}, bf16[128,2048]{0,1:T(8,128)(2,1)}, u32[]{:S(2)}, u32[]{:S(2)}) collective-permute-start(bf16[128,2048]{0,1:T(8,128)(2,1)S(1)} %collective-permute-done.1), channel_id=1, source_target_pairs={{0,4},{4,8},{8,12},{12,14},{14,10},{10,6},{6,2},{2,0},{1,5},{5,9},... | collective-permute-start | bytes 1572872 | tf_op jit(solution)/shard_map/ppermute | solution.py:164
  25.5 0.9 %constant_dynamic-update-slice_fusion.14 = bf16[2048,2048]{0,1:T(8,128)(2,1)} fusion(bf16[2048,2048]{0,1:T(8,128)(2,1)} %constant_dynamic-update-slice_fusion.15, bf16[128,2048]{0,1:T(8,128)(2,1)S(1)} %collective-permute-done.7, s32[]{:T(128)S(6)} %select_n.115), kind=kLoop, calls=%fused_computation.22 | loop fusion | bytes 1048580 | tf_op jit(solution)/shard_map/dynamic_update_slice | solution.py:152
  26.4 0.9 %constant_dynamic-update-slice_fusion.13 = bf16[2048,2048]{0,1:T(8,128)(2,1)} fusion(bf16[2048,2048]{0,1:T(8,128)(2,1)} %constant_dynamic-update-slice_fusion.14, bf16[128,2048]{0,1:T(8,128)(2,1)S(1)} %collective-permute-done.1, s32[]{:T(128)S(6)} %select_n.121), kind=kLoop, calls=%fused_computation.21 | loop fusion | bytes 1048580 | tf_op jit(solution)/shard_map/dynamic_update_slice | solution.py:152
  28.0 8.6 %shard_map.64 = bf16[512,1024]{1,0:T(8,128)(2,1)} custom-call(f32[128,384]{1,0:T(8,128)} %pad_convert_fusion.fw_ref, f32[1,2048]{1,0:T(1,128)} %bitcast.24, f32[3,3,2048]{2,1,0:T(4,128)} %bitcast.17, bf16[3,2,2048]{2,1,0:T(2,128)(2,1)} %bitcast.22, bf16[128,2048]{1,0:T(8,128)(2,1)} %slice.83.halo_ref, bf16[512,6144]{1,0:T(8,128)(2,1)} %carrier_ref.2, ...), custom_call_target="tpu_custom_call" | custom-call | tf_op jit(solution)/shard_map/pallas_call | solution.py:101
  36.7 0.9 %constant_dynamic-update-slice_fusion.12 = bf16[2048,2048]{0,1:T(8,128)(2,1)} fusion(bf16[2048,2048]{0,1:T(8,128)(2,1)} %constant_dynamic-update-slice_fusion.13, bf16[128,2048]{0,1:T(8,128)(2,1)S(1)} %collective-permute-done.8, s32[]{:T(128)S(6)} %select_n.122), kind=kLoop, calls=%fused_computation.20 | loop fusion | bytes 1048580 | tf_op jit(solution)/shard_map/dynamic_update_slice | solution.py:152
  37.6 3.6 %collective-permute-start.5 = (bf16[128,2048]{0,1:T(8,128)(2,1)}, bf16[128,2048]{0,1:T(8,128)(2,1)S(1)}, u32[]{:S(2)}, u32[]{:S(2)}) collective-permute-start(bf16[128,2048]{0,1:T(8,128)(2,1)} %collective-permute-done.3), channel_id=1, source_target_pairs={{0,4},{4,8},{8,12},{12,14},{14,10},{10,6},{6,2},{2,0},{1,5},{5,9},... | collective-permute-start | bytes 1572872 | tf_op jit(solution)/shard_map/ppermute | solution.py:164
  41.2 0.9 %constant_dynamic-update-slice_fusion.11 = bf16[2048,2048]{0,1:T(8,128)(2,1)} fusion(bf16[2048,2048]{0,1:T(8,128)(2,1)} %constant_dynamic-update-slice_fusion.12, bf16[128,2048]{0,1:T(8,128)(2,1)S(1)} %collective-permute-done.2, s32[]{:T(128)S(6)} %select_n.125), kind=kLoop, calls=%fused_computation.19 | loop fusion | bytes 1048580 | tf_op jit(solution)/shard_map/dynamic_update_slice | solution.py:152
  42.1 2.0 %constant_dynamic-update-slice_fusion.10 = bf16[2048,2048]{0,1:T(8,128)(2,1)} fusion(bf16[2048,2048]{0,1:T(8,128)(2,1)} %constant_dynamic-update-slice_fusion.11, bf16[128,2048]{0,1:T(8,128)(2,1)} %collective-permute-done.9, s32[]{:T(128)S(6)} %select_n.126), kind=kLoop, calls=%fused_computation.18 | loop fusion | bytes 1048580 | tf_op jit(solution)/shard_map/dynamic_update_slice | solution.py:152
  44.6 1.9 %constant_dynamic-update-slice_fusion.9 = bf16[2048,2048]{0,1:T(8,128)(2,1)} fusion(bf16[2048,2048]{0,1:T(8,128)(2,1)} %constant_dynamic-update-slice_fusion.10, bf16[128,2048]{0,1:T(8,128)(2,1)} %collective-permute-done.3, s32[]{:T(128)S(6)} %select_n.129), kind=kLoop, calls=%fused_computation.17 | loop fusion | bytes 1048580 | tf_op jit(solution)/shard_map/dynamic_update_slice | solution.py:152
  46.5 8.6 %shard_map.65 = bf16[512,1024]{1,0:T(8,128)(2,1)} custom-call(f32[128,384]{1,0:T(8,128)} %pad_convert_fusion.fw_ref, f32[1,2048]{1,0:T(1,128)} %bitcast.25, f32[3,3,2048]{2,1,0:T(4,128)} %bitcast.18, bf16[3,2,2048]{2,1,0:T(2,128)(2,1)} %bitcast.23, bf16[128,2048]{1,0:T(8,128)(2,1)} %slice.83.halo_ref, bf16[512,6144]{1,0:T(8,128)(2,1)} %carrier_ref.2, ...), custom_call_target="tpu_custom_call" | custom-call | tf_op jit(solution)/shard_map/pallas_call | solution.py:101
  55.3 2.1 %collective-permute-start.14 = (bf16[128,1024]{0,1:T(8,128)(2,1)S(1)}, bf16[128,1024]{0,1:T(8,128)(2,1)S(1)}, u32[]{:S(2)}, u32[]{:S(2)}) collective-permute-start(bf16[128,1024]{0,1:T(8,128)(2,1)S(1)} %slice.81), channel_id=1, source_target_pairs={{0,4},{4,8},{8,12},{12,14},{14,10},{10,6},{6,2},{2,0},{1,5},{5,9},... | collective-permute-start | bytes 786440 | tf_op jit(solution)/shard_map/ppermute | solution.py:158
  58.0 0.9 %constant_dynamic-update-slice_fusion.8 = bf16[2048,2048]{0,1:T(8,128)(2,1)} fusion(bf16[2048,2048]{0,1:T(8,128)(2,1)} %constant_dynamic-update-slice_fusion.9, bf16[128,2048]{0,1:T(8,128)(2,1)S(1)} %collective-permute-done.10, s32[]{:T(128)S(6)} %select_n.130), kind=kLoop, calls=%fused_computation.16 | loop fusion | bytes 1048580 | tf_op jit(solution)/shard_map/dynamic_update_slice | solution.py:152
  58.9 1.9 %constant_dynamic-update-slice_fusion.7 = bf16[2048,2048]{0,1:T(8,128)(2,1)} fusion(bf16[2048,2048]{0,1:T(8,128)(2,1)} %constant_dynamic-update-slice_fusion.8, bf16[128,2048]{0,1:T(8,128)(2,1)} %collective-permute-done.4, s32[]{:T(128)S(6)} %select_n.133), kind=kLoop, calls=%fused_computation.15 | loop fusion | bytes 1048580 | tf_op jit(solution)/shard_map/dynamic_update_slice | solution.py:152
  60.8 0.9 %constant_dynamic-update-slice_fusion.6 = bf16[2048,2048]{0,1:T(8,128)(2,1)} fusion(bf16[2048,2048]{0,1:T(8,128)(2,1)} %constant_dynamic-update-slice_fusion.7, bf16[128,2048]{0,1:T(8,128)(2,1)S(1)} %collective-permute-done.11, s32[]{:T(128)S(6)} %select_n.134), kind=kLoop, calls=%fused_computation.14 | loop fusion | bytes 1048580 | tf_op jit(solution)/shard_map/dynamic_update_slice | solution.py:152
  61.7 0.9 %constant_dynamic-update-slice_fusion.5 = bf16[2048,2048]{0,1:T(8,128)(2,1)} fusion(bf16[2048,2048]{0,1:T(8,128)(2,1)} %constant_dynamic-update-slice_fusion.6, bf16[128,2048]{0,1:T(8,128)(2,1)S(1)} %collective-permute-done.5, s32[]{:T(128)S(6)} %select_n.137), kind=kLoop, calls=%fused_computation.13 | loop fusion | bytes 1048580 | tf_op jit(solution)/shard_map/dynamic_update_slice | solution.py:152
  62.6 0.9 %collective-permute-done.14 = bf16[128,1024]{0,1:T(8,128)(2,1)S(1)} collective-permute-done((bf16[128,1024]{0,1:T(8,128)(2,1)S(1)}, bf16[128,1024]{0,1:T(8,128)(2,1)S(1)}, u32[]{:S(2)}, u32[]{:S(2)}) %collective-permute-start.14) | collective-permute-done | bytes 262176 | tf_op jit(solution)/shard_map/ppermute | solution.py:158
  63.5 1.9 %collective-permute-done.16 = bf16[128,1024]{0,1:T(8,128)(2,1)S(1)} collective-permute-done((bf16[128,1024]{0,1:T(8,128)(2,1)S(1)}, bf16[128,1024]{0,1:T(8,128)(2,1)S(1)}, u32[]{:S(2)}, u32[]{:S(2)}) %collective-permute-start.16) | collective-permute-done | bytes 262176 | tf_op jit(solution)/shard_map/ppermute | solution.py:159
  65.4 0.9 %constant_dynamic-update-slice_fusion.4 = bf16[2048,2048]{0,1:T(8,128)(2,1)} fusion(bf16[2048,2048]{0,1:T(8,128)(2,1)} %constant_dynamic-update-slice_fusion.5, bf16[128,2048]{0,1:T(8,128)(2,1)S(1)} %collective-permute-done.12, s32[]{:T(128)S(6)} %select_n.138), kind=kLoop, calls=%fused_computation.12 | loop fusion | bytes 1048580 | tf_op jit(solution)/shard_map/dynamic_update_slice | solution.py:152
  66.3 0.9 %constant_dynamic-update-slice_fusion.3 = bf16[2048,2048]{0,1:T(8,128)(2,1)} fusion(bf16[2048,2048]{0,1:T(8,128)(2,1)} %constant_dynamic-update-slice_fusion.4, bf16[128,2048]{0,1:T(8,128)(2,1)S(1)} %collective-permute-done.6, s32[]{:T(128)S(6)} %select_n.141), kind=kLoop, calls=%fused_computation.11 | loop fusion | bytes 1048580 | tf_op jit(solution)/shard_map/dynamic_update_slice | solution.py:152
  67.1 0.9 %constant_dynamic-update-slice_fusion.2 = bf16[2048,2048]{0,1:T(8,128)(2,1)} fusion(bf16[2048,2048]{0,1:T(8,128)(2,1)} %constant_dynamic-update-slice_fusion.3, bf16[128,2048]{0,1:T(8,128)(2,1)S(1)} %collective-permute-done.13, s32[]{:T(128)S(6)} %select_n.142), kind=kLoop, calls=%fused_computation.10 | loop fusion | bytes 1048580 | tf_op jit(solution)/shard_map/dynamic_update_slice | solution.py:152
  71.1 9.2 %add_convert_fusion = bf16[512,2048]{1,0:T(8,128)(2,1)} fusion(bf16[512,2048]{1,0:T(8,128)(2,1)S(1)} %copy-done.3, bf16[2048,2048]{0,1:T(8,128)(2,1)} %constant_dynamic-update-slice_fusion.16, bf16[512,1024]{1,0:T(8,128)(2,1)S(1)} %copy-done.1, bf16[512,1024]{1,0:T(8,128)(2,1)S(1)} %copy-done), kind=kOutput, calls=%fused_computation | convolution fusion | flops 4302307328 | bytes 14680064 | tf_op jit(solution)/shard_map/dot_general | solution.py:201
  (47 shorter events, 5.5 us)
Async XLA Ops:
  0.0 15.3 %copy-start.2 = (bf16[2048,128]{1,0:T(8,128)(2,1)S(1)}, bf16[2048,128]{1,0:T(8,128)(2,1)}, u32[]{:S(2)}) copy-start(bf16[2048,128]{1,0:T(8,128)(2,1)} %param.11) | copy-start | bytes 1572868
  0.0 25.5 %collective-permute-start.7 = (bf16[128,2048]{0,1:T(8,128)(2,1)}, bf16[128,2048]{0,1:T(8,128)(2,1)S(1)}, u32[]{:S(2)}, u32[]{:S(2)}) collective-permute-start(bf16[128,2048]{0,1:T(8,128)(2,1)} %bitcast.19), channel_id=1, source_target_pairs={{0,1},{1,0},{2,3},{3,2},{4,5},{5,4},{6,7},{7,6},{8,9},{9,8},{10,11... | collective-permute-start | bytes 1572872 | tf_op jit(solution)/shard_map/ppermute | solution.py:150
  0.5 15.7 %collective-permute-start.1 = (bf16[128,2048]{0,1:T(8,128)(2,1)}, bf16[128,2048]{0,1:T(8,128)(2,1)S(1)}, u32[]{:S(2)}, u32[]{:S(2)}) collective-permute-start(bf16[128,2048]{0,1:T(8,128)(2,1)} %bitcast.20), channel_id=1, source_target_pairs={{0,4},{4,8},{8,12},{12,14},{14,10},{10,6},{6,2},{2,0},{1,5},{5,9},... | collective-permute-start | bytes 1572872 | tf_op jit(solution)/shard_map/ppermute | solution.py:164
  3.1 15.7 %collective-permute-start.2 = (bf16[128,2048]{0,1:T(8,128)(2,1)}, bf16[128,2048]{0,1:T(8,128)(2,1)S(1)}, u32[]{:S(2)}, u32[]{:S(2)}) collective-permute-start(bf16[128,2048]{0,1:T(8,128)(2,1)} %bitcast.21), channel_id=1, source_target_pairs={{4,0},{8,4},{12,8},{14,12},{10,14},{6,10},{2,6},{0,2},{5,1},{9,5},... | collective-permute-start | bytes 1572872 | tf_op jit(solution)/shard_map/ppermute | solution.py:165
  8.0 10.9 %collective-permute-start = (bf16[134,2048]{1,0:T(8,128)(2,1)S(1)}, bf16[134,2048]{1,0:T(8,128)(2,1)S(1)}, u32[]{:S(2)}, u32[]{:S(2)}) collective-permute-start(bf16[134,2048]{1,0:T(8,128)(2,1)S(1)} %pad_maximum_fusion), channel_id=1, source_target_pairs={{0,1},{1,2},{2,3},{3,4},{4,5},{5,6},{6,7},{7,8},{8,9},{9,10},{10,1... | collective-permute-start | bytes 1646600 | tf_op jit(solution)/shard_map/ppermute | solution.py:22
  16.1 20.5 %collective-permute-start.8 = (bf16[128,2048]{0,1:T(8,128)(2,1)S(1)}, bf16[128,2048]{0,1:T(8,128)(2,1)S(1)}, u32[]{:S(2)}, u32[]{:S(2)}) collective-permute-start(bf16[128,2048]{0,1:T(8,128)(2,1)S(1)} %collective-permute-done.1), channel_id=1, source_target_pairs={{0,1},{1,0},{2,3},{3,2},{4,5},{5,4},{6,7},{7,6},{8,9},{9,8},{10,11... | collective-permute-start | bytes 1572872 | tf_op jit(solution)/shard_map/ppermute | solution.py:150
  18.8 23.3 %collective-permute-start.9 = (bf16[128,2048]{0,1:T(8,128)(2,1)S(1)}, bf16[128,2048]{0,1:T(8,128)(2,1)}, u32[]{:S(2)}, u32[]{:S(2)}) collective-permute-start(bf16[128,2048]{0,1:T(8,128)(2,1)S(1)} %collective-permute-done.2), channel_id=1, source_target_pairs={{0,1},{1,0},{2,3},{3,2},{4,5},{5,4},{6,7},{7,6},{8,9},{9,8},{10,11... | collective-permute-start | bytes 1572872 | tf_op jit(solution)/shard_map/ppermute | solution.py:150
  19.7 17.9 %collective-permute-start.3 = (bf16[128,2048]{0,1:T(8,128)(2,1)S(1)}, bf16[128,2048]{0,1:T(8,128)(2,1)}, u32[]{:S(2)}, u32[]{:S(2)}) collective-permute-start(bf16[128,2048]{0,1:T(8,128)(2,1)S(1)} %collective-permute-done.1), channel_id=1, source_target_pairs={{0,4},{4,8},{8,12},{12,14},{14,10},{10,6},{6,2},{2,0},{1,5},{5,9},... | collective-permute-start | bytes 1572872 | tf_op jit(solution)/shard_map/ppermute | solution.py:164
  25.5 12.1 %collective-permute-start.4 = (bf16[128,2048]{0,1:T(8,128)(2,1)S(1)}, bf16[128,2048]{0,1:T(8,128)(2,1)}, u32[]{:S(2)}, u32[]{:S(2)}) collective-permute-start(bf16[128,2048]{0,1:T(8,128)(2,1)S(1)} %collective-permute-done.2), channel_id=1, source_target_pairs={{4,0},{8,4},{12,8},{14,12},{10,14},{6,10},{2,6},{0,2},{5,1},{9,5},... | collective-permute-start | bytes 1572872 | tf_op jit(solution)/shard_map/ppermute | solution.py:165
  37.6 17.6 %collective-permute-start.5 = (bf16[128,2048]{0,1:T(8,128)(2,1)}, bf16[128,2048]{0,1:T(8,128)(2,1)S(1)}, u32[]{:S(2)}, u32[]{:S(2)}) collective-permute-start(bf16[128,2048]{0,1:T(8,128)(2,1)} %collective-permute-done.3), channel_id=1, source_target_pairs={{0,4},{4,8},{8,12},{12,14},{14,10},{10,6},{6,2},{2,0},{1,5},{5,9},... | collective-permute-start | bytes 1572872 | tf_op jit(solution)/shard_map/ppermute | solution.py:164
  41.2 14.0 %collective-permute-start.6 = (bf16[128,2048]{0,1:T(8,128)(2,1)}, bf16[128,2048]{0,1:T(8,128)(2,1)S(1)}, u32[]{:S(2)}, u32[]{:S(2)}) collective-permute-start(bf16[128,2048]{0,1:T(8,128)(2,1)} %collective-permute-done.4), channel_id=1, source_target_pairs={{4,0},{8,4},{12,8},{14,12},{10,14},{6,10},{2,6},{0,2},{5,1},{9,5},... | collective-permute-start | bytes 1572872 | tf_op jit(solution)/shard_map/ppermute | solution.py:165
  41.2 16.3 %collective-permute-start.10 = (bf16[128,2048]{0,1:T(8,128)(2,1)}, bf16[128,2048]{0,1:T(8,128)(2,1)S(1)}, u32[]{:S(2)}, u32[]{:S(2)}) collective-permute-start(bf16[128,2048]{0,1:T(8,128)(2,1)} %collective-permute-done.3), channel_id=1, source_target_pairs={{0,1},{1,0},{2,3},{3,2},{4,5},{5,4},{6,7},{7,6},{8,9},{9,8},{10,11... | collective-permute-start | bytes 1572872 | tf_op jit(solution)/shard_map/ppermute | solution.py:150
  44.1 16.7 %collective-permute-start.11 = (bf16[128,2048]{0,1:T(8,128)(2,1)}, bf16[128,2048]{0,1:T(8,128)(2,1)S(1)}, u32[]{:S(2)}, u32[]{:S(2)}) collective-permute-start(bf16[128,2048]{0,1:T(8,128)(2,1)} %collective-permute-done.4), channel_id=1, source_target_pairs={{0,1},{1,0},{2,3},{3,2},{4,5},{5,4},{6,7},{7,6},{8,9},{9,8},{10,11... | collective-permute-start | bytes 1572872 | tf_op jit(solution)/shard_map/ppermute | solution.py:150
  55.2 15.9 %copy-start = (bf16[512,1024]{1,0:T(8,128)(2,1)S(1)}, bf16[512,1024]{1,0:T(8,128)(2,1)}, u32[]{:S(2)}) copy-start(bf16[512,1024]{1,0:T(8,128)(2,1)} %shard_map.64) | copy-start | bytes 3145732
  55.2 15.9 %copy-start.1 = (bf16[512,1024]{1,0:T(8,128)(2,1)S(1)}, bf16[512,1024]{1,0:T(8,128)(2,1)}, u32[]{:S(2)}) copy-start(bf16[512,1024]{1,0:T(8,128)(2,1)} %shard_map.65) | copy-start | bytes 3145732
  55.2 15.9 %copy-start.3 = (bf16[512,2048]{1,0:T(8,128)(2,1)S(1)}, bf16[512,2048]{1,0:T(8,128)(2,1)}, u32[]{:S(2)}) copy-start(bf16[512,2048]{1,0:T(8,128)(2,1)} %param.6) | copy-start | bytes 6291460
  55.3 8.2 %collective-permute-start.14 = (bf16[128,1024]{0,1:T(8,128)(2,1)S(1)}, bf16[128,1024]{0,1:T(8,128)(2,1)S(1)}, u32[]{:S(2)}, u32[]{:S(2)}) collective-permute-start(bf16[128,1024]{0,1:T(8,128)(2,1)S(1)} %slice.81), channel_id=1, source_target_pairs={{0,4},{4,8},{8,12},{12,14},{14,10},{10,6},{6,2},{2,0},{1,5},{5,9},... | collective-permute-start | bytes 786440 | tf_op jit(solution)/shard_map/ppermute | solution.py:158
  57.4 8.0 %collective-permute-start.16 = (bf16[128,1024]{0,1:T(8,128)(2,1)S(1)}, bf16[128,1024]{0,1:T(8,128)(2,1)S(1)}, u32[]{:S(2)}, u32[]{:S(2)}) collective-permute-start(bf16[128,1024]{0,1:T(8,128)(2,1)S(1)} %slice.82), channel_id=1, source_target_pairs={{4,0},{8,4},{12,8},{14,12},{10,14},{6,10},{2,6},{0,2},{5,1},{9,5},... | collective-permute-start | bytes 786440 | tf_op jit(solution)/shard_map/ppermute | solution.py:159
  57.4 7.9 %collective-permute-start.12 = (bf16[128,2048]{0,1:T(8,128)(2,1)S(1)}, bf16[128,2048]{0,1:T(8,128)(2,1)S(1)}, u32[]{:S(2)}, u32[]{:S(2)}) collective-permute-start(bf16[128,2048]{0,1:T(8,128)(2,1)S(1)} %collective-permute-done.5), channel_id=1, source_target_pairs={{0,1},{1,0},{2,3},{3,2},{4,5},{5,4},{6,7},{7,6},{8,9},{9,8},{10,11... | collective-permute-start | bytes 1572872 | tf_op jit(solution)/shard_map/ppermute | solution.py:150
  57.5 9.6 %collective-permute-start.13 = (bf16[128,2048]{0,1:T(8,128)(2,1)S(1)}, bf16[128,2048]{0,1:T(8,128)(2,1)S(1)}, u32[]{:S(2)}, u32[]{:S(2)}) collective-permute-start(bf16[128,2048]{0,1:T(8,128)(2,1)S(1)} %collective-permute-done.6), channel_id=1, source_target_pairs={{0,1},{1,0},{2,3},{3,2},{4,5},{5,4},{6,7},{7,6},{8,9},{9,8},{10,11... | collective-permute-start | bytes 1572872 | tf_op jit(solution)/shard_map/ppermute | solution.py:150
  63.5 5.3 %collective-permute-start.15 = (bf16[128,1024]{0,1:T(8,128)(2,1)S(1)}, bf16[128,1024]{0,1:T(8,128)(2,1)S(1)}, u32[]{:S(2)}, u32[]{:S(2)}) collective-permute-start(bf16[128,1024]{0,1:T(8,128)(2,1)S(1)} %collective-permute-done.14), channel_id=1, source_target_pairs={{0,1},{1,0},{2,3},{3,2},{4,5},{5,4},{6,7},{7,6},{8,9},{9,8},{10,11... | collective-permute-start | bytes 786440 | tf_op jit(solution)/shard_map/ppermute | solution.py:150
  65.4 4.9 %collective-permute-start.17 = (bf16[128,1024]{0,1:T(8,128)(2,1)S(1)}, bf16[128,1024]{0,1:T(8,128)(2,1)S(1)}, u32[]{:S(2)}, u32[]{:S(2)}) collective-permute-start(bf16[128,1024]{0,1:T(8,128)(2,1)S(1)} %collective-permute-done.16), channel_id=1, source_target_pairs={{0,1},{1,0},{2,3},{3,2},{4,5},{5,4},{6,7},{7,6},{8,9},{9,8},{10,11... | collective-permute-start | bytes 786440 | tf_op jit(solution)/shard_map/ppermute | solution.py:150

commit v16 on v15

--- a/solution.py
+++ b/solution.py
@@ -185,19 +185,20 @@
         weight, ahead, behind = ring_step(2, weight, ahead, behind)
 
     inputs = (halo, projected) + gate_operands(edge, short_filter, long_filter) + (conv_bias,)
-    first = hyena_gate(*inputs, 0, 2)
+    pieces = [hyena_gate(*inputs, 0, 4), hyena_gate(*inputs, 1, 4)]
     if ring:
-        first, ahead, behind, inputs = lax.optimization_barrier((first, ahead, behind, inputs))
+        pieces, ahead, behind, inputs = lax.optimization_barrier((pieces, ahead, behind, inputs))
         if steps >= 3:
             weight, ahead, behind = ring_step(3, weight, ahead, behind)
-    second = hyena_gate(*inputs, 1, 2)
+    pieces.append(hyena_gate(*inputs, 2, 4))
     if ring:
-        second, ahead, behind = lax.optimization_barrier((second, ahead, behind))
+        pieces, ahead, behind, inputs = lax.optimization_barrier((pieces, ahead, behind, inputs))
         for step in range(4, steps + 1):
             weight, ahead, behind = ring_step(step, weight, ahead, behind)
-    else:
+    pieces.append(hyena_gate(*inputs, 3, 4))
+    if not ring:
         weight = lax.all_gather(out_weight.T, CTX, axis=0, tiled=True)
-    gated = jnp.concatenate([first, second], axis=1)
+    gated = jnp.concatenate(pieces, axis=1)
     branch = lax.dot_general(gated, weight, (((1,), (1,)), ((), ())), preferred_element_type=jnp.float32)
     return (tokens.astype(jnp.float32) + branch).astype(jnp.bfloat16)
 

time: 81.2 us -> 87 us (1.071)
  Pallas kernels: 17.3 us -> 20.1 us
  local copies, waits for them, and re-layouts: 27.4 us -> 29.7 us
  waiting for transfers between devices: 2.79 us -> 3.9 us
  starting transfers between devices: 19.8 us -> 18.7 us
    pallas_call x2 -> x4, Pallas kernels: 17.3 us -> 20.1 us  [hyena_gate(): pl.pallas_call(_gate_kernel, grid=(share,), in_specs=[pl.BlockSpec((per_t...]
    ppermute x3, waiting for transfers between devices: 0.01 us -> 2.46 us  [ring_step(): behind = lax.ppermute(behind, 'chip', backward)]
    ppermute x1, waiting for transfers between devices: 1.86 us -> 0.01 us  [ring_step(): behind = lax.ppermute(behind[:, half:], 'chip', backward)]
    ppermute x3, starting transfers between devices: 12.1 us -> 10.6 us  [ring_step(): ahead = lax.ppermute(ahead, 'chip', forward)]
    ppermute x3, waiting for transfers between devices: 0.01 us -> 1.42 us  [ring_step(): ahead = lax.ppermute(ahead, 'chip', forward)]
    dynamic_update_slice x18, local copies, waits for them, and re-layouts: 18.7 us -> 19.7 us  [place(): lax.dynamic_update_slice(weight, part, ((owner_chip * 2 + k) * width, row))]
    ppermute x1, waiting for transfers between devices: 0.89 us -> 0.01 us  [ring_step(): ahead = lax.ppermute(ahead[:, :half], 'chip', forward)]
  transfers between devices with their start and end apart: 18 -> 18, of which waited for: 2 -> 2; matrix products, arithmetic and copies ran while one was open for 38% -> 38% of each run, Pallas kernels for 22% -> 23%
where the time goes in v16:
time: 87 us; the launch traced here: 86.2 us
  local copies, waits for them, and re-layouts  29.7 us (34%)
  Pallas kernels  20.1 us (23%)
  starting transfers between devices  18.7 us (21%)
  matrix products  9.94 us (11%)
  waiting for transfers between devices  3.9 us (4%)
  other arithmetic  3.73 us (4%)
    pallas_call x4, Pallas kernels, hyena_gate(): pl.pallas_call(_gate_kernel, grid=(share,), in_specs=[pl.BlockSpec((per_t...  20.1 us
    dynamic_update_slice x18, local copies, waits for them, and re-layouts, place(): lax.dynamic_update_slice(weight, part, ((owner_chip * 2 + k) * width, row))  19.7 us
    ppermute x3, starting transfers between devices, ring_step(): ahead = lax.ppermute(ahead, 'chip', forward)  10.6 us
    dot_general x1, matrix products, on_device(): lax.dot_general(gated, weight, (((1,), (1,)), ((), ())), preferred_elemen...  9.94 us
    broadcast_in_dim x1, local copies, waits for them, and re-layouts, on_device(): weight = jnp.zeros((chips * 2 * width, channels), out_weight.dtype)  4.32 us
    ppermute x9, starting transfers between devices, place(): other = lax.ppermute(piece, 'core', swap)  3.95 us
    convert_element_type x1, other arithmetic, carried_of(): return (second * carrier).astype(jnp.bfloat16)  2.9 us
    ppermute x3, waiting for transfers between devices, ring_step(): behind = lax.ppermute(behind, 'chip', backward)  2.46 us
  transfers between devices with their start and end apart: 18, of which 2 were waited for; matrix products, arithmetic and copies ran while one was open for 38% of the time, Pallas kernels for 23%

profile of v16, /device:TPU:0, one launch (start us, length us, event | category | flops | bytes accessed | tf_op | source)
XLA Modules:
  0.0 86.2 jit_solution(3811233504766064295)
XLA Ops:
  0.5 2.6 %collective-permute-start.1 = (bf16[128,2048]{0,1:T(8,128)(2,1)}, bf16[128,2048]{0,1:T(8,128)(2,1)S(1)}, u32[]{:S(2)}, u32[]{:S(2)}) collective-permute-start(bf16[128,2048]{0,1:T(8,128)(2,1)} %bitcast.27), channel_id=1, source_target_pairs={{0,4},{4,8},{8,12},{12,14},{14,10},{10,6},{6,2},{2,0},{1,5},{5,9},... | collective-permute-start | bytes 1572872 | tf_op jit(solution)/shard_map/ppermute | solution.py:164
  3.1 0.9 %slice.78 = bf16[2,6144]{1,0:T(2,128)(2,1)S(1)} slice(bf16[512,6144]{1,0:T(8,128)(2,1)} %carrier_ref.5), slice={[510:512], [0:6144]} | slice | bytes 49152 | tf_op jit(solution)/shard_map/slice | solution.py:180
  4.0 1.0 %fusion.8 = (f32[1,2048]{1,0:T(1,128)S(1)}, f32[1,2048]{1,0:T(1,128)S(1)}, f32[1,2048]{1,0:T(1,128)S(1)}, f32[1,2048]{1,0:T(1,128)S(1)}, f32[1,2048]{1,0:T(1,128)S(1)}, /*index=5*/f32[1,2048]{1,0:T(1,128)S(1)}) fusion(f32[3,6144]{1,0:T(4,128)} %param.8), kind=kLoop, calls=%fused_computation.31 | loop fusion | bytes 98304 | tf_op jit(solution)/shard_map/slice | solution.py:34
  5.0 2.9 %multiply_convert_fusion = bf16[128,2048]{1,0:T(8,128)(2,1)S(1)} fusion(bf16[512,6144]{1,0:T(8,128)(2,1)} %carrier_ref.5, f32[2048]{0:T(1024)S(1)} %bitcast.37, f32[2048]{0:T(1024)S(1)} %bitcast.38, f32[2048]{0:T(1024)S(1)} %bitcast.34, f32[2048]{0:T(1024)S(1)} %bitcast.35, f32[2048]{0:T(1024)S(1)} %bitcast.36, f32[2048]{0:T(1024)S(1)} %bitcast.33), kind=kLoop, calls=%fused_computation.8 | loop fusion | flops 4718592 | bytes 3719168 | tf_op jit(solution)/shard_map/convert_element_type | solution.py:128
  8.0 2.1 %collective-permute-start = (bf16[134,2048]{1,0:T(8,128)(2,1)S(1)}, bf16[134,2048]{1,0:T(8,128)(2,1)S(1)}, u32[]{:S(2)}, u32[]{:S(2)}) collective-permute-start(bf16[134,2048]{1,0:T(8,128)(2,1)S(1)} %pad_maximum_fusion), channel_id=1, source_target_pairs={{0,1},{1,2},{2,3},{3,4},{4,5},{5,6},{6,7},{7,8},{8,9},{9,10},{10,1... | collective-permute-start | bytes 1646600 | tf_op jit(solution)/shard_map/ppermute | solution.py:22
  10.9 4.3 %broadcast_in_dim.3 = bf16[2048,2048]{0,1:T(8,128)(2,1)} broadcast(bf16[]{:T(256)} %constant.75.clone.1), dimensions={} | broadcast | bytes 8388610 | tf_op jit(solution)/shard_map/broadcast_in_dim | solution.py:147
  15.3 0.9 %constant_dynamic-update-slice_fusion.15 = bf16[2048,2048]{0,1:T(8,128)(2,1)} fusion(bf16[2048,2048]{0,1:T(8,128)(2,1)} %broadcast_in_dim.3, s32[]{:T(128)S(6)} %select_n.114, bf16[2048,128]{1,0:T(8,128)(2,1)S(1)} %copy-done.3), kind=kLoop, calls=%fused_computation.27 | loop fusion | bytes 1048580 | tf_op jit(solution)/shard_map/dynamic_update_slice | solution.py:152
  16.1 1.9 %collective-permute-start.8 = (bf16[128,2048]{0,1:T(8,128)(2,1)S(1)}, bf16[128,2048]{0,1:T(8,128)(2,1)S(1)}, u32[]{:S(2)}, u32[]{:S(2)}) collective-permute-start(bf16[128,2048]{0,1:T(8,128)(2,1)S(1)} %collective-permute-done.1), channel_id=1, source_target_pairs={{0,1},{1,0},{2,3},{3,2},{4,5},{5,4},{6,7},{7,6},{8,9},{9,8},{10,11... | collective-permute-start | bytes 1572872 | tf_op jit(solution)/shard_map/ppermute | solution.py:150
  19.7 5.8 %collective-permute-start.3 = (bf16[128,2048]{0,1:T(8,128)(2,1)S(1)}, bf16[128,2048]{0,1:T(8,128)(2,1)S(1)}, u32[]{:S(2)}, u32[]{:S(2)}) collective-permute-start(bf16[128,2048]{0,1:T(8,128)(2,1)S(1)} %collective-permute-done.1), channel_id=1, source_target_pairs={{0,4},{4,8},{8,12},{12,14},{14,10},{10,6},{6,2},{2,0},{1,5},{5,9},... | collective-permute-start | bytes 1572872 | tf_op jit(solution)/shard_map/ppermute | solution.py:164
  25.5 0.9 %constant_dynamic-update-slice_fusion.14 = bf16[2048,2048]{0,1:T(8,128)(2,1)} fusion(bf16[2048,2048]{0,1:T(8,128)(2,1)} %constant_dynamic-update-slice_fusion.15, bf16[128,2048]{0,1:T(8,128)(2,1)S(1)} %collective-permute-done.7, s32[]{:T(128)S(6)} %select_n.115), kind=kLoop, calls=%fused_computation.26 | loop fusion | bytes 1048580 | tf_op jit(solution)/shard_map/dynamic_update_slice | solution.py:152
  26.4 0.9 %constant_dynamic-update-slice_fusion.13 = bf16[2048,2048]{0,1:T(8,128)(2,1)} fusion(bf16[2048,2048]{0,1:T(8,128)(2,1)} %constant_dynamic-update-slice_fusion.14, bf16[128,2048]{0,1:T(8,128)(2,1)S(1)} %collective-permute-done.1, s32[]{:T(128)S(6)} %select_n.121), kind=kLoop, calls=%fused_computation.25 | loop fusion | bytes 1048580 | tf_op jit(solution)/shard_map/dynamic_update_slice | solution.py:152
  28.0 5.0 %shard_map.64 = bf16[512,512]{1,0:T(8,128)(2,1)} custom-call(f32[128,384]{1,0:T(8,128)} %pad_convert_fusion.fw_ref, f32[1,2048]{1,0:T(1,128)} %bitcast.29, f32[3,3,2048]{2,1,0:T(4,128)} %bitcast.18, bf16[3,2,2048]{2,1,0:T(2,128)(2,1)} %bitcast.22, bf16[128,2048]{1,0:T(8,128)(2,1)} %slice.83.halo_ref, bf16[512,6144]{1,0:T(8,128)(2,1)} %carrier_ref.5, ...), custom_call_target="tpu_custom_call" | custom-call | tf_op jit(solution)/shard_map/pallas_call | solution.py:101
  33.0 5.0 %shard_map.65 = bf16[512,512]{1,0:T(8,128)(2,1)} custom-call(f32[128,384]{1,0:T(8,128)} %pad_convert_fusion.fw_ref, f32[1,2048]{1,0:T(1,128)} %bitcast.30, f32[3,3,2048]{2,1,0:T(4,128)} %bitcast.19, bf16[3,2,2048]{2,1,0:T(2,128)(2,1)} %bitcast.23, bf16[128,2048]{1,0:T(8,128)(2,1)} %slice.83.halo_ref, bf16[512,6144]{1,0:T(8,128)(2,1)} %carrier_ref.5, ...), custom_call_target="tpu_custom_call" | custom-call | tf_op jit(solution)/shard_map/pallas_call | solution.py:101
  38.0 0.9 %constant_dynamic-update-slice_fusion.12 = bf16[2048,2048]{0,1:T(8,128)(2,1)} fusion(bf16[2048,2048]{0,1:T(8,128)(2,1)} %constant_dynamic-update-slice_fusion.13, bf16[128,2048]{0,1:T(8,128)(2,1)S(1)} %collective-permute-done.8, s32[]{:T(128)S(6)} %select_n.122), kind=kLoop, calls=%fused_computation.24 | loop fusion | bytes 1048580 | tf_op jit(solution)/shard_map/dynamic_update_slice | solution.py:152
  39.0 2.2 %collective-permute-start.5 = (bf16[128,2048]{0,1:T(8,128)(2,1)S(1)}, bf16[128,2048]{0,1:T(8,128)(2,1)S(1)}, u32[]{:S(2)}, u32[]{:S(2)}) collective-permute-start(bf16[128,2048]{0,1:T(8,128)(2,1)S(1)} %collective-permute-done.3), channel_id=1, source_target_pairs={{0,4},{4,8},{8,12},{12,14},{14,10},{10,6},{6,2},{2,0},{1,5},{5,9},... | collective-permute-start | bytes 1572872 | tf_op jit(solution)/shard_map/ppermute | solution.py:164
  41.1 0.9 %constant_dynamic-update-slice_fusion.11 = bf16[2048,2048]{0,1:T(8,128)(2,1)} fusion(bf16[2048,2048]{0,1:T(8,128)(2,1)} %constant_dynamic-update-slice_fusion.12, bf16[128,2048]{0,1:T(8,128)(2,1)S(1)} %collective-permute-done.2, s32[]{:T(128)S(6)} %select_n.125), kind=kLoop, calls=%fused_computation.23 | loop fusion | bytes 1048580 | tf_op jit(solution)/shard_map/dynamic_update_slice | solution.py:152
  42.0 2.0 %constant_dynamic-update-slice_fusion.10 = bf16[2048,2048]{0,1:T(8,128)(2,1)} fusion(bf16[2048,2048]{0,1:T(8,128)(2,1)} %constant_dynamic-update-slice_fusion.11, bf16[128,2048]{0,1:T(8,128)(2,1)} %collective-permute-done.9, s32[]{:T(128)S(6)} %select_n.126), kind=kLoop, calls=%fused_computation.22 | loop fusion | bytes 1048580 | tf_op jit(solution)/shard_map/dynamic_update_slice | solution.py:152
  44.5 0.9 %constant_dynamic-update-slice_fusion.9 = bf16[2048,2048]{0,1:T(8,128)(2,1)} fusion(bf16[2048,2048]{0,1:T(8,128)(2,1)} %constant_dynamic-update-slice_fusion.10, bf16[128,2048]{0,1:T(8,128)(2,1)S(1)} %collective-permute-done.3, s32[]{:T(128)S(6)} %select_n.129), kind=kLoop, calls=%fused_computation.21 | loop fusion | bytes 1048580 | tf_op jit(solution)/shard_map/dynamic_update_slice | solution.py:152
  45.4 5.0 %shard_map.66 = bf16[512,512]{1,0:T(8,128)(2,1)} custom-call(f32[128,384]{1,0:T(8,128)} %pad_convert_fusion.fw_ref, f32[1,2048]{1,0:T(1,128)} %bitcast.31, f32[3,3,2048]{2,1,0:T(4,128)} %bitcast.20, bf16[3,2,2048]{2,1,0:T(2,128)(2,1)} %bitcast.24, bf16[128,2048]{1,0:T(8,128)(2,1)} %slice.83.halo_ref, bf16[512,6144]{1,0:T(8,128)(2,1)} %carrier_ref.5, ...), custom_call_target="tpu_custom_call" | custom-call | tf_op jit(solution)/shard_map/pallas_call | solution.py:101
  50.4 1.4 %collective-permute-done.5 = bf16[128,2048]{0,1:T(8,128)(2,1)S(1)} collective-permute-done((bf16[128,2048]{0,1:T(8,128)(2,1)S(1)}, bf16[128,2048]{0,1:T(8,128)(2,1)S(1)}, u32[]{:S(2)}, u32[]{:S(2)}) %collective-permute-start.5) | collective-permute-done | bytes 524320 | tf_op jit(solution)/shard_map/ppermute | solution.py:164
  51.8 2.5 %collective-permute-done.6 = bf16[128,2048]{0,1:T(8,128)(2,1)S(1)} collective-permute-done((bf16[128,2048]{0,1:T(8,128)(2,1)S(1)}, bf16[128,2048]{0,1:T(8,128)(2,1)S(1)}, u32[]{:S(2)}, u32[]{:S(2)}) %collective-permute-start.6) | collective-permute-done | bytes 524320 | tf_op jit(solution)/shard_map/ppermute | solution.py:165
  55.0 1.7 %collective-permute-start.14 = (bf16[128,1024]{0,1:T(8,128)(2,1)}, bf16[128,1024]{0,1:T(8,128)(2,1)}, u32[]{:S(2)}, u32[]{:S(2)}) collective-permute-start(bf16[128,1024]{0,1:T(8,128)(2,1)} %slice.81), channel_id=1, source_target_pairs={{0,4},{4,8},{8,12},{12,14},{14,10},{10,6},{6,2},{2,0},{1,5},{5,9},... | collective-permute-start | bytes 786440 | tf_op jit(solution)/shard_map/ppermute | solution.py:158
  58.2 1.9 %constant_dynamic-update-slice_fusion.8 = bf16[2048,2048]{0,1:T(8,128)(2,1)} fusion(bf16[2048,2048]{0,1:T(8,128)(2,1)} %constant_dynamic-update-slice_fusion.9, bf16[128,2048]{0,1:T(8,128)(2,1)} %collective-permute-done.10, s32[]{:T(128)S(6)} %select_n.130), kind=kLoop, calls=%fused_computation.20 | loop fusion | bytes 1048580 | tf_op jit(solution)/shard_map/dynamic_update_slice | solution.py:152
  60.1 0.9 %constant_dynamic-update-slice_fusion.7 = bf16[2048,2048]{0,1:T(8,128)(2,1)} fusion(bf16[2048,2048]{0,1:T(8,128)(2,1)} %constant_dynamic-update-slice_fusion.8, bf16[128,2048]{0,1:T(8,128)(2,1)S(1)} %collective-permute-done.4, s32[]{:T(128)S(6)} %select_n.133), kind=kLoop, calls=%fused_computation.19 | loop fusion | bytes 1048580 | tf_op jit(solution)/shard_map/dynamic_update_slice | solution.py:152
  61.0 0.9 %constant_dynamic-update-slice_fusion.6 = bf16[2048,2048]{0,1:T(8,128)(2,1)} fusion(bf16[2048,2048]{0,1:T(8,128)(2,1)} %constant_dynamic-update-slice_fusion.7, bf16[128,2048]{0,1:T(8,128)(2,1)S(1)} %collective-permute-done.11, s32[]{:T(128)S(6)} %select_n.134), kind=kLoop, calls=%fused_computation.18 | loop fusion | bytes 1048580 | tf_op jit(solution)/shard_map/dynamic_update_slice | solution.py:152
  61.9 0.9 %constant_dynamic-update-slice_fusion.5 = bf16[2048,2048]{0,1:T(8,128)(2,1)} fusion(bf16[2048,2048]{0,1:T(8,128)(2,1)} %constant_dynamic-update-slice_fusion.6, bf16[128,2048]{0,1:T(8,128)(2,1)S(1)} %collective-permute-done.5, s32[]{:T(128)S(6)} %select_n.137), kind=kLoop, calls=%fused_computation.17 | loop fusion | bytes 1048580 | tf_op jit(solution)/shard_map/dynamic_update_slice | solution.py:152
  62.9 5.2 %shard_map.67 = bf16[512,512]{1,0:T(8,128)(2,1)} custom-call(f32[128,384]{1,0:T(8,128)} %pad_convert_fusion.fw_ref, f32[1,2048]{1,0:T(1,128)} %bitcast.32, f32[3,3,2048]{2,1,0:T(4,128)} %bitcast.21, bf16[3,2,2048]{2,1,0:T(2,128)(2,1)} %bitcast.25, bf16[128,2048]{1,0:T(8,128)(2,1)} %slice.83.halo_ref, bf16[512,6144]{1,0:T(8,128)(2,1)} %carrier_ref.5, ...), custom_call_target="tpu_custom_call" | custom-call | tf_op jit(solution)/shard_map/pallas_call | solution.py:101
  68.6 1.9 %constant_dynamic-update-slice_fusion.4 = bf16[2048,2048]{0,1:T(8,128)(2,1)} fusion(bf16[2048,2048]{0,1:T(8,128)(2,1)} %constant_dynamic-update-slice_fusion.5, bf16[128,2048]{0,1:T(8,128)(2,1)} %collective-permute-done.12, s32[]{:T(128)S(6)} %select_n.138), kind=kLoop, calls=%fused_computation.16 | loop fusion | bytes 1048580 | tf_op jit(solution)/shard_map/dynamic_update_slice | solution.py:152
  70.5 0.9 %constant_dynamic-update-slice_fusion.3 = bf16[2048,2048]{0,1:T(8,128)(2,1)} fusion(bf16[2048,2048]{0,1:T(8,128)(2,1)} %constant_dynamic-update-slice_fusion.4, bf16[128,2048]{0,1:T(8,128)(2,1)S(1)} %collective-permute-done.6, s32[]{:T(128)S(6)} %select_n.141), kind=kLoop, calls=%fused_computation.15 | loop fusion | bytes 1048580 | tf_op jit(solution)/shard_map/dynamic_update_slice | solution.py:152
  71.4 0.9 %constant_dynamic-update-slice_fusion.2 = bf16[2048,2048]{0,1:T(8,128)(2,1)} fusion(bf16[2048,2048]{0,1:T(8,128)(2,1)} %constant_dynamic-update-slice_fusion.3, bf16[128,2048]{0,1:T(8,128)(2,1)S(1)} %collective-permute-done.13, s32[]{:T(128)S(6)} %select_n.142), kind=kLoop, calls=%fused_computation.14 | loop fusion | bytes 1048580 | tf_op jit(solution)/shard_map/dynamic_update_slice | solution.py:152
  72.3 1.7 %constant_dynamic-update-slice_fusion.1 = bf16[2048,2048]{0,1:T(8,128)(2,1)} fusion(bf16[2048,2048]{0,1:T(8,128)(2,1)} %constant_dynamic-update-slice_fusion.2, bf16[128,1024]{0,1:T(8,128)(2,1)} %collective-permute-done.14, s32[]{:T(128)S(6)} %select_n.145), kind=kLoop, calls=%fused_computation.13 | loop fusion | bytes 524292 | tf_op jit(solution)/shard_map/dynamic_update_slice | solution.py:152
  76.3 9.9 %add_convert_fusion = bf16[512,2048]{1,0:T(8,128)(2,1)} fusion(bf16[512,2048]{1,0:T(8,128)(2,1)} %param.6, bf16[2048,2048]{0,1:T(8,128)(2,1)} %constant_dynamic-update-slice_fusion.16, bf16[512,512]{1,0:T(8,128)(2,1)} %shard_map.67, bf16[512,512]{1,0:T(8,128)(2,1)S(1)} %copy-done.2, bf16[512,512]{1,0:T(8,128)(2,1)S(1)} %copy-done.1, ...), kind=kOutput, calls=%fused_computation | convolution fusion | flops 4306501632 | bytes 14680064 | tf_op jit(solution)/shard_map/dot_general | solution.py:202
  (49 shorter events, 9.3 us)
Async XLA Ops:
  0.0 15.3 %copy-start.3 = (bf16[2048,128]{1,0:T(8,128)(2,1)S(1)}, bf16[2048,128]{1,0:T(8,128)(2,1)}, u32[]{:S(2)}) copy-start(bf16[2048,128]{1,0:T(8,128)(2,1)} %param.11) | copy-start | bytes 1572868
  0.0 25.5 %collective-permute-start.7 = (bf16[128,2048]{0,1:T(8,128)(2,1)}, bf16[128,2048]{0,1:T(8,128)(2,1)S(1)}, u32[]{:S(2)}, u32[]{:S(2)}) collective-permute-start(bf16[128,2048]{0,1:T(8,128)(2,1)} %bitcast.26), channel_id=1, source_target_pairs={{0,1},{1,0},{2,3},{3,2},{4,5},{5,4},{6,7},{7,6},{8,9},{9,8},{10,11... | collective-permute-start | bytes 1572872 | tf_op jit(solution)/shard_map/ppermute | solution.py:150
  0.5 15.7 %collective-permute-start.1 = (bf16[128,2048]{0,1:T(8,128)(2,1)}, bf16[128,2048]{0,1:T(8,128)(2,1)S(1)}, u32[]{:S(2)}, u32[]{:S(2)}) collective-permute-start(bf16[128,2048]{0,1:T(8,128)(2,1)} %bitcast.27), channel_id=1, source_target_pairs={{0,4},{4,8},{8,12},{12,14},{14,10},{10,6},{6,2},{2,0},{1,5},{5,9},... | collective-permute-start | bytes 1572872 | tf_op jit(solution)/shard_map/ppermute | solution.py:164
  3.1 15.7 %collective-permute-start.2 = (bf16[128,2048]{0,1:T(8,128)(2,1)}, bf16[128,2048]{0,1:T(8,128)(2,1)S(1)}, u32[]{:S(2)}, u32[]{:S(2)}) collective-permute-start(bf16[128,2048]{0,1:T(8,128)(2,1)} %bitcast.28), channel_id=1, source_target_pairs={{4,0},{8,4},{12,8},{14,12},{10,14},{6,10},{2,6},{0,2},{5,1},{9,5},... | collective-permute-start | bytes 1572872 | tf_op jit(solution)/shard_map/ppermute | solution.py:165
  8.0 10.9 %collective-permute-start = (bf16[134,2048]{1,0:T(8,128)(2,1)S(1)}, bf16[134,2048]{1,0:T(8,128)(2,1)S(1)}, u32[]{:S(2)}, u32[]{:S(2)}) collective-permute-start(bf16[134,2048]{1,0:T(8,128)(2,1)S(1)} %pad_maximum_fusion), channel_id=1, source_target_pairs={{0,1},{1,2},{2,3},{3,4},{4,5},{5,6},{6,7},{7,8},{8,9},{9,10},{10,1... | collective-permute-start | bytes 1646600 | tf_op jit(solution)/shard_map/ppermute | solution.py:22
  16.1 21.9 %collective-permute-start.8 = (bf16[128,2048]{0,1:T(8,128)(2,1)S(1)}, bf16[128,2048]{0,1:T(8,128)(2,1)S(1)}, u32[]{:S(2)}, u32[]{:S(2)}) collective-permute-start(bf16[128,2048]{0,1:T(8,128)(2,1)S(1)} %collective-permute-done.1), channel_id=1, source_target_pairs={{0,1},{1,0},{2,3},{3,2},{4,5},{5,4},{6,7},{7,6},{8,9},{9,8},{10,11... | collective-permute-start | bytes 1572872 | tf_op jit(solution)/shard_map/ppermute | solution.py:150
  18.8 23.2 %collective-permute-start.9 = (bf16[128,2048]{0,1:T(8,128)(2,1)S(1)}, bf16[128,2048]{0,1:T(8,128)(2,1)}, u32[]{:S(2)}, u32[]{:S(2)}) collective-permute-start(bf16[128,2048]{0,1:T(8,128)(2,1)S(1)} %collective-permute-done.2), channel_id=1, source_target_pairs={{0,1},{1,0},{2,3},{3,2},{4,5},{5,4},{6,7},{7,6},{8,9},{9,8},{10,11... | collective-permute-start | bytes 1572872 | tf_op jit(solution)/shard_map/ppermute | solution.py:150
  19.7 19.3 %collective-permute-start.3 = (bf16[128,2048]{0,1:T(8,128)(2,1)S(1)}, bf16[128,2048]{0,1:T(8,128)(2,1)S(1)}, u32[]{:S(2)}, u32[]{:S(2)}) collective-permute-start(bf16[128,2048]{0,1:T(8,128)(2,1)S(1)} %collective-permute-done.1), channel_id=1, source_target_pairs={{0,4},{4,8},{8,12},{12,14},{14,10},{10,6},{6,2},{2,0},{1,5},{5,9},... | collective-permute-start | bytes 1572872 | tf_op jit(solution)/shard_map/ppermute | solution.py:164
  25.5 13.4 %collective-permute-start.4 = (bf16[128,2048]{0,1:T(8,128)(2,1)S(1)}, bf16[128,2048]{0,1:T(8,128)(2,1)S(1)}, u32[]{:S(2)}, u32[]{:S(2)}) collective-permute-start(bf16[128,2048]{0,1:T(8,128)(2,1)S(1)} %collective-permute-done.2), channel_id=1, source_target_pairs={{4,0},{8,4},{12,8},{14,12},{10,14},{6,10},{2,6},{0,2},{5,1},{9,5},... | collective-permute-start | bytes 1572872 | tf_op jit(solution)/shard_map/ppermute | solution.py:165
  39.0 12.9 %collective-permute-start.5 = (bf16[128,2048]{0,1:T(8,128)(2,1)S(1)}, bf16[128,2048]{0,1:T(8,128)(2,1)S(1)}, u32[]{:S(2)}, u32[]{:S(2)}) collective-permute-start(bf16[128,2048]{0,1:T(8,128)(2,1)S(1)} %collective-permute-done.3), channel_id=1, source_target_pairs={{0,4},{4,8},{8,12},{12,14},{14,10},{10,6},{6,2},{2,0},{1,5},{5,9},... | collective-permute-start | bytes 1572872 | tf_op jit(solution)/shard_map/ppermute | solution.py:164
  41.1 13.2 %collective-permute-start.6 = (bf16[128,2048]{0,1:T(8,128)(2,1)S(1)}, bf16[128,2048]{0,1:T(8,128)(2,1)S(1)}, u32[]{:S(2)}, u32[]{:S(2)}) collective-permute-start(bf16[128,2048]{0,1:T(8,128)(2,1)S(1)} %collective-permute-done.4), channel_id=1, source_target_pairs={{4,0},{8,4},{12,8},{14,12},{10,14},{6,10},{2,6},{0,2},{5,1},{9,5},... | collective-permute-start | bytes 1572872 | tf_op jit(solution)/shard_map/ppermute | solution.py:165
  41.1 16.6 %collective-permute-start.10 = (bf16[128,2048]{0,1:T(8,128)(2,1)S(1)}, bf16[128,2048]{0,1:T(8,128)(2,1)}, u32[]{:S(2)}, u32[]{:S(2)}) collective-permute-start(bf16[128,2048]{0,1:T(8,128)(2,1)S(1)} %collective-permute-done.3), channel_id=1, source_target_pairs={{0,1},{1,0},{2,3},{3,2},{4,5},{5,4},{6,7},{7,6},{8,9},{9,8},{10,11... | collective-permute-start | bytes 1572872 | tf_op jit(solution)/shard_map/ppermute | solution.py:150
  44.0 17.0 %collective-permute-start.11 = (bf16[128,2048]{0,1:T(8,128)(2,1)S(1)}, bf16[128,2048]{0,1:T(8,128)(2,1)S(1)}, u32[]{:S(2)}, u32[]{:S(2)}) collective-permute-start(bf16[128,2048]{0,1:T(8,128)(2,1)S(1)} %collective-permute-done.4), channel_id=1, source_target_pairs={{0,1},{1,0},{2,3},{3,2},{4,5},{5,4},{6,7},{7,6},{8,9},{9,8},{10,11... | collective-permute-start | bytes 1572872 | tf_op jit(solution)/shard_map/ppermute | solution.py:150
  55.0 13.0 %collective-permute-start.14 = (bf16[128,1024]{0,1:T(8,128)(2,1)}, bf16[128,1024]{0,1:T(8,128)(2,1)}, u32[]{:S(2)}, u32[]{:S(2)}) collective-permute-start(bf16[128,1024]{0,1:T(8,128)(2,1)} %slice.81), channel_id=1, source_target_pairs={{0,4},{4,8},{8,12},{12,14},{14,10},{10,6},{6,2},{2,0},{1,5},{5,9},... | collective-permute-start | bytes 786440 | tf_op jit(solution)/shard_map/ppermute | solution.py:158
  57.4 10.7 %collective-permute-start.16 = (bf16[128,1024]{0,1:T(8,128)(2,1)}, bf16[128,1024]{0,1:T(8,128)(2,1)S(1)}, u32[]{:S(2)}, u32[]{:S(2)}) collective-permute-start(bf16[128,1024]{0,1:T(8,128)(2,1)} %slice.82), channel_id=1, source_target_pairs={{4,0},{8,4},{12,8},{14,12},{10,14},{6,10},{2,6},{0,2},{5,1},{9,5},... | collective-permute-start | bytes 786440 | tf_op jit(solution)/shard_map/ppermute | solution.py:159
  57.7 10.9 %collective-permute-start.12 = (bf16[128,2048]{0,1:T(8,128)(2,1)S(1)}, bf16[128,2048]{0,1:T(8,128)(2,1)}, u32[]{:S(2)}, u32[]{:S(2)}) collective-permute-start(bf16[128,2048]{0,1:T(8,128)(2,1)S(1)} %collective-permute-done.5), channel_id=1, source_target_pairs={{0,1},{1,0},{2,3},{3,2},{4,5},{5,4},{6,7},{7,6},{8,9},{9,8},{10,11... | collective-permute-start | bytes 1572872 | tf_op jit(solution)/shard_map/ppermute | solution.py:150
  57.7 13.7 %collective-permute-start.13 = (bf16[128,2048]{0,1:T(8,128)(2,1)S(1)}, bf16[128,2048]{0,1:T(8,128)(2,1)S(1)}, u32[]{:S(2)}, u32[]{:S(2)}) collective-permute-start(bf16[128,2048]{0,1:T(8,128)(2,1)S(1)} %collective-permute-done.6), channel_id=1, source_target_pairs={{0,1},{1,0},{2,3},{3,2},{4,5},{5,4},{6,7},{7,6},{8,9},{9,8},{10,11... | collective-permute-start | bytes 1572872 | tf_op jit(solution)/shard_map/ppermute | solution.py:150
  62.8 13.4 %copy-start = (bf16[512,512]{1,0:T(8,128)(2,1)S(1)}, bf16[512,512]{1,0:T(8,128)(2,1)}, u32[]{:S(2)}) copy-start(bf16[512,512]{1,0:T(8,128)(2,1)} %shard_map.64) | copy-start | bytes 1572868
  62.9 13.4 %copy-start.1 = (bf16[512,512]{1,0:T(8,128)(2,1)S(1)}, bf16[512,512]{1,0:T(8,128)(2,1)}, u32[]{:S(2)}) copy-start(bf16[512,512]{1,0:T(8,128)(2,1)} %shard_map.65) | copy-start | bytes 1572868
  62.9 13.4 %copy-start.2 = (bf16[512,512]{1,0:T(8,128)(2,1)S(1)}, bf16[512,512]{1,0:T(8,128)(2,1)}, u32[]{:S(2)}) copy-start(bf16[512,512]{1,0:T(8,128)(2,1)} %shard_map.66) | copy-start | bytes 1572868
  68.0 6.0 %collective-permute-start.15 = (bf16[128,1024]{0,1:T(8,128)(2,1)}, bf16[128,1024]{0,1:T(8,128)(2,1)S(1)}, u32[]{:S(2)}, u32[]{:S(2)}) collective-permute-start(bf16[128,1024]{0,1:T(8,128)(2,1)} %collective-permute-done.14), channel_id=1, source_target_pairs={{0,1},{1,0},{2,3},{3,2},{4,5},{5,4},{6,7},{7,6},{8,9},{9,8},{10,11... | collective-permute-start | bytes 786440 | tf_op jit(solution)/shard_map/ppermute | solution.py:150
  68.1 7.4 %collective-permute-start.17 = (bf16[128,1024]{0,1:T(8,128)(2,1)S(1)}, bf16[128,1024]{0,1:T(8,128)(2,1)S(1)}, u32[]{:S(2)}, u32[]{:S(2)}) collective-permute-start(bf16[128,1024]{0,1:T(8,128)(2,1)S(1)} %collective-permute-done.16), channel_id=1, source_target_pairs={{0,1},{1,0},{2,3},{3,2},{4,5},{5,4},{6,7},{7,6},{8,9},{9,8},{10,11... | collective-permute-start | bytes 786440 | tf_op jit(solution)/shard_map/ppermute | solution.py:150

commit v17 on v11

--- a/solution.py
+++ b/solution.py
@@ -127,7 +127,7 @@
     channels = out_weight.shape[0]
     chips = lax.axis_size("chip")
     width = out_weight.shape[1]
-    ring = chips % 2 == 0 and chips <= 8
+    ring = chips == 8
 
     chip = lax.axis_index("chip")
     core = lax.axis_index("core")
@@ -184,14 +184,22 @@
         if steps >= 3:
             weight, ahead, behind = ring_step(3, weight, ahead, behind)
     second = hyena_gate(*inputs, 1, 2)
-    if ring:
-        second, ahead, behind = lax.optimization_barrier((second, ahead, behind))
-        for step in range(4, steps + 1):
-            weight, ahead, behind = ring_step(step, weight, ahead, behind)
-    else:
+    gated = jnp.concatenate([first, second], axis=1)
+    if not ring:
         weight = lax.all_gather(out_weight.T, CTX, axis=0, tiled=True)
-    gated = jnp.concatenate([first, second], axis=1)
+        branch = lax.dot_general(gated, weight, (((1,), (1,)), ((), ())), preferred_element_type=jnp.float32)
+        return (tokens.astype(jnp.float32) + branch).astype(jnp.bfloat16)
+    gated, ahead, behind = lax.optimization_barrier((gated, ahead, behind))
+    half = channels // 2
+    ahead = lax.ppermute(ahead[:, :half], "chip", forward)
+    behind = lax.ppermute(behind[:, half:], "chip", backward)
+    source = ring_chip((position - steps) % chips, chips)
     branch = lax.dot_general(gated, weight, (((1,), (1,)), ((), ())), preferred_element_type=jnp.float32)
+    mine = jnp.concatenate([ahead, behind], axis=1)
+    other = lax.ppermute(mine, "core", swap)
+    pair = jnp.where(core == 0, jnp.concatenate([mine, other]), jnp.concatenate([other, mine]))
+    last = lax.dot_general(gated, pair, (((1,), (1,)), ((), ())), preferred_element_type=jnp.float32)
+    branch = lax.dynamic_update_slice(branch, last, (0, source * 2 * width))
     return (tokens.astype(jnp.float32) + branch).astype(jnp.bfloat16)
 
 

time: 80.8 us -> 78.5 us (0.972)
  other arithmetic: 4.43 us -> 7.88 us
  local copies, waits for them, and re-layouts: 26.3 us -> 23 us
  matrix products: 9.18 us -> 7.61 us
  waiting for transfers between devices: 2.82 us -> 1.83 us
    dynamic_update_slice x18 -> x14, local copies, waits for them, and re-layouts: 19.8 us -> 15.7 us  [place(): lax.dynamic_update_slice(weight, part, ((owner_chip * 2 + k) * width, row))]
    dot_general x1, matrix products: 9.18 us -> 6.88 us  [on_device(): lax.dot_general(gated, weight, (((1,), (1,)), ((), ())), preferred_elemen...]
    convert_element_type x0 -> x1, other arithmetic: none -> 2.07 us  [on_device(): return (tokens.astype(jnp.float32) + branch).astype(jnp.bfloat16)]
    concatenate x0 -> x1, other arithmetic: none -> 1.39 us  [on_device(): gated = jnp.concatenate([first, second], axis=1)]
    ppermute x2 -> x3, waiting for transfers between devices: 2.78 us -> 1.44 us  [the longest x1 1.43 us: on_device(): behind = lax.ppermute(behind[:, half:], 'chip', backward)]
    unnamed x14 -> x13, local copies, waits for them, and re-layouts: 0.03 us -> 0.87 us
    ppermute x2 -> x3, starting transfers between devices: 2.13 us -> 2.2 us  [the longest x1 1.72 us: on_device(): ahead = lax.ppermute(ahead[:, :half], 'chip', forward)]
    ppermute x9 -> x7, starting transfers between devices: 4.16 us -> 4.14 us  [place(): other = lax.ppermute(piece, 'core', swap)]
  transfers between devices with their start and end apart: 19 -> 18, of which waited for: 2 -> 2; matrix products, arithmetic and copies ran while one was open for 37% -> 45% of each run, Pallas kernels for 22% -> 22%
where the time goes in v17:
time: 78.5 us; the launch traced here: 77.6 us
  local copies, waits for them, and re-layouts  23 us (29%)
  starting transfers between devices  19.6 us (25%)
  Pallas kernels  17.4 us (22%)
  other arithmetic  7.88 us (10%)
  matrix products  7.61 us (10%)
  waiting for transfers between devices  1.83 us (2%)
    pallas_call x2, Pallas kernels, hyena_gate(): pl.pallas_call(_gate_kernel, grid=(share,), in_specs=[pl.BlockSpec((per_t...  17.4 us
    dynamic_update_slice x14, local copies, waits for them, and re-layouts, place(): lax.dynamic_update_slice(weight, part, ((owner_chip * 2 + k) * width, row))  15.7 us
    ppermute x3, starting transfers between devices, ring_step(): ahead = lax.ppermute(ahead, 'chip', forward)  9.55 us
    dot_general x1, matrix products, on_device(): lax.dot_general(gated, weight, (((1,), (1,)), ((), ())), preferred_elemen...  6.88 us
    broadcast_in_dim x1, local copies, waits for them, and re-layouts, on_device(): weight = jnp.zeros((chips * 2 * width, channels), out_weight.dtype)  4.31 us
    ppermute x7, starting transfers between devices, place(): other = lax.ppermute(piece, 'core', swap)  4.14 us
    ppermute x2, starting transfers between devices, shifted(): return lax.ppermute(block, CTX, route)  3.42 us
    convert_element_type x1, other arithmetic, carried_of(): return (second * carrier).astype(jnp.bfloat16)  2.9 us
  transfers between devices with their start and end apart: 18, of which 2 were waited for; matrix products, arithmetic and copies ran while one was open for 45% of the time, Pallas kernels for 22%

profile of v17, /device:TPU:0, one launch (start us, length us, event | category | flops | bytes accessed | tf_op | source)
XLA Modules:
  0.0 77.6 jit_solution(2031653751268865130)
XLA Ops:
  0.0 3.0 %collective-permute-start.2 = (bf16[128,2048]{0,1:T(8,128)(2,1)}, bf16[128,2048]{0,1:T(8,128)(2,1)S(1)}, u32[]{:S(2)}, u32[]{:S(2)}) collective-permute-start(bf16[128,2048]{0,1:T(8,128)(2,1)} %bitcast.27), channel_id=1, source_target_pairs={{0,4},{4,8},{8,12},{12,14},{14,10},{10,6},{6,2},{2,0},{1,5},{5,9},... | collective-permute-start | bytes 1572872 | tf_op jit(solution)/shard_map/ppermute | solution.py:158
  3.0 1.0 %fusion.7 = (f32[1,2048]{1,0:T(1,128)S(1)}, f32[1,2048]{1,0:T(1,128)S(1)}, f32[1,2048]{1,0:T(1,128)S(1)}, f32[1,2048]{1,0:T(1,128)S(1)}, f32[1,2048]{1,0:T(1,128)S(1)}, /*index=5*/f32[1,2048]{1,0:T(1,128)S(1)}) fusion(f32[3,6144]{1,0:T(4,128)} %param.8), kind=kLoop, calls=%fused_computation.30 | loop fusion | bytes 98304 | tf_op jit(solution)/shard_map/slice | solution.py:34
  4.0 2.9 %multiply_convert_fusion = bf16[128,2048]{1,0:T(8,128)(2,1)S(1)} fusion(bf16[512,6144]{1,0:T(8,128)(2,1)} %carrier_ref.2, f32[2048]{0:T(1024)S(1)} %bitcast.39, f32[2048]{0:T(1024)S(1)} %bitcast.35, f32[2048]{0:T(1024)S(1)} %bitcast.36, f32[2048]{0:T(1024)S(1)} %bitcast.37, f32[2048]{0:T(1024)S(1)} %bitcast.38, f32[2048]{0:T(1024)S(1)} %bitcast.34), kind=kLoop, calls=%fused_computation.9 | loop fusion | flops 4718592 | bytes 3719168 | tf_op jit(solution)/shard_map/convert_element_type | solution.py:122
  6.9 1.5 %collective-permute-start = (bf16[128,2048]{1,0:T(8,128)(2,1)S(1)}, bf16[128,2048]{1,0:T(8,128)(2,1)S(1)}, u32[]{:S(2)}, u32[]{:S(2)}) collective-permute-start(bf16[128,2048]{1,0:T(8,128)(2,1)S(1)} %multiply_convert_fusion), channel_id=1, source_target_pairs={{0,1},{1,2},{2,3},{3,4},{4,5},{5,6},{6,7},{7,8},{8,9},{9,10},{10,1... | collective-permute-start | bytes 1572872 | tf_op jit(solution)/shard_map/ppermute | solution.py:22
  8.4 2.6 %collective-permute-start.8 = (bf16[128,2048]{0,1:T(8,128)(2,1)}, bf16[128,2048]{0,1:T(8,128)(2,1)S(1)}, u32[]{:S(2)}, u32[]{:S(2)}) collective-permute-start(bf16[128,2048]{0,1:T(8,128)(2,1)} %bitcast.29), channel_id=1, source_target_pairs={{0,1},{1,0},{2,3},{3,2},{4,5},{5,4},{6,7},{7,6},{8,9},{9,8},{10,11... | collective-permute-start | bytes 1572872 | tf_op jit(solution)/shard_map/ppermute | solution.py:144
  11.0 0.9 %slice.72 = bf16[2,6144]{1,0:T(2,128)(2,1)S(1)} slice(bf16[512,6144]{1,0:T(8,128)(2,1)} %carrier_ref.2), slice={[510:512], [0:6144]} | slice | bytes 49152 | tf_op jit(solution)/shard_map/slice | solution.py:175
  11.9 1.9 %collective-permute-start.1 = (bf16[2,6144]{1,0:T(2,128)(2,1)S(1)}, bf16[2,6144]{1,0:T(2,128)(2,1)S(1)}, u32[]{:S(2)}, u32[]{:S(2)}) collective-permute-start(bf16[2,6144]{1,0:T(2,128)(2,1)S(1)} %slice.72), channel_id=1, source_target_pairs={{0,1},{1,2},{2,3},{3,4},{4,5},{5,6},{6,7},{7,8},{8,9},{9,10},{10,1... | collective-permute-start | bytes 73736 | tf_op jit(solution)/shard_map/ppermute | solution.py:22
  13.8 4.3 %broadcast_in_dim.3 = bf16[2048,2048]{0,1:T(8,128)(2,1)} broadcast(bf16[]{:T(256)} %constant.75.clone.1), dimensions={} | broadcast | bytes 8388610 | tf_op jit(solution)/shard_map/broadcast_in_dim | solution.py:141
  18.1 0.9 %constant_dynamic-update-slice_fusion.15 = bf16[2048,2048]{0,1:T(8,128)(2,1)} fusion(bf16[2048,2048]{0,1:T(8,128)(2,1)} %broadcast_in_dim.3, s32[]{:T(128)S(6)} %select_n.117, bf16[2048,128]{1,0:T(8,128)(2,1)S(1)} %copy-done.3), kind=kLoop, calls=%fused_computation.28 | loop fusion | bytes 1048580 | tf_op jit(solution)/shard_map/dynamic_update_slice | solution.py:146
  19.2 4.8 %collective-permute-start.4 = (bf16[128,2048]{0,1:T(8,128)(2,1)S(1)}, bf16[128,2048]{0,1:T(8,128)(2,1)}, u32[]{:S(2)}, u32[]{:S(2)}) collective-permute-start(bf16[128,2048]{0,1:T(8,128)(2,1)S(1)} %collective-permute-done.2), channel_id=1, source_target_pairs={{0,4},{4,8},{8,12},{12,14},{14,10},{10,6},{6,2},{2,0},{1,5},{5,9},... | collective-permute-start | bytes 1572872 | tf_op jit(solution)/shard_map/ppermute | solution.py:158
  25.3 0.9 %constant_dynamic-update-slice_fusion.14 = bf16[2048,2048]{0,1:T(8,128)(2,1)} fusion(bf16[2048,2048]{0,1:T(8,128)(2,1)} %constant_dynamic-update-slice_fusion.15, bf16[128,2048]{0,1:T(8,128)(2,1)S(1)} %collective-permute-done.8, s32[]{:T(128)S(6)} %select_n.118), kind=kLoop, calls=%fused_computation.27 | loop fusion | bytes 1048580 | tf_op jit(solution)/shard_map/dynamic_update_slice | solution.py:146
  26.2 0.9 %constant_dynamic-update-slice_fusion.13 = bf16[2048,2048]{0,1:T(8,128)(2,1)} fusion(bf16[2048,2048]{0,1:T(8,128)(2,1)} %constant_dynamic-update-slice_fusion.14, bf16[128,2048]{0,1:T(8,128)(2,1)S(1)} %collective-permute-done.2, s32[]{:T(128)S(6)} %select_n.124), kind=kLoop, calls=%fused_computation.26 | loop fusion | bytes 1048580 | tf_op jit(solution)/shard_map/dynamic_update_slice | solution.py:146
  27.1 8.7 %shard_map.64 = bf16[512,1024]{1,0:T(8,128)(2,1)} custom-call(f32[128,384]{1,0:T(8,128)} %pad_convert_fusion.1.fw_ref, f32[1,2048]{1,0:T(1,128)} %bitcast.32, f32[3,3,2048]{2,1,0:T(4,128)} %bitcast.25, bf16[3,2,2048]{2,1,0:T(2,128)(2,1)} %bitcast.30, bf16[128,2048]{1,0:T(8,128)(2,1)} %copy-done.1, bf16[512,6144]{1,0:T(8,128)(2,1)} %carrier_ref.2, ...), custom_call_target="tpu_custom_call" | custom-call | tf_op jit(solution)/shard_map/pallas_call | solution.py:95
  36.1 1.7 %collective-permute-start.6 = (bf16[128,2048]{0,1:T(8,128)(2,1)}, bf16[128,2048]{0,1:T(8,128)(2,1)S(1)}, u32[]{:S(2)}, u32[]{:S(2)}) collective-permute-start(bf16[128,2048]{0,1:T(8,128)(2,1)} %collective-permute-done.4), channel_id=1, source_target_pairs={{0,4},{4,8},{8,12},{12,14},{14,10},{10,6},{6,2},{2,0},{1,5},{5,9},... | collective-permute-start | bytes 1572872 | tf_op jit(solution)/shard_map/ppermute | solution.py:158
  38.8 0.9 %constant_dynamic-update-slice_fusion.12 = bf16[2048,2048]{0,1:T(8,128)(2,1)} fusion(bf16[2048,2048]{0,1:T(8,128)(2,1)} %constant_dynamic-update-slice_fusion.13, bf16[128,2048]{0,1:T(8,128)(2,1)S(1)} %collective-permute-done.9, s32[]{:T(128)S(6)} %select_n.125), kind=kLoop, calls=%fused_computation.25 | loop fusion | bytes 1048580 | tf_op jit(solution)/shard_map/dynamic_update_slice | solution.py:146
  39.8 0.9 %constant_dynamic-update-slice_fusion.11 = bf16[2048,2048]{0,1:T(8,128)(2,1)} fusion(bf16[2048,2048]{0,1:T(8,128)(2,1)} %constant_dynamic-update-slice_fusion.12, bf16[128,2048]{0,1:T(8,128)(2,1)S(1)} %collective-permute-done.3, s32[]{:T(128)S(6)} %select_n.128), kind=kLoop, calls=%fused_computation.24 | loop fusion | bytes 1048580 | tf_op jit(solution)/shard_map/dynamic_update_slice | solution.py:146
  40.7 0.9 %constant_dynamic-update-slice_fusion.10 = bf16[2048,2048]{0,1:T(8,128)(2,1)} fusion(bf16[2048,2048]{0,1:T(8,128)(2,1)} %constant_dynamic-update-slice_fusion.11, bf16[128,2048]{0,1:T(8,128)(2,1)S(1)} %collective-permute-done.10, s32[]{:T(128)S(6)} %select_n.129), kind=kLoop, calls=%fused_computation.23 | loop fusion | bytes 1048580 | tf_op jit(solution)/shard_map/dynamic_update_slice | solution.py:146
  42.4 8.8 %shard_map.65 = bf16[512,1024]{1,0:T(8,128)(2,1)} custom-call(f32[128,384]{1,0:T(8,128)} %pad_convert_fusion.fw_ref, f32[1,2048]{1,0:T(1,128)} %bitcast.33, f32[3,3,2048]{2,1,0:T(4,128)} %bitcast.26, bf16[3,2,2048]{2,1,0:T(2,128)(2,1)} %bitcast.31, bf16[128,2048]{1,0:T(8,128)(2,1)} %copy-done.1, bf16[512,6144]{1,0:T(8,128)(2,1)} %carrier_ref.2, ...), custom_call_target="tpu_custom_call" | custom-call | tf_op jit(solution)/shard_map/pallas_call | solution.py:95
  51.2 1.4 %pad_maximum_fusion = bf16[512,2048]{1,0:T(8,128)(2,1)S(1)} fusion(bf16[512,1024]{1,0:T(8,128)(2,1)} %shard_map.65, bf16[512,1024]{1,0:T(8,128)(2,1)S(1)} %copy-done), kind=kLoop, calls=%fused_computation.1 | loop fusion | flops 4194304 | bytes 4194304 | tf_op jit(solution)/shard_map/concatenate | solution.py:187
  52.6 1.9 %constant_dynamic-update-slice_fusion.9 = bf16[2048,2048]{0,1:T(8,128)(2,1)} fusion(bf16[2048,2048]{0,1:T(8,128)(2,1)} %constant_dynamic-update-slice_fusion.10, bf16[128,2048]{0,1:T(8,128)(2,1)} %collective-permute-done.4, s32[]{:T(128)S(6)} %select_n.132), kind=kLoop, calls=%fused_computation.22 | loop fusion | bytes 1048580 | tf_op jit(solution)/shard_map/dynamic_update_slice | solution.py:146
  54.5 1.7 %collective-permute-start.15 = (bf16[128,1024]{0,1:T(8,128)(2,1)S(1)}, bf16[128,1024]{0,1:T(8,128)(2,1)S(1)}, u32[]{:S(2)}, u32[]{:S(2)}) collective-permute-start(bf16[128,1024]{0,1:T(8,128)(2,1)S(1)} %slice.73), channel_id=1, source_target_pairs={{0,4},{4,8},{8,12},{12,14},{14,10},{10,6},{6,2},{2,0},{1,5},{5,9},... | collective-permute-start | bytes 786440 | tf_op jit(solution)/shard_map/ppermute | solution.py:194
  57.2 1.9 %constant_dynamic-update-slice_fusion.8 = bf16[2048,2048]{0,1:T(8,128)(2,1)} fusion(bf16[2048,2048]{0,1:T(8,128)(2,1)} %constant_dynamic-update-slice_fusion.9, bf16[128,2048]{0,1:T(8,128)(2,1)} %collective-permute-done.11, s32[]{:T(128)S(6)} %select_n.133), kind=kLoop, calls=%fused_computation.21 | loop fusion | bytes 1048580 | tf_op jit(solution)/shard_map/dynamic_update_slice | solution.py:146
  59.1 1.9 %constant_dynamic-update-slice_fusion.7 = bf16[2048,2048]{0,1:T(8,128)(2,1)} fusion(bf16[2048,2048]{0,1:T(8,128)(2,1)} %constant_dynamic-update-slice_fusion.8, bf16[128,2048]{0,1:T(8,128)(2,1)} %collective-permute-done.5, s32[]{:T(128)S(6)} %select_n.136), kind=kLoop, calls=%fused_computation.20 | loop fusion | bytes 1048580 | tf_op jit(solution)/shard_map/dynamic_update_slice | solution.py:146
  61.0 0.9 %constant_dynamic-update-slice_fusion.6 = bf16[2048,2048]{0,1:T(8,128)(2,1)} fusion(bf16[2048,2048]{0,1:T(8,128)(2,1)} %constant_dynamic-update-slice_fusion.7, bf16[128,2048]{0,1:T(8,128)(2,1)S(1)} %collective-permute-done.12, s32[]{:T(128)S(6)} %select_n.137), kind=kLoop, calls=%fused_computation.19 | loop fusion | bytes 1048580 | tf_op jit(solution)/shard_map/dynamic_update_slice | solution.py:146
  61.9 0.9 %constant_dynamic-update-slice_fusion.5 = bf16[2048,2048]{0,1:T(8,128)(2,1)} fusion(bf16[2048,2048]{0,1:T(8,128)(2,1)} %constant_dynamic-update-slice_fusion.6, bf16[128,2048]{0,1:T(8,128)(2,1)S(1)} %collective-permute-done.6, s32[]{:T(128)S(6)} %select_n.140), kind=kLoop, calls=%fused_computation.18 | loop fusion | bytes 1048580 | tf_op jit(solution)/shard_map/dynamic_update_slice | solution.py:146
  62.9 1.4 %collective-permute-done.16 = bf16[128,1024]{0,1:T(8,128)(2,1)S(1)} collective-permute-done((bf16[128,1024]{0,1:T(8,128)(2,1)S(1)}, bf16[128,1024]{0,1:T(8,128)(2,1)S(1)}, u32[]{:S(2)}, u32[]{:S(2)}) %collective-permute-start.16) | collective-permute-done | bytes 262176 | tf_op jit(solution)/shard_map/ppermute | solution.py:195
  64.4 0.9 %constant_dynamic-update-slice_fusion.4 = bf16[2048,2048]{0,1:T(8,128)(2,1)} fusion(bf16[2048,2048]{0,1:T(8,128)(2,1)} %constant_dynamic-update-slice_fusion.5, bf16[128,2048]{0,1:T(8,128)(2,1)S(1)} %collective-permute-done.13, s32[]{:T(128)S(6)} %select_n.141), kind=kLoop, calls=%fused_computation.17 | loop fusion | bytes 1048580 | tf_op jit(solution)/shard_map/dynamic_update_slice | solution.py:146
  65.3 0.9 %constant_dynamic-update-slice_fusion.3 = bf16[2048,2048]{0,1:T(8,128)(2,1)} fusion(bf16[2048,2048]{0,1:T(8,128)(2,1)} %constant_dynamic-update-slice_fusion.4, bf16[128,2048]{0,1:T(8,128)(2,1)S(1)} %collective-permute-done.7, s32[]{:T(128)S(6)} %select_n.144), kind=kLoop, calls=%fused_computation.16 | loop fusion | bytes 1048580 | tf_op jit(solution)/shard_map/dynamic_update_slice | solution.py:146
  66.2 0.9 %constant_dynamic-update-slice_fusion.2 = bf16[2048,2048]{0,1:T(8,128)(2,1)} fusion(bf16[2048,2048]{0,1:T(8,128)(2,1)} %constant_dynamic-update-slice_fusion.3, bf16[128,2048]{0,1:T(8,128)(2,1)S(1)} %collective-permute-done.14, s32[]{:T(128)S(6)} %select_n.145), kind=kLoop, calls=%fused_computation.15 | loop fusion | bytes 1048580 | tf_op jit(solution)/shard_map/dynamic_update_slice | solution.py:146
  67.1 6.9 %fusion.8 = f32[512,2048]{1,0:T(8,128)S(1)} fusion(bf16[512,2048]{1,0:T(8,128)(2,1)S(1)} %pad_maximum_fusion, bf16[2048,2048]{0,1:T(8,128)(2,1)} %constant_dynamic-update-slice_fusion.2), kind=kOutput, calls=%fused_computation.31 | convolution fusion | flops 4294967296 | bytes 14680064 | tf_op jit(solution)/shard_map/dot_general | solution.py:197
  74.7 0.8 %copy-done.2 = bf16[512,2048]{1,0:T(8,128)(2,1)S(1)} copy-done((bf16[512,2048]{1,0:T(8,128)(2,1)S(1)}, bf16[512,2048]{1,0:T(8,128)(2,1)}, u32[]{:S(2)}) %copy-start.2) | copy-done | bytes 2097176
  75.6 2.1 %add_convert_fusion = bf16[512,2048]{1,0:T(8,128)(2,1)} fusion(f32[512,2048]{1,0:T(8,128)S(1)} %convolution_dynamic-update-slice_fusion, bf16[512,2048]{1,0:T(8,128)(2,1)S(1)} %copy-done.2), kind=kLoop, calls=%fused_computation | loop fusion | flops 3145728 | bytes 8388608 | tf_op jit(solution)/shard_map/convert_element_type | solution.py:203
  (48 shorter events, 5.4 us)
Async XLA Ops:
  0.0 18.1 %copy-start.3 = (bf16[2048,128]{1,0:T(8,128)(2,1)S(1)}, bf16[2048,128]{1,0:T(8,128)(2,1)}, u32[]{:S(2)}) copy-start(bf16[2048,128]{1,0:T(8,128)(2,1)} %param.11) | copy-start | bytes 1572868
  0.0 19.0 %copy-start.4 = (bf16[128,128]{1,0:T(8,128)(2,1)S(1)}, bf16[128,128]{1,0:T(8,128)(2,1)}, u32[]{:S(2)}) copy-start(bf16[128,128]{1,0:T(8,128)(2,1)} %param.9) | copy-start | bytes 98308
  0.0 19.1 %collective-permute-start.2 = (bf16[128,2048]{0,1:T(8,128)(2,1)}, bf16[128,2048]{0,1:T(8,128)(2,1)S(1)}, u32[]{:S(2)}, u32[]{:S(2)}) collective-permute-start(bf16[128,2048]{0,1:T(8,128)(2,1)} %bitcast.27), channel_id=1, source_target_pairs={{0,4},{4,8},{8,12},{12,14},{14,10},{10,6},{6,2},{2,0},{1,5},{5,9},... | collective-permute-start | bytes 1572872 | tf_op jit(solution)/shard_map/ppermute | solution.py:158
  3.0 16.1 %collective-permute-start.3 = (bf16[128,2048]{0,1:T(8,128)(2,1)}, bf16[128,2048]{0,1:T(8,128)(2,1)S(1)}, u32[]{:S(2)}, u32[]{:S(2)}) collective-permute-start(bf16[128,2048]{0,1:T(8,128)(2,1)} %bitcast.28), channel_id=1, source_target_pairs={{4,0},{8,4},{12,8},{14,12},{10,14},{6,10},{2,6},{0,2},{5,1},{9,5},... | collective-permute-start | bytes 1572872 | tf_op jit(solution)/shard_map/ppermute | solution.py:159
  6.9 12.3 %collective-permute-start = (bf16[128,2048]{1,0:T(8,128)(2,1)S(1)}, bf16[128,2048]{1,0:T(8,128)(2,1)S(1)}, u32[]{:S(2)}, u32[]{:S(2)}) collective-permute-start(bf16[128,2048]{1,0:T(8,128)(2,1)S(1)} %multiply_convert_fusion), channel_id=1, source_target_pairs={{0,1},{1,2},{2,3},{3,4},{4,5},{5,6},{6,7},{7,8},{8,9},{9,10},{10,1... | collective-permute-start | bytes 1572872 | tf_op jit(solution)/shard_map/ppermute | solution.py:22
  8.4 16.9 %collective-permute-start.8 = (bf16[128,2048]{0,1:T(8,128)(2,1)}, bf16[128,2048]{0,1:T(8,128)(2,1)S(1)}, u32[]{:S(2)}, u32[]{:S(2)}) collective-permute-start(bf16[128,2048]{0,1:T(8,128)(2,1)} %bitcast.29), channel_id=1, source_target_pairs={{0,1},{1,0},{2,3},{3,2},{4,5},{5,4},{6,7},{7,6},{8,9},{9,8},{10,11... | collective-permute-start | bytes 1572872 | tf_op jit(solution)/shard_map/ppermute | solution.py:144
  11.9 7.2 %collective-permute-start.1 = (bf16[2,6144]{1,0:T(2,128)(2,1)S(1)}, bf16[2,6144]{1,0:T(2,128)(2,1)S(1)}, u32[]{:S(2)}, u32[]{:S(2)}) collective-permute-start(bf16[2,6144]{1,0:T(2,128)(2,1)S(1)} %slice.72), channel_id=1, source_target_pairs={{0,1},{1,2},{2,3},{3,4},{4,5},{5,6},{6,7},{7,8},{8,9},{9,10},{10,1... | collective-permute-start | bytes 73736 | tf_op jit(solution)/shard_map/ppermute | solution.py:22
  19.1 8.0 %copy-start.5 = (bf16[2,6144]{1,0:T(2,128)(2,1)}, bf16[2,6144]{1,0:T(2,128)(2,1)S(1)}, u32[]{:S(2)}) copy-start(bf16[2,6144]{1,0:T(2,128)(2,1)S(1)} %collective-permute-done.1) | copy-start | bytes 73732
  19.2 7.9 %copy-start.1 = (bf16[128,2048]{1,0:T(8,128)(2,1)}, bf16[128,2048]{1,0:T(8,128)(2,1)S(1)}, u32[]{:S(2)}) copy-start(bf16[128,2048]{1,0:T(8,128)(2,1)S(1)} %collective-permute-done.halo_ref) | copy-start | bytes 1572868
  19.2 16.6 %collective-permute-start.4 = (bf16[128,2048]{0,1:T(8,128)(2,1)S(1)}, bf16[128,2048]{0,1:T(8,128)(2,1)}, u32[]{:S(2)}, u32[]{:S(2)}) collective-permute-start(bf16[128,2048]{0,1:T(8,128)(2,1)S(1)} %collective-permute-done.2), channel_id=1, source_target_pairs={{0,4},{4,8},{8,12},{12,14},{14,10},{10,6},{6,2},{2,0},{1,5},{5,9},... | collective-permute-start | bytes 1572872 | tf_op jit(solution)/shard_map/ppermute | solution.py:158
  24.0 12.2 %collective-permute-start.5 = (bf16[128,2048]{0,1:T(8,128)(2,1)S(1)}, bf16[128,2048]{0,1:T(8,128)(2,1)}, u32[]{:S(2)}, u32[]{:S(2)}) collective-permute-start(bf16[128,2048]{0,1:T(8,128)(2,1)S(1)} %collective-permute-done.3), channel_id=1, source_target_pairs={{4,0},{8,4},{12,8},{14,12},{10,14},{6,10},{2,6},{0,2},{5,1},{9,5},... | collective-permute-start | bytes 1572872 | tf_op jit(solution)/shard_map/ppermute | solution.py:159
  24.0 14.3 %collective-permute-start.9 = (bf16[128,2048]{0,1:T(8,128)(2,1)S(1)}, bf16[128,2048]{0,1:T(8,128)(2,1)S(1)}, u32[]{:S(2)}, u32[]{:S(2)}) collective-permute-start(bf16[128,2048]{0,1:T(8,128)(2,1)S(1)} %collective-permute-done.2), channel_id=1, source_target_pairs={{0,1},{1,0},{2,3},{3,2},{4,5},{5,4},{6,7},{7,6},{8,9},{9,8},{10,11... | collective-permute-start | bytes 1572872 | tf_op jit(solution)/shard_map/ppermute | solution.py:144
  24.8 15.9 %collective-permute-start.10 = (bf16[128,2048]{0,1:T(8,128)(2,1)S(1)}, bf16[128,2048]{0,1:T(8,128)(2,1)S(1)}, u32[]{:S(2)}, u32[]{:S(2)}) collective-permute-start(bf16[128,2048]{0,1:T(8,128)(2,1)S(1)} %collective-permute-done.3), channel_id=1, source_target_pairs={{0,1},{1,0},{2,3},{3,2},{4,5},{5,4},{6,7},{7,6},{8,9},{9,8},{10,11... | collective-permute-start | bytes 1572872 | tf_op jit(solution)/shard_map/ppermute | solution.py:144
  36.1 18.4 %collective-permute-start.6 = (bf16[128,2048]{0,1:T(8,128)(2,1)}, bf16[128,2048]{0,1:T(8,128)(2,1)S(1)}, u32[]{:S(2)}, u32[]{:S(2)}) collective-permute-start(bf16[128,2048]{0,1:T(8,128)(2,1)} %collective-permute-done.4), channel_id=1, source_target_pairs={{0,4},{4,8},{8,12},{12,14},{14,10},{10,6},{6,2},{2,0},{1,5},{5,9},... | collective-permute-start | bytes 1572872 | tf_op jit(solution)/shard_map/ppermute | solution.py:158
  37.9 16.6 %collective-permute-start.7 = (bf16[128,2048]{0,1:T(8,128)(2,1)}, bf16[128,2048]{0,1:T(8,128)(2,1)S(1)}, u32[]{:S(2)}, u32[]{:S(2)}) collective-permute-start(bf16[128,2048]{0,1:T(8,128)(2,1)} %collective-permute-done.5), channel_id=1, source_target_pairs={{4,0},{8,4},{12,8},{14,12},{10,14},{6,10},{2,6},{0,2},{5,1},{9,5},... | collective-permute-start | bytes 1572872 | tf_op jit(solution)/shard_map/ppermute | solution.py:159
  38.3 18.4 %collective-permute-start.11 = (bf16[128,2048]{0,1:T(8,128)(2,1)}, bf16[128,2048]{0,1:T(8,128)(2,1)}, u32[]{:S(2)}, u32[]{:S(2)}) collective-permute-start(bf16[128,2048]{0,1:T(8,128)(2,1)} %collective-permute-done.4), channel_id=1, source_target_pairs={{0,1},{1,0},{2,3},{3,2},{4,5},{5,4},{6,7},{7,6},{8,9},{9,8},{10,11... | collective-permute-start | bytes 1572872 | tf_op jit(solution)/shard_map/ppermute | solution.py:144
  38.4 22.7 %collective-permute-start.12 = (bf16[128,2048]{0,1:T(8,128)(2,1)}, bf16[128,2048]{0,1:T(8,128)(2,1)S(1)}, u32[]{:S(2)}, u32[]{:S(2)}) collective-permute-start(bf16[128,2048]{0,1:T(8,128)(2,1)} %collective-permute-done.5), channel_id=1, source_target_pairs={{0,1},{1,0},{2,3},{3,2},{4,5},{5,4},{6,7},{7,6},{8,9},{9,8},{10,11... | collective-permute-start | bytes 1572872 | tf_op jit(solution)/shard_map/ppermute | solution.py:144
  42.4 8.8 %copy-start = (bf16[512,1024]{1,0:T(8,128)(2,1)S(1)}, bf16[512,1024]{1,0:T(8,128)(2,1)}, u32[]{:S(2)}) copy-start(bf16[512,1024]{1,0:T(8,128)(2,1)} %shard_map.64) | copy-start | bytes 3145732
  54.5 8.3 %collective-permute-start.15 = (bf16[128,1024]{0,1:T(8,128)(2,1)S(1)}, bf16[128,1024]{0,1:T(8,128)(2,1)S(1)}, u32[]{:S(2)}, u32[]{:S(2)}) collective-permute-start(bf16[128,1024]{0,1:T(8,128)(2,1)S(1)} %slice.73), channel_id=1, source_target_pairs={{0,4},{4,8},{8,12},{12,14},{14,10},{10,6},{6,2},{2,0},{1,5},{5,9},... | collective-permute-start | bytes 786440 | tf_op jit(solution)/shard_map/ppermute | solution.py:194
  56.3 8.0 %collective-permute-start.16 = (bf16[128,1024]{0,1:T(8,128)(2,1)S(1)}, bf16[128,1024]{0,1:T(8,128)(2,1)S(1)}, u32[]{:S(2)}, u32[]{:S(2)}) collective-permute-start(bf16[128,1024]{0,1:T(8,128)(2,1)S(1)} %slice.74), channel_id=1, source_target_pairs={{4,0},{8,4},{12,8},{14,12},{10,14},{6,10},{2,6},{0,2},{5,1},{9,5},... | collective-permute-start | bytes 786440 | tf_op jit(solution)/shard_map/ppermute | solution.py:195
  56.7 7.8 %collective-permute-start.13 = (bf16[128,2048]{0,1:T(8,128)(2,1)S(1)}, bf16[128,2048]{0,1:T(8,128)(2,1)S(1)}, u32[]{:S(2)}, u32[]{:S(2)}) collective-permute-start(bf16[128,2048]{0,1:T(8,128)(2,1)S(1)} %collective-permute-done.6), channel_id=1, source_target_pairs={{0,1},{1,0},{2,3},{3,2},{4,5},{5,4},{6,7},{7,6},{8,9},{9,8},{10,11... | collective-permute-start | bytes 1572872 | tf_op jit(solution)/shard_map/ppermute | solution.py:144
  56.7 9.5 %collective-permute-start.14 = (bf16[128,2048]{0,1:T(8,128)(2,1)S(1)}, bf16[128,2048]{0,1:T(8,128)(2,1)S(1)}, u32[]{:S(2)}, u32[]{:S(2)}) collective-permute-start(bf16[128,2048]{0,1:T(8,128)(2,1)S(1)} %collective-permute-done.7), channel_id=1, source_target_pairs={{0,1},{1,0},{2,3},{3,2},{4,5},{5,4},{6,7},{7,6},{8,9},{9,8},{10,11... | collective-permute-start | bytes 1572872 | tf_op jit(solution)/shard_map/ppermute | solution.py:144
  64.3 9.6 %collective-permute-start.17 = (bf16[128,2048]{0,1:T(8,128)(2,1)S(1)}, bf16[128,2048]{0,1:T(8,128)(2,1)S(1)}, u32[]{:S(2)}, u32[]{:S(2)}) collective-permute-start(bf16[128,2048]{0,1:T(8,128)(2,1)S(1)} %constant_dynamic-update-slice_fusion), channel_id=1, source_target_pairs={{0,1},{1,0},{2,3},{3,2},{4,5},{5,4},{6,7},{7,6},{8,9},{9,8},{10,11... | collective-permute-start | bytes 1572872 | tf_op jit(solution)/shard_map/ppermute | solution.py:199
  74.0 1.6 %copy-start.2 = (bf16[512,2048]{1,0:T(8,128)(2,1)S(1)}, bf16[512,2048]{1,0:T(8,128)(2,1)}, u32[]{:S(2)}) copy-start(bf16[512,2048]{1,0:T(8,128)(2,1)} %param.6) | copy-start | bytes 6291460

commit v18 on v17

--- a/solution.py
+++ b/solution.py
@@ -181,8 +181,9 @@
     first = hyena_gate(*inputs, 0, 2)
     if ring:
         first, ahead, behind, inputs = lax.optimization_barrier((first, ahead, behind, inputs))
-        if steps >= 3:
-            weight, ahead, behind = ring_step(3, weight, ahead, behind)
+        ahead = lax.ppermute(ahead, "chip", forward)
+        behind = lax.ppermute(behind, "chip", backward)
+        late = [(ahead, ring_chip((position - 3) % chips, chips)), (behind, ring_chip((position + 3) % chips, chips))]
     second = hyena_gate(*inputs, 1, 2)
     gated = jnp.concatenate([first, second], axis=1)
     if not ring:
@@ -195,11 +196,12 @@
     behind = lax.ppermute(behind[:, half:], "chip", backward)
     source = ring_chip((position - steps) % chips, chips)
     branch = lax.dot_general(gated, weight, (((1,), (1,)), ((), ())), preferred_element_type=jnp.float32)
-    mine = jnp.concatenate([ahead, behind], axis=1)
-    other = lax.ppermute(mine, "core", swap)
-    pair = jnp.where(core == 0, jnp.concatenate([mine, other]), jnp.concatenate([other, mine]))
-    last = lax.dot_general(gated, pair, (((1,), (1,)), ((), ())), preferred_element_type=jnp.float32)
-    branch = lax.dynamic_update_slice(branch, last, (0, source * 2 * width))
+    late.append((jnp.concatenate([ahead, behind], axis=1), source))
+    for mine, owner_chip in late:
+        other = lax.ppermute(mine, "core", swap)
+        pair = jnp.where(core == 0, jnp.concatenate([mine, other]), jnp.concatenate([other, mine]))
+        part = lax.dot_general(gated, pair, (((1,), (1,)), ((), ())), preferred_element_type=jnp.float32)
+        branch = lax.dynamic_update_slice(branch, part, (0, owner_chip * 2 * width))
     return (tokens.astype(jnp.float32) + branch).astype(jnp.bfloat16)
 
 

time: 78.5 us -> 79.2 us (level)
  matrix products: 7.61 us -> 11.5 us
  waiting for transfers between devices: 1.83 us -> 0.05 us
  local copies, waits for them, and re-layouts: 23 us -> 21.4 us
    dot_general x1 -> x3, matrix products: 0.73 us -> 4.6 us  [on_device(): lax.dot_general(gated, pair, (((1,), (1,)), ((), ())), preferred_element_...]
    dynamic_update_slice x14 -> x10, local copies, waits for them, and re-layouts: 15.7 us -> 12.2 us  [place(): lax.dynamic_update_slice(weight, part, ((owner_chip * 2 + k) * width, row))]
    ppermute x0 -> x2, starting transfers between devices: none -> 2.08 us  [the longest x1 2.06 us: on_device(): ahead = lax.ppermute(ahead, 'chip', forward)]
    ppermute x3 -> x2, starting transfers between devices: 9.55 us -> 7.82 us  [ring_step(): ahead = lax.ppermute(ahead, 'chip', forward)]
    ppermute x1, waiting for transfers between devices: 1.43 us -> 0.01 us  [on_device(): behind = lax.ppermute(behind[:, half:], 'chip', backward)]
    slice x1, local copies, waits for them, and re-layouts: 0.02 us -> 0.97 us  [on_device(): ahead = lax.ppermute(ahead[:, :half], 'chip', forward)]
    slice x1, local copies, waits for them, and re-layouts: 0.02 us -> 0.97 us  [on_device(): behind = lax.ppermute(behind[:, half:], 'chip', backward)]
    ppermute x7 -> x5, starting transfers between devices: 4.14 us -> 3.58 us  [place(): other = lax.ppermute(piece, 'core', swap)]
  transfers between devices with their start and end apart: 18 -> 18, of which waited for: 2 -> 0; matrix products, arithmetic and copies ran while one was open for 45% -> 47% of each run, Pallas kernels for 22% -> 22%
where the time goes in v18:
time: 79.2 us; the launch traced here: 78.2 us
  local copies, waits for them, and re-layouts  21.4 us (27%)
  starting transfers between devices  19.7 us (25%)
  Pallas kernels  17.4 us (22%)
  matrix products  11.5 us (15%)
  other arithmetic  7.88 us (10%)
    pallas_call x2, Pallas kernels, hyena_gate(): pl.pallas_call(_gate_kernel, grid=(share,), in_specs=[pl.BlockSpec((per_t...  17.4 us
    dynamic_update_slice x10, local copies, waits for them, and re-layouts, place(): lax.dynamic_update_slice(weight, part, ((owner_chip * 2 + k) * width, row))  12.2 us
    ppermute x2, starting transfers between devices, ring_step(): ahead = lax.ppermute(ahead, 'chip', forward)  7.82 us
    dot_general x1, matrix products, on_device(): lax.dot_general(gated, weight, (((1,), (1,)), ((), ())), preferred_elemen...  6.88 us
    dot_general x3, matrix products, on_device(): lax.dot_general(gated, pair, (((1,), (1,)), ((), ())), preferred_element_...  4.6 us
    broadcast_in_dim x1, local copies, waits for them, and re-layouts, on_device(): weight = jnp.zeros((chips * 2 * width, channels), out_weight.dtype)  4.31 us
    ppermute x5, starting transfers between devices, place(): other = lax.ppermute(piece, 'core', swap)  3.58 us
    ppermute x2, starting transfers between devices, shifted(): return lax.ppermute(block, CTX, route)  3.42 us
  transfers between devices with their start and end apart: 18, of which 0 were waited for; matrix products, arithmetic and copies ran while one was open for 47% of the time, Pallas kernels for 22%

profile of v18, /device:TPU:0, one launch (start us, length us, event | category | flops | bytes accessed | tf_op | source)
XLA Modules:
  0.0 78.2 jit_solution(17158337881729565728)
XLA Ops:
  0.0 3.0 %collective-permute-start.2 = (bf16[128,2048]{0,1:T(8,128)(2,1)}, bf16[128,2048]{0,1:T(8,128)(2,1)S(1)}, u32[]{:S(2)}, u32[]{:S(2)}) collective-permute-start(bf16[128,2048]{0,1:T(8,128)(2,1)} %bitcast.29), channel_id=1, source_target_pairs={{0,4},{4,8},{8,12},{12,14},{14,10},{10,6},{6,2},{2,0},{1,5},{5,9},... | collective-permute-start | bytes 1572872 | tf_op jit(solution)/shard_map/ppermute | solution.py:158
  3.0 1.0 %fusion.21 = (f32[1,2048]{1,0:T(1,128)S(1)}, f32[1,2048]{1,0:T(1,128)S(1)}, f32[1,2048]{1,0:T(1,128)S(1)}, f32[1,2048]{1,0:T(1,128)S(1)}, f32[1,2048]{1,0:T(1,128)S(1)}, /*index=5*/f32[1,2048]{1,0:T(1,128)S(1)}) fusion(f32[3,6144]{1,0:T(4,128)} %param.8), kind=kLoop, calls=%fused_computation.44 | loop fusion | bytes 98304 | tf_op jit(solution)/shard_map/slice | solution.py:34
  4.0 2.9 %multiply_convert_fusion = bf16[128,2048]{1,0:T(8,128)(2,1)S(1)} fusion(bf16[512,6144]{1,0:T(8,128)(2,1)} %carrier_ref.2, f32[2048]{0:T(1024)S(1)} %bitcast.41, f32[2048]{0:T(1024)S(1)} %bitcast.37, f32[2048]{0:T(1024)S(1)} %bitcast.38, f32[2048]{0:T(1024)S(1)} %bitcast.39, f32[2048]{0:T(1024)S(1)} %bitcast.40, f32[2048]{0:T(1024)S(1)} %bitcast.36), kind=kLoop, calls=%fused_computation.23 | loop fusion | flops 4718592 | bytes 3719168 | tf_op jit(solution)/shard_map/convert_element_type | solution.py:122
  6.9 1.5 %collective-permute-start = (bf16[128,2048]{1,0:T(8,128)(2,1)S(1)}, bf16[128,2048]{1,0:T(8,128)(2,1)S(1)}, u32[]{:S(2)}, u32[]{:S(2)}) collective-permute-start(bf16[128,2048]{1,0:T(8,128)(2,1)S(1)} %multiply_convert_fusion), channel_id=1, source_target_pairs={{0,1},{1,2},{2,3},{3,4},{4,5},{5,6},{6,7},{7,8},{8,9},{9,10},{10,1... | collective-permute-start | bytes 1572872 | tf_op jit(solution)/shard_map/ppermute | solution.py:22
  8.4 2.6 %collective-permute-start.8 = (bf16[128,2048]{0,1:T(8,128)(2,1)}, bf16[128,2048]{0,1:T(8,128)(2,1)}, u32[]{:S(2)}, u32[]{:S(2)}) collective-permute-start(bf16[128,2048]{0,1:T(8,128)(2,1)} %bitcast.31), channel_id=1, source_target_pairs={{0,1},{1,0},{2,3},{3,2},{4,5},{5,4},{6,7},{7,6},{8,9},{9,8},{10,11... | collective-permute-start | bytes 1572872 | tf_op jit(solution)/shard_map/ppermute | solution.py:144
  11.0 0.9 %slice.72 = bf16[2,6144]{1,0:T(2,128)(2,1)S(1)} slice(bf16[512,6144]{1,0:T(8,128)(2,1)} %carrier_ref.2), slice={[510:512], [0:6144]} | slice | bytes 49152 | tf_op jit(solution)/shard_map/slice | solution.py:175
  11.9 1.9 %collective-permute-start.1 = (bf16[2,6144]{1,0:T(2,128)(2,1)S(1)}, bf16[2,6144]{1,0:T(2,128)(2,1)S(1)}, u32[]{:S(2)}, u32[]{:S(2)}) collective-permute-start(bf16[2,6144]{1,0:T(2,128)(2,1)S(1)} %slice.72), channel_id=1, source_target_pairs={{0,1},{1,2},{2,3},{3,4},{4,5},{5,6},{6,7},{7,8},{8,9},{9,10},{10,1... | collective-permute-start | bytes 73736 | tf_op jit(solution)/shard_map/ppermute | solution.py:22
  13.8 4.3 %broadcast_in_dim.3 = bf16[2048,2048]{0,1:T(8,128)(2,1)} broadcast(bf16[]{:T(256)} %constant.77.clone.1), dimensions={} | broadcast | bytes 8388610 | tf_op jit(solution)/shard_map/broadcast_in_dim | solution.py:141
  18.2 0.9 %constant_dynamic-update-slice_fusion.11 = bf16[2048,2048]{0,1:T(8,128)(2,1)} fusion(bf16[2048,2048]{0,1:T(8,128)(2,1)} %broadcast_in_dim.3, s32[]{:T(128)S(6)} %select_n.119, bf16[2048,128]{1,0:T(8,128)(2,1)S(1)} %copy-done.3), kind=kLoop, calls=%fused_computation.40 | loop fusion | bytes 1048580 | tf_op jit(solution)/shard_map/dynamic_update_slice | solution.py:146
  19.2 4.8 %collective-permute-start.4 = (bf16[128,2048]{0,1:T(8,128)(2,1)S(1)}, bf16[128,2048]{0,1:T(8,128)(2,1)}, u32[]{:S(2)}, u32[]{:S(2)}) collective-permute-start(bf16[128,2048]{0,1:T(8,128)(2,1)S(1)} %collective-permute-done.2), channel_id=1, source_target_pairs={{0,4},{4,8},{8,12},{12,14},{14,10},{10,6},{6,2},{2,0},{1,5},{5,9},... | collective-permute-start | bytes 1572872 | tf_op jit(solution)/shard_map/ppermute | solution.py:158
  24.0 0.8 pad_convert_fusion.1.fw_ref
  25.3 1.9 %constant_dynamic-update-slice_fusion.10 = bf16[2048,2048]{0,1:T(8,128)(2,1)} fusion(bf16[2048,2048]{0,1:T(8,128)(2,1)} %constant_dynamic-update-slice_fusion.11, bf16[128,2048]{0,1:T(8,128)(2,1)} %collective-permute-done.8, s32[]{:T(128)S(6)} %select_n.120), kind=kLoop, calls=%fused_computation.39 | loop fusion | bytes 1048580 | tf_op jit(solution)/shard_map/dynamic_update_slice | solution.py:146
  27.2 0.9 %constant_dynamic-update-slice_fusion.9 = bf16[2048,2048]{0,1:T(8,128)(2,1)} fusion(bf16[2048,2048]{0,1:T(8,128)(2,1)} %constant_dynamic-update-slice_fusion.10, bf16[128,2048]{0,1:T(8,128)(2,1)S(1)} %collective-permute-done.2, s32[]{:T(128)S(6)} %select_n.126), kind=kLoop, calls=%fused_computation.38 | loop fusion | bytes 1048580 | tf_op jit(solution)/shard_map/dynamic_update_slice | solution.py:146
  28.1 8.7 %shard_map.64 = bf16[512,1024]{1,0:T(8,128)(2,1)} custom-call(f32[128,384]{1,0:T(8,128)} %pad_convert_fusion.1.fw_ref, f32[1,2048]{1,0:T(1,128)} %bitcast.34, f32[3,3,2048]{2,1,0:T(4,128)} %bitcast.27, bf16[3,2,2048]{2,1,0:T(2,128)(2,1)} %bitcast.32, bf16[128,2048]{1,0:T(8,128)(2,1)} %copy-done.1, bf16[512,6144]{1,0:T(8,128)(2,1)} %carrier_ref.2, ...), custom_call_target="tpu_custom_call" | custom-call | tf_op jit(solution)/shard_map/pallas_call | solution.py:95
  36.9 2.1 %collective-permute-start.6 = (bf16[128,2048]{0,1:T(8,128)(2,1)}, bf16[128,2048]{0,1:T(8,128)(2,1)}, u32[]{:S(2)}, u32[]{:S(2)}) collective-permute-start(bf16[128,2048]{0,1:T(8,128)(2,1)} %collective-permute-done.4), channel_id=1, source_target_pairs={{0,4},{4,8},{8,12},{12,14},{14,10},{10,6},{6,2},{2,0},{1,5},{5,9},... | collective-permute-start | bytes 1572872 | tf_op jit(solution)/shard_map/ppermute | solution.py:184
  39.5 0.9 %constant_dynamic-update-slice_fusion.8 = bf16[2048,2048]{0,1:T(8,128)(2,1)} fusion(bf16[2048,2048]{0,1:T(8,128)(2,1)} %constant_dynamic-update-slice_fusion.9, bf16[128,2048]{0,1:T(8,128)(2,1)S(1)} %collective-permute-done.9, s32[]{:T(128)S(6)} %select_n.127), kind=kLoop, calls=%fused_computation.37 | loop fusion | bytes 1048580 | tf_op jit(solution)/shard_map/dynamic_update_slice | solution.py:146
  40.4 0.9 %constant_dynamic-update-slice_fusion.7 = bf16[2048,2048]{0,1:T(8,128)(2,1)} fusion(bf16[2048,2048]{0,1:T(8,128)(2,1)} %constant_dynamic-update-slice_fusion.8, bf16[128,2048]{0,1:T(8,128)(2,1)S(1)} %collective-permute-done.3, s32[]{:T(128)S(6)} %select_n.130), kind=kLoop, calls=%fused_computation.36 | loop fusion | bytes 1048580 | tf_op jit(solution)/shard_map/dynamic_update_slice | solution.py:146
  41.4 0.9 %constant_dynamic-update-slice_fusion.6 = bf16[2048,2048]{0,1:T(8,128)(2,1)} fusion(bf16[2048,2048]{0,1:T(8,128)(2,1)} %constant_dynamic-update-slice_fusion.7, bf16[128,2048]{0,1:T(8,128)(2,1)S(1)} %collective-permute-done.10, s32[]{:T(128)S(6)} %select_n.131), kind=kLoop, calls=%fused_computation.35 | loop fusion | bytes 1048580 | tf_op jit(solution)/shard_map/dynamic_update_slice | solution.py:146
  43.1 8.8 %shard_map.65 = bf16[512,1024]{1,0:T(8,128)(2,1)} custom-call(f32[128,384]{1,0:T(8,128)} %pad_convert_fusion.fw_ref, f32[1,2048]{1,0:T(1,128)} %bitcast.35, f32[3,3,2048]{2,1,0:T(4,128)} %bitcast.28, bf16[3,2,2048]{2,1,0:T(2,128)(2,1)} %bitcast.33, bf16[128,2048]{1,0:T(8,128)(2,1)} %copy-done.1, bf16[512,6144]{1,0:T(8,128)(2,1)} %carrier_ref.2, ...), custom_call_target="tpu_custom_call" | custom-call | tf_op jit(solution)/shard_map/pallas_call | solution.py:95
  51.8 1.4 %pad_maximum_fusion = bf16[512,2048]{1,0:T(8,128)(2,1)S(1)} fusion(bf16[512,1024]{1,0:T(8,128)(2,1)} %shard_map.65, bf16[512,1024]{1,0:T(8,128)(2,1)S(1)} %copy-done), kind=kLoop, calls=%fused_computation.1 | loop fusion | flops 4194304 | bytes 4194304 | tf_op jit(solution)/shard_map/concatenate | solution.py:188
  53.2 1.9 %constant_dynamic-update-slice_fusion.5 = bf16[2048,2048]{0,1:T(8,128)(2,1)} fusion(bf16[2048,2048]{0,1:T(8,128)(2,1)} %constant_dynamic-update-slice_fusion.6, bf16[128,2048]{0,1:T(8,128)(2,1)} %collective-permute-done.4, s32[]{:T(128)S(6)} %select_n.134), kind=kLoop, calls=%fused_computation.34 | loop fusion | bytes 1048580 | tf_op jit(solution)/shard_map/dynamic_update_slice | solution.py:146
  55.2 1.0 %slice.73 = bf16[128,1024]{0,1:T(8,128)(2,1)S(1)} slice(bf16[128,2048]{0,1:T(8,128)(2,1)} %collective-permute-done.6), slice={[0:128], [0:1024]} | slice | bytes 524288 | tf_op jit(solution)/shard_map/slice | solution.py:195
  56.1 2.0 %collective-permute-start.15 = (bf16[128,1024]{0,1:T(8,128)(2,1)S(1)}, bf16[128,1024]{0,1:T(8,128)(2,1)S(1)}, u32[]{:S(2)}, u32[]{:S(2)}) collective-permute-start(bf16[128,1024]{0,1:T(8,128)(2,1)S(1)} %slice.73), channel_id=1, source_target_pairs={{0,4},{4,8},{8,12},{12,14},{14,10},{10,6},{6,2},{2,0},{1,5},{5,9},... | collective-permute-start | bytes 786440 | tf_op jit(solution)/shard_map/ppermute | solution.py:195
  58.2 1.0 %slice.74 = bf16[128,1024]{0,1:T(8,128)(2,1)S(1)} slice(bf16[128,2048]{0,1:T(8,128)(2,1)} %collective-permute-done.7), slice={[0:128], [1024:2048]} | slice | bytes 524288 | tf_op jit(solution)/shard_map/slice | solution.py:196
  59.3 1.9 %constant_dynamic-update-slice_fusion.4 = bf16[2048,2048]{0,1:T(8,128)(2,1)} fusion(bf16[2048,2048]{0,1:T(8,128)(2,1)} %constant_dynamic-update-slice_fusion.5, bf16[128,2048]{0,1:T(8,128)(2,1)} %collective-permute-done.11, s32[]{:T(128)S(6)} %select_n.135), kind=kLoop, calls=%fused_computation.33 | loop fusion | bytes 1048580 | tf_op jit(solution)/shard_map/dynamic_update_slice | solution.py:146
  61.2 0.9 %constant_dynamic-update-slice_fusion.3 = bf16[2048,2048]{0,1:T(8,128)(2,1)} fusion(bf16[2048,2048]{0,1:T(8,128)(2,1)} %constant_dynamic-update-slice_fusion.4, bf16[128,2048]{0,1:T(8,128)(2,1)S(1)} %collective-permute-done.5, s32[]{:T(128)S(6)} %select_n.138), kind=kLoop, calls=%fused_computation.32 | loop fusion | bytes 1048580 | tf_op jit(solution)/shard_map/dynamic_update_slice | solution.py:146
  62.1 0.9 %constant_dynamic-update-slice_fusion.2 = bf16[2048,2048]{0,1:T(8,128)(2,1)} fusion(bf16[2048,2048]{0,1:T(8,128)(2,1)} %constant_dynamic-update-slice_fusion.3, bf16[128,2048]{0,1:T(8,128)(2,1)S(1)} %collective-permute-done.12, s32[]{:T(128)S(6)} %select_n.139), kind=kLoop, calls=%fused_computation.31 | loop fusion | bytes 1048580 | tf_op jit(solution)/shard_map/dynamic_update_slice | solution.py:146
  63.0 6.9 %fusion.22 = f32[512,2048]{1,0:T(8,128)S(1)} fusion(bf16[512,2048]{1,0:T(8,128)(2,1)S(1)} %pad_maximum_fusion, bf16[2048,2048]{0,1:T(8,128)(2,1)} %constant_dynamic-update-slice_fusion.2), kind=kOutput, calls=%fused_computation.45 | convolution fusion | flops 4294967296 | bytes 14680064 | tf_op jit(solution)/shard_map/dot_general | solution.py:198
  70.6 1.9 %convolution_dynamic-update-slice_fusion.2 = f32[512,2048]{1,0:T(8,128)S(1)} fusion(f32[512,2048]{1,0:T(8,128)S(1)} %fusion.22, s32[]{:T(128)S(6)} %select_n.144, bf16[512,2048]{1,0:T(8,128)(2,1)S(1)} %pad_maximum_fusion, bf16[128,2048]{0,1:T(8,128)(2,1)S(1)} %collective-permute-done.13, bf16[128,2048]{0,1:T(8,128)(2,1)} %collective-permute-done.6, pred[]{:T(512)S(6)} %eq.18), kind=kOutput, calls=%fused_computation.4 | convolution fusion | flops 541589504 | bytes 3670021 | tf_op jit(solution)/shard_map/dot_general | solution.py:203
  72.6 1.9 %convolution_dynamic-update-slice_fusion.1 = f32[512,2048]{1,0:T(8,128)S(1)} fusion(f32[512,2048]{1,0:T(8,128)S(1)} %convolution_dynamic-update-slice_fusion.2, s32[]{:T(128)S(6)} %select_n.148, bf16[512,2048]{1,0:T(8,128)(2,1)S(1)} %pad_maximum_fusion, bf16[128,2048]{0,1:T(8,128)(2,1)S(1)} %collective-permute-done.14, ...), kind=kOutput, calls=%fused_computation.3 | convolution fusion | flops 541589504 | bytes 3670021 | tf_op jit(solution)/shard_map/dot_general | solution.py:203
  75.3 0.8 %copy-done.2 = bf16[512,2048]{1,0:T(8,128)(2,1)S(1)} copy-done((bf16[512,2048]{1,0:T(8,128)(2,1)S(1)}, bf16[512,2048]{1,0:T(8,128)(2,1)}, u32[]{:S(2)}) %copy-start.2) | copy-done | bytes 2097176
  76.1 2.1 %add_convert_fusion = bf16[512,2048]{1,0:T(8,128)(2,1)} fusion(f32[512,2048]{1,0:T(8,128)S(1)} %convolution_dynamic-update-slice_fusion, bf16[512,2048]{1,0:T(8,128)(2,1)S(1)} %copy-done.2), kind=kLoop, calls=%fused_computation | loop fusion | flops 3145728 | bytes 8388608 | tf_op jit(solution)/shard_map/convert_element_type | solution.py:205
  (46 shorter events, 3.6 us)
Async XLA Ops:
  0.0 19.2 %collective-permute-start.2 = (bf16[128,2048]{0,1:T(8,128)(2,1)}, bf16[128,2048]{0,1:T(8,128)(2,1)S(1)}, u32[]{:S(2)}, u32[]{:S(2)}) collective-permute-start(bf16[128,2048]{0,1:T(8,128)(2,1)} %bitcast.29), channel_id=1, source_target_pairs={{0,4},{4,8},{8,12},{12,14},{14,10},{10,6},{6,2},{2,0},{1,5},{5,9},... | collective-permute-start | bytes 1572872 | tf_op jit(solution)/shard_map/ppermute | solution.py:158
  3.0 16.1 %collective-permute-start.3 = (bf16[128,2048]{0,1:T(8,128)(2,1)}, bf16[128,2048]{0,1:T(8,128)(2,1)S(1)}, u32[]{:S(2)}, u32[]{:S(2)}) collective-permute-start(bf16[128,2048]{0,1:T(8,128)(2,1)} %bitcast.30), channel_id=1, source_target_pairs={{4,0},{8,4},{12,8},{14,12},{10,14},{6,10},{2,6},{0,2},{5,1},{9,5},... | collective-permute-start | bytes 1572872 | tf_op jit(solution)/shard_map/ppermute | solution.py:159
  6.9 12.3 %collective-permute-start = (bf16[128,2048]{1,0:T(8,128)(2,1)S(1)}, bf16[128,2048]{1,0:T(8,128)(2,1)S(1)}, u32[]{:S(2)}, u32[]{:S(2)}) collective-permute-start(bf16[128,2048]{1,0:T(8,128)(2,1)S(1)} %multiply_convert_fusion), channel_id=1, source_target_pairs={{0,1},{1,2},{2,3},{3,4},{4,5},{5,6},{6,7},{7,8},{8,9},{9,10},{10,1... | collective-permute-start | bytes 1572872 | tf_op jit(solution)/shard_map/ppermute | solution.py:22
  8.4 16.9 %collective-permute-start.8 = (bf16[128,2048]{0,1:T(8,128)(2,1)}, bf16[128,2048]{0,1:T(8,128)(2,1)}, u32[]{:S(2)}, u32[]{:S(2)}) collective-permute-start(bf16[128,2048]{0,1:T(8,128)(2,1)} %bitcast.31), channel_id=1, source_target_pairs={{0,1},{1,0},{2,3},{3,2},{4,5},{5,4},{6,7},{7,6},{8,9},{9,8},{10,11... | collective-permute-start | bytes 1572872 | tf_op jit(solution)/shard_map/ppermute | solution.py:144
  11.9 7.3 %collective-permute-start.1 = (bf16[2,6144]{1,0:T(2,128)(2,1)S(1)}, bf16[2,6144]{1,0:T(2,128)(2,1)S(1)}, u32[]{:S(2)}, u32[]{:S(2)}) collective-permute-start(bf16[2,6144]{1,0:T(2,128)(2,1)S(1)} %slice.72), channel_id=1, source_target_pairs={{0,1},{1,2},{2,3},{3,4},{4,5},{5,6},{6,7},{7,8},{8,9},{9,10},{10,1... | collective-permute-start | bytes 73736 | tf_op jit(solution)/shard_map/ppermute | solution.py:22
  13.8 4.3 %copy-start.3 = (bf16[2048,128]{1,0:T(8,128)(2,1)S(1)}, bf16[2048,128]{1,0:T(8,128)(2,1)}, u32[]{:S(2)}) copy-start(bf16[2048,128]{1,0:T(8,128)(2,1)} %param.11) | copy-start | bytes 1572868
  13.8 5.2 %copy-start.4 = (bf16[128,128]{1,0:T(8,128)(2,1)S(1)}, bf16[128,128]{1,0:T(8,128)(2,1)}, u32[]{:S(2)}) copy-start(bf16[128,128]{1,0:T(8,128)(2,1)} %param.9) | copy-start | bytes 98308
  19.1 9.0 %copy-start.5 = (bf16[2,6144]{1,0:T(2,128)(2,1)}, bf16[2,6144]{1,0:T(2,128)(2,1)S(1)}, u32[]{:S(2)}) copy-start(bf16[2,6144]{1,0:T(2,128)(2,1)S(1)} %collective-permute-done.1) | copy-start | bytes 73732
  19.2 9.0 %copy-start.1 = (bf16[128,2048]{1,0:T(8,128)(2,1)}, bf16[128,2048]{1,0:T(8,128)(2,1)S(1)}, u32[]{:S(2)}) copy-start(bf16[128,2048]{1,0:T(8,128)(2,1)S(1)} %collective-permute-done.halo_ref) | copy-start | bytes 1572868
  19.2 17.6 %collective-permute-start.4 = (bf16[128,2048]{0,1:T(8,128)(2,1)S(1)}, bf16[128,2048]{0,1:T(8,128)(2,1)}, u32[]{:S(2)}, u32[]{:S(2)}) collective-permute-start(bf16[128,2048]{0,1:T(8,128)(2,1)S(1)} %collective-permute-done.2), channel_id=1, source_target_pairs={{0,4},{4,8},{8,12},{12,14},{14,10},{10,6},{6,2},{2,0},{1,5},{5,9},... | collective-permute-start | bytes 1572872 | tf_op jit(solution)/shard_map/ppermute | solution.py:158
  24.0 12.8 %collective-permute-start.5 = (bf16[128,2048]{0,1:T(8,128)(2,1)S(1)}, bf16[128,2048]{0,1:T(8,128)(2,1)S(1)}, u32[]{:S(2)}, u32[]{:S(2)}) collective-permute-start(bf16[128,2048]{0,1:T(8,128)(2,1)S(1)} %collective-permute-done.3), channel_id=1, source_target_pairs={{4,0},{8,4},{12,8},{14,12},{10,14},{6,10},{2,6},{0,2},{5,1},{9,5},... | collective-permute-start | bytes 1572872 | tf_op jit(solution)/shard_map/ppermute | solution.py:159
  24.0 15.0 %collective-permute-start.9 = (bf16[128,2048]{0,1:T(8,128)(2,1)S(1)}, bf16[128,2048]{0,1:T(8,128)(2,1)S(1)}, u32[]{:S(2)}, u32[]{:S(2)}) collective-permute-start(bf16[128,2048]{0,1:T(8,128)(2,1)S(1)} %collective-permute-done.2), channel_id=1, source_target_pairs={{0,1},{1,0},{2,3},{3,2},{4,5},{5,4},{6,7},{7,6},{8,9},{9,8},{10,11... | collective-permute-start | bytes 1572872 | tf_op jit(solution)/shard_map/ppermute | solution.py:144
  24.8 16.6 %collective-permute-start.10 = (bf16[128,2048]{0,1:T(8,128)(2,1)S(1)}, bf16[128,2048]{0,1:T(8,128)(2,1)S(1)}, u32[]{:S(2)}, u32[]{:S(2)}) collective-permute-start(bf16[128,2048]{0,1:T(8,128)(2,1)S(1)} %collective-permute-done.3), channel_id=1, source_target_pairs={{0,1},{1,0},{2,3},{3,2},{4,5},{5,4},{6,7},{7,6},{8,9},{9,8},{10,11... | collective-permute-start | bytes 1572872 | tf_op jit(solution)/shard_map/ppermute | solution.py:144
  36.9 18.2 %collective-permute-start.6 = (bf16[128,2048]{0,1:T(8,128)(2,1)}, bf16[128,2048]{0,1:T(8,128)(2,1)}, u32[]{:S(2)}, u32[]{:S(2)}) collective-permute-start(bf16[128,2048]{0,1:T(8,128)(2,1)} %collective-permute-done.4), channel_id=1, source_target_pairs={{0,4},{4,8},{8,12},{12,14},{14,10},{10,6},{6,2},{2,0},{1,5},{5,9},... | collective-permute-start | bytes 1572872 | tf_op jit(solution)/shard_map/ppermute | solution.py:184
  39.0 16.2 %collective-permute-start.7 = (bf16[128,2048]{0,1:T(8,128)(2,1)S(1)}, bf16[128,2048]{0,1:T(8,128)(2,1)}, u32[]{:S(2)}, u32[]{:S(2)}) collective-permute-start(bf16[128,2048]{0,1:T(8,128)(2,1)S(1)} %collective-permute-done.5), channel_id=1, source_target_pairs={{4,0},{8,4},{12,8},{14,12},{10,14},{6,10},{2,6},{0,2},{5,1},{9,5},... | collective-permute-start | bytes 1572872 | tf_op jit(solution)/shard_map/ppermute | solution.py:185
  39.0 20.3 %collective-permute-start.11 = (bf16[128,2048]{0,1:T(8,128)(2,1)}, bf16[128,2048]{0,1:T(8,128)(2,1)}, u32[]{:S(2)}, u32[]{:S(2)}) collective-permute-start(bf16[128,2048]{0,1:T(8,128)(2,1)} %collective-permute-done.4), channel_id=1, source_target_pairs={{0,1},{1,0},{2,3},{3,2},{4,5},{5,4},{6,7},{7,6},{8,9},{9,8},{10,11... | collective-permute-start | bytes 1572872 | tf_op jit(solution)/shard_map/ppermute | solution.py:144
  39.0 23.1 %collective-permute-start.12 = (bf16[128,2048]{0,1:T(8,128)(2,1)S(1)}, bf16[128,2048]{0,1:T(8,128)(2,1)S(1)}, u32[]{:S(2)}, u32[]{:S(2)}) collective-permute-start(bf16[128,2048]{0,1:T(8,128)(2,1)S(1)} %collective-permute-done.5), channel_id=1, source_target_pairs={{0,1},{1,0},{2,3},{3,2},{4,5},{5,4},{6,7},{7,6},{8,9},{9,8},{10,11... | collective-permute-start | bytes 1572872 | tf_op jit(solution)/shard_map/ppermute | solution.py:144
  43.1 8.8 %copy-start = (bf16[512,1024]{1,0:T(8,128)(2,1)S(1)}, bf16[512,1024]{1,0:T(8,128)(2,1)}, u32[]{:S(2)}) copy-start(bf16[512,1024]{1,0:T(8,128)(2,1)} %shard_map.64) | copy-start | bytes 3145732
  56.1 14.3 %collective-permute-start.15 = (bf16[128,1024]{0,1:T(8,128)(2,1)S(1)}, bf16[128,1024]{0,1:T(8,128)(2,1)S(1)}, u32[]{:S(2)}, u32[]{:S(2)}) collective-permute-start(bf16[128,1024]{0,1:T(8,128)(2,1)S(1)} %slice.73), channel_id=1, source_target_pairs={{0,4},{4,8},{8,12},{12,14},{14,10},{10,6},{6,2},{2,0},{1,5},{5,9},... | collective-permute-start | bytes 786440 | tf_op jit(solution)/shard_map/ppermute | solution.py:195
  59.1 11.4 %collective-permute-start.16 = (bf16[128,1024]{0,1:T(8,128)(2,1)S(1)}, bf16[128,1024]{0,1:T(8,128)(2,1)S(1)}, u32[]{:S(2)}, u32[]{:S(2)}) collective-permute-start(bf16[128,1024]{0,1:T(8,128)(2,1)S(1)} %slice.74), channel_id=1, source_target_pairs={{4,0},{8,4},{12,8},{14,12},{10,14},{6,10},{2,6},{0,2},{5,1},{9,5},... | collective-permute-start | bytes 786440 | tf_op jit(solution)/shard_map/ppermute | solution.py:196
  59.2 11.4 %collective-permute-start.13 = (bf16[128,2048]{0,1:T(8,128)(2,1)}, bf16[128,2048]{0,1:T(8,128)(2,1)S(1)}, u32[]{:S(2)}, u32[]{:S(2)}) collective-permute-start(bf16[128,2048]{0,1:T(8,128)(2,1)} %collective-permute-done.6), channel_id=1, source_target_pairs={{0,1},{1,0},{2,3},{3,2},{4,5},{5,4},{6,7},{7,6},{8,9},{9,8},{10,11... | collective-permute-start | bytes 1572872 | tf_op jit(solution)/shard_map/ppermute | solution.py:201
  69.9 2.7 %collective-permute-start.14 = (bf16[128,2048]{0,1:T(8,128)(2,1)}, bf16[128,2048]{0,1:T(8,128)(2,1)S(1)}, u32[]{:S(2)}, u32[]{:S(2)}) collective-permute-start(bf16[128,2048]{0,1:T(8,128)(2,1)} %collective-permute-done.7), channel_id=1, source_target_pairs={{0,1},{1,0},{2,3},{3,2},{4,5},{5,4},{6,7},{7,6},{8,9},{9,8},{10,11... | collective-permute-start | bytes 1572872 | tf_op jit(solution)/shard_map/ppermute | solution.py:201
  70.5 4.0 %collective-permute-start.17 = (bf16[128,2048]{0,1:T(8,128)(2,1)S(1)}, bf16[128,2048]{0,1:T(8,128)(2,1)S(1)}, u32[]{:S(2)}, u32[]{:S(2)}) collective-permute-start(bf16[128,2048]{0,1:T(8,128)(2,1)S(1)} %constant_dynamic-update-slice_fusion), channel_id=1, source_target_pairs={{0,1},{1,0},{2,3},{3,2},{4,5},{5,4},{6,7},{7,6},{8,9},{9,8},{10,11... | collective-permute-start | bytes 1572872 | tf_op jit(solution)/shard_map/ppermute | solution.py:201
  74.5 1.6 %copy-start.2 = (bf16[512,2048]{1,0:T(8,128)(2,1)S(1)}, bf16[512,2048]{1,0:T(8,128)(2,1)}, u32[]{:S(2)}) copy-start(bf16[512,2048]{1,0:T(8,128)(2,1)} %param.6) | copy-start | bytes 6291460

commit v19 on v17

--- a/solution.py
+++ b/solution.py
@@ -80,17 +80,23 @@
         out_ref[BLOCK * b : BLOCK * (b + 1), :] = (gate * (acc + direct)).astype(out_ref.dtype)
 
 
-def hyena_gate(halo, edge, projected, short_filter, long_filter, conv_bias, part, parts):
-    groups, taps = long_filter.shape
+def gate_operands(edge, short_filter, long_filter):
+    taps = long_filter.shape[1]
+    channels = edge.shape[1]
+    fw = jnp.pad(long_filter[:, ::-1].astype(jnp.float32), ((0, 0), (1, 3 * BLOCK - 1 - taps)))
+    edges = edge.reshape(2, 3, channels).transpose(1, 0, 2)
+    filters = short_filter.reshape(3, 3, channels).transpose(1, 0, 2)
+    return fw, edges, filters
+
+
+def hyena_gate(halo, projected, fw, edges, filters, conv_bias, part, parts):
+    groups = fw.shape[0]
     row_count = projected.shape[0]
     channels = halo.shape[1]
     per_tile = LANES // (channels // groups)
     tiles = channels // LANES
     share = tiles // parts
     first = part * share
-    fw = jnp.pad(long_filter[:, ::-1].astype(jnp.float32), ((0, 0), (1, 3 * BLOCK - 1 - taps)))
-    edges = edge.reshape(2, 3, channels).transpose(1, 0, 2)
-    filters = short_filter.reshape(3, 3, channels).transpose(1, 0, 2)
     column = lambda k: pl.BlockSpec((row_count, LANES), lambda j: (0, first + j + k * tiles))
     return pl.pallas_call(
         _gate_kernel,
@@ -171,13 +177,14 @@
         short_mixed(tail[:2, k * channels : (k + 1) * channels], tail[2:, k * channels : (k + 1) * channels], short_filter[:, k * channels : (k + 1) * channels])
         for k in (1, 2)
     ]
-    halo = shifted(carried_of(*tail_mixed), 1)
-    edge = shifted(projected[row_count - 2 :], 1)
+    packed = jnp.concatenate([carried_of(*tail_mixed), projected[row_count - 2 :].reshape(-1, channels)], axis=0)
+    packed = shifted(packed, 1)
+    halo, edge = packed[:BLOCK], packed[BLOCK:]
     halo, edge, ahead, behind = lax.optimization_barrier((halo, edge, ahead, behind))
     if ring and steps >= 2:
         weight, ahead, behind = ring_step(2, weight, ahead, behind)
 
-    inputs = (halo, edge, projected, short_filter, long_filter, conv_bias)
+    inputs = (halo, projected) + gate_operands(edge, short_filter, long_filter) + (conv_bias,)
     first = hyena_gate(*inputs, 0, 2)
     if ring:
         first, ahead, behind, inputs = lax.optimization_barrier((first, ahead, behind, inputs))

time: 78.5 us -> 82.2 us (1.047)
  local copies, waits for them, and re-layouts: 23 us -> 25.6 us
  waiting for transfers between devices: 1.83 us -> 3.13 us
    ppermute x3, starting transfers between devices: 9.55 us -> 12.8 us  [ring_step(): ahead = lax.ppermute(ahead, 'chip', forward)]
    ppermute x2 -> x1, starting transfers between devices: 3.42 us -> 2.08 us  [shifted(): return lax.ppermute(block, CTX, route)]
    dynamic_update_slice x14, local copies, waits for them, and re-layouts: 15.7 us -> 16.8 us  [place(): lax.dynamic_update_slice(weight, part, ((owner_chip * 2 + k) * width, row))]
    ppermute x7, starting transfers between devices: 4.14 us -> 3.1 us  [place(): other = lax.ppermute(piece, 'core', swap)]
    ppermute x1, waiting for transfers between devices: 0.01 us -> 0.91 us  [on_device(): ahead = lax.ppermute(ahead[:, :half], 'chip', forward)]
    slice x1 -> x3, local copies, waits for them, and re-layouts: 0.92 us -> 1.75 us  [the longest x1 0.92 us: on_device(): projected[row_count - 2:].reshape(-1, channels)]
  transfers between devices with their start and end apart: 18 -> 17, of which waited for: 2 -> 3; matrix products, arithmetic and copies ran while one was open for 45% -> 45% of each run, Pallas kernels for 22% -> 21%
where the time goes in v19:
time: 82.2 us; the launch traced here: 81.3 us
  local copies, waits for them, and re-layouts  25.6 us (31%)
  starting transfers between devices  20.3 us (25%)
  Pallas kernels  17.4 us (21%)
  matrix products  7.61 us (9%)
  other arithmetic  7.16 us (9%)
  waiting for transfers between devices  3.13 us (4%)
    pallas_call x2, Pallas kernels, hyena_gate(): pl.pallas_call(_gate_kernel, grid=(share,), in_specs=[pl.BlockSpec((per_t...  17.4 us
    dynamic_update_slice x14, local copies, waits for them, and re-layouts, place(): lax.dynamic_update_slice(weight, part, ((owner_chip * 2 + k) * width, row))  16.8 us
    ppermute x3, starting transfers between devices, ring_step(): ahead = lax.ppermute(ahead, 'chip', forward)  12.8 us
    dot_general x1, matrix products, on_device(): lax.dot_general(gated, weight, (((1,), (1,)), ((), ())), preferred_elemen...  6.88 us
    broadcast_in_dim x1, local copies, waits for them, and re-layouts, on_device(): weight = jnp.zeros((chips * 2 * width, channels), out_weight.dtype)  4.31 us
    ppermute x7, starting transfers between devices, place(): other = lax.ppermute(piece, 'core', swap)  3.1 us
    convert_element_type x1, other arithmetic, carried_of(): return (second * carrier).astype(jnp.bfloat16)  2.9 us
    ppermute x1, starting transfers between devices, on_device(): ahead = lax.ppermute(ahead[:, :half], 'chip', forward)  2.08 us
  transfers between devices with their start and end apart: 17, of which 3 were waited for; matrix products, arithmetic and copies ran while one was open for 45% of the time, Pallas kernels for 21%

profile of v19, /device:TPU:0, one launch (start us, length us, event | category | flops | bytes accessed | tf_op | source)
XLA Modules:
  0.0 81.3 jit_solution(2383810524311051818)
XLA Ops:
  0.5 2.6 %collective-permute-start.1 = (bf16[128,2048]{0,1:T(8,128)(2,1)}, bf16[128,2048]{0,1:T(8,128)(2,1)S(1)}, u32[]{:S(2)}, u32[]{:S(2)}) collective-permute-start(bf16[128,2048]{0,1:T(8,128)(2,1)} %bitcast.22), channel_id=1, source_target_pairs={{0,4},{4,8},{8,12},{12,14},{14,10},{10,6},{6,2},{2,0},{1,5},{5,9},... | collective-permute-start | bytes 1572872 | tf_op jit(solution)/shard_map/ppermute | solution.py:164
  3.1 1.0 %fusion.7 = (f32[1,2048]{1,0:T(1,128)S(1)}, f32[1,2048]{1,0:T(1,128)S(1)}, f32[1,2048]{1,0:T(1,128)S(1)}, f32[1,2048]{1,0:T(1,128)S(1)}, f32[1,2048]{1,0:T(1,128)S(1)}, /*index=5*/f32[1,2048]{1,0:T(1,128)S(1)}) fusion(f32[3,6144]{1,0:T(4,128)} %param.8), kind=kLoop, calls=%fused_computation.31 | loop fusion | bytes 98304 | tf_op jit(solution)/shard_map/slice | solution.py:34
  4.1 0.9 %slice.78 = bf16[2,6144]{1,0:T(2,128)(2,1)S(1)} slice(bf16[512,6144]{1,0:T(8,128)(2,1)} %carrier_ref.2), slice={[510:512], [0:6144]} | slice | bytes 49152 | tf_op jit(solution)/shard_map/slice | solution.py:180
  5.0 2.9 %multiply_convert_fusion = bf16[128,2048]{1,0:T(8,128)(2,1)S(1)} fusion(bf16[512,6144]{1,0:T(8,128)(2,1)} %carrier_ref.2, f32[2048]{0:T(1024)S(1)} %bitcast.32, f32[2048]{0:T(1024)S(1)} %bitcast.33, f32[2048]{0:T(1024)S(1)} %bitcast.29, f32[2048]{0:T(1024)S(1)} %bitcast.30, f32[2048]{0:T(1024)S(1)} %bitcast.31, f32[2048]{0:T(1024)S(1)} %bitcast.28), kind=kLoop, calls=%fused_computation.9 | loop fusion | flops 4718592 | bytes 3719168 | tf_op jit(solution)/shard_map/convert_element_type | solution.py:128
  8.0 2.1 %collective-permute-start = (bf16[134,2048]{1,0:T(8,128)(2,1)S(1)}, bf16[134,2048]{1,0:T(8,128)(2,1)S(1)}, u32[]{:S(2)}, u32[]{:S(2)}) collective-permute-start(bf16[134,2048]{1,0:T(8,128)(2,1)S(1)} %pad_maximum_fusion.1), channel_id=1, source_target_pairs={{0,1},{1,2},{2,3},{3,4},{4,5},{5,6},{6,7},{7,8},{8,9},{9,10},{10,1... | collective-permute-start | bytes 1646600 | tf_op jit(solution)/shard_map/ppermute | solution.py:22
  10.1 4.3 %broadcast_in_dim.3 = bf16[2048,2048]{0,1:T(8,128)(2,1)} broadcast(bf16[]{:T(256)} %constant.75.clone.1), dimensions={} | broadcast | bytes 8388610 | tf_op jit(solution)/shard_map/broadcast_in_dim | solution.py:147
  14.4 0.9 %constant_dynamic-update-slice_fusion.15 = bf16[2048,2048]{0,1:T(8,128)(2,1)} fusion(bf16[2048,2048]{0,1:T(8,128)(2,1)} %broadcast_in_dim.3, s32[]{:T(128)S(6)} %select_n.117, bf16[2048,128]{1,0:T(8,128)(2,1)S(1)} %copy-done.2), kind=kLoop, calls=%fused_computation.29 | loop fusion | bytes 1048580 | tf_op jit(solution)/shard_map/dynamic_update_slice | solution.py:152
  15.8 1.6 %collective-permute-start.8 = (bf16[128,2048]{0,1:T(8,128)(2,1)S(1)}, bf16[128,2048]{0,1:T(8,128)(2,1)S(1)}, u32[]{:S(2)}, u32[]{:S(2)}) collective-permute-start(bf16[128,2048]{0,1:T(8,128)(2,1)S(1)} %collective-permute-done.1), channel_id=1, source_target_pairs={{0,1},{1,0},{2,3},{3,2},{4,5},{5,4},{6,7},{7,6},{8,9},{9,8},{10,11... | collective-permute-start | bytes 1572872 | tf_op jit(solution)/shard_map/ppermute | solution.py:150
  18.2 1.9 %constant_dynamic-update-slice_fusion.14 = bf16[2048,2048]{0,1:T(8,128)(2,1)} fusion(bf16[2048,2048]{0,1:T(8,128)(2,1)} %constant_dynamic-update-slice_fusion.15, bf16[128,2048]{0,1:T(8,128)(2,1)} %collective-permute-done.7, s32[]{:T(128)S(6)} %select_n.118), kind=kLoop, calls=%fused_computation.28 | loop fusion | bytes 1048580 | tf_op jit(solution)/shard_map/dynamic_update_slice | solution.py:152
  20.9 4.6 %collective-permute-start.3 = (bf16[128,2048]{0,1:T(8,128)(2,1)S(1)}, bf16[128,2048]{0,1:T(8,128)(2,1)}, u32[]{:S(2)}, u32[]{:S(2)}) collective-permute-start(bf16[128,2048]{0,1:T(8,128)(2,1)S(1)} %collective-permute-done.1), channel_id=1, source_target_pairs={{0,4},{4,8},{8,12},{12,14},{14,10},{10,6},{6,2},{2,0},{1,5},{5,9},... | collective-permute-start | bytes 1572872 | tf_op jit(solution)/shard_map/ppermute | solution.py:164
  25.5 0.9 %constant_dynamic-update-slice_fusion.13 = bf16[2048,2048]{0,1:T(8,128)(2,1)} fusion(bf16[2048,2048]{0,1:T(8,128)(2,1)} %constant_dynamic-update-slice_fusion.14, bf16[128,2048]{0,1:T(8,128)(2,1)S(1)} %collective-permute-done.1, s32[]{:T(128)S(6)} %select_n.124), kind=kLoop, calls=%fused_computation.27 | loop fusion | bytes 1048580 | tf_op jit(solution)/shard_map/dynamic_update_slice | solution.py:152
  27.1 8.7 %shard_map.64 = bf16[512,1024]{1,0:T(8,128)(2,1)} custom-call(f32[128,384]{1,0:T(8,128)} %pad_convert_fusion.fw_ref, f32[1,2048]{1,0:T(1,128)} %bitcast.26, f32[3,3,2048]{2,1,0:T(4,128)} %bitcast.19, bf16[3,2,2048]{2,1,0:T(2,128)(2,1)} %bitcast.24, bf16[128,2048]{1,0:T(8,128)(2,1)} %slice.83.halo_ref, bf16[512,6144]{1,0:T(8,128)(2,1)} %carrier_ref.2, ...), custom_call_target="tpu_custom_call" | custom-call | tf_op jit(solution)/shard_map/pallas_call | solution.py:101
  35.7 0.9 %constant_dynamic-update-slice_fusion.12 = bf16[2048,2048]{0,1:T(8,128)(2,1)} fusion(bf16[2048,2048]{0,1:T(8,128)(2,1)} %constant_dynamic-update-slice_fusion.13, bf16[128,2048]{0,1:T(8,128)(2,1)S(1)} %collective-permute-done.8, s32[]{:T(128)S(6)} %select_n.125), kind=kLoop, calls=%fused_computation.26 | loop fusion | bytes 1048580 | tf_op jit(solution)/shard_map/dynamic_update_slice | solution.py:152
  36.6 0.9 %constant_dynamic-update-slice_fusion.11 = bf16[2048,2048]{0,1:T(8,128)(2,1)} fusion(bf16[2048,2048]{0,1:T(8,128)(2,1)} %constant_dynamic-update-slice_fusion.12, bf16[128,2048]{0,1:T(8,128)(2,1)S(1)} %collective-permute-done.2, s32[]{:T(128)S(6)} %select_n.128), kind=kLoop, calls=%fused_computation.25 | loop fusion | bytes 1048580 | tf_op jit(solution)/shard_map/dynamic_update_slice | solution.py:152
  37.5 5.6 %collective-permute-start.5 = (bf16[128,2048]{0,1:T(8,128)(2,1)}, bf16[128,2048]{0,1:T(8,128)(2,1)S(1)}, u32[]{:S(2)}, u32[]{:S(2)}) collective-permute-start(bf16[128,2048]{0,1:T(8,128)(2,1)} %collective-permute-done.3), channel_id=1, source_target_pairs={{0,4},{4,8},{8,12},{12,14},{14,10},{10,6},{6,2},{2,0},{1,5},{5,9},... | collective-permute-start | bytes 1572872 | tf_op jit(solution)/shard_map/ppermute | solution.py:164
  43.2 1.9 %constant_dynamic-update-slice_fusion.10 = bf16[2048,2048]{0,1:T(8,128)(2,1)} fusion(bf16[2048,2048]{0,1:T(8,128)(2,1)} %constant_dynamic-update-slice_fusion.11, bf16[128,2048]{0,1:T(8,128)(2,1)} %collective-permute-done.9, s32[]{:T(128)S(6)} %select_n.129), kind=kLoop, calls=%fused_computation.24 | loop fusion | bytes 1048580 | tf_op jit(solution)/shard_map/dynamic_update_slice | solution.py:152
  45.1 8.8 %shard_map.65 = bf16[512,1024]{1,0:T(8,128)(2,1)} custom-call(f32[128,384]{1,0:T(8,128)} %pad_convert_fusion.fw_ref, f32[1,2048]{1,0:T(1,128)} %bitcast.27, f32[3,3,2048]{2,1,0:T(4,128)} %bitcast.20, bf16[3,2,2048]{2,1,0:T(2,128)(2,1)} %bitcast.25, bf16[128,2048]{1,0:T(8,128)(2,1)} %slice.83.halo_ref, bf16[512,6144]{1,0:T(8,128)(2,1)} %carrier_ref.2, ...), custom_call_target="tpu_custom_call" | custom-call | tf_op jit(solution)/shard_map/pallas_call | solution.py:101
  54.3 1.4 %pad_maximum_fusion = bf16[512,2048]{1,0:T(8,128)(2,1)S(1)} fusion(bf16[512,1024]{1,0:T(8,128)(2,1)} %shard_map.65, bf16[512,1024]{1,0:T(8,128)(2,1)S(1)} %copy-done), kind=kLoop, calls=%fused_computation.1 | loop fusion | flops 4194304 | bytes 4194304 | tf_op jit(solution)/shard_map/concatenate | solution.py:194
  55.7 1.9 %constant_dynamic-update-slice_fusion.9 = bf16[2048,2048]{0,1:T(8,128)(2,1)} fusion(bf16[2048,2048]{0,1:T(8,128)(2,1)} %constant_dynamic-update-slice_fusion.10, bf16[128,2048]{0,1:T(8,128)(2,1)} %collective-permute-done.3, s32[]{:T(128)S(6)} %select_n.132), kind=kLoop, calls=%fused_computation.23 | loop fusion | bytes 1048580 | tf_op jit(solution)/shard_map/dynamic_update_slice | solution.py:152
  57.7 2.1 %collective-permute-start.14 = (bf16[128,1024]{0,1:T(8,128)(2,1)S(1)}, bf16[128,1024]{0,1:T(8,128)(2,1)S(1)}, u32[]{:S(2)}, u32[]{:S(2)}) collective-permute-start(bf16[128,1024]{0,1:T(8,128)(2,1)S(1)} %slice.81), channel_id=1, source_target_pairs={{0,4},{4,8},{8,12},{12,14},{14,10},{10,6},{6,2},{2,0},{1,5},{5,9},... | collective-permute-start | bytes 786440 | tf_op jit(solution)/shard_map/ppermute | solution.py:201
  60.5 0.9 %constant_dynamic-update-slice_fusion.8 = bf16[2048,2048]{0,1:T(8,128)(2,1)} fusion(bf16[2048,2048]{0,1:T(8,128)(2,1)} %constant_dynamic-update-slice_fusion.9, bf16[128,2048]{0,1:T(8,128)(2,1)S(1)} %collective-permute-done.10, s32[]{:T(128)S(6)} %select_n.133), kind=kLoop, calls=%fused_computation.22 | loop fusion | bytes 1048580 | tf_op jit(solution)/shard_map/dynamic_update_slice | solution.py:152
  61.4 1.9 %constant_dynamic-update-slice_fusion.7 = bf16[2048,2048]{0,1:T(8,128)(2,1)} fusion(bf16[2048,2048]{0,1:T(8,128)(2,1)} %constant_dynamic-update-slice_fusion.8, bf16[128,2048]{0,1:T(8,128)(2,1)} %collective-permute-done.4, s32[]{:T(128)S(6)} %select_n.136), kind=kLoop, calls=%fused_computation.21 | loop fusion | bytes 1048580 | tf_op jit(solution)/shard_map/dynamic_update_slice | solution.py:152
  63.3 0.9 %constant_dynamic-update-slice_fusion.6 = bf16[2048,2048]{0,1:T(8,128)(2,1)} fusion(bf16[2048,2048]{0,1:T(8,128)(2,1)} %constant_dynamic-update-slice_fusion.7, bf16[128,2048]{0,1:T(8,128)(2,1)S(1)} %collective-permute-done.11, s32[]{:T(128)S(6)} %select_n.137), kind=kLoop, calls=%fused_computation.20 | loop fusion | bytes 1048580 | tf_op jit(solution)/shard_map/dynamic_update_slice | solution.py:152
  64.2 0.9 %constant_dynamic-update-slice_fusion.5 = bf16[2048,2048]{0,1:T(8,128)(2,1)} fusion(bf16[2048,2048]{0,1:T(8,128)(2,1)} %constant_dynamic-update-slice_fusion.6, bf16[128,2048]{0,1:T(8,128)(2,1)S(1)} %collective-permute-done.5, s32[]{:T(128)S(6)} %select_n.140), kind=kLoop, calls=%fused_computation.19 | loop fusion | bytes 1048580 | tf_op jit(solution)/shard_map/dynamic_update_slice | solution.py:152
  65.1 0.9 %collective-permute-done.14 = bf16[128,1024]{0,1:T(8,128)(2,1)S(1)} collective-permute-done((bf16[128,1024]{0,1:T(8,128)(2,1)S(1)}, bf16[128,1024]{0,1:T(8,128)(2,1)S(1)}, u32[]{:S(2)}, u32[]{:S(2)}) %collective-permute-start.14) | collective-permute-done | bytes 262176 | tf_op jit(solution)/shard_map/ppermute | solution.py:201
  66.1 1.8 %collective-permute-done.15 = bf16[128,1024]{0,1:T(8,128)(2,1)S(1)} collective-permute-done((bf16[128,1024]{0,1:T(8,128)(2,1)S(1)}, bf16[128,1024]{0,1:T(8,128)(2,1)S(1)}, u32[]{:S(2)}, u32[]{:S(2)}) %collective-permute-start.15) | collective-permute-done | bytes 262176 | tf_op jit(solution)/shard_map/ppermute | solution.py:202
  68.0 0.9 %constant_dynamic-update-slice_fusion.4 = bf16[2048,2048]{0,1:T(8,128)(2,1)} fusion(bf16[2048,2048]{0,1:T(8,128)(2,1)} %constant_dynamic-update-slice_fusion.5, bf16[128,2048]{0,1:T(8,128)(2,1)S(1)} %collective-permute-done.12, s32[]{:T(128)S(6)} %select_n.141), kind=kLoop, calls=%fused_computation.18 | loop fusion | bytes 1048580 | tf_op jit(solution)/shard_map/dynamic_update_slice | solution.py:152
  68.9 0.9 %constant_dynamic-update-slice_fusion.3 = bf16[2048,2048]{0,1:T(8,128)(2,1)} fusion(bf16[2048,2048]{0,1:T(8,128)(2,1)} %constant_dynamic-update-slice_fusion.4, bf16[128,2048]{0,1:T(8,128)(2,1)S(1)} %collective-permute-done.6, s32[]{:T(128)S(6)} %select_n.144), kind=kLoop, calls=%fused_computation.17 | loop fusion | bytes 1048580 | tf_op jit(solution)/shard_map/dynamic_update_slice | solution.py:152
  69.8 0.9 %constant_dynamic-update-slice_fusion.2 = bf16[2048,2048]{0,1:T(8,128)(2,1)} fusion(bf16[2048,2048]{0,1:T(8,128)(2,1)} %constant_dynamic-update-slice_fusion.3, bf16[128,2048]{0,1:T(8,128)(2,1)S(1)} %collective-permute-done.13, s32[]{:T(128)S(6)} %select_n.145), kind=kLoop, calls=%fused_computation.16 | loop fusion | bytes 1048580 | tf_op jit(solution)/shard_map/dynamic_update_slice | solution.py:152
  70.8 6.9 %fusion.8 = f32[512,2048]{1,0:T(8,128)S(1)} fusion(bf16[512,2048]{1,0:T(8,128)(2,1)S(1)} %pad_maximum_fusion, bf16[2048,2048]{0,1:T(8,128)(2,1)} %constant_dynamic-update-slice_fusion.2), kind=kOutput, calls=%fused_computation.32 | convolution fusion | flops 4294967296 | bytes 14680064 | tf_op jit(solution)/shard_map/dot_general | solution.py:204
  78.4 0.8 %copy-done.1 = bf16[512,2048]{1,0:T(8,128)(2,1)S(1)} copy-done((bf16[512,2048]{1,0:T(8,128)(2,1)S(1)}, bf16[512,2048]{1,0:T(8,128)(2,1)}, u32[]{:S(2)}) %copy-start.1) | copy-done | bytes 2097176
  79.3 2.1 %add_convert_fusion = bf16[512,2048]{1,0:T(8,128)(2,1)} fusion(f32[512,2048]{1,0:T(8,128)S(1)} %convolution_dynamic-update-slice_fusion, bf16[512,2048]{1,0:T(8,128)(2,1)S(1)} %copy-done.1), kind=kLoop, calls=%fused_computation | loop fusion | flops 3145728 | bytes 8388608 | tf_op jit(solution)/shard_map/convert_element_type | solution.py:210
  (46 shorter events, 5.3 us)
Async XLA Ops:
  0.0 14.4 %copy-start.2 = (bf16[2048,128]{1,0:T(8,128)(2,1)S(1)}, bf16[2048,128]{1,0:T(8,128)(2,1)}, u32[]{:S(2)}) copy-start(bf16[2048,128]{1,0:T(8,128)(2,1)} %param.11) | copy-start | bytes 1572868
  0.0 15.3 %copy-start.3 = (bf16[128,128]{1,0:T(8,128)(2,1)S(1)}, bf16[128,128]{1,0:T(8,128)(2,1)}, u32[]{:S(2)}) copy-start(bf16[128,128]{1,0:T(8,128)(2,1)} %param.9) | copy-start | bytes 98308
  0.0 18.1 %collective-permute-start.7 = (bf16[128,2048]{0,1:T(8,128)(2,1)}, bf16[128,2048]{0,1:T(8,128)(2,1)}, u32[]{:S(2)}, u32[]{:S(2)}) collective-permute-start(bf16[128,2048]{0,1:T(8,128)(2,1)} %bitcast.21), channel_id=1, source_target_pairs={{0,1},{1,0},{2,3},{3,2},{4,5},{5,4},{6,7},{7,6},{8,9},{9,8},{10,11... | collective-permute-start | bytes 1572872 | tf_op jit(solution)/shard_map/ppermute | solution.py:150
  0.5 15.3 %collective-permute-start.1 = (bf16[128,2048]{0,1:T(8,128)(2,1)}, bf16[128,2048]{0,1:T(8,128)(2,1)S(1)}, u32[]{:S(2)}, u32[]{:S(2)}) collective-permute-start(bf16[128,2048]{0,1:T(8,128)(2,1)} %bitcast.22), channel_id=1, source_target_pairs={{0,4},{4,8},{8,12},{12,14},{14,10},{10,6},{6,2},{2,0},{1,5},{5,9},... | collective-permute-start | bytes 1572872 | tf_op jit(solution)/shard_map/ppermute | solution.py:164
  3.1 15.0 %collective-permute-start.2 = (bf16[128,2048]{0,1:T(8,128)(2,1)}, bf16[128,2048]{0,1:T(8,128)(2,1)S(1)}, u32[]{:S(2)}, u32[]{:S(2)}) collective-permute-start(bf16[128,2048]{0,1:T(8,128)(2,1)} %bitcast.23), channel_id=1, source_target_pairs={{4,0},{8,4},{12,8},{14,12},{10,14},{6,10},{2,6},{0,2},{5,1},{9,5},... | collective-permute-start | bytes 1572872 | tf_op jit(solution)/shard_map/ppermute | solution.py:165
  8.0 12.1 %collective-permute-start = (bf16[134,2048]{1,0:T(8,128)(2,1)S(1)}, bf16[134,2048]{1,0:T(8,128)(2,1)S(1)}, u32[]{:S(2)}, u32[]{:S(2)}) collective-permute-start(bf16[134,2048]{1,0:T(8,128)(2,1)S(1)} %pad_maximum_fusion.1), channel_id=1, source_target_pairs={{0,1},{1,2},{2,3},{3,4},{4,5},{5,6},{6,7},{7,8},{8,9},{9,10},{10,1... | collective-permute-start | bytes 1646600 | tf_op jit(solution)/shard_map/ppermute | solution.py:22
  15.8 20.0 %collective-permute-start.8 = (bf16[128,2048]{0,1:T(8,128)(2,1)S(1)}, bf16[128,2048]{0,1:T(8,128)(2,1)S(1)}, u32[]{:S(2)}, u32[]{:S(2)}) collective-permute-start(bf16[128,2048]{0,1:T(8,128)(2,1)S(1)} %collective-permute-done.1), channel_id=1, source_target_pairs={{0,1},{1,0},{2,3},{3,2},{4,5},{5,4},{6,7},{7,6},{8,9},{9,8},{10,11... | collective-permute-start | bytes 1572872 | tf_op jit(solution)/shard_map/ppermute | solution.py:150
  18.1 25.0 %collective-permute-start.9 = (bf16[128,2048]{0,1:T(8,128)(2,1)S(1)}, bf16[128,2048]{0,1:T(8,128)(2,1)}, u32[]{:S(2)}, u32[]{:S(2)}) collective-permute-start(bf16[128,2048]{0,1:T(8,128)(2,1)S(1)} %collective-permute-done.2), channel_id=1, source_target_pairs={{0,1},{1,0},{2,3},{3,2},{4,5},{5,4},{6,7},{7,6},{8,9},{9,8},{10,11... | collective-permute-start | bytes 1572872 | tf_op jit(solution)/shard_map/ppermute | solution.py:150
  20.9 16.6 %collective-permute-start.3 = (bf16[128,2048]{0,1:T(8,128)(2,1)S(1)}, bf16[128,2048]{0,1:T(8,128)(2,1)}, u32[]{:S(2)}, u32[]{:S(2)}) collective-permute-start(bf16[128,2048]{0,1:T(8,128)(2,1)S(1)} %collective-permute-done.1), channel_id=1, source_target_pairs={{0,4},{4,8},{8,12},{12,14},{14,10},{10,6},{6,2},{2,0},{1,5},{5,9},... | collective-permute-start | bytes 1572872 | tf_op jit(solution)/shard_map/ppermute | solution.py:164
  25.5 12.0 %collective-permute-start.4 = (bf16[128,2048]{0,1:T(8,128)(2,1)S(1)}, bf16[128,2048]{0,1:T(8,128)(2,1)}, u32[]{:S(2)}, u32[]{:S(2)}) collective-permute-start(bf16[128,2048]{0,1:T(8,128)(2,1)S(1)} %collective-permute-done.2), channel_id=1, source_target_pairs={{4,0},{8,4},{12,8},{14,12},{10,14},{6,10},{2,6},{0,2},{5,1},{9,5},... | collective-permute-start | bytes 1572872 | tf_op jit(solution)/shard_map/ppermute | solution.py:165
  37.5 20.2 %collective-permute-start.5 = (bf16[128,2048]{0,1:T(8,128)(2,1)}, bf16[128,2048]{0,1:T(8,128)(2,1)S(1)}, u32[]{:S(2)}, u32[]{:S(2)}) collective-permute-start(bf16[128,2048]{0,1:T(8,128)(2,1)} %collective-permute-done.3), channel_id=1, source_target_pairs={{0,4},{4,8},{8,12},{12,14},{14,10},{10,6},{6,2},{2,0},{1,5},{5,9},... | collective-permute-start | bytes 1572872 | tf_op jit(solution)/shard_map/ppermute | solution.py:164
  43.1 14.5 %collective-permute-start.6 = (bf16[128,2048]{0,1:T(8,128)(2,1)}, bf16[128,2048]{0,1:T(8,128)(2,1)S(1)}, u32[]{:S(2)}, u32[]{:S(2)}) collective-permute-start(bf16[128,2048]{0,1:T(8,128)(2,1)} %collective-permute-done.4), channel_id=1, source_target_pairs={{4,0},{8,4},{12,8},{14,12},{10,14},{6,10},{2,6},{0,2},{5,1},{9,5},... | collective-permute-start | bytes 1572872 | tf_op jit(solution)/shard_map/ppermute | solution.py:165
  43.1 16.8 %collective-permute-start.10 = (bf16[128,2048]{0,1:T(8,128)(2,1)}, bf16[128,2048]{0,1:T(8,128)(2,1)S(1)}, u32[]{:S(2)}, u32[]{:S(2)}) collective-permute-start(bf16[128,2048]{0,1:T(8,128)(2,1)} %collective-permute-done.3), channel_id=1, source_target_pairs={{0,1},{1,0},{2,3},{3,2},{4,5},{5,4},{6,7},{7,6},{8,9},{9,8},{10,11... | collective-permute-start | bytes 1572872 | tf_op jit(solution)/shard_map/ppermute | solution.py:150
  45.1 9.2 %copy-start = (bf16[512,1024]{1,0:T(8,128)(2,1)S(1)}, bf16[512,1024]{1,0:T(8,128)(2,1)}, u32[]{:S(2)}) copy-start(bf16[512,1024]{1,0:T(8,128)(2,1)} %shard_map.64) | copy-start | bytes 3145732
  53.9 9.4 %collective-permute-start.11 = (bf16[128,2048]{0,1:T(8,128)(2,1)}, bf16[128,2048]{0,1:T(8,128)(2,1)S(1)}, u32[]{:S(2)}, u32[]{:S(2)}) collective-permute-start(bf16[128,2048]{0,1:T(8,128)(2,1)} %collective-permute-done.4), channel_id=1, source_target_pairs={{0,1},{1,0},{2,3},{3,2},{4,5},{5,4},{6,7},{7,6},{8,9},{9,8},{10,11... | collective-permute-start | bytes 1572872 | tf_op jit(solution)/shard_map/ppermute | solution.py:150
  57.7 8.3 %collective-permute-start.14 = (bf16[128,1024]{0,1:T(8,128)(2,1)S(1)}, bf16[128,1024]{0,1:T(8,128)(2,1)S(1)}, u32[]{:S(2)}, u32[]{:S(2)}) collective-permute-start(bf16[128,1024]{0,1:T(8,128)(2,1)S(1)} %slice.81), channel_id=1, source_target_pairs={{0,4},{4,8},{8,12},{12,14},{14,10},{10,6},{6,2},{2,0},{1,5},{5,9},... | collective-permute-start | bytes 786440 | tf_op jit(solution)/shard_map/ppermute | solution.py:201
  59.8 8.1 %collective-permute-start.15 = (bf16[128,1024]{0,1:T(8,128)(2,1)S(1)}, bf16[128,1024]{0,1:T(8,128)(2,1)S(1)}, u32[]{:S(2)}, u32[]{:S(2)}) collective-permute-start(bf16[128,1024]{0,1:T(8,128)(2,1)S(1)} %slice.82), channel_id=1, source_target_pairs={{4,0},{8,4},{12,8},{14,12},{10,14},{6,10},{2,6},{0,2},{5,1},{9,5},... | collective-permute-start | bytes 786440 | tf_op jit(solution)/shard_map/ppermute | solution.py:202
  59.9 8.1 %collective-permute-start.12 = (bf16[128,2048]{0,1:T(8,128)(2,1)S(1)}, bf16[128,2048]{0,1:T(8,128)(2,1)S(1)}, u32[]{:S(2)}, u32[]{:S(2)}) collective-permute-start(bf16[128,2048]{0,1:T(8,128)(2,1)S(1)} %collective-permute-done.5), channel_id=1, source_target_pairs={{0,1},{1,0},{2,3},{3,2},{4,5},{5,4},{6,7},{7,6},{8,9},{9,8},{10,11... | collective-permute-start | bytes 1572872 | tf_op jit(solution)/shard_map/ppermute | solution.py:150
  60.0 9.9 %collective-permute-start.13 = (bf16[128,2048]{0,1:T(8,128)(2,1)S(1)}, bf16[128,2048]{0,1:T(8,128)(2,1)S(1)}, u32[]{:S(2)}, u32[]{:S(2)}) collective-permute-start(bf16[128,2048]{0,1:T(8,128)(2,1)S(1)} %collective-permute-done.6), channel_id=1, source_target_pairs={{0,1},{1,0},{2,3},{3,2},{4,5},{5,4},{6,7},{7,6},{8,9},{9,8},{10,11... | collective-permute-start | bytes 1572872 | tf_op jit(solution)/shard_map/ppermute | solution.py:150
  67.9 9.8 %collective-permute-start.16 = (bf16[128,2048]{0,1:T(8,128)(2,1)S(1)}, bf16[128,2048]{0,1:T(8,128)(2,1)S(1)}, u32[]{:S(2)}, u32[]{:S(2)}) collective-permute-start(bf16[128,2048]{0,1:T(8,128)(2,1)S(1)} %constant_dynamic-update-slice_fusion), channel_id=1, source_target_pairs={{0,1},{1,0},{2,3},{3,2},{4,5},{5,4},{6,7},{7,6},{8,9},{9,8},{10,11... | collective-permute-start | bytes 1572872 | tf_op jit(solution)/shard_map/ppermute | solution.py:206
  77.7 1.6 %copy-start.1 = (bf16[512,2048]{1,0:T(8,128)(2,1)S(1)}, bf16[512,2048]{1,0:T(8,128)(2,1)}, u32[]{:S(2)}) copy-start(bf16[512,2048]{1,0:T(8,128)(2,1)} %param.6) | copy-start | bytes 6291460

commit v20 on v18

--- a/solution.py
+++ b/solution.py
@@ -138,33 +138,19 @@
     swap = [(0, 1), (1, 0)]
     steps = chips // 2
 
-    weight = jnp.zeros((chips * 2 * width, channels), out_weight.dtype)
+    late = []
 
-    def place(weight, piece, owner_chip, row=0):
-        other = lax.ppermute(piece, "core", swap)
-        for k, part in ((core, piece), (1 - core, other)):
-            weight = lax.dynamic_update_slice(weight, part, ((owner_chip * 2 + k) * width, row))
-        return weight
-
-    def ring_step(step, weight, ahead, behind):
-        if step == steps:
-            half = channels // 2
-            ahead = lax.ppermute(ahead[:, :half], "chip", forward)
-            behind = lax.ppermute(behind[:, half:], "chip", backward)
-            source = ring_chip((position - step) % chips, chips)
-            weight = place(weight, ahead, source, 0)
-            weight = place(weight, behind, source, half)
-        else:
-            ahead = lax.ppermute(ahead, "chip", forward)
-            behind = lax.ppermute(behind, "chip", backward)
-            weight = place(weight, ahead, ring_chip((position - step) % chips, chips))
-            weight = place(weight, behind, ring_chip((position + step) % chips, chips))
-        return weight, ahead, behind
+    def ring_step(step, ahead, behind):
+        ahead = lax.ppermute(ahead, "chip", forward)
+        behind = lax.ppermute(behind, "chip", backward)
+        late.append((ahead, lax.ppermute(ahead, "core", swap), ring_chip((position - step) % chips, chips)))
+        late.append((behind, lax.ppermute(behind, "core", swap), ring_chip((position + step) % chips, chips)))
+        return ahead, behind
 
     ahead = behind = out_weight.T
     if ring:
-        weight = place(weight, ahead, chip)
-        weight, ahead, behind = ring_step(1, weight, ahead, behind)
+        late.append((ahead, lax.ppermute(ahead, "core", swap), chip))
+        ahead, behind = ring_step(1, ahead, behind)
 
     tail = projected[row_count - BLOCK - 2 :]
     tail_mixed = [
@@ -174,16 +160,14 @@
     halo = shifted(carried_of(*tail_mixed), 1)
     edge = shifted(projected[row_count - 2 :], 1)
     halo, edge, ahead, behind = lax.optimization_barrier((halo, edge, ahead, behind))
-    if ring and steps >= 2:
-        weight, ahead, behind = ring_step(2, weight, ahead, behind)
+    if ring:
+        ahead, behind = ring_step(2, ahead, behind)
 
     inputs = (halo, edge, projected, short_filter, long_filter, conv_bias)
     first = hyena_gate(*inputs, 0, 2)
     if ring:
         first, ahead, behind, inputs = lax.optimization_barrier((first, ahead, behind, inputs))
-        ahead = lax.ppermute(ahead, "chip", forward)
-        behind = lax.ppermute(behind, "chip", backward)
-        late = [(ahead, ring_chip((position - 3) % chips, chips)), (behind, ring_chip((position + 3) % chips, chips))]
+        ahead, behind = ring_step(3, ahead, behind)
     second = hyena_gate(*inputs, 1, 2)
     gated = jnp.concatenate([first, second], axis=1)
     if not ring:
@@ -195,10 +179,10 @@
     ahead = lax.ppermute(ahead[:, :half], "chip", forward)
     behind = lax.ppermute(behind[:, half:], "chip", backward)
     source = ring_chip((position - steps) % chips, chips)
-    branch = lax.dot_general(gated, weight, (((1,), (1,)), ((), ())), preferred_element_type=jnp.float32)
-    late.append((jnp.concatenate([ahead, behind], axis=1), source))
-    for mine, owner_chip in late:
-        other = lax.ppermute(mine, "core", swap)
+    branch = jnp.zeros((row_count, chips * 2 * width), jnp.float32)
+    last = jnp.concatenate([ahead, behind], axis=1)
+    late.append((last, lax.ppermute(last, "core", swap), source))
+    for mine, other, owner_chip in late:
         pair = jnp.where(core == 0, jnp.concatenate([mine, other]), jnp.concatenate([other, mine]))
         part = lax.dot_general(gated, pair, (((1,), (1,)), ((), ())), preferred_element_type=jnp.float32)
         branch = lax.dynamic_update_slice(branch, part, (0, owner_chip * 2 * width))

time: 79.2 us -> 76.9 us (0.971)
  local copies, waits for them, and re-layouts: 21.4 us -> 3.29 us
  waiting for transfers between devices: 0.05 us -> 11.9 us
  starting transfers between devices: 19.7 us -> 22.8 us
  matrix products: 11.5 us -> 12.5 us
    dynamic_update_slice x10 -> x0, local copies, waits for them, and re-layouts: 12.2 us -> none  [place(): lax.dynamic_update_slice(weight, part, ((owner_chip * 2 + k) * width, row))]
    ppermute x2 -> x3, waiting for transfers between devices: 0.01 us -> 7.93 us  [ring_step(): ahead = lax.ppermute(ahead, 'chip', forward)]
    dot_general x3 -> x8, matrix products: 4.6 us -> 12.5 us  [on_device(): lax.dot_general(gated, pair, (((1,), (1,)), ((), ())), preferred_element_...]
    dot_general x1 -> x0, matrix products: 6.88 us -> none  [on_device(): lax.dot_general(gated, weight, (((1,), (1,)), ((), ())), preferred_elemen...]
    ppermute x2 -> x3, starting transfers between devices: 7.82 us -> 12.9 us  [ring_step(): ahead = lax.ppermute(ahead, 'chip', forward)]
    ppermute x10 -> x8, starting transfers between devices: 6.36 us -> 1.94 us  [the longest x3 1.28 us: ring_step(): lax.ppermute(ahead, 'core', swap)]
    broadcast_in_dim x1, local copies, waits for them, and re-layouts: 4.31 us -> 0.49 us  [on_device(): branch = jnp.zeros((row_count, chips * 2 * width), jnp.float32)]
    ppermute x2 -> x3, waiting for transfers between devices: 0.01 us -> 2.87 us  [ring_step(): behind = lax.ppermute(behind, 'chip', backward)]
  transfers between devices with their start and end apart: 18 -> 18, of which waited for: 0 -> 6; matrix products, arithmetic and copies ran while one was open for 47% -> 22% of each run, Pallas kernels for 22% -> 23%
where the time goes in v20:
time: 76.9 us; the launch traced here: 76.1 us
  starting transfers between devices  22.8 us (30%)
  Pallas kernels  17.4 us (23%)
  matrix products  12.5 us (16%)
  waiting for transfers between devices  11.9 us (15%)
  other arithmetic  8.01 us (10%)
  local copies, waits for them, and re-layouts  3.29 us (4%)
    pallas_call x2, Pallas kernels, hyena_gate(): pl.pallas_call(_gate_kernel, grid=(share,), in_specs=[pl.BlockSpec((per_t...  17.4 us
    ppermute x3, starting transfers between devices, ring_step(): ahead = lax.ppermute(ahead, 'chip', forward)  12.9 us
    dot_general x8, matrix products, on_device(): lax.dot_general(gated, pair, (((1,), (1,)), ((), ())), preferred_element_...  12.5 us
    ppermute x3, waiting for transfers between devices, ring_step(): ahead = lax.ppermute(ahead, 'chip', forward)  7.93 us
    ppermute x2, starting transfers between devices, shifted(): return lax.ppermute(block, CTX, route)  5.8 us
    convert_element_type x1, other arithmetic, carried_of(): return (second * carrier).astype(jnp.bfloat16)  2.95 us
    ppermute x3, waiting for transfers between devices, ring_step(): behind = lax.ppermute(behind, 'chip', backward)  2.87 us
    ppermute x1, starting transfers between devices, on_device(): ahead = lax.ppermute(ahead[:, :half], 'chip', forward)  2.08 us
  transfers between devices with their start and end apart: 18, of which 6 were waited for; matrix products, arithmetic and copies ran while one was open for 22% of the time, Pallas kernels for 23%

profile of v20, /device:TPU:0, one launch (start us, length us, event | category | flops | bytes accessed | tf_op | source)
XLA Modules:
  0.0 76.1 jit_solution(12102271434254315645)
XLA Ops:
  0.0 1.0 %fusion.56 = (f32[1,2048]{1,0:T(1,128)S(1)}, f32[1,2048]{1,0:T(1,128)S(1)}, f32[1,2048]{1,0:T(1,128)S(1)}, f32[1,2048]{1,0:T(1,128)S(1)}, f32[1,2048]{1,0:T(1,128)S(1)}, /*index=5*/f32[1,2048]{1,0:T(1,128)S(1)}) fusion(f32[3,6144]{1,0:T(4,128)} %param.8), kind=kLoop, calls=%fused_computation.79 | loop fusion | bytes 98304 | tf_op jit(solution)/shard_map/slice | solution.py:34
  1.0 3.0 %multiply_convert_fusion = bf16[128,2048]{1,0:T(8,128)(2,1)S(1)} fusion(bf16[512,6144]{1,0:T(8,128)(2,1)} %carrier_ref.2, f32[2048]{0:T(1024)S(1)} %bitcast.40, f32[2048]{0:T(1024)S(1)} %bitcast.36, f32[2048]{0:T(1024)S(1)} %bitcast.37, f32[2048]{0:T(1024)S(1)} %bitcast.38, f32[2048]{0:T(1024)S(1)} %bitcast.39, f32[2048]{0:T(1024)S(1)} %bitcast.35), kind=kLoop, calls=%fused_computation.58 | loop fusion | flops 4718592 | bytes 3719168 | tf_op jit(solution)/shard_map/convert_element_type | solution.py:122
  3.9 2.4 %collective-permute-start = (bf16[128,2048]{1,0:T(8,128)(2,1)S(1)}, bf16[128,2048]{1,0:T(8,128)(2,1)S(1)}, u32[]{:S(2)}, u32[]{:S(2)}) collective-permute-start(bf16[128,2048]{1,0:T(8,128)(2,1)S(1)} %multiply_convert_fusion), channel_id=1, source_target_pairs={{0,1},{1,2},{2,3},{3,4},{4,5},{5,6},{6,7},{7,8},{8,9},{9,10},{10,1... | collective-permute-start | bytes 1572872 | tf_op jit(solution)/shard_map/ppermute | solution.py:22
  6.3 2.6 %collective-permute-start.2 = (bf16[128,2048]{0,1:T(8,128)(2,1)S(1)}, bf16[128,2048]{0,1:T(8,128)(2,1)}, u32[]{:S(2)}, u32[]{:S(2)}) collective-permute-start(bf16[128,2048]{0,1:T(8,128)(2,1)S(1)} %bitcast.41), channel_id=1, source_target_pairs={{0,4},{4,8},{8,12},{12,14},{14,10},{10,6},{6,2},{2,0},{1,5},{5,9},... | collective-permute-start | bytes 1572872 | tf_op jit(solution)/shard_map/ppermute | solution.py:144
  8.9 0.9 %slice.72 = bf16[2,6144]{1,0:T(2,128)(2,1)S(1)} slice(bf16[512,6144]{1,0:T(8,128)(2,1)} %carrier_ref.2), slice={[510:512], [0:6144]} | slice | bytes 49152 | tf_op jit(solution)/shard_map/slice | solution.py:161
  9.9 3.4 %collective-permute-start.1 = (bf16[2,6144]{1,0:T(2,128)(2,1)S(1)}, bf16[2,6144]{1,0:T(2,128)(2,1)S(1)}, u32[]{:S(2)}, u32[]{:S(2)}) collective-permute-start(bf16[2,6144]{1,0:T(2,128)(2,1)S(1)} %slice.72), channel_id=1, source_target_pairs={{0,1},{1,2},{2,3},{3,4},{4,5},{5,6},{6,7},{7,8},{8,9},{9,10},{10,1... | collective-permute-start | bytes 73736 | tf_op jit(solution)/shard_map/ppermute | solution.py:22
  13.3 0.8 %collective-permute-done.1 = bf16[2,6144]{1,0:T(2,128)(2,1)S(1)} collective-permute-done((bf16[2,6144]{1,0:T(2,128)(2,1)S(1)}, bf16[2,6144]{1,0:T(2,128)(2,1)S(1)}, u32[]{:S(2)}, u32[]{:S(2)}) %collective-permute-start.1) | collective-permute-done | bytes 24608 | tf_op jit(solution)/shard_map/ppermute | solution.py:22
  14.1 6.5 %collective-permute-done.2 = bf16[128,2048]{0,1:T(8,128)(2,1)} collective-permute-done((bf16[128,2048]{0,1:T(8,128)(2,1)S(1)}, bf16[128,2048]{0,1:T(8,128)(2,1)}, u32[]{:S(2)}, u32[]{:S(2)}) %collective-permute-start.2) | collective-permute-done | bytes 524320 | tf_op jit(solution)/shard_map/ppermute | solution.py:144
  20.7 2.8 %collective-permute-done.3 = bf16[128,2048]{0,1:T(8,128)(2,1)S(1)} collective-permute-done((bf16[128,2048]{0,1:T(8,128)(2,1)S(1)}, bf16[128,2048]{0,1:T(8,128)(2,1)S(1)}, u32[]{:S(2)}, u32[]{:S(2)}) %collective-permute-start.3) | collective-permute-done | bytes 524320 | tf_op jit(solution)/shard_map/ppermute | solution.py:145
  23.5 6.5 %collective-permute-start.4 = (bf16[128,2048]{0,1:T(8,128)(2,1)}, bf16[128,2048]{0,1:T(8,128)(2,1)}, u32[]{:S(2)}, u32[]{:S(2)}) collective-permute-start(bf16[128,2048]{0,1:T(8,128)(2,1)} %collective-permute-done.2), channel_id=1, source_target_pairs={{0,4},{4,8},{8,12},{12,14},{14,10},{10,6},{6,2},{2,0},{1,5},{5,9},... | collective-permute-start | bytes 1572872 | tf_op jit(solution)/shard_map/ppermute | solution.py:144
  30.0 0.8 %pad_convert_fusion.1.fw_ref = f32[128,384]{1,0:T(8,128)} fusion(bf16[128,128]{1,0:T(8,128)(2,1)S(1)} %rev.6), kind=kLoop, calls=%fused_computation.68 | loop fusion | flops 49152 | bytes 229376 | tf_op jit(solution)/shard_map/jit(_pad)/pad | solution.py:91
  30.8 8.7 %shard_map.64 = bf16[512,1024]{1,0:T(8,128)(2,1)} custom-call(f32[128,384]{1,0:T(8,128)} %pad_convert_fusion.1.fw_ref, f32[1,2048]{1,0:T(1,128)} %bitcast.33, f32[3,3,2048]{2,1,0:T(4,128)} %bitcast.29, bf16[3,2,2048]{2,1,0:T(2,128)(2,1)} %bitcast.31, bf16[128,2048]{1,0:T(8,128)(2,1)} %copy-done.1, bf16[512,6144]{1,0:T(8,128)(2,1)} %carrier_ref.2, ...), custom_call_target="tpu_custom_call" | custom-call | tf_op jit(solution)/shard_map/pallas_call | solution.py:95
  39.5 1.4 %collective-permute-done.4 = bf16[128,2048]{0,1:T(8,128)(2,1)} collective-permute-done((bf16[128,2048]{0,1:T(8,128)(2,1)}, bf16[128,2048]{0,1:T(8,128)(2,1)}, u32[]{:S(2)}, u32[]{:S(2)}) %collective-permute-start.4) | collective-permute-done | bytes 524320 | tf_op jit(solution)/shard_map/ppermute | solution.py:144
  40.9 3.8 %collective-permute-start.6 = (bf16[128,2048]{0,1:T(8,128)(2,1)}, bf16[128,2048]{0,1:T(8,128)(2,1)S(1)}, u32[]{:S(2)}, u32[]{:S(2)}) collective-permute-start(bf16[128,2048]{0,1:T(8,128)(2,1)} %collective-permute-done.4), channel_id=1, source_target_pairs={{0,4},{4,8},{8,12},{12,14},{14,10},{10,6},{6,2},{2,0},{1,5},{5,9},... | collective-permute-start | bytes 1572872 | tf_op jit(solution)/shard_map/ppermute | solution.py:144
  44.7 0.5 collective-permute-start.9
  45.3 0.8 %pad_convert_fusion.fw_ref = f32[128,384]{1,0:T(8,128)} fusion(bf16[128,128]{1,0:T(8,128)(2,1)S(1)} %rev.7), kind=kLoop, calls=%fused_computation.67 | loop fusion | flops 49152 | bytes 229376 | tf_op jit(solution)/shard_map/jit(_pad)/pad | solution.py:91
  46.1 8.8 %shard_map.65 = bf16[512,1024]{1,0:T(8,128)(2,1)} custom-call(f32[128,384]{1,0:T(8,128)} %pad_convert_fusion.fw_ref, f32[1,2048]{1,0:T(1,128)} %bitcast.34, f32[3,3,2048]{2,1,0:T(4,128)} %bitcast.30, bf16[3,2,2048]{2,1,0:T(2,128)(2,1)} %bitcast.32, bf16[128,2048]{1,0:T(8,128)(2,1)} %copy-done.1, bf16[512,6144]{1,0:T(8,128)(2,1)} %carrier_ref.2, ...), custom_call_target="tpu_custom_call" | custom-call | tf_op jit(solution)/shard_map/pallas_call | solution.py:95
  54.9 1.4 %pad_maximum_fusion = bf16[512,2048]{1,0:T(8,128)(2,1)S(1)} fusion(bf16[512,1024]{1,0:T(8,128)(2,1)} %shard_map.65, bf16[512,1024]{1,0:T(8,128)(2,1)S(1)} %copy-done), kind=kLoop, calls=%fused_computation.1 | loop fusion | flops 4194304 | bytes 4194304 | tf_op jit(solution)/shard_map/concatenate | solution.py:172
  56.3 0.6 collective-permute-start.11
  57.0 2.1 %collective-permute-start.15 = (bf16[128,1024]{0,1:T(8,128)(2,1)S(1)}, bf16[128,1024]{0,1:T(8,128)(2,1)S(1)}, u32[]{:S(2)}, u32[]{:S(2)}) collective-permute-start(bf16[128,1024]{0,1:T(8,128)(2,1)S(1)} %slice.73), channel_id=1, source_target_pairs={{0,4},{4,8},{8,12},{12,14},{14,10},{10,6},{6,2},{2,0},{1,5},{5,9},... | collective-permute-start | bytes 786440 | tf_op jit(solution)/shard_map/ppermute | solution.py:179
  59.1 0.5 broadcast_in_dim.3
  59.6 2.0 %convolution_dynamic-update-slice_fusion.7 = f32[512,2048]{1,0:T(8,128)S(1)} fusion(f32[512,2048]{1,0:T(8,128)S(1)} %broadcast_in_dim.3, s32[]{:T(128)S(6)} %select_n.126, bf16[512,2048]{1,0:T(8,128)(2,1)S(1)} %pad_maximum_fusion, bf16[128,2048]{0,1:T(8,128)(2,1)} %collective-permute-done.8, bf16[128,2048]{0,1:T(8,128)(2,1)S(1)} %bitcast.44, pred[]{:T(512)S(6)} %eq.22), kind=kOutput, calls=%fused_computation.9 | convolution fusion | flops 541589504 | bytes 3670021 | tf_op jit(solution)/shard_map/dot_general | solution.py:187
  61.6 2.4 %convolution_dynamic-update-slice_fusion.6 = f32[512,2048]{1,0:T(8,128)S(1)} fusion(f32[512,2048]{1,0:T(8,128)S(1)} %convolution_dynamic-update-slice_fusion.7, s32[]{:T(128)S(6)} %select_n.133, bf16[512,2048]{1,0:T(8,128)(2,1)S(1)} %pad_maximum_fusion, bf16[128,2048]{0,1:T(8,128)(2,1)} %collective-permute-done.9, ...), kind=kOutput, calls=%fused_computation.8 | convolution fusion | flops 541589504 | bytes 3670021 | tf_op jit(solution)/shard_map/dot_general | solution.py:187
  64.3 2.0 %convolution_dynamic-update-slice_fusion.5 = f32[512,2048]{1,0:T(8,128)S(1)} fusion(f32[512,2048]{1,0:T(8,128)S(1)} %convolution_dynamic-update-slice_fusion.6, s32[]{:T(128)S(6)} %select_n.137, bf16[512,2048]{1,0:T(8,128)(2,1)S(1)} %pad_maximum_fusion, bf16[128,2048]{0,1:T(8,128)(2,1)} %collective-permute-done.10, ...), kind=kOutput, calls=%fused_computation.7 | convolution fusion | flops 541589504 | bytes 3670021 | tf_op jit(solution)/shard_map/dot_general | solution.py:187
  66.3 0.4 collective-permute-start.14
  66.7 2.0 %convolution_dynamic-update-slice_fusion.4 = f32[512,2048]{1,0:T(8,128)S(1)} fusion(f32[512,2048]{1,0:T(8,128)S(1)} %convolution_dynamic-update-slice_fusion.5, s32[]{:T(128)S(6)} %select_n.141, bf16[512,2048]{1,0:T(8,128)(2,1)S(1)} %pad_maximum_fusion, bf16[128,2048]{0,1:T(8,128)(2,1)S(1)} %collective-permute-done.11, ...), kind=kOutput, calls=%fused_computation.6 | convolution fusion | flops 541589504 | bytes 3670021 | tf_op jit(solution)/shard_map/dot_general | solution.py:187
  68.6 2.0 %convolution_dynamic-update-slice_fusion.3 = f32[512,2048]{1,0:T(8,128)S(1)} fusion(f32[512,2048]{1,0:T(8,128)S(1)} %convolution_dynamic-update-slice_fusion.4, s32[]{:T(128)S(6)} %select_n.145, bf16[512,2048]{1,0:T(8,128)(2,1)S(1)} %pad_maximum_fusion, bf16[128,2048]{0,1:T(8,128)(2,1)S(1)} %collective-permute-done.12, ...), kind=kOutput, calls=%fused_computation.5 | convolution fusion | flops 541589504 | bytes 3670021 | tf_op jit(solution)/shard_map/dot_general | solution.py:187
  71.0 0.7 convolution_dynamic-update-slice_fusion.2
  71.7 0.7 convolution_dynamic-update-slice_fusion.1
  72.7 0.7 convolution_dynamic-update-slice_fusion
  73.4 0.6 copy-done.2
  74.1 2.1 %add_convert_fusion = bf16[512,2048]{1,0:T(8,128)(2,1)} fusion(f32[512,2048]{1,0:T(8,128)S(1)} %convolution_dynamic-update-slice_fusion, bf16[512,2048]{1,0:T(8,128)(2,1)S(1)} %copy-done.2), kind=kLoop, calls=%fused_computation | loop fusion | flops 3145728 | bytes 8388608 | tf_op jit(solution)/shard_map/convert_element_type | solution.py:189
  (40 shorter events, 1.2 us)
Async XLA Ops:
  0.0 6.3 %copy-start.5 = (bf16[2048,128]{1,0:T(8,128)(2,1)S(1)}, bf16[2048,128]{1,0:T(8,128)(2,1)}, u32[]{:S(2)}) copy-start(bf16[2048,128]{1,0:T(8,128)(2,1)} %param.11) | copy-start | bytes 1572868
  0.0 29.9 %copy-start.3 = (bf16[128,128]{1,0:T(8,128)(2,1)S(1)}, bf16[128,128]{1,0:T(8,128)(2,1)}, u32[]{:S(2)}) copy-start(bf16[128,128]{1,0:T(8,128)(2,1)} %param.9) | copy-start | bytes 98308
  3.9 10.2 %collective-permute-start = (bf16[128,2048]{1,0:T(8,128)(2,1)S(1)}, bf16[128,2048]{1,0:T(8,128)(2,1)S(1)}, u32[]{:S(2)}, u32[]{:S(2)}) collective-permute-start(bf16[128,2048]{1,0:T(8,128)(2,1)S(1)} %multiply_convert_fusion), channel_id=1, source_target_pairs={{0,1},{1,2},{2,3},{3,4},{4,5},{5,6},{6,7},{7,8},{8,9},{9,10},{10,1... | collective-permute-start | bytes 1572872 | tf_op jit(solution)/shard_map/ppermute | solution.py:22
  6.3 14.3 %collective-permute-start.2 = (bf16[128,2048]{0,1:T(8,128)(2,1)S(1)}, bf16[128,2048]{0,1:T(8,128)(2,1)}, u32[]{:S(2)}, u32[]{:S(2)}) collective-permute-start(bf16[128,2048]{0,1:T(8,128)(2,1)S(1)} %bitcast.41), channel_id=1, source_target_pairs={{0,4},{4,8},{8,12},{12,14},{14,10},{10,6},{6,2},{2,0},{1,5},{5,9},... | collective-permute-start | bytes 1572872 | tf_op jit(solution)/shard_map/ppermute | solution.py:144
  8.9 14.5 %collective-permute-start.3 = (bf16[128,2048]{0,1:T(8,128)(2,1)S(1)}, bf16[128,2048]{0,1:T(8,128)(2,1)S(1)}, u32[]{:S(2)}, u32[]{:S(2)}) collective-permute-start(bf16[128,2048]{0,1:T(8,128)(2,1)S(1)} %bitcast.42), channel_id=1, source_target_pairs={{4,0},{8,4},{12,8},{14,12},{10,14},{6,10},{2,6},{0,2},{5,1},{9,5},... | collective-permute-start | bytes 1572872 | tf_op jit(solution)/shard_map/ppermute | solution.py:145
  9.9 4.2 %collective-permute-start.1 = (bf16[2,6144]{1,0:T(2,128)(2,1)S(1)}, bf16[2,6144]{1,0:T(2,128)(2,1)S(1)}, u32[]{:S(2)}, u32[]{:S(2)}) collective-permute-start(bf16[2,6144]{1,0:T(2,128)(2,1)S(1)} %slice.72), channel_id=1, source_target_pairs={{0,1},{1,2},{2,3},{3,4},{4,5},{5,6},{6,7},{7,8},{8,9},{9,10},{10,1... | collective-permute-start | bytes 73736 | tf_op jit(solution)/shard_map/ppermute | solution.py:22
  14.1 16.7 %copy-start.4 = (bf16[2,6144]{1,0:T(2,128)(2,1)}, bf16[2,6144]{1,0:T(2,128)(2,1)S(1)}, u32[]{:S(2)}) copy-start(bf16[2,6144]{1,0:T(2,128)(2,1)S(1)} %collective-permute-done.1) | copy-start | bytes 73732
  14.1 16.7 %copy-start.1 = (bf16[128,2048]{1,0:T(8,128)(2,1)}, bf16[128,2048]{1,0:T(8,128)(2,1)S(1)}, u32[]{:S(2)}) copy-start(bf16[128,2048]{1,0:T(8,128)(2,1)S(1)} %collective-permute-done.halo_ref) | copy-start | bytes 1572868
  23.5 17.4 %collective-permute-start.4 = (bf16[128,2048]{0,1:T(8,128)(2,1)}, bf16[128,2048]{0,1:T(8,128)(2,1)}, u32[]{:S(2)}, u32[]{:S(2)}) collective-permute-start(bf16[128,2048]{0,1:T(8,128)(2,1)} %collective-permute-done.2), channel_id=1, source_target_pairs={{0,4},{4,8},{8,12},{12,14},{14,10},{10,6},{6,2},{2,0},{1,5},{5,9},... | collective-permute-start | bytes 1572872 | tf_op jit(solution)/shard_map/ppermute | solution.py:144
  29.9 10.9 %collective-permute-start.5 = (bf16[128,2048]{0,1:T(8,128)(2,1)S(1)}, bf16[128,2048]{0,1:T(8,128)(2,1)}, u32[]{:S(2)}, u32[]{:S(2)}) collective-permute-start(bf16[128,2048]{0,1:T(8,128)(2,1)S(1)} %collective-permute-done.3), channel_id=1, source_target_pairs={{4,0},{8,4},{12,8},{14,12},{10,14},{6,10},{2,6},{0,2},{5,1},{9,5},... | collective-permute-start | bytes 1572872 | tf_op jit(solution)/shard_map/ppermute | solution.py:145
  40.9 15.5 %collective-permute-start.6 = (bf16[128,2048]{0,1:T(8,128)(2,1)}, bf16[128,2048]{0,1:T(8,128)(2,1)S(1)}, u32[]{:S(2)}, u32[]{:S(2)}) collective-permute-start(bf16[128,2048]{0,1:T(8,128)(2,1)} %collective-permute-done.4), channel_id=1, source_target_pairs={{0,4},{4,8},{8,12},{12,14},{14,10},{10,6},{6,2},{2,0},{1,5},{5,9},... | collective-permute-start | bytes 1572872 | tf_op jit(solution)/shard_map/ppermute | solution.py:144
  44.7 12.3 %collective-permute-start.7 = (bf16[128,2048]{0,1:T(8,128)(2,1)}, bf16[128,2048]{0,1:T(8,128)(2,1)S(1)}, u32[]{:S(2)}, u32[]{:S(2)}) collective-permute-start(bf16[128,2048]{0,1:T(8,128)(2,1)} %collective-permute-done.5), channel_id=1, source_target_pairs={{4,0},{8,4},{12,8},{14,12},{10,14},{6,10},{2,6},{0,2},{5,1},{9,5},... | collective-permute-start | bytes 1572872 | tf_op jit(solution)/shard_map/ppermute | solution.py:145
  44.7 12.3 %collective-permute-start.8 = (bf16[128,2048]{0,1:T(8,128)(2,1)S(1)}, bf16[128,2048]{0,1:T(8,128)(2,1)}, u32[]{:S(2)}, u32[]{:S(2)}) collective-permute-start(bf16[128,2048]{0,1:T(8,128)(2,1)S(1)} %bitcast.43), channel_id=1, source_target_pairs={{0,1},{1,0},{2,3},{3,2},{4,5},{5,4},{6,7},{7,6},{8,9},{9,8},{10,11... | collective-permute-start | bytes 1572872 | tf_op jit(solution)/shard_map/ppermute | solution.py:152
  44.7 16.9 %collective-permute-start.9 = (bf16[128,2048]{0,1:T(8,128)(2,1)}, bf16[128,2048]{0,1:T(8,128)(2,1)}, u32[]{:S(2)}, u32[]{:S(2)}) collective-permute-start(bf16[128,2048]{0,1:T(8,128)(2,1)} %collective-permute-done.2), channel_id=1, source_target_pairs={{0,1},{1,0},{2,3},{3,2},{4,5},{5,4},{6,7},{7,6},{8,9},{9,8},{10,11... | collective-permute-start | bytes 1572872 | tf_op jit(solution)/shard_map/ppermute | solution.py:146
  45.2 18.8 %collective-permute-start.10 = (bf16[128,2048]{0,1:T(8,128)(2,1)S(1)}, bf16[128,2048]{0,1:T(8,128)(2,1)}, u32[]{:S(2)}, u32[]{:S(2)}) collective-permute-start(bf16[128,2048]{0,1:T(8,128)(2,1)S(1)} %collective-permute-done.3), channel_id=1, source_target_pairs={{0,1},{1,0},{2,3},{3,2},{4,5},{5,4},{6,7},{7,6},{8,9},{9,8},{10,11... | collective-permute-start | bytes 1572872 | tf_op jit(solution)/shard_map/ppermute | solution.py:147
  46.1 8.8 %copy-start = (bf16[512,1024]{1,0:T(8,128)(2,1)S(1)}, bf16[512,1024]{1,0:T(8,128)(2,1)}, u32[]{:S(2)}) copy-start(bf16[512,1024]{1,0:T(8,128)(2,1)} %shard_map.64) | copy-start | bytes 3145732
  56.3 9.9 %collective-permute-start.11 = (bf16[128,2048]{0,1:T(8,128)(2,1)}, bf16[128,2048]{0,1:T(8,128)(2,1)S(1)}, u32[]{:S(2)}, u32[]{:S(2)}) collective-permute-start(bf16[128,2048]{0,1:T(8,128)(2,1)} %collective-permute-done.4), channel_id=1, source_target_pairs={{0,1},{1,0},{2,3},{3,2},{4,5},{5,4},{6,7},{7,6},{8,9},{9,8},{10,11... | collective-permute-start | bytes 1572872 | tf_op jit(solution)/shard_map/ppermute | solution.py:146
  56.9 11.7 %collective-permute-start.12 = (bf16[128,2048]{0,1:T(8,128)(2,1)}, bf16[128,2048]{0,1:T(8,128)(2,1)S(1)}, u32[]{:S(2)}, u32[]{:S(2)}) collective-permute-start(bf16[128,2048]{0,1:T(8,128)(2,1)} %collective-permute-done.5), channel_id=1, source_target_pairs={{0,1},{1,0},{2,3},{3,2},{4,5},{5,4},{6,7},{7,6},{8,9},{9,8},{10,11... | collective-permute-start | bytes 1572872 | tf_op jit(solution)/shard_map/ppermute | solution.py:147
  57.0 13.7 %collective-permute-start.15 = (bf16[128,1024]{0,1:T(8,128)(2,1)S(1)}, bf16[128,1024]{0,1:T(8,128)(2,1)S(1)}, u32[]{:S(2)}, u32[]{:S(2)}) collective-permute-start(bf16[128,1024]{0,1:T(8,128)(2,1)S(1)} %slice.73), channel_id=1, source_target_pairs={{0,4},{4,8},{8,12},{12,14},{14,10},{10,6},{6,2},{2,0},{1,5},{5,9},... | collective-permute-start | bytes 786440 | tf_op jit(solution)/shard_map/ppermute | solution.py:179
  61.6 9.1 %collective-permute-start.16 = (bf16[128,1024]{0,1:T(8,128)(2,1)S(1)}, bf16[128,1024]{0,1:T(8,128)(2,1)S(1)}, u32[]{:S(2)}, u32[]{:S(2)}) collective-permute-start(bf16[128,1024]{0,1:T(8,128)(2,1)S(1)} %slice.74), channel_id=1, source_target_pairs={{4,0},{8,4},{12,8},{14,12},{10,14},{6,10},{2,6},{0,2},{5,1},{9,5},... | collective-permute-start | bytes 786440 | tf_op jit(solution)/shard_map/ppermute | solution.py:180
  64.1 6.9 %collective-permute-start.13 = (bf16[128,2048]{0,1:T(8,128)(2,1)S(1)}, bf16[128,2048]{0,1:T(8,128)(2,1)S(1)}, u32[]{:S(2)}, u32[]{:S(2)}) collective-permute-start(bf16[128,2048]{0,1:T(8,128)(2,1)S(1)} %collective-permute-done.6), channel_id=1, source_target_pairs={{0,1},{1,0},{2,3},{3,2},{4,5},{5,4},{6,7},{7,6},{8,9},{9,8},{10,11... | collective-permute-start | bytes 1572872 | tf_op jit(solution)/shard_map/ppermute | solution.py:146
  66.3 5.5 %collective-permute-start.14 = (bf16[128,2048]{0,1:T(8,128)(2,1)S(1)}, bf16[128,2048]{0,1:T(8,128)(2,1)S(1)}, u32[]{:S(2)}, u32[]{:S(2)}) collective-permute-start(bf16[128,2048]{0,1:T(8,128)(2,1)S(1)} %collective-permute-done.7), channel_id=1, source_target_pairs={{0,1},{1,0},{2,3},{3,2},{4,5},{5,4},{6,7},{7,6},{8,9},{9,8},{10,11... | collective-permute-start | bytes 1572872 | tf_op jit(solution)/shard_map/ppermute | solution.py:147
  70.7 2.0 %collective-permute-start.17 = (bf16[128,2048]{0,1:T(8,128)(2,1)S(1)}, bf16[128,2048]{0,1:T(8,128)(2,1)S(1)}, u32[]{:S(2)}, u32[]{:S(2)}) collective-permute-start(bf16[128,2048]{0,1:T(8,128)(2,1)S(1)} %constant_dynamic-update-slice_fusion), channel_id=1, source_target_pairs={{0,1},{1,0},{2,3},{3,2},{4,5},{5,4},{6,7},{7,6},{8,9},{9,8},{10,11... | collective-permute-start | bytes 1572872 | tf_op jit(solution)/shard_map/ppermute | solution.py:184
  72.5 1.6 %copy-start.2 = (bf16[512,2048]{1,0:T(8,128)(2,1)S(1)}, bf16[512,2048]{1,0:T(8,128)(2,1)}, u32[]{:S(2)}) copy-start(bf16[512,2048]{1,0:T(8,128)(2,1)} %param.6) | copy-start | bytes 6291460

commit v21 on v20

--- a/solution.py
+++ b/solution.py
@@ -179,14 +179,16 @@
     ahead = lax.ppermute(ahead[:, :half], "chip", forward)
     behind = lax.ppermute(behind[:, half:], "chip", backward)
     source = ring_chip((position - steps) % chips, chips)
-    branch = jnp.zeros((row_count, chips * 2 * width), jnp.float32)
+    result = tokens
     last = jnp.concatenate([ahead, behind], axis=1)
     late.append((last, lax.ppermute(last, "core", swap), source))
     for mine, other, owner_chip in late:
         pair = jnp.where(core == 0, jnp.concatenate([mine, other]), jnp.concatenate([other, mine]))
         part = lax.dot_general(gated, pair, (((1,), (1,)), ((), ())), preferred_element_type=jnp.float32)
-        branch = lax.dynamic_update_slice(branch, part, (0, owner_chip * 2 * width))
-    return (tokens.astype(jnp.float32) + branch).astype(jnp.bfloat16)
+        column = owner_chip * 2 * width
+        rows = lax.dynamic_slice_in_dim(tokens, column, 2 * width, 1).astype(jnp.float32)
+        result = lax.dynamic_update_slice(result, (rows + part).astype(jnp.bfloat16), (0, column))
+    return result
 
 
 def solution(mesh):

time: 76.9 us -> 75.5 us (0.982)
  other arithmetic: 8.01 us -> 6.08 us
    convert_element_type x1 -> x0, other arithmetic: 2.07 us -> none  [on_device(): return (tokens.astype(jnp.float32) + branch).astype(jnp.bfloat16)]
  transfers between devices with their start and end apart: 18 -> 18, of which waited for: 6 -> 5; matrix products, arithmetic and copies ran while one was open for 22% -> 21% of each run, Pallas kernels for 23% -> 23%
where the time goes in v21:
time: 75.5 us; the launch traced here: 74.9 us
  starting transfers between devices  22.9 us (30%)
  Pallas kernels  17.4 us (23%)
  matrix products  13.2 us (17%)
  waiting for transfers between devices  11.8 us (16%)
  other arithmetic  6.08 us (8%)
  local copies, waits for them, and re-layouts  3.28 us (4%)
    pallas_call x2, Pallas kernels, hyena_gate(): pl.pallas_call(_gate_kernel, grid=(share,), in_specs=[pl.BlockSpec((per_t...  17.4 us
    dot_general x8, matrix products, on_device(): lax.dot_general(gated, pair, (((1,), (1,)), ((), ())), preferred_element_...  13.2 us
    ppermute x3, starting transfers between devices, ring_step(): ahead = lax.ppermute(ahead, 'chip', forward)  12.9 us
    ppermute x3, waiting for transfers between devices, ring_step(): ahead = lax.ppermute(ahead, 'chip', forward)  7.93 us
    ppermute x2, starting transfers between devices, shifted(): return lax.ppermute(block, CTX, route)  5.8 us
    convert_element_type x1, other arithmetic, carried_of(): return (second * carrier).astype(jnp.bfloat16)  2.95 us
    ppermute x3, waiting for transfers between devices, ring_step(): behind = lax.ppermute(behind, 'chip', backward)  2.8 us
    ppermute x1, starting transfers between devices, on_device(): ahead = lax.ppermute(ahead[:, :half], 'chip', forward)  2.07 us
  transfers between devices with their start and end apart: 18, of which 5 were waited for; matrix products, arithmetic and copies ran while one was open for 21% of the time, Pallas kernels for 23%

profile of v21, /device:TPU:0, one launch (start us, length us, event | category | flops | bytes accessed | tf_op | source)
XLA Modules:
  0.0 74.9 jit_solution(13027415118622936039)
XLA Ops:
  0.0 1.0 %fusion.72 = (f32[1,2048]{1,0:T(1,128)S(1)}, f32[1,2048]{1,0:T(1,128)S(1)}, f32[1,2048]{1,0:T(1,128)S(1)}, f32[1,2048]{1,0:T(1,128)S(1)}, f32[1,2048]{1,0:T(1,128)S(1)}, /*index=5*/f32[1,2048]{1,0:T(1,128)S(1)}) fusion(f32[3,6144]{1,0:T(4,128)} %param.8), kind=kLoop, calls=%fused_computation.94 | loop fusion | bytes 98304 | tf_op jit(solution)/shard_map/slice | solution.py:34
  1.0 3.0 %multiply_convert_fusion = bf16[128,2048]{1,0:T(8,128)(2,1)S(1)} fusion(bf16[512,6144]{1,0:T(8,128)(2,1)} %carrier_ref.2, f32[2048]{0:T(1024)S(1)} %bitcast.40, f32[2048]{0:T(1024)S(1)} %bitcast.36, f32[2048]{0:T(1024)S(1)} %bitcast.37, f32[2048]{0:T(1024)S(1)} %bitcast.38, f32[2048]{0:T(1024)S(1)} %bitcast.39, f32[2048]{0:T(1024)S(1)} %bitcast.35), kind=kLoop, calls=%fused_computation.73 | loop fusion | flops 4718592 | bytes 3719168 | tf_op jit(solution)/shard_map/convert_element_type | solution.py:122
  3.9 2.4 %collective-permute-start = (bf16[128,2048]{1,0:T(8,128)(2,1)S(1)}, bf16[128,2048]{1,0:T(8,128)(2,1)S(1)}, u32[]{:S(2)}, u32[]{:S(2)}) collective-permute-start(bf16[128,2048]{1,0:T(8,128)(2,1)S(1)} %multiply_convert_fusion), channel_id=1, source_target_pairs={{0,1},{1,2},{2,3},{3,4},{4,5},{5,6},{6,7},{7,8},{8,9},{9,10},{10,1... | collective-permute-start | bytes 1572872 | tf_op jit(solution)/shard_map/ppermute | solution.py:22
  6.3 2.6 %collective-permute-start.2 = (bf16[128,2048]{0,1:T(8,128)(2,1)S(1)}, bf16[128,2048]{0,1:T(8,128)(2,1)}, u32[]{:S(2)}, u32[]{:S(2)}) collective-permute-start(bf16[128,2048]{0,1:T(8,128)(2,1)S(1)} %bitcast.41), channel_id=1, source_target_pairs={{0,4},{4,8},{8,12},{12,14},{14,10},{10,6},{6,2},{2,0},{1,5},{5,9},... | collective-permute-start | bytes 1572872 | tf_op jit(solution)/shard_map/ppermute | solution.py:144
  8.9 0.9 %slice.72 = bf16[2,6144]{1,0:T(2,128)(2,1)S(1)} slice(bf16[512,6144]{1,0:T(8,128)(2,1)} %carrier_ref.2), slice={[510:512], [0:6144]} | slice | bytes 49152 | tf_op jit(solution)/shard_map/slice | solution.py:161
  9.9 3.4 %collective-permute-start.1 = (bf16[2,6144]{1,0:T(2,128)(2,1)S(1)}, bf16[2,6144]{1,0:T(2,128)(2,1)S(1)}, u32[]{:S(2)}, u32[]{:S(2)}) collective-permute-start(bf16[2,6144]{1,0:T(2,128)(2,1)S(1)} %slice.72), channel_id=1, source_target_pairs={{0,1},{1,2},{2,3},{3,4},{4,5},{5,6},{6,7},{7,8},{8,9},{9,10},{10,1... | collective-permute-start | bytes 73736 | tf_op jit(solution)/shard_map/ppermute | solution.py:22
  13.3 0.8 %collective-permute-done.1 = bf16[2,6144]{1,0:T(2,128)(2,1)S(1)} collective-permute-done((bf16[2,6144]{1,0:T(2,128)(2,1)S(1)}, bf16[2,6144]{1,0:T(2,128)(2,1)S(1)}, u32[]{:S(2)}, u32[]{:S(2)}) %collective-permute-start.1) | collective-permute-done | bytes 24608 | tf_op jit(solution)/shard_map/ppermute | solution.py:22
  14.1 6.5 %collective-permute-done.2 = bf16[128,2048]{0,1:T(8,128)(2,1)} collective-permute-done((bf16[128,2048]{0,1:T(8,128)(2,1)S(1)}, bf16[128,2048]{0,1:T(8,128)(2,1)}, u32[]{:S(2)}, u32[]{:S(2)}) %collective-permute-start.2) | collective-permute-done | bytes 524320 | tf_op jit(solution)/shard_map/ppermute | solution.py:144
  20.7 2.8 %collective-permute-done.3 = bf16[128,2048]{0,1:T(8,128)(2,1)S(1)} collective-permute-done((bf16[128,2048]{0,1:T(8,128)(2,1)S(1)}, bf16[128,2048]{0,1:T(8,128)(2,1)S(1)}, u32[]{:S(2)}, u32[]{:S(2)}) %collective-permute-start.3) | collective-permute-done | bytes 524320 | tf_op jit(solution)/shard_map/ppermute | solution.py:145
  23.5 6.5 %collective-permute-start.4 = (bf16[128,2048]{0,1:T(8,128)(2,1)}, bf16[128,2048]{0,1:T(8,128)(2,1)}, u32[]{:S(2)}, u32[]{:S(2)}) collective-permute-start(bf16[128,2048]{0,1:T(8,128)(2,1)} %collective-permute-done.2), channel_id=1, source_target_pairs={{0,4},{4,8},{8,12},{12,14},{14,10},{10,6},{6,2},{2,0},{1,5},{5,9},... | collective-permute-start | bytes 1572872 | tf_op jit(solution)/shard_map/ppermute | solution.py:144
  30.0 0.8 %pad_convert_fusion.1.fw_ref = f32[128,384]{1,0:T(8,128)} fusion(bf16[128,128]{1,0:T(8,128)(2,1)S(1)} %rev.6), kind=kLoop, calls=%fused_computation.83 | loop fusion | flops 49152 | bytes 229376 | tf_op jit(solution)/shard_map/jit(_pad)/pad | solution.py:91
  30.8 8.7 %shard_map.64 = bf16[512,1024]{1,0:T(8,128)(2,1)} custom-call(f32[128,384]{1,0:T(8,128)} %pad_convert_fusion.1.fw_ref, f32[1,2048]{1,0:T(1,128)} %bitcast.33, f32[3,3,2048]{2,1,0:T(4,128)} %bitcast.29, bf16[3,2,2048]{2,1,0:T(2,128)(2,1)} %bitcast.31, bf16[128,2048]{1,0:T(8,128)(2,1)} %copy-done.1, bf16[512,6144]{1,0:T(8,128)(2,1)} %carrier_ref.2, ...), custom_call_target="tpu_custom_call" | custom-call | tf_op jit(solution)/shard_map/pallas_call | solution.py:95
  39.4 1.4 %collective-permute-done.4 = bf16[128,2048]{0,1:T(8,128)(2,1)} collective-permute-done((bf16[128,2048]{0,1:T(8,128)(2,1)}, bf16[128,2048]{0,1:T(8,128)(2,1)}, u32[]{:S(2)}, u32[]{:S(2)}) %collective-permute-start.4) | collective-permute-done | bytes 524320 | tf_op jit(solution)/shard_map/ppermute | solution.py:144
  40.9 3.8 %collective-permute-start.6 = (bf16[128,2048]{0,1:T(8,128)(2,1)}, bf16[128,2048]{0,1:T(8,128)(2,1)S(1)}, u32[]{:S(2)}, u32[]{:S(2)}) collective-permute-start(bf16[128,2048]{0,1:T(8,128)(2,1)} %collective-permute-done.4), channel_id=1, source_target_pairs={{0,4},{4,8},{8,12},{12,14},{14,10},{10,6},{6,2},{2,0},{1,5},{5,9},... | collective-permute-start | bytes 1572872 | tf_op jit(solution)/shard_map/ppermute | solution.py:144
  44.7 0.5 collective-permute-start.9
  45.3 0.8 %pad_convert_fusion.fw_ref = f32[128,384]{1,0:T(8,128)} fusion(bf16[128,128]{1,0:T(8,128)(2,1)S(1)} %rev.7), kind=kLoop, calls=%fused_computation.82 | loop fusion | flops 49152 | bytes 229376 | tf_op jit(solution)/shard_map/jit(_pad)/pad | solution.py:91
  46.1 8.8 %shard_map.65 = bf16[512,1024]{1,0:T(8,128)(2,1)} custom-call(f32[128,384]{1,0:T(8,128)} %pad_convert_fusion.fw_ref, f32[1,2048]{1,0:T(1,128)} %bitcast.34, f32[3,3,2048]{2,1,0:T(4,128)} %bitcast.30, bf16[3,2,2048]{2,1,0:T(2,128)(2,1)} %bitcast.32, bf16[128,2048]{1,0:T(8,128)(2,1)} %copy-done.1, bf16[512,6144]{1,0:T(8,128)(2,1)} %carrier_ref.2, ...), custom_call_target="tpu_custom_call" | custom-call | tf_op jit(solution)/shard_map/pallas_call | solution.py:95
  54.9 1.6 %pad_maximum_fusion = bf16[512,2048]{1,0:T(8,128)(2,1)S(1)} fusion(bf16[512,1024]{1,0:T(8,128)(2,1)} %shard_map.65, bf16[512,1024]{1,0:T(8,128)(2,1)S(1)} %copy-done), kind=kLoop, calls=%fused_computation | loop fusion | flops 4194304 | bytes 4194304 | tf_op jit(solution)/shard_map/concatenate | solution.py:172
  56.5 0.6 collective-permute-start.11
  57.2 2.1 %collective-permute-start.15 = (bf16[128,1024]{0,1:T(8,128)(2,1)S(1)}, bf16[128,1024]{0,1:T(8,128)(2,1)S(1)}, u32[]{:S(2)}, u32[]{:S(2)}) collective-permute-start(bf16[128,1024]{0,1:T(8,128)(2,1)S(1)} %slice.73), channel_id=1, source_target_pairs={{0,4},{4,8},{8,12},{12,14},{14,10},{10,6},{6,2},{2,0},{1,5},{5,9},... | collective-permute-start | bytes 786440 | tf_op jit(solution)/shard_map/ppermute | solution.py:179
  59.2 2.0 %fusion.15 = bf16[512,2048]{1,0:T(8,128)(2,1)S(1)} fusion(bf16[512,2048]{1,0:T(8,128)(2,1)S(1)} %copy-done.4, s32[]{:T(128)S(6)} %select_n.132, bf16[512,2048]{1,0:T(8,128)(2,1)S(1)} %pad_maximum_fusion, bf16[128,2048]{0,1:T(8,128)(2,1)} %collective-permute-done.8, bf16[128,2048]{0,1:T(8,128)(2,1)S(1)} %bitcast.44, pred[]{:T(512)S(6)} %eq.22), kind=kOutput, calls=%fused_computation.24 | convolution fusion | flops 541982720 | bytes 3670021 | tf_op jit(solution)/shard_map/dot_general | solution.py:187
  61.3 2.3 %fusion.14 = bf16[512,2048]{1,0:T(8,128)(2,1)S(1)} fusion(bf16[512,2048]{1,0:T(8,128)(2,1)S(1)} %fusion.15, s32[]{:T(128)S(6)} %select_n.140, bf16[512,2048]{1,0:T(8,128)(2,1)S(1)} %pad_maximum_fusion, bf16[128,2048]{0,1:T(8,128)(2,1)} %collective-permute-done.9, bf16[128,2048]{0,1:T(8,128)(2,1)} %collective-permute-done.2, pred[]{:T(512)S(6)} %eq.22, ...), kind=kOutput, calls=%fused_computation.23 | convolution fusion | flops 541982720 | bytes 3670021 | tf_op jit(solution)/shard_map/dot_general | solution.py:187
  63.7 0.2 collective-permute-start.13
  63.9 2.0 %fusion.13 = bf16[512,2048]{1,0:T(8,128)(2,1)S(1)} fusion(bf16[512,2048]{1,0:T(8,128)(2,1)S(1)} %fusion.14, s32[]{:T(128)S(6)} %select_n.144, bf16[512,2048]{1,0:T(8,128)(2,1)S(1)} %pad_maximum_fusion, bf16[128,2048]{0,1:T(8,128)(2,1)} %collective-permute-done.10, bf16[128,2048]{0,1:T(8,128)(2,1)S(1)} %collective-permute-done.3, pred[]{:T(512)S(6)} %eq.22, ...), kind=kOutput, calls=%fused_computation.22 | convolution fusion | flops 541982720 | bytes 3670021 | tf_op jit(solution)/shard_map/dot_general | solution.py:187
  65.9 0.4 collective-permute-start.14
  66.3 2.0 %fusion.12 = bf16[512,2048]{1,0:T(8,128)(2,1)S(1)} fusion(bf16[512,2048]{1,0:T(8,128)(2,1)S(1)} %fusion.13, s32[]{:T(128)S(6)} %select_n.148, bf16[512,2048]{1,0:T(8,128)(2,1)S(1)} %pad_maximum_fusion, bf16[128,2048]{0,1:T(8,128)(2,1)S(1)} %collective-permute-done.11, bf16[128,2048]{0,1:T(8,128)(2,1)} %collective-permute-done.4, pred[]{:T(512)S(6)} %eq.22, ...), kind=kOutput, calls=%fused_computation.21 | convolution fusion | flops 541982720 | bytes 3670021 | tf_op jit(solution)/shard_map/dot_general | solution.py:187
  68.3 2.0 %fusion.11 = bf16[512,2048]{1,0:T(8,128)(2,1)S(1)} fusion(bf16[512,2048]{1,0:T(8,128)(2,1)S(1)} %fusion.12, s32[]{:T(128)S(6)} %select_n.152, bf16[512,2048]{1,0:T(8,128)(2,1)S(1)} %pad_maximum_fusion, bf16[128,2048]{0,1:T(8,128)(2,1)S(1)} %collective-permute-done.12, bf16[128,2048]{0,1:T(8,128)(2,1)} %collective-permute-done.5, pred[]{:T(512)S(6)} %eq.22, ...), kind=kOutput, calls=%fused_computation.20 | convolution fusion | flops 541982720 | bytes 3670021 | tf_op jit(solution)/shard_map/dot_general | solution.py:187
  70.6 0.7 fusion.10
  71.4 0.7 fusion.9
  72.1 0.2 collective-permute-done.17
  72.3 1.1 %copy-done.3 = bf16[512,2048]{1,0:T(8,128)(2,1)} copy-done((bf16[512,2048]{1,0:T(8,128)(2,1)}, bf16[512,2048]{1,0:T(8,128)(2,1)S(1)}, u32[]{:S(2)}) %copy-start.3) | copy-done | bytes 2097176
  73.4 1.4 %fusion.8 = bf16[512,2048]{1,0:T(8,128)(2,1)} fusion(bf16[512,2048]{1,0:T(8,128)(2,1)} %copy-done.3, s32[]{:T(128)S(6)} %select_n.164, bf16[512,2048]{1,0:T(8,128)(2,1)S(1)} %pad_maximum_fusion, bf16[128,2048]{0,1:T(8,128)(2,1)S(1)} %collective-permute-done.17, bf16[128,2048]{0,1:T(8,128)(2,1)S(1)} %constant_dynamic-update-slice_fusion, pred[]{:T(512)S(6)} %eq.22, ...), kind=kOutput, calls=%fused_computation.17 | convolution fusion | flops 541982720 | bytes 3670021 | tf_op jit(solution)/shard_map/dot_general | solution.py:187
  (42 shorter events, 0.7 us)
Async XLA Ops:
  0.0 6.3 %copy-start.7 = (bf16[2048,128]{1,0:T(8,128)(2,1)S(1)}, bf16[2048,128]{1,0:T(8,128)(2,1)}, u32[]{:S(2)}) copy-start(bf16[2048,128]{1,0:T(8,128)(2,1)} %param.11) | copy-start | bytes 1572868
  0.0 29.9 %copy-start.5 = (bf16[128,128]{1,0:T(8,128)(2,1)S(1)}, bf16[128,128]{1,0:T(8,128)(2,1)}, u32[]{:S(2)}) copy-start(bf16[128,128]{1,0:T(8,128)(2,1)} %param.9) | copy-start | bytes 98308
  3.9 10.2 %collective-permute-start = (bf16[128,2048]{1,0:T(8,128)(2,1)S(1)}, bf16[128,2048]{1,0:T(8,128)(2,1)S(1)}, u32[]{:S(2)}, u32[]{:S(2)}) collective-permute-start(bf16[128,2048]{1,0:T(8,128)(2,1)S(1)} %multiply_convert_fusion), channel_id=1, source_target_pairs={{0,1},{1,2},{2,3},{3,4},{4,5},{5,6},{6,7},{7,8},{8,9},{9,10},{10,1... | collective-permute-start | bytes 1572872 | tf_op jit(solution)/shard_map/ppermute | solution.py:22
  6.3 14.3 %collective-permute-start.2 = (bf16[128,2048]{0,1:T(8,128)(2,1)S(1)}, bf16[128,2048]{0,1:T(8,128)(2,1)}, u32[]{:S(2)}, u32[]{:S(2)}) collective-permute-start(bf16[128,2048]{0,1:T(8,128)(2,1)S(1)} %bitcast.41), channel_id=1, source_target_pairs={{0,4},{4,8},{8,12},{12,14},{14,10},{10,6},{6,2},{2,0},{1,5},{5,9},... | collective-permute-start | bytes 1572872 | tf_op jit(solution)/shard_map/ppermute | solution.py:144
  8.9 14.5 %collective-permute-start.3 = (bf16[128,2048]{0,1:T(8,128)(2,1)S(1)}, bf16[128,2048]{0,1:T(8,128)(2,1)S(1)}, u32[]{:S(2)}, u32[]{:S(2)}) collective-permute-start(bf16[128,2048]{0,1:T(8,128)(2,1)S(1)} %bitcast.42), channel_id=1, source_target_pairs={{4,0},{8,4},{12,8},{14,12},{10,14},{6,10},{2,6},{0,2},{5,1},{9,5},... | collective-permute-start | bytes 1572872 | tf_op jit(solution)/shard_map/ppermute | solution.py:145
  9.9 4.2 %collective-permute-start.1 = (bf16[2,6144]{1,0:T(2,128)(2,1)S(1)}, bf16[2,6144]{1,0:T(2,128)(2,1)S(1)}, u32[]{:S(2)}, u32[]{:S(2)}) collective-permute-start(bf16[2,6144]{1,0:T(2,128)(2,1)S(1)} %slice.72), channel_id=1, source_target_pairs={{0,1},{1,2},{2,3},{3,4},{4,5},{5,6},{6,7},{7,8},{8,9},{9,10},{10,1... | collective-permute-start | bytes 73736 | tf_op jit(solution)/shard_map/ppermute | solution.py:22
  14.1 16.7 %copy-start.6 = (bf16[2,6144]{1,0:T(2,128)(2,1)}, bf16[2,6144]{1,0:T(2,128)(2,1)S(1)}, u32[]{:S(2)}) copy-start(bf16[2,6144]{1,0:T(2,128)(2,1)S(1)} %collective-permute-done.1) | copy-start | bytes 73732
  14.1 16.7 %copy-start.1 = (bf16[128,2048]{1,0:T(8,128)(2,1)}, bf16[128,2048]{1,0:T(8,128)(2,1)S(1)}, u32[]{:S(2)}) copy-start(bf16[128,2048]{1,0:T(8,128)(2,1)S(1)} %collective-permute-done.halo_ref) | copy-start | bytes 1572868
  23.5 17.4 %collective-permute-start.4 = (bf16[128,2048]{0,1:T(8,128)(2,1)}, bf16[128,2048]{0,1:T(8,128)(2,1)}, u32[]{:S(2)}, u32[]{:S(2)}) collective-permute-start(bf16[128,2048]{0,1:T(8,128)(2,1)} %collective-permute-done.2), channel_id=1, source_target_pairs={{0,4},{4,8},{8,12},{12,14},{14,10},{10,6},{6,2},{2,0},{1,5},{5,9},... | collective-permute-start | bytes 1572872 | tf_op jit(solution)/shard_map/ppermute | solution.py:144
  29.9 10.9 %collective-permute-start.5 = (bf16[128,2048]{0,1:T(8,128)(2,1)S(1)}, bf16[128,2048]{0,1:T(8,128)(2,1)}, u32[]{:S(2)}, u32[]{:S(2)}) collective-permute-start(bf16[128,2048]{0,1:T(8,128)(2,1)S(1)} %collective-permute-done.3), channel_id=1, source_target_pairs={{4,0},{8,4},{12,8},{14,12},{10,14},{6,10},{2,6},{0,2},{5,1},{9,5},... | collective-permute-start | bytes 1572872 | tf_op jit(solution)/shard_map/ppermute | solution.py:145
  40.9 15.6 %collective-permute-start.6 = (bf16[128,2048]{0,1:T(8,128)(2,1)}, bf16[128,2048]{0,1:T(8,128)(2,1)S(1)}, u32[]{:S(2)}, u32[]{:S(2)}) collective-permute-start(bf16[128,2048]{0,1:T(8,128)(2,1)} %collective-permute-done.4), channel_id=1, source_target_pairs={{0,4},{4,8},{8,12},{12,14},{14,10},{10,6},{6,2},{2,0},{1,5},{5,9},... | collective-permute-start | bytes 1572872 | tf_op jit(solution)/shard_map/ppermute | solution.py:144
  44.7 12.3 %collective-permute-start.7 = (bf16[128,2048]{0,1:T(8,128)(2,1)}, bf16[128,2048]{0,1:T(8,128)(2,1)S(1)}, u32[]{:S(2)}, u32[]{:S(2)}) collective-permute-start(bf16[128,2048]{0,1:T(8,128)(2,1)} %collective-permute-done.5), channel_id=1, source_target_pairs={{4,0},{8,4},{12,8},{14,12},{10,14},{6,10},{2,6},{0,2},{5,1},{9,5},... | collective-permute-start | bytes 1572872 | tf_op jit(solution)/shard_map/ppermute | solution.py:145
  44.7 12.5 %collective-permute-start.8 = (bf16[128,2048]{0,1:T(8,128)(2,1)S(1)}, bf16[128,2048]{0,1:T(8,128)(2,1)}, u32[]{:S(2)}, u32[]{:S(2)}) collective-permute-start(bf16[128,2048]{0,1:T(8,128)(2,1)S(1)} %bitcast.43), channel_id=1, source_target_pairs={{0,1},{1,0},{2,3},{3,2},{4,5},{5,4},{6,7},{7,6},{8,9},{9,8},{10,11... | collective-permute-start | bytes 1572872 | tf_op jit(solution)/shard_map/ppermute | solution.py:152
  44.7 16.5 %collective-permute-start.9 = (bf16[128,2048]{0,1:T(8,128)(2,1)}, bf16[128,2048]{0,1:T(8,128)(2,1)}, u32[]{:S(2)}, u32[]{:S(2)}) collective-permute-start(bf16[128,2048]{0,1:T(8,128)(2,1)} %collective-permute-done.2), channel_id=1, source_target_pairs={{0,1},{1,0},{2,3},{3,2},{4,5},{5,4},{6,7},{7,6},{8,9},{9,8},{10,11... | collective-permute-start | bytes 1572872 | tf_op jit(solution)/shard_map/ppermute | solution.py:146
  45.2 18.5 %collective-permute-start.10 = (bf16[128,2048]{0,1:T(8,128)(2,1)S(1)}, bf16[128,2048]{0,1:T(8,128)(2,1)}, u32[]{:S(2)}, u32[]{:S(2)}) collective-permute-start(bf16[128,2048]{0,1:T(8,128)(2,1)S(1)} %collective-permute-done.3), channel_id=1, source_target_pairs={{0,1},{1,0},{2,3},{3,2},{4,5},{5,4},{6,7},{7,6},{8,9},{9,8},{10,11... | collective-permute-start | bytes 1572872 | tf_op jit(solution)/shard_map/ppermute | solution.py:147
  46.1 8.8 %copy-start = (bf16[512,1024]{1,0:T(8,128)(2,1)S(1)}, bf16[512,1024]{1,0:T(8,128)(2,1)}, u32[]{:S(2)}) copy-start(bf16[512,1024]{1,0:T(8,128)(2,1)} %shard_map.64) | copy-start | bytes 3145732
  54.9 4.4 %copy-start.4 = (bf16[512,2048]{1,0:T(8,128)(2,1)S(1)}, bf16[512,2048]{1,0:T(8,128)(2,1)}, u32[]{:S(2)}) copy-start(bf16[512,2048]{1,0:T(8,128)(2,1)} %param.6) | copy-start | bytes 6291460
  56.5 9.4 %collective-permute-start.11 = (bf16[128,2048]{0,1:T(8,128)(2,1)}, bf16[128,2048]{0,1:T(8,128)(2,1)S(1)}, u32[]{:S(2)}, u32[]{:S(2)}) collective-permute-start(bf16[128,2048]{0,1:T(8,128)(2,1)} %collective-permute-done.4), channel_id=1, source_target_pairs={{0,1},{1,0},{2,3},{3,2},{4,5},{5,4},{6,7},{7,6},{8,9},{9,8},{10,11... | collective-permute-start | bytes 1572872 | tf_op jit(solution)/shard_map/ppermute | solution.py:146
  57.0 11.2 %collective-permute-start.12 = (bf16[128,2048]{0,1:T(8,128)(2,1)}, bf16[128,2048]{0,1:T(8,128)(2,1)S(1)}, u32[]{:S(2)}, u32[]{:S(2)}) collective-permute-start(bf16[128,2048]{0,1:T(8,128)(2,1)} %collective-permute-done.5), channel_id=1, source_target_pairs={{0,1},{1,0},{2,3},{3,2},{4,5},{5,4},{6,7},{7,6},{8,9},{9,8},{10,11... | collective-permute-start | bytes 1572872 | tf_op jit(solution)/shard_map/ppermute | solution.py:147
  57.1 4.2 %copy-start.2 = (bf16[512,2048]{1,0:T(8,128)(2,1)S(1)}, bf16[512,2048]{1,0:T(8,128)(2,1)}, u32[]{:S(2)}) copy-start(bf16[512,2048]{1,0:T(8,128)(2,1)} %param.6) | copy-start | bytes 6291460
  57.2 13.1 %collective-permute-start.15 = (bf16[128,1024]{0,1:T(8,128)(2,1)S(1)}, bf16[128,1024]{0,1:T(8,128)(2,1)S(1)}, u32[]{:S(2)}, u32[]{:S(2)}) collective-permute-start(bf16[128,1024]{0,1:T(8,128)(2,1)S(1)} %slice.73), channel_id=1, source_target_pairs={{0,4},{4,8},{8,12},{12,14},{14,10},{10,6},{6,2},{2,0},{1,5},{5,9},... | collective-permute-start | bytes 786440 | tf_op jit(solution)/shard_map/ppermute | solution.py:179
  61.2 9.1 %collective-permute-start.16 = (bf16[128,1024]{0,1:T(8,128)(2,1)S(1)}, bf16[128,1024]{0,1:T(8,128)(2,1)S(1)}, u32[]{:S(2)}, u32[]{:S(2)}) collective-permute-start(bf16[128,1024]{0,1:T(8,128)(2,1)S(1)} %slice.74), channel_id=1, source_target_pairs={{4,0},{8,4},{12,8},{14,12},{10,14},{6,10},{2,6},{0,2},{5,1},{9,5},... | collective-permute-start | bytes 786440 | tf_op jit(solution)/shard_map/ppermute | solution.py:180
  63.7 6.9 %collective-permute-start.13 = (bf16[128,2048]{0,1:T(8,128)(2,1)S(1)}, bf16[128,2048]{0,1:T(8,128)(2,1)S(1)}, u32[]{:S(2)}, u32[]{:S(2)}) collective-permute-start(bf16[128,2048]{0,1:T(8,128)(2,1)S(1)} %collective-permute-done.6), channel_id=1, source_target_pairs={{0,1},{1,0},{2,3},{3,2},{4,5},{5,4},{6,7},{7,6},{8,9},{9,8},{10,11... | collective-permute-start | bytes 1572872 | tf_op jit(solution)/shard_map/ppermute | solution.py:146
  65.9 5.5 %collective-permute-start.14 = (bf16[128,2048]{0,1:T(8,128)(2,1)S(1)}, bf16[128,2048]{0,1:T(8,128)(2,1)S(1)}, u32[]{:S(2)}, u32[]{:S(2)}) collective-permute-start(bf16[128,2048]{0,1:T(8,128)(2,1)S(1)} %collective-permute-done.7), channel_id=1, source_target_pairs={{0,1},{1,0},{2,3},{3,2},{4,5},{5,4},{6,7},{7,6},{8,9},{9,8},{10,11... | collective-permute-start | bytes 1572872 | tf_op jit(solution)/shard_map/ppermute | solution.py:147
  70.4 2.0 %collective-permute-start.17 = (bf16[128,2048]{0,1:T(8,128)(2,1)S(1)}, bf16[128,2048]{0,1:T(8,128)(2,1)S(1)}, u32[]{:S(2)}, u32[]{:S(2)}) collective-permute-start(bf16[128,2048]{0,1:T(8,128)(2,1)S(1)} %constant_dynamic-update-slice_fusion), channel_id=1, source_target_pairs={{0,1},{1,0},{2,3},{3,2},{4,5},{5,4},{6,7},{7,6},{8,9},{9,8},{10,11... | collective-permute-start | bytes 1572872 | tf_op jit(solution)/shard_map/ppermute | solution.py:184
  72.1 1.3 %copy-start.3 = (bf16[512,2048]{1,0:T(8,128)(2,1)}, bf16[512,2048]{1,0:T(8,128)(2,1)S(1)}, u32[]{:S(2)}) copy-start(bf16[512,2048]{1,0:T(8,128)(2,1)S(1)} %fusion.9) | copy-start | bytes 6291460

commit v22 on v21

--- a/solution.py
+++ b/solution.py
@@ -174,7 +174,6 @@
         weight = lax.all_gather(out_weight.T, CTX, axis=0, tiled=True)
         branch = lax.dot_general(gated, weight, (((1,), (1,)), ((), ())), preferred_element_type=jnp.float32)
         return (tokens.astype(jnp.float32) + branch).astype(jnp.bfloat16)
-    gated, ahead, behind = lax.optimization_barrier((gated, ahead, behind))
     half = channels // 2
     ahead = lax.ppermute(ahead[:, :half], "chip", forward)
     behind = lax.ppermute(behind[:, half:], "chip", backward)

time: 75.5 us -> 84.6 us (1.12)
  waiting for transfers between devices: 11.8 us -> 16.2 us
  matrix products: 13.2 us -> 16.7 us
  local copies, waits for them, and re-layouts: 3.28 us -> 6.13 us
  other arithmetic: 6.08 us -> 4.5 us
    ppermute x1, waiting for transfers between devices: 0.01 us -> 5.11 us  [on_device(): behind = lax.ppermute(behind[:, half:], 'chip', backward)]
    dot_general x8, matrix products: 13.2 us -> 16.7 us  [on_device(): lax.dot_general(gated, pair, (((1,), (1,)), ((), ())), preferred_element_...]
    concatenate x1 -> x0, other arithmetic: 1.58 us -> none  [on_device(): gated = jnp.concatenate([first, second], axis=1)]
    unnamed x17, local copies, waits for them, and re-layouts: 1.14 us -> 2.1 us
    slice x1, local copies, waits for them, and re-layouts: 0.02 us -> 0.97 us  [on_device(): ahead = lax.ppermute(ahead[:, :half], 'chip', forward)]
    slice x1, local copies, waits for them, and re-layouts: 0.02 us -> 0.97 us  [on_device(): behind = lax.ppermute(behind[:, half:], 'chip', backward)]
    ppermute x3, waiting for transfers between devices: 7.93 us -> 7.06 us  [ring_step(): ahead = lax.ppermute(ahead, 'chip', forward)]
  transfers between devices with their start and end apart: 18 -> 18, of which waited for: 5 -> 6; matrix products, arithmetic and copies ran while one was open for 21% -> 24% of each run, Pallas kernels for 23% -> 21%
where the time goes in v22:
time: 84.6 us; the launch traced here: 83.7 us
  starting transfers between devices  22.4 us (26%)
  Pallas kernels  17.5 us (21%)
  matrix products  16.7 us (20%)
  waiting for transfers between devices  16.2 us (19%)
  local copies, waits for them, and re-layouts  6.13 us (7%)
  other arithmetic  4.5 us (5%)
    pallas_call x2, Pallas kernels, hyena_gate(): pl.pallas_call(_gate_kernel, grid=(share,), in_specs=[pl.BlockSpec((per_t...  17.5 us
    dot_general x8, matrix products, on_device(): lax.dot_general(gated, pair, (((1,), (1,)), ((), ())), preferred_element_...  16.7 us
    ppermute x3, starting transfers between devices, ring_step(): ahead = lax.ppermute(ahead, 'chip', forward)  12.9 us
    ppermute x3, waiting for transfers between devices, ring_step(): ahead = lax.ppermute(ahead, 'chip', forward)  7.06 us
    ppermute x2, starting transfers between devices, shifted(): return lax.ppermute(block, CTX, route)  5.8 us
    ppermute x1, waiting for transfers between devices, on_device(): behind = lax.ppermute(behind[:, half:], 'chip', backward)  5.11 us
    convert_element_type x1, other arithmetic, carried_of(): return (second * carrier).astype(jnp.bfloat16)  2.95 us
    ppermute x3, waiting for transfers between devices, ring_step(): behind = lax.ppermute(behind, 'chip', backward)  2.8 us
  transfers between devices with their start and end apart: 18, of which 6 were waited for; matrix products, arithmetic and copies ran while one was open for 24% of the time, Pallas kernels for 21%

profile of v22, /device:TPU:0, one launch (start us, length us, event | category | flops | bytes accessed | tf_op | source)
XLA Modules:
  0.0 83.7 jit_solution(9094245139167013877)
XLA Ops:
  0.0 1.0 %fusion.72 = (f32[1,2048]{1,0:T(1,128)S(1)}, f32[1,2048]{1,0:T(1,128)S(1)}, f32[1,2048]{1,0:T(1,128)S(1)}, f32[1,2048]{1,0:T(1,128)S(1)}, f32[1,2048]{1,0:T(1,128)S(1)}, /*index=5*/f32[1,2048]{1,0:T(1,128)S(1)}) fusion(f32[3,6144]{1,0:T(4,128)} %param.8), kind=kLoop, calls=%fused_computation.94 | loop fusion | bytes 98304 | tf_op jit(solution)/shard_map/slice | solution.py:34
  1.0 3.0 %multiply_convert_fusion = bf16[128,2048]{1,0:T(8,128)(2,1)S(1)} fusion(bf16[512,6144]{1,0:T(8,128)(2,1)} %carrier_ref.2, f32[2048]{0:T(1024)S(1)} %bitcast.32, f32[2048]{0:T(1024)S(1)} %bitcast.28, f32[2048]{0:T(1024)S(1)} %bitcast.29, f32[2048]{0:T(1024)S(1)} %bitcast.30, f32[2048]{0:T(1024)S(1)} %bitcast.31, f32[2048]{0:T(1024)S(1)} %bitcast.27), kind=kLoop, calls=%fused_computation.73 | loop fusion | flops 4718592 | bytes 3719168 | tf_op jit(solution)/shard_map/convert_element_type | solution.py:122
  3.9 2.4 %collective-permute-start = (bf16[128,2048]{1,0:T(8,128)(2,1)S(1)}, bf16[128,2048]{1,0:T(8,128)(2,1)S(1)}, u32[]{:S(2)}, u32[]{:S(2)}) collective-permute-start(bf16[128,2048]{1,0:T(8,128)(2,1)S(1)} %multiply_convert_fusion), channel_id=1, source_target_pairs={{0,1},{1,2},{2,3},{3,4},{4,5},{5,6},{6,7},{7,8},{8,9},{9,10},{10,1... | collective-permute-start | bytes 1572872 | tf_op jit(solution)/shard_map/ppermute | solution.py:22
  6.3 2.6 %collective-permute-start.2 = (bf16[128,2048]{0,1:T(8,128)(2,1)}, bf16[128,2048]{0,1:T(8,128)(2,1)}, u32[]{:S(2)}, u32[]{:S(2)}) collective-permute-start(bf16[128,2048]{0,1:T(8,128)(2,1)} %bitcast.9), channel_id=1, source_target_pairs={{0,4},{4,8},{8,12},{12,14},{14,10},{10,6},{6,2},{2,0},{1,5},{5,9},... | collective-permute-start | bytes 1572872 | tf_op jit(solution)/shard_map/ppermute | solution.py:144
  8.9 0.9 %slice.72 = bf16[2,6144]{1,0:T(2,128)(2,1)S(1)} slice(bf16[512,6144]{1,0:T(8,128)(2,1)} %carrier_ref.2), slice={[510:512], [0:6144]} | slice | bytes 49152 | tf_op jit(solution)/shard_map/slice | solution.py:161
  9.9 3.4 %collective-permute-start.1 = (bf16[2,6144]{1,0:T(2,128)(2,1)S(1)}, bf16[2,6144]{1,0:T(2,128)(2,1)S(1)}, u32[]{:S(2)}, u32[]{:S(2)}) collective-permute-start(bf16[2,6144]{1,0:T(2,128)(2,1)S(1)} %slice.72), channel_id=1, source_target_pairs={{0,1},{1,2},{2,3},{3,4},{4,5},{5,6},{6,7},{7,8},{8,9},{9,10},{10,1... | collective-permute-start | bytes 73736 | tf_op jit(solution)/shard_map/ppermute | solution.py:22
  13.3 0.8 collective-permute-done.1
  14.1 6.8 %collective-permute-done.2 = bf16[128,2048]{0,1:T(8,128)(2,1)} collective-permute-done((bf16[128,2048]{0,1:T(8,128)(2,1)}, bf16[128,2048]{0,1:T(8,128)(2,1)}, u32[]{:S(2)}, u32[]{:S(2)}) %collective-permute-start.2) | collective-permute-done | bytes 524320 | tf_op jit(solution)/shard_map/ppermute | solution.py:144
  21.0 2.8 %collective-permute-done.3 = bf16[128,2048]{0,1:T(8,128)(2,1)} collective-permute-done((bf16[128,2048]{0,1:T(8,128)(2,1)}, bf16[128,2048]{0,1:T(8,128)(2,1)}, u32[]{:S(2)}, u32[]{:S(2)}) %collective-permute-start.3) | collective-permute-done | bytes 524320 | tf_op jit(solution)/shard_map/ppermute | solution.py:145
  23.8 6.2 %collective-permute-start.4 = (bf16[128,2048]{0,1:T(8,128)(2,1)}, bf16[128,2048]{0,1:T(8,128)(2,1)}, u32[]{:S(2)}, u32[]{:S(2)}) collective-permute-start(bf16[128,2048]{0,1:T(8,128)(2,1)} %collective-permute-done.2), channel_id=1, source_target_pairs={{0,4},{4,8},{8,12},{12,14},{14,10},{10,6},{6,2},{2,0},{1,5},{5,9},... | collective-permute-start | bytes 1572872 | tf_op jit(solution)/shard_map/ppermute | solution.py:144
  29.9 0.5 collective-permute-start.7
  30.4 0.8 copy-done.6
  31.3 0.8 pad_convert_fusion.1.fw_ref
  32.1 8.6 %shard_map.64 = bf16[512,1024]{1,0:T(8,128)(2,1)} custom-call(f32[128,384]{1,0:T(8,128)} %pad_convert_fusion.1.fw_ref, f32[1,2048]{1,0:T(1,128)} %bitcast.25, f32[3,3,2048]{2,1,0:T(4,128)} %bitcast.21, bf16[3,2,2048]{2,1,0:T(2,128)(2,1)} %bitcast.23, bf16[128,2048]{1,0:T(8,128)(2,1)} %copy-done, bf16[512,6144]{1,0:T(8,128)(2,1)} %carrier_ref.2, ...), custom_call_target="tpu_custom_call" | custom-call | tf_op jit(solution)/shard_map/pallas_call | solution.py:95
  41.0 4.1 %collective-permute-start.11 = (bf16[128,2048]{0,1:T(8,128)(2,1)}, bf16[128,2048]{0,1:T(8,128)(2,1)}, u32[]{:S(2)}, u32[]{:S(2)}) collective-permute-start(bf16[128,2048]{0,1:T(8,128)(2,1)} %collective-permute-done.4), channel_id=1, source_target_pairs={{0,4},{4,8},{8,12},{12,14},{14,10},{10,6},{6,2},{2,0},{1,5},{5,9},... | collective-permute-start | bytes 1572872 | tf_op jit(solution)/shard_map/ppermute | solution.py:144
  45.1 0.8 pad_convert_fusion.fw_ref
  45.9 8.8 %shard_map.65 = bf16[512,1024]{1,0:T(8,128)(2,1)} custom-call(f32[128,384]{1,0:T(8,128)} %pad_convert_fusion.fw_ref, f32[1,2048]{1,0:T(1,128)} %bitcast.26, f32[3,3,2048]{2,1,0:T(4,128)} %bitcast.22, bf16[3,2,2048]{2,1,0:T(2,128)(2,1)} %bitcast.24, bf16[128,2048]{1,0:T(8,128)(2,1)} %copy-done, bf16[512,6144]{1,0:T(8,128)(2,1)} %carrier_ref.2, ...), custom_call_target="tpu_custom_call" | custom-call | tf_op jit(solution)/shard_map/pallas_call | solution.py:95
  54.9 2.7 %fusion.15 = bf16[512,2048]{1,0:T(8,128)(2,1)S(1)} fusion(bf16[512,2048]{1,0:T(8,128)(2,1)S(1)} %copy-done.3, s32[]{:T(128)S(6)} %select_n.132, bf16[128,2048]{0,1:T(8,128)(2,1)} %collective-permute-done.6, bf16[128,2048]{0,1:T(8,128)(2,1)} %bitcast.9, pred[]{:T(512)S(6)} %eq.22, bf16[512,1024]{1,0:T(8,128)(2,1)} %shard_map.65, ...), kind=kOutput, calls=%fused_computation.24 | convolution fusion | flops 546177024 | bytes 3670021 | tf_op jit(solution)/shard_map/dot_general | solution.py:186
  58.0 2.3 %fusion.14 = bf16[512,2048]{1,0:T(8,128)(2,1)S(1)} fusion(bf16[512,2048]{1,0:T(8,128)(2,1)S(1)} %fusion.15, s32[]{:T(128)S(6)} %select_n.140, bf16[128,2048]{0,1:T(8,128)(2,1)} %collective-permute-done.7, bf16[128,2048]{0,1:T(8,128)(2,1)} %collective-permute-done.2, pred[]{:T(512)S(6)} %eq.22, bf16[512,2048]{1,0:T(8,128)(2,1)S(1)} %copy-done.1, ...), kind=kOutput, calls=%fused_computation.23 | convolution fusion | flops 546177024 | bytes 3670021 | tf_op jit(solution)/shard_map/dot_general | solution.py:186
  60.3 1.0 %slice.75 = bf16[128,1024]{0,1:T(8,128)(2,1)S(1)} slice(bf16[128,2048]{0,1:T(8,128)(2,1)} %collective-permute-done.11), slice={[0:128], [0:1024]} | slice | bytes 524288 | tf_op jit(solution)/shard_map/slice | solution.py:178
  61.3 2.1 %collective-permute-start.15 = (bf16[128,1024]{0,1:T(8,128)(2,1)S(1)}, bf16[128,1024]{0,1:T(8,128)(2,1)S(1)}, u32[]{:S(2)}, u32[]{:S(2)}) collective-permute-start(bf16[128,1024]{0,1:T(8,128)(2,1)S(1)} %slice.75), channel_id=1, source_target_pairs={{0,4},{4,8},{8,12},{12,14},{14,10},{10,6},{6,2},{2,0},{1,5},{5,9},... | collective-permute-start | bytes 786440 | tf_op jit(solution)/shard_map/ppermute | solution.py:178
  63.4 2.3 %fusion.13 = bf16[512,2048]{1,0:T(8,128)(2,1)S(1)} fusion(bf16[512,2048]{1,0:T(8,128)(2,1)S(1)} %fusion.14, s32[]{:T(128)S(6)} %select_n.144, bf16[128,2048]{0,1:T(8,128)(2,1)} %collective-permute-done.8, bf16[128,2048]{0,1:T(8,128)(2,1)} %collective-permute-done.3, pred[]{:T(512)S(6)} %eq.22, bf16[512,2048]{1,0:T(8,128)(2,1)S(1)} %copy-done.1, ...), kind=kOutput, calls=%fused_computation.22 | convolution fusion | flops 546177024 | bytes 3670021 | tf_op jit(solution)/shard_map/dot_general | solution.py:186
  65.7 1.0 %slice.76 = bf16[128,1024]{0,1:T(8,128)(2,1)S(1)} slice(bf16[128,2048]{0,1:T(8,128)(2,1)} %collective-permute-done.13), slice={[0:128], [1024:2048]} | slice | bytes 524288 | tf_op jit(solution)/shard_map/slice | solution.py:179
  66.9 0.5 collective-permute-start.14
  67.4 2.0 %fusion.12 = bf16[512,2048]{1,0:T(8,128)(2,1)S(1)} fusion(bf16[512,2048]{1,0:T(8,128)(2,1)S(1)} %fusion.13, s32[]{:T(128)S(6)} %select_n.148, bf16[128,2048]{0,1:T(8,128)(2,1)S(1)} %collective-permute-done.9, bf16[128,2048]{0,1:T(8,128)(2,1)} %collective-permute-done.4, pred[]{:T(512)S(6)} %eq.22, bf16[512,2048]{1,0:T(8,128)(2,1)S(1)} %copy-done.1, ...), kind=kOutput, calls=%fused_computation.21 | convolution fusion | flops 546177024 | bytes 3670021 | tf_op jit(solution)/shard_map/dot_general | solution.py:186
  69.4 0.4 collective-permute-done.15
  69.8 5.1 %collective-permute-done.16 = bf16[128,1024]{0,1:T(8,128)(2,1)S(1)} collective-permute-done((bf16[128,1024]{0,1:T(8,128)(2,1)S(1)}, bf16[128,1024]{0,1:T(8,128)(2,1)S(1)}, u32[]{:S(2)}, u32[]{:S(2)}) %collective-permute-start.16) | collective-permute-done | bytes 262176 | tf_op jit(solution)/shard_map/ppermute | solution.py:179
  75.0 2.0 %fusion.11 = bf16[512,2048]{1,0:T(8,128)(2,1)S(1)} fusion(bf16[512,2048]{1,0:T(8,128)(2,1)S(1)} %fusion.12, s32[]{:T(128)S(6)} %select_n.152, bf16[128,2048]{0,1:T(8,128)(2,1)S(1)} %collective-permute-done.10, bf16[128,2048]{0,1:T(8,128)(2,1)} %collective-permute-done.5, pred[]{:T(512)S(6)} %eq.22, bf16[512,2048]{1,0:T(8,128)(2,1)S(1)} %copy-done.1, ...), kind=kOutput, calls=%fused_computation.20 | convolution fusion | flops 546177024 | bytes 3670021 | tf_op jit(solution)/shard_map/dot_general | solution.py:186
  77.0 2.0 %fusion.10 = bf16[512,2048]{1,0:T(8,128)(2,1)S(1)} fusion(bf16[512,2048]{1,0:T(8,128)(2,1)S(1)} %fusion.11, s32[]{:T(128)S(6)} %select_n.156, bf16[128,2048]{0,1:T(8,128)(2,1)S(1)} %collective-permute-done.12, bf16[128,2048]{0,1:T(8,128)(2,1)} %collective-permute-done.11, pred[]{:T(512)S(6)} %eq.22, bf16[512,2048]{1,0:T(8,128)(2,1)S(1)} %copy-done.1, ...), kind=kOutput, calls=%fused_computation.19 | convolution fusion | flops 546177024 | bytes 3670021 | tf_op jit(solution)/shard_map/dot_general | solution.py:186
  79.0 2.0 %fusion.9 = bf16[512,2048]{1,0:T(8,128)(2,1)S(1)} fusion(bf16[512,2048]{1,0:T(8,128)(2,1)S(1)} %fusion.10, s32[]{:T(128)S(6)} %select_n.160, bf16[128,2048]{0,1:T(8,128)(2,1)S(1)} %collective-permute-done.14, bf16[128,2048]{0,1:T(8,128)(2,1)} %collective-permute-done.13, pred[]{:T(512)S(6)} %eq.22, bf16[512,2048]{1,0:T(8,128)(2,1)S(1)} %copy-done.1, ...), kind=kOutput, calls=%fused_computation.18 | convolution fusion | flops 546177024 | bytes 3670021 | tf_op jit(solution)/shard_map/dot_general | solution.py:186
  81.0 1.3 %copy-done.2 = bf16[512,2048]{1,0:T(8,128)(2,1)} copy-done((bf16[512,2048]{1,0:T(8,128)(2,1)}, bf16[512,2048]{1,0:T(8,128)(2,1)S(1)}, u32[]{:S(2)}) %copy-start.2) | copy-done | bytes 2097176
  82.3 1.4 %fusion.8 = bf16[512,2048]{1,0:T(8,128)(2,1)} fusion(bf16[512,2048]{1,0:T(8,128)(2,1)} %copy-done.2, s32[]{:T(128)S(6)} %select_n.164, bf16[128,2048]{0,1:T(8,128)(2,1)S(1)} %collective-permute-done.17, bf16[128,2048]{0,1:T(8,128)(2,1)S(1)} %constant_dynamic-update-slice_fusion, pred[]{:T(512)S(6)} %eq.22, bf16[512,2048]{1,0:T(8,128)(2,1)S(1)} %copy-done.1, ...), kind=kOutput, calls=%fused_computation.17 | convolution fusion | flops 546177024 | bytes 3670021 | tf_op jit(solution)/shard_map/dot_general | solution.py:186
  (41 shorter events, 1.2 us)
Async XLA Ops:
  3.9 10.2 %collective-permute-start = (bf16[128,2048]{1,0:T(8,128)(2,1)S(1)}, bf16[128,2048]{1,0:T(8,128)(2,1)S(1)}, u32[]{:S(2)}, u32[]{:S(2)}) collective-permute-start(bf16[128,2048]{1,0:T(8,128)(2,1)S(1)} %multiply_convert_fusion), channel_id=1, source_target_pairs={{0,1},{1,2},{2,3},{3,4},{4,5},{5,6},{6,7},{7,8},{8,9},{9,10},{10,1... | collective-permute-start | bytes 1572872 | tf_op jit(solution)/shard_map/ppermute | solution.py:22
  6.3 14.6 %collective-permute-start.2 = (bf16[128,2048]{0,1:T(8,128)(2,1)}, bf16[128,2048]{0,1:T(8,128)(2,1)}, u32[]{:S(2)}, u32[]{:S(2)}) collective-permute-start(bf16[128,2048]{0,1:T(8,128)(2,1)} %bitcast.9), channel_id=1, source_target_pairs={{0,4},{4,8},{8,12},{12,14},{14,10},{10,6},{6,2},{2,0},{1,5},{5,9},... | collective-permute-start | bytes 1572872 | tf_op jit(solution)/shard_map/ppermute | solution.py:144
  8.9 14.8 %collective-permute-start.3 = (bf16[128,2048]{0,1:T(8,128)(2,1)}, bf16[128,2048]{0,1:T(8,128)(2,1)}, u32[]{:S(2)}, u32[]{:S(2)}) collective-permute-start(bf16[128,2048]{0,1:T(8,128)(2,1)} %bitcast.9), channel_id=1, source_target_pairs={{4,0},{8,4},{12,8},{14,12},{10,14},{6,10},{2,6},{0,2},{5,1},{9,5},... | collective-permute-start | bytes 1572872 | tf_op jit(solution)/shard_map/ppermute | solution.py:145
  9.9 4.2 %collective-permute-start.1 = (bf16[2,6144]{1,0:T(2,128)(2,1)S(1)}, bf16[2,6144]{1,0:T(2,128)(2,1)S(1)}, u32[]{:S(2)}, u32[]{:S(2)}) collective-permute-start(bf16[2,6144]{1,0:T(2,128)(2,1)S(1)} %slice.72), channel_id=1, source_target_pairs={{0,1},{1,2},{2,3},{3,4},{4,5},{5,6},{6,7},{7,8},{8,9},{9,10},{10,1... | collective-permute-start | bytes 73736 | tf_op jit(solution)/shard_map/ppermute | solution.py:22
  14.1 16.3 %copy-start.7 = (bf16[2,6144]{1,0:T(2,128)(2,1)}, bf16[2,6144]{1,0:T(2,128)(2,1)S(1)}, u32[]{:S(2)}) copy-start(bf16[2,6144]{1,0:T(2,128)(2,1)S(1)} %collective-permute-done.1) | copy-start | bytes 73732
  14.1 16.3 %copy-start = (bf16[128,2048]{1,0:T(8,128)(2,1)}, bf16[128,2048]{1,0:T(8,128)(2,1)S(1)}, u32[]{:S(2)}) copy-start(bf16[128,2048]{1,0:T(8,128)(2,1)S(1)} %collective-permute-done.halo_ref) | copy-start | bytes 1572868
  23.8 17.2 %collective-permute-start.4 = (bf16[128,2048]{0,1:T(8,128)(2,1)}, bf16[128,2048]{0,1:T(8,128)(2,1)}, u32[]{:S(2)}, u32[]{:S(2)}) collective-permute-start(bf16[128,2048]{0,1:T(8,128)(2,1)} %collective-permute-done.2), channel_id=1, source_target_pairs={{0,4},{4,8},{8,12},{12,14},{14,10},{10,6},{6,2},{2,0},{1,5},{5,9},... | collective-permute-start | bytes 1572872 | tf_op jit(solution)/shard_map/ppermute | solution.py:144
  29.9 11.0 %collective-permute-start.5 = (bf16[128,2048]{0,1:T(8,128)(2,1)}, bf16[128,2048]{0,1:T(8,128)(2,1)}, u32[]{:S(2)}, u32[]{:S(2)}) collective-permute-start(bf16[128,2048]{0,1:T(8,128)(2,1)} %collective-permute-done.3), channel_id=1, source_target_pairs={{4,0},{8,4},{12,8},{14,12},{10,14},{6,10},{2,6},{0,2},{5,1},{9,5},... | collective-permute-start | bytes 1572872 | tf_op jit(solution)/shard_map/ppermute | solution.py:145
  29.9 24.8 %collective-permute-start.6 = (bf16[128,2048]{0,1:T(8,128)(2,1)}, bf16[128,2048]{0,1:T(8,128)(2,1)}, u32[]{:S(2)}, u32[]{:S(2)}) collective-permute-start(bf16[128,2048]{0,1:T(8,128)(2,1)} %bitcast.9), channel_id=1, source_target_pairs={{0,1},{1,0},{2,3},{3,2},{4,5},{5,4},{6,7},{7,6},{8,9},{9,8},{10,11... | collective-permute-start | bytes 1572872 | tf_op jit(solution)/shard_map/ppermute | solution.py:152
  29.9 27.7 %collective-permute-start.7 = (bf16[128,2048]{0,1:T(8,128)(2,1)}, bf16[128,2048]{0,1:T(8,128)(2,1)}, u32[]{:S(2)}, u32[]{:S(2)}) collective-permute-start(bf16[128,2048]{0,1:T(8,128)(2,1)} %collective-permute-done.2), channel_id=1, source_target_pairs={{0,1},{1,0},{2,3},{3,2},{4,5},{5,4},{6,7},{7,6},{8,9},{9,8},{10,11... | collective-permute-start | bytes 1572872 | tf_op jit(solution)/shard_map/ppermute | solution.py:146
  30.4 0.8 copy-start.6
  40.7 22.7 %collective-permute-start.8 = (bf16[128,2048]{0,1:T(8,128)(2,1)}, bf16[128,2048]{0,1:T(8,128)(2,1)}, u32[]{:S(2)}, u32[]{:S(2)}) collective-permute-start(bf16[128,2048]{0,1:T(8,128)(2,1)} %collective-permute-done.3), channel_id=1, source_target_pairs={{0,1},{1,0},{2,3},{3,2},{4,5},{5,4},{6,7},{7,6},{8,9},{9,8},{10,11... | collective-permute-start | bytes 1572872 | tf_op jit(solution)/shard_map/ppermute | solution.py:147
  41.0 19.3 %collective-permute-start.11 = (bf16[128,2048]{0,1:T(8,128)(2,1)}, bf16[128,2048]{0,1:T(8,128)(2,1)}, u32[]{:S(2)}, u32[]{:S(2)}) collective-permute-start(bf16[128,2048]{0,1:T(8,128)(2,1)} %collective-permute-done.4), channel_id=1, source_target_pairs={{0,4},{4,8},{8,12},{12,14},{14,10},{10,6},{6,2},{2,0},{1,5},{5,9},... | collective-permute-start | bytes 1572872 | tf_op jit(solution)/shard_map/ppermute | solution.py:144
  45.9 19.8 %collective-permute-start.13 = (bf16[128,2048]{0,1:T(8,128)(2,1)}, bf16[128,2048]{0,1:T(8,128)(2,1)}, u32[]{:S(2)}, u32[]{:S(2)}) collective-permute-start(bf16[128,2048]{0,1:T(8,128)(2,1)} %collective-permute-done.5), channel_id=1, source_target_pairs={{4,0},{8,4},{12,8},{14,12},{10,14},{6,10},{2,6},{0,2},{5,1},{9,5},... | collective-permute-start | bytes 1572872 | tf_op jit(solution)/shard_map/ppermute | solution.py:145
  45.9 8.9 %copy-start.3 = (bf16[512,2048]{1,0:T(8,128)(2,1)S(1)}, bf16[512,2048]{1,0:T(8,128)(2,1)}, u32[]{:S(2)}) copy-start(bf16[512,2048]{1,0:T(8,128)(2,1)} %param.6) | copy-start | bytes 6291460
  45.9 8.9 %copy-start.4 = (bf16[512,1024]{1,0:T(8,128)(2,1)S(1)}, bf16[512,1024]{1,0:T(8,128)(2,1)}, u32[]{:S(2)}) copy-start(bf16[512,1024]{1,0:T(8,128)(2,1)} %shard_map.64) | copy-start | bytes 3145732
  54.8 3.3 %copy-start.1 = (bf16[512,2048]{1,0:T(8,128)(2,1)S(1)}, bf16[512,2048]{1,0:T(8,128)(2,1)}, u32[]{:S(2)}) copy-start(bf16[512,2048]{1,0:T(8,128)(2,1)} %param.6) | copy-start | bytes 6291460
  54.8 3.3 %copy-start.5 = (bf16[512,1024]{1,0:T(8,128)(2,1)S(1)}, bf16[512,1024]{1,0:T(8,128)(2,1)}, u32[]{:S(2)}) copy-start(bf16[512,1024]{1,0:T(8,128)(2,1)} %shard_map.65) | copy-start | bytes 3145732
  54.8 12.1 %collective-permute-start.9 = (bf16[128,2048]{0,1:T(8,128)(2,1)}, bf16[128,2048]{0,1:T(8,128)(2,1)S(1)}, u32[]{:S(2)}, u32[]{:S(2)}) collective-permute-start(bf16[128,2048]{0,1:T(8,128)(2,1)} %collective-permute-done.4), channel_id=1, source_target_pairs={{0,1},{1,0},{2,3},{3,2},{4,5},{5,4},{6,7},{7,6},{8,9},{9,8},{10,11... | collective-permute-start | bytes 1572872 | tf_op jit(solution)/shard_map/ppermute | solution.py:146
  57.6 17.4 %collective-permute-start.10 = (bf16[128,2048]{0,1:T(8,128)(2,1)}, bf16[128,2048]{0,1:T(8,128)(2,1)S(1)}, u32[]{:S(2)}, u32[]{:S(2)}) collective-permute-start(bf16[128,2048]{0,1:T(8,128)(2,1)} %collective-permute-done.5), channel_id=1, source_target_pairs={{0,1},{1,0},{2,3},{3,2},{4,5},{5,4},{6,7},{7,6},{8,9},{9,8},{10,11... | collective-permute-start | bytes 1572872 | tf_op jit(solution)/shard_map/ppermute | solution.py:147
  61.3 8.4 %collective-permute-start.15 = (bf16[128,1024]{0,1:T(8,128)(2,1)S(1)}, bf16[128,1024]{0,1:T(8,128)(2,1)S(1)}, u32[]{:S(2)}, u32[]{:S(2)}) collective-permute-start(bf16[128,1024]{0,1:T(8,128)(2,1)S(1)} %slice.75), channel_id=1, source_target_pairs={{0,4},{4,8},{8,12},{12,14},{14,10},{10,6},{6,2},{2,0},{1,5},{5,9},... | collective-permute-start | bytes 786440 | tf_op jit(solution)/shard_map/ppermute | solution.py:178
  66.7 8.2 %collective-permute-start.16 = (bf16[128,1024]{0,1:T(8,128)(2,1)S(1)}, bf16[128,1024]{0,1:T(8,128)(2,1)S(1)}, u32[]{:S(2)}, u32[]{:S(2)}) collective-permute-start(bf16[128,1024]{0,1:T(8,128)(2,1)S(1)} %slice.76), channel_id=1, source_target_pairs={{4,0},{8,4},{12,8},{14,12},{10,14},{6,10},{2,6},{0,2},{5,1},{9,5},... | collective-permute-start | bytes 786440 | tf_op jit(solution)/shard_map/ppermute | solution.py:179
  66.8 10.2 %collective-permute-start.12 = (bf16[128,2048]{0,1:T(8,128)(2,1)}, bf16[128,2048]{0,1:T(8,128)(2,1)S(1)}, u32[]{:S(2)}, u32[]{:S(2)}) collective-permute-start(bf16[128,2048]{0,1:T(8,128)(2,1)} %collective-permute-done.11), channel_id=1, source_target_pairs={{0,1},{1,0},{2,3},{3,2},{4,5},{5,4},{6,7},{7,6},{8,9},{9,8},{10,11... | collective-permute-start | bytes 1572872 | tf_op jit(solution)/shard_map/ppermute | solution.py:146
  66.9 12.1 %collective-permute-start.14 = (bf16[128,2048]{0,1:T(8,128)(2,1)}, bf16[128,2048]{0,1:T(8,128)(2,1)S(1)}, u32[]{:S(2)}, u32[]{:S(2)}) collective-permute-start(bf16[128,2048]{0,1:T(8,128)(2,1)} %collective-permute-done.13), channel_id=1, source_target_pairs={{0,1},{1,0},{2,3},{3,2},{4,5},{5,4},{6,7},{7,6},{8,9},{9,8},{10,11... | collective-permute-start | bytes 1572872 | tf_op jit(solution)/shard_map/ppermute | solution.py:147
  74.9 6.0 %collective-permute-start.17 = (bf16[128,2048]{0,1:T(8,128)(2,1)S(1)}, bf16[128,2048]{0,1:T(8,128)(2,1)S(1)}, u32[]{:S(2)}, u32[]{:S(2)}) collective-permute-start(bf16[128,2048]{0,1:T(8,128)(2,1)S(1)} %constant_dynamic-update-slice_fusion), channel_id=1, source_target_pairs={{0,1},{1,0},{2,3},{3,2},{4,5},{5,4},{6,7},{7,6},{8,9},{9,8},{10,11... | collective-permute-start | bytes 1572872 | tf_op jit(solution)/shard_map/ppermute | solution.py:183
  81.0 1.3 %copy-start.2 = (bf16[512,2048]{1,0:T(8,128)(2,1)}, bf16[512,2048]{1,0:T(8,128)(2,1)S(1)}, u32[]{:S(2)}) copy-start(bf16[512,2048]{1,0:T(8,128)(2,1)S(1)} %fusion.9) | copy-start | bytes 6291460
